TPU v7x, 32 devices: a whole 2x2x4 slice. The times are simulated.
32 devices in a mesh: grp: 2 (over y), mem: 4 (over z), lev: 2 (over x), half: 2 (over core).
Axes of the slice: x: 2, y: 2, z: 4, core: 2. Of those that a mesh axis runs over, the one named last changes fastest.
Arguments:
- anomalies: bfloat16 [512, 48, 4, 512], P('half', ('grp', 'mem'), 'lev'), parts along dimension 1, may hold values from -3.5 to 3.5
- control: bfloat16 [256, 48, 4, 256], P('half', ('grp', 'mem'), 'lev'), parts along dimension 1, may hold values from -6 to 6
- precision: float32 [512, 8, 512], P('half', ('grp', 'lev')), parts along dimension 1, may hold values from 0.3 to 3
- row_factor: bfloat16 [512, 256], P('half'), may hold values from -0.375 to 0.375
- col_factor: bfloat16 [512, 256], replicated, may hold values from -0.375 to 0.375
Outputs:
- hessian_product: bfloat16 [256, 48, 4, 256], P('half', ('grp', 'mem'), 'lev'), parts along dimension 1
There are 2 independent parts, one for each index of `grp`. A program takes and returns all parts, laid end to end along the dimension named above; an argument that names none is the same for every part. Nothing has to cross between parts.
All inputs are finite; a program needn't handle non-finite values.
Results may differ from a plain program's by a relative error of at most 0.0095.
Values may be sent and summed in bfloat16 or wider, within the bound.
No kernel may reach another device: no remote copies, remote signals or barrier semaphores. Data moves between devices by JAX's collectives and lax.ppermute only.
A program may use at most 64 MiB of HBM per device.

v0:
```python
import jax
import jax.numpy as jnp
from jax import lax
from jax.sharding import PartitionSpec as P


def local(anomalies, control, precision, row_factor, col_factor):
    columns = row_factor
    expanded = jnp.einsum(
        "rk,kmlc->rmlc",
        columns,
        lax.all_gather(control, "half", axis=0, tiled=True),
        preferred_element_type=jnp.float32,
    ).astype(jnp.bfloat16)
    fields = jnp.einsum("rmlc,nc->rmln", expanded, col_factor, preferred_element_type=jnp.float32)
    members = anomalies
    summed_all = lax.psum(jnp.sum(members.astype(jnp.float32) * fields, axis=1), "mem")
    weighted = (precision * summed_all).astype(jnp.bfloat16)
    members = anomalies
    scaled = (members.astype(jnp.float32) * weighted.astype(jnp.float32)[:, None]).astype(
        jnp.bfloat16
    )
    projected = jnp.einsum(
        "rmln,nc->rmlc", scaled, col_factor, preferred_element_type=jnp.float32
    ).astype(jnp.bfloat16)
    columns = row_factor
    summed = lax.psum_scatter(
        jnp.einsum("rk,rmlc->kmlc", columns, projected, preferred_element_type=jnp.float32),
        "half",
        scatter_dimension=0,
        tiled=True,
    )
    return (control.astype(jnp.float32) + summed).astype(jnp.bfloat16)


def solution(mesh):
    return jax.shard_map(
        local,
        mesh=mesh,
        in_specs=(
            P("half", ("grp", "mem"), "lev", None),
            P("half", ("grp", "mem"), "lev", None),
            P("half", ("grp", "lev"), None),
            P("half", None),
            P(),
        ),
        out_specs=P("half", ("grp", "mem"), "lev", None),
        check_vma=False,
    )
```

profile of v0, /device:TPU:0, one launch (start us, length us, event | category | flops | bytes accessed | tf_op | source)
XLA Modules:
  0.0 123.1 jit_solution(9185707390861467493)
XLA Ops:
  6.5 0.0 copy-start
  6.5 0.0 all-gather.2.cloned.1.call-start
  6.5 0.7 all-gather.2.cloned.1.call-update
  7.3 0.0 all-reduce.2.cloned.1.call-start
  7.3 14.1 %all-gather.2.cloned.1.call-done = bf16[256,6,2,256]{3,2,1,0:T(2,128)(2,1)} async-done(((bf16[128,6,2,256]{3,2,1,0:T(2,128)(2,1)}), bf16[256,6,2,256]{3,2,1,0:T(2,128)(2,1)}) %all-gather.2.cloned.1.call-update) | async-done | bytes 1572880 | tf_op jit(solution)/shard_map/all_gather | solution.py:12
  21.4 2.1 %convolution_convert_fusion = bf16[256,6,2,256]{3,0,2,1:T(8,128)(2,1)S(1)} fusion(bf16[256,6,2,256]{3,2,1,0:T(2,128)(2,1)} %all-gather.2.cloned.1.call-done, bf16[256,256]{1,0:T(8,128)(2,1)} %param.8), kind=kOutput, calls=%fused_computation.7 | convolution fusion | flops 403439616 | bytes 3276800 | tf_op jit(solution)/shard_map/rk,kmlc->rmlc/dot_general | solution.py:9
  23.5 1.6 %copy.17 = bf16[256,6,2,256]{3,2,1,0:T(2,128)(2,1)S(1)} copy(bf16[256,6,2,256]{3,0,2,1:T(8,128)(2,1)S(1)} %convolution_convert_fusion) | data formatting | bytes 3145728
  25.1 0.0 copy-done
  25.1 0.0 copy-start.1
  25.2 3.7 %fusion.7 = f32[256,6,2,512]{3,0,2,1:T(8,128)} fusion(bf16[256,6,2,256]{3,2,1,0:T(2,128)(2,1)S(1)} %copy.17, bf16[512,256]{1,0:T(8,128)(2,1)S(1)} %copy-done), kind=kOutput, calls=%fused_computation.9 | convolution fusion | flops 805306368 | bytes 8126464 | tf_op jit(solution)/shard_map/rmlc,nc->rmln/dot_general | solution.py:15
  28.8 11.8 %fusion = f32[256,2,512]{2,1,0:T(2,128)} fusion(bf16[256,6,2,512]{3,2,1,0:T(2,128)(2,1)S(1)} %copy-done.1, f32[256,6,2,512]{3,0,2,1:T(8,128)} %fusion.7), kind=kLoop, calls=%fused_computation.2 | loop fusion | flops 4456448 | bytes 10485760 | tf_op jit(solution)/shard_map/reduce_sum | solution.py:17
  40.7 0.0 all-reduce.2.cloned.1.call-update
  40.7 0.2 reduce-scatter.2.cloned.1.call-start
  40.9 52.9 %all-reduce.2.cloned.1.call-done = f32[256,2,512]{2,1,0:T(2,128)} async-done(((f32[256,2,512]{2,1,0:T(2,128)}), f32[256,2,512]{2,1,0:T(2,128)}) %all-reduce.2.cloned.1.call-update) | async-done | bytes 1048592 | tf_op jit(solution)/shard_map/psum | solution.py:17
  93.8 2.2 %fusion.12 = f32[256,2,512]{2,1,0:T(2,128)S(1)} fusion(f32[256,2,512]{2,1,0:T(2,128)} %param.7, f32[256,2,512]{2,1,0:T(2,128)} %all-reduce.2.cloned.1.call-done), kind=kLoop, calls=%fused_computation.14 | loop fusion | flops 786432 | bytes 3145728 | tf_op jit(solution)/shard_map/convert_element_type | solution.py:20
  96.1 0.3 copy-done.2
  96.4 3.2 %fusion.1 = bf16[256,6,2,512]{3,2,1,0:T(2,128)(2,1)S(1)} fusion(bf16[256,6,2,512]{3,2,1,0:T(2,128)(2,1)S(1)} %copy-done.2, f32[256,2,512]{2,1,0:T(2,128)S(1)} %fusion.12), kind=kLoop, calls=%fused_computation.3 | loop fusion | flops 4718592 | bytes 7340032 | tf_op jit(solution)/shard_map/convert_element_type | solution.py:20
  99.6 3.1 %convolution_bitcast_fusion = f32[256,6,2,256]{0,3,2,1:T(8,128)} fusion(bf16[256,6,2,512]{3,2,1,0:T(2,128)(2,1)S(1)} %fusion.1, bf16[512,256]{1,0:T(8,128)(2,1)S(1)} %copy-done, bf16[256,256]{1,0:T(8,128)(2,1)S(1)} %copy-done.4), kind=kOutput, calls=%fused_computation.6 | convolution fusion | flops 1208745984 | bytes 6684672 | tf_op jit(solution)/shard_map/rk,rmlc->kmlc/dot_general | solution.py:28
  102.7 0.0 reduce-scatter.2.cloned.1.call-update
  102.7 1.1 copy-done.3
  103.9 0.8 copy.8
  104.6 8.5 %reduce-scatter.2.cloned.1.call-done = f32[128,6,2,256]{0,3,2,1:T(8,128)} async-done(((f32[256,6,2,256]{0,3,2,1:T(8,128)}), f32[128,6,2,256]{0,3,2,1:T(8,128)}) %reduce-scatter.2.cloned.1.call-update) | async-done | bytes 1572880 | tf_op jit(solution)/shard_map/reduce_scatter | solution.py:27
  113.2 1.6 %add_convert_fusion = bf16[128,6,2,256]{0,3,2,1:T(8,128)(2,1)S(1)} fusion(f32[128,6,2,256]{0,3,2,1:T(8,128)} %reduce-scatter.2.cloned.1.call-done, bf16[128,6,2,256]{0,3,2,1:T(8,128)(2,1)S(1)} %copy.8), kind=kLoop, calls=%fused_computation.12 | loop fusion | flops 1179648 | bytes 3145728 | tf_op jit(solution)/shard_map/convert_element_type | solution.py:33
  114.8 1.8 %copy.9 = bf16[128,6,2,256]{3,2,1,0:T(2,128)(2,1)} copy(bf16[128,6,2,256]{0,3,2,1:T(8,128)(2,1)S(1)} %add_convert_fusion) | data formatting | bytes 1572864 | tf_op jit(solution)/shard_map/convert_element_type | solution.py:33
  (5 shorter events, 0.0 us)
Async XLA Ops:
  6.5 18.6 %copy-start = (bf16[512,256]{1,0:T(8,128)(2,1)S(1)}, bf16[512,256]{1,0:T(8,128)(2,1)}, u32[]{:S(2)}) copy-start(bf16[512,256]{1,0:T(8,128)(2,1)} %param.9) | copy-start | bytes 786436
  6.5 14.9 %all-gather.2.cloned.1.call-start = ((), (), s32[]{:S(2)}) async-start(), calls=%async_computation.1 | async-start | bytes 2359296 | tf_op jit(solution)/shard_map/all_gather | solution.py:12
  7.3 86.6 %all-reduce.2.cloned.1.call-start = ((), (), s32[]{:S(2)}) async-start(), calls=%async_computation.2 | async-start | bytes 2097152 | tf_op jit(solution)/shard_map/psum | solution.py:17
  25.1 3.7 %copy-start.1 = (bf16[256,6,2,512]{3,2,1,0:T(2,128)(2,1)S(1)}, bf16[256,6,2,512]{3,2,1,0:T(2,128)(2,1)}, u32[]{:S(2)}) copy-start(bf16[256,6,2,512]{3,2,1,0:T(2,128)(2,1)} %param.5) | copy-start | bytes 9437188
  40.7 72.5 %reduce-scatter.2.cloned.1.call-start = ((), (), s32[]{:S(2)}) async-start(), calls=%async_computation.3 | async-start | bytes 4718592 | tf_op jit(solution)/shard_map/reduce_scatter | solution.py:27
  93.8 2.5 %copy-start.2 = (bf16[256,6,2,512]{3,2,1,0:T(2,128)(2,1)S(1)}, bf16[256,6,2,512]{3,2,1,0:T(2,128)(2,1)}, u32[]{:S(2)}) copy-start(bf16[256,6,2,512]{3,2,1,0:T(2,128)(2,1)} %param.5) | copy-start | bytes 9437188
  96.4 3.2 %copy-start.4 = (bf16[256,256]{1,0:T(8,128)(2,1)S(1)}, bf16[256,256]{1,0:T(8,128)(2,1)}, u32[]{:S(2)}) copy-start(bf16[256,256]{1,0:T(8,128)(2,1)} %param.8) | copy-start | bytes 393220
  102.7 1.1 copy-start.3
Sparse Core Ops, SparseCore 0:
  8.9 12.4 all-gather.1
  40.8 52.9 all-reduce.1
  102.9 10.2 reduce-scatter.1
where the time goes:
time: 123 us
  waiting for transfers between devices  76.3 us (62%)
  other arithmetic  18.9 us (15%)
  between operations  13.2 us (11%)
  matrix products  8.84 us (7%)
  local copies, waits for them, and re-layouts  5.62 us (5%)
    psum x1, waiting for transfers between devices, local(): lax.psum(jnp.sum(members.astype(jnp.float32) * fields, axis=1), 'mem')  52.9 us
    all_gather x1, waiting for transfers between devices, local(): lax.all_gather(control, 'half', axis=0, tiled=True)  14.1 us
    reduce_sum x1, other arithmetic, local(): jnp.sum(members.astype(jnp.float32) * fields, axis=1)  11.8 us
    reduce_scatter x1, waiting for transfers between devices, local(): lax.psum_scatter(jnp.einsum('rk,rmlc->kmlc', columns, projected, preferre...  8.53 us
    unnamed x12, local copies, waits for them, and re-layouts  3.81 us
    dot_general x1, matrix products, local(): jnp.einsum('rmlc,nc->rmln', expanded, col_factor, preferred_element_type=...  3.67 us
    convert_element_type x1, other arithmetic, local(): (members.astype(jnp.float32) * weighted.astype(jnp.float32)[:, None]).ast...  3.24 us
    dot_general x1, matrix products, local(): jnp.einsum('rk,rmlc->kmlc', columns, projected, preferred_element_type=jn...  3.11 us
  transfers between devices with their start and end apart: 3, of which 3 were waited for; matrix products, arithmetic and copies ran while one was open for 1% of the time, Pallas kernels for 0%

commit v1 on v0

v1 whole, which is shorter than its diff:
```python
import jax
import jax.numpy as jnp
from jax import lax
from jax.sharding import PartitionSpec as P


def _swap(x, axis):
    return lax.ppermute(x, axis, [(0, 1), (1, 0)])


def _reduce_scatter_rows(x, axis, size):
    idx = lax.axis_index(axis)
    d = 1
    while d < size:
        half = x.shape[0] // 2
        bit = (idx // d) % 2
        keep = lax.dynamic_slice_in_dim(x, bit * half, half, 0)
        send = lax.dynamic_slice_in_dim(x, (1 - bit) * half, half, 0)
        recv = lax.ppermute(send, axis, [(i, i ^ d) for i in range(size)])
        x = keep + recv
        d *= 2
    return x


def _all_gather_rows(x, axis, size):
    idx = lax.axis_index(axis)
    d = size // 2
    while d >= 1:
        bit = (idx // d) % 2
        recv = lax.ppermute(x, axis, [(i, i ^ d) for i in range(size)])
        lo = jnp.where(bit == 0, x, recv)
        hi = jnp.where(bit == 0, recv, x)
        x = jnp.concatenate([lo, hi], axis=0)
        d //= 2
    return x


def _block_start(axis, size, rows):
    idx = lax.axis_index(axis)
    start = 0
    d, span = 1, rows
    while d < size:
        span //= 2
        start = start + ((idx // d) % 2) * span
        d *= 2
    return start


def local(anomalies, control, precision, row_factor, col_factor, n_mem):
    h = lax.axis_index("half")
    kh = control.shape[0]
    rows = anomalies.shape[0]
    n_lev = anomalies.shape[2]

    ctrl_other = _swap(control, "half")
    rf_own = lax.dynamic_slice_in_dim(row_factor, h * kh, kh, 1)
    rf_other = lax.dynamic_slice_in_dim(row_factor, (1 - h) * kh, kh, 1)
    rf_for_partner = _swap(rf_other, "half")

    pow2 = n_mem & (n_mem - 1) == 0 and rows % n_mem == 0
    blk = rows // n_mem
    start = _block_start("mem", n_mem, rows) if pow2 else 0

    outs = []
    for l in range(n_lev):
        a = anomalies[:, :, l, :]
        c_own = control[:, :, l, :]
        c_oth = ctrl_other[:, :, l, :]
        expanded = (
            jnp.einsum("rk,kmc->rmc", rf_own, c_own, preferred_element_type=jnp.float32)
            + jnp.einsum("rk,kmc->rmc", rf_other, c_oth, preferred_element_type=jnp.float32)
        ).astype(jnp.bfloat16)
        fields = jnp.einsum("rmc,nc->rmn", expanded, col_factor, preferred_element_type=jnp.float32)
        inc = jnp.sum(a.astype(jnp.float32) * fields, axis=1)
        prec = precision[:, l, :]
        if pow2:
            part = _reduce_scatter_rows(inc, "mem", n_mem)
            w_blk = (lax.dynamic_slice_in_dim(prec, start, blk, 0) * part).astype(jnp.bfloat16)
            weighted = _all_gather_rows(w_blk, "mem", n_mem)
        else:
            weighted = (prec * lax.psum(inc, "mem")).astype(jnp.bfloat16)
        scaled = (a.astype(jnp.float32) * weighted.astype(jnp.float32)[:, None, :]).astype(jnp.bfloat16)
        projected = jnp.einsum(
            "rmn,nc->rmc", scaled, col_factor, preferred_element_type=jnp.float32
        ).astype(jnp.bfloat16)
        proj_other = _swap(projected, "half")
        summed = jnp.einsum(
            "rk,rmc->kmc", rf_own, projected, preferred_element_type=jnp.float32
        ) + jnp.einsum("rk,rmc->kmc", rf_for_partner, proj_other, preferred_element_type=jnp.float32)
        outs.append((c_own.astype(jnp.float32) + summed).astype(jnp.bfloat16))
    return jnp.stack(outs, axis=2)


def solution(mesh):
    n_mem = mesh.shape["mem"]

    def f(anomalies, control, precision, row_factor, col_factor):
        return local(anomalies, control, precision, row_factor, col_factor, n_mem)

    return jax.shard_map(
        f,
        mesh=mesh,
        in_specs=(
            P("half", ("grp", "mem"), "lev", None),
            P("half", ("grp", "mem"), "lev", None),
            P("half", ("grp", "lev"), None),
            P("half", None),
            P(),
        ),
        out_specs=P("half", ("grp", "mem"), "lev", None),
        check_vma=False,
    )
```

time: 123 us -> 85.8 us (0.70)
  waiting for transfers between devices: 76.3 us -> 19.9 us
  local copies, waits for them, and re-layouts: 5.62 us -> 27 us
  between operations: 13.2 us -> 0.24 us
  other arithmetic: 18.9 us -> 6.61 us
  starting transfers between devices: 0.26 us -> 12.1 us
  matrix products: 8.84 us -> 19.3 us
    psum x1 -> x0, waiting for transfers between devices: 52.9 us -> none  [local(): lax.psum(jnp.sum(members.astype(jnp.float32) * fields, axis=1), 'mem')]
    ppermute x0 -> x12, waiting for transfers between devices: none -> 19.9 us  [the longest x4 12.7 us: _reduce_scatter_rows(): recv = lax.ppermute(send, axis, [(i, i ^ d) for i in range(size)])]
    all_gather x1 -> x0, waiting for transfers between devices: 14.1 us -> none  [local(): lax.all_gather(control, 'half', axis=0, tiled=True)]
    slice x0 -> x3, local copies, waits for them, and re-layouts: none -> 13.7 us  [the longest x1 6.1 us: local(): a = anomalies[:, :, l, :]]
    ppermute x0 -> x12, starting transfers between devices: none -> 12.1 us  [the longest x4 6.02 us: _reduce_scatter_rows(): recv = lax.ppermute(send, axis, [(i, i ^ d) for i in range(size)])]
    reduce_sum x1 -> x0, other arithmetic: 11.8 us -> none  [local(): jnp.sum(members.astype(jnp.float32) * fields, axis=1)]
    dot_general x3 -> x10, matrix products: 8.84 us -> 19.3 us  [the longest x2 8.11 us: local(): jnp.einsum('rmc,nc->rmn', expanded, col_factor, preferred_element_type=jn...]
    reduce_scatter x1 -> x0, waiting for transfers between devices: 8.53 us -> none  [local(): lax.psum_scatter(jnp.einsum('rk,rmlc->kmlc', columns, projected, preferre...]
  transfers between devices with their start and end apart: 3 -> 12, of which waited for: 3 -> 7; matrix products, arithmetic and copies ran while one was open for 1% -> 44% of each run, Pallas kernels for 0% -> 0%
where the time goes in v1:
time: 85.8 us; the launch traced here: 85.2 us
  local copies, waits for them, and re-layouts  27 us (31%)
  waiting for transfers between devices  19.9 us (23%)
  matrix products  19.3 us (22%)
  starting transfers between devices  12.1 us (14%)
  other arithmetic  6.61 us (8%)
    ppermute x4, waiting for transfers between devices, _reduce_scatter_rows(): recv = lax.ppermute(send, axis, [(i, i ^ d) for i in range(size)])  12.7 us
    dot_general x2, matrix products, local(): jnp.einsum('rmc,nc->rmn', expanded, col_factor, preferred_element_type=jn...  8.11 us
    ppermute x4, waiting for transfers between devices, _all_gather_rows(): recv = lax.ppermute(x, axis, [(i, i ^ d) for i in range(size)])  7.17 us
    slice x1, local copies, waits for them, and re-layouts, local(): a = anomalies[:, :, l, :]  6.1 us
    ppermute x4, starting transfers between devices, _reduce_scatter_rows(): recv = lax.ppermute(send, axis, [(i, i ^ d) for i in range(size)])  6.02 us
    dot_general x2, matrix products, local(): jnp.einsum('rk,kmc->rmc', rf_own, c_own, preferred_element_type=jnp.float32)  5.35 us
    ppermute x4, starting transfers between devices, _all_gather_rows(): recv = lax.ppermute(x, axis, [(i, i ^ d) for i in range(size)])  5.03 us
    unnamed x26, local copies, waits for them, and re-layouts  5 us
  transfers between devices with their start and end apart: 12, of which 7 were waited for; matrix products, arithmetic and copies ran while one was open for 44% of the time, Pallas kernels for 0%

profile of v1, /device:TPU:0, one launch (start us, length us, event | category | flops | bytes accessed | tf_op | source)
XLA Modules:
  0.0 85.2 jit_solution(4022923479661579998)
XLA Ops:
  0.0 2.2 %copy.18 = bf16[128,6,2,256]{3,0,2,1:T(8,128)(2,1)} copy(bf16[128,6,2,256]{3,2,1,0:T(2,128)(2,1)} %param.6) | data formatting | bytes 1572864 | tf_op args[1]
  2.6 4.0 %fusion.54 = (bf16[128,6,1,256]{3,2,1,0:T(2,128)(2,1)}, bf16[128,6,1,256]{3,2,1,0:T(2,128)(2,1)}) fusion(bf16[128,6,2,256]{3,2,1,0:T(2,128)(2,1)} %param.6), kind=kLoop, calls=%fused_computation.84 | loop fusion | bytes 1572864 | tf_op jit(solution)/shard_map/slice | solution.py:67
  6.7 3.6 %fusion.53 = (f32[256,1,512]{2,1,0:T(1,128)}, f32[256,1,512]{2,1,0:T(1,128)}) fusion(f32[256,2,512]{2,1,0:T(2,128)} %param.7), kind=kLoop, calls=%fused_computation.83 | loop fusion | bytes 2097152 | tf_op jit(solution)/shard_map/slice | solution.py:75
  10.9 2.7 %fusion.26 = f32[256,6,256]{2,0,1:T(8,128)} fusion(bf16[128,6,1,256]{3,2,1,0:T(2,128)(2,1)} %get-tuple-element.9, bf16[256,256]{1,0:T(8,128)(2,1)S(1)} %copy-done.7, s32[]{:T(128)S(6)} %select_n.106), kind=kOutput, calls=%fused_computation.39 | convolution fusion | flops 100663296 | bytes 2031620 | tf_op jit(solution)/shard_map/rk,kmc->rmc/dot_general | solution.py:70
  13.6 2.6 %fusion.27 = f32[256,6,256]{2,0,1:T(8,128)} fusion(bf16[128,6,1,256]{3,2,1,0:T(2,128)(2,1)} %get-tuple-element.10, bf16[256,256]{1,0:T(8,128)(2,1)S(1)} %copy-done.7, s32[]{:T(128)S(6)} %select_n.106), kind=kOutput, calls=%fused_computation.40 | convolution fusion | flops 100663296 | bytes 2031620 | tf_op jit(solution)/shard_map/rk,kmc->rmc/dot_general | solution.py:70
  16.2 1.6 %constant_dynamic-slice_fusion.6 = f32[64,1,512]{2,1,0:T(1,128)} fusion(f32[256,1,512]{2,1,0:T(1,128)} %get-tuple-element.7, s32[]{:T(128)S(6)} %select_n.112), kind=kLoop, calls=%fused_computation.80 | loop fusion | bytes 262148 | tf_op jit(solution)/shard_map/dynamic_slice | solution.py:78
  17.8 1.6 %constant_dynamic-slice_fusion.2 = f32[64,1,512]{2,1,0:T(1,128)} fusion(f32[256,1,512]{2,1,0:T(1,128)} %get-tuple-element.8, s32[]{:T(128)S(6)} %select_n.112), kind=kLoop, calls=%fused_computation.76 | loop fusion | bytes 262148 | tf_op jit(solution)/shard_map/dynamic_slice | solution.py:78
  19.4 6.1 %fusion.52 = (bf16[256,6,1,512]{3,2,1,0:T(2,128)(2,1)}, bf16[256,6,1,512]{3,2,1,0:T(2,128)(2,1)}) fusion(bf16[256,6,2,512]{3,2,1,0:T(2,128)(2,1)S(1)} %copy-done.1), kind=kLoop, calls=%fused_computation.82 | loop fusion | bytes 6291456 | tf_op jit(solution)/shard_map/slice | solution.py:66
  25.5 4.6 %fusion = f32[256,512]{1,0:T(8,128)} fusion(f32[256,6,256]{2,0,1:T(8,128)} %fusion.26, bf16[256,6,1,512]{3,2,1,0:T(2,128)(2,1)} %get-tuple-element.5, bf16[128,6,2,256]{3,0,2,1:T(8,128)(2,1)} %collective-permute-done, bf16[512,256]{1,0:T(8,128)(2,1)S(1)} %copy-done, bf16[256,128]{1,0:T(8,128)(2,1)} %constant_dynamic-slice_fusion.5), kind=kOutput, calls=%fused_computation.4 | convolution fusion | flops 506331136 | bytes 5963776 | tf_op jit(solution)/shard_map/rmc,nc->rmn/dot_general | solution.py:73
  30.1 1.7 %constant_dynamic-slice_fusion.4 = f32[128,512]{1,0:T(8,128)} fusion(f32[256,512]{1,0:T(8,128)} %fusion, s32[]{:T(128)S(6)} %select_n.115), kind=kLoop, calls=%fused_computation.78 | loop fusion | bytes 524292 | tf_op jit(solution)/shard_map/dynamic_slice | solution.py:18
  31.8 2.6 %collective-permute-start.1 = (f32[128,512]{1,0:T(8,128)}, f32[128,512]{1,0:T(8,128)}, u32[]{:S(2)}, u32[]{:S(2)}) collective-permute-start(f32[128,512]{1,0:T(8,128)} %constant_dynamic-slice_fusion.4), channel_id=1, source_target_pairs={{0,4},{4,0},{8,12},{12,8},{1,5},{5,1},{9,13},{13,9},{2,6},{6,2},{1... | collective-permute-start | bytes 786440 | tf_op jit(solution)/shard_map/ppermute | solution.py:19
  34.3 3.5 %fusion.2 = f32[256,512]{1,0:T(8,128)} fusion(f32[256,6,256]{2,0,1:T(8,128)} %fusion.27, bf16[256,6,1,512]{3,2,1,0:T(2,128)(2,1)S(1)} %copy-done.4, bf16[128,6,2,256]{3,0,2,1:T(8,128)(2,1)} %collective-permute-done, bf16[512,256]{1,0:T(8,128)(2,1)S(1)} %copy-done, bf16[256,128]{1,0:T(8,128)(2,1)} %constant_dynamic-slice_fusion.5), kind=kOutput, calls=%fused_computation.6 | convolution fusion | flops 506331136 | bytes 4390912 | tf_op jit(solution)/shard_map/rmc,nc->rmn/dot_general | solution.py:73
  39.1 2.6 %collective-permute-done.1 = f32[128,512]{1,0:T(8,128)} collective-permute-done((f32[128,512]{1,0:T(8,128)}, f32[128,512]{1,0:T(8,128)}, u32[]{:S(2)}, u32[]{:S(2)}) %collective-permute-start.1) | collective-permute-done | bytes 262176 | tf_op jit(solution)/shard_map/ppermute | solution.py:19
  42.7 2.8 %collective-permute-start.2 = (f32[64,512]{1,0:T(8,128)S(1)}, f32[64,512]{1,0:T(8,128)S(1)}, u32[]{:S(2)}, u32[]{:S(2)}) collective-permute-start(f32[64,512]{1,0:T(8,128)S(1)} %constant_dynamic-slice_fusion.3), channel_id=1, source_target_pairs={{0,8},{4,12},{8,0},{12,4},{1,9},{5,13},{9,1},{13,5},{2,10},{6,14},... | collective-permute-start | bytes 393224 | tf_op jit(solution)/shard_map/ppermute | solution.py:19
  45.5 4.8 %collective-permute-done.7 = f32[128,512]{1,0:T(8,128)S(1)} collective-permute-done((f32[128,512]{1,0:T(8,128)S(1)}, f32[128,512]{1,0:T(8,128)S(1)}, u32[]{:S(2)}, u32[]{:S(2)}) %collective-permute-start.7) | collective-permute-done | bytes 262176 | tf_op jit(solution)/shard_map/ppermute | solution.py:19
  52.8 2.5 %collective-permute-start.3 = (bf16[64,512]{1,0:T(8,128)(2,1)S(1)}, bf16[64,512]{1,0:T(8,128)(2,1)S(1)}, u32[]{:S(2)}, u32[]{:S(2)}) collective-permute-start(bf16[64,512]{1,0:T(8,128)(2,1)S(1)} %fusion.31), channel_id=1, source_target_pairs={{0,8},{4,12},{8,0},{12,4},{1,9},{5,13},{9,1},{13,5},{2,10},{6,14},... | collective-permute-start | bytes 196616 | tf_op jit(solution)/shard_map/ppermute | solution.py:30
  55.3 5.4 %collective-permute-done.8 = f32[64,512]{1,0:T(8,128)S(1)} collective-permute-done((f32[64,512]{1,0:T(8,128)S(1)}, f32[64,512]{1,0:T(8,128)S(1)}, u32[]{:S(2)}, u32[]{:S(2)}) %collective-permute-start.8) | collective-permute-done | bytes 131104 | tf_op jit(solution)/shard_map/ppermute | solution.py:19
  63.3 2.4 %collective-permute-start.4 = (bf16[128,512]{1,0:T(8,128)(2,1)}, bf16[128,512]{1,0:T(8,128)(2,1)}, u32[]{:S(2)}, u32[]{:S(2)}) collective-permute-start(bf16[128,512]{1,0:T(8,128)(2,1)} %pad_maximum_fusion.1), channel_id=1, source_target_pairs={{0,4},{4,0},{8,12},{12,8},{1,5},{5,1},{9,13},{13,9},{2,6},{6,2},{1... | collective-permute-start | bytes 393224 | tf_op jit(solution)/shard_map/ppermute | solution.py:30
  65.8 1.6 %collective-permute-done.9 = bf16[64,512]{1,0:T(8,128)(2,1)S(1)} collective-permute-done((bf16[64,512]{1,0:T(8,128)(2,1)S(1)}, bf16[64,512]{1,0:T(8,128)(2,1)S(1)}, u32[]{:S(2)}, u32[]{:S(2)}) %collective-permute-start.9) | collective-permute-done | bytes 65568 | tf_op jit(solution)/shard_map/ppermute | solution.py:30
  70.0 3.9 %collective-permute-done.10 = bf16[128,512]{1,0:T(8,128)(2,1)} collective-permute-done((bf16[128,512]{1,0:T(8,128)(2,1)}, bf16[128,512]{1,0:T(8,128)(2,1)}, u32[]{:S(2)}, u32[]{:S(2)}) %collective-permute-start.10) | collective-permute-done | bytes 131104 | tf_op jit(solution)/shard_map/ppermute | solution.py:30
  75.2 1.7 %fusion.10 = bf16[256,6,256]{2,0,1:T(8,128)(2,1)} fusion(f32[256,512]{1,0:T(8,128)S(1)} %maximum_convert_fusion, bf16[256,6,1,512]{3,2,1,0:T(2,128)(2,1)S(1)} %copy-done.6, bf16[512,256]{1,0:T(8,128)(2,1)S(1)} %copy-done), kind=kOutput, calls=%fused_computation.16 | convolution fusion | flops 405405696 | bytes 3145728 | tf_op jit(solution)/shard_map/rmn,nc->rmc/dot_general | solution.py:83
  78.3 1.6 %copy.28 = bf16[256,128]{0,1:T(8,128)(2,1)} copy(bf16[256,128]{1,0:T(8,128)(2,1)} %constant_dynamic-slice_fusion.5) | data formatting | bytes 131072
  79.9 1.4 %fusion.36 = f32[128,6,256]{2,0,1:T(8,128)S(1)} fusion(bf16[256,6,256]{2,0,1:T(8,128)(2,1)} %fusion.10, bf16[256,256]{1,0:T(8,128)(2,1)S(1)} %copy-done.7, s32[]{:T(128)S(6)} %select_n.106), kind=kOutput, calls=%fused_computation.57 | convolution fusion | flops 100663296 | bytes 1638404 | tf_op jit(solution)/shard_map/rk,rmc->kmc/dot_general | solution.py:87
  83.5 1.7 %copy.22 = bf16[128,6,2,256]{3,2,1,0:T(2,128)(2,1)} copy(bf16[128,6,2,256]{3,0,1,2:T(8,128)(2,1)S(1)} %pad_maximum_fusion) | data formatting | bytes 1572864 | tf_op jit(solution)/shard_map/stack | solution.py:91
  (59 shorter events, 15.9 us)
Async XLA Ops:
  0.0 25.5 %copy-start = (bf16[512,256]{1,0:T(8,128)(2,1)S(1)}, bf16[512,256]{1,0:T(8,128)(2,1)}, u32[]{:S(2)}) copy-start(bf16[512,256]{1,0:T(8,128)(2,1)} %param.9) | copy-start | bytes 786436
  0.0 10.2 %copy-start.7 = (bf16[256,256]{1,0:T(8,128)(2,1)S(1)}, bf16[256,256]{1,0:T(8,128)(2,1)}, u32[]{:S(2)}) copy-start(bf16[256,256]{1,0:T(8,128)(2,1)} %param.8) | copy-start | bytes 393220
  2.2 23.3 %collective-permute-start = (bf16[128,6,2,256]{3,0,2,1:T(8,128)(2,1)}, bf16[128,6,2,256]{3,0,2,1:T(8,128)(2,1)}, u32[]{:S(2)}, u32[]{:S(2)}) collective-permute-start(bf16[128,6,2,256]{3,0,2,1:T(8,128)(2,1)} %copy.18), channel_id=1, source_target_pairs={{0,1},{1,0},{2,3},{3,2},{4,5},{5,4},{6,7},{7,6},{8,9},{9,8},{10,11... | collective-permute-start | bytes 2359304 | tf_op jit(solution)/shard_map/ppermute | solution.py:8
  6.7 12.7 %copy-start.1 = (bf16[256,6,2,512]{3,2,1,0:T(2,128)(2,1)S(1)}, bf16[256,6,2,512]{3,2,1,0:T(2,128)(2,1)}, u32[]{:S(2)}) copy-start(bf16[256,6,2,512]{3,2,1,0:T(2,128)(2,1)} %param.5) | copy-start | bytes 9437188
  25.5 8.9 %copy-start.4 = (bf16[256,6,1,512]{3,2,1,0:T(2,128)(2,1)S(1)}, bf16[256,6,1,512]{3,2,1,0:T(2,128)(2,1)}, u32[]{:S(2)}) copy-start(bf16[256,6,1,512]{3,2,1,0:T(2,128)(2,1)} %get-tuple-element.6) | copy-start | bytes 4718596
  31.8 9.9 %collective-permute-start.1 = (f32[128,512]{1,0:T(8,128)}, f32[128,512]{1,0:T(8,128)}, u32[]{:S(2)}, u32[]{:S(2)}) collective-permute-start(f32[128,512]{1,0:T(8,128)} %constant_dynamic-slice_fusion.4), channel_id=1, source_target_pairs={{0,4},{4,0},{8,12},{12,8},{1,5},{5,1},{9,13},{13,9},{2,6},{6,2},{1... | collective-permute-start | bytes 786440 | tf_op jit(solution)/shard_map/ppermute | solution.py:19
  37.9 37.3 %copy-start.6 = (bf16[256,6,1,512]{3,2,1,0:T(2,128)(2,1)S(1)}, bf16[256,6,1,512]{3,2,1,0:T(2,128)(2,1)}, u32[]{:S(2)}) copy-start(bf16[256,6,1,512]{3,2,1,0:T(2,128)(2,1)} %get-tuple-element.5) | copy-start | bytes 4718596
  39.0 11.3 %collective-permute-start.7 = (f32[128,512]{1,0:T(8,128)S(1)}, f32[128,512]{1,0:T(8,128)S(1)}, u32[]{:S(2)}, u32[]{:S(2)}) collective-permute-start(f32[128,512]{1,0:T(8,128)S(1)} %constant_dynamic-slice_fusion.1), channel_id=1, source_target_pairs={{0,4},{4,0},{8,12},{12,8},{1,5},{5,1},{9,13},{13,9},{2,6},{6,2},{1... | collective-permute-start | bytes 786440 | tf_op jit(solution)/shard_map/ppermute | solution.py:19
  42.7 9.2 %collective-permute-start.2 = (f32[64,512]{1,0:T(8,128)S(1)}, f32[64,512]{1,0:T(8,128)S(1)}, u32[]{:S(2)}, u32[]{:S(2)}) collective-permute-start(f32[64,512]{1,0:T(8,128)S(1)} %constant_dynamic-slice_fusion.3), channel_id=1, source_target_pairs={{0,8},{4,12},{8,0},{12,4},{1,9},{5,13},{9,1},{13,5},{2,10},{6,14},... | collective-permute-start | bytes 393224 | tf_op jit(solution)/shard_map/ppermute | solution.py:19
  51.3 9.4 %collective-permute-start.8 = (f32[64,512]{1,0:T(8,128)S(1)}, f32[64,512]{1,0:T(8,128)S(1)}, u32[]{:S(2)}, u32[]{:S(2)}) collective-permute-start(f32[64,512]{1,0:T(8,128)S(1)} %constant_dynamic-slice_fusion), channel_id=1, source_target_pairs={{0,8},{4,12},{8,0},{12,4},{1,9},{5,13},{9,1},{13,5},{2,10},{6,14},... | collective-permute-start | bytes 393224 | tf_op jit(solution)/shard_map/ppermute | solution.py:19
  52.8 9.2 %collective-permute-start.3 = (bf16[64,512]{1,0:T(8,128)(2,1)S(1)}, bf16[64,512]{1,0:T(8,128)(2,1)S(1)}, u32[]{:S(2)}, u32[]{:S(2)}) collective-permute-start(bf16[64,512]{1,0:T(8,128)(2,1)S(1)} %fusion.31), channel_id=1, source_target_pairs={{0,8},{4,12},{8,0},{12,4},{1,9},{5,13},{9,1},{13,5},{2,10},{6,14},... | collective-permute-start | bytes 196616 | tf_op jit(solution)/shard_map/ppermute | solution.py:30
  61.6 5.7 %collective-permute-start.9 = (bf16[64,512]{1,0:T(8,128)(2,1)S(1)}, bf16[64,512]{1,0:T(8,128)(2,1)S(1)}, u32[]{:S(2)}, u32[]{:S(2)}) collective-permute-start(bf16[64,512]{1,0:T(8,128)(2,1)S(1)} %fusion.29), channel_id=1, source_target_pairs={{0,8},{4,12},{8,0},{12,4},{1,9},{5,13},{9,1},{13,5},{2,10},{6,14},... | collective-permute-start | bytes 196616 | tf_op jit(solution)/shard_map/ppermute | solution.py:30
  62.0 0.6 copy-start.8
  62.0 1.3 %copy-start.9 = (bf16[64,512]{1,0:T(8,128)(2,1)}, bf16[64,512]{1,0:T(8,128)(2,1)S(1)}, u32[]{:S(2)}) copy-start(bf16[64,512]{1,0:T(8,128)(2,1)S(1)} %get-tuple-element.16) | copy-start | bytes 196612
  63.3 6.7 %collective-permute-start.4 = (bf16[128,512]{1,0:T(8,128)(2,1)}, bf16[128,512]{1,0:T(8,128)(2,1)}, u32[]{:S(2)}, u32[]{:S(2)}) collective-permute-start(bf16[128,512]{1,0:T(8,128)(2,1)} %pad_maximum_fusion.1), channel_id=1, source_target_pairs={{0,4},{4,0},{8,12},{12,8},{1,5},{5,1},{9,13},{13,9},{2,6},{6,2},{1... | collective-permute-start | bytes 393224 | tf_op jit(solution)/shard_map/ppermute | solution.py:30
  67.3 0.6 copy-start.10
  67.4 1.3 %copy-start.11 = (bf16[64,512]{1,0:T(8,128)(2,1)}, bf16[64,512]{1,0:T(8,128)(2,1)S(1)}, u32[]{:S(2)}) copy-start(bf16[64,512]{1,0:T(8,128)(2,1)S(1)} %get-tuple-element.18) | copy-start | bytes 196612
  68.6 5.3 %collective-permute-start.10 = (bf16[128,512]{1,0:T(8,128)(2,1)}, bf16[128,512]{1,0:T(8,128)(2,1)}, u32[]{:S(2)}, u32[]{:S(2)}) collective-permute-start(bf16[128,512]{1,0:T(8,128)(2,1)} %pad_maximum_fusion.2), channel_id=1, source_target_pairs={{0,4},{4,0},{8,12},{12,8},{1,5},{5,1},{9,13},{13,9},{2,6},{6,2},{1... | collective-permute-start | bytes 393224 | tf_op jit(solution)/shard_map/ppermute | solution.py:30
  68.7 8.3 %copy-start.5 = (bf16[256,6,1,512]{3,2,1,0:T(2,128)(2,1)S(1)}, bf16[256,6,1,512]{3,2,1,0:T(2,128)(2,1)}, u32[]{:S(2)}) copy-start(bf16[256,6,1,512]{3,2,1,0:T(2,128)(2,1)} %get-tuple-element.6) | copy-start | bytes 4718596
  76.8 4.8 %collective-permute-start.6 = (bf16[256,6,256]{2,0,1:T(8,128)(2,1)}, bf16[256,6,256]{2,0,1:T(8,128)(2,1)S(1)}, u32[]{:S(2)}, u32[]{:S(2)}) collective-permute-start(bf16[256,6,256]{2,0,1:T(8,128)(2,1)} %fusion.10), channel_id=1, source_target_pairs={{0,1},{1,0},{2,3},{3,2},{4,5},{5,4},{6,7},{7,6},{8,9},{9,8},{10,11... | collective-permute-start | bytes 2359304 | tf_op jit(solution)/shard_map/ppermute | solution.py:8
  76.9 4.8 %copy-start.3 = (bf16[128,6,1,256]{3,2,1,0:T(2,128)(2,1)S(1)}, bf16[128,6,1,256]{3,2,1,0:T(2,128)(2,1)}, u32[]{:S(2)}) copy-start(bf16[128,6,1,256]{3,2,1,0:T(2,128)(2,1)} %get-tuple-element.9) | copy-start | bytes 1179652
  77.7 4.3 %copy-start.2 = (bf16[128,6,1,256]{3,2,1,0:T(2,128)(2,1)S(1)}, bf16[128,6,1,256]{3,2,1,0:T(2,128)(2,1)}, u32[]{:S(2)}) copy-start(bf16[128,6,1,256]{3,2,1,0:T(2,128)(2,1)} %get-tuple-element.10) | copy-start | bytes 1179652
  77.7 4.3 %collective-permute-start.11 = (bf16[256,6,256]{2,0,1:T(8,128)(2,1)S(1)}, bf16[256,6,256]{2,0,1:T(8,128)(2,1)}, u32[]{:S(2)}, u32[]{:S(2)}) collective-permute-start(bf16[256,6,256]{2,0,1:T(8,128)(2,1)S(1)} %fusion.13), channel_id=1, source_target_pairs={{0,1},{1,0},{2,3},{3,2},{4,5},{5,4},{6,7},{7,6},{8,9},{9,8},{10,11... | collective-permute-start | bytes 2359304 | tf_op jit(solution)/shard_map/ppermute | solution.py:8
  79.9 1.8 %collective-permute-start.5 = (bf16[256,128]{0,1:T(8,128)(2,1)}, bf16[256,128]{0,1:T(8,128)(2,1)S(1)}, u32[]{:S(2)}, u32[]{:S(2)}) collective-permute-start(bf16[256,128]{0,1:T(8,128)(2,1)} %copy.28), channel_id=1, source_target_pairs={{0,1},{1,0},{2,3},{3,2},{4,5},{5,4},{6,7},{7,6},{8,9},{9,8},{10,11... | collective-permute-start | bytes 196616 | tf_op jit(solution)/shard_map/ppermute | solution.py:8

commit v2 on v1

--- a/solution.py
+++ b/solution.py
@@ -52,7 +52,11 @@
     rows = anomalies.shape[0]
     n_lev = anomalies.shape[2]
 
-    ctrl_other = _swap(control, "half")
+    anom_t = jnp.transpose(anomalies, (2, 1, 0, 3))
+    ctrl_t = jnp.transpose(control, (2, 1, 0, 3))
+    prec_t = jnp.transpose(precision, (1, 0, 2))
+
+    ctrl_other = _swap(ctrl_t, "half")
     rf_own = lax.dynamic_slice_in_dim(row_factor, h * kh, kh, 1)
     rf_other = lax.dynamic_slice_in_dim(row_factor, (1 - h) * kh, kh, 1)
     rf_for_partner = _swap(rf_other, "half")
@@ -63,32 +67,32 @@
 
     outs = []
     for l in range(n_lev):
-        a = anomalies[:, :, l, :]
-        c_own = control[:, :, l, :]
-        c_oth = ctrl_other[:, :, l, :]
+        a = anom_t[l]
+        c_own = ctrl_t[l]
+        c_oth = ctrl_other[l]
         expanded = (
-            jnp.einsum("rk,kmc->rmc", rf_own, c_own, preferred_element_type=jnp.float32)
-            + jnp.einsum("rk,kmc->rmc", rf_other, c_oth, preferred_element_type=jnp.float32)
+            jnp.einsum("rk,mkc->mrc", rf_own, c_own, preferred_element_type=jnp.float32)
+            + jnp.einsum("rk,mkc->mrc", rf_other, c_oth, preferred_element_type=jnp.float32)
         ).astype(jnp.bfloat16)
-        fields = jnp.einsum("rmc,nc->rmn", expanded, col_factor, preferred_element_type=jnp.float32)
-        inc = jnp.sum(a.astype(jnp.float32) * fields, axis=1)
-        prec = precision[:, l, :]
+        fields = jnp.einsum("mrc,nc->mrn", expanded, col_factor, preferred_element_type=jnp.float32)
+        inc = jnp.sum(a.astype(jnp.float32) * fields, axis=0)
+        prec = prec_t[l]
         if pow2:
             part = _reduce_scatter_rows(inc, "mem", n_mem)
             w_blk = (lax.dynamic_slice_in_dim(prec, start, blk, 0) * part).astype(jnp.bfloat16)
             weighted = _all_gather_rows(w_blk, "mem", n_mem)
         else:
             weighted = (prec * lax.psum(inc, "mem")).astype(jnp.bfloat16)
-        scaled = (a.astype(jnp.float32) * weighted.astype(jnp.float32)[:, None, :]).astype(jnp.bfloat16)
+        scaled = (a.astype(jnp.float32) * weighted.astype(jnp.float32)[None]).astype(jnp.bfloat16)
         projected = jnp.einsum(
-            "rmn,nc->rmc", scaled, col_factor, preferred_element_type=jnp.float32
+            "mrn,nc->mrc", scaled, col_factor, preferred_element_type=jnp.float32
         ).astype(jnp.bfloat16)
         proj_other = _swap(projected, "half")
         summed = jnp.einsum(
-            "rk,rmc->kmc", rf_own, projected, preferred_element_type=jnp.float32
-        ) + jnp.einsum("rk,rmc->kmc", rf_for_partner, proj_other, preferred_element_type=jnp.float32)
+            "rk,mrc->mkc", rf_own, projected, preferred_element_type=jnp.float32
+        ) + jnp.einsum("rk,mrc->mkc", rf_for_partner, proj_other, preferred_element_type=jnp.float32)
         outs.append((c_own.astype(jnp.float32) + summed).astype(jnp.bfloat16))
-    return jnp.stack(outs, axis=2)
+    return jnp.transpose(jnp.stack(outs, axis=0), (2, 1, 0, 3))
 
 
 def solution(mesh):

time: 85.8 us -> 61.4 us (0.72)
  local copies, waits for them, and re-layouts: 27 us -> 10.9 us
  matrix products: 19.3 us -> 11.5 us
  other arithmetic: 6.61 us -> 1.49 us
  starting transfers between devices: 12.1 us -> 15.4 us
  waiting for transfers between devices: 19.9 us -> 21.5 us
    slice x3 -> x1, local copies, waits for them, and re-layouts: 13.7 us -> 0.81 us  [local(): prec = prec_t[l]]
    dot_general x10, matrix products: 19.3 us -> 11.5 us  [the longest x2 5.27 us: local(): jnp.einsum('mrc,nc->mrn', expanded, col_factor, preferred_element_type=jn...]
    dynamic_slice x2, local copies, waits for them, and re-layouts: 3.11 us -> 0.03 us  [local(): lax.dynamic_slice_in_dim(prec, start, blk, 0) * part]
    ppermute x4, starting transfers between devices: 5.03 us -> 7.95 us  [_all_gather_rows(): recv = lax.ppermute(x, axis, [(i, i ^ d) for i in range(size)])]
    ppermute x4, waiting for transfers between devices: 12.7 us -> 14.9 us  [_reduce_scatter_rows(): recv = lax.ppermute(send, axis, [(i, i ^ d) for i in range(size)])]
    dynamic_slice x4, local copies, waits for them, and re-layouts: 2.86 us -> 0.87 us  [_reduce_scatter_rows(): send = lax.dynamic_slice_in_dim(x, (1 - bit) * half, half, 0)]
    transpose x0 -> x1, local copies, waits for them, and re-layouts: none -> 1.81 us  [local(): return jnp.transpose(jnp.stack(outs, axis=0), (2, 1, 0, 3))]
    convert_element_type x2, other arithmetic: 1.87 us -> 0.06 us  [local(): (lax.dynamic_slice_in_dim(prec, start, blk, 0) * part).astype(jnp.bfloat16)]
  transfers between devices with their start and end apart: 12 -> 12, of which waited for: 7 -> 8; matrix products, arithmetic and copies ran while one was open for 44% -> 21% of each run, Pallas kernels for 0% -> 0%
where the time goes in v2:
time: 61.4 us; the launch traced here: 61.1 us
  waiting for transfers between devices  21.5 us (35%)
  starting transfers between devices  15.4 us (25%)
  matrix products  11.5 us (19%)
  local copies, waits for them, and re-layouts  10.9 us (18%)
  other arithmetic  1.49 us (2%)
    ppermute x4, waiting for transfers between devices, _reduce_scatter_rows(): recv = lax.ppermute(send, axis, [(i, i ^ d) for i in range(size)])  14.9 us
    ppermute x4, starting transfers between devices, _all_gather_rows(): recv = lax.ppermute(x, axis, [(i, i ^ d) for i in range(size)])  7.95 us
    unnamed x14, local copies, waits for them, and re-layouts  6.79 us
    ppermute x4, starting transfers between devices, _reduce_scatter_rows(): recv = lax.ppermute(send, axis, [(i, i ^ d) for i in range(size)])  6.14 us
    ppermute x4, waiting for transfers between devices, _all_gather_rows(): recv = lax.ppermute(x, axis, [(i, i ^ d) for i in range(size)])  5.39 us
    dot_general x2, matrix products, local(): jnp.einsum('mrc,nc->mrn', expanded, col_factor, preferred_element_type=jn...  5.27 us
    dot_general x2, matrix products, local(): jnp.einsum('mrn,nc->mrc', scaled, col_factor, preferred_element_type=jnp....  2.72 us
    dot_general x2, matrix products, local(): jnp.einsum('rk,mkc->mrc', rf_own, c_own, preferred_element_type=jnp.float32)  1.89 us
  transfers between devices with their start and end apart: 12, of which 8 were waited for; matrix products, arithmetic and copies ran while one was open for 21% of the time, Pallas kernels for 0%

profile of v2, /device:TPU:0, one launch (start us, length us, event | category | flops | bytes accessed | tf_op | source)
XLA Modules:
  0.0 61.1 jit_solution(12843996783361071809)
XLA Ops:
  0.0 2.4 %copy.6 = bf16[128,6,2,256]{0,3,1,2:T(8,128)(2,1)S(1)} copy(bf16[128,6,2,256]{3,2,1,0:T(2,128)(2,1)} %param.6) | data formatting | bytes 1572864 | tf_op args[1]
  3.0 0.8 %fusion.54 = (f32[1,256,512]{2,0,1:T(1,128)S(1)}, f32[1,256,512]{2,0,1:T(1,128)S(1)}) fusion(f32[2,256,512]{2,0,1:T(2,128)S(1)} %bitcast.120), kind=kLoop, calls=%fused_computation.85 | loop fusion | bytes 2097152 | tf_op jit(solution)/shard_map/slice | solution.py:79
  3.8 0.6 %constant_dynamic-slice_fusion.5 = bf16[256,128]{1,0:T(8,128)(2,1)} fusion(bf16[256,256]{1,0:T(8,128)(2,1)S(1)} %copy-done.3, s32[]{:T(128)S(6)} %select_n.113), kind=kLoop, calls=%fused_computation.82 | loop fusion | bytes 131076 | tf_op jit(solution)/shard_map/dynamic_slice | solution.py:61
  4.5 4.2 %copy.22 = bf16[256,6,2,512]{3,0,1,2:T(8,128)(2,1)} copy(bf16[256,6,2,512]{3,2,1,0:T(2,128)(2,1)} %param.5) | data formatting | bytes 6291456 | tf_op args[0]
  8.7 1.5 %fusion.27 = f32[256,6,256]{2,0,1:T(8,128)} fusion(bf16[2,6,128,256]{2,3,1,0:T(8,128)(2,1)S(1)} %bitcast.112, bf16[256,256]{1,0:T(8,128)(2,1)S(1)} %copy-done.3, s32[]{:T(128)S(6)} %select_n.112), kind=kOutput, calls=%fused_computation.37 | convolution fusion | flops 100663296 | bytes 2031620 | tf_op jit(solution)/shard_map/rk,mkc->mrc/dot_general | solution.py:74
  10.6 2.9 %fusion.2 = f32[256,512]{1,0:T(8,128)S(1)} fusion(bf16[2,6,256,512]{3,2,1,0:T(8,128)(2,1)} %bitcast.116, f32[256,6,256]{2,0,1:T(8,128)} %fusion.27, bf16[2,6,128,256]{2,3,1,0:T(8,128)(2,1)} %collective-permute-done, bf16[512,256]{1,0:T(8,128)(2,1)S(1)} %copy-done, bf16[256,128]{1,0:T(8,128)(2,1)} %constant_dynamic-slice_fusion.5), kind=kOutput, calls=%fused_computation.6 | convolution fusion | flops 506331136 | bytes 4390912 | tf_op jit(solution)/shard_map/mrc,nc->mrn/dot_general | solution.py:77
  13.5 0.8 %constant_dynamic-slice_fusion.1 = f32[128,512]{1,0:T(8,128)} fusion(f32[256,512]{1,0:T(8,128)S(1)} %fusion.2, s32[]{:T(128)S(6)} %select_n.115), kind=kLoop, calls=%fused_computation.78 | loop fusion | bytes 524292 | tf_op jit(solution)/shard_map/dynamic_slice | solution.py:18
  14.4 2.6 %collective-permute-start.7 = (f32[128,512]{1,0:T(8,128)}, f32[128,512]{1,0:T(8,128)}, u32[]{:S(2)}, u32[]{:S(2)}) collective-permute-start(f32[128,512]{1,0:T(8,128)} %constant_dynamic-slice_fusion.1), channel_id=1, source_target_pairs={{0,4},{4,0},{8,12},{12,8},{1,5},{5,1},{9,13},{13,9},{2,6},{6,2},{1... | collective-permute-start | bytes 786440 | tf_op jit(solution)/shard_map/ppermute | solution.py:19
  17.0 2.4 %fusion = f32[256,512]{1,0:T(8,128)S(1)} fusion(bf16[2,6,256,512]{3,2,1,0:T(8,128)(2,1)} %bitcast.117, f32[256,6,256]{2,0,1:T(8,128)S(1)} %fusion.26, bf16[2,6,128,256]{2,3,1,0:T(8,128)(2,1)} %collective-permute-done, bf16[512,256]{1,0:T(8,128)(2,1)S(1)} %copy-done, bf16[256,128]{1,0:T(8,128)(2,1)} %constant_dynamic-slice_fusion.5), kind=kOutput, calls=%fused_computation.4 | convolution fusion | flops 506331136 | bytes 4390912 | tf_op jit(solution)/shard_map/mrc,nc->mrn/dot_general | solution.py:77
  19.5 4.9 %collective-permute-done.7 = f32[128,512]{1,0:T(8,128)} collective-permute-done((f32[128,512]{1,0:T(8,128)}, f32[128,512]{1,0:T(8,128)}, u32[]{:S(2)}, u32[]{:S(2)}) %collective-permute-start.7) | collective-permute-done | bytes 262176 | tf_op jit(solution)/shard_map/ppermute | solution.py:19
  24.5 1.1 %dynamic-slice_add_fusion = f32[128,512]{1,0:T(8,128)S(1)} fusion(f32[128,512]{1,0:T(8,128)} %collective-permute-done.7, f32[256,512]{1,0:T(8,128)} %copy-done.4, s32[]{:T(128)S(6)} %select_n.114), kind=kLoop, calls=%fused_computation.44 | loop fusion | flops 65536 | bytes 786436 | tf_op jit(solution)/shard_map/add | solution.py:20
  25.5 3.0 %collective-permute-start.8 = (f32[64,512]{1,0:T(8,128)S(1)}, f32[64,512]{1,0:T(8,128)S(1)}, u32[]{:S(2)}, u32[]{:S(2)}) collective-permute-start(f32[64,512]{1,0:T(8,128)S(1)} %constant_dynamic-slice_fusion), channel_id=1, source_target_pairs={{0,8},{4,12},{8,0},{12,4},{1,9},{5,13},{9,1},{13,5},{2,10},{6,14},... | collective-permute-start | bytes 393224 | tf_op jit(solution)/shard_map/ppermute | solution.py:19
  28.6 4.0 %collective-permute-done.1 = f32[128,512]{1,0:T(8,128)S(1)} collective-permute-done((f32[128,512]{1,0:T(8,128)S(1)}, f32[128,512]{1,0:T(8,128)S(1)}, u32[]{:S(2)}, u32[]{:S(2)}) %collective-permute-start.1) | collective-permute-done | bytes 262176 | tf_op jit(solution)/shard_map/ppermute | solution.py:19
  33.1 2.6 %collective-permute-start.9 = (bf16[64,512]{1,0:T(8,128)(2,1)S(1)}, bf16[64,512]{1,0:T(8,128)(2,1)S(1)}, u32[]{:S(2)}, u32[]{:S(2)}) collective-permute-start(bf16[64,512]{1,0:T(8,128)(2,1)S(1)} %fusion.32), channel_id=1, source_target_pairs={{0,8},{4,12},{8,0},{12,4},{1,9},{5,13},{9,1},{13,5},{2,10},{6,14},... | collective-permute-start | bytes 196616 | tf_op jit(solution)/shard_map/ppermute | solution.py:30
  35.7 5.9 %collective-permute-done.2 = f32[64,512]{1,0:T(8,128)S(1)} collective-permute-done((f32[64,512]{1,0:T(8,128)S(1)}, f32[64,512]{1,0:T(8,128)S(1)}, u32[]{:S(2)}, u32[]{:S(2)}) %collective-permute-start.2) | collective-permute-done | bytes 131104 | tf_op jit(solution)/shard_map/ppermute | solution.py:19
  41.8 1.2 %collective-permute-done.9 = bf16[64,512]{1,0:T(8,128)(2,1)S(1)} collective-permute-done((bf16[64,512]{1,0:T(8,128)(2,1)S(1)}, bf16[64,512]{1,0:T(8,128)(2,1)S(1)}, u32[]{:S(2)}, u32[]{:S(2)}) %collective-permute-start.9) | collective-permute-done | bytes 65568 | tf_op jit(solution)/shard_map/ppermute | solution.py:30
  43.0 3.3 %collective-permute-start.10 = (bf16[128,512]{1,0:T(8,128)(2,1)S(1)}, bf16[128,512]{1,0:T(8,128)(2,1)S(1)}, u32[]{:S(2)}, u32[]{:S(2)}) collective-permute-start(bf16[128,512]{1,0:T(8,128)(2,1)S(1)} %pad_maximum_fusion.1), channel_id=1, source_target_pairs={{0,4},{4,0},{8,12},{12,8},{1,5},{5,1},{9,13},{13,9},{2,6},{6,2},{1... | collective-permute-start | bytes 393224 | tf_op jit(solution)/shard_map/ppermute | solution.py:30
  46.3 1.1 %collective-permute-done.3 = bf16[64,512]{1,0:T(8,128)(2,1)S(1)} collective-permute-done((bf16[64,512]{1,0:T(8,128)(2,1)S(1)}, bf16[64,512]{1,0:T(8,128)(2,1)S(1)}, u32[]{:S(2)}, u32[]{:S(2)}) %collective-permute-start.3) | collective-permute-done | bytes 65568 | tf_op jit(solution)/shard_map/ppermute | solution.py:30
  47.4 2.0 %collective-permute-start.4 = (bf16[128,512]{1,0:T(8,128)(2,1)S(1)}, bf16[128,512]{1,0:T(8,128)(2,1)S(1)}, u32[]{:S(2)}, u32[]{:S(2)}) collective-permute-start(bf16[128,512]{1,0:T(8,128)(2,1)S(1)} %pad_maximum_fusion), channel_id=1, source_target_pairs={{0,4},{4,0},{8,12},{12,8},{1,5},{5,1},{9,13},{13,9},{2,6},{6,2},{1... | collective-permute-start | bytes 393224 | tf_op jit(solution)/shard_map/ppermute | solution.py:30
  49.4 0.8 %collective-permute-done.10 = bf16[128,512]{1,0:T(8,128)(2,1)S(1)} collective-permute-done((bf16[128,512]{1,0:T(8,128)(2,1)S(1)}, bf16[128,512]{1,0:T(8,128)(2,1)S(1)}, u32[]{:S(2)}, u32[]{:S(2)}) %collective-permute-start.10) | collective-permute-done | bytes 131104 | tf_op jit(solution)/shard_map/ppermute | solution.py:30
  50.1 2.3 %collective-permute-done.4 = bf16[128,512]{1,0:T(8,128)(2,1)S(1)} collective-permute-done((bf16[128,512]{1,0:T(8,128)(2,1)S(1)}, bf16[128,512]{1,0:T(8,128)(2,1)S(1)}, u32[]{:S(2)}, u32[]{:S(2)}) %collective-permute-start.4) | collective-permute-done | bytes 131104 | tf_op jit(solution)/shard_map/ppermute | solution.py:30
  52.6 2.1 %fusion.13 = bf16[6,256,256]{2,1,0:T(8,128)(2,1)S(1)} fusion(f32[256,512]{1,0:T(8,128)S(1)} %maximum_convert_fusion.1, bf16[2,6,256,512]{3,2,1,0:T(8,128)(2,1)} %bitcast.118, bf16[512,256]{1,0:T(8,128)(2,1)S(1)} %copy-done), kind=kOutput, calls=%fused_computation.18 | convolution fusion | flops 405405696 | bytes 3145728 | tf_op jit(solution)/shard_map/mrn,nc->mrc/dot_general | solution.py:87
  57.1 1.3 %collective-permute-done.6 = bf16[256,128]{1,0:T(8,128)(2,1)S(1)} collective-permute-done((bf16[256,128]{1,0:T(8,128)(2,1)S(1)}, bf16[256,128]{1,0:T(8,128)(2,1)S(1)}, u32[]{:S(2)}, u32[]{:S(2)}) %collective-permute-start.6) | collective-permute-done | bytes 65568 | tf_op jit(solution)/shard_map/ppermute | solution.py:8
  59.3 1.8 %copy.12 = bf16[128,6,2,256]{3,2,1,0:T(2,128)(2,1)} copy(bf16[128,6,2,256]{0,3,1,2:T(8,128)(2,1)S(1)} %maximum_bitcast_fusion) | data formatting | bytes 1572864 | tf_op jit(solution)/shard_map/transpose | solution.py:95
  (45 shorter events, 5.1 us)
Async XLA Ops:
  0.0 10.6 %copy-start = (bf16[512,256]{1,0:T(8,128)(2,1)S(1)}, bf16[512,256]{1,0:T(8,128)(2,1)}, u32[]{:S(2)}) copy-start(bf16[512,256]{1,0:T(8,128)(2,1)} %param.9) | copy-start | bytes 786436
  0.0 3.0 %copy-start.2 = (f32[256,2,512]{2,1,0:T(2,128)S(1)}, f32[256,2,512]{2,1,0:T(2,128)}, u32[]{:S(2)}) copy-start(f32[256,2,512]{2,1,0:T(2,128)} %param.7) | copy-start | bytes 3145732
  0.0 3.8 %copy-start.3 = (bf16[256,256]{1,0:T(8,128)(2,1)S(1)}, bf16[256,256]{1,0:T(8,128)(2,1)}, u32[]{:S(2)}) copy-start(bf16[256,256]{1,0:T(8,128)(2,1)} %param.8) | copy-start | bytes 393220
  2.4 8.1 %collective-permute-start = (bf16[2,6,128,256]{2,3,1,0:T(8,128)(2,1)S(1)}, bf16[2,6,128,256]{2,3,1,0:T(8,128)(2,1)}, u32[]{:S(2)}, u32[]{:S(2)}) collective-permute-start(bf16[2,6,128,256]{2,3,1,0:T(8,128)(2,1)S(1)} %bitcast.111), channel_id=1, source_target_pairs={{0,1},{1,0},{2,3},{3,2},{4,5},{5,4},{6,7},{7,6},{8,9},{9,8},{10,11... | collective-permute-start | bytes 2359304 | tf_op jit(solution)/shard_map/ppermute | solution.py:8
  13.5 0.9 %copy-start.4 = (f32[256,512]{1,0:T(8,128)}, f32[256,512]{1,0:T(8,128)S(1)}, u32[]{:S(2)}) copy-start(f32[256,512]{1,0:T(8,128)S(1)} %fusion.2) | copy-start | bytes 1572868
  14.4 10.1 %collective-permute-start.7 = (f32[128,512]{1,0:T(8,128)}, f32[128,512]{1,0:T(8,128)}, u32[]{:S(2)}, u32[]{:S(2)}) collective-permute-start(f32[128,512]{1,0:T(8,128)} %constant_dynamic-slice_fusion.1), channel_id=1, source_target_pairs={{0,4},{4,0},{8,12},{12,8},{1,5},{5,1},{9,13},{13,9},{2,6},{6,2},{1... | collective-permute-start | bytes 786440 | tf_op jit(solution)/shard_map/ppermute | solution.py:19
  19.4 13.1 %collective-permute-start.1 = (f32[128,512]{1,0:T(8,128)S(1)}, f32[128,512]{1,0:T(8,128)S(1)}, u32[]{:S(2)}, u32[]{:S(2)}) collective-permute-start(f32[128,512]{1,0:T(8,128)S(1)} %constant_dynamic-slice_fusion.4), channel_id=1, source_target_pairs={{0,4},{4,0},{8,12},{12,8},{1,5},{5,1},{9,13},{13,9},{2,6},{6,2},{1... | collective-permute-start | bytes 786440 | tf_op jit(solution)/shard_map/ppermute | solution.py:19
  25.5 7.5 %collective-permute-start.8 = (f32[64,512]{1,0:T(8,128)S(1)}, f32[64,512]{1,0:T(8,128)S(1)}, u32[]{:S(2)}, u32[]{:S(2)}) collective-permute-start(f32[64,512]{1,0:T(8,128)S(1)} %constant_dynamic-slice_fusion), channel_id=1, source_target_pairs={{0,8},{4,12},{8,0},{12,4},{1,9},{5,13},{9,1},{13,5},{2,10},{6,14},... | collective-permute-start | bytes 393224 | tf_op jit(solution)/shard_map/ppermute | solution.py:19
  32.6 9.0 %collective-permute-start.2 = (f32[64,512]{1,0:T(8,128)S(1)}, f32[64,512]{1,0:T(8,128)S(1)}, u32[]{:S(2)}, u32[]{:S(2)}) collective-permute-start(f32[64,512]{1,0:T(8,128)S(1)} %constant_dynamic-slice_fusion.3), channel_id=1, source_target_pairs={{0,8},{4,12},{8,0},{12,4},{1,9},{5,13},{9,1},{13,5},{2,10},{6,14},... | collective-permute-start | bytes 393224 | tf_op jit(solution)/shard_map/ppermute | solution.py:19
  33.1 9.9 %collective-permute-start.9 = (bf16[64,512]{1,0:T(8,128)(2,1)S(1)}, bf16[64,512]{1,0:T(8,128)(2,1)S(1)}, u32[]{:S(2)}, u32[]{:S(2)}) collective-permute-start(bf16[64,512]{1,0:T(8,128)(2,1)S(1)} %fusion.32), channel_id=1, source_target_pairs={{0,8},{4,12},{8,0},{12,4},{1,9},{5,13},{9,1},{13,5},{2,10},{6,14},... | collective-permute-start | bytes 196616 | tf_op jit(solution)/shard_map/ppermute | solution.py:30
  41.7 5.7 %collective-permute-start.3 = (bf16[64,512]{1,0:T(8,128)(2,1)S(1)}, bf16[64,512]{1,0:T(8,128)(2,1)S(1)}, u32[]{:S(2)}, u32[]{:S(2)}) collective-permute-start(bf16[64,512]{1,0:T(8,128)(2,1)S(1)} %fusion.33), channel_id=1, source_target_pairs={{0,8},{4,12},{8,0},{12,4},{1,9},{5,13},{9,1},{13,5},{2,10},{6,14},... | collective-permute-start | bytes 196616 | tf_op jit(solution)/shard_map/ppermute | solution.py:30
  43.0 7.1 %collective-permute-start.10 = (bf16[128,512]{1,0:T(8,128)(2,1)S(1)}, bf16[128,512]{1,0:T(8,128)(2,1)S(1)}, u32[]{:S(2)}, u32[]{:S(2)}) collective-permute-start(bf16[128,512]{1,0:T(8,128)(2,1)S(1)} %pad_maximum_fusion.1), channel_id=1, source_target_pairs={{0,4},{4,0},{8,12},{12,8},{1,5},{5,1},{9,13},{13,9},{2,6},{6,2},{1... | collective-permute-start | bytes 393224 | tf_op jit(solution)/shard_map/ppermute | solution.py:30
  47.4 5.1 %collective-permute-start.4 = (bf16[128,512]{1,0:T(8,128)(2,1)S(1)}, bf16[128,512]{1,0:T(8,128)(2,1)S(1)}, u32[]{:S(2)}, u32[]{:S(2)}) collective-permute-start(bf16[128,512]{1,0:T(8,128)(2,1)S(1)} %pad_maximum_fusion), channel_id=1, source_target_pairs={{0,4},{4,0},{8,12},{12,8},{1,5},{5,1},{9,13},{13,9},{2,6},{6,2},{1... | collective-permute-start | bytes 393224 | tf_op jit(solution)/shard_map/ppermute | solution.py:30
  52.6 2.4 %copy-start.1 = (bf16[256,6,2,512]{3,0,1,2:T(8,128)(2,1)S(1)}, bf16[256,6,2,512]{3,0,1,2:T(8,128)(2,1)}, u32[]{:S(2)}) copy-start(bf16[256,6,2,512]{3,0,1,2:T(8,128)(2,1)} %copy.22) | copy-start | bytes 9437188
  54.8 3.6 %collective-permute-start.11 = (bf16[6,256,256]{2,1,0:T(8,128)(2,1)S(1)}, bf16[6,256,256]{2,1,0:T(8,128)(2,1)S(1)}, u32[]{:S(2)}, u32[]{:S(2)}) collective-permute-start(bf16[6,256,256]{2,1,0:T(8,128)(2,1)S(1)} %fusion.13), channel_id=1, source_target_pairs={{0,1},{1,0},{2,3},{3,2},{4,5},{5,4},{6,7},{7,6},{8,9},{9,8},{10,11... | collective-permute-start | bytes 2359304 | tf_op jit(solution)/shard_map/ppermute | solution.py:8
  55.0 1.1 %copy-start.5 = (bf16[256,128]{1,0:T(8,128)(2,1)S(1)}, bf16[256,128]{1,0:T(8,128)(2,1)}, u32[]{:S(2)}) copy-start(bf16[256,128]{1,0:T(8,128)(2,1)} %constant_dynamic-slice_fusion.5) | copy-start | bytes 196612
  55.6 3.2 %collective-permute-start.5 = (bf16[6,256,256]{2,1,0:T(8,128)(2,1)S(1)}, bf16[6,256,256]{2,1,0:T(8,128)(2,1)S(1)}, u32[]{:S(2)}, u32[]{:S(2)}) collective-permute-start(bf16[6,256,256]{2,1,0:T(8,128)(2,1)S(1)} %fusion.10), channel_id=1, source_target_pairs={{0,1},{1,0},{2,3},{3,2},{4,5},{5,4},{6,7},{7,6},{8,9},{9,8},{10,11... | collective-permute-start | bytes 2359304 | tf_op jit(solution)/shard_map/ppermute | solution.py:8
  56.1 2.3 %collective-permute-start.6 = (bf16[256,128]{1,0:T(8,128)(2,1)S(1)}, bf16[256,128]{1,0:T(8,128)(2,1)S(1)}, u32[]{:S(2)}, u32[]{:S(2)}) collective-permute-start(bf16[256,128]{1,0:T(8,128)(2,1)S(1)} %copy-done.5), channel_id=1, source_target_pairs={{0,1},{1,0},{2,3},{3,2},{4,5},{5,4},{6,7},{7,6},{8,9},{9,8},{10,11... | collective-permute-start | bytes 196616 | tf_op jit(solution)/shard_map/ppermute | solution.py:8

commit v3 on v2

--- a/solution.py
+++ b/solution.py
@@ -8,7 +8,7 @@
     return lax.ppermute(x, axis, [(0, 1), (1, 0)])
 
 
-def _reduce_scatter_rows(x, axis, size):
+def _reduce_scatter_rows(x, axis, size, wire):
     idx = lax.axis_index(axis)
     d = 1
     while d < size:
@@ -16,8 +16,8 @@
         bit = (idx // d) % 2
         keep = lax.dynamic_slice_in_dim(x, bit * half, half, 0)
         send = lax.dynamic_slice_in_dim(x, (1 - bit) * half, half, 0)
-        recv = lax.ppermute(send, axis, [(i, i ^ d) for i in range(size)])
-        x = keep + recv
+        recv = lax.ppermute(send.astype(wire), axis, [(i, i ^ d) for i in range(size)])
+        x = keep + recv.astype(x.dtype)
         d *= 2
     return x
 
@@ -78,7 +78,7 @@
         inc = jnp.sum(a.astype(jnp.float32) * fields, axis=0)
         prec = prec_t[l]
         if pow2:
-            part = _reduce_scatter_rows(inc, "mem", n_mem)
+            part = _reduce_scatter_rows(inc, "mem", n_mem, jnp.bfloat16)
             w_blk = (lax.dynamic_slice_in_dim(prec, start, blk, 0) * part).astype(jnp.bfloat16)
             weighted = _all_gather_rows(w_blk, "mem", n_mem)
         else:

time: 61.4 us -> 56.8 us (0.925)
  starting transfers between devices: 15.4 us -> 10.3 us
  waiting for transfers between devices: 21.5 us -> 19.1 us
  matrix products: 11.5 us -> 13.1 us
  other arithmetic: 1.49 us -> 2.33 us
    ppermute x4, waiting for transfers between devices: 14.9 us -> 7.6 us  [_reduce_scatter_rows(): lax.ppermute(send.astype(wire), axis, [(i, i ^ d) for i in range(size)])]
    ppermute x4, starting transfers between devices: 7.95 us -> 1.34 us  [_all_gather_rows(): recv = lax.ppermute(x, axis, [(i, i ^ d) for i in range(size)])]
    ppermute x4, waiting for transfers between devices: 5.39 us -> 10.1 us  [_all_gather_rows(): recv = lax.ppermute(x, axis, [(i, i ^ d) for i in range(size)])]
    convert_element_type x0 -> x4, local copies, waits for them, and re-layouts: none -> 1.97 us  [_reduce_scatter_rows(): send.astype(wire)]
    ppermute x4, starting transfers between devices: 6.14 us -> 7.77 us  [_reduce_scatter_rows(): lax.ppermute(send.astype(wire), axis, [(i, i ^ d) for i in range(size)])]
    dot_general x2, matrix products: 5.27 us -> 6.8 us  [local(): jnp.einsum('mrc,nc->mrn', expanded, col_factor, preferred_element_type=jn...]
    dynamic_slice x4 -> x0, local copies, waits for them, and re-layouts: 0.87 us -> none  [_reduce_scatter_rows(): send = lax.dynamic_slice_in_dim(x, (1 - bit) * half, half, 0)]
    add x2, other arithmetic: 1.1 us -> 1.96 us  [_reduce_scatter_rows(): x = keep + recv.astype(x.dtype)]
  transfers between devices with their start and end apart: 12 -> 12, of which waited for: 8 -> 7; matrix products, arithmetic and copies ran while one was open for 21% -> 27% of each run, Pallas kernels for 0% -> 0%
where the time goes in v3:
time: 56.8 us; the launch traced here: 56.4 us
  waiting for transfers between devices  19.1 us (34%)
  matrix products  13.1 us (23%)
  local copies, waits for them, and re-layouts  11.3 us (20%)
  starting transfers between devices  10.3 us (18%)
  other arithmetic  2.33 us (4%)
    ppermute x4, waiting for transfers between devices, _all_gather_rows(): recv = lax.ppermute(x, axis, [(i, i ^ d) for i in range(size)])  10.1 us
    ppermute x4, starting transfers between devices, _reduce_scatter_rows(): lax.ppermute(send.astype(wire), axis, [(i, i ^ d) for i in range(size)])  7.77 us
    ppermute x4, waiting for transfers between devices, _reduce_scatter_rows(): lax.ppermute(send.astype(wire), axis, [(i, i ^ d) for i in range(size)])  7.6 us
    dot_general x2, matrix products, local(): jnp.einsum('mrc,nc->mrn', expanded, col_factor, preferred_element_type=jn...  6.8 us
    unnamed x10, local copies, waits for them, and re-layouts  6.69 us
    dot_general x2, matrix products, local(): jnp.einsum('mrn,nc->mrc', scaled, col_factor, preferred_element_type=jnp....  2.73 us
    convert_element_type x4, local copies, waits for them, and re-layouts, _reduce_scatter_rows(): send.astype(wire)  1.97 us
    add x2, other arithmetic, _reduce_scatter_rows(): x = keep + recv.astype(x.dtype)  1.96 us
  transfers between devices with their start and end apart: 12, of which 7 were waited for; matrix products, arithmetic and copies ran while one was open for 27% of the time, Pallas kernels for 0%

profile of v3, /device:TPU:0, one launch (start us, length us, event | category | flops | bytes accessed | tf_op | source)
XLA Modules:
  0.0 56.4 jit_solution(4550521175487528101)
XLA Ops:
  0.0 2.4 %copy.6 = bf16[128,6,2,256]{0,3,1,2:T(8,128)(2,1)S(1)} copy(bf16[128,6,2,256]{3,2,1,0:T(2,128)(2,1)} %param.6) | data formatting | bytes 1572864 | tf_op args[1]
  3.0 0.8 %fusion.54 = (f32[1,256,512]{2,0,1:T(1,128)S(1)}, f32[1,256,512]{2,0,1:T(1,128)S(1)}) fusion(f32[2,256,512]{2,0,1:T(2,128)S(1)} %bitcast.120), kind=kLoop, calls=%fused_computation.85 | loop fusion | bytes 2097152 | tf_op jit(solution)/shard_map/slice | solution.py:79
  3.9 4.2 %copy.22 = bf16[256,6,2,512]{3,0,1,2:T(8,128)(2,1)} copy(bf16[256,6,2,512]{3,2,1,0:T(2,128)(2,1)} %param.5) | data formatting | bytes 6291456 | tf_op args[0]
  8.1 1.5 %fusion.27 = f32[256,6,256]{2,0,1:T(8,128)} fusion(bf16[2,6,128,256]{2,3,1,0:T(8,128)(2,1)S(1)} %bitcast.112, bf16[256,256]{1,0:T(8,128)(2,1)S(1)} %copy-done.3, s32[]{:T(128)S(6)} %select_n.112), kind=kOutput, calls=%fused_computation.37 | convolution fusion | flops 100663296 | bytes 2031620 | tf_op jit(solution)/shard_map/rk,mkc->mrc/dot_general | solution.py:74
  10.0 3.6 %fusion.2 = f32[256,512]{1,0:T(8,128)} fusion(bf16[2,6,256,512]{3,2,1,0:T(8,128)(2,1)} %bitcast.116, f32[256,6,256]{2,0,1:T(8,128)} %fusion.27, bf16[2,6,128,256]{2,3,1,0:T(8,128)(2,1)} %collective-permute-done, bf16[512,256]{1,0:T(8,128)(2,1)S(1)} %copy-done, bf16[256,128]{1,0:T(8,128)(2,1)S(1)} %constant_dynamic-slice_fusion.1), kind=kOutput, calls=%fused_computation.6 | convolution fusion | flops 506331136 | bytes 4390912 | tf_op jit(solution)/shard_map/mrc,nc->mrn/dot_general | solution.py:77
  13.6 1.0 %dynamic-slice_convert_fusion = bf16[128,512]{1,0:T(8,128)(2,1)S(1)} fusion(f32[256,512]{1,0:T(8,128)} %fusion.2, s32[]{:T(128)S(6)} %select_n.115), kind=kLoop, calls=%fused_computation.45 | loop fusion | bytes 262148 | tf_op jit(solution)/shard_map/convert_element_type | solution.py:19
  14.6 2.7 %collective-permute-start.7 = (bf16[128,512]{1,0:T(8,128)(2,1)S(1)}, bf16[128,512]{1,0:T(8,128)(2,1)S(1)}, u32[]{:S(2)}, u32[]{:S(2)}) collective-permute-start(bf16[128,512]{1,0:T(8,128)(2,1)S(1)} %dynamic-slice_convert_fusion), channel_id=1, source_target_pairs={{0,4},{4,0},{8,12},{12,8},{1,5},{5,1},{9,13},{13,9},{2,6},{6,2},{1... | collective-permute-start | bytes 393224 | tf_op jit(solution)/shard_map/ppermute | solution.py:19
  17.3 3.2 %fusion = f32[256,512]{1,0:T(8,128)} fusion(bf16[2,6,256,512]{3,2,1,0:T(8,128)(2,1)} %bitcast.117, f32[256,6,256]{2,0,1:T(8,128)S(1)} %fusion.26, bf16[2,6,128,256]{2,3,1,0:T(8,128)(2,1)} %collective-permute-done, bf16[512,256]{1,0:T(8,128)(2,1)S(1)} %copy-done, bf16[256,128]{1,0:T(8,128)(2,1)S(1)} %constant_dynamic-slice_fusion.1), kind=kOutput, calls=%fused_computation.4 | convolution fusion | flops 506331136 | bytes 4390912 | tf_op jit(solution)/shard_map/mrc,nc->mrn/dot_general | solution.py:77
  20.5 1.0 %dynamic-slice_convert_fusion.1 = bf16[128,512]{1,0:T(8,128)(2,1)S(1)} fusion(f32[256,512]{1,0:T(8,128)} %fusion, s32[]{:T(128)S(6)} %select_n.115), kind=kLoop, calls=%fused_computation.47 | loop fusion | bytes 262148 | tf_op jit(solution)/shard_map/convert_element_type | solution.py:19
  21.5 1.0 %convert_add_fusion = f32[128,512]{1,0:T(8,128)S(1)} fusion(bf16[128,512]{1,0:T(8,128)(2,1)S(1)} %collective-permute-done.7, f32[256,512]{1,0:T(8,128)} %fusion.2, s32[]{:T(128)S(6)} %select_n.114), kind=kLoop, calls=%fused_computation.44 | loop fusion | flops 131072 | bytes 655364 | tf_op jit(solution)/shard_map/add | solution.py:20
  22.5 3.1 %collective-permute-start.8 = (bf16[64,512]{1,0:T(8,128)(2,1)S(1)}, bf16[64,512]{1,0:T(8,128)(2,1)S(1)}, u32[]{:S(2)}, u32[]{:S(2)}) collective-permute-start(bf16[64,512]{1,0:T(8,128)(2,1)S(1)} %dynamic-slice_convert_fusion.2), channel_id=1, source_target_pairs={{0,8},{4,12},{8,0},{12,4},{1,9},{5,13},{9,1},{13,5},{2,10},{6,14},... | collective-permute-start | bytes 196616 | tf_op jit(solution)/shard_map/ppermute | solution.py:19
  25.6 2.9 %collective-permute-done.1 = bf16[128,512]{1,0:T(8,128)(2,1)S(1)} collective-permute-done((bf16[128,512]{1,0:T(8,128)(2,1)S(1)}, bf16[128,512]{1,0:T(8,128)(2,1)S(1)}, u32[]{:S(2)}, u32[]{:S(2)}) %collective-permute-start.1) | collective-permute-done | bytes 131104 | tf_op jit(solution)/shard_map/ppermute | solution.py:19
  28.5 1.0 %convert_add_fusion.1 = f32[128,512]{1,0:T(8,128)S(1)} fusion(bf16[128,512]{1,0:T(8,128)(2,1)S(1)} %collective-permute-done.1, f32[256,512]{1,0:T(8,128)} %fusion, s32[]{:T(128)S(6)} %select_n.114), kind=kLoop, calls=%fused_computation.46 | loop fusion | flops 131072 | bytes 655364 | tf_op jit(solution)/shard_map/add | solution.py:20
  29.5 1.9 %collective-permute-start.2 = (bf16[64,512]{1,0:T(8,128)(2,1)S(1)}, bf16[64,512]{1,0:T(8,128)(2,1)S(1)}, u32[]{:S(2)}, u32[]{:S(2)}) collective-permute-start(bf16[64,512]{1,0:T(8,128)(2,1)S(1)} %dynamic-slice_convert_fusion.3), channel_id=1, source_target_pairs={{0,8},{4,12},{8,0},{12,4},{1,9},{5,13},{9,1},{13,5},{2,10},{6,14},... | collective-permute-start | bytes 196616 | tf_op jit(solution)/shard_map/ppermute | solution.py:19
  31.5 1.1 %collective-permute-start.9 = (bf16[64,512]{1,0:T(8,128)(2,1)S(1)}, bf16[64,512]{1,0:T(8,128)(2,1)S(1)}, u32[]{:S(2)}, u32[]{:S(2)}) collective-permute-start(bf16[64,512]{1,0:T(8,128)(2,1)S(1)} %fusion.32), channel_id=1, source_target_pairs={{0,8},{4,12},{8,0},{12,4},{1,9},{5,13},{9,1},{13,5},{2,10},{6,14},... | collective-permute-start | bytes 196616 | tf_op jit(solution)/shard_map/ppermute | solution.py:30
  32.6 4.7 %collective-permute-done.2 = bf16[64,512]{1,0:T(8,128)(2,1)S(1)} collective-permute-done((bf16[64,512]{1,0:T(8,128)(2,1)S(1)}, bf16[64,512]{1,0:T(8,128)(2,1)S(1)}, u32[]{:S(2)}, u32[]{:S(2)}) %collective-permute-start.2) | collective-permute-done | bytes 65568 | tf_op jit(solution)/shard_map/ppermute | solution.py:19
  37.4 1.2 %collective-permute-done.9 = bf16[64,512]{1,0:T(8,128)(2,1)S(1)} collective-permute-done((bf16[64,512]{1,0:T(8,128)(2,1)S(1)}, bf16[64,512]{1,0:T(8,128)(2,1)S(1)}, u32[]{:S(2)}, u32[]{:S(2)}) %collective-permute-start.9) | collective-permute-done | bytes 65568 | tf_op jit(solution)/shard_map/ppermute | solution.py:30
  38.8 3.9 %collective-permute-done.3 = bf16[64,512]{1,0:T(8,128)(2,1)S(1)} collective-permute-done((bf16[64,512]{1,0:T(8,128)(2,1)S(1)}, bf16[64,512]{1,0:T(8,128)(2,1)S(1)}, u32[]{:S(2)}, u32[]{:S(2)}) %collective-permute-start.3) | collective-permute-done | bytes 65568 | tf_op jit(solution)/shard_map/ppermute | solution.py:30
  42.8 2.1 %collective-permute-done.10 = bf16[128,512]{1,0:T(8,128)(2,1)S(1)} collective-permute-done((bf16[128,512]{1,0:T(8,128)(2,1)S(1)}, bf16[128,512]{1,0:T(8,128)(2,1)S(1)}, u32[]{:S(2)}, u32[]{:S(2)}) %collective-permute-start.10) | collective-permute-done | bytes 131104 | tf_op jit(solution)/shard_map/ppermute | solution.py:30
  44.9 2.8 %collective-permute-done.4 = bf16[128,512]{1,0:T(8,128)(2,1)S(1)} collective-permute-done((bf16[128,512]{1,0:T(8,128)(2,1)S(1)}, bf16[128,512]{1,0:T(8,128)(2,1)S(1)}, u32[]{:S(2)}, u32[]{:S(2)}) %collective-permute-start.4) | collective-permute-done | bytes 131104 | tf_op jit(solution)/shard_map/ppermute | solution.py:30
  47.9 2.1 %fusion.13 = bf16[6,256,256]{2,1,0:T(8,128)(2,1)S(1)} fusion(f32[256,512]{1,0:T(8,128)S(1)} %maximum_convert_fusion.1, bf16[2,6,256,512]{3,2,1,0:T(8,128)(2,1)} %bitcast.118, bf16[512,256]{1,0:T(8,128)(2,1)S(1)} %copy-done), kind=kOutput, calls=%fused_computation.18 | convolution fusion | flops 405405696 | bytes 3145728 | tf_op jit(solution)/shard_map/mrn,nc->mrc/dot_general | solution.py:87
  50.3 0.6 %fusion.10 = bf16[6,256,256]{2,1,0:T(8,128)(2,1)S(1)} fusion(f32[256,512]{1,0:T(8,128)S(1)} %maximum_convert_fusion, bf16[2,6,256,512]{3,2,1,0:T(8,128)(2,1)S(1)} %bitcast.119, bf16[512,256]{1,0:T(8,128)(2,1)S(1)} %copy-done), kind=kOutput, calls=%fused_computation.17 | convolution fusion | flops 405405696 | bytes 3145728 | tf_op jit(solution)/shard_map/mrn,nc->mrc/dot_general | solution.py:87
  52.3 1.4 %collective-permute-done.6 = bf16[256,128]{1,0:T(8,128)(2,1)S(1)} collective-permute-done((bf16[256,128]{1,0:T(8,128)(2,1)S(1)}, bf16[256,128]{1,0:T(8,128)(2,1)S(1)}, u32[]{:S(2)}, u32[]{:S(2)}) %collective-permute-start.6) | collective-permute-done | bytes 65568 | tf_op jit(solution)/shard_map/ppermute | solution.py:8
  54.6 1.8 %copy.12 = bf16[128,6,2,256]{3,2,1,0:T(2,128)(2,1)} copy(bf16[128,6,2,256]{0,3,1,2:T(8,128)(2,1)S(1)} %maximum_bitcast_fusion) | data formatting | bytes 1572864 | tf_op jit(solution)/shard_map/transpose | solution.py:95
  (41 shorter events, 4.0 us)
Async XLA Ops:
  0.0 10.0 %copy-start = (bf16[512,256]{1,0:T(8,128)(2,1)S(1)}, bf16[512,256]{1,0:T(8,128)(2,1)}, u32[]{:S(2)}) copy-start(bf16[512,256]{1,0:T(8,128)(2,1)} %param.9) | copy-start | bytes 786436
  0.0 3.0 %copy-start.2 = (f32[256,2,512]{2,1,0:T(2,128)S(1)}, f32[256,2,512]{2,1,0:T(2,128)}, u32[]{:S(2)}) copy-start(f32[256,2,512]{2,1,0:T(2,128)} %param.7) | copy-start | bytes 3145732
  0.0 3.8 %copy-start.3 = (bf16[256,256]{1,0:T(8,128)(2,1)S(1)}, bf16[256,256]{1,0:T(8,128)(2,1)}, u32[]{:S(2)}) copy-start(bf16[256,256]{1,0:T(8,128)(2,1)} %param.8) | copy-start | bytes 393220
  2.4 7.6 %collective-permute-start = (bf16[2,6,128,256]{2,3,1,0:T(8,128)(2,1)S(1)}, bf16[2,6,128,256]{2,3,1,0:T(8,128)(2,1)}, u32[]{:S(2)}, u32[]{:S(2)}) collective-permute-start(bf16[2,6,128,256]{2,3,1,0:T(8,128)(2,1)S(1)} %bitcast.111), channel_id=1, source_target_pairs={{0,1},{1,0},{2,3},{3,2},{4,5},{5,4},{6,7},{7,6},{8,9},{9,8},{10,11... | collective-permute-start | bytes 2359304 | tf_op jit(solution)/shard_map/ppermute | solution.py:8
  14.6 6.9 %collective-permute-start.7 = (bf16[128,512]{1,0:T(8,128)(2,1)S(1)}, bf16[128,512]{1,0:T(8,128)(2,1)S(1)}, u32[]{:S(2)}, u32[]{:S(2)}) collective-permute-start(bf16[128,512]{1,0:T(8,128)(2,1)S(1)} %dynamic-slice_convert_fusion), channel_id=1, source_target_pairs={{0,4},{4,0},{8,12},{12,8},{1,5},{5,1},{9,13},{13,9},{2,6},{6,2},{1... | collective-permute-start | bytes 393224 | tf_op jit(solution)/shard_map/ppermute | solution.py:19
  21.4 7.1 %collective-permute-start.1 = (bf16[128,512]{1,0:T(8,128)(2,1)S(1)}, bf16[128,512]{1,0:T(8,128)(2,1)S(1)}, u32[]{:S(2)}, u32[]{:S(2)}) collective-permute-start(bf16[128,512]{1,0:T(8,128)(2,1)S(1)} %dynamic-slice_convert_fusion.1), channel_id=1, source_target_pairs={{0,4},{4,0},{8,12},{12,8},{1,5},{5,1},{9,13},{13,9},{2,6},{6,2},{1... | collective-permute-start | bytes 393224 | tf_op jit(solution)/shard_map/ppermute | solution.py:19
  22.5 8.9 %collective-permute-start.8 = (bf16[64,512]{1,0:T(8,128)(2,1)S(1)}, bf16[64,512]{1,0:T(8,128)(2,1)S(1)}, u32[]{:S(2)}, u32[]{:S(2)}) collective-permute-start(bf16[64,512]{1,0:T(8,128)(2,1)S(1)} %dynamic-slice_convert_fusion.2), channel_id=1, source_target_pairs={{0,8},{4,12},{8,0},{12,4},{1,9},{5,13},{9,1},{13,5},{2,10},{6,14},... | collective-permute-start | bytes 196616 | tf_op jit(solution)/shard_map/ppermute | solution.py:19
  29.5 7.8 %collective-permute-start.2 = (bf16[64,512]{1,0:T(8,128)(2,1)S(1)}, bf16[64,512]{1,0:T(8,128)(2,1)S(1)}, u32[]{:S(2)}, u32[]{:S(2)}) collective-permute-start(bf16[64,512]{1,0:T(8,128)(2,1)S(1)} %dynamic-slice_convert_fusion.3), channel_id=1, source_target_pairs={{0,8},{4,12},{8,0},{12,4},{1,9},{5,13},{9,1},{13,5},{2,10},{6,14},... | collective-permute-start | bytes 196616 | tf_op jit(solution)/shard_map/ppermute | solution.py:19
  31.5 7.2 %collective-permute-start.9 = (bf16[64,512]{1,0:T(8,128)(2,1)S(1)}, bf16[64,512]{1,0:T(8,128)(2,1)S(1)}, u32[]{:S(2)}, u32[]{:S(2)}) collective-permute-start(bf16[64,512]{1,0:T(8,128)(2,1)S(1)} %fusion.32), channel_id=1, source_target_pairs={{0,8},{4,12},{8,0},{12,4},{1,9},{5,13},{9,1},{13,5},{2,10},{6,14},... | collective-permute-start | bytes 196616 | tf_op jit(solution)/shard_map/ppermute | solution.py:30
  37.4 5.3 %collective-permute-start.3 = (bf16[64,512]{1,0:T(8,128)(2,1)S(1)}, bf16[64,512]{1,0:T(8,128)(2,1)S(1)}, u32[]{:S(2)}, u32[]{:S(2)}) collective-permute-start(bf16[64,512]{1,0:T(8,128)(2,1)S(1)} %fusion.33), channel_id=1, source_target_pairs={{0,8},{4,12},{8,0},{12,4},{1,9},{5,13},{9,1},{13,5},{2,10},{6,14},... | collective-permute-start | bytes 196616 | tf_op jit(solution)/shard_map/ppermute | solution.py:30
  38.7 6.2 %collective-permute-start.10 = (bf16[128,512]{1,0:T(8,128)(2,1)S(1)}, bf16[128,512]{1,0:T(8,128)(2,1)S(1)}, u32[]{:S(2)}, u32[]{:S(2)}) collective-permute-start(bf16[128,512]{1,0:T(8,128)(2,1)S(1)} %pad_maximum_fusion.1), channel_id=1, source_target_pairs={{0,4},{4,0},{8,12},{12,8},{1,5},{5,1},{9,13},{13,9},{2,6},{6,2},{1... | collective-permute-start | bytes 393224 | tf_op jit(solution)/shard_map/ppermute | solution.py:30
  42.7 5.0 %collective-permute-start.4 = (bf16[128,512]{1,0:T(8,128)(2,1)S(1)}, bf16[128,512]{1,0:T(8,128)(2,1)S(1)}, u32[]{:S(2)}, u32[]{:S(2)}) collective-permute-start(bf16[128,512]{1,0:T(8,128)(2,1)S(1)} %pad_maximum_fusion), channel_id=1, source_target_pairs={{0,4},{4,0},{8,12},{12,8},{1,5},{5,1},{9,13},{13,9},{2,6},{6,2},{1... | collective-permute-start | bytes 393224 | tf_op jit(solution)/shard_map/ppermute | solution.py:30
  47.9 2.4 %copy-start.1 = (bf16[256,6,2,512]{3,0,1,2:T(8,128)(2,1)S(1)}, bf16[256,6,2,512]{3,0,1,2:T(8,128)(2,1)}, u32[]{:S(2)}) copy-start(bf16[256,6,2,512]{3,0,1,2:T(8,128)(2,1)} %copy.22) | copy-start | bytes 9437188
  50.1 3.6 %collective-permute-start.11 = (bf16[6,256,256]{2,1,0:T(8,128)(2,1)S(1)}, bf16[6,256,256]{2,1,0:T(8,128)(2,1)S(1)}, u32[]{:S(2)}, u32[]{:S(2)}) collective-permute-start(bf16[6,256,256]{2,1,0:T(8,128)(2,1)S(1)} %fusion.13), channel_id=1, source_target_pairs={{0,1},{1,0},{2,3},{3,2},{4,5},{5,4},{6,7},{7,6},{8,9},{9,8},{10,11... | collective-permute-start | bytes 2359304 | tf_op jit(solution)/shard_map/ppermute | solution.py:8
  50.9 3.2 %collective-permute-start.5 = (bf16[6,256,256]{2,1,0:T(8,128)(2,1)S(1)}, bf16[6,256,256]{2,1,0:T(8,128)(2,1)S(1)}, u32[]{:S(2)}, u32[]{:S(2)}) collective-permute-start(bf16[6,256,256]{2,1,0:T(8,128)(2,1)S(1)} %fusion.10), channel_id=1, source_target_pairs={{0,1},{1,0},{2,3},{3,2},{4,5},{5,4},{6,7},{7,6},{8,9},{9,8},{10,11... | collective-permute-start | bytes 2359304 | tf_op jit(solution)/shard_map/ppermute | solution.py:8
  51.4 2.3 %collective-permute-start.6 = (bf16[256,128]{1,0:T(8,128)(2,1)S(1)}, bf16[256,128]{1,0:T(8,128)(2,1)S(1)}, u32[]{:S(2)}, u32[]{:S(2)}) collective-permute-start(bf16[256,128]{1,0:T(8,128)(2,1)S(1)} %constant_dynamic-slice_fusion.1), channel_id=1, source_target_pairs={{0,1},{1,0},{2,3},{3,2},{4,5},{5,4},{6,7},{7,6},{8,9},{9,8},{10,11... | collective-permute-start | bytes 196616 | tf_op jit(solution)/shard_map/ppermute | solution.py:8

commit v4 on v3

--- a/solution.py
+++ b/solution.py
@@ -11,7 +11,7 @@
 def _reduce_scatter_rows(x, axis, size, wire):
     idx = lax.axis_index(axis)
     d = 1
-    while d < size:
+    while 2 * d < size:
         half = x.shape[0] // 2
         bit = (idx // d) % 2
         keep = lax.dynamic_slice_in_dim(x, bit * half, half, 0)
@@ -19,12 +19,15 @@
         recv = lax.ppermute(send.astype(wire), axis, [(i, i ^ d) for i in range(size)])
         x = keep + recv.astype(x.dtype)
         d *= 2
+    if d < size:
+        recv = lax.ppermute(x.astype(wire), axis, [(i, i ^ d) for i in range(size)])
+        x = x + recv.astype(x.dtype)
     return x
 
 
 def _all_gather_rows(x, axis, size):
     idx = lax.axis_index(axis)
-    d = size // 2
+    d = size // 4
     while d >= 1:
         bit = (idx // d) % 2
         recv = lax.ppermute(x, axis, [(i, i ^ d) for i in range(size)])
@@ -39,7 +42,7 @@
     idx = lax.axis_index(axis)
     start = 0
     d, span = 1, rows
-    while d < size:
+    while 2 * d < size:
         span //= 2
         start = start + ((idx // d) % 2) * span
         d *= 2
@@ -62,7 +65,7 @@
     rf_for_partner = _swap(rf_other, "half")
 
     pow2 = n_mem & (n_mem - 1) == 0 and rows % n_mem == 0
-    blk = rows // n_mem
+    blk = rows // max(n_mem // 2, 1)
     start = _block_start("mem", n_mem, rows) if pow2 else 0
 
     outs = []

time: 56.8 us -> 49.6 us (0.87)
  waiting for transfers between devices: 19.1 us -> 11.7 us
  matrix products: 13.1 us -> 11.5 us
  other arithmetic: 2.33 us -> 3.5 us
    ppermute x4 -> x2, waiting for transfers between devices: 10.1 us -> 4.04 us  [_all_gather_rows(): recv = lax.ppermute(x, axis, [(i, i ^ d) for i in range(size)])]
    ppermute x4 -> x2, starting transfers between devices: 7.77 us -> 2.74 us  [_reduce_scatter_rows(): lax.ppermute(send.astype(wire), axis, [(i, i ^ d) for i in range(size)])]
    ppermute x0 -> x2, starting transfers between devices: none -> 3.79 us  [_reduce_scatter_rows(): recv = lax.ppermute(x.astype(wire), axis, [(i, i ^ d) for i in range(size)])]
    ppermute x4 -> x2, waiting for transfers between devices: 7.6 us -> 4.19 us  [_reduce_scatter_rows(): lax.ppermute(send.astype(wire), axis, [(i, i ^ d) for i in range(size)])]
    ppermute x0 -> x2, waiting for transfers between devices: none -> 2.41 us  [_reduce_scatter_rows(): recv = lax.ppermute(x.astype(wire), axis, [(i, i ^ d) for i in range(size)])]
    convert_element_type x0 -> x2, other arithmetic: none -> 1.97 us  [_reduce_scatter_rows(): recv = lax.ppermute(x.astype(wire), axis, [(i, i ^ d) for i in range(size)])]
    add x2 -> x0, other arithmetic: 1.96 us -> none  [_reduce_scatter_rows(): x = keep + recv.astype(x.dtype)]
    ppermute x4 -> x2, starting transfers between devices: 1.34 us -> 3.24 us  [_all_gather_rows(): recv = lax.ppermute(x, axis, [(i, i ^ d) for i in range(size)])]
  transfers between devices with their start and end apart: 12 -> 10, of which waited for: 7 -> 5; matrix products, arithmetic and copies ran while one was open for 27% -> 34% of each run, Pallas kernels for 0% -> 0%
where the time goes in v4:
time: 49.6 us; the launch traced here: 49.3 us
  waiting for transfers between devices  11.7 us (24%)
  local copies, waits for them, and re-layouts  11.5 us (23%)
  matrix products  11.5 us (23%)
  starting transfers between devices  10.8 us (22%)
  other arithmetic  3.5 us (7%)
    dot_general x2, matrix products, local(): jnp.einsum('mrc,nc->mrn', expanded, col_factor, preferred_element_type=jn...  6.83 us
    unnamed x16, local copies, waits for them, and re-layouts  6.82 us
    ppermute x2, waiting for transfers between devices, _reduce_scatter_rows(): lax.ppermute(send.astype(wire), axis, [(i, i ^ d) for i in range(size)])  4.19 us
    ppermute x2, waiting for transfers between devices, _all_gather_rows(): recv = lax.ppermute(x, axis, [(i, i ^ d) for i in range(size)])  4.04 us
    ppermute x2, starting transfers between devices, _reduce_scatter_rows(): recv = lax.ppermute(x.astype(wire), axis, [(i, i ^ d) for i in range(size)])  3.79 us
    ppermute x2, starting transfers between devices, _all_gather_rows(): recv = lax.ppermute(x, axis, [(i, i ^ d) for i in range(size)])  3.24 us
    ppermute x2, starting transfers between devices, _reduce_scatter_rows(): lax.ppermute(send.astype(wire), axis, [(i, i ^ d) for i in range(size)])  2.74 us
    ppermute x2, waiting for transfers between devices, _reduce_scatter_rows(): recv = lax.ppermute(x.astype(wire), axis, [(i, i ^ d) for i in range(size)])  2.41 us
  transfers between devices with their start and end apart: 10, of which 5 were waited for; matrix products, arithmetic and copies ran while one was open for 34% of the time, Pallas kernels for 0%

profile of v4, /device:TPU:0, one launch (start us, length us, event | category | flops | bytes accessed | tf_op | source)
XLA Modules:
  0.0 49.3 jit_solution(1337379654136534514)
XLA Ops:
  0.0 2.4 %copy.6 = bf16[128,6,2,256]{0,3,1,2:T(8,128)(2,1)S(1)} copy(bf16[128,6,2,256]{3,2,1,0:T(2,128)(2,1)} %param.6) | data formatting | bytes 1572864 | tf_op args[1]
  3.0 0.8 %fusion.56 = (f32[1,256,512]{2,0,1:T(1,128)S(1)}, f32[1,256,512]{2,0,1:T(1,128)S(1)}) fusion(f32[2,256,512]{2,0,1:T(2,128)S(1)} %bitcast.120), kind=kLoop, calls=%fused_computation.79 | loop fusion | bytes 2097152 | tf_op jit(solution)/shard_map/slice | solution.py:82
  3.9 4.2 %copy.22 = bf16[256,6,2,512]{3,0,1,2:T(8,128)(2,1)} copy(bf16[256,6,2,512]{3,2,1,0:T(2,128)(2,1)} %param.5) | data formatting | bytes 6291456 | tf_op args[0]
  8.1 1.5 %fusion.27 = f32[256,6,256]{2,0,1:T(8,128)} fusion(bf16[2,6,128,256]{2,3,1,0:T(8,128)(2,1)S(1)} %bitcast.112, bf16[256,256]{1,0:T(8,128)(2,1)S(1)} %copy-done.3, s32[]{:T(128)S(6)} %select_n.60), kind=kOutput, calls=%fused_computation.37 | convolution fusion | flops 100663296 | bytes 2031620 | tf_op jit(solution)/shard_map/rk,mkc->mrc/dot_general | solution.py:77
  10.0 3.6 %fusion.2 = f32[256,512]{1,0:T(8,128)} fusion(bf16[2,6,256,512]{3,2,1,0:T(8,128)(2,1)} %bitcast.116, f32[256,6,256]{2,0,1:T(8,128)} %fusion.27, bf16[2,6,128,256]{2,3,1,0:T(8,128)(2,1)} %collective-permute-done, bf16[512,256]{1,0:T(8,128)(2,1)S(1)} %copy-done, bf16[256,128]{1,0:T(8,128)(2,1)S(1)} %constant_dynamic-slice_fusion.1), kind=kOutput, calls=%fused_computation.6 | convolution fusion | flops 506331136 | bytes 4390912 | tf_op jit(solution)/shard_map/mrc,nc->mrn/dot_general | solution.py:80
  13.7 1.0 %dynamic-slice_convert_fusion = bf16[128,512]{1,0:T(8,128)(2,1)S(1)} fusion(f32[256,512]{1,0:T(8,128)} %fusion.2, s32[]{:T(128)S(6)} %select_n.62), kind=kLoop, calls=%fused_computation.49 | loop fusion | bytes 262148 | tf_op jit(solution)/shard_map/convert_element_type | solution.py:19
  14.6 2.7 %collective-permute-start.6 = (bf16[128,512]{1,0:T(8,128)(2,1)S(1)}, bf16[128,512]{1,0:T(8,128)(2,1)S(1)}, u32[]{:S(2)}, u32[]{:S(2)}) collective-permute-start(bf16[128,512]{1,0:T(8,128)(2,1)S(1)} %dynamic-slice_convert_fusion), channel_id=1, source_target_pairs={{0,4},{4,0},{8,12},{12,8},{1,5},{5,1},{9,13},{13,9},{2,6},{6,2},{1... | collective-permute-start | bytes 393224 | tf_op jit(solution)/shard_map/ppermute | solution.py:19
  17.3 3.2 %fusion = f32[256,512]{1,0:T(8,128)} fusion(bf16[2,6,256,512]{3,2,1,0:T(8,128)(2,1)} %bitcast.117, f32[256,6,256]{2,0,1:T(8,128)S(1)} %fusion.26, bf16[2,6,128,256]{2,3,1,0:T(8,128)(2,1)} %collective-permute-done, bf16[512,256]{1,0:T(8,128)(2,1)S(1)} %copy-done, bf16[256,128]{1,0:T(8,128)(2,1)} %copy-done.5), kind=kOutput, calls=%fused_computation.4 | convolution fusion | flops 506331136 | bytes 4390912 | tf_op jit(solution)/shard_map/mrc,nc->mrn/dot_general | solution.py:80
  20.5 1.0 %dynamic-slice_convert_fusion.1 = bf16[128,512]{1,0:T(8,128)(2,1)S(1)} fusion(f32[256,512]{1,0:T(8,128)} %fusion, s32[]{:T(128)S(6)} %select_n.62), kind=kLoop, calls=%fused_computation.51 | loop fusion | bytes 262148 | tf_op jit(solution)/shard_map/convert_element_type | solution.py:19
  21.6 1.0 %fusion.35 = bf16[128,512]{1,0:T(8,128)(2,1)S(1)} fusion(bf16[128,512]{1,0:T(8,128)(2,1)S(1)} %collective-permute-done.6, f32[256,512]{1,0:T(8,128)} %fusion.2, s32[]{:T(128)S(6)} %select_n.59), kind=kLoop, calls=%fused_computation.53 | loop fusion | flops 196608 | bytes 524292 | tf_op jit(solution)/shard_map/convert_element_type | solution.py:23
  22.6 3.1 %collective-permute-start.7 = (bf16[128,512]{1,0:T(8,128)(2,1)S(1)}, bf16[128,512]{1,0:T(8,128)(2,1)S(1)}, u32[]{:S(2)}, u32[]{:S(2)}) collective-permute-start(bf16[128,512]{1,0:T(8,128)(2,1)S(1)} %fusion.35), channel_id=1, source_target_pairs={{0,8},{4,12},{8,0},{12,4},{1,9},{5,13},{9,1},{13,5},{2,10},{6,14},... | collective-permute-start | bytes 393224 | tf_op jit(solution)/shard_map/ppermute | solution.py:23
  25.7 4.2 %collective-permute-done.1 = bf16[128,512]{1,0:T(8,128)(2,1)S(1)} collective-permute-done((bf16[128,512]{1,0:T(8,128)(2,1)S(1)}, bf16[128,512]{1,0:T(8,128)(2,1)S(1)}, u32[]{:S(2)}, u32[]{:S(2)}) %collective-permute-start.1) | collective-permute-done | bytes 131104 | tf_op jit(solution)/shard_map/ppermute | solution.py:19
  29.9 1.0 %fusion.34 = bf16[128,512]{1,0:T(8,128)(2,1)S(1)} fusion(bf16[128,512]{1,0:T(8,128)(2,1)S(1)} %collective-permute-done.1, f32[256,512]{1,0:T(8,128)} %fusion, s32[]{:T(128)S(6)} %select_n.59), kind=kLoop, calls=%fused_computation.52 | loop fusion | flops 196608 | bytes 524292 | tf_op jit(solution)/shard_map/convert_element_type | solution.py:23
  30.9 0.7 %collective-permute-start.2 = (bf16[128,512]{1,0:T(8,128)(2,1)S(1)}, bf16[128,512]{1,0:T(8,128)(2,1)S(1)}, u32[]{:S(2)}, u32[]{:S(2)}) collective-permute-start(bf16[128,512]{1,0:T(8,128)(2,1)S(1)} %fusion.34), channel_id=1, source_target_pairs={{0,8},{4,12},{8,0},{12,4},{1,9},{5,13},{9,1},{13,5},{2,10},{6,14},... | collective-permute-start | bytes 393224 | tf_op jit(solution)/shard_map/ppermute | solution.py:23
  31.6 1.2 %fusion.28 = bf16[128,512]{1,0:T(8,128)(2,1)S(1)} fusion(f32[1,128,512]{2,0,1:T(1,128)S(1)} %constant_dynamic-slice_fusion, bf16[128,512]{1,0:T(8,128)(2,1)S(1)} %collective-permute-done.7, bf16[128,512]{1,0:T(8,128)(2,1)S(1)} %collective-permute-done.6, f32[256,512]{1,0:T(8,128)} %fusion.2, s32[]{:T(128)S(6)} %select_n.59), kind=kLoop, calls=%fused_computation.41 | loop fusion | flops 393216 | bytes 917508 | tf_op jit(solution)/shard_map/convert_element_type | solution.py:85
  32.8 2.6 %collective-permute-start.8 = (bf16[128,512]{1,0:T(8,128)(2,1)S(1)}, bf16[128,512]{1,0:T(8,128)(2,1)S(1)}, u32[]{:S(2)}, u32[]{:S(2)}) collective-permute-start(bf16[128,512]{1,0:T(8,128)(2,1)S(1)} %fusion.28), channel_id=1, source_target_pairs={{0,4},{4,0},{8,12},{12,8},{1,5},{5,1},{9,13},{13,9},{2,6},{6,2},{1... | collective-permute-start | bytes 393224 | tf_op jit(solution)/shard_map/ppermute | solution.py:33
  35.4 2.4 %collective-permute-done.2 = bf16[128,512]{1,0:T(8,128)(2,1)S(1)} collective-permute-done((bf16[128,512]{1,0:T(8,128)(2,1)S(1)}, bf16[128,512]{1,0:T(8,128)(2,1)S(1)}, u32[]{:S(2)}, u32[]{:S(2)}) %collective-permute-start.2) | collective-permute-done | bytes 131104 | tf_op jit(solution)/shard_map/ppermute | solution.py:23
  37.9 0.6 %collective-permute-start.3 = (bf16[128,512]{1,0:T(8,128)(2,1)S(1)}, bf16[128,512]{1,0:T(8,128)(2,1)S(1)}, u32[]{:S(2)}, u32[]{:S(2)}) collective-permute-start(bf16[128,512]{1,0:T(8,128)(2,1)S(1)} %fusion.29), channel_id=1, source_target_pairs={{0,4},{4,0},{8,12},{12,8},{1,5},{5,1},{9,13},{13,9},{2,6},{6,2},{1... | collective-permute-start | bytes 393224 | tf_op jit(solution)/shard_map/ppermute | solution.py:33
  38.6 2.1 %collective-permute-done.8 = bf16[128,512]{1,0:T(8,128)(2,1)S(1)} collective-permute-done((bf16[128,512]{1,0:T(8,128)(2,1)S(1)}, bf16[128,512]{1,0:T(8,128)(2,1)S(1)}, u32[]{:S(2)}, u32[]{:S(2)}) %collective-permute-start.8) | collective-permute-done | bytes 131104 | tf_op jit(solution)/shard_map/ppermute | solution.py:33
  40.7 0.6 %fusion.13 = bf16[6,256,256]{2,1,0:T(8,128)(2,1)S(1)} fusion(f32[256,512]{1,0:T(8,128)S(1)} %maximum_convert_fusion.1, bf16[2,6,256,512]{3,2,1,0:T(8,128)(2,1)S(1)} %bitcast.118, bf16[512,256]{1,0:T(8,128)(2,1)S(1)} %copy-done), kind=kOutput, calls=%fused_computation.18 | convolution fusion | flops 405405696 | bytes 3145728 | tf_op jit(solution)/shard_map/mrn,nc->mrc/dot_general | solution.py:90
  41.4 2.0 %collective-permute-done.3 = bf16[128,512]{1,0:T(8,128)(2,1)S(1)} collective-permute-done((bf16[128,512]{1,0:T(8,128)(2,1)S(1)}, bf16[128,512]{1,0:T(8,128)(2,1)S(1)}, u32[]{:S(2)}, u32[]{:S(2)}) %collective-permute-start.3) | collective-permute-done | bytes 131104 | tf_op jit(solution)/shard_map/ppermute | solution.py:33
  43.5 0.6 %fusion.10 = bf16[6,256,256]{2,1,0:T(8,128)(2,1)S(1)} fusion(f32[256,512]{1,0:T(8,128)S(1)} %maximum_convert_fusion, bf16[2,6,256,512]{3,2,1,0:T(8,128)(2,1)S(1)} %bitcast.119, bf16[512,256]{1,0:T(8,128)(2,1)S(1)} %copy-done), kind=kOutput, calls=%fused_computation.17 | convolution fusion | flops 405405696 | bytes 3145728 | tf_op jit(solution)/shard_map/mrn,nc->mrc/dot_general | solution.py:90
  45.5 1.0 %collective-permute-done.5 = bf16[256,128]{1,0:T(8,128)(2,1)S(1)} collective-permute-done((bf16[256,128]{1,0:T(8,128)(2,1)S(1)}, bf16[256,128]{1,0:T(8,128)(2,1)S(1)}, u32[]{:S(2)}, u32[]{:S(2)}) %collective-permute-start.5) | collective-permute-done | bytes 65568 | tf_op jit(solution)/shard_map/ppermute | solution.py:8
  47.4 1.8 %copy.12 = bf16[128,6,2,256]{3,2,1,0:T(2,128)(2,1)} copy(bf16[128,6,2,256]{0,3,1,2:T(8,128)(2,1)S(1)} %maximum_bitcast_fusion) | data formatting | bytes 1572864 | tf_op jit(solution)/shard_map/transpose | solution.py:98
  (38 shorter events, 3.7 us)
Async XLA Ops:
  0.0 10.0 %copy-start = (bf16[512,256]{1,0:T(8,128)(2,1)S(1)}, bf16[512,256]{1,0:T(8,128)(2,1)}, u32[]{:S(2)}) copy-start(bf16[512,256]{1,0:T(8,128)(2,1)} %param.9) | copy-start | bytes 786436
  0.0 3.0 %copy-start.2 = (f32[256,2,512]{2,1,0:T(2,128)S(1)}, f32[256,2,512]{2,1,0:T(2,128)}, u32[]{:S(2)}) copy-start(f32[256,2,512]{2,1,0:T(2,128)} %param.7) | copy-start | bytes 3145732
  0.0 3.8 %copy-start.3 = (bf16[256,256]{1,0:T(8,128)(2,1)S(1)}, bf16[256,256]{1,0:T(8,128)(2,1)}, u32[]{:S(2)}) copy-start(bf16[256,256]{1,0:T(8,128)(2,1)} %param.8) | copy-start | bytes 393220
  2.4 7.6 %collective-permute-start = (bf16[2,6,128,256]{2,3,1,0:T(8,128)(2,1)S(1)}, bf16[2,6,128,256]{2,3,1,0:T(8,128)(2,1)}, u32[]{:S(2)}, u32[]{:S(2)}) collective-permute-start(bf16[2,6,128,256]{2,3,1,0:T(8,128)(2,1)S(1)} %bitcast.111), channel_id=1, source_target_pairs={{0,1},{1,0},{2,3},{3,2},{4,5},{5,4},{6,7},{7,6},{8,9},{9,8},{10,11... | collective-permute-start | bytes 2359304 | tf_op jit(solution)/shard_map/ppermute | solution.py:8
  3.8 6.2 %copy-start.5 = (bf16[256,128]{1,0:T(8,128)(2,1)}, bf16[256,128]{1,0:T(8,128)(2,1)S(1)}, u32[]{:S(2)}) copy-start(bf16[256,128]{1,0:T(8,128)(2,1)S(1)} %constant_dynamic-slice_fusion.1) | copy-start | bytes 196612
  14.6 7.0 %collective-permute-start.6 = (bf16[128,512]{1,0:T(8,128)(2,1)S(1)}, bf16[128,512]{1,0:T(8,128)(2,1)S(1)}, u32[]{:S(2)}, u32[]{:S(2)}) collective-permute-start(bf16[128,512]{1,0:T(8,128)(2,1)S(1)} %dynamic-slice_convert_fusion), channel_id=1, source_target_pairs={{0,4},{4,0},{8,12},{12,8},{1,5},{5,1},{9,13},{13,9},{2,6},{6,2},{1... | collective-permute-start | bytes 393224 | tf_op jit(solution)/shard_map/ppermute | solution.py:19
  20.5 17.4 %copy-start.4 = (f32[256,512]{1,0:T(8,128)S(1)}, f32[256,512]{1,0:T(8,128)}, u32[]{:S(2)}) copy-start(f32[256,512]{1,0:T(8,128)} %fusion) | copy-start | bytes 1572868
  21.5 8.3 %collective-permute-start.1 = (bf16[128,512]{1,0:T(8,128)(2,1)S(1)}, bf16[128,512]{1,0:T(8,128)(2,1)S(1)}, u32[]{:S(2)}, u32[]{:S(2)}) collective-permute-start(bf16[128,512]{1,0:T(8,128)(2,1)S(1)} %dynamic-slice_convert_fusion.1), channel_id=1, source_target_pairs={{0,4},{4,0},{8,12},{12,8},{1,5},{5,1},{9,13},{13,9},{2,6},{6,2},{1... | collective-permute-start | bytes 393224 | tf_op jit(solution)/shard_map/ppermute | solution.py:19
  22.6 9.0 %collective-permute-start.7 = (bf16[128,512]{1,0:T(8,128)(2,1)S(1)}, bf16[128,512]{1,0:T(8,128)(2,1)S(1)}, u32[]{:S(2)}, u32[]{:S(2)}) collective-permute-start(bf16[128,512]{1,0:T(8,128)(2,1)S(1)} %fusion.35), channel_id=1, source_target_pairs={{0,8},{4,12},{8,0},{12,4},{1,9},{5,13},{9,1},{13,5},{2,10},{6,14},... | collective-permute-start | bytes 393224 | tf_op jit(solution)/shard_map/ppermute | solution.py:23
  30.9 9.8 %copy-start.1 = (bf16[256,6,2,512]{3,0,1,2:T(8,128)(2,1)S(1)}, bf16[256,6,2,512]{3,0,1,2:T(8,128)(2,1)}, u32[]{:S(2)}) copy-start(bf16[256,6,2,512]{3,0,1,2:T(8,128)(2,1)} %copy.22) | copy-start | bytes 9437188
  30.9 7.0 %collective-permute-start.2 = (bf16[128,512]{1,0:T(8,128)(2,1)S(1)}, bf16[128,512]{1,0:T(8,128)(2,1)S(1)}, u32[]{:S(2)}, u32[]{:S(2)}) collective-permute-start(bf16[128,512]{1,0:T(8,128)(2,1)S(1)} %fusion.34), channel_id=1, source_target_pairs={{0,8},{4,12},{8,0},{12,4},{1,9},{5,13},{9,1},{13,5},{2,10},{6,14},... | collective-permute-start | bytes 393224 | tf_op jit(solution)/shard_map/ppermute | solution.py:23
  32.8 7.8 %collective-permute-start.8 = (bf16[128,512]{1,0:T(8,128)(2,1)S(1)}, bf16[128,512]{1,0:T(8,128)(2,1)S(1)}, u32[]{:S(2)}, u32[]{:S(2)}) collective-permute-start(bf16[128,512]{1,0:T(8,128)(2,1)S(1)} %fusion.28), channel_id=1, source_target_pairs={{0,4},{4,0},{8,12},{12,8},{1,5},{5,1},{9,13},{13,9},{2,6},{6,2},{1... | collective-permute-start | bytes 393224 | tf_op jit(solution)/shard_map/ppermute | solution.py:33
  37.9 5.4 %collective-permute-start.3 = (bf16[128,512]{1,0:T(8,128)(2,1)S(1)}, bf16[128,512]{1,0:T(8,128)(2,1)S(1)}, u32[]{:S(2)}, u32[]{:S(2)}) collective-permute-start(bf16[128,512]{1,0:T(8,128)(2,1)S(1)} %fusion.29), channel_id=1, source_target_pairs={{0,4},{4,0},{8,12},{12,8},{1,5},{5,1},{9,13},{13,9},{2,6},{6,2},{1... | collective-permute-start | bytes 393224 | tf_op jit(solution)/shard_map/ppermute | solution.py:33
  41.3 5.2 %collective-permute-start.9 = (bf16[6,256,256]{2,1,0:T(8,128)(2,1)S(1)}, bf16[6,256,256]{2,1,0:T(8,128)(2,1)S(1)}, u32[]{:S(2)}, u32[]{:S(2)}) collective-permute-start(bf16[6,256,256]{2,1,0:T(8,128)(2,1)S(1)} %fusion.13), channel_id=1, source_target_pairs={{0,1},{1,0},{2,3},{3,2},{4,5},{5,4},{6,7},{7,6},{8,9},{9,8},{10,11... | collective-permute-start | bytes 2359304 | tf_op jit(solution)/shard_map/ppermute | solution.py:8
  43.5 0.8 %copy-start.6 = (bf16[256,128]{1,0:T(8,128)(2,1)S(1)}, bf16[256,128]{1,0:T(8,128)(2,1)}, u32[]{:S(2)}) copy-start(bf16[256,128]{1,0:T(8,128)(2,1)} %copy-done.5) | copy-start | bytes 196612
  44.0 2.9 %collective-permute-start.4 = (bf16[6,256,256]{2,1,0:T(8,128)(2,1)S(1)}, bf16[6,256,256]{2,1,0:T(8,128)(2,1)S(1)}, u32[]{:S(2)}, u32[]{:S(2)}) collective-permute-start(bf16[6,256,256]{2,1,0:T(8,128)(2,1)S(1)} %fusion.10), channel_id=1, source_target_pairs={{0,1},{1,0},{2,3},{3,2},{4,5},{5,4},{6,7},{7,6},{8,9},{9,8},{10,11... | collective-permute-start | bytes 2359304 | tf_op jit(solution)/shard_map/ppermute | solution.py:8
  44.3 2.2 %collective-permute-start.5 = (bf16[256,128]{1,0:T(8,128)(2,1)S(1)}, bf16[256,128]{1,0:T(8,128)(2,1)S(1)}, u32[]{:S(2)}, u32[]{:S(2)}) collective-permute-start(bf16[256,128]{1,0:T(8,128)(2,1)S(1)} %copy-done.6), channel_id=1, source_target_pairs={{0,1},{1,0},{2,3},{3,2},{4,5},{5,4},{6,7},{7,6},{8,9},{9,8},{10,11... | collective-permute-start | bytes 196616 | tf_op jit(solution)/shard_map/ppermute | solution.py:8

commit v5 on v4

--- a/solution.py
+++ b/solution.py
@@ -55,11 +55,6 @@
     rows = anomalies.shape[0]
     n_lev = anomalies.shape[2]
 
-    anom_t = jnp.transpose(anomalies, (2, 1, 0, 3))
-    ctrl_t = jnp.transpose(control, (2, 1, 0, 3))
-    prec_t = jnp.transpose(precision, (1, 0, 2))
-
-    ctrl_other = _swap(ctrl_t, "half")
     rf_own = lax.dynamic_slice_in_dim(row_factor, h * kh, kh, 1)
     rf_other = lax.dynamic_slice_in_dim(row_factor, (1 - h) * kh, kh, 1)
     rf_for_partner = _swap(rf_other, "half")
@@ -70,16 +65,16 @@
 
     outs = []
     for l in range(n_lev):
-        a = anom_t[l]
-        c_own = ctrl_t[l]
-        c_oth = ctrl_other[l]
+        a = jnp.transpose(anomalies[:, :, l, :], (1, 0, 2))
+        c_own = jnp.transpose(control[:, :, l, :], (1, 0, 2))
+        c_oth = _swap(c_own, "half")
         expanded = (
             jnp.einsum("rk,mkc->mrc", rf_own, c_own, preferred_element_type=jnp.float32)
             + jnp.einsum("rk,mkc->mrc", rf_other, c_oth, preferred_element_type=jnp.float32)
         ).astype(jnp.bfloat16)
         fields = jnp.einsum("mrc,nc->mrn", expanded, col_factor, preferred_element_type=jnp.float32)
         inc = jnp.sum(a.astype(jnp.float32) * fields, axis=0)
-        prec = prec_t[l]
+        prec = precision[:, l, :]
         if pow2:
             part = _reduce_scatter_rows(inc, "mem", n_mem, jnp.bfloat16)
             w_blk = (lax.dynamic_slice_in_dim(prec, start, blk, 0) * part).astype(jnp.bfloat16)
@@ -94,8 +89,8 @@
         summed = jnp.einsum(
             "rk,mrc->mkc", rf_own, projected, preferred_element_type=jnp.float32
         ) + jnp.einsum("rk,mrc->mkc", rf_for_partner, proj_other, preferred_element_type=jnp.float32)
-        outs.append((c_own.astype(jnp.float32) + summed).astype(jnp.bfloat16))
-    return jnp.transpose(jnp.stack(outs, axis=0), (2, 1, 0, 3))
+        outs.append(control[:, :, l, :].astype(jnp.float32) + jnp.transpose(summed, (1, 0, 2)))
+    return jnp.stack(outs, axis=2).astype(jnp.bfloat16)
 
 
 def solution(mesh):

time: 49.6 us -> 64.9 us (1.31)
  local copies, waits for them, and re-layouts: 11.5 us -> 19.7 us
  matrix products: 11.5 us -> 18.2 us
  other arithmetic: 3.5 us -> 4.53 us
    slice x1 -> x3, local copies, waits for them, and re-layouts: 0.81 us -> 9.8 us  [the longest x1 6.09 us: local(): a = jnp.transpose(anomalies[:, :, l, :], (1, 0, 2))]
    unnamed x16 -> x25, local copies, waits for them, and re-layouts: 6.82 us -> 3.4 us
    dot_general x2, matrix products: 1.89 us -> 5.24 us  [local(): jnp.einsum('rk,mkc->mrc', rf_own, c_own, preferred_element_type=jnp.float32)]
    dot_general x2, matrix products: 0.84 us -> 2.82 us  [local(): jnp.einsum('rk,mrc->mkc', rf_for_partner, proj_other, preferred_element_t...]
    transpose x1 -> x0, local copies, waits for them, and re-layouts: 1.81 us -> none  [local(): return jnp.transpose(jnp.stack(outs, axis=0), (2, 1, 0, 3))]
    ppermute x2, starting transfers between devices: 3.24 us -> 1.47 us  [_all_gather_rows(): recv = lax.ppermute(x, axis, [(i, i ^ d) for i in range(size)])]
    another operation x0 -> x1, local copies, waits for them, and re-layouts: none -> 1.69 us  [local(): return jnp.stack(outs, axis=2).astype(jnp.bfloat16)]
    ppermute x2, waiting for transfers between devices: 2.41 us -> 3.88 us  [_reduce_scatter_rows(): recv = lax.ppermute(x.astype(wire), axis, [(i, i ^ d) for i in range(size)])]
  transfers between devices with their start and end apart: 10 -> 11, of which waited for: 5 -> 6; matrix products, arithmetic and copies ran while one was open for 34% -> 55% of each run, Pallas kernels for 0% -> 0%
where the time goes in v5:
time: 64.9 us; the launch traced here: 64.5 us
  local copies, waits for them, and re-layouts  19.7 us (30%)
  matrix products  18.2 us (28%)
  waiting for transfers between devices  11.4 us (18%)
  starting transfers between devices  10.5 us (16%)
  other arithmetic  4.53 us (7%)
    dot_general x2, matrix products, local(): jnp.einsum('mrc,nc->mrn', expanded, col_factor, preferred_element_type=jn...  8.02 us
    slice x1, local copies, waits for them, and re-layouts, local(): a = jnp.transpose(anomalies[:, :, l, :], (1, 0, 2))  6.09 us
    dot_general x2, matrix products, local(): jnp.einsum('rk,mkc->mrc', rf_own, c_own, preferred_element_type=jnp.float32)  5.24 us
    ppermute x2, starting transfers between devices, _reduce_scatter_rows(): recv = lax.ppermute(x.astype(wire), axis, [(i, i ^ d) for i in range(size)])  4.85 us
    ppermute x2, waiting for transfers between devices, _reduce_scatter_rows(): recv = lax.ppermute(x.astype(wire), axis, [(i, i ^ d) for i in range(size)])  3.88 us
    ppermute x2, waiting for transfers between devices, _all_gather_rows(): recv = lax.ppermute(x, axis, [(i, i ^ d) for i in range(size)])  3.85 us
    unnamed x25, local copies, waits for them, and re-layouts  3.4 us
    ppermute x2, waiting for transfers between devices, _reduce_scatter_rows(): lax.ppermute(send.astype(wire), axis, [(i, i ^ d) for i in range(size)])  3.12 us
  transfers between devices with their start and end apart: 11, of which 6 were waited for; matrix products, arithmetic and copies ran while one was open for 55% of the time, Pallas kernels for 0%

profile of v5, /device:TPU:0, one launch (start us, length us, event | category | flops | bytes accessed | tf_op | source)
XLA Modules:
  0.0 64.5 jit_solution(10564656476974775823)
XLA Ops:
  0.0 2.9 %fusion.62 = (bf16[128,6,1,256]{3,2,1,0:T(2,128)(2,1)S(1)}, bf16[128,6,1,256]{3,2,1,0:T(2,128)(2,1)S(1)}) fusion(bf16[128,6,2,256]{3,2,1,0:T(2,128)(2,1)} %param.6), kind=kLoop, calls=%fused_computation.80 | loop fusion | bytes 1572864 | tf_op jit(solution)/shard_map/slice | solution.py:92
  5.2 6.1 %fusion.60 = (bf16[256,6,1,512]{3,2,1,0:T(2,128)(2,1)}, bf16[256,6,1,512]{3,2,1,0:T(2,128)(2,1)}) fusion(bf16[256,6,2,512]{3,2,1,0:T(2,128)(2,1)S(1)} %copy-done.1), kind=kLoop, calls=%fused_computation.78 | loop fusion | bytes 6291456 | tf_op jit(solution)/shard_map/slice | solution.py:68
  12.1 2.6 %fusion.42 = f32[256,6,256]{2,0,1:T(8,128)} fusion(bf16[6,128,256]{2,1,0:T(8,128)(2,1)} %bitcast.121, bf16[256,256]{1,0:T(8,128)(2,1)S(1)} %copy-done.10, s32[]{:T(128)S(6)} %select_n.57), kind=kOutput, calls=%fused_computation.59 | convolution fusion | flops 100663296 | bytes 2031620 | tf_op jit(solution)/shard_map/rk,mkc->mrc/dot_general | solution.py:72
  16.8 2.6 %fusion.38 = f32[256,6,256]{2,0,1:T(8,128)} fusion(bf16[6,128,256]{2,1,0:T(8,128)(2,1)} %bitcast.120, bf16[256,256]{1,0:T(8,128)(2,1)S(1)} %copy-done.10, s32[]{:T(128)S(6)} %select_n.57), kind=kOutput, calls=%fused_computation.55 | convolution fusion | flops 100663296 | bytes 2031620 | tf_op jit(solution)/shard_map/rk,mkc->mrc/dot_general | solution.py:72
  19.4 4.5 %fusion.6 = f32[256,512]{1,0:T(8,128)} fusion(f32[256,6,256]{2,0,1:T(8,128)} %fusion.42, bf16[6,128,256]{2,1,0:T(8,128)(2,1)} %collective-permute-done, bf16[256,6,1,512]{3,2,1,0:T(2,128)(2,1)} %get-tuple-element.5, bf16[512,256]{1,0:T(8,128)(2,1)S(1)} %copy-done, bf16[256,128]{1,0:T(8,128)(2,1)} %constant_dynamic-slice_fusion.1), kind=kOutput, calls=%fused_computation.8 | convolution fusion | flops 506331136 | bytes 4390912 | tf_op jit(solution)/shard_map/mrc,nc->mrn/dot_general | solution.py:75
  23.9 1.6 %dynamic-slice_convert_fusion.1 = bf16[128,512]{1,0:T(8,128)(2,1)} fusion(f32[256,512]{1,0:T(8,128)} %fusion.6, s32[]{:T(128)S(6)} %select_n.62), kind=kLoop, calls=%fused_computation.46 | loop fusion | bytes 262148 | tf_op jit(solution)/shard_map/convert_element_type | solution.py:19
  25.5 3.0 %collective-permute-start.1 = (bf16[128,512]{1,0:T(8,128)(2,1)}, bf16[128,512]{1,0:T(8,128)(2,1)}, u32[]{:S(2)}, u32[]{:S(2)}) collective-permute-start(bf16[128,512]{1,0:T(8,128)(2,1)} %dynamic-slice_convert_fusion.1), channel_id=1, source_target_pairs={{0,4},{4,0},{8,12},{12,8},{1,5},{5,1},{9,13},{13,9},{2,6},{6,2},{1... | collective-permute-start | bytes 393224 | tf_op jit(solution)/shard_map/ppermute | solution.py:19
  28.5 3.5 %fusion.2 = f32[256,512]{1,0:T(8,128)} fusion(f32[256,6,256]{2,0,1:T(8,128)} %fusion.38, bf16[6,128,256]{2,1,0:T(8,128)(2,1)} %collective-permute-done.6, bf16[256,6,1,512]{3,2,1,0:T(2,128)(2,1)S(1)} %copy-done.6, bf16[512,256]{1,0:T(8,128)(2,1)S(1)} %copy-done, bf16[256,128]{1,0:T(8,128)(2,1)} %constant_dynamic-slice_fusion.1), kind=kOutput, calls=%fused_computation.3 | convolution fusion | flops 506331136 | bytes 4390912 | tf_op jit(solution)/shard_map/mrc,nc->mrn/dot_general | solution.py:75
  32.1 1.1 %dynamic-slice_convert_fusion = bf16[128,512]{1,0:T(8,128)(2,1)S(1)} fusion(f32[256,512]{1,0:T(8,128)} %fusion.2, s32[]{:T(128)S(6)} %select_n.62), kind=kLoop, calls=%fused_computation.44 | loop fusion | bytes 262148 | tf_op jit(solution)/shard_map/convert_element_type | solution.py:19
  33.3 1.1 %fusion.36 = bf16[128,512]{1,0:T(8,128)(2,1)S(1)} fusion(bf16[128,512]{1,0:T(8,128)(2,1)} %collective-permute-done.1, f32[256,512]{1,0:T(8,128)} %fusion.6, s32[]{:T(128)S(6)} %select_n.60), kind=kLoop, calls=%fused_computation.47 | loop fusion | flops 196608 | bytes 524292 | tf_op jit(solution)/shard_map/convert_element_type | solution.py:23
  34.4 3.1 %collective-permute-start.2 = (bf16[128,512]{1,0:T(8,128)(2,1)S(1)}, bf16[128,512]{1,0:T(8,128)(2,1)S(1)}, u32[]{:S(2)}, u32[]{:S(2)}) collective-permute-start(bf16[128,512]{1,0:T(8,128)(2,1)S(1)} %fusion.36), channel_id=1, source_target_pairs={{0,8},{4,12},{8,0},{12,4},{1,9},{5,13},{9,1},{13,5},{2,10},{6,14},... | collective-permute-start | bytes 393224 | tf_op jit(solution)/shard_map/ppermute | solution.py:23
  37.4 3.1 %collective-permute-done.7 = bf16[128,512]{1,0:T(8,128)(2,1)S(1)} collective-permute-done((bf16[128,512]{1,0:T(8,128)(2,1)S(1)}, bf16[128,512]{1,0:T(8,128)(2,1)S(1)}, u32[]{:S(2)}, u32[]{:S(2)}) %collective-permute-start.7) | collective-permute-done | bytes 131104 | tf_op jit(solution)/shard_map/ppermute | solution.py:19
  40.5 1.0 %fusion.37 = bf16[128,512]{1,0:T(8,128)(2,1)S(1)} fusion(bf16[128,512]{1,0:T(8,128)(2,1)S(1)} %collective-permute-done.7, f32[256,512]{1,0:T(8,128)} %fusion.2, s32[]{:T(128)S(6)} %select_n.60), kind=kLoop, calls=%fused_computation.48 | loop fusion | flops 196608 | bytes 524292 | tf_op jit(solution)/shard_map/convert_element_type | solution.py:23
  41.5 1.8 %collective-permute-start.8 = (bf16[128,512]{1,0:T(8,128)(2,1)S(1)}, bf16[128,512]{1,0:T(8,128)(2,1)S(1)}, u32[]{:S(2)}, u32[]{:S(2)}) collective-permute-start(bf16[128,512]{1,0:T(8,128)(2,1)S(1)} %fusion.37), channel_id=1, source_target_pairs={{0,8},{4,12},{8,0},{12,4},{1,9},{5,13},{9,1},{13,5},{2,10},{6,14},... | collective-permute-start | bytes 393224 | tf_op jit(solution)/shard_map/ppermute | solution.py:23
  43.3 1.6 %collective-permute-done.2 = bf16[128,512]{1,0:T(8,128)(2,1)S(1)} collective-permute-done((bf16[128,512]{1,0:T(8,128)(2,1)S(1)}, bf16[128,512]{1,0:T(8,128)(2,1)S(1)}, u32[]{:S(2)}, u32[]{:S(2)}) %collective-permute-start.2) | collective-permute-done | bytes 131104 | tf_op jit(solution)/shard_map/ppermute | solution.py:23
  44.9 1.2 %fusion.31 = bf16[128,512]{1,0:T(8,128)(2,1)S(1)} fusion(f32[128,1,512]{2,1,0:T(1,128)} %constant_dynamic-slice_fusion.2, bf16[128,512]{1,0:T(8,128)(2,1)S(1)} %collective-permute-done.2, bf16[128,512]{1,0:T(8,128)(2,1)} %collective-permute-done.1, f32[256,512]{1,0:T(8,128)} %fusion.6, s32[]{:T(128)S(6)} %select_n.60), kind=kLoop, calls=%fused_computation.38 | loop fusion | flops 393216 | bytes 917508 | tf_op jit(solution)/shard_map/convert_element_type | solution.py:80
  46.9 2.3 %collective-permute-done.8 = bf16[128,512]{1,0:T(8,128)(2,1)S(1)} collective-permute-done((bf16[128,512]{1,0:T(8,128)(2,1)S(1)}, bf16[128,512]{1,0:T(8,128)(2,1)S(1)}, u32[]{:S(2)}, u32[]{:S(2)}) %collective-permute-start.8) | collective-permute-done | bytes 131104 | tf_op jit(solution)/shard_map/ppermute | solution.py:23
  49.2 1.1 %fusion.29 = bf16[128,512]{1,0:T(8,128)(2,1)S(1)} fusion(f32[128,1,512]{2,1,0:T(1,128)} %constant_dynamic-slice_fusion, bf16[128,512]{1,0:T(8,128)(2,1)S(1)} %collective-permute-done.8, bf16[128,512]{1,0:T(8,128)(2,1)S(1)} %collective-permute-done.7, f32[256,512]{1,0:T(8,128)} %fusion.2, s32[]{:T(128)S(6)} %select_n.60), kind=kLoop, calls=%fused_computation.35 | loop fusion | flops 393216 | bytes 917508 | tf_op jit(solution)/shard_map/convert_element_type | solution.py:80
  50.9 1.0 %collective-permute-done.3 = bf16[128,512]{1,0:T(8,128)(2,1)S(1)} collective-permute-done((bf16[128,512]{1,0:T(8,128)(2,1)S(1)}, bf16[128,512]{1,0:T(8,128)(2,1)S(1)}, u32[]{:S(2)}, u32[]{:S(2)}) %collective-permute-start.3) | collective-permute-done | bytes 131104 | tf_op jit(solution)/shard_map/ppermute | solution.py:33
  52.9 2.9 %collective-permute-done.9 = bf16[128,512]{1,0:T(8,128)(2,1)S(1)} collective-permute-done((bf16[128,512]{1,0:T(8,128)(2,1)S(1)}, bf16[128,512]{1,0:T(8,128)(2,1)S(1)}, u32[]{:S(2)}, u32[]{:S(2)}) %collective-permute-start.9) | collective-permute-done | bytes 131104 | tf_op jit(solution)/shard_map/ppermute | solution.py:33
  56.7 1.6 %copy.27 = bf16[256,128]{0,1:T(8,128)(2,1)} copy(bf16[256,128]{1,0:T(8,128)(2,1)} %constant_dynamic-slice_fusion.1) | data formatting | bytes 131072
  59.9 1.4 %fusion.26 = bf16[128,6,1,256]{3,0,1,2:T(8,128)(2,1)S(1)} fusion(f32[128,6,256]{2,0,1:T(8,128)S(1)} %fusion.44, bf16[6,256,256]{2,1,0:T(8,128)(2,1)} %collective-permute-done.5, bf16[128,6,1,256]{3,2,1,0:T(2,128)(2,1)S(1)} %copy-done.5, bf16[256,128]{0,1:T(8,128)(2,1)S(1)} %collective-permute-done.4), kind=kOutput, calls=%fused_computation.28 | convolution fusion | flops 101449728 | bytes 2424832 | tf_op jit(solution)/shard_map/rk,mrc->mkc/dot_general | solution.py:91
  61.3 1.4 %fusion.27 = bf16[128,6,1,256]{3,0,1,2:T(8,128)(2,1)S(1)} fusion(f32[128,6,256]{2,0,1:T(8,128)S(1)} %fusion.40, bf16[6,256,256]{2,1,0:T(8,128)(2,1)} %collective-permute-done.10, bf16[128,6,1,256]{3,2,1,0:T(2,128)(2,1)S(1)} %copy-done.3, bf16[256,128]{0,1:T(8,128)(2,1)S(1)} %collective-permute-done.4), kind=kOutput, calls=%fused_computation.29 | convolution fusion | flops 101449728 | bytes 2424832 | tf_op jit(solution)/shard_map/rk,mrc->mkc/dot_general | solution.py:91
  62.8 1.7 %copy.21 = bf16[128,6,2,256]{3,2,1,0:T(2,128)(2,1)} copy(bf16[128,6,2,256]{3,0,1,2:T(8,128)(2,1)S(1)} %pad_maximum_fusion) | data formatting | bytes 1572864 | tf_op jit(solution)/shard_map/stack | solution.py:93
  (51 shorter events, 10.2 us)
Async XLA Ops:
  0.0 19.4 %copy-start = (bf16[512,256]{1,0:T(8,128)(2,1)S(1)}, bf16[512,256]{1,0:T(8,128)(2,1)}, u32[]{:S(2)}) copy-start(bf16[512,256]{1,0:T(8,128)(2,1)} %param.9) | copy-start | bytes 786436
  0.0 5.2 %copy-start.1 = (bf16[256,6,2,512]{3,2,1,0:T(2,128)(2,1)S(1)}, bf16[256,6,2,512]{3,2,1,0:T(2,128)(2,1)}, u32[]{:S(2)}) copy-start(bf16[256,6,2,512]{3,2,1,0:T(2,128)(2,1)} %param.5) | copy-start | bytes 9437188
  2.9 1.4 %copy-start.2 = (bf16[128,6,1,256]{3,2,1,0:T(2,128)(2,1)}, bf16[128,6,1,256]{3,2,1,0:T(2,128)(2,1)S(1)}, u32[]{:S(2)}) copy-start(bf16[128,6,1,256]{3,2,1,0:T(2,128)(2,1)S(1)} %get-tuple-element.10) | copy-start | bytes 1179652
  2.9 2.2 %copy-start.4 = (bf16[128,6,1,256]{3,2,1,0:T(2,128)(2,1)}, bf16[128,6,1,256]{3,2,1,0:T(2,128)(2,1)S(1)}, u32[]{:S(2)}) copy-start(bf16[128,6,1,256]{3,2,1,0:T(2,128)(2,1)S(1)} %get-tuple-element.9) | copy-start | bytes 1179652
  3.8 15.6 %collective-permute-start = (bf16[6,128,256]{2,1,0:T(8,128)(2,1)}, bf16[6,128,256]{2,1,0:T(8,128)(2,1)}, u32[]{:S(2)}, u32[]{:S(2)}) collective-permute-start(bf16[6,128,256]{2,1,0:T(8,128)(2,1)} %bitcast.121), channel_id=1, source_target_pairs={{0,1},{1,0},{2,3},{3,2},{4,5},{5,4},{6,7},{7,6},{8,9},{9,8},{10,11... | collective-permute-start | bytes 1179656 | tf_op jit(solution)/shard_map/ppermute | solution.py:8
  5.1 23.4 %collective-permute-start.6 = (bf16[6,128,256]{2,1,0:T(8,128)(2,1)}, bf16[6,128,256]{2,1,0:T(8,128)(2,1)}, u32[]{:S(2)}, u32[]{:S(2)}) collective-permute-start(bf16[6,128,256]{2,1,0:T(8,128)(2,1)} %bitcast.120), channel_id=1, source_target_pairs={{0,1},{1,0},{2,3},{3,2},{4,5},{5,4},{6,7},{7,6},{8,9},{9,8},{10,11... | collective-permute-start | bytes 1179656 | tf_op jit(solution)/shard_map/ppermute | solution.py:8
  5.2 6.1 %copy-start.9 = (f32[256,2,512]{2,1,0:T(2,128)S(1)}, f32[256,2,512]{2,1,0:T(2,128)}, u32[]{:S(2)}) copy-start(f32[256,2,512]{2,1,0:T(2,128)} %param.7) | copy-start | bytes 3145732
  5.2 6.9 %copy-start.10 = (bf16[256,256]{1,0:T(8,128)(2,1)S(1)}, bf16[256,256]{1,0:T(8,128)(2,1)}, u32[]{:S(2)}) copy-start(bf16[256,256]{1,0:T(8,128)(2,1)} %param.8) | copy-start | bytes 393220
  16.8 11.8 %copy-start.6 = (bf16[256,6,1,512]{3,2,1,0:T(2,128)(2,1)S(1)}, bf16[256,6,1,512]{3,2,1,0:T(2,128)(2,1)}, u32[]{:S(2)}) copy-start(bf16[256,6,1,512]{3,2,1,0:T(2,128)(2,1)} %get-tuple-element.6) | copy-start | bytes 4718596
  25.5 7.8 %collective-permute-start.1 = (bf16[128,512]{1,0:T(8,128)(2,1)}, bf16[128,512]{1,0:T(8,128)(2,1)}, u32[]{:S(2)}, u32[]{:S(2)}) collective-permute-start(bf16[128,512]{1,0:T(8,128)(2,1)} %dynamic-slice_convert_fusion.1), channel_id=1, source_target_pairs={{0,4},{4,0},{8,12},{12,8},{1,5},{5,1},{9,13},{13,9},{2,6},{6,2},{1... | collective-permute-start | bytes 393224 | tf_op jit(solution)/shard_map/ppermute | solution.py:19
  32.1 19.9 %copy-start.8 = (bf16[256,6,1,512]{3,2,1,0:T(2,128)(2,1)S(1)}, bf16[256,6,1,512]{3,2,1,0:T(2,128)(2,1)}, u32[]{:S(2)}) copy-start(bf16[256,6,1,512]{3,2,1,0:T(2,128)(2,1)} %get-tuple-element.5) | copy-start | bytes 4718596
  33.2 7.3 %collective-permute-start.7 = (bf16[128,512]{1,0:T(8,128)(2,1)S(1)}, bf16[128,512]{1,0:T(8,128)(2,1)S(1)}, u32[]{:S(2)}, u32[]{:S(2)}) collective-permute-start(bf16[128,512]{1,0:T(8,128)(2,1)S(1)} %dynamic-slice_convert_fusion), channel_id=1, source_target_pairs={{0,4},{4,0},{8,12},{12,8},{1,5},{5,1},{9,13},{13,9},{2,6},{6,2},{1... | collective-permute-start | bytes 393224 | tf_op jit(solution)/shard_map/ppermute | solution.py:19
  34.4 10.5 %collective-permute-start.2 = (bf16[128,512]{1,0:T(8,128)(2,1)S(1)}, bf16[128,512]{1,0:T(8,128)(2,1)S(1)}, u32[]{:S(2)}, u32[]{:S(2)}) collective-permute-start(bf16[128,512]{1,0:T(8,128)(2,1)S(1)} %fusion.36), channel_id=1, source_target_pairs={{0,8},{4,12},{8,0},{12,4},{1,9},{5,13},{9,1},{13,5},{2,10},{6,14},... | collective-permute-start | bytes 393224 | tf_op jit(solution)/shard_map/ppermute | solution.py:23
  41.5 7.7 %collective-permute-start.8 = (bf16[128,512]{1,0:T(8,128)(2,1)S(1)}, bf16[128,512]{1,0:T(8,128)(2,1)S(1)}, u32[]{:S(2)}, u32[]{:S(2)}) collective-permute-start(bf16[128,512]{1,0:T(8,128)(2,1)S(1)} %fusion.37), channel_id=1, source_target_pairs={{0,8},{4,12},{8,0},{12,4},{1,9},{5,13},{9,1},{13,5},{2,10},{6,14},... | collective-permute-start | bytes 393224 | tf_op jit(solution)/shard_map/ppermute | solution.py:23
  46.0 5.9 %collective-permute-start.3 = (bf16[128,512]{1,0:T(8,128)(2,1)S(1)}, bf16[128,512]{1,0:T(8,128)(2,1)S(1)}, u32[]{:S(2)}, u32[]{:S(2)}) collective-permute-start(bf16[128,512]{1,0:T(8,128)(2,1)S(1)} %fusion.31), channel_id=1, source_target_pairs={{0,4},{4,0},{8,12},{12,8},{1,5},{5,1},{9,13},{13,9},{2,6},{6,2},{1... | collective-permute-start | bytes 393224 | tf_op jit(solution)/shard_map/ppermute | solution.py:33
  50.3 5.4 %collective-permute-start.9 = (bf16[128,512]{1,0:T(8,128)(2,1)S(1)}, bf16[128,512]{1,0:T(8,128)(2,1)S(1)}, u32[]{:S(2)}, u32[]{:S(2)}) collective-permute-start(bf16[128,512]{1,0:T(8,128)(2,1)S(1)} %fusion.29), channel_id=1, source_target_pairs={{0,4},{4,0},{8,12},{12,8},{1,5},{5,1},{9,13},{13,9},{2,6},{6,2},{1... | collective-permute-start | bytes 393224 | tf_op jit(solution)/shard_map/ppermute | solution.py:33
  51.9 3.9 %copy-start.7 = (bf16[256,6,1,512]{3,2,1,0:T(2,128)(2,1)S(1)}, bf16[256,6,1,512]{3,2,1,0:T(2,128)(2,1)}, u32[]{:S(2)}) copy-start(bf16[256,6,1,512]{3,2,1,0:T(2,128)(2,1)} %get-tuple-element.6) | copy-start | bytes 4718596
  52.8 7.1 %collective-permute-start.5 = (bf16[6,256,256]{2,1,0:T(8,128)(2,1)S(1)}, bf16[6,256,256]{2,1,0:T(8,128)(2,1)}, u32[]{:S(2)}, u32[]{:S(2)}) collective-permute-start(bf16[6,256,256]{2,1,0:T(8,128)(2,1)S(1)} %fusion.17), channel_id=1, source_target_pairs={{0,1},{1,0},{2,3},{3,2},{4,5},{5,4},{6,7},{7,6},{8,9},{9,8},{10,11... | collective-permute-start | bytes 2359304 | tf_op jit(solution)/shard_map/ppermute | solution.py:8
  55.8 4.1 %copy-start.5 = (bf16[128,6,1,256]{3,2,1,0:T(2,128)(2,1)S(1)}, bf16[128,6,1,256]{3,2,1,0:T(2,128)(2,1)}, u32[]{:S(2)}) copy-start(bf16[128,6,1,256]{3,2,1,0:T(2,128)(2,1)} %copy-done.4) | copy-start | bytes 1179652
  56.6 4.7 %copy-start.3 = (bf16[128,6,1,256]{3,2,1,0:T(2,128)(2,1)S(1)}, bf16[128,6,1,256]{3,2,1,0:T(2,128)(2,1)}, u32[]{:S(2)}) copy-start(bf16[128,6,1,256]{3,2,1,0:T(2,128)(2,1)} %copy-done.2) | copy-start | bytes 1179652
  56.6 4.7 %collective-permute-start.10 = (bf16[6,256,256]{2,1,0:T(8,128)(2,1)S(1)}, bf16[6,256,256]{2,1,0:T(8,128)(2,1)}, u32[]{:S(2)}, u32[]{:S(2)}) collective-permute-start(bf16[6,256,256]{2,1,0:T(8,128)(2,1)S(1)} %fusion.14), channel_id=1, source_target_pairs={{0,1},{1,0},{2,3},{3,2},{4,5},{5,4},{6,7},{7,6},{8,9},{9,8},{10,11... | collective-permute-start | bytes 2359304 | tf_op jit(solution)/shard_map/ppermute | solution.py:8
  58.3 1.6 %collective-permute-start.4 = (bf16[256,128]{0,1:T(8,128)(2,1)}, bf16[256,128]{0,1:T(8,128)(2,1)S(1)}, u32[]{:S(2)}, u32[]{:S(2)}) collective-permute-start(bf16[256,128]{0,1:T(8,128)(2,1)} %copy.27), channel_id=1, source_target_pairs={{0,1},{1,0},{2,3},{3,2},{4,5},{5,4},{6,7},{7,6},{8,9},{9,8},{10,11... | collective-permute-start | bytes 196616 | tf_op jit(solution)/shard_map/ppermute | solution.py:8

commit v6 on v4

--- a/solution.py
+++ b/solution.py
@@ -56,13 +56,16 @@
     n_lev = anomalies.shape[2]
 
     anom_t = jnp.transpose(anomalies, (2, 1, 0, 3))
-    ctrl_t = jnp.transpose(control, (2, 1, 0, 3))
     prec_t = jnp.transpose(precision, (1, 0, 2))
 
-    ctrl_other = _swap(ctrl_t, "half")
     rf_own = lax.dynamic_slice_in_dim(row_factor, h * kh, kh, 1)
     rf_other = lax.dynamic_slice_in_dim(row_factor, (1 - h) * kh, kh, 1)
     rf_for_partner = _swap(rf_other, "half")
+    ctrl_other = _swap(control, "half")
+    expanded_all = (
+        jnp.einsum("rk,kmlc->lmrc", rf_own, control, preferred_element_type=jnp.float32)
+        + jnp.einsum("rk,kmlc->lmrc", rf_other, ctrl_other, preferred_element_type=jnp.float32)
+    ).astype(jnp.bfloat16)
 
     pow2 = n_mem & (n_mem - 1) == 0 and rows % n_mem == 0
     blk = rows // max(n_mem // 2, 1)
@@ -71,12 +74,7 @@
     outs = []
     for l in range(n_lev):
         a = anom_t[l]
-        c_own = ctrl_t[l]
-        c_oth = ctrl_other[l]
-        expanded = (
-            jnp.einsum("rk,mkc->mrc", rf_own, c_own, preferred_element_type=jnp.float32)
-            + jnp.einsum("rk,mkc->mrc", rf_other, c_oth, preferred_element_type=jnp.float32)
-        ).astype(jnp.bfloat16)
+        expanded = expanded_all[l]
         fields = jnp.einsum("mrc,nc->mrn", expanded, col_factor, preferred_element_type=jnp.float32)
         inc = jnp.sum(a.astype(jnp.float32) * fields, axis=0)
         prec = prec_t[l]
@@ -94,8 +92,9 @@
         summed = jnp.einsum(
             "rk,mrc->mkc", rf_own, projected, preferred_element_type=jnp.float32
         ) + jnp.einsum("rk,mrc->mkc", rf_for_partner, proj_other, preferred_element_type=jnp.float32)
-        outs.append((c_own.astype(jnp.float32) + summed).astype(jnp.bfloat16))
-    return jnp.transpose(jnp.stack(outs, axis=0), (2, 1, 0, 3))
+        outs.append(summed)
+    summed_all = jnp.transpose(jnp.stack(outs, axis=0), (2, 1, 0, 3))
+    return (control.astype(jnp.float32) + summed_all).astype(jnp.bfloat16)
 
 
 def solution(mesh):

time: 49.6 us -> 47.1 us (0.950)
  waiting for transfers between devices: 11.7 us -> 16.8 us
  other arithmetic: 3.5 us -> 0.58 us
  matrix products: 11.5 us -> 8.93 us
  local copies, waits for them, and re-layouts: 11.5 us -> 9.95 us
    ppermute x2, waiting for transfers between devices: 2.41 us -> 8.54 us  [_reduce_scatter_rows(): recv = lax.ppermute(x.astype(wire), axis, [(i, i ^ d) for i in range(size)])]
    dot_general x2, matrix products: 6.83 us -> 1.32 us  [local(): jnp.einsum('mrc,nc->mrn', expanded, col_factor, preferred_element_type=jn...]
    ppermute x2, starting transfers between devices: 3.24 us -> 0.66 us  [_all_gather_rows(): recv = lax.ppermute(x, axis, [(i, i ^ d) for i in range(size)])]
    dot_general x2, matrix products: 0.84 us -> 3.1 us  [local(): jnp.einsum('rk,mrc->mkc', rf_for_partner, proj_other, preferred_element_t...]
    ppermute x2, starting transfers between devices: 3.79 us -> 5.79 us  [_reduce_scatter_rows(): recv = lax.ppermute(x.astype(wire), axis, [(i, i ^ d) for i in range(size)])]
    convert_element_type x2, local copies, waits for them, and re-layouts: 2.01 us -> 0.05 us  [_reduce_scatter_rows(): send.astype(wire)]
    convert_element_type x2, other arithmetic: 1.97 us -> 0.07 us  [_reduce_scatter_rows(): recv = lax.ppermute(x.astype(wire), axis, [(i, i ^ d) for i in range(size)])]
    convert_element_type x0 -> x1, local copies, waits for them, and re-layouts: none -> 1.81 us  [local(): return (control.astype(jnp.float32) + summed_all).astype(jnp.bfloat16)]
  transfers between devices with their start and end apart: 10 -> 10, of which waited for: 5 -> 6; matrix products, arithmetic and copies ran while one was open for 34% -> 25% of each run, Pallas kernels for 0% -> 0%
where the time goes in v6:
time: 47.1 us; the launch traced here: 46.9 us
  waiting for transfers between devices  16.8 us (36%)
  starting transfers between devices  10.4 us (22%)
  local copies, waits for them, and re-layouts  9.95 us (21%)
  matrix products  8.93 us (19%)
  other arithmetic  0.58 us (1%)
    ppermute x2, waiting for transfers between devices, _reduce_scatter_rows(): recv = lax.ppermute(x.astype(wire), axis, [(i, i ^ d) for i in range(size)])  8.54 us
    unnamed x13, local copies, waits for them, and re-layouts  6.59 us
    ppermute x2, starting transfers between devices, _reduce_scatter_rows(): recv = lax.ppermute(x.astype(wire), axis, [(i, i ^ d) for i in range(size)])  5.79 us
    ppermute x2, waiting for transfers between devices, _all_gather_rows(): recv = lax.ppermute(x, axis, [(i, i ^ d) for i in range(size)])  4.31 us
    ppermute x2, waiting for transfers between devices, _reduce_scatter_rows(): lax.ppermute(send.astype(wire), axis, [(i, i ^ d) for i in range(size)])  3.57 us
    dot_general x2, matrix products, local(): jnp.einsum('rk,mrc->mkc', rf_for_partner, proj_other, preferred_element_t...  3.1 us
    ppermute x2, starting transfers between devices, _reduce_scatter_rows(): lax.ppermute(send.astype(wire), axis, [(i, i ^ d) for i in range(size)])  2.79 us
    dot_general x1, matrix products, local(): jnp.einsum('rk,kmlc->lmrc', rf_other, ctrl_other, preferred_element_type=...  1.88 us
  transfers between devices with their start and end apart: 10, of which 6 were waited for; matrix products, arithmetic and copies ran while one was open for 25% of the time, Pallas kernels for 0%

profile of v6, /device:TPU:0, one launch (start us, length us, event | category | flops | bytes accessed | tf_op | source)
XLA Modules:
  0.0 46.9 jit_solution(12833337266557001716)
XLA Ops:
  0.0 1.3 %copy.8 = bf16[128,6,2,256]{3,0,2,1:T(8,128)(2,1)S(1)} copy(bf16[128,6,2,256]{3,2,1,0:T(2,128)(2,1)} %param.6) | data formatting | bytes 1572864 | tf_op args[1]
  1.3 0.5 %collective-permute-start = (bf16[128,6,2,256]{3,0,2,1:T(8,128)(2,1)S(1)}, bf16[128,6,2,256]{3,0,2,1:T(8,128)(2,1)}, u32[]{:S(2)}, u32[]{:S(2)}) collective-permute-start(bf16[128,6,2,256]{3,0,2,1:T(8,128)(2,1)S(1)} %copy.8), channel_id=1, source_target_pairs={{0,1},{1,0},{2,3},{3,2},{4,5},{5,4},{6,7},{7,6},{8,9},{9,8},{10,11... | collective-permute-start | bytes 2359304 | tf_op jit(solution)/shard_map/ppermute | solution.py:8
  1.8 4.3 %copy.28 = bf16[256,6,2,512]{3,0,1,2:T(8,128)(2,1)} copy(bf16[256,6,2,512]{3,2,1,0:T(2,128)(2,1)} %param.5) | data formatting | bytes 6291456 | tf_op args[0]
  6.1 0.6 %constant_dynamic-slice_fusion.1 = bf16[256,128]{1,0:T(8,128)(2,1)} fusion(bf16[256,256]{1,0:T(8,128)(2,1)S(1)} %copy-done.4, s32[]{:T(128)S(6)} %select_n.61), kind=kLoop, calls=%fused_computation.63 | loop fusion | bytes 131076 | tf_op jit(solution)/shard_map/dynamic_slice | solution.py:62
  6.7 0.8 %fusion.45 = (f32[1,256,512]{2,0,1:T(1,128)S(1)}, f32[1,256,512]{2,0,1:T(1,128)S(1)}) fusion(f32[2,256,512]{2,0,1:T(2,128)S(1)} %bitcast.88), kind=kLoop, calls=%fused_computation.67 | loop fusion | bytes 2097152 | tf_op jit(solution)/shard_map/slice | solution.py:80
  7.6 0.6 %fusion.30 = f32[256,6,2,256]{3,0,2,1:T(8,128)S(1)} fusion(bf16[256,256]{1,0:T(8,128)(2,1)S(1)} %copy-done.4, s32[]{:T(128)S(6)} %select_n.60, bf16[128,6,2,256]{3,2,1,0:T(2,128)(2,1)S(1)} %copy-done.1), kind=kOutput, calls=%fused_computation.49 | convolution fusion | flops 201326592 | bytes 3997700 | tf_op jit(solution)/shard_map/rk,kmlc->lmrc/dot_general | solution.py:66
  8.2 1.9 %fusion.12 = bf16[2,6,256,256]{3,2,0,1:T(8,128)(2,1)S(1)} fusion(f32[256,6,2,256]{3,0,2,1:T(8,128)S(1)} %fusion.30, bf16[128,6,2,256]{3,0,2,1:T(8,128)(2,1)} %collective-permute-done, bf16[256,128]{1,0:T(8,128)(2,1)} %constant_dynamic-slice_fusion.1), kind=kOutput, calls=%fused_computation.19 | convolution fusion | flops 202899456 | bytes 5570560 | tf_op jit(solution)/shard_map/rk,kmlc->lmrc/dot_general | solution.py:67
  10.3 0.7 %fusion = f32[256,512]{1,0:T(8,128)S(1)} fusion(bf16[2,6,256,512]{3,2,1,0:T(8,128)(2,1)S(1)} %bitcast.84, bf16[2,6,256,256]{3,2,0,1:T(8,128)(2,1)S(1)} %fusion.12, bf16[512,256]{1,0:T(8,128)(2,1)S(1)} %copy-done), kind=kOutput, calls=%fused_computation.4 | convolution fusion | flops 404881408 | bytes 3145728 | tf_op jit(solution)/shard_map/mrc,nc->mrn/dot_general | solution.py:78
  11.0 2.7 %collective-permute-start.1 = (bf16[128,512]{1,0:T(8,128)(2,1)S(1)}, bf16[128,512]{1,0:T(8,128)(2,1)S(1)}, u32[]{:S(2)}, u32[]{:S(2)}) collective-permute-start(bf16[128,512]{1,0:T(8,128)(2,1)S(1)} %dynamic-slice_convert_fusion.1), channel_id=1, source_target_pairs={{0,4},{4,0},{8,12},{12,8},{1,5},{5,1},{9,13},{13,9},{2,6},{6,2},{1... | collective-permute-start | bytes 393224 | tf_op jit(solution)/shard_map/ppermute | solution.py:19
  13.7 0.7 %fusion.2 = f32[256,512]{1,0:T(8,128)S(1)} fusion(bf16[2,6,256,512]{3,2,1,0:T(8,128)(2,1)S(1)} %bitcast.85, bf16[2,6,256,256]{3,2,0,1:T(8,128)(2,1)S(1)} %fusion.12, bf16[512,256]{1,0:T(8,128)(2,1)S(1)} %copy-done), kind=kOutput, calls=%fused_computation.6 | convolution fusion | flops 404881408 | bytes 3145728 | tf_op jit(solution)/shard_map/mrc,nc->mrn/dot_general | solution.py:78
  14.5 3.6 %collective-permute-done.1 = bf16[128,512]{1,0:T(8,128)(2,1)S(1)} collective-permute-done((bf16[128,512]{1,0:T(8,128)(2,1)S(1)}, bf16[128,512]{1,0:T(8,128)(2,1)S(1)}, u32[]{:S(2)}, u32[]{:S(2)}) %collective-permute-start.1) | collective-permute-done | bytes 131104 | tf_op jit(solution)/shard_map/ppermute | solution.py:19
  18.1 3.0 %collective-permute-start.2 = (bf16[128,512]{1,0:T(8,128)(2,1)S(1)}, bf16[128,512]{1,0:T(8,128)(2,1)S(1)}, u32[]{:S(2)}, u32[]{:S(2)}) collective-permute-start(bf16[128,512]{1,0:T(8,128)(2,1)S(1)} %fusion.27), channel_id=1, source_target_pairs={{0,8},{4,12},{8,0},{12,4},{1,9},{5,13},{9,1},{13,5},{2,10},{6,14},... | collective-permute-start | bytes 393224 | tf_op jit(solution)/shard_map/ppermute | solution.py:23
  21.2 2.8 %collective-permute-start.7 = (bf16[128,512]{1,0:T(8,128)(2,1)S(1)}, bf16[128,512]{1,0:T(8,128)(2,1)S(1)}, u32[]{:S(2)}, u32[]{:S(2)}) collective-permute-start(bf16[128,512]{1,0:T(8,128)(2,1)S(1)} %fusion.28), channel_id=1, source_target_pairs={{0,8},{4,12},{8,0},{12,4},{1,9},{5,13},{9,1},{13,5},{2,10},{6,14},... | collective-permute-start | bytes 393224 | tf_op jit(solution)/shard_map/ppermute | solution.py:23
  24.0 7.0 %collective-permute-done.2 = bf16[128,512]{1,0:T(8,128)(2,1)S(1)} collective-permute-done((bf16[128,512]{1,0:T(8,128)(2,1)S(1)}, bf16[128,512]{1,0:T(8,128)(2,1)S(1)}, u32[]{:S(2)}, u32[]{:S(2)}) %collective-permute-start.2) | collective-permute-done | bytes 131104 | tf_op jit(solution)/shard_map/ppermute | solution.py:23
  31.1 1.6 %collective-permute-done.7 = bf16[128,512]{1,0:T(8,128)(2,1)S(1)} collective-permute-done((bf16[128,512]{1,0:T(8,128)(2,1)S(1)}, bf16[128,512]{1,0:T(8,128)(2,1)S(1)}, u32[]{:S(2)}, u32[]{:S(2)}) %collective-permute-start.7) | collective-permute-done | bytes 131104 | tf_op jit(solution)/shard_map/ppermute | solution.py:23
  32.7 0.6 %collective-permute-start.8 = (bf16[128,512]{1,0:T(8,128)(2,1)S(1)}, bf16[128,512]{1,0:T(8,128)(2,1)S(1)}, u32[]{:S(2)}, u32[]{:S(2)}) collective-permute-start(bf16[128,512]{1,0:T(8,128)(2,1)S(1)} %fusion.21), channel_id=1, source_target_pairs={{0,4},{4,0},{8,12},{12,8},{1,5},{5,1},{9,13},{13,9},{2,6},{6,2},{1... | collective-permute-start | bytes 393224 | tf_op jit(solution)/shard_map/ppermute | solution.py:33
  33.3 3.7 %collective-permute-done.3 = bf16[128,512]{1,0:T(8,128)(2,1)S(1)} collective-permute-done((bf16[128,512]{1,0:T(8,128)(2,1)S(1)}, bf16[128,512]{1,0:T(8,128)(2,1)S(1)}, u32[]{:S(2)}, u32[]{:S(2)}) %collective-permute-start.3) | collective-permute-done | bytes 131104 | tf_op jit(solution)/shard_map/ppermute | solution.py:33
  37.1 0.6 %fusion.13 = bf16[6,256,256]{2,1,0:T(8,128)(2,1)S(1)} fusion(f32[256,512]{1,0:T(8,128)S(1)} %maximum_convert_fusion, bf16[2,6,256,512]{3,2,1,0:T(8,128)(2,1)S(1)} %bitcast.86, bf16[512,256]{1,0:T(8,128)(2,1)S(1)} %copy-done), kind=kOutput, calls=%fused_computation.20 | convolution fusion | flops 405405696 | bytes 3145728 | tf_op jit(solution)/shard_map/mrn,nc->mrc/dot_general | solution.py:88
  37.8 0.6 %collective-permute-done.8 = bf16[128,512]{1,0:T(8,128)(2,1)S(1)} collective-permute-done((bf16[128,512]{1,0:T(8,128)(2,1)S(1)}, bf16[128,512]{1,0:T(8,128)(2,1)S(1)}, u32[]{:S(2)}, u32[]{:S(2)}) %collective-permute-start.8) | collective-permute-done | bytes 131104 | tf_op jit(solution)/shard_map/ppermute | solution.py:33
  38.5 0.6 %fusion.16 = bf16[6,256,256]{2,1,0:T(8,128)(2,1)S(1)} fusion(f32[256,512]{1,0:T(8,128)S(1)} %maximum_convert_fusion.1, bf16[2,6,256,512]{3,2,1,0:T(8,128)(2,1)S(1)} %bitcast.87, bf16[512,256]{1,0:T(8,128)(2,1)S(1)} %copy-done), kind=kOutput, calls=%fused_computation.21 | convolution fusion | flops 405405696 | bytes 3145728 | tf_op jit(solution)/shard_map/mrn,nc->mrc/dot_general | solution.py:88
  39.7 0.8 %copy.6 = bf16[128,6,2,256]{0,3,1,2:T(8,128)(2,1)S(1)} copy(bf16[128,6,2,256]{3,2,1,0:T(2,128)(2,1)S(1)} %copy-done.1) | data formatting | bytes 1572864 | tf_op args[1]
  41.7 1.6 %fusion.20 = f32[1,6,128,256]{2,3,1,0:T(8,128)S(1)} fusion(f32[6,256,128]{2,1,0:T(8,128)S(1)} %fusion.36, bf16[6,256,256]{2,1,0:T(8,128)(2,1)} %collective-permute-done.4, bf16[256,128]{1,0:T(8,128)(2,1)} %collective-permute-done.5), kind=kOutput, calls=%fused_computation.25 | convolution fusion | flops 100859904 | bytes 2424832 | tf_op jit(solution)/shard_map/rk,mrc->mkc/dot_general | solution.py:94
  43.3 1.6 %fusion.19 = f32[1,6,128,256]{2,3,1,0:T(8,128)S(1)} fusion(f32[6,256,128]{2,1,0:T(8,128)S(1)} %fusion.34, bf16[6,256,256]{2,1,0:T(8,128)(2,1)} %collective-permute-done.9, bf16[256,128]{1,0:T(8,128)(2,1)} %collective-permute-done.5), kind=kOutput, calls=%fused_computation.23 | convolution fusion | flops 100859904 | bytes 2424832 | tf_op jit(solution)/shard_map/rk,mrc->mkc/dot_general | solution.py:94
  45.1 1.8 %copy.14 = bf16[128,6,2,256]{3,2,1,0:T(2,128)(2,1)} copy(bf16[128,6,2,256]{0,3,1,2:T(8,128)(2,1)S(1)} %fusion.9) | data formatting | bytes 1572864 | tf_op jit(solution)/shard_map/convert_element_type | solution.py:97
  (35 shorter events, 2.9 us)
Async XLA Ops:
  0.0 10.1 %copy-start = (bf16[512,256]{1,0:T(8,128)(2,1)S(1)}, bf16[512,256]{1,0:T(8,128)(2,1)}, u32[]{:S(2)}) copy-start(bf16[512,256]{1,0:T(8,128)(2,1)} %param.9) | copy-start | bytes 786436
  1.3 6.9 %collective-permute-start = (bf16[128,6,2,256]{3,0,2,1:T(8,128)(2,1)S(1)}, bf16[128,6,2,256]{3,0,2,1:T(8,128)(2,1)}, u32[]{:S(2)}, u32[]{:S(2)}) collective-permute-start(bf16[128,6,2,256]{3,0,2,1:T(8,128)(2,1)S(1)} %copy.8), channel_id=1, source_target_pairs={{0,1},{1,0},{2,3},{3,2},{4,5},{5,4},{6,7},{7,6},{8,9},{9,8},{10,11... | collective-permute-start | bytes 2359304 | tf_op jit(solution)/shard_map/ppermute | solution.py:8
  1.8 4.3 %copy-start.4 = (bf16[256,256]{1,0:T(8,128)(2,1)S(1)}, bf16[256,256]{1,0:T(8,128)(2,1)}, u32[]{:S(2)}) copy-start(bf16[256,256]{1,0:T(8,128)(2,1)} %param.8) | copy-start | bytes 393220
  1.8 4.9 %copy-start.3 = (f32[256,2,512]{2,1,0:T(2,128)S(1)}, f32[256,2,512]{2,1,0:T(2,128)}, u32[]{:S(2)}) copy-start(f32[256,2,512]{2,1,0:T(2,128)} %param.7) | copy-start | bytes 3145732
  6.1 1.5 %copy-start.1 = (bf16[128,6,2,256]{3,2,1,0:T(2,128)(2,1)S(1)}, bf16[128,6,2,256]{3,2,1,0:T(2,128)(2,1)}, u32[]{:S(2)}) copy-start(bf16[128,6,2,256]{3,2,1,0:T(2,128)(2,1)} %param.6) | copy-start | bytes 2359300
  8.2 2.2 %copy-start.2 = (bf16[256,6,2,512]{3,0,1,2:T(8,128)(2,1)S(1)}, bf16[256,6,2,512]{3,0,1,2:T(8,128)(2,1)}, u32[]{:S(2)}) copy-start(bf16[256,6,2,512]{3,0,1,2:T(8,128)(2,1)} %copy.28) | copy-start | bytes 9437188
  11.0 7.0 %collective-permute-start.1 = (bf16[128,512]{1,0:T(8,128)(2,1)S(1)}, bf16[128,512]{1,0:T(8,128)(2,1)S(1)}, u32[]{:S(2)}, u32[]{:S(2)}) collective-permute-start(bf16[128,512]{1,0:T(8,128)(2,1)S(1)} %dynamic-slice_convert_fusion.1), channel_id=1, source_target_pairs={{0,4},{4,0},{8,12},{12,8},{1,5},{5,1},{9,13},{13,9},{2,6},{6,2},{1... | collective-permute-start | bytes 393224 | tf_op jit(solution)/shard_map/ppermute | solution.py:19
  14.4 6.7 %collective-permute-start.6 = (bf16[128,512]{1,0:T(8,128)(2,1)S(1)}, bf16[128,512]{1,0:T(8,128)(2,1)S(1)}, u32[]{:S(2)}, u32[]{:S(2)}) collective-permute-start(bf16[128,512]{1,0:T(8,128)(2,1)S(1)} %dynamic-slice_convert_fusion), channel_id=1, source_target_pairs={{0,4},{4,0},{8,12},{12,8},{1,5},{5,1},{9,13},{13,9},{2,6},{6,2},{1... | collective-permute-start | bytes 393224 | tf_op jit(solution)/shard_map/ppermute | solution.py:19
  18.1 12.8 %collective-permute-start.2 = (bf16[128,512]{1,0:T(8,128)(2,1)S(1)}, bf16[128,512]{1,0:T(8,128)(2,1)S(1)}, u32[]{:S(2)}, u32[]{:S(2)}) collective-permute-start(bf16[128,512]{1,0:T(8,128)(2,1)S(1)} %fusion.27), channel_id=1, source_target_pairs={{0,8},{4,12},{8,0},{12,4},{1,9},{5,13},{9,1},{13,5},{2,10},{6,14},... | collective-permute-start | bytes 393224 | tf_op jit(solution)/shard_map/ppermute | solution.py:23
  21.2 11.5 %collective-permute-start.7 = (bf16[128,512]{1,0:T(8,128)(2,1)S(1)}, bf16[128,512]{1,0:T(8,128)(2,1)S(1)}, u32[]{:S(2)}, u32[]{:S(2)}) collective-permute-start(bf16[128,512]{1,0:T(8,128)(2,1)S(1)} %fusion.28), channel_id=1, source_target_pairs={{0,8},{4,12},{8,0},{12,4},{1,9},{5,13},{9,1},{13,5},{2,10},{6,14},... | collective-permute-start | bytes 393224 | tf_op jit(solution)/shard_map/ppermute | solution.py:23
  31.0 6.0 %collective-permute-start.3 = (bf16[128,512]{1,0:T(8,128)(2,1)S(1)}, bf16[128,512]{1,0:T(8,128)(2,1)S(1)}, u32[]{:S(2)}, u32[]{:S(2)}) collective-permute-start(bf16[128,512]{1,0:T(8,128)(2,1)S(1)} %fusion.22), channel_id=1, source_target_pairs={{0,4},{4,0},{8,12},{12,8},{1,5},{5,1},{9,13},{13,9},{2,6},{6,2},{1... | collective-permute-start | bytes 393224 | tf_op jit(solution)/shard_map/ppermute | solution.py:33
  32.7 5.7 %collective-permute-start.8 = (bf16[128,512]{1,0:T(8,128)(2,1)S(1)}, bf16[128,512]{1,0:T(8,128)(2,1)S(1)}, u32[]{:S(2)}, u32[]{:S(2)}) collective-permute-start(bf16[128,512]{1,0:T(8,128)(2,1)S(1)} %fusion.21), channel_id=1, source_target_pairs={{0,4},{4,0},{8,12},{12,8},{1,5},{5,1},{9,13},{13,9},{2,6},{6,2},{1... | collective-permute-start | bytes 393224 | tf_op jit(solution)/shard_map/ppermute | solution.py:33
  37.8 4.0 %collective-permute-start.4 = (bf16[6,256,256]{2,1,0:T(8,128)(2,1)S(1)}, bf16[6,256,256]{2,1,0:T(8,128)(2,1)}, u32[]{:S(2)}, u32[]{:S(2)}) collective-permute-start(bf16[6,256,256]{2,1,0:T(8,128)(2,1)S(1)} %fusion.13), channel_id=1, source_target_pairs={{0,1},{1,0},{2,3},{3,2},{4,5},{5,4},{6,7},{7,6},{8,9},{9,8},{10,11... | collective-permute-start | bytes 2359304 | tf_op jit(solution)/shard_map/ppermute | solution.py:8
  39.2 4.1 %collective-permute-start.9 = (bf16[6,256,256]{2,1,0:T(8,128)(2,1)S(1)}, bf16[6,256,256]{2,1,0:T(8,128)(2,1)}, u32[]{:S(2)}, u32[]{:S(2)}) collective-permute-start(bf16[6,256,256]{2,1,0:T(8,128)(2,1)S(1)} %fusion.16), channel_id=1, source_target_pairs={{0,1},{1,0},{2,3},{3,2},{4,5},{5,4},{6,7},{7,6},{8,9},{9,8},{10,11... | collective-permute-start | bytes 2359304 | tf_op jit(solution)/shard_map/ppermute | solution.py:8
  39.2 2.5 %collective-permute-start.5 = (bf16[256,128]{1,0:T(8,128)(2,1)}, bf16[256,128]{1,0:T(8,128)(2,1)}, u32[]{:S(2)}, u32[]{:S(2)}) collective-permute-start(bf16[256,128]{1,0:T(8,128)(2,1)} %constant_dynamic-slice_fusion.1), channel_id=1, source_target_pairs={{0,1},{1,0},{2,3},{3,2},{4,5},{5,4},{6,7},{7,6},{8,9},{9,8},{10,11... | collective-permute-start | bytes 196616 | tf_op jit(solution)/shard_map/ppermute | solution.py:8

commit v7 on v6

--- a/solution.py
+++ b/solution.py
@@ -60,7 +60,6 @@
 
     rf_own = lax.dynamic_slice_in_dim(row_factor, h * kh, kh, 1)
     rf_other = lax.dynamic_slice_in_dim(row_factor, (1 - h) * kh, kh, 1)
-    rf_for_partner = _swap(rf_other, "half")
     ctrl_other = _swap(control, "half")
     expanded_all = (
         jnp.einsum("rk,kmlc->lmrc", rf_own, control, preferred_element_type=jnp.float32)
@@ -88,10 +87,11 @@
         projected = jnp.einsum(
             "mrn,nc->mrc", scaled, col_factor, preferred_element_type=jnp.float32
         ).astype(jnp.bfloat16)
-        proj_other = _swap(projected, "half")
+        for_partner = jnp.einsum("rk,mrc->mkc", rf_other, projected, preferred_element_type=jnp.float32)
+        from_partner = _swap(for_partner.astype(jnp.bfloat16), "half")
         summed = jnp.einsum(
             "rk,mrc->mkc", rf_own, projected, preferred_element_type=jnp.float32
-        ) + jnp.einsum("rk,mrc->mkc", rf_for_partner, proj_other, preferred_element_type=jnp.float32)
+        ) + from_partner.astype(jnp.float32)
         outs.append(summed)
     summed_all = jnp.transpose(jnp.stack(outs, axis=0), (2, 1, 0, 3))
     return (control.astype(jnp.float32) + summed_all).astype(jnp.bfloat16)

time: 47.1 us -> 47.6 us (1.011)
  matrix products: 8.93 us -> 10.2 us
  waiting for transfers between devices: 16.8 us -> 15.9 us
    dot_general x2, matrix products: 0.82 us -> 2.84 us  [local(): jnp.einsum('rk,mrc->mkc', rf_own, projected, preferred_element_type=jnp.f...]
    unnamed x13, local copies, waits for them, and re-layouts: 6.59 us -> 7.7 us
    dot_general x2, matrix products: 3.1 us -> 2.34 us  [local(): jnp.einsum('rk,mrc->mkc', rf_other, projected, preferred_element_type=jnp...]
    dynamic_slice x1 -> x0, local copies, waits for them, and re-layouts: 0.63 us -> none  [local(): rf_other = lax.dynamic_slice_in_dim(row_factor, (1 - h) * kh, kh, 1)]
    ppermute x2, waiting for transfers between devices: 4.31 us -> 3.67 us  [_all_gather_rows(): recv = lax.ppermute(x, axis, [(i, i ^ d) for i in range(size)])]
    ppermute x4 -> x3, starting transfers between devices: 1.16 us -> 0.96 us  [_swap(): return lax.ppermute(x, axis, [(0, 1), (1, 0)])]
  transfers between devices with their start and end apart: 10 -> 9, of which waited for: 6 -> 4; matrix products, arithmetic and copies ran while one was open for 25% -> 26% of each run, Pallas kernels for 0% -> 0%
where the time goes in v7:
time: 47.6 us; the launch traced here: 47.4 us
  waiting for transfers between devices  15.9 us (33%)
  local copies, waits for them, and re-layouts  10.4 us (22%)
  matrix products  10.2 us (21%)
  starting transfers between devices  10.1 us (21%)
  other arithmetic  0.55 us (1%)
    ppermute x2, waiting for transfers between devices, _reduce_scatter_rows(): recv = lax.ppermute(x.astype(wire), axis, [(i, i ^ d) for i in range(size)])  8.67 us
    unnamed x13, local copies, waits for them, and re-layouts  7.7 us
    ppermute x2, starting transfers between devices, _reduce_scatter_rows(): recv = lax.ppermute(x.astype(wire), axis, [(i, i ^ d) for i in range(size)])  5.78 us
    ppermute x2, waiting for transfers between devices, _all_gather_rows(): recv = lax.ppermute(x, axis, [(i, i ^ d) for i in range(size)])  3.67 us
    ppermute x2, waiting for transfers between devices, _reduce_scatter_rows(): lax.ppermute(send.astype(wire), axis, [(i, i ^ d) for i in range(size)])  3.57 us
    dot_general x2, matrix products, local(): jnp.einsum('rk,mrc->mkc', rf_own, projected, preferred_element_type=jnp.f...  2.84 us
    ppermute x2, starting transfers between devices, _reduce_scatter_rows(): lax.ppermute(send.astype(wire), axis, [(i, i ^ d) for i in range(size)])  2.72 us
    dot_general x2, matrix products, local(): jnp.einsum('rk,mrc->mkc', rf_other, projected, preferred_element_type=jnp...  2.34 us
  transfers between devices with their start and end apart: 9, of which 4 were waited for; matrix products, arithmetic and copies ran while one was open for 26% of the time, Pallas kernels for 0%

profile of v7, /device:TPU:0, one launch (start us, length us, event | category | flops | bytes accessed | tf_op | source)
XLA Modules:
  0.0 47.4 jit_solution(1673622558055010710)
XLA Ops:
  0.0 2.2 %copy.8 = bf16[128,6,2,256]{3,0,2,1:T(8,128)(2,1)} copy(bf16[128,6,2,256]{3,2,1,0:T(2,128)(2,1)} %param.6) | data formatting | bytes 1572864 | tf_op args[1]
  2.6 4.3 %copy.28 = bf16[256,6,2,512]{3,0,1,2:T(8,128)(2,1)} copy(bf16[256,6,2,512]{3,2,1,0:T(2,128)(2,1)} %param.5) | data formatting | bytes 6291456 | tf_op args[0]
  6.9 0.8 %fusion.53 = (f32[1,256,512]{2,0,1:T(1,128)S(1)}, f32[1,256,512]{2,0,1:T(1,128)S(1)}) fusion(f32[2,256,512]{2,0,1:T(2,128)S(1)} %bitcast.100), kind=kLoop, calls=%fused_computation.74 | loop fusion | bytes 2097152 | tf_op jit(solution)/shard_map/slice | solution.py:79
  8.0 0.6 %fusion.30 = f32[256,6,2,256]{3,0,2,1:T(8,128)S(1)} fusion(bf16[256,256]{1,0:T(8,128)(2,1)S(1)} %copy-done.3, s32[]{:T(128)S(6)} %select_n.60, bf16[128,6,2,256]{3,2,1,0:T(2,128)(2,1)S(1)} %copy-done.1), kind=kOutput, calls=%fused_computation.53 | convolution fusion | flops 201326592 | bytes 3997700 | tf_op jit(solution)/shard_map/rk,kmlc->lmrc/dot_general | solution.py:65
  8.6 1.9 %fusion.12 = bf16[2,6,256,256]{3,2,0,1:T(8,128)(2,1)S(1)} fusion(f32[256,6,2,256]{3,0,2,1:T(8,128)S(1)} %fusion.30, bf16[128,6,2,256]{3,0,2,1:T(8,128)(2,1)} %collective-permute-done, bf16[256,256]{1,0:T(8,128)(2,1)S(1)} %copy-done.3, s32[]{:T(128)S(6)} %select_n.61), kind=kOutput, calls=%fused_computation.19 | convolution fusion | flops 202899456 | bytes 5570564 | tf_op jit(solution)/shard_map/rk,kmlc->lmrc/dot_general | solution.py:66
  10.7 0.7 %fusion = f32[256,512]{1,0:T(8,128)S(1)} fusion(bf16[2,6,256,512]{3,2,1,0:T(8,128)(2,1)S(1)} %bitcast.96, bf16[2,6,256,256]{3,2,0,1:T(8,128)(2,1)S(1)} %fusion.12, bf16[512,256]{1,0:T(8,128)(2,1)S(1)} %copy-done), kind=kOutput, calls=%fused_computation.4 | convolution fusion | flops 404881408 | bytes 3145728 | tf_op jit(solution)/shard_map/mrc,nc->mrn/dot_general | solution.py:77
  11.4 2.6 %collective-permute-start.1 = (bf16[128,512]{1,0:T(8,128)(2,1)S(1)}, bf16[128,512]{1,0:T(8,128)(2,1)S(1)}, u32[]{:S(2)}, u32[]{:S(2)}) collective-permute-start(bf16[128,512]{1,0:T(8,128)(2,1)S(1)} %dynamic-slice_convert_fusion.1), channel_id=1, source_target_pairs={{0,4},{4,0},{8,12},{12,8},{1,5},{5,1},{9,13},{13,9},{2,6},{6,2},{1... | collective-permute-start | bytes 393224 | tf_op jit(solution)/shard_map/ppermute | solution.py:19
  14.1 0.7 %fusion.2 = f32[256,512]{1,0:T(8,128)S(1)} fusion(bf16[2,6,256,512]{3,2,1,0:T(8,128)(2,1)S(1)} %bitcast.97, bf16[2,6,256,256]{3,2,0,1:T(8,128)(2,1)S(1)} %fusion.12, bf16[512,256]{1,0:T(8,128)(2,1)S(1)} %copy-done), kind=kOutput, calls=%fused_computation.6 | convolution fusion | flops 404881408 | bytes 3145728 | tf_op jit(solution)/shard_map/mrc,nc->mrn/dot_general | solution.py:77
  14.8 3.6 %collective-permute-done.1 = bf16[128,512]{1,0:T(8,128)(2,1)S(1)} collective-permute-done((bf16[128,512]{1,0:T(8,128)(2,1)S(1)}, bf16[128,512]{1,0:T(8,128)(2,1)S(1)}, u32[]{:S(2)}, u32[]{:S(2)}) %collective-permute-start.1) | collective-permute-done | bytes 131104 | tf_op jit(solution)/shard_map/ppermute | solution.py:19
  18.4 3.0 %collective-permute-start.2 = (bf16[128,512]{1,0:T(8,128)(2,1)S(1)}, bf16[128,512]{1,0:T(8,128)(2,1)S(1)}, u32[]{:S(2)}, u32[]{:S(2)}) collective-permute-start(bf16[128,512]{1,0:T(8,128)(2,1)S(1)} %fusion.27), channel_id=1, source_target_pairs={{0,8},{4,12},{8,0},{12,4},{1,9},{5,13},{9,1},{13,5},{2,10},{6,14},... | collective-permute-start | bytes 393224 | tf_op jit(solution)/shard_map/ppermute | solution.py:23
  21.5 2.8 %collective-permute-start.6 = (bf16[128,512]{1,0:T(8,128)(2,1)S(1)}, bf16[128,512]{1,0:T(8,128)(2,1)S(1)}, u32[]{:S(2)}, u32[]{:S(2)}) collective-permute-start(bf16[128,512]{1,0:T(8,128)(2,1)S(1)} %fusion.28), channel_id=1, source_target_pairs={{0,8},{4,12},{8,0},{12,4},{1,9},{5,13},{9,1},{13,5},{2,10},{6,14},... | collective-permute-start | bytes 393224 | tf_op jit(solution)/shard_map/ppermute | solution.py:23
  24.3 7.1 %collective-permute-done.2 = bf16[128,512]{1,0:T(8,128)(2,1)S(1)} collective-permute-done((bf16[128,512]{1,0:T(8,128)(2,1)S(1)}, bf16[128,512]{1,0:T(8,128)(2,1)S(1)}, u32[]{:S(2)}, u32[]{:S(2)}) %collective-permute-start.2) | collective-permute-done | bytes 131104 | tf_op jit(solution)/shard_map/ppermute | solution.py:23
  31.5 1.6 %collective-permute-done.6 = bf16[128,512]{1,0:T(8,128)(2,1)S(1)} collective-permute-done((bf16[128,512]{1,0:T(8,128)(2,1)S(1)}, bf16[128,512]{1,0:T(8,128)(2,1)S(1)}, u32[]{:S(2)}, u32[]{:S(2)}) %collective-permute-start.6) | collective-permute-done | bytes 131104 | tf_op jit(solution)/shard_map/ppermute | solution.py:23
  33.2 0.6 %collective-permute-start.7 = (bf16[128,512]{1,0:T(8,128)(2,1)S(1)}, bf16[128,512]{1,0:T(8,128)(2,1)S(1)}, u32[]{:S(2)}, u32[]{:S(2)}) collective-permute-start(bf16[128,512]{1,0:T(8,128)(2,1)S(1)} %fusion.21), channel_id=1, source_target_pairs={{0,4},{4,0},{8,12},{12,8},{1,5},{5,1},{9,13},{13,9},{2,6},{6,2},{1... | collective-permute-start | bytes 393224 | tf_op jit(solution)/shard_map/ppermute | solution.py:33
  33.8 3.7 %collective-permute-done.3 = bf16[128,512]{1,0:T(8,128)(2,1)S(1)} collective-permute-done((bf16[128,512]{1,0:T(8,128)(2,1)S(1)}, bf16[128,512]{1,0:T(8,128)(2,1)S(1)}, u32[]{:S(2)}, u32[]{:S(2)}) %collective-permute-start.3) | collective-permute-done | bytes 131104 | tf_op jit(solution)/shard_map/ppermute | solution.py:33
  37.5 0.6 %fusion.13 = bf16[6,256,256]{2,1,0:T(8,128)(2,1)S(1)} fusion(f32[256,512]{1,0:T(8,128)S(1)} %maximum_convert_fusion, bf16[2,6,256,512]{3,2,1,0:T(8,128)(2,1)S(1)} %bitcast.98, bf16[512,256]{1,0:T(8,128)(2,1)S(1)} %copy-done), kind=kOutput, calls=%fused_computation.20 | convolution fusion | flops 405405696 | bytes 3145728 | tf_op jit(solution)/shard_map/mrn,nc->mrc/dot_general | solution.py:87
  38.2 1.2 %fusion.19 = bf16[6,128,256]{1,2,0:T(8,128)(2,1)} fusion(bf16[6,256,256]{2,1,0:T(8,128)(2,1)S(1)} %fusion.13, bf16[256,256]{1,0:T(8,128)(2,1)S(1)} %copy-done.3, s32[]{:T(128)S(6)} %select_n.61), kind=kOutput, calls=%fused_computation.26 | convolution fusion | flops 100859904 | bytes 1245188 | tf_op jit(solution)/shard_map/rk,mrc->mkc/dot_general | solution.py:90
  39.4 0.6 %fusion.16 = bf16[6,256,256]{2,1,0:T(8,128)(2,1)S(1)} fusion(f32[256,512]{1,0:T(8,128)S(1)} %maximum_convert_fusion.1, bf16[2,6,256,512]{3,2,1,0:T(8,128)(2,1)S(1)} %bitcast.99, bf16[512,256]{1,0:T(8,128)(2,1)S(1)} %copy-done), kind=kOutput, calls=%fused_computation.21 | convolution fusion | flops 405405696 | bytes 3145728 | tf_op jit(solution)/shard_map/mrn,nc->mrc/dot_general | solution.py:87
  40.0 1.2 %fusion.20 = bf16[6,128,256]{1,2,0:T(8,128)(2,1)} fusion(bf16[6,256,256]{2,1,0:T(8,128)(2,1)S(1)} %fusion.16, bf16[256,256]{1,0:T(8,128)(2,1)S(1)} %copy-done.3, s32[]{:T(128)S(6)} %select_n.61), kind=kOutput, calls=%fused_computation.27 | convolution fusion | flops 100859904 | bytes 1245188 | tf_op jit(solution)/shard_map/rk,mrc->mkc/dot_general | solution.py:90
  41.2 0.5 %collective-permute-start.8 = (bf16[6,128,256]{1,2,0:T(8,128)(2,1)}, bf16[6,128,256]{1,2,0:T(8,128)(2,1)}, u32[]{:S(2)}, u32[]{:S(2)}) collective-permute-start(bf16[6,128,256]{1,2,0:T(8,128)(2,1)} %fusion.20), channel_id=1, source_target_pairs={{0,1},{1,0},{2,3},{3,2},{4,5},{5,4},{6,7},{7,6},{8,9},{9,8},{10,11... | collective-permute-start | bytes 1179656 | tf_op jit(solution)/shard_map/ppermute | solution.py:8
  41.7 0.8 %copy.6 = bf16[128,6,2,256]{0,3,1,2:T(8,128)(2,1)S(1)} copy(bf16[128,6,2,256]{3,2,1,0:T(2,128)(2,1)S(1)} %copy-done.1) | data formatting | bytes 1572864 | tf_op args[1]
  42.5 1.4 %add_bitcast_fusion.1 = f32[1,6,128,256]{2,3,1,0:T(8,128)S(1)} fusion(bf16[6,128,256]{1,2,0:T(8,128)(2,1)} %collective-permute-done.4, bf16[6,256,256]{2,1,0:T(8,128)(2,1)S(1)} %fusion.13, bf16[256,256]{1,0:T(8,128)(2,1)S(1)} %copy-done.3, s32[]{:T(128)S(6)} %select_n.60), kind=kOutput, calls=%fused_computation.31 | convolution fusion | flops 101056512 | bytes 2031620 | tf_op jit(solution)/shard_map/rk,mrc->mkc/dot_general | solution.py:92
  43.9 1.4 %add_bitcast_fusion = f32[1,6,128,256]{2,3,1,0:T(8,128)S(1)} fusion(bf16[6,128,256]{1,2,0:T(8,128)(2,1)} %collective-permute-done.8, bf16[6,256,256]{2,1,0:T(8,128)(2,1)S(1)} %fusion.16, bf16[256,256]{1,0:T(8,128)(2,1)S(1)} %copy-done.3, s32[]{:T(128)S(6)} %select_n.60), kind=kOutput, calls=%fused_computation.30 | convolution fusion | flops 101056512 | bytes 2031620 | tf_op jit(solution)/shard_map/rk,mrc->mkc/dot_general | solution.py:92
  45.6 1.8 %copy.14 = bf16[128,6,2,256]{3,2,1,0:T(2,128)(2,1)} copy(bf16[128,6,2,256]{0,3,1,2:T(8,128)(2,1)S(1)} %fusion.9) | data formatting | bytes 1572864 | tf_op jit(solution)/shard_map/convert_element_type | solution.py:97
  (32 shorter events, 1.8 us)
Async XLA Ops:
  0.0 10.5 %copy-start = (bf16[512,256]{1,0:T(8,128)(2,1)S(1)}, bf16[512,256]{1,0:T(8,128)(2,1)}, u32[]{:S(2)}) copy-start(bf16[512,256]{1,0:T(8,128)(2,1)} %param.9) | copy-start | bytes 786436
  2.2 6.4 %collective-permute-start = (bf16[128,6,2,256]{3,0,2,1:T(8,128)(2,1)}, bf16[128,6,2,256]{3,0,2,1:T(8,128)(2,1)}, u32[]{:S(2)}, u32[]{:S(2)}) collective-permute-start(bf16[128,6,2,256]{3,0,2,1:T(8,128)(2,1)} %copy.8), channel_id=1, source_target_pairs={{0,1},{1,0},{2,3},{3,2},{4,5},{5,4},{6,7},{7,6},{8,9},{9,8},{10,11... | collective-permute-start | bytes 2359304 | tf_op jit(solution)/shard_map/ppermute | solution.py:8
  2.6 4.3 %copy-start.4 = (f32[256,2,512]{2,1,0:T(2,128)S(1)}, f32[256,2,512]{2,1,0:T(2,128)}, u32[]{:S(2)}) copy-start(f32[256,2,512]{2,1,0:T(2,128)} %param.7) | copy-start | bytes 3145732
  6.9 1.1 %copy-start.1 = (bf16[128,6,2,256]{3,2,1,0:T(2,128)(2,1)S(1)}, bf16[128,6,2,256]{3,2,1,0:T(2,128)(2,1)}, u32[]{:S(2)}) copy-start(bf16[128,6,2,256]{3,2,1,0:T(2,128)(2,1)} %param.6) | copy-start | bytes 2359300
  6.9 1.1 %copy-start.3 = (bf16[256,256]{1,0:T(8,128)(2,1)S(1)}, bf16[256,256]{1,0:T(8,128)(2,1)}, u32[]{:S(2)}) copy-start(bf16[256,256]{1,0:T(8,128)(2,1)} %param.8) | copy-start | bytes 393220
  8.6 2.1 %copy-start.2 = (bf16[256,6,2,512]{3,0,1,2:T(8,128)(2,1)S(1)}, bf16[256,6,2,512]{3,0,1,2:T(8,128)(2,1)}, u32[]{:S(2)}) copy-start(bf16[256,6,2,512]{3,0,1,2:T(8,128)(2,1)} %copy.28) | copy-start | bytes 9437188
  11.4 7.0 %collective-permute-start.1 = (bf16[128,512]{1,0:T(8,128)(2,1)S(1)}, bf16[128,512]{1,0:T(8,128)(2,1)S(1)}, u32[]{:S(2)}, u32[]{:S(2)}) collective-permute-start(bf16[128,512]{1,0:T(8,128)(2,1)S(1)} %dynamic-slice_convert_fusion.1), channel_id=1, source_target_pairs={{0,4},{4,0},{8,12},{12,8},{1,5},{5,1},{9,13},{13,9},{2,6},{6,2},{1... | collective-permute-start | bytes 393224 | tf_op jit(solution)/shard_map/ppermute | solution.py:19
  14.8 6.7 %collective-permute-start.5 = (bf16[128,512]{1,0:T(8,128)(2,1)S(1)}, bf16[128,512]{1,0:T(8,128)(2,1)S(1)}, u32[]{:S(2)}, u32[]{:S(2)}) collective-permute-start(bf16[128,512]{1,0:T(8,128)(2,1)S(1)} %dynamic-slice_convert_fusion), channel_id=1, source_target_pairs={{0,4},{4,0},{8,12},{12,8},{1,5},{5,1},{9,13},{13,9},{2,6},{6,2},{1... | collective-permute-start | bytes 393224 | tf_op jit(solution)/shard_map/ppermute | solution.py:19
  18.4 12.9 %collective-permute-start.2 = (bf16[128,512]{1,0:T(8,128)(2,1)S(1)}, bf16[128,512]{1,0:T(8,128)(2,1)S(1)}, u32[]{:S(2)}, u32[]{:S(2)}) collective-permute-start(bf16[128,512]{1,0:T(8,128)(2,1)S(1)} %fusion.27), channel_id=1, source_target_pairs={{0,8},{4,12},{8,0},{12,4},{1,9},{5,13},{9,1},{13,5},{2,10},{6,14},... | collective-permute-start | bytes 393224 | tf_op jit(solution)/shard_map/ppermute | solution.py:23
  21.5 11.6 %collective-permute-start.6 = (bf16[128,512]{1,0:T(8,128)(2,1)S(1)}, bf16[128,512]{1,0:T(8,128)(2,1)S(1)}, u32[]{:S(2)}, u32[]{:S(2)}) collective-permute-start(bf16[128,512]{1,0:T(8,128)(2,1)S(1)} %fusion.28), channel_id=1, source_target_pairs={{0,8},{4,12},{8,0},{12,4},{1,9},{5,13},{9,1},{13,5},{2,10},{6,14},... | collective-permute-start | bytes 393224 | tf_op jit(solution)/shard_map/ppermute | solution.py:23
  31.5 6.0 %collective-permute-start.3 = (bf16[128,512]{1,0:T(8,128)(2,1)S(1)}, bf16[128,512]{1,0:T(8,128)(2,1)S(1)}, u32[]{:S(2)}, u32[]{:S(2)}) collective-permute-start(bf16[128,512]{1,0:T(8,128)(2,1)S(1)} %fusion.22), channel_id=1, source_target_pairs={{0,4},{4,0},{8,12},{12,8},{1,5},{5,1},{9,13},{13,9},{2,6},{6,2},{1... | collective-permute-start | bytes 393224 | tf_op jit(solution)/shard_map/ppermute | solution.py:33
  33.2 6.2 %collective-permute-start.7 = (bf16[128,512]{1,0:T(8,128)(2,1)S(1)}, bf16[128,512]{1,0:T(8,128)(2,1)S(1)}, u32[]{:S(2)}, u32[]{:S(2)}) collective-permute-start(bf16[128,512]{1,0:T(8,128)(2,1)S(1)} %fusion.21), channel_id=1, source_target_pairs={{0,4},{4,0},{8,12},{12,8},{1,5},{5,1},{9,13},{13,9},{2,6},{6,2},{1... | collective-permute-start | bytes 393224 | tf_op jit(solution)/shard_map/ppermute | solution.py:33
  39.3 3.2 %collective-permute-start.4 = (bf16[6,128,256]{1,2,0:T(8,128)(2,1)}, bf16[6,128,256]{1,2,0:T(8,128)(2,1)}, u32[]{:S(2)}, u32[]{:S(2)}) collective-permute-start(bf16[6,128,256]{1,2,0:T(8,128)(2,1)} %fusion.19), channel_id=1, source_target_pairs={{0,1},{1,0},{2,3},{3,2},{4,5},{5,4},{6,7},{7,6},{8,9},{9,8},{10,11... | collective-permute-start | bytes 1179656 | tf_op jit(solution)/shard_map/ppermute | solution.py:8
  41.2 2.7 %collective-permute-start.8 = (bf16[6,128,256]{1,2,0:T(8,128)(2,1)}, bf16[6,128,256]{1,2,0:T(8,128)(2,1)}, u32[]{:S(2)}, u32[]{:S(2)}) collective-permute-start(bf16[6,128,256]{1,2,0:T(8,128)(2,1)} %fusion.20), channel_id=1, source_target_pairs={{0,1},{1,0},{2,3},{3,2},{4,5},{5,4},{6,7},{7,6},{8,9},{9,8},{10,11... | collective-permute-start | bytes 1179656 | tf_op jit(solution)/shard_map/ppermute | solution.py:8

commit v8 on v6

--- a/solution.py
+++ b/solution.py
@@ -8,44 +8,43 @@
     return lax.ppermute(x, axis, [(0, 1), (1, 0)])
 
 
-def _reduce_scatter_rows(x, axis, size, wire):
+def _pairs(size, d):
+    return [(i, i ^ d) for i in range(size)]
+
+
+def _reduce_scatter_rows(x, axis, size, dists, wire):
     idx = lax.axis_index(axis)
-    d = 1
-    while 2 * d < size:
+    for d in dists[:-1]:
         half = x.shape[0] // 2
         bit = (idx // d) % 2
         keep = lax.dynamic_slice_in_dim(x, bit * half, half, 0)
         send = lax.dynamic_slice_in_dim(x, (1 - bit) * half, half, 0)
-        recv = lax.ppermute(send.astype(wire), axis, [(i, i ^ d) for i in range(size)])
+        recv = lax.ppermute(send.astype(wire), axis, _pairs(size, d))
         x = keep + recv.astype(x.dtype)
-        d *= 2
-    if d < size:
-        recv = lax.ppermute(x.astype(wire), axis, [(i, i ^ d) for i in range(size)])
+    if dists:
+        recv = lax.ppermute(x.astype(wire), axis, _pairs(size, dists[-1]))
         x = x + recv.astype(x.dtype)
     return x
 
 
-def _all_gather_rows(x, axis, size):
+def _all_gather_rows(x, axis, size, dists):
     idx = lax.axis_index(axis)
-    d = size // 4
-    while d >= 1:
+    for d in reversed(dists[:-1]):
         bit = (idx // d) % 2
-        recv = lax.ppermute(x, axis, [(i, i ^ d) for i in range(size)])
+        recv = lax.ppermute(x, axis, _pairs(size, d))
         lo = jnp.where(bit == 0, x, recv)
         hi = jnp.where(bit == 0, recv, x)
         x = jnp.concatenate([lo, hi], axis=0)
-        d //= 2
     return x
 
 
-def _block_start(axis, size, rows):
+def _block_start(axis, dists, rows):
     idx = lax.axis_index(axis)
     start = 0
-    d, span = 1, rows
-    while 2 * d < size:
+    span = rows
+    for d in dists[:-1]:
         span //= 2
         start = start + ((idx // d) % 2) * span
-        d *= 2
     return start
 
 
@@ -69,7 +68,12 @@
 
     pow2 = n_mem & (n_mem - 1) == 0 and rows % n_mem == 0
     blk = rows // max(n_mem // 2, 1)
-    start = _block_start("mem", n_mem, rows) if pow2 else 0
+    near_first = []
+    d = 1
+    while d < n_mem:
+        near_first.append(d)
+        d *= 2
+    far_first = near_first[::-1]
 
     outs = []
     for l in range(n_lev):
@@ -79,9 +83,11 @@
         inc = jnp.sum(a.astype(jnp.float32) * fields, axis=0)
         prec = prec_t[l]
         if pow2:
-            part = _reduce_scatter_rows(inc, "mem", n_mem, jnp.bfloat16)
+            dists = near_first if l % 2 == 0 else far_first
+            part = _reduce_scatter_rows(inc, "mem", n_mem, dists, jnp.bfloat16)
+            start = _block_start("mem", dists, rows)
             w_blk = (lax.dynamic_slice_in_dim(prec, start, blk, 0) * part).astype(jnp.bfloat16)
-            weighted = _all_gather_rows(w_blk, "mem", n_mem)
+            weighted = _all_gather_rows(w_blk, "mem", n_mem, dists)
         else:
             weighted = (prec * lax.psum(inc, "mem")).astype(jnp.bfloat16)
         scaled = (a.astype(jnp.float32) * weighted.astype(jnp.float32)[None]).astype(jnp.bfloat16)

time: 47.1 us -> 49.2 us (1.045)
  waiting for transfers between devices: 16.8 us -> 18.5 us
    ppermute x6, waiting for transfers between devices: 16.4 us -> 18.1 us  [the longest x2 7.04 us: _reduce_scatter_rows(): recv = lax.ppermute(send.astype(wire), axis, _pairs(size, d))]
  transfers between devices with their start and end apart: 10 -> 10, of which waited for: 6 -> 7; matrix products, arithmetic and copies ran while one was open for 25% -> 24% of each run, Pallas kernels for 0% -> 0%
where the time goes in v8:
time: 49.2 us; the launch traced here: 49 us
  waiting for transfers between devices  18.5 us (38%)
  starting transfers between devices  10.8 us (22%)
  local copies, waits for them, and re-layouts  9.95 us (20%)
  matrix products  8.94 us (18%)
  other arithmetic  0.58 us (1%)
    ppermute x2, waiting for transfers between devices, _reduce_scatter_rows(): recv = lax.ppermute(send.astype(wire), axis, _pairs(size, d))  7.04 us
    unnamed x13, local copies, waits for them, and re-layouts  6.59 us
    ppermute x2, waiting for transfers between devices, _reduce_scatter_rows(): recv = lax.ppermute(x.astype(wire), axis, _pairs(size, dists[-1]))  5.77 us
    ppermute x2, starting transfers between devices, _reduce_scatter_rows(): recv = lax.ppermute(send.astype(wire), axis, _pairs(size, d))  5.37 us
    ppermute x2, waiting for transfers between devices, _all_gather_rows(): recv = lax.ppermute(x, axis, _pairs(size, d))  5.32 us
    ppermute x2, starting transfers between devices, _reduce_scatter_rows(): recv = lax.ppermute(x.astype(wire), axis, _pairs(size, dists[-1]))  3.37 us
    dot_general x2, matrix products, local(): jnp.einsum('rk,mrc->mkc', rf_for_partner, proj_other, preferred_element_t...  3.1 us
    dot_general x1, matrix products, local(): jnp.einsum('rk,kmlc->lmrc', rf_other, ctrl_other, preferred_element_type=...  1.88 us
  transfers between devices with their start and end apart: 10, of which 7 were waited for; matrix products, arithmetic and copies ran while one was open for 24% of the time, Pallas kernels for 0%

profile of v8, /device:TPU:0, one launch (start us, length us, event | category | flops | bytes accessed | tf_op | source)
XLA Modules:
  0.0 49.0 jit_solution(12781941348858837444)
XLA Ops:
  0.0 1.3 %copy.8 = bf16[128,6,2,256]{3,0,2,1:T(8,128)(2,1)S(1)} copy(bf16[128,6,2,256]{3,2,1,0:T(2,128)(2,1)} %param.6) | data formatting | bytes 1572864 | tf_op args[1]
  1.8 4.3 %copy.28 = bf16[256,6,2,512]{3,0,1,2:T(8,128)(2,1)} copy(bf16[256,6,2,512]{3,2,1,0:T(2,128)(2,1)} %param.5) | data formatting | bytes 6291456 | tf_op args[0]
  6.1 0.6 %constant_dynamic-slice_fusion.1 = bf16[256,128]{1,0:T(8,128)(2,1)} fusion(bf16[256,256]{1,0:T(8,128)(2,1)S(1)} %copy-done.4, s32[]{:T(128)S(6)} %select_n.74), kind=kLoop, calls=%fused_computation.63 | loop fusion | bytes 131076 | tf_op jit(solution)/shard_map/dynamic_slice | solution.py:61
  6.7 0.8 %fusion.45 = (f32[1,256,512]{2,0,1:T(1,128)S(1)}, f32[1,256,512]{2,0,1:T(1,128)S(1)}) fusion(f32[2,256,512]{2,0,1:T(2,128)S(1)} %bitcast.88), kind=kLoop, calls=%fused_computation.67 | loop fusion | bytes 2097152 | tf_op jit(solution)/shard_map/slice | solution.py:84
  7.6 0.6 %fusion.30 = f32[256,6,2,256]{3,0,2,1:T(8,128)S(1)} fusion(bf16[256,256]{1,0:T(8,128)(2,1)S(1)} %copy-done.4, s32[]{:T(128)S(6)} %select_n.73, bf16[128,6,2,256]{3,2,1,0:T(2,128)(2,1)S(1)} %copy-done.1), kind=kOutput, calls=%fused_computation.49 | convolution fusion | flops 201326592 | bytes 3997700 | tf_op jit(solution)/shard_map/rk,kmlc->lmrc/dot_general | solution.py:65
  8.2 1.9 %fusion.12 = bf16[2,6,256,256]{3,2,0,1:T(8,128)(2,1)S(1)} fusion(f32[256,6,2,256]{3,0,2,1:T(8,128)S(1)} %fusion.30, bf16[128,6,2,256]{3,0,2,1:T(8,128)(2,1)} %collective-permute-done, bf16[256,128]{1,0:T(8,128)(2,1)} %constant_dynamic-slice_fusion.1), kind=kOutput, calls=%fused_computation.19 | convolution fusion | flops 202899456 | bytes 5570560 | tf_op jit(solution)/shard_map/rk,kmlc->lmrc/dot_general | solution.py:66
  10.3 0.7 %fusion = f32[256,512]{1,0:T(8,128)S(1)} fusion(bf16[2,6,256,512]{3,2,1,0:T(8,128)(2,1)S(1)} %bitcast.84, bf16[2,6,256,256]{3,2,0,1:T(8,128)(2,1)S(1)} %fusion.12, bf16[512,256]{1,0:T(8,128)(2,1)S(1)} %copy-done), kind=kOutput, calls=%fused_computation.4 | convolution fusion | flops 404881408 | bytes 3145728 | tf_op jit(solution)/shard_map/mrc,nc->mrn/dot_general | solution.py:82
  11.0 2.7 %collective-permute-start.1 = (bf16[128,512]{1,0:T(8,128)(2,1)S(1)}, bf16[128,512]{1,0:T(8,128)(2,1)S(1)}, u32[]{:S(2)}, u32[]{:S(2)}) collective-permute-start(bf16[128,512]{1,0:T(8,128)(2,1)S(1)} %dynamic-slice_convert_fusion.1), channel_id=1, source_target_pairs={{0,4},{4,0},{8,12},{12,8},{1,5},{5,1},{9,13},{13,9},{2,6},{6,2},{1... | collective-permute-start | bytes 393224 | tf_op jit(solution)/shard_map/ppermute | solution.py:22
  13.8 0.7 %fusion.2 = f32[256,512]{1,0:T(8,128)S(1)} fusion(bf16[2,6,256,512]{3,2,1,0:T(8,128)(2,1)S(1)} %bitcast.85, bf16[2,6,256,256]{3,2,0,1:T(8,128)(2,1)S(1)} %fusion.12, bf16[512,256]{1,0:T(8,128)(2,1)S(1)} %copy-done), kind=kOutput, calls=%fused_computation.6 | convolution fusion | flops 404881408 | bytes 3145728 | tf_op jit(solution)/shard_map/mrc,nc->mrn/dot_general | solution.py:82
  14.5 2.6 %collective-permute-start.6 = (bf16[128,512]{1,0:T(8,128)(2,1)S(1)}, bf16[128,512]{1,0:T(8,128)(2,1)S(1)}, u32[]{:S(2)}, u32[]{:S(2)}) collective-permute-start(bf16[128,512]{1,0:T(8,128)(2,1)S(1)} %dynamic-slice_convert_fusion), channel_id=1, source_target_pairs={{0,8},{4,12},{8,0},{12,4},{1,9},{5,13},{9,1},{13,5},{2,10},{6,14},... | collective-permute-start | bytes 393224 | tf_op jit(solution)/shard_map/ppermute | solution.py:22
  17.1 0.7 %collective-permute-done.1 = bf16[128,512]{1,0:T(8,128)(2,1)S(1)} collective-permute-done((bf16[128,512]{1,0:T(8,128)(2,1)S(1)}, bf16[128,512]{1,0:T(8,128)(2,1)S(1)}, u32[]{:S(2)}, u32[]{:S(2)}) %collective-permute-start.1) | collective-permute-done | bytes 131104 | tf_op jit(solution)/shard_map/ppermute | solution.py:22
  17.9 3.3 %collective-permute-start.2 = (bf16[128,512]{1,0:T(8,128)(2,1)S(1)}, bf16[128,512]{1,0:T(8,128)(2,1)S(1)}, u32[]{:S(2)}, u32[]{:S(2)}) collective-permute-start(bf16[128,512]{1,0:T(8,128)(2,1)S(1)} %fusion.27), channel_id=1, source_target_pairs={{0,8},{4,12},{8,0},{12,4},{1,9},{5,13},{9,1},{13,5},{2,10},{6,14},... | collective-permute-start | bytes 393224 | tf_op jit(solution)/shard_map/ppermute | solution.py:25
  21.2 6.3 %collective-permute-done.6 = bf16[128,512]{1,0:T(8,128)(2,1)S(1)} collective-permute-done((bf16[128,512]{1,0:T(8,128)(2,1)S(1)}, bf16[128,512]{1,0:T(8,128)(2,1)S(1)}, u32[]{:S(2)}, u32[]{:S(2)}) %collective-permute-start.6) | collective-permute-done | bytes 131104 | tf_op jit(solution)/shard_map/ppermute | solution.py:22
  27.6 1.9 %collective-permute-done.2 = bf16[128,512]{1,0:T(8,128)(2,1)S(1)} collective-permute-done((bf16[128,512]{1,0:T(8,128)(2,1)S(1)}, bf16[128,512]{1,0:T(8,128)(2,1)S(1)}, u32[]{:S(2)}, u32[]{:S(2)}) %collective-permute-start.2) | collective-permute-done | bytes 131104 | tf_op jit(solution)/shard_map/ppermute | solution.py:25
  29.8 3.9 %collective-permute-done.7 = bf16[128,512]{1,0:T(8,128)(2,1)S(1)} collective-permute-done((bf16[128,512]{1,0:T(8,128)(2,1)S(1)}, bf16[128,512]{1,0:T(8,128)(2,1)S(1)}, u32[]{:S(2)}, u32[]{:S(2)}) %collective-permute-start.7) | collective-permute-done | bytes 131104 | tf_op jit(solution)/shard_map/ppermute | solution.py:25
  33.7 0.7 %collective-permute-start.8 = (bf16[128,512]{1,0:T(8,128)(2,1)S(1)}, bf16[128,512]{1,0:T(8,128)(2,1)S(1)}, u32[]{:S(2)}, u32[]{:S(2)}) collective-permute-start(bf16[128,512]{1,0:T(8,128)(2,1)S(1)} %fusion.21), channel_id=1, source_target_pairs={{0,8},{4,12},{8,0},{12,4},{1,9},{5,13},{9,1},{13,5},{2,10},{6,14},... | collective-permute-start | bytes 393224 | tf_op jit(solution)/shard_map/ppermute | solution.py:34
  34.4 2.4 %collective-permute-done.3 = bf16[128,512]{1,0:T(8,128)(2,1)S(1)} collective-permute-done((bf16[128,512]{1,0:T(8,128)(2,1)S(1)}, bf16[128,512]{1,0:T(8,128)(2,1)S(1)}, u32[]{:S(2)}, u32[]{:S(2)}) %collective-permute-start.3) | collective-permute-done | bytes 131104 | tf_op jit(solution)/shard_map/ppermute | solution.py:34
  36.9 0.6 %fusion.13 = bf16[6,256,256]{2,1,0:T(8,128)(2,1)S(1)} fusion(f32[256,512]{1,0:T(8,128)S(1)} %maximum_convert_fusion, bf16[2,6,256,512]{3,2,1,0:T(8,128)(2,1)S(1)} %bitcast.86, bf16[512,256]{1,0:T(8,128)(2,1)S(1)} %copy-done), kind=kOutput, calls=%fused_computation.20 | convolution fusion | flops 405405696 | bytes 3145728 | tf_op jit(solution)/shard_map/mrn,nc->mrc/dot_general | solution.py:94
  37.6 3.0 %collective-permute-done.8 = bf16[128,512]{1,0:T(8,128)(2,1)S(1)} collective-permute-done((bf16[128,512]{1,0:T(8,128)(2,1)S(1)}, bf16[128,512]{1,0:T(8,128)(2,1)S(1)}, u32[]{:S(2)}, u32[]{:S(2)}) %collective-permute-start.8) | collective-permute-done | bytes 131104 | tf_op jit(solution)/shard_map/ppermute | solution.py:34
  40.6 0.6 %fusion.16 = bf16[6,256,256]{2,1,0:T(8,128)(2,1)S(1)} fusion(f32[256,512]{1,0:T(8,128)S(1)} %maximum_convert_fusion.1, bf16[2,6,256,512]{3,2,1,0:T(8,128)(2,1)S(1)} %bitcast.87, bf16[512,256]{1,0:T(8,128)(2,1)S(1)} %copy-done), kind=kOutput, calls=%fused_computation.21 | convolution fusion | flops 405405696 | bytes 3145728 | tf_op jit(solution)/shard_map/mrn,nc->mrc/dot_general | solution.py:94
  41.8 0.8 %copy.6 = bf16[128,6,2,256]{0,3,1,2:T(8,128)(2,1)S(1)} copy(bf16[128,6,2,256]{3,2,1,0:T(2,128)(2,1)S(1)} %copy-done.1) | data formatting | bytes 1572864 | tf_op args[1]
  43.8 1.6 %fusion.20 = f32[1,6,128,256]{2,3,1,0:T(8,128)S(1)} fusion(f32[6,256,128]{2,1,0:T(8,128)S(1)} %fusion.36, bf16[6,256,256]{2,1,0:T(8,128)(2,1)} %collective-permute-done.4, bf16[256,128]{1,0:T(8,128)(2,1)} %collective-permute-done.5), kind=kOutput, calls=%fused_computation.25 | convolution fusion | flops 100859904 | bytes 2424832 | tf_op jit(solution)/shard_map/rk,mrc->mkc/dot_general | solution.py:100
  45.4 1.6 %fusion.19 = f32[1,6,128,256]{2,3,1,0:T(8,128)S(1)} fusion(f32[6,256,128]{2,1,0:T(8,128)S(1)} %fusion.34, bf16[6,256,256]{2,1,0:T(8,128)(2,1)} %collective-permute-done.9, bf16[256,128]{1,0:T(8,128)(2,1)} %collective-permute-done.5), kind=kOutput, calls=%fused_computation.23 | convolution fusion | flops 100859904 | bytes 2424832 | tf_op jit(solution)/shard_map/rk,mrc->mkc/dot_general | solution.py:100
  47.2 1.8 %copy.14 = bf16[128,6,2,256]{3,2,1,0:T(2,128)(2,1)} copy(bf16[128,6,2,256]{0,3,1,2:T(8,128)(2,1)S(1)} %fusion.9) | data formatting | bytes 1572864 | tf_op jit(solution)/shard_map/convert_element_type | solution.py:103
  (35 shorter events, 3.5 us)
Async XLA Ops:
  0.0 10.1 %copy-start = (bf16[512,256]{1,0:T(8,128)(2,1)S(1)}, bf16[512,256]{1,0:T(8,128)(2,1)}, u32[]{:S(2)}) copy-start(bf16[512,256]{1,0:T(8,128)(2,1)} %param.9) | copy-start | bytes 786436
  1.3 6.9 %collective-permute-start = (bf16[128,6,2,256]{3,0,2,1:T(8,128)(2,1)S(1)}, bf16[128,6,2,256]{3,0,2,1:T(8,128)(2,1)}, u32[]{:S(2)}, u32[]{:S(2)}) collective-permute-start(bf16[128,6,2,256]{3,0,2,1:T(8,128)(2,1)S(1)} %copy.8), channel_id=1, source_target_pairs={{0,1},{1,0},{2,3},{3,2},{4,5},{5,4},{6,7},{7,6},{8,9},{9,8},{10,11... | collective-permute-start | bytes 2359304 | tf_op jit(solution)/shard_map/ppermute | solution.py:8
  1.8 4.3 %copy-start.4 = (bf16[256,256]{1,0:T(8,128)(2,1)S(1)}, bf16[256,256]{1,0:T(8,128)(2,1)}, u32[]{:S(2)}) copy-start(bf16[256,256]{1,0:T(8,128)(2,1)} %param.8) | copy-start | bytes 393220
  1.8 4.9 %copy-start.3 = (f32[256,2,512]{2,1,0:T(2,128)S(1)}, f32[256,2,512]{2,1,0:T(2,128)}, u32[]{:S(2)}) copy-start(f32[256,2,512]{2,1,0:T(2,128)} %param.7) | copy-start | bytes 3145732
  6.1 1.5 %copy-start.1 = (bf16[128,6,2,256]{3,2,1,0:T(2,128)(2,1)S(1)}, bf16[128,6,2,256]{3,2,1,0:T(2,128)(2,1)}, u32[]{:S(2)}) copy-start(bf16[128,6,2,256]{3,2,1,0:T(2,128)(2,1)} %param.6) | copy-start | bytes 2359300
  8.2 2.2 %copy-start.2 = (bf16[256,6,2,512]{3,0,1,2:T(8,128)(2,1)S(1)}, bf16[256,6,2,512]{3,0,1,2:T(8,128)(2,1)}, u32[]{:S(2)}) copy-start(bf16[256,6,2,512]{3,0,1,2:T(8,128)(2,1)} %copy.28) | copy-start | bytes 9437188
  11.0 6.8 %collective-permute-start.1 = (bf16[128,512]{1,0:T(8,128)(2,1)S(1)}, bf16[128,512]{1,0:T(8,128)(2,1)S(1)}, u32[]{:S(2)}, u32[]{:S(2)}) collective-permute-start(bf16[128,512]{1,0:T(8,128)(2,1)S(1)} %dynamic-slice_convert_fusion.1), channel_id=1, source_target_pairs={{0,4},{4,0},{8,12},{12,8},{1,5},{5,1},{9,13},{13,9},{2,6},{6,2},{1... | collective-permute-start | bytes 393224 | tf_op jit(solution)/shard_map/ppermute | solution.py:22
  14.5 13.0 %collective-permute-start.6 = (bf16[128,512]{1,0:T(8,128)(2,1)S(1)}, bf16[128,512]{1,0:T(8,128)(2,1)S(1)}, u32[]{:S(2)}, u32[]{:S(2)}) collective-permute-start(bf16[128,512]{1,0:T(8,128)(2,1)S(1)} %dynamic-slice_convert_fusion), channel_id=1, source_target_pairs={{0,8},{4,12},{8,0},{12,4},{1,9},{5,13},{9,1},{13,5},{2,10},{6,14},... | collective-permute-start | bytes 393224 | tf_op jit(solution)/shard_map/ppermute | solution.py:22
  17.9 11.6 %collective-permute-start.2 = (bf16[128,512]{1,0:T(8,128)(2,1)S(1)}, bf16[128,512]{1,0:T(8,128)(2,1)S(1)}, u32[]{:S(2)}, u32[]{:S(2)}) collective-permute-start(bf16[128,512]{1,0:T(8,128)(2,1)S(1)} %fusion.27), channel_id=1, source_target_pairs={{0,8},{4,12},{8,0},{12,4},{1,9},{5,13},{9,1},{13,5},{2,10},{6,14},... | collective-permute-start | bytes 393224 | tf_op jit(solution)/shard_map/ppermute | solution.py:25
  27.5 6.1 %collective-permute-start.7 = (bf16[128,512]{1,0:T(8,128)(2,1)S(1)}, bf16[128,512]{1,0:T(8,128)(2,1)S(1)}, u32[]{:S(2)}, u32[]{:S(2)}) collective-permute-start(bf16[128,512]{1,0:T(8,128)(2,1)S(1)} %fusion.28), channel_id=1, source_target_pairs={{0,4},{4,0},{8,12},{12,8},{1,5},{5,1},{9,13},{13,9},{2,6},{6,2},{1... | collective-permute-start | bytes 393224 | tf_op jit(solution)/shard_map/ppermute | solution.py:25
  29.6 7.2 %collective-permute-start.3 = (bf16[128,512]{1,0:T(8,128)(2,1)S(1)}, bf16[128,512]{1,0:T(8,128)(2,1)S(1)}, u32[]{:S(2)}, u32[]{:S(2)}) collective-permute-start(bf16[128,512]{1,0:T(8,128)(2,1)S(1)} %fusion.22), channel_id=1, source_target_pairs={{0,4},{4,0},{8,12},{12,8},{1,5},{5,1},{9,13},{13,9},{2,6},{6,2},{1... | collective-permute-start | bytes 393224 | tf_op jit(solution)/shard_map/ppermute | solution.py:34
  33.7 6.8 %collective-permute-start.8 = (bf16[128,512]{1,0:T(8,128)(2,1)S(1)}, bf16[128,512]{1,0:T(8,128)(2,1)S(1)}, u32[]{:S(2)}, u32[]{:S(2)}) collective-permute-start(bf16[128,512]{1,0:T(8,128)(2,1)S(1)} %fusion.21), channel_id=1, source_target_pairs={{0,8},{4,12},{8,0},{12,4},{1,9},{5,13},{9,1},{13,5},{2,10},{6,14},... | collective-permute-start | bytes 393224 | tf_op jit(solution)/shard_map/ppermute | solution.py:34
  37.5 6.3 %collective-permute-start.4 = (bf16[6,256,256]{2,1,0:T(8,128)(2,1)S(1)}, bf16[6,256,256]{2,1,0:T(8,128)(2,1)}, u32[]{:S(2)}, u32[]{:S(2)}) collective-permute-start(bf16[6,256,256]{2,1,0:T(8,128)(2,1)S(1)} %fusion.13), channel_id=1, source_target_pairs={{0,1},{1,0},{2,3},{3,2},{4,5},{5,4},{6,7},{7,6},{8,9},{9,8},{10,11... | collective-permute-start | bytes 2359304 | tf_op jit(solution)/shard_map/ppermute | solution.py:8
  41.3 4.1 %collective-permute-start.9 = (bf16[6,256,256]{2,1,0:T(8,128)(2,1)S(1)}, bf16[6,256,256]{2,1,0:T(8,128)(2,1)}, u32[]{:S(2)}, u32[]{:S(2)}) collective-permute-start(bf16[6,256,256]{2,1,0:T(8,128)(2,1)S(1)} %fusion.16), channel_id=1, source_target_pairs={{0,1},{1,0},{2,3},{3,2},{4,5},{5,4},{6,7},{7,6},{8,9},{9,8},{10,11... | collective-permute-start | bytes 2359304 | tf_op jit(solution)/shard_map/ppermute | solution.py:8
  41.3 2.5 %collective-permute-start.5 = (bf16[256,128]{1,0:T(8,128)(2,1)}, bf16[256,128]{1,0:T(8,128)(2,1)}, u32[]{:S(2)}, u32[]{:S(2)}) collective-permute-start(bf16[256,128]{1,0:T(8,128)(2,1)} %constant_dynamic-slice_fusion.1), channel_id=1, source_target_pairs={{0,1},{1,0},{2,3},{3,2},{4,5},{5,4},{6,7},{7,6},{8,9},{9,8},{10,11... | collective-permute-start | bytes 196616 | tf_op jit(solution)/shard_map/ppermute | solution.py:8

commit v9 on v8

--- a/solution.py
+++ b/solution.py
@@ -27,15 +27,20 @@
     return x
 
 
-def _all_gather_rows(x, axis, size, dists):
+def _all_gather_pieces(x, start, axis, size, dists):
     idx = lax.axis_index(axis)
+    pieces = [(x, start)]
+    span = x.shape[0]
     for d in reversed(dists[:-1]):
         bit = (idx // d) % 2
         recv = lax.ppermute(x, axis, _pairs(size, d))
+        pieces.append((recv, start + (1 - 2 * bit) * span))
         lo = jnp.where(bit == 0, x, recv)
         hi = jnp.where(bit == 0, recv, x)
         x = jnp.concatenate([lo, hi], axis=0)
-    return x
+        start = start - bit * span
+        span *= 2
+    return pieces
 
 
 def _block_start(axis, dists, rows):
@@ -73,7 +78,6 @@
     while d < n_mem:
         near_first.append(d)
         d *= 2
-    far_first = near_first[::-1]
 
     outs = []
     for l in range(n_lev):
@@ -83,21 +87,31 @@
         inc = jnp.sum(a.astype(jnp.float32) * fields, axis=0)
         prec = prec_t[l]
         if pow2:
-            dists = near_first if l % 2 == 0 else far_first
+            dists = near_first
             part = _reduce_scatter_rows(inc, "mem", n_mem, dists, jnp.bfloat16)
             start = _block_start("mem", dists, rows)
             w_blk = (lax.dynamic_slice_in_dim(prec, start, blk, 0) * part).astype(jnp.bfloat16)
-            weighted = _all_gather_rows(w_blk, "mem", n_mem, dists)
+            pieces = _all_gather_pieces(w_blk, start, "mem", n_mem, dists)
         else:
             weighted = (prec * lax.psum(inc, "mem")).astype(jnp.bfloat16)
-        scaled = (a.astype(jnp.float32) * weighted.astype(jnp.float32)[None]).astype(jnp.bfloat16)
-        projected = jnp.einsum(
-            "mrn,nc->mrc", scaled, col_factor, preferred_element_type=jnp.float32
-        ).astype(jnp.bfloat16)
-        proj_other = _swap(projected, "half")
-        summed = jnp.einsum(
-            "rk,mrc->mkc", rf_own, projected, preferred_element_type=jnp.float32
-        ) + jnp.einsum("rk,mrc->mkc", rf_for_partner, proj_other, preferred_element_type=jnp.float32)
+            pieces = [(weighted, 0)]
+        summed = None
+        for w, off in pieces:
+            n = w.shape[0]
+            a_p = lax.dynamic_slice_in_dim(a, off, n, 1)
+            scaled = (a_p.astype(jnp.float32) * w.astype(jnp.float32)[None]).astype(jnp.bfloat16)
+            projected = jnp.einsum(
+                "mrn,nc->mrc", scaled, col_factor, preferred_element_type=jnp.float32
+            ).astype(jnp.bfloat16)
+            proj_other = _swap(projected, "half")
+            part_sum = jnp.einsum(
+                "rk,mrc->mkc", lax.dynamic_slice_in_dim(rf_own, off, n, 0), projected,
+                preferred_element_type=jnp.float32,
+            ) + jnp.einsum(
+                "rk,mrc->mkc", lax.dynamic_slice_in_dim(rf_for_partner, off, n, 0), proj_other,
+                preferred_element_type=jnp.float32,
+            )
+            summed = part_sum if summed is None else summed + part_sum
         outs.append(summed)
     summed_all = jnp.transpose(jnp.stack(outs, axis=0), (2, 1, 0, 3))
     return (control.astype(jnp.float32) + summed_all).astype(jnp.bfloat16)

time: 49.2 us -> 52.2 us (1.061)
  waiting for transfers between devices: 18.5 us -> 13.8 us
  local copies, waits for them, and re-layouts: 9.95 us -> 13.6 us
  matrix products: 8.94 us -> 11.8 us
  starting transfers between devices: 10.8 us -> 11.8 us
    ppermute x2, waiting for transfers between devices: 7.04 us -> 3.43 us  [_reduce_scatter_rows(): recv = lax.ppermute(send.astype(wire), axis, _pairs(size, d))]
    ppermute x2, starting transfers between devices: 3.37 us -> 5.81 us  [_reduce_scatter_rows(): recv = lax.ppermute(x.astype(wire), axis, _pairs(size, dists[-1]))]
    ppermute x2, waiting for transfers between devices: 5.32 us -> 2.97 us  [_all_gather_pieces(): recv = lax.ppermute(x, axis, _pairs(size, d))]
    ppermute x2, starting transfers between devices: 5.37 us -> 3.18 us  [_reduce_scatter_rows(): recv = lax.ppermute(send.astype(wire), axis, _pairs(size, d))]
    dot_general x4 -> x8, matrix products: 3.93 us -> 5.62 us  [the longest x4 4.3 us: local(): jnp.einsum('rk,mrc->mkc', lax.dynamic_slice_in_dim(rf_for_partner, off, n...]
    dynamic_slice x2, local copies, waits for them, and re-layouts: 0.05 us -> 1.71 us  [local(): lax.dynamic_slice_in_dim(prec, start, blk, 0) * part]
    ppermute x2, waiting for transfers between devices: 5.77 us -> 7.41 us  [_reduce_scatter_rows(): recv = lax.ppermute(x.astype(wire), axis, _pairs(size, dists[-1]))]
    dot_general x1, matrix products: 0.56 us -> 1.69 us  [local(): jnp.einsum('rk,kmlc->lmrc', rf_own, control, preferred_element_type=jnp.f...]
  transfers between devices with their start and end apart: 10 -> 12, of which waited for: 7 -> 5; matrix products, arithmetic and copies ran while one was open for 24% -> 41% of each run, Pallas kernels for 0% -> 0%
where the time goes in v9:
time: 52.2 us; the launch traced here: 51.7 us
  waiting for transfers between devices  13.8 us (26%)
  local copies, waits for them, and re-layouts  13.6 us (26%)
  starting transfers between devices  11.8 us (23%)
  matrix products  11.8 us (23%)
    ppermute x2, waiting for transfers between devices, _reduce_scatter_rows(): recv = lax.ppermute(x.astype(wire), axis, _pairs(size, dists[-1]))  7.41 us
    unnamed x15, local copies, waits for them, and re-layouts  6.58 us
    ppermute x2, starting transfers between devices, _reduce_scatter_rows(): recv = lax.ppermute(x.astype(wire), axis, _pairs(size, dists[-1]))  5.81 us
    dot_general x4, matrix products, local(): jnp.einsum('rk,mrc->mkc', lax.dynamic_slice_in_dim(rf_for_partner, off, n...  4.3 us
    ppermute x2, waiting for transfers between devices, _reduce_scatter_rows(): recv = lax.ppermute(send.astype(wire), axis, _pairs(size, d))  3.43 us
    ppermute x2, starting transfers between devices, _reduce_scatter_rows(): recv = lax.ppermute(send.astype(wire), axis, _pairs(size, d))  3.18 us
    ppermute x2, waiting for transfers between devices, _all_gather_pieces(): recv = lax.ppermute(x, axis, _pairs(size, d))  2.97 us
    convert_element_type x1, local copies, waits for them, and re-layouts, local(): return (control.astype(jnp.float32) + summed_all).astype(jnp.bfloat16)  1.81 us
  transfers between devices with their start and end apart: 12, of which 5 were waited for; matrix products, arithmetic and copies ran while one was open for 41% of the time, Pallas kernels for 0%

profile of v9, /device:TPU:0, one launch (start us, length us, event | category | flops | bytes accessed | tf_op | source)
XLA Modules:
  0.0 51.7 jit_solution(13814843396169383707)
XLA Ops:
  0.0 1.6 %constant_dynamic-slice_fusion.1 = bf16[256,128]{1,0:T(8,128)(2,1)} fusion(bf16[256,256]{1,0:T(8,128)(2,1)} %param.8, s32[]{:T(128)S(6)} %select_n.63), kind=kLoop, calls=%fused_computation.92 | loop fusion | bytes 131076 | tf_op jit(solution)/shard_map/dynamic_slice | solution.py:66
  2.0 2.1 %copy.8 = bf16[128,6,2,256]{3,0,2,1:T(8,128)(2,1)} copy(bf16[128,6,2,256]{3,2,1,0:T(2,128)(2,1)} %param.6) | data formatting | bytes 1572864 | tf_op args[1]
  4.2 1.6 %fusion.78 = (f32[1,256,512]{2,0,1:T(1,128)S(1)}, f32[1,256,512]{2,0,1:T(1,128)}) fusion(f32[2,256,512]{2,0,1:T(2,128)S(1)} %bitcast.121), kind=kLoop, calls=%fused_computation.100 | loop fusion | bytes 2097152 | tf_op jit(solution)/shard_map/slice | solution.py:88
  5.9 0.7 %constant_dynamic-slice_fusion.2 = f32[1,128,512]{2,0,1:T(1,128)} fusion(f32[1,256,512]{2,0,1:T(1,128)S(1)} %get-tuple-element.11, s32[]{:T(128)S(6)} %select_n.61), kind=kLoop, calls=%fused_computation.94 | loop fusion | bytes 524292 | tf_op jit(solution)/shard_map/dynamic_slice | solution.py:93
  6.6 1.9 %copy.6 = bf16[128,6,2,256]{0,3,1,2:T(8,128)(2,1)} copy(bf16[128,6,2,256]{3,2,1,0:T(2,128)(2,1)S(1)} %copy-done.1) | data formatting | bytes 1572864 | tf_op args[1]
  8.4 2.6 %copy.38 = bf16[256,6,2,512]{3,0,1,2:T(8,128)(2,1)S(1)} copy(bf16[256,6,2,512]{3,2,1,0:T(2,128)(2,1)} %param.5) | data formatting | bytes 6291456 | tf_op args[0]
  11.0 1.0 %constant_dynamic-slice_fusion = f32[1,128,512]{2,0,1:T(1,128)S(1)} fusion(f32[1,256,512]{2,0,1:T(1,128)} %get-tuple-element.12, s32[]{:T(128)S(6)} %select_n.61), kind=kLoop, calls=%fused_computation.87 | loop fusion | bytes 524292 | tf_op jit(solution)/shard_map/dynamic_slice | solution.py:93
  12.0 1.7 %fusion.40 = f32[256,6,2,256]{3,0,2,1:T(8,128)S(1)} fusion(bf16[256,256]{1,0:T(8,128)(2,1)S(1)} %copy-done.5, s32[]{:T(128)S(6)} %select_n.62, bf16[128,6,2,256]{3,2,1,0:T(2,128)(2,1)} %param.6), kind=kOutput, calls=%fused_computation.61 | convolution fusion | flops 201326592 | bytes 3997700 | tf_op jit(solution)/shard_map/rk,kmlc->lmrc/dot_general | solution.py:70
  13.9 1.7 %fusion.8 = bf16[2,6,256,256]{3,2,0,1:T(8,128)(2,1)S(1)} fusion(f32[256,6,2,256]{3,0,2,1:T(8,128)S(1)} %fusion.40, bf16[128,6,2,256]{3,0,2,1:T(8,128)(2,1)} %collective-permute-done, bf16[256,128]{1,0:T(8,128)(2,1)} %constant_dynamic-slice_fusion.1), kind=kOutput, calls=%fused_computation.17 | convolution fusion | flops 202899456 | bytes 5570560 | tf_op jit(solution)/shard_map/rk,kmlc->lmrc/dot_general | solution.py:71
  15.7 0.6 %fusion = f32[256,512]{1,0:T(8,128)S(1)} fusion(bf16[2,6,256,256]{3,2,0,1:T(8,128)(2,1)S(1)} %fusion.8, bf16[512,256]{1,0:T(8,128)(2,1)S(1)} %copy-done, bf16[2,6,256,512]{3,2,1,0:T(8,128)(2,1)S(1)} %bitcast.119), kind=kOutput, calls=%fused_computation.1 | convolution fusion | flops 404881408 | bytes 3145728 | tf_op jit(solution)/shard_map/mrc,nc->mrn/dot_general | solution.py:86
  16.4 3.1 %collective-permute-start.7 = (bf16[128,512]{1,0:T(8,128)(2,1)S(1)}, bf16[128,512]{1,0:T(8,128)(2,1)S(1)}, u32[]{:S(2)}, u32[]{:S(2)}) collective-permute-start(bf16[128,512]{1,0:T(8,128)(2,1)S(1)} %dynamic-slice_convert_fusion), channel_id=1, source_target_pairs={{0,4},{4,0},{8,12},{12,8},{1,5},{5,1},{9,13},{13,9},{2,6},{6,2},{1... | collective-permute-start | bytes 393224 | tf_op jit(solution)/shard_map/ppermute | solution.py:22
  20.2 3.4 %collective-permute-done.7 = bf16[128,512]{1,0:T(8,128)(2,1)S(1)} collective-permute-done((bf16[128,512]{1,0:T(8,128)(2,1)S(1)}, bf16[128,512]{1,0:T(8,128)(2,1)S(1)}, u32[]{:S(2)}, u32[]{:S(2)}) %collective-permute-start.7) | collective-permute-done | bytes 131104 | tf_op jit(solution)/shard_map/ppermute | solution.py:22
  23.7 3.0 %collective-permute-start.8 = (bf16[128,512]{1,0:T(8,128)(2,1)S(1)}, bf16[128,512]{1,0:T(8,128)(2,1)S(1)}, u32[]{:S(2)}, u32[]{:S(2)}) collective-permute-start(bf16[128,512]{1,0:T(8,128)(2,1)S(1)} %fusion.38), channel_id=1, source_target_pairs={{0,8},{4,12},{8,0},{12,4},{1,9},{5,13},{9,1},{13,5},{2,10},{6,14},... | collective-permute-start | bytes 393224 | tf_op jit(solution)/shard_map/ppermute | solution.py:25
  26.8 2.8 %collective-permute-start.2 = (bf16[128,512]{1,0:T(8,128)(2,1)S(1)}, bf16[128,512]{1,0:T(8,128)(2,1)S(1)}, u32[]{:S(2)}, u32[]{:S(2)}) collective-permute-start(bf16[128,512]{1,0:T(8,128)(2,1)S(1)} %fusion.37), channel_id=1, source_target_pairs={{0,8},{4,12},{8,0},{12,4},{1,9},{5,13},{9,1},{13,5},{2,10},{6,14},... | collective-permute-start | bytes 393224 | tf_op jit(solution)/shard_map/ppermute | solution.py:25
  29.5 6.3 %collective-permute-done.8 = bf16[128,512]{1,0:T(8,128)(2,1)S(1)} collective-permute-done((bf16[128,512]{1,0:T(8,128)(2,1)S(1)}, bf16[128,512]{1,0:T(8,128)(2,1)S(1)}, u32[]{:S(2)}, u32[]{:S(2)}) %collective-permute-start.8) | collective-permute-done | bytes 131104 | tf_op jit(solution)/shard_map/ppermute | solution.py:25
  36.0 0.6 %collective-permute-start.10 = (bf16[128,512]{1,0:T(8,128)(2,1)S(1)}, bf16[128,512]{1,0:T(8,128)(2,1)S(1)}, u32[]{:S(2)}, u32[]{:S(2)}) collective-permute-start(bf16[128,512]{1,0:T(8,128)(2,1)S(1)} %get-tuple-element.8), channel_id=1, source_target_pairs={{0,4},{4,0},{8,12},{12,8},{1,5},{5,1},{9,13},{13,9},{2,6},{6,2},{1... | collective-permute-start | bytes 393224 | tf_op jit(solution)/shard_map/ppermute | solution.py:36
  36.6 1.1 %collective-permute-done.2 = bf16[128,512]{1,0:T(8,128)(2,1)S(1)} collective-permute-done((bf16[128,512]{1,0:T(8,128)(2,1)S(1)}, bf16[128,512]{1,0:T(8,128)(2,1)S(1)}, u32[]{:S(2)}, u32[]{:S(2)}) %collective-permute-start.2) | collective-permute-done | bytes 131104 | tf_op jit(solution)/shard_map/ppermute | solution.py:25
  40.3 2.0 %collective-permute-done.10 = bf16[128,512]{1,0:T(8,128)(2,1)S(1)} collective-permute-done((bf16[128,512]{1,0:T(8,128)(2,1)S(1)}, bf16[128,512]{1,0:T(8,128)(2,1)S(1)}, u32[]{:S(2)}, u32[]{:S(2)}) %collective-permute-start.10) | collective-permute-done | bytes 131104 | tf_op jit(solution)/shard_map/ppermute | solution.py:36
  42.7 1.0 %collective-permute-done.5 = bf16[128,512]{1,0:T(8,128)(2,1)S(1)} collective-permute-done((bf16[128,512]{1,0:T(8,128)(2,1)S(1)}, bf16[128,512]{1,0:T(8,128)(2,1)S(1)}, u32[]{:S(2)}, u32[]{:S(2)}) %collective-permute-start.5) | collective-permute-done | bytes 131104 | tf_op jit(solution)/shard_map/ppermute | solution.py:36
  45.4 1.1 %convolution_add_fusion.1 = f32[6,256,128]{2,1,0:T(8,128)S(1)} fusion(f32[6,256,128]{2,1,0:T(8,128)S(1)} %fusion.51, bf16[6,128,256]{2,1,0:T(8,128)(2,1)S(1)} %collective-permute-done.9, bf16[256,128]{1,0:T(8,128)(2,1)} %collective-permute-done.4, s32[]{:T(128)S(6)} %select_n.61), kind=kOutput, calls=%fused_computation.21 | convolution fusion | flops 50528256 | bytes 1998852 | tf_op jit(solution)/shard_map/rk,mrc->mkc/dot_general | solution.py:110
  46.4 1.1 %convolution_add_fusion.3 = f32[6,256,128]{2,1,0:T(8,128)S(1)} fusion(f32[6,256,128]{2,1,0:T(8,128)S(1)} %fusion.53, bf16[6,128,256]{2,1,0:T(8,128)(2,1)S(1)} %collective-permute-done.3, bf16[256,128]{1,0:T(8,128)(2,1)} %collective-permute-done.4, s32[]{:T(128)S(6)} %select_n.61), kind=kOutput, calls=%fused_computation.25 | convolution fusion | flops 50528256 | bytes 1998852 | tf_op jit(solution)/shard_map/rk,mrc->mkc/dot_general | solution.py:110
  47.5 1.1 %fusion.10 = f32[1,6,128,256]{2,3,1,0:T(8,128)S(1)} fusion(f32[6,256,128]{2,1,0:T(8,128)S(1)} %convolution_add_fusion.1, f32[6,256,128]{2,1,0:T(8,128)S(1)} %fusion.45, bf16[6,128,256]{2,1,0:T(8,128)(2,1)S(1)} %collective-permute-done.11, bf16[256,128]{1,0:T(8,128)(2,1)} %collective-permute-done.4, s32[]{:T(128)S(6)} %select_n.67), kind=kOutput, calls=%fused_computation.20 | convolution fusion | flops 50724864 | bytes 2785284 | tf_op jit(solution)/shard_map/rk,mrc->mkc/dot_general | solution.py:110
  48.6 1.1 %fusion.12 = f32[1,6,128,256]{2,3,1,0:T(8,128)S(1)} fusion(f32[6,256,128]{2,1,0:T(8,128)S(1)} %convolution_add_fusion.3, f32[6,256,128]{2,1,0:T(8,128)S(1)} %fusion.47, bf16[6,128,256]{2,1,0:T(8,128)(2,1)S(1)} %collective-permute-done.6, bf16[256,128]{1,0:T(8,128)(2,1)} %collective-permute-done.4, s32[]{:T(128)S(6)} %select_n.67), kind=kOutput, calls=%fused_computation.24 | convolution fusion | flops 50724864 | bytes 2785284 | tf_op jit(solution)/shard_map/rk,mrc->mkc/dot_general | solution.py:110
  49.9 1.8 %copy.18 = bf16[128,6,2,256]{3,2,1,0:T(2,128)(2,1)} copy(bf16[128,6,2,256]{0,3,1,2:T(8,128)(2,1)S(1)} %fusion.3) | data formatting | bytes 1572864 | tf_op jit(solution)/shard_map/convert_element_type | solution.py:117
  (46 shorter events, 6.5 us)
Async XLA Ops:
  0.0 15.7 %copy-start = (bf16[512,256]{1,0:T(8,128)(2,1)S(1)}, bf16[512,256]{1,0:T(8,128)(2,1)}, u32[]{:S(2)}) copy-start(bf16[512,256]{1,0:T(8,128)(2,1)} %param.9) | copy-start | bytes 786436
  0.0 4.2 %copy-start.3 = (f32[256,2,512]{2,1,0:T(2,128)S(1)}, f32[256,2,512]{2,1,0:T(2,128)}, u32[]{:S(2)}) copy-start(f32[256,2,512]{2,1,0:T(2,128)} %param.7) | copy-start | bytes 3145732
  1.6 43.8 %collective-permute-start.4 = (bf16[256,128]{1,0:T(8,128)(2,1)}, bf16[256,128]{1,0:T(8,128)(2,1)}, u32[]{:S(2)}, u32[]{:S(2)}) collective-permute-start(bf16[256,128]{1,0:T(8,128)(2,1)} %constant_dynamic-slice_fusion.1), channel_id=1, source_target_pairs={{0,1},{1,0},{2,3},{3,2},{4,5},{5,4},{6,7},{7,6},{8,9},{9,8},{10,11... | collective-permute-start | bytes 196616 | tf_op jit(solution)/shard_map/ppermute | solution.py:8
  4.2 2.4 %copy-start.1 = (bf16[128,6,2,256]{3,2,1,0:T(2,128)(2,1)S(1)}, bf16[128,6,2,256]{3,2,1,0:T(2,128)(2,1)}, u32[]{:S(2)}) copy-start(bf16[128,6,2,256]{3,2,1,0:T(2,128)(2,1)} %param.6) | copy-start | bytes 2359300
  4.2 9.8 %collective-permute-start = (bf16[128,6,2,256]{3,0,2,1:T(8,128)(2,1)}, bf16[128,6,2,256]{3,0,2,1:T(8,128)(2,1)}, u32[]{:S(2)}, u32[]{:S(2)}) collective-permute-start(bf16[128,6,2,256]{3,0,2,1:T(8,128)(2,1)} %copy.8), channel_id=1, source_target_pairs={{0,1},{1,0},{2,3},{3,2},{4,5},{5,4},{6,7},{7,6},{8,9},{9,8},{10,11... | collective-permute-start | bytes 2359304 | tf_op jit(solution)/shard_map/ppermute | solution.py:8
  8.4 3.6 %copy-start.5 = (bf16[256,256]{1,0:T(8,128)(2,1)S(1)}, bf16[256,256]{1,0:T(8,128)(2,1)}, u32[]{:S(2)}) copy-start(bf16[256,256]{1,0:T(8,128)(2,1)} %param.8) | copy-start | bytes 393220
  16.4 7.3 %collective-permute-start.7 = (bf16[128,512]{1,0:T(8,128)(2,1)S(1)}, bf16[128,512]{1,0:T(8,128)(2,1)S(1)}, u32[]{:S(2)}, u32[]{:S(2)}) collective-permute-start(bf16[128,512]{1,0:T(8,128)(2,1)S(1)} %dynamic-slice_convert_fusion), channel_id=1, source_target_pairs={{0,4},{4,0},{8,12},{12,8},{1,5},{5,1},{9,13},{13,9},{2,6},{6,2},{1... | collective-permute-start | bytes 393224 | tf_op jit(solution)/shard_map/ppermute | solution.py:22
  20.1 17.6 %copy-start.4 = (f32[1,128,512]{2,0,1:T(1,128)S(1)}, f32[1,128,512]{2,0,1:T(1,128)}, u32[]{:S(2)}) copy-start(f32[1,128,512]{2,0,1:T(1,128)} %constant_dynamic-slice_fusion.2) | copy-start | bytes 786436
  20.1 6.6 %collective-permute-start.1 = (bf16[128,512]{1,0:T(8,128)(2,1)S(1)}, bf16[128,512]{1,0:T(8,128)(2,1)S(1)}, u32[]{:S(2)}, u32[]{:S(2)}) collective-permute-start(bf16[128,512]{1,0:T(8,128)(2,1)S(1)} %dynamic-slice_convert_fusion.1), channel_id=1, source_target_pairs={{0,4},{4,0},{8,12},{12,8},{1,5},{5,1},{9,13},{13,9},{2,6},{6,2},{1... | collective-permute-start | bytes 393224 | tf_op jit(solution)/shard_map/ppermute | solution.py:22
  23.7 12.2 %collective-permute-start.8 = (bf16[128,512]{1,0:T(8,128)(2,1)S(1)}, bf16[128,512]{1,0:T(8,128)(2,1)S(1)}, u32[]{:S(2)}, u32[]{:S(2)}) collective-permute-start(bf16[128,512]{1,0:T(8,128)(2,1)S(1)} %fusion.38), channel_id=1, source_target_pairs={{0,8},{4,12},{8,0},{12,4},{1,9},{5,13},{9,1},{13,5},{2,10},{6,14},... | collective-permute-start | bytes 393224 | tf_op jit(solution)/shard_map/ppermute | solution.py:25
  26.8 10.9 %collective-permute-start.2 = (bf16[128,512]{1,0:T(8,128)(2,1)S(1)}, bf16[128,512]{1,0:T(8,128)(2,1)S(1)}, u32[]{:S(2)}, u32[]{:S(2)}) collective-permute-start(bf16[128,512]{1,0:T(8,128)(2,1)S(1)} %fusion.37), channel_id=1, source_target_pairs={{0,8},{4,12},{8,0},{12,4},{1,9},{5,13},{9,1},{13,5},{2,10},{6,14},... | collective-permute-start | bytes 393224 | tf_op jit(solution)/shard_map/ppermute | solution.py:25
  36.0 6.3 %collective-permute-start.10 = (bf16[128,512]{1,0:T(8,128)(2,1)S(1)}, bf16[128,512]{1,0:T(8,128)(2,1)S(1)}, u32[]{:S(2)}, u32[]{:S(2)}) collective-permute-start(bf16[128,512]{1,0:T(8,128)(2,1)S(1)} %get-tuple-element.8), channel_id=1, source_target_pairs={{0,4},{4,0},{8,12},{12,8},{1,5},{5,1},{9,13},{13,9},{2,6},{6,2},{1... | collective-permute-start | bytes 393224 | tf_op jit(solution)/shard_map/ppermute | solution.py:36
  37.7 5.9 %collective-permute-start.5 = (bf16[128,512]{1,0:T(8,128)(2,1)S(1)}, bf16[128,512]{1,0:T(8,128)(2,1)S(1)}, u32[]{:S(2)}, u32[]{:S(2)}) collective-permute-start(bf16[128,512]{1,0:T(8,128)(2,1)S(1)} %get-tuple-element.6), channel_id=1, source_target_pairs={{0,4},{4,0},{8,12},{12,8},{1,5},{5,1},{9,13},{13,9},{2,6},{6,2},{1... | collective-permute-start | bytes 393224 | tf_op jit(solution)/shard_map/ppermute | solution.py:36
  38.6 7.8 %collective-permute-start.3 = (bf16[6,128,256]{2,1,0:T(8,128)(2,1)S(1)}, bf16[6,128,256]{2,1,0:T(8,128)(2,1)S(1)}, u32[]{:S(2)}, u32[]{:S(2)}) collective-permute-start(bf16[6,128,256]{2,1,0:T(8,128)(2,1)S(1)} %convolution_convert_fusion.3), channel_id=1, source_target_pairs={{0,1},{1,0},{2,3},{3,2},{4,5},{5,4},{6,7},{7,6},{8,9},{9,8},{10,11... | collective-permute-start | bytes 1179656 | tf_op jit(solution)/shard_map/ppermute | solution.py:8
  39.1 6.3 %collective-permute-start.9 = (bf16[6,128,256]{2,1,0:T(8,128)(2,1)S(1)}, bf16[6,128,256]{2,1,0:T(8,128)(2,1)S(1)}, u32[]{:S(2)}, u32[]{:S(2)}) collective-permute-start(bf16[6,128,256]{2,1,0:T(8,128)(2,1)S(1)} %convolution_convert_fusion.1), channel_id=1, source_target_pairs={{0,1},{1,0},{2,3},{3,2},{4,5},{5,4},{6,7},{7,6},{8,9},{9,8},{10,11... | collective-permute-start | bytes 1179656 | tf_op jit(solution)/shard_map/ppermute | solution.py:8
  44.1 4.5 %collective-permute-start.6 = (bf16[6,128,256]{2,1,0:T(8,128)(2,1)S(1)}, bf16[6,128,256]{2,1,0:T(8,128)(2,1)S(1)}, u32[]{:S(2)}, u32[]{:S(2)}) collective-permute-start(bf16[6,128,256]{2,1,0:T(8,128)(2,1)S(1)} %convolution_convert_fusion.2), channel_id=1, source_target_pairs={{0,1},{1,0},{2,3},{3,2},{4,5},{5,4},{6,7},{7,6},{8,9},{9,8},{10,11... | collective-permute-start | bytes 1179656 | tf_op jit(solution)/shard_map/ppermute | solution.py:8
  44.2 3.3 %collective-permute-start.11 = (bf16[6,128,256]{2,1,0:T(8,128)(2,1)S(1)}, bf16[6,128,256]{2,1,0:T(8,128)(2,1)S(1)}, u32[]{:S(2)}, u32[]{:S(2)}) collective-permute-start(bf16[6,128,256]{2,1,0:T(8,128)(2,1)S(1)} %convolution_convert_fusion), channel_id=1, source_target_pairs={{0,1},{1,0},{2,3},{3,2},{4,5},{5,4},{6,7},{7,6},{8,9},{9,8},{10,11... | collective-permute-start | bytes 1179656 | tf_op jit(solution)/shard_map/ppermute | solution.py:8
  48.6 1.2 %copy-start.2 = (bf16[128,6,2,256]{0,3,1,2:T(8,128)(2,1)S(1)}, bf16[128,6,2,256]{0,3,1,2:T(8,128)(2,1)}, u32[]{:S(2)}) copy-start(bf16[128,6,2,256]{0,3,1,2:T(8,128)(2,1)} %copy.6) | copy-start | bytes 2359300

commit v10 on v6

--- a/solution.py
+++ b/solution.py
@@ -88,13 +88,19 @@
         projected = jnp.einsum(
             "mrn,nc->mrc", scaled, col_factor, preferred_element_type=jnp.float32
         ).astype(jnp.bfloat16)
-        proj_other = _swap(projected, "half")
-        summed = jnp.einsum(
-            "rk,mrc->mkc", rf_own, projected, preferred_element_type=jnp.float32
-        ) + jnp.einsum("rk,mrc->mkc", rf_for_partner, proj_other, preferred_element_type=jnp.float32)
-        outs.append(summed)
-    summed_all = jnp.transpose(jnp.stack(outs, axis=0), (2, 1, 0, 3))
-    return (control.astype(jnp.float32) + summed_all).astype(jnp.bfloat16)
+        n_m = projected.shape[0]
+        mh = n_m // 2
+        chunks = [(0, mh), (mh, n_m)] if mh > 0 else [(0, n_m)]
+        summed = jnp.einsum("rk,mrc->kmc", rf_own, projected, preferred_element_type=jnp.float32)
+        other = []
+        for lo, hi in chunks:
+            proj_other = _swap(projected[lo:hi], "half")
+            other.append(jnp.einsum(
+                "rk,mrc->kmc", rf_for_partner, proj_other, preferred_element_type=jnp.float32
+            ))
+        summed = summed + jnp.concatenate(other, axis=1)
+        outs.append(control[:, :, l, :].astype(jnp.float32) + summed)
+    return jnp.stack(outs, axis=2).astype(jnp.bfloat16)
 
 
 def solution(mesh):

time: 47.1 us -> 46.8 us (level)
  matrix products: 8.93 us -> 5.13 us
  local copies, waits for them, and re-layouts: 9.95 us -> 13.2 us
  starting transfers between devices: 10.4 us -> 11.8 us
  waiting for transfers between devices: 16.8 us -> 15.8 us
    dot_general x4 -> x6, matrix products: 3.92 us -> 1.52 us  [the longest x4 0.91 us: local(): jnp.einsum('rk,mrc->kmc', rf_for_partner, proj_other, preferred_element_t...]
    convert_element_type x1 -> x0, local copies, waits for them, and re-layouts: 1.81 us -> none  [local(): return (control.astype(jnp.float32) + summed_all).astype(jnp.bfloat16)]
    another operation x0 -> x1, local copies, waits for them, and re-layouts: none -> 1.69 us  [local(): return jnp.stack(outs, axis=2).astype(jnp.bfloat16)]
    slice x1, local copies, waits for them, and re-layouts: 0.81 us -> 2.48 us  [local(): prec = prec_t[l]]
    dot_general x1, matrix products: 1.88 us -> 0.57 us  [local(): jnp.einsum('rk,kmlc->lmrc', rf_other, ctrl_other, preferred_element_type=...]
    slice x0 -> x3, local copies, waits for them, and re-layouts: none -> 1.2 us  [the longest x1 1.09 us: local(): outs.append(control[:, :, l, :].astype(jnp.float32) + summed)]
    ppermute x2, waiting for transfers between devices: 8.54 us -> 7.42 us  [_reduce_scatter_rows(): recv = lax.ppermute(x.astype(wire), axis, [(i, i ^ d) for i in range(size)])]
    ppermute x4 -> x6, starting transfers between devices: 1.16 us -> 1.71 us  [_swap(): return lax.ppermute(x, axis, [(0, 1), (1, 0)])]
  transfers between devices with their start and end apart: 10 -> 12, of which waited for: 6 -> 8; matrix products, arithmetic and copies ran while one was open for 25% -> 30% of each run, Pallas kernels for 0% -> 0%
where the time goes in v10:
time: 46.8 us; the launch traced here: 46.6 us
  waiting for transfers between devices  15.8 us (34%)
  local copies, waits for them, and re-layouts  13.2 us (28%)
  starting transfers between devices  11.8 us (25%)
  matrix products  5.13 us (11%)
    ppermute x2, waiting for transfers between devices, _reduce_scatter_rows(): recv = lax.ppermute(x.astype(wire), axis, [(i, i ^ d) for i in range(size)])  7.42 us
    unnamed x10, local copies, waits for them, and re-layouts  6.87 us
    ppermute x2, starting transfers between devices, _reduce_scatter_rows(): recv = lax.ppermute(x.astype(wire), axis, [(i, i ^ d) for i in range(size)])  5.8 us
    ppermute x2, waiting for transfers between devices, _all_gather_rows(): recv = lax.ppermute(x, axis, [(i, i ^ d) for i in range(size)])  4.17 us
    ppermute x2, waiting for transfers between devices, _reduce_scatter_rows(): lax.ppermute(send.astype(wire), axis, [(i, i ^ d) for i in range(size)])  3.42 us
    ppermute x2, starting transfers between devices, _reduce_scatter_rows(): lax.ppermute(send.astype(wire), axis, [(i, i ^ d) for i in range(size)])  3.17 us
    slice x1, local copies, waits for them, and re-layouts, local(): prec = prec_t[l]  2.48 us
    ppermute x6, starting transfers between devices, _swap(): return lax.ppermute(x, axis, [(0, 1), (1, 0)])  1.71 us
  transfers between devices with their start and end apart: 12, of which 8 were waited for; matrix products, arithmetic and copies ran while one was open for 30% of the time, Pallas kernels for 0%

profile of v10, /device:TPU:0, one launch (start us, length us, event | category | flops | bytes accessed | tf_op | source)
XLA Modules:
  0.0 46.6 jit_solution(8455755346810647707)
XLA Ops:
  0.0 1.3 %copy.8 = bf16[128,6,2,256]{3,0,2,1:T(8,128)(2,1)S(1)} copy(bf16[128,6,2,256]{3,2,1,0:T(2,128)(2,1)} %param.6) | data formatting | bytes 1572864 | tf_op args[1]
  1.3 0.5 %collective-permute-start = (bf16[128,6,2,256]{3,0,2,1:T(8,128)(2,1)S(1)}, bf16[128,6,2,256]{3,0,2,1:T(8,128)(2,1)S(1)}, u32[]{:S(2)}, u32[]{:S(2)}) collective-permute-start(bf16[128,6,2,256]{3,0,2,1:T(8,128)(2,1)S(1)} %copy.8), channel_id=1, source_target_pairs={{0,1},{1,0},{2,3},{3,2},{4,5},{5,4},{6,7},{7,6},{8,9},{9,8},{10,11... | collective-permute-start | bytes 2359304 | tf_op jit(solution)/shard_map/ppermute | solution.py:8
  1.8 0.8 %constant_dynamic-slice_fusion.1 = bf16[256,128]{1,0:T(8,128)(2,1)S(1)} fusion(bf16[256,256]{1,0:T(8,128)(2,1)} %param.8, s32[]{:T(128)S(6)} %select_n.61), kind=kLoop, calls=%fused_computation.73 | loop fusion | bytes 131076 | tf_op jit(solution)/shard_map/dynamic_slice | solution.py:62
  2.7 2.5 %fusion.57 = (f32[1,256,512]{2,0,1:T(1,128)S(1)}, f32[1,256,512]{2,0,1:T(1,128)S(1)}) fusion(f32[2,256,512]{2,0,1:T(2,128)} %bitcast.102), kind=kLoop, calls=%fused_computation.77 | loop fusion | bytes 2097152 | tf_op jit(solution)/shard_map/slice | solution.py:80
  5.3 4.3 %copy.47 = bf16[256,6,2,512]{3,0,1,2:T(8,128)(2,1)} copy(bf16[256,6,2,512]{3,2,1,0:T(2,128)(2,1)} %param.5) | data formatting | bytes 6291456 | tf_op args[0]
  9.6 1.1 %fusion.58 = (bf16[128,6,1,256]{3,2,1,0:T(2,128)(2,1)S(1)}, bf16[128,6,1,256]{3,2,1,0:T(2,128)(2,1)S(1)}) fusion(bf16[128,6,2,256]{3,2,1,0:T(2,128)(2,1)S(1)} %copy-done.1), kind=kLoop, calls=%fused_computation.78 | loop fusion | bytes 1572864 | tf_op jit(solution)/shard_map/slice | solution.py:102
  10.7 0.6 %fusion.32 = f32[256,6,2,256]{3,0,2,1:T(8,128)S(1)} fusion(bf16[256,256]{1,0:T(8,128)(2,1)S(1)} %copy-done.3, s32[]{:T(128)S(6)} %select_n.57, bf16[128,6,2,256]{3,2,1,0:T(2,128)(2,1)S(1)} %copy-done.1), kind=kOutput, calls=%fused_computation.53 | convolution fusion | flops 201326592 | bytes 3997700 | tf_op jit(solution)/shard_map/rk,kmlc->lmrc/dot_general | solution.py:66
  11.3 0.6 %fusion.10 = bf16[2,6,256,256]{3,2,0,1:T(8,128)(2,1)S(1)} fusion(f32[256,6,2,256]{3,0,2,1:T(8,128)S(1)} %fusion.32, bf16[128,6,2,256]{3,0,2,1:T(8,128)(2,1)S(1)} %collective-permute-done, bf16[256,128]{1,0:T(8,128)(2,1)S(1)} %constant_dynamic-slice_fusion.1), kind=kOutput, calls=%fused_computation.16 | convolution fusion | flops 202899456 | bytes 5570560 | tf_op jit(solution)/shard_map/rk,kmlc->lmrc/dot_general | solution.py:67
  11.8 1.3 %copy-done.2 = bf16[256,6,2,512]{3,0,1,2:T(8,128)(2,1)S(1)} copy-done((bf16[256,6,2,512]{3,0,1,2:T(8,128)(2,1)S(1)}, bf16[256,6,2,512]{3,0,1,2:T(8,128)(2,1)}, u32[]{:S(2)}) %copy-start.2) | copy-done | bytes 3145752
  13.1 0.7 %fusion = f32[256,512]{1,0:T(8,128)S(1)} fusion(bf16[2,6,256,512]{3,2,1,0:T(8,128)(2,1)S(1)} %bitcast.98, bf16[2,6,256,256]{3,2,0,1:T(8,128)(2,1)S(1)} %fusion.10, bf16[512,256]{1,0:T(8,128)(2,1)S(1)} %copy-done), kind=kOutput, calls=%fused_computation.4 | convolution fusion | flops 404881408 | bytes 3145728 | tf_op jit(solution)/shard_map/mrc,nc->mrn/dot_general | solution.py:78
  13.8 3.1 %collective-permute-start.1 = (bf16[128,512]{1,0:T(8,128)(2,1)S(1)}, bf16[128,512]{1,0:T(8,128)(2,1)S(1)}, u32[]{:S(2)}, u32[]{:S(2)}) collective-permute-start(bf16[128,512]{1,0:T(8,128)(2,1)S(1)} %dynamic-slice_convert_fusion.1), channel_id=1, source_target_pairs={{0,4},{4,0},{8,12},{12,8},{1,5},{5,1},{9,13},{13,9},{2,6},{6,2},{1... | collective-permute-start | bytes 393224 | tf_op jit(solution)/shard_map/ppermute | solution.py:19
  16.9 0.7 %fusion.2 = f32[256,512]{1,0:T(8,128)S(1)} fusion(bf16[2,6,256,512]{3,2,1,0:T(8,128)(2,1)S(1)} %bitcast.99, bf16[2,6,256,256]{3,2,0,1:T(8,128)(2,1)S(1)} %fusion.10, bf16[512,256]{1,0:T(8,128)(2,1)S(1)} %copy-done), kind=kOutput, calls=%fused_computation.6 | convolution fusion | flops 404881408 | bytes 3145728 | tf_op jit(solution)/shard_map/mrc,nc->mrn/dot_general | solution.py:78
  17.7 3.4 %collective-permute-done.1 = bf16[128,512]{1,0:T(8,128)(2,1)S(1)} collective-permute-done((bf16[128,512]{1,0:T(8,128)(2,1)S(1)}, bf16[128,512]{1,0:T(8,128)(2,1)S(1)}, u32[]{:S(2)}, u32[]{:S(2)}) %collective-permute-start.1) | collective-permute-done | bytes 131104 | tf_op jit(solution)/shard_map/ppermute | solution.py:19
  21.2 3.0 %collective-permute-start.2 = (bf16[128,512]{1,0:T(8,128)(2,1)S(1)}, bf16[128,512]{1,0:T(8,128)(2,1)S(1)}, u32[]{:S(2)}, u32[]{:S(2)}) collective-permute-start(bf16[128,512]{1,0:T(8,128)(2,1)S(1)} %fusion.29), channel_id=1, source_target_pairs={{0,8},{4,12},{8,0},{12,4},{1,9},{5,13},{9,1},{13,5},{2,10},{6,14},... | collective-permute-start | bytes 393224 | tf_op jit(solution)/shard_map/ppermute | solution.py:23
  24.2 2.8 %collective-permute-start.8 = (bf16[128,512]{1,0:T(8,128)(2,1)S(1)}, bf16[128,512]{1,0:T(8,128)(2,1)S(1)}, u32[]{:S(2)}, u32[]{:S(2)}) collective-permute-start(bf16[128,512]{1,0:T(8,128)(2,1)S(1)} %fusion.30), channel_id=1, source_target_pairs={{0,8},{4,12},{8,0},{12,4},{1,9},{5,13},{9,1},{13,5},{2,10},{6,14},... | collective-permute-start | bytes 393224 | tf_op jit(solution)/shard_map/ppermute | solution.py:23
  27.0 6.4 %collective-permute-done.2 = bf16[128,512]{1,0:T(8,128)(2,1)S(1)} collective-permute-done((bf16[128,512]{1,0:T(8,128)(2,1)S(1)}, bf16[128,512]{1,0:T(8,128)(2,1)S(1)}, u32[]{:S(2)}, u32[]{:S(2)}) %collective-permute-start.2) | collective-permute-done | bytes 131104 | tf_op jit(solution)/shard_map/ppermute | solution.py:23
  33.4 0.6 %collective-permute-start.3 = (bf16[128,512]{1,0:T(8,128)(2,1)S(1)}, bf16[128,512]{1,0:T(8,128)(2,1)S(1)}, u32[]{:S(2)}, u32[]{:S(2)}) collective-permute-start(bf16[128,512]{1,0:T(8,128)(2,1)S(1)} %fusion.24), channel_id=1, source_target_pairs={{0,4},{4,0},{8,12},{12,8},{1,5},{5,1},{9,13},{13,9},{2,6},{6,2},{1... | collective-permute-start | bytes 393224 | tf_op jit(solution)/shard_map/ppermute | solution.py:33
  34.1 1.1 %collective-permute-done.8 = bf16[128,512]{1,0:T(8,128)(2,1)S(1)} collective-permute-done((bf16[128,512]{1,0:T(8,128)(2,1)S(1)}, bf16[128,512]{1,0:T(8,128)(2,1)S(1)}, u32[]{:S(2)}, u32[]{:S(2)}) %collective-permute-start.8) | collective-permute-done | bytes 131104 | tf_op jit(solution)/shard_map/ppermute | solution.py:23
  35.7 4.1 %collective-permute-done.3 = bf16[128,512]{1,0:T(8,128)(2,1)S(1)} collective-permute-done((bf16[128,512]{1,0:T(8,128)(2,1)S(1)}, bf16[128,512]{1,0:T(8,128)(2,1)S(1)}, u32[]{:S(2)}, u32[]{:S(2)}) %collective-permute-start.3) | collective-permute-done | bytes 131104 | tf_op jit(solution)/shard_map/ppermute | solution.py:33
  39.8 0.6 %fusion.11 = bf16[6,256,256]{2,1,0:T(8,128)(2,1)S(1)} fusion(f32[256,512]{1,0:T(8,128)S(1)} %maximum_convert_fusion, bf16[2,6,256,512]{3,2,1,0:T(8,128)(2,1)S(1)} %bitcast.100, bf16[512,256]{1,0:T(8,128)(2,1)S(1)} %copy-done), kind=kOutput, calls=%fused_computation.17 | convolution fusion | flops 405405696 | bytes 3145728 | tf_op jit(solution)/shard_map/mrn,nc->mrc/dot_general | solution.py:88
  40.6 0.5 %collective-permute-start.6 = (bf16[3,256,256]{2,1,0:T(8,128)(2,1)S(1)}, bf16[3,256,256]{2,1,0:T(8,128)(2,1)S(1)}, u32[]{:S(2)}, u32[]{:S(2)}) collective-permute-start(bf16[3,256,256]{2,1,0:T(8,128)(2,1)S(1)} %get-tuple-element.10), channel_id=1, source_target_pairs={{0,1},{1,0},{2,3},{3,2},{4,5},{5,4},{6,7},{7,6},{8,9},{9,8},{10,11... | collective-permute-start | bytes 1179656 | tf_op jit(solution)/shard_map/ppermute | solution.py:8
  41.2 0.6 %fusion.14 = bf16[6,256,256]{2,1,0:T(8,128)(2,1)S(1)} fusion(f32[256,512]{1,0:T(8,128)S(1)} %maximum_convert_fusion.1, bf16[2,6,256,512]{3,2,1,0:T(8,128)(2,1)S(1)} %bitcast.101, bf16[512,256]{1,0:T(8,128)(2,1)S(1)} %copy-done), kind=kOutput, calls=%fused_computation.18 | convolution fusion | flops 405405696 | bytes 3145728 | tf_op jit(solution)/shard_map/mrn,nc->mrc/dot_general | solution.py:88
  42.0 0.5 %collective-permute-start.11 = (bf16[3,256,256]{2,1,0:T(8,128)(2,1)S(1)}, bf16[3,256,256]{2,1,0:T(8,128)(2,1)S(1)}, u32[]{:S(2)}, u32[]{:S(2)}) collective-permute-start(bf16[3,256,256]{2,1,0:T(8,128)(2,1)S(1)} %get-tuple-element.12), channel_id=1, source_target_pairs={{0,1},{1,0},{2,3},{3,2},{4,5},{5,4},{6,7},{7,6},{8,9},{9,8},{10,11... | collective-permute-start | bytes 1179656 | tf_op jit(solution)/shard_map/ppermute | solution.py:8
  44.9 1.7 %copy.17 = bf16[128,6,2,256]{3,2,1,0:T(2,128)(2,1)} copy(bf16[128,6,2,256]{3,0,1,2:T(8,128)(2,1)S(1)} %pad_maximum_fusion) | data formatting | bytes 1572864 | tf_op jit(solution)/shard_map/stack | solution.py:103
  (41 shorter events, 3.8 us)
Async XLA Ops:
  0.0 11.8 %copy-start = (bf16[512,256]{1,0:T(8,128)(2,1)S(1)}, bf16[512,256]{1,0:T(8,128)(2,1)}, u32[]{:S(2)}) copy-start(bf16[512,256]{1,0:T(8,128)(2,1)} %param.9) | copy-start | bytes 786436
  1.3 10.0 %collective-permute-start = (bf16[128,6,2,256]{3,0,2,1:T(8,128)(2,1)S(1)}, bf16[128,6,2,256]{3,0,2,1:T(8,128)(2,1)S(1)}, u32[]{:S(2)}, u32[]{:S(2)}) collective-permute-start(bf16[128,6,2,256]{3,0,2,1:T(8,128)(2,1)S(1)} %copy.8), channel_id=1, source_target_pairs={{0,1},{1,0},{2,3},{3,2},{4,5},{5,4},{6,7},{7,6},{8,9},{9,8},{10,11... | collective-permute-start | bytes 2359304 | tf_op jit(solution)/shard_map/ppermute | solution.py:8
  2.7 39.8 %collective-permute-start.4 = (bf16[256,128]{1,0:T(8,128)(2,1)S(1)}, bf16[256,128]{1,0:T(8,128)(2,1)S(1)}, u32[]{:S(2)}, u32[]{:S(2)}) collective-permute-start(bf16[256,128]{1,0:T(8,128)(2,1)S(1)} %constant_dynamic-slice_fusion.1), channel_id=1, source_target_pairs={{0,1},{1,0},{2,3},{3,2},{4,5},{5,4},{6,7},{7,6},{8,9},{9,8},{10,11... | collective-permute-start | bytes 196616 | tf_op jit(solution)/shard_map/ppermute | solution.py:8
  5.3 4.3 %copy-start.1 = (bf16[128,6,2,256]{3,2,1,0:T(2,128)(2,1)S(1)}, bf16[128,6,2,256]{3,2,1,0:T(2,128)(2,1)}, u32[]{:S(2)}) copy-start(bf16[128,6,2,256]{3,2,1,0:T(2,128)(2,1)} %param.6) | copy-start | bytes 2359300
  9.5 1.1 %copy-start.3 = (bf16[256,256]{1,0:T(8,128)(2,1)S(1)}, bf16[256,256]{1,0:T(8,128)(2,1)}, u32[]{:S(2)}) copy-start(bf16[256,256]{1,0:T(8,128)(2,1)} %param.8) | copy-start | bytes 393220
  11.2 1.9 %copy-start.2 = (bf16[256,6,2,512]{3,0,1,2:T(8,128)(2,1)S(1)}, bf16[256,6,2,512]{3,0,1,2:T(8,128)(2,1)}, u32[]{:S(2)}) copy-start(bf16[256,6,2,512]{3,0,1,2:T(8,128)(2,1)} %copy.47) | copy-start | bytes 9437188
  13.8 7.3 %collective-permute-start.1 = (bf16[128,512]{1,0:T(8,128)(2,1)S(1)}, bf16[128,512]{1,0:T(8,128)(2,1)S(1)}, u32[]{:S(2)}, u32[]{:S(2)}) collective-permute-start(bf16[128,512]{1,0:T(8,128)(2,1)S(1)} %dynamic-slice_convert_fusion.1), channel_id=1, source_target_pairs={{0,4},{4,0},{8,12},{12,8},{1,5},{5,1},{9,13},{13,9},{2,6},{6,2},{1... | collective-permute-start | bytes 393224 | tf_op jit(solution)/shard_map/ppermute | solution.py:19
  17.6 6.6 %collective-permute-start.7 = (bf16[128,512]{1,0:T(8,128)(2,1)S(1)}, bf16[128,512]{1,0:T(8,128)(2,1)S(1)}, u32[]{:S(2)}, u32[]{:S(2)}) collective-permute-start(bf16[128,512]{1,0:T(8,128)(2,1)S(1)} %dynamic-slice_convert_fusion), channel_id=1, source_target_pairs={{0,4},{4,0},{8,12},{12,8},{1,5},{5,1},{9,13},{13,9},{2,6},{6,2},{1... | collective-permute-start | bytes 393224 | tf_op jit(solution)/shard_map/ppermute | solution.py:19
  21.2 12.2 %collective-permute-start.2 = (bf16[128,512]{1,0:T(8,128)(2,1)S(1)}, bf16[128,512]{1,0:T(8,128)(2,1)S(1)}, u32[]{:S(2)}, u32[]{:S(2)}) collective-permute-start(bf16[128,512]{1,0:T(8,128)(2,1)S(1)} %fusion.29), channel_id=1, source_target_pairs={{0,8},{4,12},{8,0},{12,4},{1,9},{5,13},{9,1},{13,5},{2,10},{6,14},... | collective-permute-start | bytes 393224 | tf_op jit(solution)/shard_map/ppermute | solution.py:23
  24.2 10.9 %collective-permute-start.8 = (bf16[128,512]{1,0:T(8,128)(2,1)S(1)}, bf16[128,512]{1,0:T(8,128)(2,1)S(1)}, u32[]{:S(2)}, u32[]{:S(2)}) collective-permute-start(bf16[128,512]{1,0:T(8,128)(2,1)S(1)} %fusion.30), channel_id=1, source_target_pairs={{0,8},{4,12},{8,0},{12,4},{1,9},{5,13},{9,1},{13,5},{2,10},{6,14},... | collective-permute-start | bytes 393224 | tf_op jit(solution)/shard_map/ppermute | solution.py:23
  33.4 6.3 %collective-permute-start.3 = (bf16[128,512]{1,0:T(8,128)(2,1)S(1)}, bf16[128,512]{1,0:T(8,128)(2,1)S(1)}, u32[]{:S(2)}, u32[]{:S(2)}) collective-permute-start(bf16[128,512]{1,0:T(8,128)(2,1)S(1)} %fusion.24), channel_id=1, source_target_pairs={{0,4},{4,0},{8,12},{12,8},{1,5},{5,1},{9,13},{13,9},{2,6},{6,2},{1... | collective-permute-start | bytes 393224 | tf_op jit(solution)/shard_map/ppermute | solution.py:33
  35.2 5.9 %collective-permute-start.9 = (bf16[128,512]{1,0:T(8,128)(2,1)S(1)}, bf16[128,512]{1,0:T(8,128)(2,1)S(1)}, u32[]{:S(2)}, u32[]{:S(2)}) collective-permute-start(bf16[128,512]{1,0:T(8,128)(2,1)S(1)} %fusion.23), channel_id=1, source_target_pairs={{0,4},{4,0},{8,12},{12,8},{1,5},{5,1},{9,13},{13,9},{2,6},{6,2},{1... | collective-permute-start | bytes 393224 | tf_op jit(solution)/shard_map/ppermute | solution.py:33
  40.5 2.0 %collective-permute-start.5 = (bf16[3,256,256]{2,1,0:T(8,128)(2,1)S(1)}, bf16[3,256,256]{2,1,0:T(8,128)(2,1)S(1)}, u32[]{:S(2)}, u32[]{:S(2)}) collective-permute-start(bf16[3,256,256]{2,1,0:T(8,128)(2,1)S(1)} %get-tuple-element.9), channel_id=1, source_target_pairs={{0,1},{1,0},{2,3},{3,2},{4,5},{5,4},{6,7},{7,6},{8,9},{9,8},{10,11... | collective-permute-start | bytes 1179656 | tf_op jit(solution)/shard_map/ppermute | solution.py:8
  40.6 2.3 %collective-permute-start.6 = (bf16[3,256,256]{2,1,0:T(8,128)(2,1)S(1)}, bf16[3,256,256]{2,1,0:T(8,128)(2,1)S(1)}, u32[]{:S(2)}, u32[]{:S(2)}) collective-permute-start(bf16[3,256,256]{2,1,0:T(8,128)(2,1)S(1)} %get-tuple-element.10), channel_id=1, source_target_pairs={{0,1},{1,0},{2,3},{3,2},{4,5},{5,4},{6,7},{7,6},{8,9},{9,8},{10,11... | collective-permute-start | bytes 1179656 | tf_op jit(solution)/shard_map/ppermute | solution.py:8
  41.9 1.8 %collective-permute-start.10 = (bf16[3,256,256]{2,1,0:T(8,128)(2,1)S(1)}, bf16[3,256,256]{2,1,0:T(8,128)(2,1)S(1)}, u32[]{:S(2)}, u32[]{:S(2)}) collective-permute-start(bf16[3,256,256]{2,1,0:T(8,128)(2,1)S(1)} %get-tuple-element.11), channel_id=1, source_target_pairs={{0,1},{1,0},{2,3},{3,2},{4,5},{5,4},{6,7},{7,6},{8,9},{9,8},{10,11... | collective-permute-start | bytes 1179656 | tf_op jit(solution)/shard_map/ppermute | solution.py:8
  42.0 2.3 %collective-permute-start.11 = (bf16[3,256,256]{2,1,0:T(8,128)(2,1)S(1)}, bf16[3,256,256]{2,1,0:T(8,128)(2,1)S(1)}, u32[]{:S(2)}, u32[]{:S(2)}) collective-permute-start(bf16[3,256,256]{2,1,0:T(8,128)(2,1)S(1)} %get-tuple-element.12), channel_id=1, source_target_pairs={{0,1},{1,0},{2,3},{3,2},{4,5},{5,4},{6,7},{7,6},{8,9},{9,8},{10,11... | collective-permute-start | bytes 1179656 | tf_op jit(solution)/shard_map/ppermute | solution.py:8

commit v11 on v10

--- a/solution.py
+++ b/solution.py
@@ -99,8 +99,8 @@
                 "rk,mrc->kmc", rf_for_partner, proj_other, preferred_element_type=jnp.float32
             ))
         summed = summed + jnp.concatenate(other, axis=1)
-        outs.append(control[:, :, l, :].astype(jnp.float32) + summed)
-    return jnp.stack(outs, axis=2).astype(jnp.bfloat16)
+        outs.append(summed)
+    return (control.astype(jnp.float32) + jnp.stack(outs, axis=2)).astype(jnp.bfloat16)
 
 
 def solution(mesh):

time: 46.8 us -> 44.7 us (0.955)
  local copies, waits for them, and re-layouts: 13.2 us -> 9.63 us
  matrix products: 5.13 us -> 6.49 us
    another operation x1 -> x0, local copies, waits for them, and re-layouts: 1.69 us -> none  [local(): return jnp.stack(outs, axis=2).astype(jnp.bfloat16)]
    convert_element_type x0 -> x1, local copies, waits for them, and re-layouts: none -> 1.69 us  [local(): (control.astype(jnp.float32) + jnp.stack(outs, axis=2)).astype(jnp.bfloat16)]
    slice x1, local copies, waits for them, and re-layouts: 2.48 us -> 0.81 us  [local(): prec = prec_t[l]]
    dot_general x1, matrix products: 0.57 us -> 1.86 us  [local(): jnp.einsum('rk,kmlc->lmrc', rf_other, ctrl_other, preferred_element_type=...]
    slice x1 -> x0, local copies, waits for them, and re-layouts: 1.09 us -> none  [local(): outs.append(control[:, :, l, :].astype(jnp.float32) + summed)]
    unnamed x10 -> x12, local copies, waits for them, and re-layouts: 6.87 us -> 6.08 us
  transfers between devices with their start and end apart: 12 -> 12, of which waited for: 8 -> 7; matrix products, arithmetic and copies ran while one was open for 30% -> 28% of each run, Pallas kernels for 0% -> 0%
where the time goes in v11:
time: 44.7 us; the launch traced here: 44.5 us
  waiting for transfers between devices  15.7 us (35%)
  starting transfers between devices  11.8 us (26%)
  local copies, waits for them, and re-layouts  9.63 us (22%)
  matrix products  6.49 us (15%)
  other arithmetic  0.63 us (1%)
    ppermute x2, waiting for transfers between devices, _reduce_scatter_rows(): recv = lax.ppermute(x.astype(wire), axis, [(i, i ^ d) for i in range(size)])  7.41 us
    unnamed x12, local copies, waits for them, and re-layouts  6.08 us
    ppermute x2, starting transfers between devices, _reduce_scatter_rows(): recv = lax.ppermute(x.astype(wire), axis, [(i, i ^ d) for i in range(size)])  5.8 us
    ppermute x2, waiting for transfers between devices, _all_gather_rows(): recv = lax.ppermute(x, axis, [(i, i ^ d) for i in range(size)])  4.12 us
    ppermute x2, waiting for transfers between devices, _reduce_scatter_rows(): lax.ppermute(send.astype(wire), axis, [(i, i ^ d) for i in range(size)])  3.42 us
    ppermute x2, starting transfers between devices, _reduce_scatter_rows(): lax.ppermute(send.astype(wire), axis, [(i, i ^ d) for i in range(size)])  3.18 us
    dot_general x1, matrix products, local(): jnp.einsum('rk,kmlc->lmrc', rf_other, ctrl_other, preferred_element_type=...  1.86 us
    ppermute x6, starting transfers between devices, _swap(): return lax.ppermute(x, axis, [(0, 1), (1, 0)])  1.72 us
  transfers between devices with their start and end apart: 12, of which 7 were waited for; matrix products, arithmetic and copies ran while one was open for 28% of the time, Pallas kernels for 0%

profile of v11, /device:TPU:0, one launch (start us, length us, event | category | flops | bytes accessed | tf_op | source)
XLA Modules:
  0.0 44.5 jit_solution(2782657254621212574)
XLA Ops:
  0.0 1.3 %copy.8 = bf16[128,6,2,256]{3,0,2,1:T(8,128)(2,1)S(1)} copy(bf16[128,6,2,256]{3,2,1,0:T(2,128)(2,1)} %param.6) | data formatting | bytes 1572864 | tf_op args[1]
  1.3 0.5 %collective-permute-start = (bf16[128,6,2,256]{3,0,2,1:T(8,128)(2,1)S(1)}, bf16[128,6,2,256]{3,0,2,1:T(8,128)(2,1)}, u32[]{:S(2)}, u32[]{:S(2)}) collective-permute-start(bf16[128,6,2,256]{3,0,2,1:T(8,128)(2,1)S(1)} %copy.8), channel_id=1, source_target_pairs={{0,1},{1,0},{2,3},{3,2},{4,5},{5,4},{6,7},{7,6},{8,9},{9,8},{10,11... | collective-permute-start | bytes 2359304 | tf_op jit(solution)/shard_map/ppermute | solution.py:8
  1.8 0.8 %constant_dynamic-slice_fusion.1 = bf16[256,128]{1,0:T(8,128)(2,1)S(1)} fusion(bf16[256,256]{1,0:T(8,128)(2,1)} %param.8, s32[]{:T(128)S(6)} %select_n.61), kind=kLoop, calls=%fused_computation.68 | loop fusion | bytes 131076 | tf_op jit(solution)/shard_map/dynamic_slice | solution.py:62
  2.7 4.3 %copy.39 = bf16[256,6,2,512]{3,0,1,2:T(8,128)(2,1)} copy(bf16[256,6,2,512]{3,2,1,0:T(2,128)(2,1)} %param.5) | data formatting | bytes 6291456 | tf_op args[0]
  7.0 0.8 %fusion.54 = (f32[1,256,512]{2,0,1:T(1,128)S(1)}, f32[1,256,512]{2,0,1:T(1,128)S(1)}) fusion(f32[2,256,512]{2,0,1:T(2,128)S(1)} %bitcast.92), kind=kLoop, calls=%fused_computation.72 | loop fusion | bytes 2097152 | tf_op jit(solution)/shard_map/slice | solution.py:80
  8.2 0.6 %fusion.29 = f32[256,6,2,256]{3,0,2,1:T(8,128)S(1)} fusion(bf16[256,256]{1,0:T(8,128)(2,1)S(1)} %copy-done.4, s32[]{:T(128)S(6)} %select_n.57, bf16[128,6,2,256]{3,2,1,0:T(2,128)(2,1)S(1)} %copy-done.1), kind=kOutput, calls=%fused_computation.48 | convolution fusion | flops 201326592 | bytes 3997700 | tf_op jit(solution)/shard_map/rk,kmlc->lmrc/dot_general | solution.py:66
  8.7 1.9 %fusion.11 = bf16[2,6,256,256]{3,2,0,1:T(8,128)(2,1)S(1)} fusion(f32[256,6,2,256]{3,0,2,1:T(8,128)S(1)} %fusion.29, bf16[128,6,2,256]{3,0,2,1:T(8,128)(2,1)} %collective-permute-done, bf16[256,128]{1,0:T(8,128)(2,1)S(1)} %constant_dynamic-slice_fusion.1), kind=kOutput, calls=%fused_computation.18 | convolution fusion | flops 202899456 | bytes 5570560 | tf_op jit(solution)/shard_map/rk,kmlc->lmrc/dot_general | solution.py:67
  10.8 0.7 %fusion = f32[256,512]{1,0:T(8,128)S(1)} fusion(bf16[2,6,256,512]{3,2,1,0:T(8,128)(2,1)S(1)} %bitcast.88, bf16[2,6,256,256]{3,2,0,1:T(8,128)(2,1)S(1)} %fusion.11, bf16[512,256]{1,0:T(8,128)(2,1)S(1)} %copy-done), kind=kOutput, calls=%fused_computation.4 | convolution fusion | flops 404881408 | bytes 3145728 | tf_op jit(solution)/shard_map/mrc,nc->mrn/dot_general | solution.py:78
  11.5 3.1 %collective-permute-start.1 = (bf16[128,512]{1,0:T(8,128)(2,1)S(1)}, bf16[128,512]{1,0:T(8,128)(2,1)S(1)}, u32[]{:S(2)}, u32[]{:S(2)}) collective-permute-start(bf16[128,512]{1,0:T(8,128)(2,1)S(1)} %dynamic-slice_convert_fusion.1), channel_id=1, source_target_pairs={{0,4},{4,0},{8,12},{12,8},{1,5},{5,1},{9,13},{13,9},{2,6},{6,2},{1... | collective-permute-start | bytes 393224 | tf_op jit(solution)/shard_map/ppermute | solution.py:19
  14.6 0.7 %fusion.2 = f32[256,512]{1,0:T(8,128)S(1)} fusion(bf16[2,6,256,512]{3,2,1,0:T(8,128)(2,1)S(1)} %bitcast.89, bf16[2,6,256,256]{3,2,0,1:T(8,128)(2,1)S(1)} %fusion.11, bf16[512,256]{1,0:T(8,128)(2,1)S(1)} %copy-done), kind=kOutput, calls=%fused_computation.6 | convolution fusion | flops 404881408 | bytes 3145728 | tf_op jit(solution)/shard_map/mrc,nc->mrn/dot_general | solution.py:78
  15.4 3.4 %collective-permute-done.1 = bf16[128,512]{1,0:T(8,128)(2,1)S(1)} collective-permute-done((bf16[128,512]{1,0:T(8,128)(2,1)S(1)}, bf16[128,512]{1,0:T(8,128)(2,1)S(1)}, u32[]{:S(2)}, u32[]{:S(2)}) %collective-permute-start.1) | collective-permute-done | bytes 131104 | tf_op jit(solution)/shard_map/ppermute | solution.py:19
  18.9 3.0 %collective-permute-start.2 = (bf16[128,512]{1,0:T(8,128)(2,1)S(1)}, bf16[128,512]{1,0:T(8,128)(2,1)S(1)}, u32[]{:S(2)}, u32[]{:S(2)}) collective-permute-start(bf16[128,512]{1,0:T(8,128)(2,1)S(1)} %fusion.26), channel_id=1, source_target_pairs={{0,8},{4,12},{8,0},{12,4},{1,9},{5,13},{9,1},{13,5},{2,10},{6,14},... | collective-permute-start | bytes 393224 | tf_op jit(solution)/shard_map/ppermute | solution.py:23
  22.0 2.8 %collective-permute-start.8 = (bf16[128,512]{1,0:T(8,128)(2,1)S(1)}, bf16[128,512]{1,0:T(8,128)(2,1)S(1)}, u32[]{:S(2)}, u32[]{:S(2)}) collective-permute-start(bf16[128,512]{1,0:T(8,128)(2,1)S(1)} %fusion.27), channel_id=1, source_target_pairs={{0,8},{4,12},{8,0},{12,4},{1,9},{5,13},{9,1},{13,5},{2,10},{6,14},... | collective-permute-start | bytes 393224 | tf_op jit(solution)/shard_map/ppermute | solution.py:23
  24.7 6.4 %collective-permute-done.2 = bf16[128,512]{1,0:T(8,128)(2,1)S(1)} collective-permute-done((bf16[128,512]{1,0:T(8,128)(2,1)S(1)}, bf16[128,512]{1,0:T(8,128)(2,1)S(1)}, u32[]{:S(2)}, u32[]{:S(2)}) %collective-permute-start.2) | collective-permute-done | bytes 131104 | tf_op jit(solution)/shard_map/ppermute | solution.py:23
  31.2 0.6 %collective-permute-start.3 = (bf16[128,512]{1,0:T(8,128)(2,1)S(1)}, bf16[128,512]{1,0:T(8,128)(2,1)S(1)}, u32[]{:S(2)}, u32[]{:S(2)}) collective-permute-start(bf16[128,512]{1,0:T(8,128)(2,1)S(1)} %fusion.21), channel_id=1, source_target_pairs={{0,4},{4,0},{8,12},{12,8},{1,5},{5,1},{9,13},{13,9},{2,6},{6,2},{1... | collective-permute-start | bytes 393224 | tf_op jit(solution)/shard_map/ppermute | solution.py:33
  31.8 1.1 %collective-permute-done.8 = bf16[128,512]{1,0:T(8,128)(2,1)S(1)} collective-permute-done((bf16[128,512]{1,0:T(8,128)(2,1)S(1)}, bf16[128,512]{1,0:T(8,128)(2,1)S(1)}, u32[]{:S(2)}, u32[]{:S(2)}) %collective-permute-start.8) | collective-permute-done | bytes 131104 | tf_op jit(solution)/shard_map/ppermute | solution.py:23
  32.9 0.5 %collective-permute-start.9 = (bf16[128,512]{1,0:T(8,128)(2,1)S(1)}, bf16[128,512]{1,0:T(8,128)(2,1)S(1)}, u32[]{:S(2)}, u32[]{:S(2)}) collective-permute-start(bf16[128,512]{1,0:T(8,128)(2,1)S(1)} %fusion.20), channel_id=1, source_target_pairs={{0,4},{4,0},{8,12},{12,8},{1,5},{5,1},{9,13},{13,9},{2,6},{6,2},{1... | collective-permute-start | bytes 393224 | tf_op jit(solution)/shard_map/ppermute | solution.py:33
  33.4 4.1 %collective-permute-done.3 = bf16[128,512]{1,0:T(8,128)(2,1)S(1)} collective-permute-done((bf16[128,512]{1,0:T(8,128)(2,1)S(1)}, bf16[128,512]{1,0:T(8,128)(2,1)S(1)}, u32[]{:S(2)}, u32[]{:S(2)}) %collective-permute-start.3) | collective-permute-done | bytes 131104 | tf_op jit(solution)/shard_map/ppermute | solution.py:33
  37.6 0.6 %fusion.12 = bf16[6,256,256]{2,1,0:T(8,128)(2,1)S(1)} fusion(f32[256,512]{1,0:T(8,128)S(1)} %maximum_convert_fusion, bf16[2,6,256,512]{3,2,1,0:T(8,128)(2,1)S(1)} %bitcast.90, bf16[512,256]{1,0:T(8,128)(2,1)S(1)} %copy-done), kind=kOutput, calls=%fused_computation.19 | convolution fusion | flops 405405696 | bytes 3145728 | tf_op jit(solution)/shard_map/mrn,nc->mrc/dot_general | solution.py:88
  38.3 0.5 %collective-permute-start.6 = (bf16[3,256,256]{2,1,0:T(8,128)(2,1)S(1)}, bf16[3,256,256]{2,1,0:T(8,128)(2,1)S(1)}, u32[]{:S(2)}, u32[]{:S(2)}) collective-permute-start(bf16[3,256,256]{2,1,0:T(8,128)(2,1)S(1)} %get-tuple-element.8), channel_id=1, source_target_pairs={{0,1},{1,0},{2,3},{3,2},{4,5},{5,4},{6,7},{7,6},{8,9},{9,8},{10,11... | collective-permute-start | bytes 1179656 | tf_op jit(solution)/shard_map/ppermute | solution.py:8
  39.0 0.6 %fusion.15 = bf16[6,256,256]{2,1,0:T(8,128)(2,1)S(1)} fusion(f32[256,512]{1,0:T(8,128)S(1)} %maximum_convert_fusion.1, bf16[2,6,256,512]{3,2,1,0:T(8,128)(2,1)S(1)} %bitcast.91, bf16[512,256]{1,0:T(8,128)(2,1)S(1)} %copy-done), kind=kOutput, calls=%fused_computation.20 | convolution fusion | flops 405405696 | bytes 3145728 | tf_op jit(solution)/shard_map/mrn,nc->mrc/dot_general | solution.py:88
  39.8 0.5 %collective-permute-start.11 = (bf16[3,256,256]{2,1,0:T(8,128)(2,1)S(1)}, bf16[3,256,256]{2,1,0:T(8,128)(2,1)S(1)}, u32[]{:S(2)}, u32[]{:S(2)}) collective-permute-start(bf16[3,256,256]{2,1,0:T(8,128)(2,1)S(1)} %get-tuple-element.10), channel_id=1, source_target_pairs={{0,1},{1,0},{2,3},{3,2},{4,5},{5,4},{6,7},{7,6},{8,9},{9,8},{10,11... | collective-permute-start | bytes 1179656 | tf_op jit(solution)/shard_map/ppermute | solution.py:8
  41.7 0.3 collective-permute-done.11
  42.8 1.7 %copy.16 = bf16[128,6,2,256]{3,2,1,0:T(2,128)(2,1)} copy(bf16[128,6,2,256]{3,0,1,2:T(8,128)(2,1)S(1)} %fusion.8) | data formatting | bytes 1572864 | tf_op jit(solution)/shard_map/convert_element_type | solution.py:103
  (42 shorter events, 3.7 us)
Async XLA Ops:
  0.0 10.6 %copy-start = (bf16[512,256]{1,0:T(8,128)(2,1)S(1)}, bf16[512,256]{1,0:T(8,128)(2,1)}, u32[]{:S(2)}) copy-start(bf16[512,256]{1,0:T(8,128)(2,1)} %param.9) | copy-start | bytes 786436
  1.3 7.4 %collective-permute-start = (bf16[128,6,2,256]{3,0,2,1:T(8,128)(2,1)S(1)}, bf16[128,6,2,256]{3,0,2,1:T(8,128)(2,1)}, u32[]{:S(2)}, u32[]{:S(2)}) collective-permute-start(bf16[128,6,2,256]{3,0,2,1:T(8,128)(2,1)S(1)} %copy.8), channel_id=1, source_target_pairs={{0,1},{1,0},{2,3},{3,2},{4,5},{5,4},{6,7},{7,6},{8,9},{9,8},{10,11... | collective-permute-start | bytes 2359304 | tf_op jit(solution)/shard_map/ppermute | solution.py:8
  2.7 37.6 %collective-permute-start.4 = (bf16[256,128]{1,0:T(8,128)(2,1)S(1)}, bf16[256,128]{1,0:T(8,128)(2,1)S(1)}, u32[]{:S(2)}, u32[]{:S(2)}) collective-permute-start(bf16[256,128]{1,0:T(8,128)(2,1)S(1)} %constant_dynamic-slice_fusion.1), channel_id=1, source_target_pairs={{0,1},{1,0},{2,3},{3,2},{4,5},{5,4},{6,7},{7,6},{8,9},{9,8},{10,11... | collective-permute-start | bytes 196616 | tf_op jit(solution)/shard_map/ppermute | solution.py:8
  2.7 4.3 %copy-start.3 = (f32[256,2,512]{2,1,0:T(2,128)S(1)}, f32[256,2,512]{2,1,0:T(2,128)}, u32[]{:S(2)}) copy-start(f32[256,2,512]{2,1,0:T(2,128)} %param.7) | copy-start | bytes 3145732
  7.0 1.1 %copy-start.1 = (bf16[128,6,2,256]{3,2,1,0:T(2,128)(2,1)S(1)}, bf16[128,6,2,256]{3,2,1,0:T(2,128)(2,1)}, u32[]{:S(2)}) copy-start(bf16[128,6,2,256]{3,2,1,0:T(2,128)(2,1)} %param.6) | copy-start | bytes 2359300
  7.0 1.1 %copy-start.4 = (bf16[256,256]{1,0:T(8,128)(2,1)S(1)}, bf16[256,256]{1,0:T(8,128)(2,1)}, u32[]{:S(2)}) copy-start(bf16[256,256]{1,0:T(8,128)(2,1)} %param.8) | copy-start | bytes 393220
  8.7 2.1 %copy-start.2 = (bf16[256,6,2,512]{3,0,1,2:T(8,128)(2,1)S(1)}, bf16[256,6,2,512]{3,0,1,2:T(8,128)(2,1)}, u32[]{:S(2)}) copy-start(bf16[256,6,2,512]{3,0,1,2:T(8,128)(2,1)} %copy.39) | copy-start | bytes 9437188
  11.5 7.3 %collective-permute-start.1 = (bf16[128,512]{1,0:T(8,128)(2,1)S(1)}, bf16[128,512]{1,0:T(8,128)(2,1)S(1)}, u32[]{:S(2)}, u32[]{:S(2)}) collective-permute-start(bf16[128,512]{1,0:T(8,128)(2,1)S(1)} %dynamic-slice_convert_fusion.1), channel_id=1, source_target_pairs={{0,4},{4,0},{8,12},{12,8},{1,5},{5,1},{9,13},{13,9},{2,6},{6,2},{1... | collective-permute-start | bytes 393224 | tf_op jit(solution)/shard_map/ppermute | solution.py:19
  15.3 6.6 %collective-permute-start.7 = (bf16[128,512]{1,0:T(8,128)(2,1)S(1)}, bf16[128,512]{1,0:T(8,128)(2,1)S(1)}, u32[]{:S(2)}, u32[]{:S(2)}) collective-permute-start(bf16[128,512]{1,0:T(8,128)(2,1)S(1)} %dynamic-slice_convert_fusion), channel_id=1, source_target_pairs={{0,4},{4,0},{8,12},{12,8},{1,5},{5,1},{9,13},{13,9},{2,6},{6,2},{1... | collective-permute-start | bytes 393224 | tf_op jit(solution)/shard_map/ppermute | solution.py:19
  18.9 12.2 %collective-permute-start.2 = (bf16[128,512]{1,0:T(8,128)(2,1)S(1)}, bf16[128,512]{1,0:T(8,128)(2,1)S(1)}, u32[]{:S(2)}, u32[]{:S(2)}) collective-permute-start(bf16[128,512]{1,0:T(8,128)(2,1)S(1)} %fusion.26), channel_id=1, source_target_pairs={{0,8},{4,12},{8,0},{12,4},{1,9},{5,13},{9,1},{13,5},{2,10},{6,14},... | collective-permute-start | bytes 393224 | tf_op jit(solution)/shard_map/ppermute | solution.py:23
  22.0 10.9 %collective-permute-start.8 = (bf16[128,512]{1,0:T(8,128)(2,1)S(1)}, bf16[128,512]{1,0:T(8,128)(2,1)S(1)}, u32[]{:S(2)}, u32[]{:S(2)}) collective-permute-start(bf16[128,512]{1,0:T(8,128)(2,1)S(1)} %fusion.27), channel_id=1, source_target_pairs={{0,8},{4,12},{8,0},{12,4},{1,9},{5,13},{9,1},{13,5},{2,10},{6,14},... | collective-permute-start | bytes 393224 | tf_op jit(solution)/shard_map/ppermute | solution.py:23
  31.2 6.3 %collective-permute-start.3 = (bf16[128,512]{1,0:T(8,128)(2,1)S(1)}, bf16[128,512]{1,0:T(8,128)(2,1)S(1)}, u32[]{:S(2)}, u32[]{:S(2)}) collective-permute-start(bf16[128,512]{1,0:T(8,128)(2,1)S(1)} %fusion.21), channel_id=1, source_target_pairs={{0,4},{4,0},{8,12},{12,8},{1,5},{5,1},{9,13},{13,9},{2,6},{6,2},{1... | collective-permute-start | bytes 393224 | tf_op jit(solution)/shard_map/ppermute | solution.py:33
  32.9 5.9 %collective-permute-start.9 = (bf16[128,512]{1,0:T(8,128)(2,1)S(1)}, bf16[128,512]{1,0:T(8,128)(2,1)S(1)}, u32[]{:S(2)}, u32[]{:S(2)}) collective-permute-start(bf16[128,512]{1,0:T(8,128)(2,1)S(1)} %fusion.20), channel_id=1, source_target_pairs={{0,4},{4,0},{8,12},{12,8},{1,5},{5,1},{9,13},{13,9},{2,6},{6,2},{1... | collective-permute-start | bytes 393224 | tf_op jit(solution)/shard_map/ppermute | solution.py:33
  38.3 2.0 %collective-permute-start.5 = (bf16[3,256,256]{2,1,0:T(8,128)(2,1)S(1)}, bf16[3,256,256]{2,1,0:T(8,128)(2,1)S(1)}, u32[]{:S(2)}, u32[]{:S(2)}) collective-permute-start(bf16[3,256,256]{2,1,0:T(8,128)(2,1)S(1)} %get-tuple-element.7), channel_id=1, source_target_pairs={{0,1},{1,0},{2,3},{3,2},{4,5},{5,4},{6,7},{7,6},{8,9},{9,8},{10,11... | collective-permute-start | bytes 1179656 | tf_op jit(solution)/shard_map/ppermute | solution.py:8
  38.3 2.3 %collective-permute-start.6 = (bf16[3,256,256]{2,1,0:T(8,128)(2,1)S(1)}, bf16[3,256,256]{2,1,0:T(8,128)(2,1)S(1)}, u32[]{:S(2)}, u32[]{:S(2)}) collective-permute-start(bf16[3,256,256]{2,1,0:T(8,128)(2,1)S(1)} %get-tuple-element.8), channel_id=1, source_target_pairs={{0,1},{1,0},{2,3},{3,2},{4,5},{5,4},{6,7},{7,6},{8,9},{9,8},{10,11... | collective-permute-start | bytes 1179656 | tf_op jit(solution)/shard_map/ppermute | solution.py:8
  39.7 1.8 %collective-permute-start.10 = (bf16[3,256,256]{2,1,0:T(8,128)(2,1)S(1)}, bf16[3,256,256]{2,1,0:T(8,128)(2,1)S(1)}, u32[]{:S(2)}, u32[]{:S(2)}) collective-permute-start(bf16[3,256,256]{2,1,0:T(8,128)(2,1)S(1)} %get-tuple-element.9), channel_id=1, source_target_pairs={{0,1},{1,0},{2,3},{3,2},{4,5},{5,4},{6,7},{7,6},{8,9},{9,8},{10,11... | collective-permute-start | bytes 1179656 | tf_op jit(solution)/shard_map/ppermute | solution.py:8
  39.8 2.2 %collective-permute-start.11 = (bf16[3,256,256]{2,1,0:T(8,128)(2,1)S(1)}, bf16[3,256,256]{2,1,0:T(8,128)(2,1)S(1)}, u32[]{:S(2)}, u32[]{:S(2)}) collective-permute-start(bf16[3,256,256]{2,1,0:T(8,128)(2,1)S(1)} %get-tuple-element.10), channel_id=1, source_target_pairs={{0,1},{1,0},{2,3},{3,2},{4,5},{5,4},{6,7},{7,6},{8,9},{9,8},{10,11... | collective-permute-start | bytes 1179656 | tf_op jit(solution)/shard_map/ppermute | solution.py:8

commit v12 on v11

--- a/solution.py
+++ b/solution.py
@@ -61,11 +61,7 @@
     rf_own = lax.dynamic_slice_in_dim(row_factor, h * kh, kh, 1)
     rf_other = lax.dynamic_slice_in_dim(row_factor, (1 - h) * kh, kh, 1)
     rf_for_partner = _swap(rf_other, "half")
-    ctrl_other = _swap(control, "half")
-    expanded_all = (
-        jnp.einsum("rk,kmlc->lmrc", rf_own, control, preferred_element_type=jnp.float32)
-        + jnp.einsum("rk,kmlc->lmrc", rf_other, ctrl_other, preferred_element_type=jnp.float32)
-    ).astype(jnp.bfloat16)
+    ctrl_t = jnp.transpose(control, (2, 1, 0, 3))
 
     pow2 = n_mem & (n_mem - 1) == 0 and rows % n_mem == 0
     blk = rows // max(n_mem // 2, 1)
@@ -74,7 +70,12 @@
     outs = []
     for l in range(n_lev):
         a = anom_t[l]
-        expanded = expanded_all[l]
+        c_own = ctrl_t[l]
+        c_oth = _swap(c_own, "half")
+        expanded = (
+            jnp.einsum("rk,mkc->mrc", rf_own, c_own, preferred_element_type=jnp.float32)
+            + jnp.einsum("rk,mkc->mrc", rf_other, c_oth, preferred_element_type=jnp.float32)
+        ).astype(jnp.bfloat16)
         fields = jnp.einsum("mrc,nc->mrn", expanded, col_factor, preferred_element_type=jnp.float32)
         inc = jnp.sum(a.astype(jnp.float32) * fields, axis=0)
         prec = prec_t[l]

time: 44.7 us -> 53.8 us (1.20)
  matrix products: 6.49 us -> 12.6 us
  local copies, waits for them, and re-layouts: 9.63 us -> 14.2 us
  other arithmetic: 0.63 us -> 3.68 us
  waiting for transfers between devices: 15.7 us -> 12.9 us
  starting transfers between devices: 11.8 us -> 9.84 us
    dot_general x2, matrix products: 1.32 us -> 6.9 us  [local(): jnp.einsum('mrc,nc->mrn', expanded, col_factor, preferred_element_type=jn...]
    ppermute x2, waiting for transfers between devices: 7.41 us -> 4.41 us  [_reduce_scatter_rows(): recv = lax.ppermute(x.astype(wire), axis, [(i, i ^ d) for i in range(size)])]
    convert_element_type x2, local copies, waits for them, and re-layouts: 0.05 us -> 2.66 us  [_reduce_scatter_rows(): send.astype(wire)]
    ppermute x2, starting transfers between devices: 5.8 us -> 3.66 us  [_reduce_scatter_rows(): recv = lax.ppermute(x.astype(wire), axis, [(i, i ^ d) for i in range(size)])]
    convert_element_type x2, other arithmetic: 0.07 us -> 2.03 us  [_reduce_scatter_rows(): recv = lax.ppermute(x.astype(wire), axis, [(i, i ^ d) for i in range(size)])]
    dynamic_slice x2, local copies, waits for them, and re-layouts: 0.05 us -> 1.48 us  [local(): lax.dynamic_slice_in_dim(prec, start, blk, 0) * part]
    convert_element_type x2, other arithmetic: 0.14 us -> 1.24 us  [local(): (lax.dynamic_slice_in_dim(prec, start, blk, 0) * part).astype(jnp.bfloat16)]
    squeeze x0 -> x1, local copies, waits for them, and re-layouts: none -> 0.92 us  [local(): c_own = ctrl_t[l]]
  transfers between devices with their start and end apart: 12 -> 13, of which waited for: 7 -> 8; matrix products, arithmetic and copies ran while one was open for 28% -> 48% of each run, Pallas kernels for 0% -> 0%
where the time goes in v12:
time: 53.8 us; the launch traced here: 53.4 us
  local copies, waits for them, and re-layouts  14.2 us (26%)
  waiting for transfers between devices  12.9 us (24%)
  matrix products  12.6 us (23%)
  starting transfers between devices  9.84 us (18%)
  other arithmetic  3.68 us (7%)
    dot_general x2, matrix products, local(): jnp.einsum('mrc,nc->mrn', expanded, col_factor, preferred_element_type=jn...  6.9 us
    unnamed x19, local copies, waits for them, and re-layouts  6.52 us
    ppermute x2, waiting for transfers between devices, _reduce_scatter_rows(): recv = lax.ppermute(x.astype(wire), axis, [(i, i ^ d) for i in range(size)])  4.41 us
    ppermute x2, waiting for transfers between devices, _reduce_scatter_rows(): lax.ppermute(send.astype(wire), axis, [(i, i ^ d) for i in range(size)])  4.25 us
    ppermute x2, starting transfers between devices, _reduce_scatter_rows(): recv = lax.ppermute(x.astype(wire), axis, [(i, i ^ d) for i in range(size)])  3.66 us
    ppermute x2, waiting for transfers between devices, _all_gather_rows(): recv = lax.ppermute(x, axis, [(i, i ^ d) for i in range(size)])  3.48 us
    dot_general x2, matrix products, local(): jnp.einsum('rk,mkc->mrc', rf_own, c_own, preferred_element_type=jnp.float32)  3.06 us
    convert_element_type x2, local copies, waits for them, and re-layouts, _reduce_scatter_rows(): send.astype(wire)  2.66 us
  transfers between devices with their start and end apart: 13, of which 8 were waited for; matrix products, arithmetic and copies ran while one was open for 48% of the time, Pallas kernels for 0%

profile of v12, /device:TPU:0, one launch (start us, length us, event | category | flops | bytes accessed | tf_op | source)
XLA Modules:
  0.0 53.4 jit_solution(7552119721614393199)
XLA Ops:
  0.0 1.3 %copy.27 = bf16[128,6,2,256]{3,0,1,2:T(8,128)(2,1)S(1)} copy(bf16[128,6,2,256]{3,2,1,0:T(2,128)(2,1)} %param.6) | data formatting | bytes 1572864 | tf_op args[1]
  1.3 0.9 %slice_bitcast_fusion.5 = (bf16[6,128,256]{2,1,0:T(8,128)(2,1)}, bf16[6,128,256]{2,1,0:T(8,128)(2,1)}) fusion(bf16[2,6,128,256]{3,2,1,0:T(8,128)(2,1)S(1)} %bitcast.101), kind=kLoop, calls=%fused_computation.29 | loop fusion | bytes 1572864 | tf_op jit(solution)/shard_map/squeeze | solution.py:73
  4.0 1.5 %fusion.33 = f32[256,6,256]{2,0,1:T(8,128)} fusion(bf16[256,256]{1,0:T(8,128)(2,1)S(1)} %copy-done.6, s32[]{:T(128)S(6)} %select_n.57, bf16[2,6,128,256]{3,2,1,0:T(8,128)(2,1)S(1)} %bitcast.102), kind=kOutput, calls=%fused_computation.54 | convolution fusion | flops 100663296 | bytes 2031620 | tf_op jit(solution)/shard_map/rk,mkc->mrc/dot_general | solution.py:76
  5.5 0.8 %fusion.61 = (f32[1,256,512]{2,0,1:T(1,128)S(1)}, f32[1,256,512]{2,0,1:T(1,128)S(1)}) fusion(f32[2,256,512]{2,0,1:T(2,128)S(1)} %bitcast.108), kind=kLoop, calls=%fused_computation.79 | loop fusion | bytes 2097152 | tf_op jit(solution)/shard_map/slice | solution.py:81
  6.3 0.8 %constant_dynamic-slice_fusion.2 = f32[1,128,512]{2,0,1:T(1,128)} fusion(f32[1,256,512]{2,0,1:T(1,128)S(1)} %get-tuple-element.5, s32[]{:T(128)S(6)} %select_n.60), kind=kLoop, calls=%fused_computation.77 | loop fusion | bytes 524292 | tf_op jit(solution)/shard_map/dynamic_slice | solution.py:84
  7.1 4.2 %copy.26 = bf16[256,6,2,512]{3,0,1,2:T(8,128)(2,1)} copy(bf16[256,6,2,512]{3,2,1,0:T(2,128)(2,1)} %param.5) | data formatting | bytes 6291456 | tf_op args[0]
  12.0 1.5 %fusion.29 = f32[256,6,256]{2,0,1:T(8,128)} fusion(bf16[256,256]{1,0:T(8,128)(2,1)S(1)} %copy-done.6, s32[]{:T(128)S(6)} %select_n.57, bf16[2,6,128,256]{3,2,1,0:T(8,128)(2,1)S(1)} %bitcast.103), kind=kOutput, calls=%fused_computation.50 | convolution fusion | flops 100663296 | bytes 2031620 | tf_op jit(solution)/shard_map/rk,mkc->mrc/dot_general | solution.py:76
  13.5 3.7 %fusion = f32[256,512]{1,0:T(8,128)} fusion(bf16[2,6,256,512]{3,2,1,0:T(8,128)(2,1)} %bitcast.104, f32[256,6,256]{2,0,1:T(8,128)} %fusion.33, bf16[6,128,256]{2,1,0:T(8,128)(2,1)} %collective-permute-done, bf16[512,256]{1,0:T(8,128)(2,1)S(1)} %copy-done, bf16[256,128]{1,0:T(8,128)(2,1)S(1)} %constant_dynamic-slice_fusion.1), kind=kOutput, calls=%fused_computation.4 | convolution fusion | flops 506331136 | bytes 4390912 | tf_op jit(solution)/shard_map/mrc,nc->mrn/dot_general | solution.py:79
  17.3 1.6 %dynamic-slice_convert_fusion.1 = bf16[128,512]{1,0:T(8,128)(2,1)} fusion(f32[256,512]{1,0:T(8,128)} %fusion, s32[]{:T(128)S(6)} %select_n.62), kind=kLoop, calls=%fused_computation.43 | loop fusion | bytes 262148 | tf_op jit(solution)/shard_map/convert_element_type | solution.py:19
  18.9 2.6 %collective-permute-start.1 = (bf16[128,512]{1,0:T(8,128)(2,1)}, bf16[128,512]{1,0:T(8,128)(2,1)}, u32[]{:S(2)}, u32[]{:S(2)}) collective-permute-start(bf16[128,512]{1,0:T(8,128)(2,1)} %dynamic-slice_convert_fusion.1), channel_id=1, source_target_pairs={{0,4},{4,0},{8,12},{12,8},{1,5},{5,1},{9,13},{13,9},{2,6},{6,2},{1... | collective-permute-start | bytes 393224 | tf_op jit(solution)/shard_map/ppermute | solution.py:19
  21.5 3.1 %fusion.2 = f32[256,512]{1,0:T(8,128)} fusion(bf16[2,6,256,512]{3,2,1,0:T(8,128)(2,1)S(1)} %bitcast.105, f32[256,6,256]{2,0,1:T(8,128)} %fusion.29, bf16[6,128,256]{2,1,0:T(8,128)(2,1)} %collective-permute-done.7, bf16[512,256]{1,0:T(8,128)(2,1)S(1)} %copy-done, bf16[256,128]{1,0:T(8,128)(2,1)S(1)} %constant_dynamic-slice_fusion.1), kind=kOutput, calls=%fused_computation.6 | convolution fusion | flops 506331136 | bytes 4390912 | tf_op jit(solution)/shard_map/mrc,nc->mrn/dot_general | solution.py:79
  24.6 1.0 %dynamic-slice_convert_fusion = bf16[128,512]{1,0:T(8,128)(2,1)S(1)} fusion(f32[256,512]{1,0:T(8,128)} %fusion.2, s32[]{:T(128)S(6)} %select_n.62), kind=kLoop, calls=%fused_computation.41 | loop fusion | bytes 262148 | tf_op jit(solution)/shard_map/convert_element_type | solution.py:19
  26.0 1.0 %fusion.27 = bf16[128,512]{1,0:T(8,128)(2,1)S(1)} fusion(bf16[128,512]{1,0:T(8,128)(2,1)} %collective-permute-done.1, f32[256,512]{1,0:T(8,128)} %fusion, s32[]{:T(128)S(6)} %select_n.60), kind=kLoop, calls=%fused_computation.44 | loop fusion | flops 196608 | bytes 524292 | tf_op jit(solution)/shard_map/convert_element_type | solution.py:23
  27.0 2.9 %collective-permute-start.2 = (bf16[128,512]{1,0:T(8,128)(2,1)S(1)}, bf16[128,512]{1,0:T(8,128)(2,1)S(1)}, u32[]{:S(2)}, u32[]{:S(2)}) collective-permute-start(bf16[128,512]{1,0:T(8,128)(2,1)S(1)} %fusion.27), channel_id=1, source_target_pairs={{0,8},{4,12},{8,0},{12,4},{1,9},{5,13},{9,1},{13,5},{2,10},{6,14},... | collective-permute-start | bytes 393224 | tf_op jit(solution)/shard_map/ppermute | solution.py:23
  29.9 4.1 %collective-permute-done.8 = bf16[128,512]{1,0:T(8,128)(2,1)S(1)} collective-permute-done((bf16[128,512]{1,0:T(8,128)(2,1)S(1)}, bf16[128,512]{1,0:T(8,128)(2,1)S(1)}, u32[]{:S(2)}, u32[]{:S(2)}) %collective-permute-start.8) | collective-permute-done | bytes 131104 | tf_op jit(solution)/shard_map/ppermute | solution.py:19
  33.9 1.0 %fusion.28 = bf16[128,512]{1,0:T(8,128)(2,1)S(1)} fusion(bf16[128,512]{1,0:T(8,128)(2,1)S(1)} %collective-permute-done.8, f32[256,512]{1,0:T(8,128)} %fusion.2, s32[]{:T(128)S(6)} %select_n.60), kind=kLoop, calls=%fused_computation.45 | loop fusion | flops 196608 | bytes 524292 | tf_op jit(solution)/shard_map/convert_element_type | solution.py:23
  34.9 0.8 %collective-permute-start.9 = (bf16[128,512]{1,0:T(8,128)(2,1)S(1)}, bf16[128,512]{1,0:T(8,128)(2,1)S(1)}, u32[]{:S(2)}, u32[]{:S(2)}) collective-permute-start(bf16[128,512]{1,0:T(8,128)(2,1)S(1)} %fusion.28), channel_id=1, source_target_pairs={{0,8},{4,12},{8,0},{12,4},{1,9},{5,13},{9,1},{13,5},{2,10},{6,14},... | collective-permute-start | bytes 393224 | tf_op jit(solution)/shard_map/ppermute | solution.py:23
  35.7 2.1 %collective-permute-done.2 = bf16[128,512]{1,0:T(8,128)(2,1)S(1)} collective-permute-done((bf16[128,512]{1,0:T(8,128)(2,1)S(1)}, bf16[128,512]{1,0:T(8,128)(2,1)S(1)}, u32[]{:S(2)}, u32[]{:S(2)}) %collective-permute-start.2) | collective-permute-done | bytes 131104 | tf_op jit(solution)/shard_map/ppermute | solution.py:23
  37.8 1.2 %fusion.22 = bf16[128,512]{1,0:T(8,128)(2,1)S(1)} fusion(f32[1,128,512]{2,0,1:T(1,128)} %constant_dynamic-slice_fusion.2, bf16[128,512]{1,0:T(8,128)(2,1)S(1)} %collective-permute-done.2, bf16[128,512]{1,0:T(8,128)(2,1)} %collective-permute-done.1, f32[256,512]{1,0:T(8,128)} %fusion, s32[]{:T(128)S(6)} %select_n.60), kind=kLoop, calls=%fused_computation.35 | loop fusion | flops 393216 | bytes 917508 | tf_op jit(solution)/shard_map/convert_element_type | solution.py:84
  38.9 0.8 %collective-permute-start.3 = (bf16[128,512]{1,0:T(8,128)(2,1)S(1)}, bf16[128,512]{1,0:T(8,128)(2,1)S(1)}, u32[]{:S(2)}, u32[]{:S(2)}) collective-permute-start(bf16[128,512]{1,0:T(8,128)(2,1)S(1)} %fusion.22), channel_id=1, source_target_pairs={{0,4},{4,0},{8,12},{12,8},{1,5},{5,1},{9,13},{13,9},{2,6},{6,2},{1... | collective-permute-start | bytes 393224 | tf_op jit(solution)/shard_map/ppermute | solution.py:33
  39.7 2.4 %collective-permute-done.9 = bf16[128,512]{1,0:T(8,128)(2,1)S(1)} collective-permute-done((bf16[128,512]{1,0:T(8,128)(2,1)S(1)}, bf16[128,512]{1,0:T(8,128)(2,1)S(1)}, u32[]{:S(2)}, u32[]{:S(2)}) %collective-permute-start.9) | collective-permute-done | bytes 131104 | tf_op jit(solution)/shard_map/ppermute | solution.py:23
  42.8 2.6 %collective-permute-done.3 = bf16[128,512]{1,0:T(8,128)(2,1)S(1)} collective-permute-done((bf16[128,512]{1,0:T(8,128)(2,1)S(1)}, bf16[128,512]{1,0:T(8,128)(2,1)S(1)}, u32[]{:S(2)}, u32[]{:S(2)}) %collective-permute-start.3) | collective-permute-done | bytes 131104 | tf_op jit(solution)/shard_map/ppermute | solution.py:33
  46.7 0.8 %collective-permute-done.10 = bf16[128,512]{1,0:T(8,128)(2,1)S(1)} collective-permute-done((bf16[128,512]{1,0:T(8,128)(2,1)S(1)}, bf16[128,512]{1,0:T(8,128)(2,1)S(1)}, u32[]{:S(2)}, u32[]{:S(2)}) %collective-permute-start.10) | collective-permute-done | bytes 131104 | tf_op jit(solution)/shard_map/ppermute | solution.py:33
  51.7 1.7 %copy.16 = bf16[128,6,2,256]{3,2,1,0:T(2,128)(2,1)} copy(bf16[128,6,2,256]{3,0,1,2:T(8,128)(2,1)S(1)} %fusion.8) | data formatting | bytes 1572864 | tf_op jit(solution)/shard_map/convert_element_type | solution.py:104
  (52 shorter events, 8.8 us)
Async XLA Ops:
  0.0 13.5 %copy-start = (bf16[512,256]{1,0:T(8,128)(2,1)S(1)}, bf16[512,256]{1,0:T(8,128)(2,1)}, u32[]{:S(2)}) copy-start(bf16[512,256]{1,0:T(8,128)(2,1)} %param.9) | copy-start | bytes 786436
  0.0 2.7 %copy-start.6 = (bf16[256,256]{1,0:T(8,128)(2,1)S(1)}, bf16[256,256]{1,0:T(8,128)(2,1)}, u32[]{:S(2)}) copy-start(bf16[256,256]{1,0:T(8,128)(2,1)} %param.8) | copy-start | bytes 393220
  1.3 4.2 %copy-start.4 = (f32[256,2,512]{2,1,0:T(2,128)S(1)}, f32[256,2,512]{2,1,0:T(2,128)}, u32[]{:S(2)}) copy-start(f32[256,2,512]{2,1,0:T(2,128)} %param.7) | copy-start | bytes 3145732
  2.2 11.3 %collective-permute-start = (bf16[6,128,256]{2,1,0:T(8,128)(2,1)}, bf16[6,128,256]{2,1,0:T(8,128)(2,1)}, u32[]{:S(2)}, u32[]{:S(2)}) collective-permute-start(bf16[6,128,256]{2,1,0:T(8,128)(2,1)} %get-tuple-element.9), channel_id=1, source_target_pairs={{0,1},{1,0},{2,3},{3,2},{4,5},{5,4},{6,7},{7,6},{8,9},{9,8},{10,11... | collective-permute-start | bytes 1179656 | tf_op jit(solution)/shard_map/ppermute | solution.py:8
  3.4 45.5 %collective-permute-start.4 = (bf16[256,128]{0,1:T(8,128)(2,1)}, bf16[256,128]{0,1:T(8,128)(2,1)S(1)}, u32[]{:S(2)}, u32[]{:S(2)}) collective-permute-start(bf16[256,128]{0,1:T(8,128)(2,1)} %copy.20), channel_id=1, source_target_pairs={{0,1},{1,0},{2,3},{3,2},{4,5},{5,4},{6,7},{7,6},{8,9},{9,8},{10,11... | collective-permute-start | bytes 196616 | tf_op jit(solution)/shard_map/ppermute | solution.py:8
  3.5 18.0 %collective-permute-start.7 = (bf16[6,128,256]{2,1,0:T(8,128)(2,1)}, bf16[6,128,256]{2,1,0:T(8,128)(2,1)}, u32[]{:S(2)}, u32[]{:S(2)}) collective-permute-start(bf16[6,128,256]{2,1,0:T(8,128)(2,1)} %get-tuple-element.10), channel_id=1, source_target_pairs={{0,1},{1,0},{2,3},{3,2},{4,5},{5,4},{6,7},{7,6},{8,9},{9,8},{10,11... | collective-permute-start | bytes 1179656 | tf_op jit(solution)/shard_map/ppermute | solution.py:8
  13.5 8.0 %copy-start.1 = (bf16[256,6,2,512]{3,0,1,2:T(8,128)(2,1)S(1)}, bf16[256,6,2,512]{3,0,1,2:T(8,128)(2,1)}, u32[]{:S(2)}) copy-start(bf16[256,6,2,512]{3,0,1,2:T(8,128)(2,1)} %copy.26) | copy-start | bytes 9437188
  18.9 7.1 %collective-permute-start.1 = (bf16[128,512]{1,0:T(8,128)(2,1)}, bf16[128,512]{1,0:T(8,128)(2,1)}, u32[]{:S(2)}, u32[]{:S(2)}) collective-permute-start(bf16[128,512]{1,0:T(8,128)(2,1)} %dynamic-slice_convert_fusion.1), channel_id=1, source_target_pairs={{0,4},{4,0},{8,12},{12,8},{1,5},{5,1},{9,13},{13,9},{2,6},{6,2},{1... | collective-permute-start | bytes 393224 | tf_op jit(solution)/shard_map/ppermute | solution.py:19
  24.6 17.5 %copy-start.3 = (f32[1,128,512]{2,0,1:T(1,128)S(1)}, f32[1,128,512]{2,0,1:T(1,128)}, u32[]{:S(2)}) copy-start(f32[1,128,512]{2,0,1:T(1,128)} %constant_dynamic-slice_fusion) | copy-start | bytes 786436
  24.6 17.5 %copy-start.5 = (f32[256,512]{1,0:T(8,128)S(1)}, f32[256,512]{1,0:T(8,128)}, u32[]{:S(2)}) copy-start(f32[256,512]{1,0:T(8,128)} %fusion.2) | copy-start | bytes 1572868
  25.7 8.3 %collective-permute-start.8 = (bf16[128,512]{1,0:T(8,128)(2,1)S(1)}, bf16[128,512]{1,0:T(8,128)(2,1)S(1)}, u32[]{:S(2)}, u32[]{:S(2)}) collective-permute-start(bf16[128,512]{1,0:T(8,128)(2,1)S(1)} %dynamic-slice_convert_fusion), channel_id=1, source_target_pairs={{0,4},{4,0},{8,12},{12,8},{1,5},{5,1},{9,13},{13,9},{2,6},{6,2},{1... | collective-permute-start | bytes 393224 | tf_op jit(solution)/shard_map/ppermute | solution.py:19
  27.0 10.8 %collective-permute-start.2 = (bf16[128,512]{1,0:T(8,128)(2,1)S(1)}, bf16[128,512]{1,0:T(8,128)(2,1)S(1)}, u32[]{:S(2)}, u32[]{:S(2)}) collective-permute-start(bf16[128,512]{1,0:T(8,128)(2,1)S(1)} %fusion.27), channel_id=1, source_target_pairs={{0,8},{4,12},{8,0},{12,4},{1,9},{5,13},{9,1},{13,5},{2,10},{6,14},... | collective-permute-start | bytes 393224 | tf_op jit(solution)/shard_map/ppermute | solution.py:23
  34.9 7.1 %collective-permute-start.9 = (bf16[128,512]{1,0:T(8,128)(2,1)S(1)}, bf16[128,512]{1,0:T(8,128)(2,1)S(1)}, u32[]{:S(2)}, u32[]{:S(2)}) collective-permute-start(bf16[128,512]{1,0:T(8,128)(2,1)S(1)} %fusion.28), channel_id=1, source_target_pairs={{0,8},{4,12},{8,0},{12,4},{1,9},{5,13},{9,1},{13,5},{2,10},{6,14},... | collective-permute-start | bytes 393224 | tf_op jit(solution)/shard_map/ppermute | solution.py:23
  38.9 6.5 %collective-permute-start.3 = (bf16[128,512]{1,0:T(8,128)(2,1)S(1)}, bf16[128,512]{1,0:T(8,128)(2,1)S(1)}, u32[]{:S(2)}, u32[]{:S(2)}) collective-permute-start(bf16[128,512]{1,0:T(8,128)(2,1)S(1)} %fusion.22), channel_id=1, source_target_pairs={{0,4},{4,0},{8,12},{12,8},{1,5},{5,1},{9,13},{13,9},{2,6},{6,2},{1... | collective-permute-start | bytes 393224 | tf_op jit(solution)/shard_map/ppermute | solution.py:33
  42.2 5.4 %collective-permute-start.10 = (bf16[128,512]{1,0:T(8,128)(2,1)S(1)}, bf16[128,512]{1,0:T(8,128)(2,1)S(1)}, u32[]{:S(2)}, u32[]{:S(2)}) collective-permute-start(bf16[128,512]{1,0:T(8,128)(2,1)S(1)} %fusion.21), channel_id=1, source_target_pairs={{0,4},{4,0},{8,12},{12,8},{1,5},{5,1},{9,13},{13,9},{2,6},{6,2},{1... | collective-permute-start | bytes 393224 | tf_op jit(solution)/shard_map/ppermute | solution.py:33
  46.2 2.8 %collective-permute-start.5 = (bf16[3,256,256]{2,1,0:T(8,128)(2,1)S(1)}, bf16[3,256,256]{2,1,0:T(8,128)(2,1)S(1)}, u32[]{:S(2)}, u32[]{:S(2)}) collective-permute-start(bf16[3,256,256]{2,1,0:T(8,128)(2,1)S(1)} %get-tuple-element.7), channel_id=1, source_target_pairs={{0,1},{1,0},{2,3},{3,2},{4,5},{5,4},{6,7},{7,6},{8,9},{9,8},{10,11... | collective-permute-start | bytes 1179656 | tf_op jit(solution)/shard_map/ppermute | solution.py:8
  46.2 2.9 %collective-permute-start.6 = (bf16[3,256,256]{2,1,0:T(8,128)(2,1)S(1)}, bf16[3,256,256]{2,1,0:T(8,128)(2,1)S(1)}, u32[]{:S(2)}, u32[]{:S(2)}) collective-permute-start(bf16[3,256,256]{2,1,0:T(8,128)(2,1)S(1)} %get-tuple-element.8), channel_id=1, source_target_pairs={{0,1},{1,0},{2,3},{3,2},{4,5},{5,4},{6,7},{7,6},{8,9},{9,8},{10,11... | collective-permute-start | bytes 1179656 | tf_op jit(solution)/shard_map/ppermute | solution.py:8
  48.3 1.1 %copy-start.7 = (bf16[256,256]{1,0:T(8,128)(2,1)S(1)}, bf16[256,256]{1,0:T(8,128)(2,1)}, u32[]{:S(2)}) copy-start(bf16[256,256]{1,0:T(8,128)(2,1)} %param.8) | copy-start | bytes 393220
  48.3 1.8 %collective-permute-start.11 = (bf16[3,256,256]{2,1,0:T(8,128)(2,1)S(1)}, bf16[3,256,256]{2,1,0:T(8,128)(2,1)S(1)}, u32[]{:S(2)}, u32[]{:S(2)}) collective-permute-start(bf16[3,256,256]{2,1,0:T(8,128)(2,1)S(1)} %get-tuple-element.11), channel_id=1, source_target_pairs={{0,1},{1,0},{2,3},{3,2},{4,5},{5,4},{6,7},{7,6},{8,9},{9,8},{10,11... | collective-permute-start | bytes 1179656 | tf_op jit(solution)/shard_map/ppermute | solution.py:8
  48.4 2.3 %collective-permute-start.12 = (bf16[3,256,256]{2,1,0:T(8,128)(2,1)S(1)}, bf16[3,256,256]{2,1,0:T(8,128)(2,1)S(1)}, u32[]{:S(2)}, u32[]{:S(2)}) collective-permute-start(bf16[3,256,256]{2,1,0:T(8,128)(2,1)S(1)} %get-tuple-element.12), channel_id=1, source_target_pairs={{0,1},{1,0},{2,3},{3,2},{4,5},{5,4},{6,7},{7,6},{8,9},{9,8},{10,11... | collective-permute-start | bytes 1179656 | tf_op jit(solution)/shard_map/ppermute | solution.py:8
  50.3 1.1 %copy-start.2 = (bf16[128,6,2,256]{3,2,1,0:T(2,128)(2,1)S(1)}, bf16[128,6,2,256]{3,2,1,0:T(2,128)(2,1)}, u32[]{:S(2)}) copy-start(bf16[128,6,2,256]{3,2,1,0:T(2,128)(2,1)} %param.6) | copy-start | bytes 2359300

commit v13 on v12

--- a/solution.py
+++ b/solution.py
@@ -61,7 +61,6 @@
     rf_own = lax.dynamic_slice_in_dim(row_factor, h * kh, kh, 1)
     rf_other = lax.dynamic_slice_in_dim(row_factor, (1 - h) * kh, kh, 1)
     rf_for_partner = _swap(rf_other, "half")
-    ctrl_t = jnp.transpose(control, (2, 1, 0, 3))
 
     pow2 = n_mem & (n_mem - 1) == 0 and rows % n_mem == 0
     blk = rows // max(n_mem // 2, 1)
@@ -70,11 +69,11 @@
     outs = []
     for l in range(n_lev):
         a = anom_t[l]
-        c_own = ctrl_t[l]
+        c_own = control[:, :, l, :]
         c_oth = _swap(c_own, "half")
         expanded = (
-            jnp.einsum("rk,mkc->mrc", rf_own, c_own, preferred_element_type=jnp.float32)
-            + jnp.einsum("rk,mkc->mrc", rf_other, c_oth, preferred_element_type=jnp.float32)
+            jnp.einsum("rk,kmc->mrc", rf_own, c_own, preferred_element_type=jnp.float32)
+            + jnp.einsum("rk,kmc->mrc", rf_other, c_oth, preferred_element_type=jnp.float32)
         ).astype(jnp.bfloat16)
         fields = jnp.einsum("mrc,nc->mrn", expanded, col_factor, preferred_element_type=jnp.float32)
         inc = jnp.sum(a.astype(jnp.float32) * fields, axis=0)

time: 53.8 us -> 60.9 us (1.13)
  local copies, waits for them, and re-layouts: 14.2 us -> 19 us
  matrix products: 12.6 us -> 14.8 us
    slice x0 -> x1, local copies, waits for them, and re-layouts: none -> 2.8 us  [local(): c_own = control[:, :, l, :]]
    slice x1, local copies, waits for them, and re-layouts: 0.81 us -> 3.46 us  [local(): prec = prec_t[l]]
    dot_general x2, matrix products: 3.06 us -> 5.26 us  [local(): jnp.einsum('rk,kmc->mrc', rf_own, c_own, preferred_element_type=jnp.float32)]
    dynamic_slice x2, local copies, waits for them, and re-layouts: 1.48 us -> 3.37 us  [local(): lax.dynamic_slice_in_dim(prec, start, blk, 0) * part]
    unnamed x19 -> x20, local copies, waits for them, and re-layouts: 6.52 us -> 4.93 us
    squeeze x1 -> x0, local copies, waits for them, and re-layouts: 0.92 us -> none  [local(): c_own = ctrl_t[l]]
  transfers between devices with their start and end apart: 13 -> 13, of which waited for: 8 -> 8; matrix products, arithmetic and copies ran while one was open for 48% -> 51% of each run, Pallas kernels for 0% -> 0%
where the time goes in v13:
time: 60.9 us; the launch traced here: 60.5 us
  local copies, waits for them, and re-layouts  19 us (31%)
  matrix products  14.8 us (24%)
  waiting for transfers between devices  12.9 us (21%)
  starting transfers between devices  9.84 us (16%)
  other arithmetic  3.68 us (6%)
    dot_general x2, matrix products, local(): jnp.einsum('mrc,nc->mrn', expanded, col_factor, preferred_element_type=jn...  6.9 us
    dot_general x2, matrix products, local(): jnp.einsum('rk,kmc->mrc', rf_own, c_own, preferred_element_type=jnp.float32)  5.26 us
    unnamed x20, local copies, waits for them, and re-layouts  4.93 us
    ppermute x2, waiting for transfers between devices, _reduce_scatter_rows(): recv = lax.ppermute(x.astype(wire), axis, [(i, i ^ d) for i in range(size)])  4.4 us
    ppermute x2, waiting for transfers between devices, _reduce_scatter_rows(): lax.ppermute(send.astype(wire), axis, [(i, i ^ d) for i in range(size)])  4.25 us
    ppermute x2, starting transfers between devices, _reduce_scatter_rows(): recv = lax.ppermute(x.astype(wire), axis, [(i, i ^ d) for i in range(size)])  3.67 us
    ppermute x2, waiting for transfers between devices, _all_gather_rows(): recv = lax.ppermute(x, axis, [(i, i ^ d) for i in range(size)])  3.48 us
    slice x1, local copies, waits for them, and re-layouts, local(): prec = prec_t[l]  3.46 us
  transfers between devices with their start and end apart: 13, of which 8 were waited for; matrix products, arithmetic and copies ran while one was open for 51% of the time, Pallas kernels for 0%

profile of v13, /device:TPU:0, one launch (start us, length us, event | category | flops | bytes accessed | tf_op | source)
XLA Modules:
  0.0 60.5 jit_solution(1008164558774326636)
XLA Ops:
  0.0 2.8 %fusion.63 = (bf16[128,6,1,256]{3,2,1,0:T(2,128)(2,1)S(1)}, bf16[128,6,1,256]{3,2,1,0:T(2,128)(2,1)S(1)}) fusion(bf16[128,6,2,256]{3,2,1,0:T(2,128)(2,1)} %param.6), kind=kLoop, calls=%fused_computation.80 | loop fusion | bytes 1572864 | tf_op jit(solution)/shard_map/slice | solution.py:72
  2.8 0.8 %copy.32 = bf16[128,6,1,256]{3,0,2,1:T(8,128)(2,1)} copy(bf16[128,6,1,256]{3,2,1,0:T(2,128)(2,1)S(1)} %get-tuple-element.9) | data formatting | bytes 786432
  4.9 0.8 %copy.31 = bf16[128,6,1,256]{3,0,2,1:T(8,128)(2,1)} copy(bf16[128,6,1,256]{3,2,1,0:T(2,128)(2,1)S(1)} %get-tuple-element.10) | data formatting | bytes 786432
  6.1 2.7 %fusion.33 = f32[256,6,256]{2,0,1:T(8,128)} fusion(bf16[128,6,256]{2,0,1:T(8,128)(2,1)} %bitcast.99, bf16[256,256]{1,0:T(8,128)(2,1)} %param.8, s32[]{:T(128)S(6)} %select_n.57), kind=kOutput, calls=%fused_computation.53 | convolution fusion | flops 100663296 | bytes 2031620 | tf_op jit(solution)/shard_map/rk,kmc->mrc/dot_general | solution.py:75
  8.8 3.5 %fusion.61 = (f32[1,256,512]{2,0,1:T(1,128)}, f32[1,256,512]{2,0,1:T(1,128)}) fusion(f32[2,256,512]{2,0,1:T(2,128)} %bitcast.104), kind=kLoop, calls=%fused_computation.78 | loop fusion | bytes 2097152 | tf_op jit(solution)/shard_map/slice | solution.py:80
  12.3 1.7 %constant_dynamic-slice_fusion.2 = f32[1,128,512]{2,0,1:T(1,128)} fusion(f32[1,256,512]{2,0,1:T(1,128)} %get-tuple-element.5, s32[]{:T(128)S(6)} %select_n.60), kind=kLoop, calls=%fused_computation.76 | loop fusion | bytes 524292 | tf_op jit(solution)/shard_map/dynamic_slice | solution.py:83
  14.0 2.3 %copy.30 = bf16[256,6,2,512]{3,0,1,2:T(8,128)(2,1)} copy(bf16[256,6,2,512]{3,2,1,0:T(2,128)(2,1)S(1)} %copy-done.2) | data formatting | bytes 6291456 | tf_op args[0]
  16.3 1.7 %constant_dynamic-slice_fusion = f32[1,128,512]{2,0,1:T(1,128)} fusion(f32[1,256,512]{2,0,1:T(1,128)} %get-tuple-element.6, s32[]{:T(128)S(6)} %select_n.60), kind=kLoop, calls=%fused_computation.74 | loop fusion | bytes 524292 | tf_op jit(solution)/shard_map/dynamic_slice | solution.py:83
  18.0 2.5 %fusion.29 = f32[256,6,256]{2,0,1:T(8,128)} fusion(bf16[128,6,256]{2,0,1:T(8,128)(2,1)} %bitcast.98, bf16[256,256]{1,0:T(8,128)(2,1)} %param.8, s32[]{:T(128)S(6)} %select_n.57), kind=kOutput, calls=%fused_computation.49 | convolution fusion | flops 100663296 | bytes 2031620 | tf_op jit(solution)/shard_map/rk,kmc->mrc/dot_general | solution.py:75
  20.5 3.8 %fusion = f32[256,512]{1,0:T(8,128)} fusion(bf16[2,6,256,512]{3,2,1,0:T(8,128)(2,1)} %bitcast.100, f32[256,6,256]{2,0,1:T(8,128)} %fusion.33, bf16[128,6,256]{2,0,1:T(8,128)(2,1)} %collective-permute-done, bf16[512,256]{1,0:T(8,128)(2,1)S(1)} %copy-done, bf16[256,128]{1,0:T(8,128)(2,1)S(1)} %constant_dynamic-slice_fusion.1), kind=kOutput, calls=%fused_computation.4 | convolution fusion | flops 506331136 | bytes 4390912 | tf_op jit(solution)/shard_map/mrc,nc->mrn/dot_general | solution.py:78
  24.3 1.6 %dynamic-slice_convert_fusion.1 = bf16[128,512]{1,0:T(8,128)(2,1)} fusion(f32[256,512]{1,0:T(8,128)} %fusion, s32[]{:T(128)S(6)} %select_n.62), kind=kLoop, calls=%fused_computation.42 | loop fusion | bytes 262148 | tf_op jit(solution)/shard_map/convert_element_type | solution.py:19
  25.9 2.6 %collective-permute-start.1 = (bf16[128,512]{1,0:T(8,128)(2,1)}, bf16[128,512]{1,0:T(8,128)(2,1)}, u32[]{:S(2)}, u32[]{:S(2)}) collective-permute-start(bf16[128,512]{1,0:T(8,128)(2,1)} %dynamic-slice_convert_fusion.1), channel_id=1, source_target_pairs={{0,4},{4,0},{8,12},{12,8},{1,5},{5,1},{9,13},{13,9},{2,6},{6,2},{1... | collective-permute-start | bytes 393224 | tf_op jit(solution)/shard_map/ppermute | solution.py:19
  28.5 3.1 %fusion.2 = f32[256,512]{1,0:T(8,128)} fusion(bf16[2,6,256,512]{3,2,1,0:T(8,128)(2,1)S(1)} %bitcast.101, f32[256,6,256]{2,0,1:T(8,128)} %fusion.29, bf16[128,6,256]{2,0,1:T(8,128)(2,1)} %collective-permute-done.7, bf16[512,256]{1,0:T(8,128)(2,1)S(1)} %copy-done, bf16[256,128]{1,0:T(8,128)(2,1)S(1)} %constant_dynamic-slice_fusion.1), kind=kOutput, calls=%fused_computation.6 | convolution fusion | flops 506331136 | bytes 4390912 | tf_op jit(solution)/shard_map/mrc,nc->mrn/dot_general | solution.py:78
  31.6 1.0 %dynamic-slice_convert_fusion = bf16[128,512]{1,0:T(8,128)(2,1)S(1)} fusion(f32[256,512]{1,0:T(8,128)} %fusion.2, s32[]{:T(128)S(6)} %select_n.62), kind=kLoop, calls=%fused_computation.40 | loop fusion | bytes 262148 | tf_op jit(solution)/shard_map/convert_element_type | solution.py:19
  33.0 1.0 %fusion.27 = bf16[128,512]{1,0:T(8,128)(2,1)S(1)} fusion(bf16[128,512]{1,0:T(8,128)(2,1)} %collective-permute-done.1, f32[256,512]{1,0:T(8,128)} %fusion, s32[]{:T(128)S(6)} %select_n.60), kind=kLoop, calls=%fused_computation.43 | loop fusion | flops 196608 | bytes 524292 | tf_op jit(solution)/shard_map/convert_element_type | solution.py:23
  34.0 2.9 %collective-permute-start.2 = (bf16[128,512]{1,0:T(8,128)(2,1)S(1)}, bf16[128,512]{1,0:T(8,128)(2,1)S(1)}, u32[]{:S(2)}, u32[]{:S(2)}) collective-permute-start(bf16[128,512]{1,0:T(8,128)(2,1)S(1)} %fusion.27), channel_id=1, source_target_pairs={{0,8},{4,12},{8,0},{12,4},{1,9},{5,13},{9,1},{13,5},{2,10},{6,14},... | collective-permute-start | bytes 393224 | tf_op jit(solution)/shard_map/ppermute | solution.py:23
  36.9 4.0 %collective-permute-done.8 = bf16[128,512]{1,0:T(8,128)(2,1)S(1)} collective-permute-done((bf16[128,512]{1,0:T(8,128)(2,1)S(1)}, bf16[128,512]{1,0:T(8,128)(2,1)S(1)}, u32[]{:S(2)}, u32[]{:S(2)}) %collective-permute-start.8) | collective-permute-done | bytes 131104 | tf_op jit(solution)/shard_map/ppermute | solution.py:19
  40.9 1.0 %fusion.28 = bf16[128,512]{1,0:T(8,128)(2,1)S(1)} fusion(bf16[128,512]{1,0:T(8,128)(2,1)S(1)} %collective-permute-done.8, f32[256,512]{1,0:T(8,128)} %fusion.2, s32[]{:T(128)S(6)} %select_n.60), kind=kLoop, calls=%fused_computation.44 | loop fusion | flops 196608 | bytes 524292 | tf_op jit(solution)/shard_map/convert_element_type | solution.py:23
  42.7 2.0 %collective-permute-done.2 = bf16[128,512]{1,0:T(8,128)(2,1)S(1)} collective-permute-done((bf16[128,512]{1,0:T(8,128)(2,1)S(1)}, bf16[128,512]{1,0:T(8,128)(2,1)S(1)}, u32[]{:S(2)}, u32[]{:S(2)}) %collective-permute-start.2) | collective-permute-done | bytes 131104 | tf_op jit(solution)/shard_map/ppermute | solution.py:23
  44.8 1.2 %fusion.22 = bf16[128,512]{1,0:T(8,128)(2,1)S(1)} fusion(f32[1,128,512]{2,0,1:T(1,128)} %constant_dynamic-slice_fusion.2, bf16[128,512]{1,0:T(8,128)(2,1)S(1)} %collective-permute-done.2, bf16[128,512]{1,0:T(8,128)(2,1)} %collective-permute-done.1, f32[256,512]{1,0:T(8,128)} %fusion, s32[]{:T(128)S(6)} %select_n.60), kind=kLoop, calls=%fused_computation.34 | loop fusion | flops 393216 | bytes 917508 | tf_op jit(solution)/shard_map/convert_element_type | solution.py:83
  46.7 2.4 %collective-permute-done.9 = bf16[128,512]{1,0:T(8,128)(2,1)S(1)} collective-permute-done((bf16[128,512]{1,0:T(8,128)(2,1)S(1)}, bf16[128,512]{1,0:T(8,128)(2,1)S(1)}, u32[]{:S(2)}, u32[]{:S(2)}) %collective-permute-start.9) | collective-permute-done | bytes 131104 | tf_op jit(solution)/shard_map/ppermute | solution.py:23
  49.8 2.6 %collective-permute-done.3 = bf16[128,512]{1,0:T(8,128)(2,1)S(1)} collective-permute-done((bf16[128,512]{1,0:T(8,128)(2,1)S(1)}, bf16[128,512]{1,0:T(8,128)(2,1)S(1)}, u32[]{:S(2)}, u32[]{:S(2)}) %collective-permute-start.3) | collective-permute-done | bytes 131104 | tf_op jit(solution)/shard_map/ppermute | solution.py:33
  53.7 0.9 %collective-permute-done.10 = bf16[128,512]{1,0:T(8,128)(2,1)S(1)} collective-permute-done((bf16[128,512]{1,0:T(8,128)(2,1)S(1)}, bf16[128,512]{1,0:T(8,128)(2,1)S(1)}, u32[]{:S(2)}, u32[]{:S(2)}) %collective-permute-start.10) | collective-permute-done | bytes 131104 | tf_op jit(solution)/shard_map/ppermute | solution.py:33
  58.8 1.7 %copy.17 = bf16[128,6,2,256]{3,2,1,0:T(2,128)(2,1)} copy(bf16[128,6,2,256]{3,0,1,2:T(8,128)(2,1)S(1)} %fusion.8) | data formatting | bytes 1572864 | tf_op jit(solution)/shard_map/convert_element_type | solution.py:103
  (53 shorter events, 9.6 us)
Async XLA Ops:
  0.0 20.5 %copy-start = (bf16[512,256]{1,0:T(8,128)(2,1)S(1)}, bf16[512,256]{1,0:T(8,128)(2,1)}, u32[]{:S(2)}) copy-start(bf16[512,256]{1,0:T(8,128)(2,1)} %param.9) | copy-start | bytes 786436
  0.0 4.1 %copy-start.6 = (bf16[256,256]{1,0:T(8,128)(2,1)S(1)}, bf16[256,256]{1,0:T(8,128)(2,1)}, u32[]{:S(2)}) copy-start(bf16[256,256]{1,0:T(8,128)(2,1)} %param.8) | copy-start | bytes 393220
  3.6 16.9 %collective-permute-start = (bf16[128,6,256]{2,0,1:T(8,128)(2,1)}, bf16[128,6,256]{2,0,1:T(8,128)(2,1)}, u32[]{:S(2)}, u32[]{:S(2)}) collective-permute-start(bf16[128,6,256]{2,0,1:T(8,128)(2,1)} %bitcast.99), channel_id=1, source_target_pairs={{0,1},{1,0},{2,3},{3,2},{4,5},{5,4},{6,7},{7,6},{8,9},{9,8},{10,11... | collective-permute-start | bytes 1179656 | tf_op jit(solution)/shard_map/ppermute | solution.py:8
  4.8 51.1 %collective-permute-start.4 = (bf16[256,128]{0,1:T(8,128)(2,1)}, bf16[256,128]{0,1:T(8,128)(2,1)S(1)}, u32[]{:S(2)}, u32[]{:S(2)}) collective-permute-start(bf16[256,128]{0,1:T(8,128)(2,1)} %copy.22), channel_id=1, source_target_pairs={{0,1},{1,0},{2,3},{3,2},{4,5},{5,4},{6,7},{7,6},{8,9},{9,8},{10,11... | collective-permute-start | bytes 196616 | tf_op jit(solution)/shard_map/ppermute | solution.py:8
  5.7 22.8 %collective-permute-start.7 = (bf16[128,6,256]{2,0,1:T(8,128)(2,1)}, bf16[128,6,256]{2,0,1:T(8,128)(2,1)}, u32[]{:S(2)}, u32[]{:S(2)}) collective-permute-start(bf16[128,6,256]{2,0,1:T(8,128)(2,1)} %bitcast.98), channel_id=1, source_target_pairs={{0,1},{1,0},{2,3},{3,2},{4,5},{5,4},{6,7},{7,6},{8,9},{9,8},{10,11... | collective-permute-start | bytes 1179656 | tf_op jit(solution)/shard_map/ppermute | solution.py:8
  6.1 7.9 %copy-start.2 = (bf16[256,6,2,512]{3,2,1,0:T(2,128)(2,1)S(1)}, bf16[256,6,2,512]{3,2,1,0:T(2,128)(2,1)}, u32[]{:S(2)}) copy-start(bf16[256,6,2,512]{3,2,1,0:T(2,128)(2,1)} %param.5) | copy-start | bytes 9437188
  20.5 8.0 %copy-start.3 = (bf16[256,6,2,512]{3,0,1,2:T(8,128)(2,1)S(1)}, bf16[256,6,2,512]{3,0,1,2:T(8,128)(2,1)}, u32[]{:S(2)}) copy-start(bf16[256,6,2,512]{3,0,1,2:T(8,128)(2,1)} %copy.30) | copy-start | bytes 9437188
  25.9 7.1 %collective-permute-start.1 = (bf16[128,512]{1,0:T(8,128)(2,1)}, bf16[128,512]{1,0:T(8,128)(2,1)}, u32[]{:S(2)}, u32[]{:S(2)}) collective-permute-start(bf16[128,512]{1,0:T(8,128)(2,1)} %dynamic-slice_convert_fusion.1), channel_id=1, source_target_pairs={{0,4},{4,0},{8,12},{12,8},{1,5},{5,1},{9,13},{13,9},{2,6},{6,2},{1... | collective-permute-start | bytes 393224 | tf_op jit(solution)/shard_map/ppermute | solution.py:19
  31.6 17.5 %copy-start.4 = (f32[1,128,512]{2,0,1:T(1,128)S(1)}, f32[1,128,512]{2,0,1:T(1,128)}, u32[]{:S(2)}) copy-start(f32[1,128,512]{2,0,1:T(1,128)} %constant_dynamic-slice_fusion) | copy-start | bytes 786436
  31.6 17.5 %copy-start.5 = (f32[256,512]{1,0:T(8,128)S(1)}, f32[256,512]{1,0:T(8,128)}, u32[]{:S(2)}) copy-start(f32[256,512]{1,0:T(8,128)} %fusion.2) | copy-start | bytes 1572868
  32.7 8.3 %collective-permute-start.8 = (bf16[128,512]{1,0:T(8,128)(2,1)S(1)}, bf16[128,512]{1,0:T(8,128)(2,1)S(1)}, u32[]{:S(2)}, u32[]{:S(2)}) collective-permute-start(bf16[128,512]{1,0:T(8,128)(2,1)S(1)} %dynamic-slice_convert_fusion), channel_id=1, source_target_pairs={{0,4},{4,0},{8,12},{12,8},{1,5},{5,1},{9,13},{13,9},{2,6},{6,2},{1... | collective-permute-start | bytes 393224 | tf_op jit(solution)/shard_map/ppermute | solution.py:19
  34.0 10.8 %collective-permute-start.2 = (bf16[128,512]{1,0:T(8,128)(2,1)S(1)}, bf16[128,512]{1,0:T(8,128)(2,1)S(1)}, u32[]{:S(2)}, u32[]{:S(2)}) collective-permute-start(bf16[128,512]{1,0:T(8,128)(2,1)S(1)} %fusion.27), channel_id=1, source_target_pairs={{0,8},{4,12},{8,0},{12,4},{1,9},{5,13},{9,1},{13,5},{2,10},{6,14},... | collective-permute-start | bytes 393224 | tf_op jit(solution)/shard_map/ppermute | solution.py:23
  41.9 7.2 %collective-permute-start.9 = (bf16[128,512]{1,0:T(8,128)(2,1)S(1)}, bf16[128,512]{1,0:T(8,128)(2,1)S(1)}, u32[]{:S(2)}, u32[]{:S(2)}) collective-permute-start(bf16[128,512]{1,0:T(8,128)(2,1)S(1)} %fusion.28), channel_id=1, source_target_pairs={{0,8},{4,12},{8,0},{12,4},{1,9},{5,13},{9,1},{13,5},{2,10},{6,14},... | collective-permute-start | bytes 393224 | tf_op jit(solution)/shard_map/ppermute | solution.py:23
  45.9 6.4 %collective-permute-start.3 = (bf16[128,512]{1,0:T(8,128)(2,1)S(1)}, bf16[128,512]{1,0:T(8,128)(2,1)S(1)}, u32[]{:S(2)}, u32[]{:S(2)}) collective-permute-start(bf16[128,512]{1,0:T(8,128)(2,1)S(1)} %fusion.22), channel_id=1, source_target_pairs={{0,4},{4,0},{8,12},{12,8},{1,5},{5,1},{9,13},{13,9},{2,6},{6,2},{1... | collective-permute-start | bytes 393224 | tf_op jit(solution)/shard_map/ppermute | solution.py:33
  49.2 5.4 %collective-permute-start.10 = (bf16[128,512]{1,0:T(8,128)(2,1)S(1)}, bf16[128,512]{1,0:T(8,128)(2,1)S(1)}, u32[]{:S(2)}, u32[]{:S(2)}) collective-permute-start(bf16[128,512]{1,0:T(8,128)(2,1)S(1)} %fusion.21), channel_id=1, source_target_pairs={{0,4},{4,0},{8,12},{12,8},{1,5},{5,1},{9,13},{13,9},{2,6},{6,2},{1... | collective-permute-start | bytes 393224 | tf_op jit(solution)/shard_map/ppermute | solution.py:33
  53.1 2.8 %collective-permute-start.5 = (bf16[3,256,256]{2,1,0:T(8,128)(2,1)S(1)}, bf16[3,256,256]{2,1,0:T(8,128)(2,1)S(1)}, u32[]{:S(2)}, u32[]{:S(2)}) collective-permute-start(bf16[3,256,256]{2,1,0:T(8,128)(2,1)S(1)} %get-tuple-element.7), channel_id=1, source_target_pairs={{0,1},{1,0},{2,3},{3,2},{4,5},{5,4},{6,7},{7,6},{8,9},{9,8},{10,11... | collective-permute-start | bytes 1179656 | tf_op jit(solution)/shard_map/ppermute | solution.py:8
  53.2 3.0 %collective-permute-start.6 = (bf16[3,256,256]{2,1,0:T(8,128)(2,1)S(1)}, bf16[3,256,256]{2,1,0:T(8,128)(2,1)S(1)}, u32[]{:S(2)}, u32[]{:S(2)}) collective-permute-start(bf16[3,256,256]{2,1,0:T(8,128)(2,1)S(1)} %get-tuple-element.8), channel_id=1, source_target_pairs={{0,1},{1,0},{2,3},{3,2},{4,5},{5,4},{6,7},{7,6},{8,9},{9,8},{10,11... | collective-permute-start | bytes 1179656 | tf_op jit(solution)/shard_map/ppermute | solution.py:8
  55.3 1.1 %copy-start.7 = (bf16[256,256]{1,0:T(8,128)(2,1)S(1)}, bf16[256,256]{1,0:T(8,128)(2,1)}, u32[]{:S(2)}) copy-start(bf16[256,256]{1,0:T(8,128)(2,1)} %param.8) | copy-start | bytes 393220
  55.4 1.8 %collective-permute-start.11 = (bf16[3,256,256]{2,1,0:T(8,128)(2,1)S(1)}, bf16[3,256,256]{2,1,0:T(8,128)(2,1)S(1)}, u32[]{:S(2)}, u32[]{:S(2)}) collective-permute-start(bf16[3,256,256]{2,1,0:T(8,128)(2,1)S(1)} %get-tuple-element.11), channel_id=1, source_target_pairs={{0,1},{1,0},{2,3},{3,2},{4,5},{5,4},{6,7},{7,6},{8,9},{9,8},{10,11... | collective-permute-start | bytes 1179656 | tf_op jit(solution)/shard_map/ppermute | solution.py:8
  55.4 2.3 %collective-permute-start.12 = (bf16[3,256,256]{2,1,0:T(8,128)(2,1)S(1)}, bf16[3,256,256]{2,1,0:T(8,128)(2,1)S(1)}, u32[]{:S(2)}, u32[]{:S(2)}) collective-permute-start(bf16[3,256,256]{2,1,0:T(8,128)(2,1)S(1)} %get-tuple-element.12), channel_id=1, source_target_pairs={{0,1},{1,0},{2,3},{3,2},{4,5},{5,4},{6,7},{7,6},{8,9},{9,8},{10,11... | collective-permute-start | bytes 1179656 | tf_op jit(solution)/shard_map/ppermute | solution.py:8
  57.4 1.1 %copy-start.1 = (bf16[128,6,2,256]{3,2,1,0:T(2,128)(2,1)S(1)}, bf16[128,6,2,256]{3,2,1,0:T(2,128)(2,1)}, u32[]{:S(2)}) copy-start(bf16[128,6,2,256]{3,2,1,0:T(2,128)(2,1)} %param.6) | copy-start | bytes 2359300

commit v14 on v6

--- a/solution.py
+++ b/solution.py
@@ -49,6 +49,31 @@
     return start
 
 
+def _pick(x, axis, take_low):
+    n = x.shape[axis] // 2
+    lo = lax.slice_in_dim(x, 0, n, axis=axis)
+    hi = lax.slice_in_dim(x, n, 2 * n, axis=axis)
+    return jnp.where(take_low, lo, hi)
+
+
+def _rows_back(a, w, rf_own, rf_for_partner, col_factor):
+    scaled = (a.astype(jnp.float32) * w.astype(jnp.float32)[None]).astype(jnp.bfloat16)
+    projected = jnp.einsum(
+        "mrn,nc->mrc", scaled, col_factor, preferred_element_type=jnp.float32
+    ).astype(jnp.bfloat16)
+    n_m = projected.shape[0]
+    mh = n_m // 2
+    chunks = [(0, mh), (mh, n_m)] if mh > 0 else [(0, n_m)]
+    summed = jnp.einsum("rk,mrc->kmc", rf_own, projected, preferred_element_type=jnp.float32)
+    other = []
+    for lo, hi in chunks:
+        proj_other = _swap(projected[lo:hi], "half")
+        other.append(jnp.einsum(
+            "rk,mrc->kmc", rf_for_partner, proj_other, preferred_element_type=jnp.float32
+        ))
+    return summed + jnp.concatenate(other, axis=1)
+
+
 def local(anomalies, control, precision, row_factor, col_factor, n_mem):
     h = lax.axis_index("half")
     kh = control.shape[0]
@@ -78,23 +103,29 @@
         fields = jnp.einsum("mrc,nc->mrn", expanded, col_factor, preferred_element_type=jnp.float32)
         inc = jnp.sum(a.astype(jnp.float32) * fields, axis=0)
         prec = prec_t[l]
-        if pow2:
+        if pow2 and n_mem == 4:
             part = _reduce_scatter_rows(inc, "mem", n_mem, jnp.bfloat16)
             w_blk = (lax.dynamic_slice_in_dim(prec, start, blk, 0) * part).astype(jnp.bfloat16)
-            weighted = _all_gather_rows(w_blk, "mem", n_mem)
+            w_recv = lax.ppermute(w_blk, "mem", [(i, i ^ 1) for i in range(n_mem)])
+            low_first = lax.axis_index("mem") % 2 == 0
+            summed = None
+            for w, own in ((w_blk, True), (w_recv, False)):
+                take_low = low_first if own else jnp.logical_not(low_first)
+                part_sum = _rows_back(
+                    _pick(a, 1, take_low), w, _pick(rf_own, 0, take_low),
+                    _pick(rf_for_partner, 0, take_low), col_factor,
+                )
+                summed = part_sum if summed is None else summed + part_sum
         else:
-            weighted = (prec * lax.psum(inc, "mem")).astype(jnp.bfloat16)
-        scaled = (a.astype(jnp.float32) * weighted.astype(jnp.float32)[None]).astype(jnp.bfloat16)
-        projected = jnp.einsum(
-            "mrn,nc->mrc", scaled, col_factor, preferred_element_type=jnp.float32
-        ).astype(jnp.bfloat16)
-        proj_other = _swap(projected, "half")
-        summed = jnp.einsum(
-            "rk,mrc->mkc", rf_own, projected, preferred_element_type=jnp.float32
-        ) + jnp.einsum("rk,mrc->mkc", rf_for_partner, proj_other, preferred_element_type=jnp.float32)
+            if pow2:
+                part = _reduce_scatter_rows(inc, "mem", n_mem, jnp.bfloat16)
+                w_blk = (lax.dynamic_slice_in_dim(prec, start, blk, 0) * part).astype(jnp.bfloat16)
+                weighted = _all_gather_rows(w_blk, "mem", n_mem)
+            else:
+                weighted = (prec * lax.psum(inc, "mem")).astype(jnp.bfloat16)
+            summed = _rows_back(a, weighted, rf_own, rf_for_partner, col_factor)
         outs.append(summed)
-    summed_all = jnp.transpose(jnp.stack(outs, axis=0), (2, 1, 0, 3))
-    return (control.astype(jnp.float32) + summed_all).astype(jnp.bfloat16)
+    return (control.astype(jnp.float32) + jnp.stack(outs, axis=2)).astype(jnp.bfloat16)
 
 
 def solution(mesh):

time: 47.1 us -> 52.2 us (1.11)
  waiting for transfers between devices: 16.8 us -> 13.6 us
  local copies, waits for them, and re-layouts: 9.95 us -> 12.9 us
  starting transfers between devices: 10.4 us -> 12.6 us
  matrix products: 8.93 us -> 11.1 us
  other arithmetic: 0.58 us -> 1.3 us
    dot_general x1, matrix products: 0.56 us -> 3.32 us  [local(): jnp.einsum('rk,kmlc->lmrc', rf_own, control, preferred_element_type=jnp.f...]
    ppermute x2, waiting for transfers between devices: 4.31 us -> 2.77 us  [local(): w_recv = lax.ppermute(w_blk, 'mem', [(i, i ^ 1) for i in range(n_mem)])]
    ppermute x4 -> x10, starting transfers between devices: 1.16 us -> 2.49 us  [_swap(): return lax.ppermute(x, axis, [(0, 1), (1, 0)])]
    ppermute x2, waiting for transfers between devices: 8.54 us -> 7.38 us  [_reduce_scatter_rows(): recv = lax.ppermute(x.astype(wire), axis, [(i, i ^ d) for i in range(size)])]
    slice x1, local copies, waits for them, and re-layouts: 0.81 us -> 1.77 us  [local(): prec = prec_t[l]]
    dynamic_slice x2, local copies, waits for them, and re-layouts: 0.05 us -> 0.98 us  [local(): lax.dynamic_slice_in_dim(prec, start, blk, 0) * part]
    dynamic_slice x1, local copies, waits for them, and re-layouts: 0.63 us -> 1.56 us  [local(): rf_other = lax.dynamic_slice_in_dim(row_factor, (1 - h) * kh, kh, 1)]
    select_n x2 -> x1, other arithmetic: 0.05 us -> 0.82 us  [_pick(): return jnp.where(take_low, lo, hi)]
  transfers between devices with their start and end apart: 10 -> 16, of which waited for: 6 -> 5; matrix products, arithmetic and copies ran while one was open for 25% -> 33% of each run, Pallas kernels for 0% -> 0%
where the time goes in v14:
time: 52.2 us; the launch traced here: 51.8 us
  waiting for transfers between devices  13.6 us (26%)
  local copies, waits for them, and re-layouts  12.9 us (25%)
  starting transfers between devices  12.6 us (24%)
  matrix products  11.1 us (21%)
  other arithmetic  1.3 us (2%)
    ppermute x2, waiting for transfers between devices, _reduce_scatter_rows(): recv = lax.ppermute(x.astype(wire), axis, [(i, i ^ d) for i in range(size)])  7.38 us
    unnamed x14, local copies, waits for them, and re-layouts  6.51 us
    ppermute x2, starting transfers between devices, _reduce_scatter_rows(): recv = lax.ppermute(x.astype(wire), axis, [(i, i ^ d) for i in range(size)])  5.81 us
    ppermute x2, waiting for transfers between devices, _reduce_scatter_rows(): lax.ppermute(send.astype(wire), axis, [(i, i ^ d) for i in range(size)])  3.45 us
    dot_general x1, matrix products, local(): jnp.einsum('rk,kmlc->lmrc', rf_own, control, preferred_element_type=jnp.f...  3.32 us
    ppermute x2, starting transfers between devices, _reduce_scatter_rows(): lax.ppermute(send.astype(wire), axis, [(i, i ^ d) for i in range(size)])  3.18 us
    ppermute x2, waiting for transfers between devices, local(): w_recv = lax.ppermute(w_blk, 'mem', [(i, i ^ 1) for i in range(n_mem)])  2.77 us
    ppermute x10, starting transfers between devices, _swap(): return lax.ppermute(x, axis, [(0, 1), (1, 0)])  2.49 us
  transfers between devices with their start and end apart: 16, of which 5 were waited for; matrix products, arithmetic and copies ran while one was open for 33% of the time, Pallas kernels for 0%

profile of v14, /device:TPU:0, one launch (start us, length us, event | category | flops | bytes accessed | tf_op | source)
XLA Modules:
  0.0 51.8 jit_solution(4391520696553193965)
XLA Ops:
  0.0 1.6 %constant_dynamic-slice_fusion.1 = bf16[256,128]{1,0:T(8,128)(2,1)} fusion(bf16[256,256]{1,0:T(8,128)(2,1)} %param.8, s32[]{:T(128)S(6)} %select_n.94), kind=kLoop, calls=%fused_computation.100 | loop fusion | bytes 131076 | tf_op jit(solution)/shard_map/dynamic_slice | solution.py:87
  2.0 2.1 %copy.8 = bf16[128,6,2,256]{3,0,2,1:T(8,128)(2,1)} copy(bf16[128,6,2,256]{3,2,1,0:T(2,128)(2,1)} %param.6) | data formatting | bytes 1572864 | tf_op args[1]
  4.2 1.8 %fusion.78 = (f32[1,256,512]{2,0,1:T(1,128)}, f32[1,256,512]{2,0,1:T(1,128)}) fusion(f32[2,256,512]{2,0,1:T(2,128)S(1)} %bitcast.113), kind=kLoop, calls=%fused_computation.106 | loop fusion | bytes 2097152 | tf_op jit(solution)/shard_map/slice | solution.py:105
  6.0 2.6 %copy.59 = bf16[256,6,2,512]{3,0,1,2:T(8,128)(2,1)S(1)} copy(bf16[256,6,2,512]{3,2,1,0:T(2,128)(2,1)} %param.5) | data formatting | bytes 6291456 | tf_op args[0]
  8.6 3.3 %fusion.37 = f32[256,6,2,256]{3,0,2,1:T(8,128)} fusion(bf16[256,256]{1,0:T(8,128)(2,1)S(1)} %copy-done.3, s32[]{:T(128)S(6)} %select_n.89, bf16[128,6,2,256]{3,2,1,0:T(2,128)(2,1)} %param.6), kind=kOutput, calls=%fused_computation.64 | convolution fusion | flops 201326592 | bytes 3997700 | tf_op jit(solution)/shard_map/rk,kmlc->lmrc/dot_general | solution.py:91
  11.9 1.0 %constant_dynamic-slice_fusion.2 = f32[1,128,512]{2,0,1:T(1,128)S(1)} fusion(f32[1,256,512]{2,0,1:T(1,128)} %get-tuple-element.11, s32[]{:T(128)S(6)} %select_n.93), kind=kLoop, calls=%fused_computation.101 | loop fusion | bytes 524292 | tf_op jit(solution)/shard_map/dynamic_slice | solution.py:108
  13.1 0.8 %copy-done.4 = f32[1,256,512]{2,0,1:T(1,128)S(1)} copy-done((f32[1,256,512]{2,0,1:T(1,128)S(1)}, f32[1,256,512]{2,0,1:T(1,128)}, u32[]{:S(2)}) %copy-start.4) | copy-done | bytes 524312
  13.9 0.8 %broadcast_select_fusion = (bf16[128,128]{1,0:T(8,128)(2,1)S(1)}, bf16[128,128]{1,0:T(8,128)(2,1)S(1)}) fusion(pred[]{:T(512)S(6)} %not.4, bf16[256,128]{1,0:T(8,128)(2,1)} %collective-permute-done.3, pred[]{:T(512)S(6)} %eq.10), kind=kLoop, calls=%fused_computation.91 | loop fusion | flops 32768 | bytes 131074 | tf_op jit(solution)/shard_map/jit(_where)/select_n | solution.py:56
  14.9 1.7 %fusion.1 = bf16[2,6,256,256]{3,2,0,1:T(8,128)(2,1)S(1)} fusion(f32[256,6,2,256]{3,0,2,1:T(8,128)S(1)} %copy-done.1, bf16[128,6,2,256]{3,0,2,1:T(8,128)(2,1)} %collective-permute-done, bf16[256,128]{1,0:T(8,128)(2,1)} %constant_dynamic-slice_fusion.1), kind=kOutput, calls=%fused_computation.12 | convolution fusion | flops 202899456 | bytes 5570560 | tf_op jit(solution)/shard_map/rk,kmlc->lmrc/dot_general | solution.py:92
  16.7 0.6 %multiply_reduce_fusion = f32[256,512]{1,0:T(8,128)S(1)} fusion(bf16[2,6,256,256]{3,2,0,1:T(8,128)(2,1)S(1)} %fusion.1, bf16[512,256]{1,0:T(8,128)(2,1)S(1)} %copy-done, bf16[2,6,256,512]{3,2,1,0:T(8,128)(2,1)S(1)} %bitcast.111), kind=kOutput, calls=%fused_computation.1 | convolution fusion | flops 404881408 | bytes 3145728 | tf_op jit(solution)/shard_map/mrc,nc->mrn/dot_general | solution.py:103
  17.4 3.1 %collective-permute-start.9 = (bf16[128,512]{1,0:T(8,128)(2,1)S(1)}, bf16[128,512]{1,0:T(8,128)(2,1)S(1)}, u32[]{:S(2)}, u32[]{:S(2)}) collective-permute-start(bf16[128,512]{1,0:T(8,128)(2,1)S(1)} %dynamic-slice_convert_fusion), channel_id=1, source_target_pairs={{0,4},{4,0},{8,12},{12,8},{1,5},{5,1},{9,13},{13,9},{2,6},{6,2},{1... | collective-permute-start | bytes 393224 | tf_op jit(solution)/shard_map/ppermute | solution.py:19
  20.5 0.6 %multiply_reduce_fusion.1 = f32[256,512]{1,0:T(8,128)S(1)} fusion(bf16[2,6,256,256]{3,2,0,1:T(8,128)(2,1)S(1)} %fusion.1, bf16[512,256]{1,0:T(8,128)(2,1)S(1)} %copy-done, bf16[2,6,256,512]{3,2,1,0:T(8,128)(2,1)S(1)} %bitcast.112), kind=kOutput, calls=%fused_computation.2 | convolution fusion | flops 404881408 | bytes 3145728 | tf_op jit(solution)/shard_map/mrc,nc->mrn/dot_general | solution.py:103
  21.2 3.4 %collective-permute-done.9 = bf16[128,512]{1,0:T(8,128)(2,1)S(1)} collective-permute-done((bf16[128,512]{1,0:T(8,128)(2,1)S(1)}, bf16[128,512]{1,0:T(8,128)(2,1)S(1)}, u32[]{:S(2)}, u32[]{:S(2)}) %collective-permute-start.9) | collective-permute-done | bytes 131104 | tf_op jit(solution)/shard_map/ppermute | solution.py:19
  24.7 3.0 %collective-permute-start.10 = (bf16[128,512]{1,0:T(8,128)(2,1)S(1)}, bf16[128,512]{1,0:T(8,128)(2,1)S(1)}, u32[]{:S(2)}, u32[]{:S(2)}) collective-permute-start(bf16[128,512]{1,0:T(8,128)(2,1)S(1)} %fusion.35), channel_id=1, source_target_pairs={{0,8},{4,12},{8,0},{12,4},{1,9},{5,13},{9,1},{13,5},{2,10},{6,14},... | collective-permute-start | bytes 393224 | tf_op jit(solution)/shard_map/ppermute | solution.py:23
  27.8 2.8 %collective-permute-start.2 = (bf16[128,512]{1,0:T(8,128)(2,1)S(1)}, bf16[128,512]{1,0:T(8,128)(2,1)S(1)}, u32[]{:S(2)}, u32[]{:S(2)}) collective-permute-start(bf16[128,512]{1,0:T(8,128)(2,1)S(1)} %fusion.34), channel_id=1, source_target_pairs={{0,8},{4,12},{8,0},{12,4},{1,9},{5,13},{9,1},{13,5},{2,10},{6,14},... | collective-permute-start | bytes 393224 | tf_op jit(solution)/shard_map/ppermute | solution.py:23
  30.6 6.3 %collective-permute-done.10 = bf16[128,512]{1,0:T(8,128)(2,1)S(1)} collective-permute-done((bf16[128,512]{1,0:T(8,128)(2,1)S(1)}, bf16[128,512]{1,0:T(8,128)(2,1)S(1)}, u32[]{:S(2)}, u32[]{:S(2)}) %collective-permute-start.10) | collective-permute-done | bytes 131104 | tf_op jit(solution)/shard_map/ppermute | solution.py:23
  37.0 0.6 %collective-permute-start.13 = (bf16[128,512]{1,0:T(8,128)(2,1)S(1)}, bf16[128,512]{1,0:T(8,128)(2,1)S(1)}, u32[]{:S(2)}, u32[]{:S(2)}) collective-permute-start(bf16[128,512]{1,0:T(8,128)(2,1)S(1)} %get-tuple-element.8), channel_id=1, source_target_pairs={{0,4},{4,0},{8,12},{12,8},{1,5},{5,1},{9,13},{13,9},{2,6},{6,2},{1... | collective-permute-start | bytes 393224 | tf_op jit(solution)/shard_map/ppermute | solution.py:109
  37.6 1.0 %collective-permute-done.2 = bf16[128,512]{1,0:T(8,128)(2,1)S(1)} collective-permute-done((bf16[128,512]{1,0:T(8,128)(2,1)S(1)}, bf16[128,512]{1,0:T(8,128)(2,1)S(1)}, u32[]{:S(2)}, u32[]{:S(2)}) %collective-permute-start.2) | collective-permute-done | bytes 131104 | tf_op jit(solution)/shard_map/ppermute | solution.py:23
  41.4 1.8 %collective-permute-done.13 = bf16[128,512]{1,0:T(8,128)(2,1)S(1)} collective-permute-done((bf16[128,512]{1,0:T(8,128)(2,1)S(1)}, bf16[128,512]{1,0:T(8,128)(2,1)S(1)}, u32[]{:S(2)}, u32[]{:S(2)}) %collective-permute-start.13) | collective-permute-done | bytes 131104 | tf_op jit(solution)/shard_map/ppermute | solution.py:109
  43.7 1.0 %collective-permute-done.6 = bf16[128,512]{1,0:T(8,128)(2,1)S(1)} collective-permute-done((bf16[128,512]{1,0:T(8,128)(2,1)S(1)}, bf16[128,512]{1,0:T(8,128)(2,1)S(1)}, u32[]{:S(2)}, u32[]{:S(2)}) %collective-permute-start.6) | collective-permute-done | bytes 131104 | tf_op jit(solution)/shard_map/ppermute | solution.py:109
  45.3 0.6 %collective-permute-start.8 = (bf16[3,128,256]{2,1,0:T(8,128)(2,1)S(1)}, bf16[3,128,256]{2,1,0:T(8,128)(2,1)S(1)}, u32[]{:S(2)}, u32[]{:S(2)}) collective-permute-start(bf16[3,128,256]{2,1,0:T(8,128)(2,1)S(1)} %get-tuple-element.14), channel_id=1, source_target_pairs={{0,1},{1,0},{2,3},{3,2},{4,5},{5,4},{6,7},{7,6},{8,9},{9,8},{10,11... | collective-permute-start | bytes 589832 | tf_op jit(solution)/shard_map/ppermute | solution.py:8
  46.4 0.6 %collective-permute-start.15 = (bf16[3,128,256]{2,1,0:T(8,128)(2,1)S(1)}, bf16[3,128,256]{2,1,0:T(8,128)(2,1)S(1)}, u32[]{:S(2)}, u32[]{:S(2)}) collective-permute-start(bf16[3,128,256]{2,1,0:T(8,128)(2,1)S(1)} %get-tuple-element.18), channel_id=1, source_target_pairs={{0,1},{1,0},{2,3},{3,2},{4,5},{5,4},{6,7},{7,6},{8,9},{9,8},{10,11... | collective-permute-start | bytes 589832 | tf_op jit(solution)/shard_map/ppermute | solution.py:8
  49.1 0.8 %copy-done.2 = bf16[128,6,2,256]{3,2,1,0:T(2,128)(2,1)S(1)} copy-done((bf16[128,6,2,256]{3,2,1,0:T(2,128)(2,1)S(1)}, bf16[128,6,2,256]{3,2,1,0:T(2,128)(2,1)}, u32[]{:S(2)}) %copy-start.2) | copy-done | bytes 786456
  50.2 1.7 %copy.22 = bf16[128,6,2,256]{3,2,1,0:T(2,128)(2,1)} copy(bf16[128,6,2,256]{3,0,1,2:T(8,128)(2,1)S(1)} %fusion) | data formatting | bytes 1572864 | tf_op jit(solution)/shard_map/convert_element_type | solution.py:128
  (62 shorter events, 7.7 us)
Async XLA Ops:
  0.0 16.7 %copy-start = (bf16[512,256]{1,0:T(8,128)(2,1)S(1)}, bf16[512,256]{1,0:T(8,128)(2,1)}, u32[]{:S(2)}) copy-start(bf16[512,256]{1,0:T(8,128)(2,1)} %param.9) | copy-start | bytes 786436
  0.0 4.2 %copy-start.5 = (f32[256,2,512]{2,1,0:T(2,128)S(1)}, f32[256,2,512]{2,1,0:T(2,128)}, u32[]{:S(2)}) copy-start(f32[256,2,512]{2,1,0:T(2,128)} %param.7) | copy-start | bytes 3145732
  1.6 12.4 %collective-permute-start.3 = (bf16[256,128]{1,0:T(8,128)(2,1)}, bf16[256,128]{1,0:T(8,128)(2,1)}, u32[]{:S(2)}, u32[]{:S(2)}) collective-permute-start(bf16[256,128]{1,0:T(8,128)(2,1)} %constant_dynamic-slice_fusion.1), channel_id=1, source_target_pairs={{0,1},{1,0},{2,3},{3,2},{4,5},{5,4},{6,7},{7,6},{8,9},{9,8},{10,11... | collective-permute-start | bytes 196616 | tf_op jit(solution)/shard_map/ppermute | solution.py:8
  4.1 10.6 %collective-permute-start = (bf16[128,6,2,256]{3,0,2,1:T(8,128)(2,1)}, bf16[128,6,2,256]{3,0,2,1:T(8,128)(2,1)}, u32[]{:S(2)}, u32[]{:S(2)}) collective-permute-start(bf16[128,6,2,256]{3,0,2,1:T(8,128)(2,1)} %copy.8), channel_id=1, source_target_pairs={{0,1},{1,0},{2,3},{3,2},{4,5},{5,4},{6,7},{7,6},{8,9},{9,8},{10,11... | collective-permute-start | bytes 2359304 | tf_op jit(solution)/shard_map/ppermute | solution.py:8
  6.0 2.6 %copy-start.3 = (bf16[256,256]{1,0:T(8,128)(2,1)S(1)}, bf16[256,256]{1,0:T(8,128)(2,1)}, u32[]{:S(2)}) copy-start(bf16[256,256]{1,0:T(8,128)(2,1)} %param.8) | copy-start | bytes 393220
  12.9 1.0 %copy-start.4 = (f32[1,256,512]{2,0,1:T(1,128)S(1)}, f32[1,256,512]{2,0,1:T(1,128)}, u32[]{:S(2)}) copy-start(f32[1,256,512]{2,0,1:T(1,128)} %get-tuple-element.12) | copy-start | bytes 1572868
  12.9 2.1 %copy-start.1 = (f32[256,6,2,256]{3,0,2,1:T(8,128)S(1)}, f32[256,6,2,256]{3,0,2,1:T(8,128)}, u32[]{:S(2)}) copy-start(f32[256,6,2,256]{3,0,2,1:T(8,128)} %fusion.37) | copy-start | bytes 9437188
  17.4 7.3 %collective-permute-start.9 = (bf16[128,512]{1,0:T(8,128)(2,1)S(1)}, bf16[128,512]{1,0:T(8,128)(2,1)S(1)}, u32[]{:S(2)}, u32[]{:S(2)}) collective-permute-start(bf16[128,512]{1,0:T(8,128)(2,1)S(1)} %dynamic-slice_convert_fusion), channel_id=1, source_target_pairs={{0,4},{4,0},{8,12},{12,8},{1,5},{5,1},{9,13},{13,9},{2,6},{6,2},{1... | collective-permute-start | bytes 393224 | tf_op jit(solution)/shard_map/ppermute | solution.py:19
  21.1 6.6 %collective-permute-start.1 = (bf16[128,512]{1,0:T(8,128)(2,1)S(1)}, bf16[128,512]{1,0:T(8,128)(2,1)S(1)}, u32[]{:S(2)}, u32[]{:S(2)}) collective-permute-start(bf16[128,512]{1,0:T(8,128)(2,1)S(1)} %dynamic-slice_convert_fusion.1), channel_id=1, source_target_pairs={{0,4},{4,0},{8,12},{12,8},{1,5},{5,1},{9,13},{13,9},{2,6},{6,2},{1... | collective-permute-start | bytes 393224 | tf_op jit(solution)/shard_map/ppermute | solution.py:19
  24.7 12.2 %collective-permute-start.10 = (bf16[128,512]{1,0:T(8,128)(2,1)S(1)}, bf16[128,512]{1,0:T(8,128)(2,1)S(1)}, u32[]{:S(2)}, u32[]{:S(2)}) collective-permute-start(bf16[128,512]{1,0:T(8,128)(2,1)S(1)} %fusion.35), channel_id=1, source_target_pairs={{0,8},{4,12},{8,0},{12,4},{1,9},{5,13},{9,1},{13,5},{2,10},{6,14},... | collective-permute-start | bytes 393224 | tf_op jit(solution)/shard_map/ppermute | solution.py:23
  27.8 10.9 %collective-permute-start.2 = (bf16[128,512]{1,0:T(8,128)(2,1)S(1)}, bf16[128,512]{1,0:T(8,128)(2,1)S(1)}, u32[]{:S(2)}, u32[]{:S(2)}) collective-permute-start(bf16[128,512]{1,0:T(8,128)(2,1)S(1)} %fusion.34), channel_id=1, source_target_pairs={{0,8},{4,12},{8,0},{12,4},{1,9},{5,13},{9,1},{13,5},{2,10},{6,14},... | collective-permute-start | bytes 393224 | tf_op jit(solution)/shard_map/ppermute | solution.py:23
  37.0 6.3 %collective-permute-start.13 = (bf16[128,512]{1,0:T(8,128)(2,1)S(1)}, bf16[128,512]{1,0:T(8,128)(2,1)S(1)}, u32[]{:S(2)}, u32[]{:S(2)}) collective-permute-start(bf16[128,512]{1,0:T(8,128)(2,1)S(1)} %get-tuple-element.8), channel_id=1, source_target_pairs={{0,4},{4,0},{8,12},{12,8},{1,5},{5,1},{9,13},{13,9},{2,6},{6,2},{1... | collective-permute-start | bytes 393224 | tf_op jit(solution)/shard_map/ppermute | solution.py:109
  38.7 5.9 %collective-permute-start.6 = (bf16[128,512]{1,0:T(8,128)(2,1)S(1)}, bf16[128,512]{1,0:T(8,128)(2,1)S(1)}, u32[]{:S(2)}, u32[]{:S(2)}) collective-permute-start(bf16[128,512]{1,0:T(8,128)(2,1)S(1)} %get-tuple-element.6), channel_id=1, source_target_pairs={{0,4},{4,0},{8,12},{12,8},{1,5},{5,1},{9,13},{13,9},{2,6},{6,2},{1... | collective-permute-start | bytes 393224 | tf_op jit(solution)/shard_map/ppermute | solution.py:109
  39.7 5.6 %collective-permute-start.4 = (bf16[3,128,256]{2,1,0:T(8,128)(2,1)S(1)}, bf16[3,128,256]{2,1,0:T(8,128)(2,1)S(1)}, u32[]{:S(2)}, u32[]{:S(2)}) collective-permute-start(bf16[3,128,256]{2,1,0:T(8,128)(2,1)S(1)} %get-tuple-element.15), channel_id=1, source_target_pairs={{0,1},{1,0},{2,3},{3,2},{4,5},{5,4},{6,7},{7,6},{8,9},{9,8},{10,11... | collective-permute-start | bytes 589832 | tf_op jit(solution)/shard_map/ppermute | solution.py:8
  39.7 6.3 %collective-permute-start.5 = (bf16[3,128,256]{2,1,0:T(8,128)(2,1)S(1)}, bf16[3,128,256]{2,1,0:T(8,128)(2,1)S(1)}, u32[]{:S(2)}, u32[]{:S(2)}) collective-permute-start(bf16[3,128,256]{2,1,0:T(8,128)(2,1)S(1)} %get-tuple-element.16), channel_id=1, source_target_pairs={{0,1},{1,0},{2,3},{3,2},{4,5},{5,4},{6,7},{7,6},{8,9},{9,8},{10,11... | collective-permute-start | bytes 589832 | tf_op jit(solution)/shard_map/ppermute | solution.py:8
  41.0 5.4 %collective-permute-start.11 = (bf16[3,128,256]{2,1,0:T(8,128)(2,1)S(1)}, bf16[3,128,256]{2,1,0:T(8,128)(2,1)S(1)}, u32[]{:S(2)}, u32[]{:S(2)}) collective-permute-start(bf16[3,128,256]{2,1,0:T(8,128)(2,1)S(1)} %get-tuple-element.19), channel_id=1, source_target_pairs={{0,1},{1,0},{2,3},{3,2},{4,5},{5,4},{6,7},{7,6},{8,9},{9,8},{10,11... | collective-permute-start | bytes 589832 | tf_op jit(solution)/shard_map/ppermute | solution.py:8
  43.3 3.9 %collective-permute-start.12 = (bf16[3,128,256]{2,1,0:T(8,128)(2,1)S(1)}, bf16[3,128,256]{2,1,0:T(8,128)(2,1)S(1)}, u32[]{:S(2)}, u32[]{:S(2)}) collective-permute-start(bf16[3,128,256]{2,1,0:T(8,128)(2,1)S(1)} %get-tuple-element.20), channel_id=1, source_target_pairs={{0,1},{1,0},{2,3},{3,2},{4,5},{5,4},{6,7},{7,6},{8,9},{9,8},{10,11... | collective-permute-start | bytes 589832 | tf_op jit(solution)/shard_map/ppermute | solution.py:8
  45.1 2.3 %collective-permute-start.7 = (bf16[3,128,256]{2,1,0:T(8,128)(2,1)S(1)}, bf16[3,128,256]{2,1,0:T(8,128)(2,1)S(1)}, u32[]{:S(2)}, u32[]{:S(2)}) collective-permute-start(bf16[3,128,256]{2,1,0:T(8,128)(2,1)S(1)} %get-tuple-element.13), channel_id=1, source_target_pairs={{0,1},{1,0},{2,3},{3,2},{4,5},{5,4},{6,7},{7,6},{8,9},{9,8},{10,11... | collective-permute-start | bytes 589832 | tf_op jit(solution)/shard_map/ppermute | solution.py:8
  45.3 2.4 %collective-permute-start.8 = (bf16[3,128,256]{2,1,0:T(8,128)(2,1)S(1)}, bf16[3,128,256]{2,1,0:T(8,128)(2,1)S(1)}, u32[]{:S(2)}, u32[]{:S(2)}) collective-permute-start(bf16[3,128,256]{2,1,0:T(8,128)(2,1)S(1)} %get-tuple-element.14), channel_id=1, source_target_pairs={{0,1},{1,0},{2,3},{3,2},{4,5},{5,4},{6,7},{7,6},{8,9},{9,8},{10,11... | collective-permute-start | bytes 589832 | tf_op jit(solution)/shard_map/ppermute | solution.py:8
  46.1 1.9 %collective-permute-start.14 = (bf16[3,128,256]{2,1,0:T(8,128)(2,1)S(1)}, bf16[3,128,256]{2,1,0:T(8,128)(2,1)S(1)}, u32[]{:S(2)}, u32[]{:S(2)}) collective-permute-start(bf16[3,128,256]{2,1,0:T(8,128)(2,1)S(1)} %get-tuple-element.17), channel_id=1, source_target_pairs={{0,1},{1,0},{2,3},{3,2},{4,5},{5,4},{6,7},{7,6},{8,9},{9,8},{10,11... | collective-permute-start | bytes 589832 | tf_op jit(solution)/shard_map/ppermute | solution.py:8
  46.4 2.1 %collective-permute-start.15 = (bf16[3,128,256]{2,1,0:T(8,128)(2,1)S(1)}, bf16[3,128,256]{2,1,0:T(8,128)(2,1)S(1)}, u32[]{:S(2)}, u32[]{:S(2)}) collective-permute-start(bf16[3,128,256]{2,1,0:T(8,128)(2,1)S(1)} %get-tuple-element.18), channel_id=1, source_target_pairs={{0,1},{1,0},{2,3},{3,2},{4,5},{5,4},{6,7},{7,6},{8,9},{9,8},{10,11... | collective-permute-start | bytes 589832 | tf_op jit(solution)/shard_map/ppermute | solution.py:8
  48.8 1.1 %copy-start.2 = (bf16[128,6,2,256]{3,2,1,0:T(2,128)(2,1)S(1)}, bf16[128,6,2,256]{3,2,1,0:T(2,128)(2,1)}, u32[]{:S(2)}) copy-start(bf16[128,6,2,256]{3,2,1,0:T(2,128)(2,1)} %param.6) | copy-start | bytes 2359300

commit v15 on v11

--- a/solution.py
+++ b/solution.py
@@ -56,7 +56,6 @@
     n_lev = anomalies.shape[2]
 
     anom_t = jnp.transpose(anomalies, (2, 1, 0, 3))
-    prec_t = jnp.transpose(precision, (1, 0, 2))
 
     rf_own = lax.dynamic_slice_in_dim(row_factor, h * kh, kh, 1)
     rf_other = lax.dynamic_slice_in_dim(row_factor, (1 - h) * kh, kh, 1)
@@ -77,13 +76,13 @@
         expanded = expanded_all[l]
         fields = jnp.einsum("mrc,nc->mrn", expanded, col_factor, preferred_element_type=jnp.float32)
         inc = jnp.sum(a.astype(jnp.float32) * fields, axis=0)
-        prec = prec_t[l]
         if pow2:
             part = _reduce_scatter_rows(inc, "mem", n_mem, jnp.bfloat16)
-            w_blk = (lax.dynamic_slice_in_dim(prec, start, blk, 0) * part).astype(jnp.bfloat16)
+            prec_blk = lax.dynamic_slice(precision, (start, l, 0), (blk, 1, precision.shape[2]))
+            w_blk = (prec_blk[:, 0, :] * part).astype(jnp.bfloat16)
             weighted = _all_gather_rows(w_blk, "mem", n_mem)
         else:
-            weighted = (prec * lax.psum(inc, "mem")).astype(jnp.bfloat16)
+            weighted = (precision[:, l, :] * lax.psum(inc, "mem")).astype(jnp.bfloat16)
         scaled = (a.astype(jnp.float32) * weighted.astype(jnp.float32)[None]).astype(jnp.bfloat16)
         projected = jnp.einsum(
             "mrn,nc->mrc", scaled, col_factor, preferred_element_type=jnp.float32

time: 44.7 us -> 45.1 us (level)
  local copies, waits for them, and re-layouts: 9.63 us -> 11.2 us
  matrix products: 6.49 us -> 5.14 us
  waiting for transfers between devices: 15.7 us -> 16.2 us
    dynamic_slice x2 -> x1, local copies, waits for them, and re-layouts: 0.05 us -> 1.67 us  [local(): lax.dynamic_slice(precision, (start, l, 0), (blk, 1, precision.shape[2]))]
    dot_general x1, matrix products: 1.86 us -> 0.57 us  [local(): jnp.einsum('rk,kmlc->lmrc', rf_other, ctrl_other, preferred_element_type=...]
    slice x1 -> x0, local copies, waits for them, and re-layouts: 0.81 us -> none  [local(): prec = prec_t[l]]
    unnamed x12 -> x10, local copies, waits for them, and re-layouts: 6.08 us -> 6.86 us
    ppermute x2, waiting for transfers between devices: 7.41 us -> 7.99 us  [_reduce_scatter_rows(): recv = lax.ppermute(x.astype(wire), axis, [(i, i ^ d) for i in range(size)])]
  transfers between devices with their start and end apart: 12 -> 12, of which waited for: 7 -> 8; matrix products, arithmetic and copies ran while one was open for 28% -> 27% of each run, Pallas kernels for 0% -> 0%
where the time goes in v15:
time: 45.1 us; the launch traced here: 44.8 us
  waiting for transfers between devices  16.2 us (36%)
  starting transfers between devices  11.4 us (25%)
  local copies, waits for them, and re-layouts  11.2 us (25%)
  matrix products  5.14 us (11%)
  other arithmetic  0.62 us (1%)
    ppermute x2, waiting for transfers between devices, _reduce_scatter_rows(): recv = lax.ppermute(x.astype(wire), axis, [(i, i ^ d) for i in range(size)])  7.99 us
    unnamed x10, local copies, waits for them, and re-layouts  6.86 us
    ppermute x2, starting transfers between devices, _reduce_scatter_rows(): recv = lax.ppermute(x.astype(wire), axis, [(i, i ^ d) for i in range(size)])  5.63 us
    ppermute x2, waiting for transfers between devices, _all_gather_rows(): recv = lax.ppermute(x, axis, [(i, i ^ d) for i in range(size)])  4.03 us
    ppermute x2, waiting for transfers between devices, _reduce_scatter_rows(): lax.ppermute(send.astype(wire), axis, [(i, i ^ d) for i in range(size)])  3.42 us
    ppermute x2, starting transfers between devices, _reduce_scatter_rows(): lax.ppermute(send.astype(wire), axis, [(i, i ^ d) for i in range(size)])  3.25 us
    ppermute x6, starting transfers between devices, _swap(): return lax.ppermute(x, axis, [(0, 1), (1, 0)])  1.71 us
    convert_element_type x1, local copies, waits for them, and re-layouts, local(): (control.astype(jnp.float32) + jnp.stack(outs, axis=2)).astype(jnp.bfloat16)  1.69 us
  transfers between devices with their start and end apart: 12, of which 8 were waited for; matrix products, arithmetic and copies ran while one was open for 27% of the time, Pallas kernels for 0%

profile of v15, /device:TPU:0, one launch (start us, length us, event | category | flops | bytes accessed | tf_op | source)
XLA Modules:
  0.0 44.8 jit_solution(14997652080481261520)
XLA Ops:
  0.0 1.3 %copy.20 = bf16[128,6,2,256]{3,0,2,1:T(8,128)(2,1)S(1)} copy(bf16[128,6,2,256]{3,2,1,0:T(2,128)(2,1)} %param.6) | data formatting | bytes 1572864 | tf_op args[1]
  1.3 0.5 %collective-permute-start = (bf16[128,6,2,256]{3,0,2,1:T(8,128)(2,1)S(1)}, bf16[128,6,2,256]{3,0,2,1:T(8,128)(2,1)S(1)}, u32[]{:S(2)}, u32[]{:S(2)}) collective-permute-start(bf16[128,6,2,256]{3,0,2,1:T(8,128)(2,1)S(1)} %copy.20), channel_id=1, source_target_pairs={{0,1},{1,0},{2,3},{3,2},{4,5},{5,4},{6,7},{7,6},{8,9},{9,8},{10,11... | collective-permute-start | bytes 2359304 | tf_op jit(solution)/shard_map/ppermute | solution.py:8
  1.8 0.8 %constant_dynamic-slice_fusion.1 = bf16[256,128]{1,0:T(8,128)(2,1)S(1)} fusion(bf16[256,256]{1,0:T(8,128)(2,1)} %param.8, s32[]{:T(128)S(6)} %select_n.61), kind=kLoop, calls=%fused_computation.70 | loop fusion | bytes 131076 | tf_op jit(solution)/shard_map/dynamic_slice | solution.py:61
  2.7 4.3 %copy.60 = bf16[256,6,2,512]{3,0,1,2:T(8,128)(2,1)} copy(bf16[256,6,2,512]{3,2,1,0:T(2,128)(2,1)} %param.5) | data formatting | bytes 6291456 | tf_op args[0]
  7.0 1.7 %constant_dynamic-slice_fusion.2 = (f32[128,1,512]{2,1,0:T(1,128)S(1)}, f32[128,1,512]{2,1,0:T(1,128)S(1)}) fusion(f32[256,2,512]{2,1,0:T(2,128)} %param.7, s32[]{:T(128)S(6)} %select_n.60), kind=kLoop, calls=%fused_computation.71 | loop fusion | bytes 1048580 | tf_op jit(solution)/shard_map/dynamic_slice | solution.py:81
  8.7 0.6 %fusion.31 = f32[256,6,2,256]{3,0,2,1:T(8,128)S(1)} fusion(bf16[256,256]{1,0:T(8,128)(2,1)S(1)} %copy-done.3, s32[]{:T(128)S(6)} %select_n.57, bf16[128,6,2,256]{3,2,1,0:T(2,128)(2,1)S(1)} %copy-done.1), kind=kOutput, calls=%fused_computation.50 | convolution fusion | flops 201326592 | bytes 3997700 | tf_op jit(solution)/shard_map/rk,kmlc->lmrc/dot_general | solution.py:65
  9.3 0.6 %fusion.11 = bf16[2,6,256,256]{3,2,0,1:T(8,128)(2,1)S(1)} fusion(f32[256,6,2,256]{3,0,2,1:T(8,128)S(1)} %fusion.31, bf16[128,6,2,256]{3,0,2,1:T(8,128)(2,1)S(1)} %collective-permute-done, bf16[256,128]{1,0:T(8,128)(2,1)S(1)} %constant_dynamic-slice_fusion.1), kind=kOutput, calls=%fused_computation.18 | convolution fusion | flops 202899456 | bytes 5570560 | tf_op jit(solution)/shard_map/rk,kmlc->lmrc/dot_general | solution.py:66
  9.9 1.3 %copy-done.2 = bf16[256,6,2,512]{3,0,1,2:T(8,128)(2,1)S(1)} copy-done((bf16[256,6,2,512]{3,0,1,2:T(8,128)(2,1)S(1)}, bf16[256,6,2,512]{3,0,1,2:T(8,128)(2,1)}, u32[]{:S(2)}) %copy-start.2) | copy-done | bytes 3145752
  11.1 0.7 %fusion = f32[256,512]{1,0:T(8,128)S(1)} fusion(bf16[2,6,256,512]{3,2,1,0:T(8,128)(2,1)S(1)} %bitcast.91, bf16[2,6,256,256]{3,2,0,1:T(8,128)(2,1)S(1)} %fusion.11, bf16[512,256]{1,0:T(8,128)(2,1)S(1)} %copy-done), kind=kOutput, calls=%fused_computation.4 | convolution fusion | flops 404881408 | bytes 3145728 | tf_op jit(solution)/shard_map/mrc,nc->mrn/dot_general | solution.py:77
  11.8 3.2 %collective-permute-start.1 = (bf16[128,512]{1,0:T(8,128)(2,1)S(1)}, bf16[128,512]{1,0:T(8,128)(2,1)S(1)}, u32[]{:S(2)}, u32[]{:S(2)}) collective-permute-start(bf16[128,512]{1,0:T(8,128)(2,1)S(1)} %dynamic-slice_convert_fusion.1), channel_id=1, source_target_pairs={{0,4},{4,0},{8,12},{12,8},{1,5},{5,1},{9,13},{13,9},{2,6},{6,2},{1... | collective-permute-start | bytes 393224 | tf_op jit(solution)/shard_map/ppermute | solution.py:19
  15.0 0.7 %fusion.2 = f32[256,512]{1,0:T(8,128)S(1)} fusion(bf16[2,6,256,512]{3,2,1,0:T(8,128)(2,1)S(1)} %bitcast.92, bf16[2,6,256,256]{3,2,0,1:T(8,128)(2,1)S(1)} %fusion.11, bf16[512,256]{1,0:T(8,128)(2,1)S(1)} %copy-done), kind=kOutput, calls=%fused_computation.6 | convolution fusion | flops 404881408 | bytes 3145728 | tf_op jit(solution)/shard_map/mrc,nc->mrn/dot_general | solution.py:77
  15.8 3.4 %collective-permute-done.1 = bf16[128,512]{1,0:T(8,128)(2,1)S(1)} collective-permute-done((bf16[128,512]{1,0:T(8,128)(2,1)S(1)}, bf16[128,512]{1,0:T(8,128)(2,1)S(1)}, u32[]{:S(2)}, u32[]{:S(2)}) %collective-permute-start.1) | collective-permute-done | bytes 131104 | tf_op jit(solution)/shard_map/ppermute | solution.py:19
  19.3 2.9 %collective-permute-start.2 = (bf16[128,512]{1,0:T(8,128)(2,1)S(1)}, bf16[128,512]{1,0:T(8,128)(2,1)S(1)}, u32[]{:S(2)}, u32[]{:S(2)}) collective-permute-start(bf16[128,512]{1,0:T(8,128)(2,1)S(1)} %fusion.28), channel_id=1, source_target_pairs={{0,8},{4,12},{8,0},{12,4},{1,9},{5,13},{9,1},{13,5},{2,10},{6,14},... | collective-permute-start | bytes 393224 | tf_op jit(solution)/shard_map/ppermute | solution.py:23
  22.2 2.8 %collective-permute-start.8 = (bf16[128,512]{1,0:T(8,128)(2,1)S(1)}, bf16[128,512]{1,0:T(8,128)(2,1)S(1)}, u32[]{:S(2)}, u32[]{:S(2)}) collective-permute-start(bf16[128,512]{1,0:T(8,128)(2,1)S(1)} %fusion.29), channel_id=1, source_target_pairs={{0,8},{4,12},{8,0},{12,4},{1,9},{5,13},{9,1},{13,5},{2,10},{6,14},... | collective-permute-start | bytes 393224 | tf_op jit(solution)/shard_map/ppermute | solution.py:23
  24.9 6.6 %collective-permute-done.2 = bf16[128,512]{1,0:T(8,128)(2,1)S(1)} collective-permute-done((bf16[128,512]{1,0:T(8,128)(2,1)S(1)}, bf16[128,512]{1,0:T(8,128)(2,1)S(1)}, u32[]{:S(2)}, u32[]{:S(2)}) %collective-permute-start.2) | collective-permute-done | bytes 131104 | tf_op jit(solution)/shard_map/ppermute | solution.py:23
  31.7 0.3 collective-permute-start.3
  32.0 1.3 %collective-permute-done.8 = bf16[128,512]{1,0:T(8,128)(2,1)S(1)} collective-permute-done((bf16[128,512]{1,0:T(8,128)(2,1)S(1)}, bf16[128,512]{1,0:T(8,128)(2,1)S(1)}, u32[]{:S(2)}, u32[]{:S(2)}) %collective-permute-start.8) | collective-permute-done | bytes 131104 | tf_op jit(solution)/shard_map/ppermute | solution.py:23
  33.4 0.5 %collective-permute-start.9 = (bf16[128,512]{1,0:T(8,128)(2,1)S(1)}, bf16[128,512]{1,0:T(8,128)(2,1)S(1)}, u32[]{:S(2)}, u32[]{:S(2)}) collective-permute-start(bf16[128,512]{1,0:T(8,128)(2,1)S(1)} %fusion.21), channel_id=1, source_target_pairs={{0,4},{4,0},{8,12},{12,8},{1,5},{5,1},{9,13},{13,9},{2,6},{6,2},{1... | collective-permute-start | bytes 393224 | tf_op jit(solution)/shard_map/ppermute | solution.py:33
  33.9 3.9 %collective-permute-done.3 = bf16[128,512]{1,0:T(8,128)(2,1)S(1)} collective-permute-done((bf16[128,512]{1,0:T(8,128)(2,1)S(1)}, bf16[128,512]{1,0:T(8,128)(2,1)S(1)}, u32[]{:S(2)}, u32[]{:S(2)}) %collective-permute-start.3) | collective-permute-done | bytes 131104 | tf_op jit(solution)/shard_map/ppermute | solution.py:33
  37.9 0.6 %fusion.12 = bf16[6,256,256]{2,1,0:T(8,128)(2,1)S(1)} fusion(f32[256,512]{1,0:T(8,128)S(1)} %maximum_convert_fusion, bf16[2,6,256,512]{3,2,1,0:T(8,128)(2,1)S(1)} %bitcast.93, bf16[512,256]{1,0:T(8,128)(2,1)S(1)} %copy-done), kind=kOutput, calls=%fused_computation.19 | convolution fusion | flops 405405696 | bytes 3145728 | tf_op jit(solution)/shard_map/mrn,nc->mrc/dot_general | solution.py:87
  38.6 0.5 %collective-permute-start.6 = (bf16[3,256,256]{2,1,0:T(8,128)(2,1)S(1)}, bf16[3,256,256]{2,1,0:T(8,128)(2,1)S(1)}, u32[]{:S(2)}, u32[]{:S(2)}) collective-permute-start(bf16[3,256,256]{2,1,0:T(8,128)(2,1)S(1)} %get-tuple-element.8), channel_id=1, source_target_pairs={{0,1},{1,0},{2,3},{3,2},{4,5},{5,4},{6,7},{7,6},{8,9},{9,8},{10,11... | collective-permute-start | bytes 1179656 | tf_op jit(solution)/shard_map/ppermute | solution.py:8
  39.3 0.6 %fusion.15 = bf16[6,256,256]{2,1,0:T(8,128)(2,1)S(1)} fusion(f32[256,512]{1,0:T(8,128)S(1)} %maximum_convert_fusion.1, bf16[2,6,256,512]{3,2,1,0:T(8,128)(2,1)S(1)} %bitcast.94, bf16[512,256]{1,0:T(8,128)(2,1)S(1)} %copy-done), kind=kOutput, calls=%fused_computation.20 | convolution fusion | flops 405405696 | bytes 3145728 | tf_op jit(solution)/shard_map/mrn,nc->mrc/dot_general | solution.py:87
  40.1 0.5 %collective-permute-start.11 = (bf16[3,256,256]{2,1,0:T(8,128)(2,1)S(1)}, bf16[3,256,256]{2,1,0:T(8,128)(2,1)S(1)}, u32[]{:S(2)}, u32[]{:S(2)}) collective-permute-start(bf16[3,256,256]{2,1,0:T(8,128)(2,1)S(1)} %get-tuple-element.10), channel_id=1, source_target_pairs={{0,1},{1,0},{2,3},{3,2},{4,5},{5,4},{6,7},{7,6},{8,9},{9,8},{10,11... | collective-permute-start | bytes 1179656 | tf_op jit(solution)/shard_map/ppermute | solution.py:8
  43.1 1.7 %copy.29 = bf16[128,6,2,256]{3,2,1,0:T(2,128)(2,1)} copy(bf16[128,6,2,256]{3,0,1,2:T(8,128)(2,1)S(1)} %fusion.8) | data formatting | bytes 1572864 | tf_op jit(solution)/shard_map/convert_element_type | solution.py:102
  (38 shorter events, 3.4 us)
Async XLA Ops:
  0.0 9.8 %copy-start = (bf16[512,256]{1,0:T(8,128)(2,1)S(1)}, bf16[512,256]{1,0:T(8,128)(2,1)}, u32[]{:S(2)}) copy-start(bf16[512,256]{1,0:T(8,128)(2,1)} %param.9) | copy-start | bytes 786436
  1.3 8.0 %collective-permute-start = (bf16[128,6,2,256]{3,0,2,1:T(8,128)(2,1)S(1)}, bf16[128,6,2,256]{3,0,2,1:T(8,128)(2,1)S(1)}, u32[]{:S(2)}, u32[]{:S(2)}) collective-permute-start(bf16[128,6,2,256]{3,0,2,1:T(8,128)(2,1)S(1)} %copy.20), channel_id=1, source_target_pairs={{0,1},{1,0},{2,3},{3,2},{4,5},{5,4},{6,7},{7,6},{8,9},{9,8},{10,11... | collective-permute-start | bytes 2359304 | tf_op jit(solution)/shard_map/ppermute | solution.py:8
  2.7 37.9 %collective-permute-start.4 = (bf16[256,128]{1,0:T(8,128)(2,1)S(1)}, bf16[256,128]{1,0:T(8,128)(2,1)S(1)}, u32[]{:S(2)}, u32[]{:S(2)}) collective-permute-start(bf16[256,128]{1,0:T(8,128)(2,1)S(1)} %constant_dynamic-slice_fusion.1), channel_id=1, source_target_pairs={{0,1},{1,0},{2,3},{3,2},{4,5},{5,4},{6,7},{7,6},{8,9},{9,8},{10,11... | collective-permute-start | bytes 196616 | tf_op jit(solution)/shard_map/ppermute | solution.py:8
  2.7 6.0 %copy-start.1 = (bf16[128,6,2,256]{3,2,1,0:T(2,128)(2,1)S(1)}, bf16[128,6,2,256]{3,2,1,0:T(2,128)(2,1)}, u32[]{:S(2)}) copy-start(bf16[128,6,2,256]{3,2,1,0:T(2,128)(2,1)} %param.6) | copy-start | bytes 2359300
  2.7 6.0 %copy-start.3 = (bf16[256,256]{1,0:T(8,128)(2,1)S(1)}, bf16[256,256]{1,0:T(8,128)(2,1)}, u32[]{:S(2)}) copy-start(bf16[256,256]{1,0:T(8,128)(2,1)} %param.8) | copy-start | bytes 393220
  9.2 1.9 %copy-start.2 = (bf16[256,6,2,512]{3,0,1,2:T(8,128)(2,1)S(1)}, bf16[256,6,2,512]{3,0,1,2:T(8,128)(2,1)}, u32[]{:S(2)}) copy-start(bf16[256,6,2,512]{3,0,1,2:T(8,128)(2,1)} %copy.60) | copy-start | bytes 9437188
  11.8 7.4 %collective-permute-start.1 = (bf16[128,512]{1,0:T(8,128)(2,1)S(1)}, bf16[128,512]{1,0:T(8,128)(2,1)S(1)}, u32[]{:S(2)}, u32[]{:S(2)}) collective-permute-start(bf16[128,512]{1,0:T(8,128)(2,1)S(1)} %dynamic-slice_convert_fusion.1), channel_id=1, source_target_pairs={{0,4},{4,0},{8,12},{12,8},{1,5},{5,1},{9,13},{13,9},{2,6},{6,2},{1... | collective-permute-start | bytes 393224 | tf_op jit(solution)/shard_map/ppermute | solution.py:19
  15.7 6.4 %collective-permute-start.7 = (bf16[128,512]{1,0:T(8,128)(2,1)S(1)}, bf16[128,512]{1,0:T(8,128)(2,1)S(1)}, u32[]{:S(2)}, u32[]{:S(2)}) collective-permute-start(bf16[128,512]{1,0:T(8,128)(2,1)S(1)} %dynamic-slice_convert_fusion), channel_id=1, source_target_pairs={{0,4},{4,0},{8,12},{12,8},{1,5},{5,1},{9,13},{13,9},{2,6},{6,2},{1... | collective-permute-start | bytes 393224 | tf_op jit(solution)/shard_map/ppermute | solution.py:19
  19.3 12.3 %collective-permute-start.2 = (bf16[128,512]{1,0:T(8,128)(2,1)S(1)}, bf16[128,512]{1,0:T(8,128)(2,1)S(1)}, u32[]{:S(2)}, u32[]{:S(2)}) collective-permute-start(bf16[128,512]{1,0:T(8,128)(2,1)S(1)} %fusion.28), channel_id=1, source_target_pairs={{0,8},{4,12},{8,0},{12,4},{1,9},{5,13},{9,1},{13,5},{2,10},{6,14},... | collective-permute-start | bytes 393224 | tf_op jit(solution)/shard_map/ppermute | solution.py:23
  22.2 11.2 %collective-permute-start.8 = (bf16[128,512]{1,0:T(8,128)(2,1)S(1)}, bf16[128,512]{1,0:T(8,128)(2,1)S(1)}, u32[]{:S(2)}, u32[]{:S(2)}) collective-permute-start(bf16[128,512]{1,0:T(8,128)(2,1)S(1)} %fusion.29), channel_id=1, source_target_pairs={{0,8},{4,12},{8,0},{12,4},{1,9},{5,13},{9,1},{13,5},{2,10},{6,14},... | collective-permute-start | bytes 393224 | tf_op jit(solution)/shard_map/ppermute | solution.py:23
  31.7 6.2 %collective-permute-start.3 = (bf16[128,512]{1,0:T(8,128)(2,1)S(1)}, bf16[128,512]{1,0:T(8,128)(2,1)S(1)}, u32[]{:S(2)}, u32[]{:S(2)}) collective-permute-start(bf16[128,512]{1,0:T(8,128)(2,1)S(1)} %fusion.23), channel_id=1, source_target_pairs={{0,4},{4,0},{8,12},{12,8},{1,5},{5,1},{9,13},{13,9},{2,6},{6,2},{1... | collective-permute-start | bytes 393224 | tf_op jit(solution)/shard_map/ppermute | solution.py:33
  33.4 5.8 %collective-permute-start.9 = (bf16[128,512]{1,0:T(8,128)(2,1)S(1)}, bf16[128,512]{1,0:T(8,128)(2,1)S(1)}, u32[]{:S(2)}, u32[]{:S(2)}) collective-permute-start(bf16[128,512]{1,0:T(8,128)(2,1)S(1)} %fusion.21), channel_id=1, source_target_pairs={{0,4},{4,0},{8,12},{12,8},{1,5},{5,1},{9,13},{13,9},{2,6},{6,2},{1... | collective-permute-start | bytes 393224 | tf_op jit(solution)/shard_map/ppermute | solution.py:33
  38.6 2.0 %collective-permute-start.5 = (bf16[3,256,256]{2,1,0:T(8,128)(2,1)S(1)}, bf16[3,256,256]{2,1,0:T(8,128)(2,1)S(1)}, u32[]{:S(2)}, u32[]{:S(2)}) collective-permute-start(bf16[3,256,256]{2,1,0:T(8,128)(2,1)S(1)} %get-tuple-element.7), channel_id=1, source_target_pairs={{0,1},{1,0},{2,3},{3,2},{4,5},{5,4},{6,7},{7,6},{8,9},{9,8},{10,11... | collective-permute-start | bytes 1179656 | tf_op jit(solution)/shard_map/ppermute | solution.py:8
  38.6 2.3 %collective-permute-start.6 = (bf16[3,256,256]{2,1,0:T(8,128)(2,1)S(1)}, bf16[3,256,256]{2,1,0:T(8,128)(2,1)S(1)}, u32[]{:S(2)}, u32[]{:S(2)}) collective-permute-start(bf16[3,256,256]{2,1,0:T(8,128)(2,1)S(1)} %get-tuple-element.8), channel_id=1, source_target_pairs={{0,1},{1,0},{2,3},{3,2},{4,5},{5,4},{6,7},{7,6},{8,9},{9,8},{10,11... | collective-permute-start | bytes 1179656 | tf_op jit(solution)/shard_map/ppermute | solution.py:8
  40.0 1.8 %collective-permute-start.10 = (bf16[3,256,256]{2,1,0:T(8,128)(2,1)S(1)}, bf16[3,256,256]{2,1,0:T(8,128)(2,1)S(1)}, u32[]{:S(2)}, u32[]{:S(2)}) collective-permute-start(bf16[3,256,256]{2,1,0:T(8,128)(2,1)S(1)} %get-tuple-element.9), channel_id=1, source_target_pairs={{0,1},{1,0},{2,3},{3,2},{4,5},{5,4},{6,7},{7,6},{8,9},{9,8},{10,11... | collective-permute-start | bytes 1179656 | tf_op jit(solution)/shard_map/ppermute | solution.py:8
  40.1 2.3 %collective-permute-start.11 = (bf16[3,256,256]{2,1,0:T(8,128)(2,1)S(1)}, bf16[3,256,256]{2,1,0:T(8,128)(2,1)S(1)}, u32[]{:S(2)}, u32[]{:S(2)}) collective-permute-start(bf16[3,256,256]{2,1,0:T(8,128)(2,1)S(1)} %get-tuple-element.10), channel_id=1, source_target_pairs={{0,1},{1,0},{2,3},{3,2},{4,5},{5,4},{6,7},{7,6},{8,9},{9,8},{10,11... | collective-permute-start | bytes 1179656 | tf_op jit(solution)/shard_map/ppermute | solution.py:8

commit v16 on v11

--- a/solution.py
+++ b/solution.py
@@ -56,7 +56,6 @@
     n_lev = anomalies.shape[2]
 
     anom_t = jnp.transpose(anomalies, (2, 1, 0, 3))
-    prec_t = jnp.transpose(precision, (1, 0, 2))
 
     rf_own = lax.dynamic_slice_in_dim(row_factor, h * kh, kh, 1)
     rf_other = lax.dynamic_slice_in_dim(row_factor, (1 - h) * kh, kh, 1)
@@ -77,6 +76,9 @@
         expanded = expanded_all[l]
         fields = jnp.einsum("mrc,nc->mrn", expanded, col_factor, preferred_element_type=jnp.float32)
         inc = jnp.sum(a.astype(jnp.float32) * fields, axis=0)
+        if l == 0:
+            precision, inc = lax.optimization_barrier((precision, inc))
+            prec_t = jnp.transpose(precision, (1, 0, 2))
         prec = prec_t[l]
         if pow2:
             part = _reduce_scatter_rows(inc, "mem", n_mem, jnp.bfloat16)
@@ -89,8 +91,8 @@
             "mrn,nc->mrc", scaled, col_factor, preferred_element_type=jnp.float32
         ).astype(jnp.bfloat16)
         n_m = projected.shape[0]
-        mh = n_m // 2
-        chunks = [(0, mh), (mh, n_m)] if mh > 0 else [(0, n_m)]
+        cuts = [i * n_m // 3 for i in range(4)]
+        chunks = [(lo, hi) for lo, hi in zip(cuts[:-1], cuts[1:]) if lo < hi]
         summed = jnp.einsum("rk,mrc->kmc", rf_own, projected, preferred_element_type=jnp.float32)
         other = []
         for lo, hi in chunks:

time: 44.7 us -> 44 us (0.984)
  waiting for transfers between devices: 15.7 us -> 14.5 us
  matrix products: 6.49 us -> 5.43 us
  local copies, waits for them, and re-layouts: 9.63 us -> 10.4 us
  starting transfers between devices: 11.8 us -> 12.5 us
    dot_general x1, matrix products: 1.86 us -> 0.57 us  [local(): jnp.einsum('rk,kmlc->lmrc', rf_other, ctrl_other, preferred_element_type=...]
    unnamed x12, local copies, waits for them, and re-layouts: 6.08 us -> 6.87 us
    ppermute x2, waiting for transfers between devices: 3.42 us -> 2.63 us  [_reduce_scatter_rows(): lax.ppermute(send.astype(wire), axis, [(i, i ^ d) for i in range(size)])]
    ppermute x6 -> x8, waiting for transfers between devices: 0.76 us -> 0.02 us  [_swap(): return lax.ppermute(x, axis, [(0, 1), (1, 0)])]
    ppermute x6 -> x8, starting transfers between devices: 1.72 us -> 2.19 us  [_swap(): return lax.ppermute(x, axis, [(0, 1), (1, 0)])]
    dot_general x4 -> x6, matrix products: 0.91 us -> 1.22 us  [local(): jnp.einsum('rk,mrc->kmc', rf_for_partner, proj_other, preferred_element_t...]
  transfers between devices with their start and end apart: 12 -> 14, of which waited for: 7 -> 4; matrix products, arithmetic and copies ran while one was open for 28% -> 26% of each run, Pallas kernels for 0% -> 0%
where the time goes in v16:
time: 44 us; the launch traced here: 43.8 us
  waiting for transfers between devices  14.5 us (33%)
  starting transfers between devices  12.5 us (28%)
  local copies, waits for them, and re-layouts  10.4 us (24%)
  matrix products  5.43 us (12%)
  other arithmetic  0.62 us (1%)
    ppermute x2, waiting for transfers between devices, _reduce_scatter_rows(): recv = lax.ppermute(x.astype(wire), axis, [(i, i ^ d) for i in range(size)])  7.66 us
    unnamed x12, local copies, waits for them, and re-layouts  6.87 us
    ppermute x2, starting transfers between devices, _reduce_scatter_rows(): recv = lax.ppermute(x.astype(wire), axis, [(i, i ^ d) for i in range(size)])  5.88 us
    ppermute x2, waiting for transfers between devices, _all_gather_rows(): recv = lax.ppermute(x, axis, [(i, i ^ d) for i in range(size)])  4.21 us
    ppermute x2, starting transfers between devices, _reduce_scatter_rows(): lax.ppermute(send.astype(wire), axis, [(i, i ^ d) for i in range(size)])  3.6 us
    ppermute x2, waiting for transfers between devices, _reduce_scatter_rows(): lax.ppermute(send.astype(wire), axis, [(i, i ^ d) for i in range(size)])  2.63 us
    ppermute x8, starting transfers between devices, _swap(): return lax.ppermute(x, axis, [(0, 1), (1, 0)])  2.19 us
    convert_element_type x1, local copies, waits for them, and re-layouts, local(): (control.astype(jnp.float32) + jnp.stack(outs, axis=2)).astype(jnp.bfloat16)  1.69 us
  transfers between devices with their start and end apart: 14, of which 4 were waited for; matrix products, arithmetic and copies ran while one was open for 26% of the time, Pallas kernels for 0%

profile of v16, /device:TPU:0, one launch (start us, length us, event | category | flops | bytes accessed | tf_op | source)
XLA Modules:
  0.0 43.8 jit_solution(11009573661540991639)
XLA Ops:
  0.0 1.3 %copy.8 = bf16[128,6,2,256]{3,0,2,1:T(8,128)(2,1)S(1)} copy(bf16[128,6,2,256]{3,2,1,0:T(2,128)(2,1)} %param.6) | data formatting | bytes 1572864 | tf_op args[1]
  1.3 0.5 %collective-permute-start = (bf16[128,6,2,256]{3,0,2,1:T(8,128)(2,1)S(1)}, bf16[128,6,2,256]{3,0,2,1:T(8,128)(2,1)S(1)}, u32[]{:S(2)}, u32[]{:S(2)}) collective-permute-start(bf16[128,6,2,256]{3,0,2,1:T(8,128)(2,1)S(1)} %copy.8), channel_id=1, source_target_pairs={{0,1},{1,0},{2,3},{3,2},{4,5},{5,4},{6,7},{7,6},{8,9},{9,8},{10,11... | collective-permute-start | bytes 2359304 | tf_op jit(solution)/shard_map/ppermute | solution.py:8
  1.8 0.8 %constant_dynamic-slice_fusion.2 = bf16[256,128]{1,0:T(8,128)(2,1)S(1)} fusion(bf16[256,256]{1,0:T(8,128)(2,1)} %param.8, s32[]{:T(128)S(6)} %select_n.60), kind=kLoop, calls=%fused_computation.73 | loop fusion | bytes 131076 | tf_op jit(solution)/shard_map/dynamic_slice | solution.py:61
  2.7 4.3 %copy.45 = bf16[256,6,2,512]{3,0,1,2:T(8,128)(2,1)} copy(bf16[256,6,2,512]{3,2,1,0:T(2,128)(2,1)} %param.5) | data formatting | bytes 6291456 | tf_op args[0]
  7.0 0.6 %fusion.29 = f32[256,6,2,256]{3,0,2,1:T(8,128)S(1)} fusion(bf16[256,256]{1,0:T(8,128)(2,1)S(1)} %copy-done.4, s32[]{:T(128)S(6)} %select_n.57, bf16[128,6,2,256]{3,2,1,0:T(2,128)(2,1)S(1)} %copy-done.1), kind=kOutput, calls=%fused_computation.48 | convolution fusion | flops 201326592 | bytes 3997700 | tf_op jit(solution)/shard_map/rk,kmlc->lmrc/dot_general | solution.py:65
  7.6 0.6 %fusion.11 = bf16[2,6,256,256]{3,2,0,1:T(8,128)(2,1)S(1)} fusion(f32[256,6,2,256]{3,0,2,1:T(8,128)S(1)} %fusion.29, bf16[128,6,2,256]{3,0,2,1:T(8,128)(2,1)S(1)} %collective-permute-done, bf16[256,128]{1,0:T(8,128)(2,1)S(1)} %constant_dynamic-slice_fusion.2), kind=kOutput, calls=%fused_computation.18 | convolution fusion | flops 202899456 | bytes 5570560 | tf_op jit(solution)/shard_map/rk,kmlc->lmrc/dot_general | solution.py:66
  8.2 1.3 %copy-done.2 = bf16[256,6,2,512]{3,0,1,2:T(8,128)(2,1)S(1)} copy-done((bf16[256,6,2,512]{3,0,1,2:T(8,128)(2,1)S(1)}, bf16[256,6,2,512]{3,0,1,2:T(8,128)(2,1)}, u32[]{:S(2)}) %copy-start.2) | copy-done | bytes 3145752
  9.5 0.7 %fusion = f32[256,512]{1,0:T(8,128)S(1)} fusion(bf16[2,6,256,512]{3,2,1,0:T(8,128)(2,1)S(1)} %bitcast.96, bf16[2,6,256,256]{3,2,0,1:T(8,128)(2,1)S(1)} %fusion.11, bf16[512,256]{1,0:T(8,128)(2,1)S(1)} %copy-done), kind=kOutput, calls=%fused_computation.4 | convolution fusion | flops 404881408 | bytes 3145728 | tf_op jit(solution)/shard_map/mrc,nc->mrn/dot_general | solution.py:77
  10.1 0.7 %fusion.2 = f32[256,512]{1,0:T(8,128)S(1)} fusion(bf16[2,6,256,512]{3,2,1,0:T(8,128)(2,1)S(1)} %bitcast.97, bf16[2,6,256,256]{3,2,0,1:T(8,128)(2,1)S(1)} %fusion.11, bf16[512,256]{1,0:T(8,128)(2,1)S(1)} %copy-done), kind=kOutput, calls=%fused_computation.6 | convolution fusion | flops 404881408 | bytes 3145728 | tf_op jit(solution)/shard_map/mrc,nc->mrn/dot_general | solution.py:77
  10.8 3.1 %collective-permute-start.1 = (bf16[128,512]{1,0:T(8,128)(2,1)S(1)}, bf16[128,512]{1,0:T(8,128)(2,1)S(1)}, u32[]{:S(2)}, u32[]{:S(2)}) collective-permute-start(bf16[128,512]{1,0:T(8,128)(2,1)S(1)} %dynamic-slice_convert_fusion.1), channel_id=1, source_target_pairs={{0,4},{4,0},{8,12},{12,8},{1,5},{5,1},{9,13},{13,9},{2,6},{6,2},{1... | collective-permute-start | bytes 393224 | tf_op jit(solution)/shard_map/ppermute | solution.py:19
  13.9 0.8 %fusion.58 = (f32[1,256,512]{2,0,1:T(1,128)S(1)}, f32[1,256,512]{2,0,1:T(1,128)S(1)}) fusion(f32[2,256,512]{2,0,1:T(2,128)S(1)} %bitcast.100), kind=kLoop, calls=%fused_computation.76 | loop fusion | bytes 2097152 | tf_op jit(solution)/shard_map/slice | solution.py:82
  14.8 0.5 %collective-permute-start.8 = (bf16[128,512]{1,0:T(8,128)(2,1)S(1)}, bf16[128,512]{1,0:T(8,128)(2,1)S(1)}, u32[]{:S(2)}, u32[]{:S(2)}) collective-permute-start(bf16[128,512]{1,0:T(8,128)(2,1)S(1)} %dynamic-slice_convert_fusion), channel_id=1, source_target_pairs={{0,4},{4,0},{8,12},{12,8},{1,5},{5,1},{9,13},{13,9},{2,6},{6,2},{1... | collective-permute-start | bytes 393224 | tf_op jit(solution)/shard_map/ppermute | solution.py:19
  15.3 2.6 %collective-permute-done.1 = bf16[128,512]{1,0:T(8,128)(2,1)S(1)} collective-permute-done((bf16[128,512]{1,0:T(8,128)(2,1)S(1)}, bf16[128,512]{1,0:T(8,128)(2,1)S(1)}, u32[]{:S(2)}, u32[]{:S(2)}) %collective-permute-start.1) | collective-permute-done | bytes 131104 | tf_op jit(solution)/shard_map/ppermute | solution.py:19
  18.0 3.0 %collective-permute-start.2 = (bf16[128,512]{1,0:T(8,128)(2,1)S(1)}, bf16[128,512]{1,0:T(8,128)(2,1)S(1)}, u32[]{:S(2)}, u32[]{:S(2)}) collective-permute-start(bf16[128,512]{1,0:T(8,128)(2,1)S(1)} %fusion.26), channel_id=1, source_target_pairs={{0,8},{4,12},{8,0},{12,4},{1,9},{5,13},{9,1},{13,5},{2,10},{6,14},... | collective-permute-start | bytes 393224 | tf_op jit(solution)/shard_map/ppermute | solution.py:23
  21.1 2.9 %collective-permute-start.9 = (bf16[128,512]{1,0:T(8,128)(2,1)S(1)}, bf16[128,512]{1,0:T(8,128)(2,1)S(1)}, u32[]{:S(2)}, u32[]{:S(2)}) collective-permute-start(bf16[128,512]{1,0:T(8,128)(2,1)S(1)} %fusion.27), channel_id=1, source_target_pairs={{0,8},{4,12},{8,0},{12,4},{1,9},{5,13},{9,1},{13,5},{2,10},{6,14},... | collective-permute-start | bytes 393224 | tf_op jit(solution)/shard_map/ppermute | solution.py:23
  23.9 6.4 %collective-permute-done.2 = bf16[128,512]{1,0:T(8,128)(2,1)S(1)} collective-permute-done((bf16[128,512]{1,0:T(8,128)(2,1)S(1)}, bf16[128,512]{1,0:T(8,128)(2,1)S(1)}, u32[]{:S(2)}, u32[]{:S(2)}) %collective-permute-start.2) | collective-permute-done | bytes 131104 | tf_op jit(solution)/shard_map/ppermute | solution.py:23
  30.4 0.5 %collective-permute-start.3 = (bf16[128,512]{1,0:T(8,128)(2,1)S(1)}, bf16[128,512]{1,0:T(8,128)(2,1)S(1)}, u32[]{:S(2)}, u32[]{:S(2)}) collective-permute-start(bf16[128,512]{1,0:T(8,128)(2,1)S(1)} %fusion.21), channel_id=1, source_target_pairs={{0,4},{4,0},{8,12},{12,8},{1,5},{5,1},{9,13},{13,9},{2,6},{6,2},{1... | collective-permute-start | bytes 393224 | tf_op jit(solution)/shard_map/ppermute | solution.py:33
  30.9 1.3 %collective-permute-done.9 = bf16[128,512]{1,0:T(8,128)(2,1)S(1)} collective-permute-done((bf16[128,512]{1,0:T(8,128)(2,1)S(1)}, bf16[128,512]{1,0:T(8,128)(2,1)S(1)}, u32[]{:S(2)}, u32[]{:S(2)}) %collective-permute-start.9) | collective-permute-done | bytes 131104 | tf_op jit(solution)/shard_map/ppermute | solution.py:23
  32.6 4.2 %collective-permute-done.3 = bf16[128,512]{1,0:T(8,128)(2,1)S(1)} collective-permute-done((bf16[128,512]{1,0:T(8,128)(2,1)S(1)}, bf16[128,512]{1,0:T(8,128)(2,1)S(1)}, u32[]{:S(2)}, u32[]{:S(2)}) %collective-permute-start.3) | collective-permute-done | bytes 131104 | tf_op jit(solution)/shard_map/ppermute | solution.py:33
  36.9 0.6 %fusion.12 = bf16[6,256,256]{2,1,0:T(8,128)(2,1)S(1)} fusion(f32[256,512]{1,0:T(8,128)S(1)} %maximum_convert_fusion, bf16[2,6,256,512]{3,2,1,0:T(8,128)(2,1)S(1)} %bitcast.98, bf16[512,256]{1,0:T(8,128)(2,1)S(1)} %copy-done), kind=kOutput, calls=%fused_computation.19 | convolution fusion | flops 405405696 | bytes 3145728 | tf_op jit(solution)/shard_map/mrn,nc->mrc/dot_general | solution.py:90
  37.6 0.5 %collective-permute-start.5 = (bf16[2,256,256]{2,1,0:T(8,128)(2,1)S(1)}, bf16[2,256,256]{2,1,0:T(8,128)(2,1)S(1)}, u32[]{:S(2)}, u32[]{:S(2)}) collective-permute-start(bf16[2,256,256]{2,1,0:T(8,128)(2,1)S(1)} %get-tuple-element.11), channel_id=1, source_target_pairs={{0,1},{1,0},{2,3},{3,2},{4,5},{5,4},{6,7},{7,6},{8,9},{9,8},{10,11... | collective-permute-start | bytes 786440 | tf_op jit(solution)/shard_map/ppermute | solution.py:8
  38.3 0.6 %fusion.15 = bf16[6,256,256]{2,1,0:T(8,128)(2,1)S(1)} fusion(f32[256,512]{1,0:T(8,128)S(1)} %maximum_convert_fusion.1, bf16[2,6,256,512]{3,2,1,0:T(8,128)(2,1)S(1)} %bitcast.99, bf16[512,256]{1,0:T(8,128)(2,1)S(1)} %copy-done), kind=kOutput, calls=%fused_computation.20 | convolution fusion | flops 405405696 | bytes 3145728 | tf_op jit(solution)/shard_map/mrn,nc->mrc/dot_general | solution.py:90
  38.9 0.5 %collective-permute-start.12 = (bf16[2,256,256]{2,1,0:T(8,128)(2,1)S(1)}, bf16[2,256,256]{2,1,0:T(8,128)(2,1)S(1)}, u32[]{:S(2)}, u32[]{:S(2)}) collective-permute-start(bf16[2,256,256]{2,1,0:T(8,128)(2,1)S(1)} %get-tuple-element.16), channel_id=1, source_target_pairs={{0,1},{1,0},{2,3},{3,2},{4,5},{5,4},{6,7},{7,6},{8,9},{9,8},{10,11... | collective-permute-start | bytes 786440 | tf_op jit(solution)/shard_map/ppermute | solution.py:8
  42.1 1.7 %copy.18 = bf16[128,6,2,256]{3,2,1,0:T(2,128)(2,1)} copy(bf16[128,6,2,256]{3,0,1,2:T(8,128)(2,1)S(1)} %fusion.8) | data formatting | bytes 1572864 | tf_op jit(solution)/shard_map/convert_element_type | solution.py:105
  (48 shorter events, 3.8 us)
Async XLA Ops:
  0.0 8.2 %copy-start = (bf16[512,256]{1,0:T(8,128)(2,1)S(1)}, bf16[512,256]{1,0:T(8,128)(2,1)}, u32[]{:S(2)}) copy-start(bf16[512,256]{1,0:T(8,128)(2,1)} %param.9) | copy-start | bytes 786436
  1.3 6.3 %collective-permute-start = (bf16[128,6,2,256]{3,0,2,1:T(8,128)(2,1)S(1)}, bf16[128,6,2,256]{3,0,2,1:T(8,128)(2,1)S(1)}, u32[]{:S(2)}, u32[]{:S(2)}) collective-permute-start(bf16[128,6,2,256]{3,0,2,1:T(8,128)(2,1)S(1)} %copy.8), channel_id=1, source_target_pairs={{0,1},{1,0},{2,3},{3,2},{4,5},{5,4},{6,7},{7,6},{8,9},{9,8},{10,11... | collective-permute-start | bytes 2359304 | tf_op jit(solution)/shard_map/ppermute | solution.py:8
  2.7 36.7 %collective-permute-start.4 = (bf16[256,128]{1,0:T(8,128)(2,1)S(1)}, bf16[256,128]{1,0:T(8,128)(2,1)S(1)}, u32[]{:S(2)}, u32[]{:S(2)}) collective-permute-start(bf16[256,128]{1,0:T(8,128)(2,1)S(1)} %constant_dynamic-slice_fusion.2), channel_id=1, source_target_pairs={{0,1},{1,0},{2,3},{3,2},{4,5},{5,4},{6,7},{7,6},{8,9},{9,8},{10,11... | collective-permute-start | bytes 196616 | tf_op jit(solution)/shard_map/ppermute | solution.py:8
  2.7 4.3 %copy-start.1 = (bf16[128,6,2,256]{3,2,1,0:T(2,128)(2,1)S(1)}, bf16[128,6,2,256]{3,2,1,0:T(2,128)(2,1)}, u32[]{:S(2)}) copy-start(bf16[128,6,2,256]{3,2,1,0:T(2,128)(2,1)} %param.6) | copy-start | bytes 2359300
  2.7 4.3 %copy-start.4 = (bf16[256,256]{1,0:T(8,128)(2,1)S(1)}, bf16[256,256]{1,0:T(8,128)(2,1)}, u32[]{:S(2)}) copy-start(bf16[256,256]{1,0:T(8,128)(2,1)} %param.8) | copy-start | bytes 393220
  7.6 1.9 %copy-start.2 = (bf16[256,6,2,512]{3,0,1,2:T(8,128)(2,1)S(1)}, bf16[256,6,2,512]{3,0,1,2:T(8,128)(2,1)}, u32[]{:S(2)}) copy-start(bf16[256,6,2,512]{3,0,1,2:T(8,128)(2,1)} %copy.45) | copy-start | bytes 9437188
  10.1 3.8 %copy-start.3 = (f32[256,2,512]{2,1,0:T(2,128)S(1)}, f32[256,2,512]{2,1,0:T(2,128)}, u32[]{:S(2)}) copy-start(f32[256,2,512]{2,1,0:T(2,128)} %param.7) | copy-start | bytes 3145732
  10.8 7.1 %collective-permute-start.1 = (bf16[128,512]{1,0:T(8,128)(2,1)S(1)}, bf16[128,512]{1,0:T(8,128)(2,1)S(1)}, u32[]{:S(2)}, u32[]{:S(2)}) collective-permute-start(bf16[128,512]{1,0:T(8,128)(2,1)S(1)} %dynamic-slice_convert_fusion.1), channel_id=1, source_target_pairs={{0,4},{4,0},{8,12},{12,8},{1,5},{5,1},{9,13},{13,9},{2,6},{6,2},{1... | collective-permute-start | bytes 393224 | tf_op jit(solution)/shard_map/ppermute | solution.py:19
  14.8 6.2 %collective-permute-start.8 = (bf16[128,512]{1,0:T(8,128)(2,1)S(1)}, bf16[128,512]{1,0:T(8,128)(2,1)S(1)}, u32[]{:S(2)}, u32[]{:S(2)}) collective-permute-start(bf16[128,512]{1,0:T(8,128)(2,1)S(1)} %dynamic-slice_convert_fusion), channel_id=1, source_target_pairs={{0,4},{4,0},{8,12},{12,8},{1,5},{5,1},{9,13},{13,9},{2,6},{6,2},{1... | collective-permute-start | bytes 393224 | tf_op jit(solution)/shard_map/ppermute | solution.py:19
  18.0 12.3 %collective-permute-start.2 = (bf16[128,512]{1,0:T(8,128)(2,1)S(1)}, bf16[128,512]{1,0:T(8,128)(2,1)S(1)}, u32[]{:S(2)}, u32[]{:S(2)}) collective-permute-start(bf16[128,512]{1,0:T(8,128)(2,1)S(1)} %fusion.26), channel_id=1, source_target_pairs={{0,8},{4,12},{8,0},{12,4},{1,9},{5,13},{9,1},{13,5},{2,10},{6,14},... | collective-permute-start | bytes 393224 | tf_op jit(solution)/shard_map/ppermute | solution.py:23
  21.1 11.1 %collective-permute-start.9 = (bf16[128,512]{1,0:T(8,128)(2,1)S(1)}, bf16[128,512]{1,0:T(8,128)(2,1)S(1)}, u32[]{:S(2)}, u32[]{:S(2)}) collective-permute-start(bf16[128,512]{1,0:T(8,128)(2,1)S(1)} %fusion.27), channel_id=1, source_target_pairs={{0,8},{4,12},{8,0},{12,4},{1,9},{5,13},{9,1},{13,5},{2,10},{6,14},... | collective-permute-start | bytes 393224 | tf_op jit(solution)/shard_map/ppermute | solution.py:23
  30.4 6.4 %collective-permute-start.3 = (bf16[128,512]{1,0:T(8,128)(2,1)S(1)}, bf16[128,512]{1,0:T(8,128)(2,1)S(1)}, u32[]{:S(2)}, u32[]{:S(2)}) collective-permute-start(bf16[128,512]{1,0:T(8,128)(2,1)S(1)} %fusion.21), channel_id=1, source_target_pairs={{0,4},{4,0},{8,12},{12,8},{1,5},{5,1},{9,13},{13,9},{2,6},{6,2},{1... | collective-permute-start | bytes 393224 | tf_op jit(solution)/shard_map/ppermute | solution.py:33
  32.3 5.9 %collective-permute-start.10 = (bf16[128,512]{1,0:T(8,128)(2,1)S(1)}, bf16[128,512]{1,0:T(8,128)(2,1)S(1)}, u32[]{:S(2)}, u32[]{:S(2)}) collective-permute-start(bf16[128,512]{1,0:T(8,128)(2,1)S(1)} %fusion.20), channel_id=1, source_target_pairs={{0,4},{4,0},{8,12},{12,8},{1,5},{5,1},{9,13},{13,9},{2,6},{6,2},{1... | collective-permute-start | bytes 393224 | tf_op jit(solution)/shard_map/ppermute | solution.py:33
  37.5 2.0 %collective-permute-start.6 = (bf16[2,256,256]{2,1,0:T(8,128)(2,1)S(1)}, bf16[2,256,256]{2,1,0:T(8,128)(2,1)S(1)}, u32[]{:S(2)}, u32[]{:S(2)}) collective-permute-start(bf16[2,256,256]{2,1,0:T(8,128)(2,1)S(1)} %get-tuple-element.13), channel_id=1, source_target_pairs={{0,1},{1,0},{2,3},{3,2},{4,5},{5,4},{6,7},{7,6},{8,9},{9,8},{10,11... | collective-permute-start | bytes 786440 | tf_op jit(solution)/shard_map/ppermute | solution.py:8
  37.6 2.5 %collective-permute-start.5 = (bf16[2,256,256]{2,1,0:T(8,128)(2,1)S(1)}, bf16[2,256,256]{2,1,0:T(8,128)(2,1)S(1)}, u32[]{:S(2)}, u32[]{:S(2)}) collective-permute-start(bf16[2,256,256]{2,1,0:T(8,128)(2,1)S(1)} %get-tuple-element.11), channel_id=1, source_target_pairs={{0,1},{1,0},{2,3},{3,2},{4,5},{5,4},{6,7},{7,6},{8,9},{9,8},{10,11... | collective-permute-start | bytes 786440 | tf_op jit(solution)/shard_map/ppermute | solution.py:8
  38.1 2.3 %collective-permute-start.7 = (bf16[2,256,256]{2,1,0:T(8,128)(2,1)S(1)}, bf16[2,256,256]{2,1,0:T(8,128)(2,1)S(1)}, u32[]{:S(2)}, u32[]{:S(2)}) collective-permute-start(bf16[2,256,256]{2,1,0:T(8,128)(2,1)S(1)} %get-tuple-element.12), channel_id=1, source_target_pairs={{0,1},{1,0},{2,3},{3,2},{4,5},{5,4},{6,7},{7,6},{8,9},{9,8},{10,11... | collective-permute-start | bytes 786440 | tf_op jit(solution)/shard_map/ppermute | solution.py:8
  38.9 1.6 %collective-permute-start.12 = (bf16[2,256,256]{2,1,0:T(8,128)(2,1)S(1)}, bf16[2,256,256]{2,1,0:T(8,128)(2,1)S(1)}, u32[]{:S(2)}, u32[]{:S(2)}) collective-permute-start(bf16[2,256,256]{2,1,0:T(8,128)(2,1)S(1)} %get-tuple-element.16), channel_id=1, source_target_pairs={{0,1},{1,0},{2,3},{3,2},{4,5},{5,4},{6,7},{7,6},{8,9},{9,8},{10,11... | collective-permute-start | bytes 786440 | tf_op jit(solution)/shard_map/ppermute | solution.py:8
  39.4 1.7 %collective-permute-start.11 = (bf16[2,256,256]{2,1,0:T(8,128)(2,1)S(1)}, bf16[2,256,256]{2,1,0:T(8,128)(2,1)S(1)}, u32[]{:S(2)}, u32[]{:S(2)}) collective-permute-start(bf16[2,256,256]{2,1,0:T(8,128)(2,1)S(1)} %get-tuple-element.14), channel_id=1, source_target_pairs={{0,1},{1,0},{2,3},{3,2},{4,5},{5,4},{6,7},{7,6},{8,9},{9,8},{10,11... | collective-permute-start | bytes 786440 | tf_op jit(solution)/shard_map/ppermute | solution.py:8
  39.5 1.8 %collective-permute-start.13 = (bf16[2,256,256]{2,1,0:T(8,128)(2,1)S(1)}, bf16[2,256,256]{2,1,0:T(8,128)(2,1)S(1)}, u32[]{:S(2)}, u32[]{:S(2)}) collective-permute-start(bf16[2,256,256]{2,1,0:T(8,128)(2,1)S(1)} %get-tuple-element.15), channel_id=1, source_target_pairs={{0,1},{1,0},{2,3},{3,2},{4,5},{5,4},{6,7},{7,6},{8,9},{9,8},{10,11... | collective-permute-start | bytes 786440 | tf_op jit(solution)/shard_map/ppermute | solution.py:8

commit v17 on v16

--- a/solution.py
+++ b/solution.py
@@ -8,21 +8,28 @@
     return lax.ppermute(x, axis, [(0, 1), (1, 0)])
 
 
-def _reduce_scatter_rows(x, axis, size, wire):
+def _reduce_scatter_rows(x, axis, size, wire, hold):
     idx = lax.axis_index(axis)
     d = 1
+    first = True
     while 2 * d < size:
         half = x.shape[0] // 2
         bit = (idx // d) % 2
         keep = lax.dynamic_slice_in_dim(x, bit * half, half, 0)
-        send = lax.dynamic_slice_in_dim(x, (1 - bit) * half, half, 0)
-        recv = lax.ppermute(send.astype(wire), axis, [(i, i ^ d) for i in range(size)])
+        send = lax.dynamic_slice_in_dim(x, (1 - bit) * half, half, 0).astype(wire)
+        if first:
+            send, hold = lax.optimization_barrier((send, hold))
+            first = False
+        recv = lax.ppermute(send, axis, [(i, i ^ d) for i in range(size)])
         x = keep + recv.astype(x.dtype)
         d *= 2
     if d < size:
-        recv = lax.ppermute(x.astype(wire), axis, [(i, i ^ d) for i in range(size)])
+        send = x.astype(wire)
+        if first:
+            send, hold = lax.optimization_barrier((send, hold))
+        recv = lax.ppermute(send, axis, [(i, i ^ d) for i in range(size)])
         x = x + recv.astype(x.dtype)
-    return x
+    return x, hold
 
 
 def _all_gather_rows(x, axis, size):
@@ -71,17 +78,18 @@
     start = _block_start("mem", n_mem, rows) if pow2 else 0
 
     outs = []
+    cf_next = col_factor
     for l in range(n_lev):
         a = anom_t[l]
         expanded = expanded_all[l]
-        fields = jnp.einsum("mrc,nc->mrn", expanded, col_factor, preferred_element_type=jnp.float32)
+        fields = jnp.einsum("mrc,nc->mrn", expanded, cf_next, preferred_element_type=jnp.float32)
         inc = jnp.sum(a.astype(jnp.float32) * fields, axis=0)
         if l == 0:
             precision, inc = lax.optimization_barrier((precision, inc))
             prec_t = jnp.transpose(precision, (1, 0, 2))
         prec = prec_t[l]
         if pow2:
-            part = _reduce_scatter_rows(inc, "mem", n_mem, jnp.bfloat16)
+            part, cf_next = _reduce_scatter_rows(inc, "mem", n_mem, jnp.bfloat16, col_factor)
             w_blk = (lax.dynamic_slice_in_dim(prec, start, blk, 0) * part).astype(jnp.bfloat16)
             weighted = _all_gather_rows(w_blk, "mem", n_mem)
         else:

time: 44 us -> 42.9 us (0.975)
  waiting for transfers between devices: 14.5 us -> 13.6 us
    ppermute x4, waiting for transfers between devices: 10.3 us -> 9.75 us  [_reduce_scatter_rows(): recv = lax.ppermute(send, axis, [(i, i ^ d) for i in range(size)])]
  transfers between devices with their start and end apart: 14 -> 14, of which waited for: 4 -> 5; matrix products, arithmetic and copies ran while one was open for 26% -> 27% of each run, Pallas kernels for 0% -> 0%
where the time goes in v17:
time: 42.9 us; the launch traced here: 42.8 us
  waiting for transfers between devices  13.6 us (32%)
  starting transfers between devices  12.4 us (29%)
  local copies, waits for them, and re-layouts  10.4 us (24%)
  matrix products  5.44 us (13%)
  other arithmetic  0.62 us (1%)
    ppermute x4, waiting for transfers between devices, _reduce_scatter_rows(): recv = lax.ppermute(send, axis, [(i, i ^ d) for i in range(size)])  9.75 us
    ppermute x4, starting transfers between devices, _reduce_scatter_rows(): recv = lax.ppermute(send, axis, [(i, i ^ d) for i in range(size)])  9.64 us
    unnamed x12, local copies, waits for them, and re-layouts  6.86 us
    ppermute x2, waiting for transfers between devices, _all_gather_rows(): recv = lax.ppermute(x, axis, [(i, i ^ d) for i in range(size)])  3.8 us
    ppermute x8, starting transfers between devices, _swap(): return lax.ppermute(x, axis, [(0, 1), (1, 0)])  2.21 us
    convert_element_type x1, local copies, waits for them, and re-layouts, local(): (control.astype(jnp.float32) + jnp.stack(outs, axis=2)).astype(jnp.bfloat16)  1.69 us
    dot_general x2, matrix products, local(): jnp.einsum('mrc,nc->mrn', expanded, cf_next, preferred_element_type=jnp.f...  1.32 us
    dot_general x6, matrix products, local(): jnp.einsum('rk,mrc->kmc', rf_for_partner, proj_other, preferred_element_t...  1.22 us
  transfers between devices with their start and end apart: 14, of which 5 were waited for; matrix products, arithmetic and copies ran while one was open for 27% of the time, Pallas kernels for 0%

profile of v17, /device:TPU:0, one launch (start us, length us, event | category | flops | bytes accessed | tf_op | source)
XLA Modules:
  0.0 42.8 jit_solution(5866413372068248606)
XLA Ops:
  0.0 1.3 %copy.8 = bf16[128,6,2,256]{3,0,2,1:T(8,128)(2,1)S(1)} copy(bf16[128,6,2,256]{3,2,1,0:T(2,128)(2,1)} %param.6) | data formatting | bytes 1572864 | tf_op args[1]
  1.3 0.5 %collective-permute-start = (bf16[128,6,2,256]{3,0,2,1:T(8,128)(2,1)S(1)}, bf16[128,6,2,256]{3,0,2,1:T(8,128)(2,1)S(1)}, u32[]{:S(2)}, u32[]{:S(2)}) collective-permute-start(bf16[128,6,2,256]{3,0,2,1:T(8,128)(2,1)S(1)} %copy.8), channel_id=1, source_target_pairs={{0,1},{1,0},{2,3},{3,2},{4,5},{5,4},{6,7},{7,6},{8,9},{9,8},{10,11... | collective-permute-start | bytes 2359304 | tf_op jit(solution)/shard_map/ppermute | solution.py:8
  1.8 0.8 %constant_dynamic-slice_fusion.2 = bf16[256,128]{1,0:T(8,128)(2,1)S(1)} fusion(bf16[256,256]{1,0:T(8,128)(2,1)} %param.8, s32[]{:T(128)S(6)} %select_n.60), kind=kLoop, calls=%fused_computation.73 | loop fusion | bytes 131076 | tf_op jit(solution)/shard_map/dynamic_slice | solution.py:68
  2.7 4.3 %copy.45 = bf16[256,6,2,512]{3,0,1,2:T(8,128)(2,1)} copy(bf16[256,6,2,512]{3,2,1,0:T(2,128)(2,1)} %param.5) | data formatting | bytes 6291456 | tf_op args[0]
  7.0 0.6 %fusion.29 = f32[256,6,2,256]{3,0,2,1:T(8,128)S(1)} fusion(bf16[256,256]{1,0:T(8,128)(2,1)S(1)} %copy-done.4, s32[]{:T(128)S(6)} %select_n.57, bf16[128,6,2,256]{3,2,1,0:T(2,128)(2,1)S(1)} %copy-done.1), kind=kOutput, calls=%fused_computation.48 | convolution fusion | flops 201326592 | bytes 3997700 | tf_op jit(solution)/shard_map/rk,kmlc->lmrc/dot_general | solution.py:72
  7.6 0.6 %fusion.11 = bf16[2,6,256,256]{3,2,0,1:T(8,128)(2,1)S(1)} fusion(f32[256,6,2,256]{3,0,2,1:T(8,128)S(1)} %fusion.29, bf16[128,6,2,256]{3,0,2,1:T(8,128)(2,1)S(1)} %collective-permute-done, bf16[256,128]{1,0:T(8,128)(2,1)S(1)} %constant_dynamic-slice_fusion.2), kind=kOutput, calls=%fused_computation.18 | convolution fusion | flops 202899456 | bytes 5570560 | tf_op jit(solution)/shard_map/rk,kmlc->lmrc/dot_general | solution.py:73
  8.2 1.3 %copy-done.2 = bf16[256,6,2,512]{3,0,1,2:T(8,128)(2,1)S(1)} copy-done((bf16[256,6,2,512]{3,0,1,2:T(8,128)(2,1)S(1)}, bf16[256,6,2,512]{3,0,1,2:T(8,128)(2,1)}, u32[]{:S(2)}) %copy-start.2) | copy-done | bytes 3145752
  9.5 0.7 %fusion = f32[256,512]{1,0:T(8,128)S(1)} fusion(bf16[2,6,256,512]{3,2,1,0:T(8,128)(2,1)S(1)} %bitcast.97, bf16[2,6,256,256]{3,2,0,1:T(8,128)(2,1)S(1)} %fusion.11, bf16[512,256]{1,0:T(8,128)(2,1)S(1)} %copy-done), kind=kOutput, calls=%fused_computation.4 | convolution fusion | flops 404881408 | bytes 3145728 | tf_op jit(solution)/shard_map/mrc,nc->mrn/dot_general | solution.py:85
  10.2 3.1 %collective-permute-start.1 = (bf16[128,512]{1,0:T(8,128)(2,1)S(1)}, bf16[128,512]{1,0:T(8,128)(2,1)S(1)}, u32[]{:S(2)}, u32[]{:S(2)}) collective-permute-start(bf16[128,512]{1,0:T(8,128)(2,1)S(1)} %dynamic-slice_convert_fusion.1), channel_id=1, source_target_pairs={{0,4},{4,0},{8,12},{12,8},{1,5},{5,1},{9,13},{13,9},{2,6},{6,2},{1... | collective-permute-start | bytes 393224 | tf_op jit(solution)/shard_map/ppermute | solution.py:23
  13.2 0.8 %fusion.58 = (f32[1,256,512]{2,0,1:T(1,128)S(1)}, f32[1,256,512]{2,0,1:T(1,128)S(1)}) fusion(f32[2,256,512]{2,0,1:T(2,128)S(1)} %bitcast.101), kind=kLoop, calls=%fused_computation.76 | loop fusion | bytes 2097152 | tf_op jit(solution)/shard_map/slice | solution.py:90
  14.1 0.7 %fusion.2 = f32[256,512]{1,0:T(8,128)S(1)} fusion(bf16[2,6,256,512]{3,2,1,0:T(8,128)(2,1)S(1)} %bitcast.98, bf16[2,6,256,256]{3,2,0,1:T(8,128)(2,1)S(1)} %fusion.11, bf16[512,256]{1,0:T(8,128)(2,1)S(1)} %copy-done), kind=kOutput, calls=%fused_computation.6 | convolution fusion | flops 404881408 | bytes 3145728 | tf_op jit(solution)/shard_map/mrc,nc->mrn/dot_general | solution.py:85
  14.9 2.2 %collective-permute-done.1 = bf16[128,512]{1,0:T(8,128)(2,1)S(1)} collective-permute-done((bf16[128,512]{1,0:T(8,128)(2,1)S(1)}, bf16[128,512]{1,0:T(8,128)(2,1)S(1)}, u32[]{:S(2)}, u32[]{:S(2)}) %collective-permute-start.1) | collective-permute-done | bytes 131104 | tf_op jit(solution)/shard_map/ppermute | solution.py:23
  17.2 2.6 %collective-permute-start.2 = (bf16[128,512]{1,0:T(8,128)(2,1)S(1)}, bf16[128,512]{1,0:T(8,128)(2,1)S(1)}, u32[]{:S(2)}, u32[]{:S(2)}) collective-permute-start(bf16[128,512]{1,0:T(8,128)(2,1)S(1)} %fusion.26), channel_id=1, source_target_pairs={{0,8},{4,12},{8,0},{12,4},{1,9},{5,13},{9,1},{13,5},{2,10},{6,14},... | collective-permute-start | bytes 393224 | tf_op jit(solution)/shard_map/ppermute | solution.py:30
  20.0 3.8 %collective-permute-start.9 = (bf16[128,512]{1,0:T(8,128)(2,1)S(1)}, bf16[128,512]{1,0:T(8,128)(2,1)S(1)}, u32[]{:S(2)}, u32[]{:S(2)}) collective-permute-start(bf16[128,512]{1,0:T(8,128)(2,1)S(1)} %fusion.27), channel_id=1, source_target_pairs={{0,8},{4,12},{8,0},{12,4},{1,9},{5,13},{9,1},{13,5},{2,10},{6,14},... | collective-permute-start | bytes 393224 | tf_op jit(solution)/shard_map/ppermute | solution.py:30
  23.8 5.8 %collective-permute-done.2 = bf16[128,512]{1,0:T(8,128)(2,1)S(1)} collective-permute-done((bf16[128,512]{1,0:T(8,128)(2,1)S(1)}, bf16[128,512]{1,0:T(8,128)(2,1)S(1)}, u32[]{:S(2)}, u32[]{:S(2)}) %collective-permute-start.2) | collective-permute-done | bytes 131104 | tf_op jit(solution)/shard_map/ppermute | solution.py:30
  29.8 1.6 %collective-permute-done.9 = bf16[128,512]{1,0:T(8,128)(2,1)S(1)} collective-permute-done((bf16[128,512]{1,0:T(8,128)(2,1)S(1)}, bf16[128,512]{1,0:T(8,128)(2,1)S(1)}, u32[]{:S(2)}, u32[]{:S(2)}) %collective-permute-start.9) | collective-permute-done | bytes 131104 | tf_op jit(solution)/shard_map/ppermute | solution.py:30
  31.4 0.5 %collective-permute-start.10 = (bf16[128,512]{1,0:T(8,128)(2,1)S(1)}, bf16[128,512]{1,0:T(8,128)(2,1)S(1)}, u32[]{:S(2)}, u32[]{:S(2)}) collective-permute-start(bf16[128,512]{1,0:T(8,128)(2,1)S(1)} %fusion.20), channel_id=1, source_target_pairs={{0,4},{4,0},{8,12},{12,8},{1,5},{5,1},{9,13},{13,9},{2,6},{6,2},{1... | collective-permute-start | bytes 393224 | tf_op jit(solution)/shard_map/ppermute | solution.py:40
  31.9 3.8 %collective-permute-done.3 = bf16[128,512]{1,0:T(8,128)(2,1)S(1)} collective-permute-done((bf16[128,512]{1,0:T(8,128)(2,1)S(1)}, bf16[128,512]{1,0:T(8,128)(2,1)S(1)}, u32[]{:S(2)}, u32[]{:S(2)}) %collective-permute-start.3) | collective-permute-done | bytes 131104 | tf_op jit(solution)/shard_map/ppermute | solution.py:40
  35.8 0.6 %fusion.12 = bf16[6,256,256]{2,1,0:T(8,128)(2,1)S(1)} fusion(f32[256,512]{1,0:T(8,128)S(1)} %maximum_convert_fusion, bf16[2,6,256,512]{3,2,1,0:T(8,128)(2,1)S(1)} %bitcast.99, bf16[512,256]{1,0:T(8,128)(2,1)S(1)} %copy-done), kind=kOutput, calls=%fused_computation.19 | convolution fusion | flops 405405696 | bytes 3145728 | tf_op jit(solution)/shard_map/mrn,nc->mrc/dot_general | solution.py:98
  36.5 0.5 %collective-permute-start.5 = (bf16[2,256,256]{2,1,0:T(8,128)(2,1)S(1)}, bf16[2,256,256]{2,1,0:T(8,128)(2,1)S(1)}, u32[]{:S(2)}, u32[]{:S(2)}) collective-permute-start(bf16[2,256,256]{2,1,0:T(8,128)(2,1)S(1)} %get-tuple-element.17), channel_id=1, source_target_pairs={{0,1},{1,0},{2,3},{3,2},{4,5},{5,4},{6,7},{7,6},{8,9},{9,8},{10,11... | collective-permute-start | bytes 786440 | tf_op jit(solution)/shard_map/ppermute | solution.py:8
  37.2 0.6 %fusion.15 = bf16[6,256,256]{2,1,0:T(8,128)(2,1)S(1)} fusion(f32[256,512]{1,0:T(8,128)S(1)} %maximum_convert_fusion.1, bf16[2,6,256,512]{3,2,1,0:T(8,128)(2,1)S(1)} %bitcast.100, bf16[512,256]{1,0:T(8,128)(2,1)S(1)} %copy-done), kind=kOutput, calls=%fused_computation.20 | convolution fusion | flops 405405696 | bytes 3145728 | tf_op jit(solution)/shard_map/mrn,nc->mrc/dot_general | solution.py:98
  37.9 0.5 %collective-permute-start.12 = (bf16[2,256,256]{2,1,0:T(8,128)(2,1)S(1)}, bf16[2,256,256]{2,1,0:T(8,128)(2,1)S(1)}, u32[]{:S(2)}, u32[]{:S(2)}) collective-permute-start(bf16[2,256,256]{2,1,0:T(8,128)(2,1)S(1)} %get-tuple-element.22), channel_id=1, source_target_pairs={{0,1},{1,0},{2,3},{3,2},{4,5},{5,4},{6,7},{7,6},{8,9},{9,8},{10,11... | collective-permute-start | bytes 786440 | tf_op jit(solution)/shard_map/ppermute | solution.py:8
  38.5 0.4 collective-permute-start.13
  41.1 1.7 %copy.18 = bf16[128,6,2,256]{3,2,1,0:T(2,128)(2,1)} copy(bf16[128,6,2,256]{3,0,1,2:T(8,128)(2,1)S(1)} %fusion.8) | data formatting | bytes 1572864 | tf_op jit(solution)/shard_map/convert_element_type | solution.py:113
  (48 shorter events, 3.3 us)
Async XLA Ops:
  0.0 8.2 %copy-start = (bf16[512,256]{1,0:T(8,128)(2,1)S(1)}, bf16[512,256]{1,0:T(8,128)(2,1)}, u32[]{:S(2)}) copy-start(bf16[512,256]{1,0:T(8,128)(2,1)} %param.9) | copy-start | bytes 786436
  1.3 6.3 %collective-permute-start = (bf16[128,6,2,256]{3,0,2,1:T(8,128)(2,1)S(1)}, bf16[128,6,2,256]{3,0,2,1:T(8,128)(2,1)S(1)}, u32[]{:S(2)}, u32[]{:S(2)}) collective-permute-start(bf16[128,6,2,256]{3,0,2,1:T(8,128)(2,1)S(1)} %copy.8), channel_id=1, source_target_pairs={{0,1},{1,0},{2,3},{3,2},{4,5},{5,4},{6,7},{7,6},{8,9},{9,8},{10,11... | collective-permute-start | bytes 2359304 | tf_op jit(solution)/shard_map/ppermute | solution.py:8
  2.7 35.7 %collective-permute-start.4 = (bf16[256,128]{1,0:T(8,128)(2,1)S(1)}, bf16[256,128]{1,0:T(8,128)(2,1)S(1)}, u32[]{:S(2)}, u32[]{:S(2)}) collective-permute-start(bf16[256,128]{1,0:T(8,128)(2,1)S(1)} %constant_dynamic-slice_fusion.2), channel_id=1, source_target_pairs={{0,1},{1,0},{2,3},{3,2},{4,5},{5,4},{6,7},{7,6},{8,9},{9,8},{10,11... | collective-permute-start | bytes 196616 | tf_op jit(solution)/shard_map/ppermute | solution.py:8
  2.7 4.3 %copy-start.1 = (bf16[128,6,2,256]{3,2,1,0:T(2,128)(2,1)S(1)}, bf16[128,6,2,256]{3,2,1,0:T(2,128)(2,1)}, u32[]{:S(2)}) copy-start(bf16[128,6,2,256]{3,2,1,0:T(2,128)(2,1)} %param.6) | copy-start | bytes 2359300
  2.7 4.3 %copy-start.4 = (bf16[256,256]{1,0:T(8,128)(2,1)S(1)}, bf16[256,256]{1,0:T(8,128)(2,1)}, u32[]{:S(2)}) copy-start(bf16[256,256]{1,0:T(8,128)(2,1)} %param.8) | copy-start | bytes 393220
  7.6 1.9 %copy-start.2 = (bf16[256,6,2,512]{3,0,1,2:T(8,128)(2,1)S(1)}, bf16[256,6,2,512]{3,0,1,2:T(8,128)(2,1)}, u32[]{:S(2)}) copy-start(bf16[256,6,2,512]{3,0,1,2:T(8,128)(2,1)} %copy.45) | copy-start | bytes 9437188
  8.2 5.1 %copy-start.3 = (f32[256,2,512]{2,1,0:T(2,128)S(1)}, f32[256,2,512]{2,1,0:T(2,128)}, u32[]{:S(2)}) copy-start(f32[256,2,512]{2,1,0:T(2,128)} %param.7) | copy-start | bytes 3145732
  10.2 7.0 %collective-permute-start.1 = (bf16[128,512]{1,0:T(8,128)(2,1)S(1)}, bf16[128,512]{1,0:T(8,128)(2,1)S(1)}, u32[]{:S(2)}, u32[]{:S(2)}) collective-permute-start(bf16[128,512]{1,0:T(8,128)(2,1)S(1)} %dynamic-slice_convert_fusion.1), channel_id=1, source_target_pairs={{0,4},{4,0},{8,12},{12,8},{1,5},{5,1},{9,13},{13,9},{2,6},{6,2},{1... | collective-permute-start | bytes 393224 | tf_op jit(solution)/shard_map/ppermute | solution.py:23
  14.8 5.2 %collective-permute-start.8 = (bf16[128,512]{1,0:T(8,128)(2,1)S(1)}, bf16[128,512]{1,0:T(8,128)(2,1)S(1)}, u32[]{:S(2)}, u32[]{:S(2)}) collective-permute-start(bf16[128,512]{1,0:T(8,128)(2,1)S(1)} %dynamic-slice_convert_fusion), channel_id=1, source_target_pairs={{0,4},{4,0},{8,12},{12,8},{1,5},{5,1},{9,13},{13,9},{2,6},{6,2},{1... | collective-permute-start | bytes 393224 | tf_op jit(solution)/shard_map/ppermute | solution.py:23
  17.2 12.5 %collective-permute-start.2 = (bf16[128,512]{1,0:T(8,128)(2,1)S(1)}, bf16[128,512]{1,0:T(8,128)(2,1)S(1)}, u32[]{:S(2)}, u32[]{:S(2)}) collective-permute-start(bf16[128,512]{1,0:T(8,128)(2,1)S(1)} %fusion.26), channel_id=1, source_target_pairs={{0,8},{4,12},{8,0},{12,4},{1,9},{5,13},{9,1},{13,5},{2,10},{6,14},... | collective-permute-start | bytes 393224 | tf_op jit(solution)/shard_map/ppermute | solution.py:30
  20.0 11.3 %collective-permute-start.9 = (bf16[128,512]{1,0:T(8,128)(2,1)S(1)}, bf16[128,512]{1,0:T(8,128)(2,1)S(1)}, u32[]{:S(2)}, u32[]{:S(2)}) collective-permute-start(bf16[128,512]{1,0:T(8,128)(2,1)S(1)} %fusion.27), channel_id=1, source_target_pairs={{0,8},{4,12},{8,0},{12,4},{1,9},{5,13},{9,1},{13,5},{2,10},{6,14},... | collective-permute-start | bytes 393224 | tf_op jit(solution)/shard_map/ppermute | solution.py:30
  29.7 6.0 %collective-permute-start.3 = (bf16[128,512]{1,0:T(8,128)(2,1)S(1)}, bf16[128,512]{1,0:T(8,128)(2,1)S(1)}, u32[]{:S(2)}, u32[]{:S(2)}) collective-permute-start(bf16[128,512]{1,0:T(8,128)(2,1)S(1)} %fusion.21), channel_id=1, source_target_pairs={{0,4},{4,0},{8,12},{12,8},{1,5},{5,1},{9,13},{13,9},{2,6},{6,2},{1... | collective-permute-start | bytes 393224 | tf_op jit(solution)/shard_map/ppermute | solution.py:40
  31.4 5.7 %collective-permute-start.10 = (bf16[128,512]{1,0:T(8,128)(2,1)S(1)}, bf16[128,512]{1,0:T(8,128)(2,1)S(1)}, u32[]{:S(2)}, u32[]{:S(2)}) collective-permute-start(bf16[128,512]{1,0:T(8,128)(2,1)S(1)} %fusion.20), channel_id=1, source_target_pairs={{0,4},{4,0},{8,12},{12,8},{1,5},{5,1},{9,13},{13,9},{2,6},{6,2},{1... | collective-permute-start | bytes 393224 | tf_op jit(solution)/shard_map/ppermute | solution.py:40
  36.5 2.0 %collective-permute-start.6 = (bf16[2,256,256]{2,1,0:T(8,128)(2,1)S(1)}, bf16[2,256,256]{2,1,0:T(8,128)(2,1)S(1)}, u32[]{:S(2)}, u32[]{:S(2)}) collective-permute-start(bf16[2,256,256]{2,1,0:T(8,128)(2,1)S(1)} %get-tuple-element.19), channel_id=1, source_target_pairs={{0,1},{1,0},{2,3},{3,2},{4,5},{5,4},{6,7},{7,6},{8,9},{9,8},{10,11... | collective-permute-start | bytes 786440 | tf_op jit(solution)/shard_map/ppermute | solution.py:8
  36.5 2.5 %collective-permute-start.5 = (bf16[2,256,256]{2,1,0:T(8,128)(2,1)S(1)}, bf16[2,256,256]{2,1,0:T(8,128)(2,1)S(1)}, u32[]{:S(2)}, u32[]{:S(2)}) collective-permute-start(bf16[2,256,256]{2,1,0:T(8,128)(2,1)S(1)} %get-tuple-element.17), channel_id=1, source_target_pairs={{0,1},{1,0},{2,3},{3,2},{4,5},{5,4},{6,7},{7,6},{8,9},{9,8},{10,11... | collective-permute-start | bytes 786440 | tf_op jit(solution)/shard_map/ppermute | solution.py:8
  37.0 2.3 %collective-permute-start.7 = (bf16[2,256,256]{2,1,0:T(8,128)(2,1)S(1)}, bf16[2,256,256]{2,1,0:T(8,128)(2,1)S(1)}, u32[]{:S(2)}, u32[]{:S(2)}) collective-permute-start(bf16[2,256,256]{2,1,0:T(8,128)(2,1)S(1)} %get-tuple-element.18), channel_id=1, source_target_pairs={{0,1},{1,0},{2,3},{3,2},{4,5},{5,4},{6,7},{7,6},{8,9},{9,8},{10,11... | collective-permute-start | bytes 786440 | tf_op jit(solution)/shard_map/ppermute | solution.py:8
  37.9 1.6 %collective-permute-start.12 = (bf16[2,256,256]{2,1,0:T(8,128)(2,1)S(1)}, bf16[2,256,256]{2,1,0:T(8,128)(2,1)S(1)}, u32[]{:S(2)}, u32[]{:S(2)}) collective-permute-start(bf16[2,256,256]{2,1,0:T(8,128)(2,1)S(1)} %get-tuple-element.22), channel_id=1, source_target_pairs={{0,1},{1,0},{2,3},{3,2},{4,5},{5,4},{6,7},{7,6},{8,9},{9,8},{10,11... | collective-permute-start | bytes 786440 | tf_op jit(solution)/shard_map/ppermute | solution.py:8
  38.4 1.7 %collective-permute-start.11 = (bf16[2,256,256]{2,1,0:T(8,128)(2,1)S(1)}, bf16[2,256,256]{2,1,0:T(8,128)(2,1)S(1)}, u32[]{:S(2)}, u32[]{:S(2)}) collective-permute-start(bf16[2,256,256]{2,1,0:T(8,128)(2,1)S(1)} %get-tuple-element.20), channel_id=1, source_target_pairs={{0,1},{1,0},{2,3},{3,2},{4,5},{5,4},{6,7},{7,6},{8,9},{9,8},{10,11... | collective-permute-start | bytes 786440 | tf_op jit(solution)/shard_map/ppermute | solution.py:8
  38.5 1.8 %collective-permute-start.13 = (bf16[2,256,256]{2,1,0:T(8,128)(2,1)S(1)}, bf16[2,256,256]{2,1,0:T(8,128)(2,1)S(1)}, u32[]{:S(2)}, u32[]{:S(2)}) collective-permute-start(bf16[2,256,256]{2,1,0:T(8,128)(2,1)S(1)} %get-tuple-element.21), channel_id=1, source_target_pairs={{0,1},{1,0},{2,3},{3,2},{4,5},{5,4},{6,7},{7,6},{8,9},{9,8},{10,11... | collective-permute-start | bytes 786440 | tf_op jit(solution)/shard_map/ppermute | solution.py:8

commit v18 on v17

--- a/solution.py
+++ b/solution.py
@@ -66,7 +66,6 @@
 
     rf_own = lax.dynamic_slice_in_dim(row_factor, h * kh, kh, 1)
     rf_other = lax.dynamic_slice_in_dim(row_factor, (1 - h) * kh, kh, 1)
-    rf_for_partner = _swap(rf_other, "half")
     ctrl_other = _swap(control, "half")
     expanded_all = (
         jnp.einsum("rk,kmlc->lmrc", rf_own, control, preferred_element_type=jnp.float32)
@@ -79,6 +78,7 @@
 
     outs = []
     cf_next = col_factor
+    rf_send = row_factor
     for l in range(n_lev):
         a = anom_t[l]
         expanded = expanded_all[l]
@@ -89,11 +89,14 @@
             prec_t = jnp.transpose(precision, (1, 0, 2))
         prec = prec_t[l]
         if pow2:
-            part, cf_next = _reduce_scatter_rows(inc, "mem", n_mem, jnp.bfloat16, col_factor)
+            part, (cf_next, rf_send) = _reduce_scatter_rows(
+                inc, "mem", n_mem, jnp.bfloat16, (col_factor, rf_send))
             w_blk = (lax.dynamic_slice_in_dim(prec, start, blk, 0) * part).astype(jnp.bfloat16)
             weighted = _all_gather_rows(w_blk, "mem", n_mem)
         else:
             weighted = (prec * lax.psum(inc, "mem")).astype(jnp.bfloat16)
+        if l == 0:
+            rf_for_partner = _swap(lax.dynamic_slice_in_dim(rf_send, (1 - h) * kh, kh, 1), "half")
         scaled = (a.astype(jnp.float32) * weighted.astype(jnp.float32)[None]).astype(jnp.bfloat16)
         projected = jnp.einsum(
             "mrn,nc->mrc", scaled, col_factor, preferred_element_type=jnp.float32

time: 42.9 us -> 44.3 us (1.033)
  matrix products: 5.44 us -> 6.71 us
  local copies, waits for them, and re-layouts: 10.4 us -> 11.2 us
  waiting for transfers between devices: 13.6 us -> 12.9 us
    ppermute x2, starting transfers between devices: 0.58 us -> 4.08 us  [_all_gather_rows(): recv = lax.ppermute(x, axis, [(i, i ^ d) for i in range(size)])]
    ppermute x4, starting transfers between devices: 9.64 us -> 6.25 us  [_reduce_scatter_rows(): recv = lax.ppermute(send, axis, [(i, i ^ d) for i in range(size)])]
    dot_general x2, matrix products: 1.32 us -> 2.73 us  [local(): jnp.einsum('mrc,nc->mrn', expanded, cf_next, preferred_element_type=jnp.f...]
    ppermute x4, waiting for transfers between devices: 9.75 us -> 8.55 us  [_reduce_scatter_rows(): recv = lax.ppermute(send, axis, [(i, i ^ d) for i in range(size)])]
    dynamic_slice x1, local copies, waits for them, and re-layouts: 0.84 us -> 0.01 us  [local(): lax.dynamic_slice_in_dim(rf_send, (1 - h) * kh, kh, 1)]
    slice x1, local copies, waits for them, and re-layouts: 0.81 us -> 1.6 us  [local(): prec = prec_t[l]]
    convert_element_type x2, local copies, waits for them, and re-layouts: 0.05 us -> 0.78 us  [_reduce_scatter_rows(): send = lax.dynamic_slice_in_dim(x, (1 - bit) * half, half, 0).astype(wire)]
    unnamed x12 -> x20, local copies, waits for them, and re-layouts: 6.86 us -> 6.87 us
  transfers between devices with their start and end apart: 14 -> 14, of which waited for: 5 -> 5; matrix products, arithmetic and copies ran while one was open for 27% -> 26% of each run, Pallas kernels for 0% -> 0%
where the time goes in v18:
time: 44.3 us; the launch traced here: 44.1 us
  waiting for transfers between devices  12.9 us (29%)
  starting transfers between devices  12.4 us (28%)
  local copies, waits for them, and re-layouts  11.2 us (25%)
  matrix products  6.71 us (15%)
  other arithmetic  0.62 us (1%)
    ppermute x4, waiting for transfers between devices, _reduce_scatter_rows(): recv = lax.ppermute(send, axis, [(i, i ^ d) for i in range(size)])  8.55 us
    unnamed x20, local copies, waits for them, and re-layouts  6.87 us
    ppermute x4, starting transfers between devices, _reduce_scatter_rows(): recv = lax.ppermute(send, axis, [(i, i ^ d) for i in range(size)])  6.25 us
    ppermute x2, starting transfers between devices, _all_gather_rows(): recv = lax.ppermute(x, axis, [(i, i ^ d) for i in range(size)])  4.08 us
    ppermute x2, waiting for transfers between devices, _all_gather_rows(): recv = lax.ppermute(x, axis, [(i, i ^ d) for i in range(size)])  3.91 us
    dot_general x2, matrix products, local(): jnp.einsum('mrc,nc->mrn', expanded, cf_next, preferred_element_type=jnp.f...  2.73 us
    ppermute x8, starting transfers between devices, _swap(): return lax.ppermute(x, axis, [(0, 1), (1, 0)])  2.05 us
    convert_element_type x1, local copies, waits for them, and re-layouts, local(): (control.astype(jnp.float32) + jnp.stack(outs, axis=2)).astype(jnp.bfloat16)  1.69 us
  transfers between devices with their start and end apart: 14, of which 5 were waited for; matrix products, arithmetic and copies ran while one was open for 26% of the time, Pallas kernels for 0%

profile of v18, /device:TPU:0, one launch (start us, length us, event | category | flops | bytes accessed | tf_op | source)
XLA Modules:
  0.0 44.1 jit_solution(10112791315978880932)
XLA Ops:
  0.0 1.3 %copy.8 = bf16[128,6,2,256]{3,0,2,1:T(8,128)(2,1)S(1)} copy(bf16[128,6,2,256]{3,2,1,0:T(2,128)(2,1)} %param.6) | data formatting | bytes 1572864 | tf_op args[1]
  1.3 0.5 %collective-permute-start = (bf16[128,6,2,256]{3,0,2,1:T(8,128)(2,1)S(1)}, bf16[128,6,2,256]{3,0,2,1:T(8,128)(2,1)S(1)}, u32[]{:S(2)}, u32[]{:S(2)}) collective-permute-start(bf16[128,6,2,256]{3,0,2,1:T(8,128)(2,1)S(1)} %copy.8), channel_id=1, source_target_pairs={{0,1},{1,0},{2,3},{3,2},{4,5},{5,4},{6,7},{7,6},{8,9},{9,8},{10,11... | collective-permute-start | bytes 2359304 | tf_op jit(solution)/shard_map/ppermute | solution.py:8
  1.8 4.3 %copy.28 = bf16[256,6,2,512]{3,0,1,2:T(8,128)(2,1)} copy(bf16[256,6,2,512]{3,2,1,0:T(2,128)(2,1)} %param.5) | data formatting | bytes 6291456 | tf_op args[0]
  6.1 0.6 %fusion.29 = f32[256,6,2,256]{3,0,2,1:T(8,128)S(1)} fusion(bf16[256,256]{1,0:T(8,128)(2,1)S(1)} %copy-done.4, s32[]{:T(128)S(6)} %select_n.58, bf16[128,6,2,256]{3,2,1,0:T(2,128)(2,1)S(1)} %copy-done.1), kind=kOutput, calls=%fused_computation.48 | convolution fusion | flops 201326592 | bytes 3997700 | tf_op jit(solution)/shard_map/rk,kmlc->lmrc/dot_general | solution.py:71
  6.7 0.6 %fusion.11 = bf16[2,6,256,256]{3,2,0,1:T(8,128)(2,1)S(1)} fusion(f32[256,6,2,256]{3,0,2,1:T(8,128)S(1)} %fusion.29, bf16[128,6,2,256]{3,0,2,1:T(8,128)(2,1)S(1)} %collective-permute-done, bf16[256,256]{1,0:T(8,128)(2,1)S(1)} %copy-done.4, s32[]{:T(128)S(6)} %select_n.61), kind=kOutput, calls=%fused_computation.18 | convolution fusion | flops 202899456 | bytes 5570564 | tf_op jit(solution)/shard_map/rk,kmlc->lmrc/dot_general | solution.py:72
  7.3 1.3 %copy-done.2 = bf16[256,6,2,512]{3,0,1,2:T(8,128)(2,1)S(1)} copy-done((bf16[256,6,2,512]{3,0,1,2:T(8,128)(2,1)S(1)}, bf16[256,6,2,512]{3,0,1,2:T(8,128)(2,1)}, u32[]{:S(2)}) %copy-start.2) | copy-done | bytes 3145752
  8.5 0.7 %fusion = f32[256,512]{1,0:T(8,128)S(1)} fusion(bf16[2,6,256,512]{3,2,1,0:T(8,128)(2,1)S(1)} %bitcast.93, bf16[2,6,256,256]{3,2,0,1:T(8,128)(2,1)S(1)} %fusion.11, bf16[512,256]{1,0:T(8,128)(2,1)S(1)} %copy-done), kind=kOutput, calls=%fused_computation.4 | convolution fusion | flops 404881408 | bytes 3145728 | tf_op jit(solution)/shard_map/mrc,nc->mrn/dot_general | solution.py:85
  9.2 0.8 %dynamic-slice_convert_fusion.1 = bf16[128,512]{1,0:T(8,128)(2,1)} fusion(f32[256,512]{1,0:T(8,128)S(1)} %fusion, s32[]{:T(128)S(6)} %select_n.63), kind=kLoop, calls=%fused_computation.40 | loop fusion | bytes 262148 | tf_op jit(solution)/shard_map/convert_element_type | solution.py:19
  10.0 2.6 %collective-permute-start.1 = (bf16[128,512]{1,0:T(8,128)(2,1)}, bf16[128,512]{1,0:T(8,128)(2,1)S(1)}, u32[]{:S(2)}, u32[]{:S(2)}) collective-permute-start(bf16[128,512]{1,0:T(8,128)(2,1)} %dynamic-slice_convert_fusion.1), channel_id=1, source_target_pairs={{0,4},{4,0},{8,12},{12,8},{1,5},{5,1},{9,13},{13,9},{2,6},{6,2},{1... | collective-permute-start | bytes 393224 | tf_op jit(solution)/shard_map/ppermute | solution.py:23
  12.6 1.6 %fusion.60 = (f32[1,256,512]{2,0,1:T(1,128)}, f32[1,256,512]{2,0,1:T(1,128)S(1)}) fusion(f32[2,256,512]{2,0,1:T(2,128)S(1)} %bitcast.96), kind=kLoop, calls=%fused_computation.78 | loop fusion | bytes 2097152 | tf_op jit(solution)/shard_map/slice | solution.py:90
  14.6 2.1 %fusion.2 = f32[256,512]{1,0:T(8,128)S(1)} fusion(bf16[2,6,256,512]{3,2,1,0:T(8,128)(2,1)} %bitcast.92, bf16[2,6,256,256]{3,2,0,1:T(8,128)(2,1)S(1)} %fusion.11, bf16[512,256]{1,0:T(8,128)(2,1)S(1)} %copy-done), kind=kOutput, calls=%fused_computation.6 | convolution fusion | flops 404881408 | bytes 3145728 | tf_op jit(solution)/shard_map/mrc,nc->mrn/dot_general | solution.py:85
  16.7 0.4 collective-permute-start.8
  17.3 2.8 %collective-permute-start.2 = (bf16[128,512]{1,0:T(8,128)(2,1)S(1)}, bf16[128,512]{1,0:T(8,128)(2,1)S(1)}, u32[]{:S(2)}, u32[]{:S(2)}) collective-permute-start(bf16[128,512]{1,0:T(8,128)(2,1)S(1)} %fusion.26), channel_id=1, source_target_pairs={{0,8},{4,12},{8,0},{12,4},{1,9},{5,13},{9,1},{13,5},{2,10},{6,14},... | collective-permute-start | bytes 393224 | tf_op jit(solution)/shard_map/ppermute | solution.py:30
  20.0 5.3 %collective-permute-done.8 = bf16[128,512]{1,0:T(8,128)(2,1)S(1)} collective-permute-done((bf16[128,512]{1,0:T(8,128)(2,1)S(1)}, bf16[128,512]{1,0:T(8,128)(2,1)S(1)}, u32[]{:S(2)}, u32[]{:S(2)}) %collective-permute-start.8) | collective-permute-done | bytes 131104 | tf_op jit(solution)/shard_map/ppermute | solution.py:23
  25.4 0.4 %collective-permute-start.9 = (bf16[128,512]{1,0:T(8,128)(2,1)S(1)}, bf16[128,512]{1,0:T(8,128)(2,1)S(1)}, u32[]{:S(2)}, u32[]{:S(2)}) collective-permute-start(bf16[128,512]{1,0:T(8,128)(2,1)S(1)} %fusion.27), channel_id=1, source_target_pairs={{0,8},{4,12},{8,0},{12,4},{1,9},{5,13},{9,1},{13,5},{2,10},{6,14},... | collective-permute-start | bytes 393224 | tf_op jit(solution)/shard_map/ppermute | solution.py:30
  25.9 4.0 %collective-permute-start.3 = (bf16[128,512]{1,0:T(8,128)(2,1)S(1)}, bf16[128,512]{1,0:T(8,128)(2,1)S(1)}, u32[]{:S(2)}, u32[]{:S(2)}) collective-permute-start(bf16[128,512]{1,0:T(8,128)(2,1)S(1)} %fusion.21), channel_id=1, source_target_pairs={{0,4},{4,0},{8,12},{12,8},{1,5},{5,1},{9,13},{13,9},{2,6},{6,2},{1... | collective-permute-start | bytes 393224 | tf_op jit(solution)/shard_map/ppermute | solution.py:40
  29.9 3.2 %collective-permute-done.9 = bf16[128,512]{1,0:T(8,128)(2,1)S(1)} collective-permute-done((bf16[128,512]{1,0:T(8,128)(2,1)S(1)}, bf16[128,512]{1,0:T(8,128)(2,1)S(1)}, u32[]{:S(2)}, u32[]{:S(2)}) %collective-permute-start.9) | collective-permute-done | bytes 131104 | tf_op jit(solution)/shard_map/ppermute | solution.py:30
  33.3 1.1 %collective-permute-done.3 = bf16[128,512]{1,0:T(8,128)(2,1)S(1)} collective-permute-done((bf16[128,512]{1,0:T(8,128)(2,1)S(1)}, bf16[128,512]{1,0:T(8,128)(2,1)S(1)}, u32[]{:S(2)}, u32[]{:S(2)}) %collective-permute-start.3) | collective-permute-done | bytes 131104 | tf_op jit(solution)/shard_map/ppermute | solution.py:40
  34.6 0.6 %fusion.12 = bf16[6,256,256]{2,1,0:T(8,128)(2,1)S(1)} fusion(f32[256,512]{1,0:T(8,128)S(1)} %maximum_convert_fusion, bf16[2,6,256,512]{3,2,1,0:T(8,128)(2,1)S(1)} %bitcast.94, bf16[512,256]{1,0:T(8,128)(2,1)S(1)} %copy-done), kind=kOutput, calls=%fused_computation.19 | convolution fusion | flops 405405696 | bytes 3145728 | tf_op jit(solution)/shard_map/mrn,nc->mrc/dot_general | solution.py:101
  35.3 0.5 %collective-permute-start.6 = (bf16[2,256,256]{2,1,0:T(8,128)(2,1)S(1)}, bf16[2,256,256]{2,1,0:T(8,128)(2,1)S(1)}, u32[]{:S(2)}, u32[]{:S(2)}) collective-permute-start(bf16[2,256,256]{2,1,0:T(8,128)(2,1)S(1)} %get-tuple-element.21), channel_id=1, source_target_pairs={{0,1},{1,0},{2,3},{3,2},{4,5},{5,4},{6,7},{7,6},{8,9},{9,8},{10,11... | collective-permute-start | bytes 786440 | tf_op jit(solution)/shard_map/ppermute | solution.py:8
  35.9 2.8 %collective-permute-done.10 = bf16[128,512]{1,0:T(8,128)(2,1)S(1)} collective-permute-done((bf16[128,512]{1,0:T(8,128)(2,1)S(1)}, bf16[128,512]{1,0:T(8,128)(2,1)S(1)}, u32[]{:S(2)}, u32[]{:S(2)}) %collective-permute-start.10) | collective-permute-done | bytes 131104 | tf_op jit(solution)/shard_map/ppermute | solution.py:40
  38.7 0.6 %fusion.15 = bf16[6,256,256]{2,1,0:T(8,128)(2,1)S(1)} fusion(f32[256,512]{1,0:T(8,128)S(1)} %maximum_convert_fusion.1, bf16[2,6,256,512]{3,2,1,0:T(8,128)(2,1)S(1)} %bitcast.95, bf16[512,256]{1,0:T(8,128)(2,1)S(1)} %copy-done), kind=kOutput, calls=%fused_computation.20 | convolution fusion | flops 405405696 | bytes 3145728 | tf_op jit(solution)/shard_map/mrn,nc->mrc/dot_general | solution.py:101
  39.4 0.5 %collective-permute-start.12 = (bf16[2,256,256]{2,1,0:T(8,128)(2,1)S(1)}, bf16[2,256,256]{2,1,0:T(8,128)(2,1)S(1)}, u32[]{:S(2)}, u32[]{:S(2)}) collective-permute-start(bf16[2,256,256]{2,1,0:T(8,128)(2,1)S(1)} %get-tuple-element.24), channel_id=1, source_target_pairs={{0,1},{1,0},{2,3},{3,2},{4,5},{5,4},{6,7},{7,6},{8,9},{9,8},{10,11... | collective-permute-start | bytes 786440 | tf_op jit(solution)/shard_map/ppermute | solution.py:8
  42.5 1.7 %copy.13 = bf16[128,6,2,256]{3,2,1,0:T(2,128)(2,1)} copy(bf16[128,6,2,256]{3,0,1,2:T(8,128)(2,1)S(1)} %fusion.8) | data formatting | bytes 1572864 | tf_op jit(solution)/shard_map/convert_element_type | solution.py:116
  (57 shorter events, 3.7 us)
Async XLA Ops:
  0.0 7.3 %copy-start = (bf16[512,256]{1,0:T(8,128)(2,1)S(1)}, bf16[512,256]{1,0:T(8,128)(2,1)}, u32[]{:S(2)}) copy-start(bf16[512,256]{1,0:T(8,128)(2,1)} %param.9) | copy-start | bytes 786436
  1.3 5.4 %collective-permute-start = (bf16[128,6,2,256]{3,0,2,1:T(8,128)(2,1)S(1)}, bf16[128,6,2,256]{3,0,2,1:T(8,128)(2,1)S(1)}, u32[]{:S(2)}, u32[]{:S(2)}) collective-permute-start(bf16[128,6,2,256]{3,0,2,1:T(8,128)(2,1)S(1)} %copy.8), channel_id=1, source_target_pairs={{0,1},{1,0},{2,3},{3,2},{4,5},{5,4},{6,7},{7,6},{8,9},{9,8},{10,11... | collective-permute-start | bytes 2359304 | tf_op jit(solution)/shard_map/ppermute | solution.py:8
  1.8 4.3 %copy-start.1 = (bf16[128,6,2,256]{3,2,1,0:T(2,128)(2,1)S(1)}, bf16[128,6,2,256]{3,2,1,0:T(2,128)(2,1)}, u32[]{:S(2)}) copy-start(bf16[128,6,2,256]{3,2,1,0:T(2,128)(2,1)} %param.6) | copy-start | bytes 2359300
  1.8 4.3 %copy-start.4 = (bf16[256,256]{1,0:T(8,128)(2,1)S(1)}, bf16[256,256]{1,0:T(8,128)(2,1)}, u32[]{:S(2)}) copy-start(bf16[256,256]{1,0:T(8,128)(2,1)} %param.8) | copy-start | bytes 393220
  6.7 1.9 %copy-start.2 = (bf16[256,6,2,512]{3,0,1,2:T(8,128)(2,1)S(1)}, bf16[256,6,2,512]{3,0,1,2:T(8,128)(2,1)}, u32[]{:S(2)}) copy-start(bf16[256,6,2,512]{3,0,1,2:T(8,128)(2,1)} %copy.28) | copy-start | bytes 9437188
  7.3 5.4 %copy-start.6 = (f32[256,2,512]{2,1,0:T(2,128)S(1)}, f32[256,2,512]{2,1,0:T(2,128)}, u32[]{:S(2)}) copy-start(f32[256,2,512]{2,1,0:T(2,128)} %param.7) | copy-start | bytes 3145732
  9.2 3.4 %copy-start.7 = (f32[256,512]{1,0:T(8,128)}, f32[256,512]{1,0:T(8,128)S(1)}, u32[]{:S(2)}) copy-start(f32[256,512]{1,0:T(8,128)S(1)} %fusion) | copy-start | bytes 1572868
  10.0 7.2 %collective-permute-start.1 = (bf16[128,512]{1,0:T(8,128)(2,1)}, bf16[128,512]{1,0:T(8,128)(2,1)S(1)}, u32[]{:S(2)}, u32[]{:S(2)}) collective-permute-start(bf16[128,512]{1,0:T(8,128)(2,1)} %dynamic-slice_convert_fusion.1), channel_id=1, source_target_pairs={{0,4},{4,0},{8,12},{12,8},{1,5},{5,1},{9,13},{13,9},{2,6},{6,2},{1... | collective-permute-start | bytes 393224 | tf_op jit(solution)/shard_map/ppermute | solution.py:23
  14.3 2.8 %copy-start.5 = (f32[1,256,512]{2,0,1:T(1,128)S(1)}, f32[1,256,512]{2,0,1:T(1,128)}, u32[]{:S(2)}) copy-start(f32[1,256,512]{2,0,1:T(1,128)} %get-tuple-element.17) | copy-start | bytes 1572868
  14.3 2.9 %copy-start.8 = (f32[256,512]{1,0:T(8,128)S(1)}, f32[256,512]{1,0:T(8,128)}, u32[]{:S(2)}) copy-start(f32[256,512]{1,0:T(8,128)} %copy-done.7) | copy-start | bytes 1572868
  14.4 25.1 %collective-permute-start.4 = (bf16[256,128]{0,1:T(8,128)(2,1)S(1)}, bf16[256,128]{0,1:T(8,128)(2,1)S(1)}, u32[]{:S(2)}, u32[]{:S(2)}) collective-permute-start(bf16[256,128]{0,1:T(8,128)(2,1)S(1)} %constant_dynamic-slice_fusion.1), channel_id=1, source_target_pairs={{0,1},{1,0},{2,3},{3,2},{4,5},{5,4},{6,7},{7,6},{8,9},{9,8},{10,11... | collective-permute-start | bytes 196616 | tf_op jit(solution)/shard_map/ppermute | solution.py:8
  16.7 17.9 %copy-start.3 = (bf16[256,6,2,512]{3,0,1,2:T(8,128)(2,1)S(1)}, bf16[256,6,2,512]{3,0,1,2:T(8,128)(2,1)}, u32[]{:S(2)}) copy-start(bf16[256,6,2,512]{3,0,1,2:T(8,128)(2,1)} %copy.28) | copy-start | bytes 9437188
  16.7 8.6 %collective-permute-start.8 = (bf16[128,512]{1,0:T(8,128)(2,1)S(1)}, bf16[128,512]{1,0:T(8,128)(2,1)S(1)}, u32[]{:S(2)}, u32[]{:S(2)}) collective-permute-start(bf16[128,512]{1,0:T(8,128)(2,1)S(1)} %dynamic-slice_convert_fusion), channel_id=1, source_target_pairs={{0,4},{4,0},{8,12},{12,8},{1,5},{5,1},{9,13},{13,9},{2,6},{6,2},{1... | collective-permute-start | bytes 393224 | tf_op jit(solution)/shard_map/ppermute | solution.py:23
  17.3 8.5 %collective-permute-start.2 = (bf16[128,512]{1,0:T(8,128)(2,1)S(1)}, bf16[128,512]{1,0:T(8,128)(2,1)S(1)}, u32[]{:S(2)}, u32[]{:S(2)}) collective-permute-start(bf16[128,512]{1,0:T(8,128)(2,1)S(1)} %fusion.26), channel_id=1, source_target_pairs={{0,8},{4,12},{8,0},{12,4},{1,9},{5,13},{9,1},{13,5},{2,10},{6,14},... | collective-permute-start | bytes 393224 | tf_op jit(solution)/shard_map/ppermute | solution.py:30
  25.4 7.8 %collective-permute-start.9 = (bf16[128,512]{1,0:T(8,128)(2,1)S(1)}, bf16[128,512]{1,0:T(8,128)(2,1)S(1)}, u32[]{:S(2)}, u32[]{:S(2)}) collective-permute-start(bf16[128,512]{1,0:T(8,128)(2,1)S(1)} %fusion.27), channel_id=1, source_target_pairs={{0,8},{4,12},{8,0},{12,4},{1,9},{5,13},{9,1},{13,5},{2,10},{6,14},... | collective-permute-start | bytes 393224 | tf_op jit(solution)/shard_map/ppermute | solution.py:30
  25.9 8.6 %collective-permute-start.3 = (bf16[128,512]{1,0:T(8,128)(2,1)S(1)}, bf16[128,512]{1,0:T(8,128)(2,1)S(1)}, u32[]{:S(2)}, u32[]{:S(2)}) collective-permute-start(bf16[128,512]{1,0:T(8,128)(2,1)S(1)} %fusion.21), channel_id=1, source_target_pairs={{0,4},{4,0},{8,12},{12,8},{1,5},{5,1},{9,13},{13,9},{2,6},{6,2},{1... | collective-permute-start | bytes 393224 | tf_op jit(solution)/shard_map/ppermute | solution.py:40
  33.2 5.4 %collective-permute-start.10 = (bf16[128,512]{1,0:T(8,128)(2,1)S(1)}, bf16[128,512]{1,0:T(8,128)(2,1)S(1)}, u32[]{:S(2)}, u32[]{:S(2)}) collective-permute-start(bf16[128,512]{1,0:T(8,128)(2,1)S(1)} %fusion.20), channel_id=1, source_target_pairs={{0,4},{4,0},{8,12},{12,8},{1,5},{5,1},{9,13},{13,9},{2,6},{6,2},{1... | collective-permute-start | bytes 393224 | tf_op jit(solution)/shard_map/ppermute | solution.py:40
  35.2 4.7 %collective-permute-start.5 = (bf16[2,256,256]{2,1,0:T(8,128)(2,1)S(1)}, bf16[2,256,256]{2,1,0:T(8,128)(2,1)S(1)}, u32[]{:S(2)}, u32[]{:S(2)}) collective-permute-start(bf16[2,256,256]{2,1,0:T(8,128)(2,1)S(1)} %get-tuple-element.19), channel_id=1, source_target_pairs={{0,1},{1,0},{2,3},{3,2},{4,5},{5,4},{6,7},{7,6},{8,9},{9,8},{10,11... | collective-permute-start | bytes 786440 | tf_op jit(solution)/shard_map/ppermute | solution.py:8
  35.3 4.9 %collective-permute-start.6 = (bf16[2,256,256]{2,1,0:T(8,128)(2,1)S(1)}, bf16[2,256,256]{2,1,0:T(8,128)(2,1)S(1)}, u32[]{:S(2)}, u32[]{:S(2)}) collective-permute-start(bf16[2,256,256]{2,1,0:T(8,128)(2,1)S(1)} %get-tuple-element.21), channel_id=1, source_target_pairs={{0,1},{1,0},{2,3},{3,2},{4,5},{5,4},{6,7},{7,6},{8,9},{9,8},{10,11... | collective-permute-start | bytes 786440 | tf_op jit(solution)/shard_map/ppermute | solution.py:8
  35.8 4.6 %collective-permute-start.7 = (bf16[2,256,256]{2,1,0:T(8,128)(2,1)S(1)}, bf16[2,256,256]{2,1,0:T(8,128)(2,1)S(1)}, u32[]{:S(2)}, u32[]{:S(2)}) collective-permute-start(bf16[2,256,256]{2,1,0:T(8,128)(2,1)S(1)} %get-tuple-element.20), channel_id=1, source_target_pairs={{0,1},{1,0},{2,3},{3,2},{4,5},{5,4},{6,7},{7,6},{8,9},{9,8},{10,11... | collective-permute-start | bytes 786440 | tf_op jit(solution)/shard_map/ppermute | solution.py:8
  39.3 1.6 %collective-permute-start.11 = (bf16[2,256,256]{2,1,0:T(8,128)(2,1)S(1)}, bf16[2,256,256]{2,1,0:T(8,128)(2,1)S(1)}, u32[]{:S(2)}, u32[]{:S(2)}) collective-permute-start(bf16[2,256,256]{2,1,0:T(8,128)(2,1)S(1)} %get-tuple-element.22), channel_id=1, source_target_pairs={{0,1},{1,0},{2,3},{3,2},{4,5},{5,4},{6,7},{7,6},{8,9},{9,8},{10,11... | collective-permute-start | bytes 786440 | tf_op jit(solution)/shard_map/ppermute | solution.py:8
  39.4 2.0 %collective-permute-start.12 = (bf16[2,256,256]{2,1,0:T(8,128)(2,1)S(1)}, bf16[2,256,256]{2,1,0:T(8,128)(2,1)S(1)}, u32[]{:S(2)}, u32[]{:S(2)}) collective-permute-start(bf16[2,256,256]{2,1,0:T(8,128)(2,1)S(1)} %get-tuple-element.24), channel_id=1, source_target_pairs={{0,1},{1,0},{2,3},{3,2},{4,5},{5,4},{6,7},{7,6},{8,9},{9,8},{10,11... | collective-permute-start | bytes 786440 | tf_op jit(solution)/shard_map/ppermute | solution.py:8
  39.9 1.8 %collective-permute-start.13 = (bf16[2,256,256]{2,1,0:T(8,128)(2,1)S(1)}, bf16[2,256,256]{2,1,0:T(8,128)(2,1)S(1)}, u32[]{:S(2)}, u32[]{:S(2)}) collective-permute-start(bf16[2,256,256]{2,1,0:T(8,128)(2,1)S(1)} %get-tuple-element.23), channel_id=1, source_target_pairs={{0,1},{1,0},{2,3},{3,2},{4,5},{5,4},{6,7},{7,6},{8,9},{9,8},{10,11... | collective-permute-start | bytes 786440 | tf_op jit(solution)/shard_map/ppermute | solution.py:8

commit v19 on v17

--- a/solution.py
+++ b/solution.py
@@ -79,21 +79,30 @@
 
     outs = []
     cf_next = col_factor
+    parts = []
     for l in range(n_lev):
         a = anom_t[l]
         expanded = expanded_all[l]
         fields = jnp.einsum("mrc,nc->mrn", expanded, cf_next, preferred_element_type=jnp.float32)
         inc = jnp.sum(a.astype(jnp.float32) * fields, axis=0)
-        if l == 0:
-            precision, inc = lax.optimization_barrier((precision, inc))
-            prec_t = jnp.transpose(precision, (1, 0, 2))
+        if pow2:
+            if l + 1 < n_lev:
+                part, cf_next = _reduce_scatter_rows(inc, "mem", n_mem, jnp.bfloat16, col_factor)
+            else:
+                part, precision = _reduce_scatter_rows(inc, "mem", n_mem, jnp.bfloat16, precision)
+        else:
+            part = inc
+        parts.append(part)
+    prec_t = jnp.transpose(precision, (1, 0, 2))
+    for l in range(n_lev):
+        a = anom_t[l]
+        part = parts[l]
         prec = prec_t[l]
         if pow2:
-            part, cf_next = _reduce_scatter_rows(inc, "mem", n_mem, jnp.bfloat16, col_factor)
             w_blk = (lax.dynamic_slice_in_dim(prec, start, blk, 0) * part).astype(jnp.bfloat16)
             weighted = _all_gather_rows(w_blk, "mem", n_mem)
         else:
-            weighted = (prec * lax.psum(inc, "mem")).astype(jnp.bfloat16)
+            weighted = (prec * lax.psum(part, "mem")).astype(jnp.bfloat16)
         scaled = (a.astype(jnp.float32) * weighted.astype(jnp.float32)[None]).astype(jnp.bfloat16)
         projected = jnp.einsum(
             "mrn,nc->mrc", scaled, col_factor, preferred_element_type=jnp.float32

time: 42.9 us -> 43 us (level)
  starting transfers between devices: 12.4 us -> 12.9 us
  waiting for transfers between devices: 13.6 us -> 13.1 us
    ppermute x4, waiting for transfers between devices: 9.75 us -> 9.26 us  [_reduce_scatter_rows(): recv = lax.ppermute(send, axis, [(i, i ^ d) for i in range(size)])]
    ppermute x4, starting transfers between devices: 9.64 us -> 10.1 us  [_reduce_scatter_rows(): recv = lax.ppermute(send, axis, [(i, i ^ d) for i in range(size)])]
where the time goes in v19:
time: 43 us; the launch traced here: 42.8 us
  waiting for transfers between devices  13.1 us (30%)
  starting transfers between devices  12.9 us (30%)
  local copies, waits for them, and re-layouts  10.4 us (24%)
  matrix products  5.43 us (13%)
  other arithmetic  0.62 us (1%)
    ppermute x4, starting transfers between devices, _reduce_scatter_rows(): recv = lax.ppermute(send, axis, [(i, i ^ d) for i in range(size)])  10.1 us
    ppermute x4, waiting for transfers between devices, _reduce_scatter_rows(): recv = lax.ppermute(send, axis, [(i, i ^ d) for i in range(size)])  9.26 us
    unnamed x12, local copies, waits for them, and re-layouts  6.87 us
    ppermute x2, waiting for transfers between devices, _all_gather_rows(): recv = lax.ppermute(x, axis, [(i, i ^ d) for i in range(size)])  3.83 us
    ppermute x8, starting transfers between devices, _swap(): return lax.ppermute(x, axis, [(0, 1), (1, 0)])  2.22 us
    convert_element_type x1, local copies, waits for them, and re-layouts, local(): (control.astype(jnp.float32) + jnp.stack(outs, axis=2)).astype(jnp.bfloat16)  1.69 us
    dot_general x2, matrix products, local(): jnp.einsum('mrc,nc->mrn', expanded, cf_next, preferred_element_type=jnp.f...  1.31 us
    dot_general x6, matrix products, local(): jnp.einsum('rk,mrc->kmc', rf_for_partner, proj_other, preferred_element_t...  1.22 us
  transfers between devices with their start and end apart: 14, of which 5 were waited for; matrix products, arithmetic and copies ran while one was open for 27% of the time, Pallas kernels for 0%

profile of v19, /device:TPU:0, one launch (start us, length us, event | category | flops | bytes accessed | tf_op | source)
XLA Modules:
  0.0 42.8 jit_solution(17156380384854818600)
XLA Ops:
  0.0 1.3 %copy.8 = bf16[128,6,2,256]{3,0,2,1:T(8,128)(2,1)S(1)} copy(bf16[128,6,2,256]{3,2,1,0:T(2,128)(2,1)} %param.6) | data formatting | bytes 1572864 | tf_op args[1]
  1.3 0.5 %collective-permute-start = (bf16[128,6,2,256]{3,0,2,1:T(8,128)(2,1)S(1)}, bf16[128,6,2,256]{3,0,2,1:T(8,128)(2,1)S(1)}, u32[]{:S(2)}, u32[]{:S(2)}) collective-permute-start(bf16[128,6,2,256]{3,0,2,1:T(8,128)(2,1)S(1)} %copy.8), channel_id=1, source_target_pairs={{0,1},{1,0},{2,3},{3,2},{4,5},{5,4},{6,7},{7,6},{8,9},{9,8},{10,11... | collective-permute-start | bytes 2359304 | tf_op jit(solution)/shard_map/ppermute | solution.py:8
  1.8 0.8 %constant_dynamic-slice_fusion.2 = bf16[256,128]{1,0:T(8,128)(2,1)S(1)} fusion(bf16[256,256]{1,0:T(8,128)(2,1)} %param.8, s32[]{:T(128)S(6)} %select_n.60), kind=kLoop, calls=%fused_computation.73 | loop fusion | bytes 131076 | tf_op jit(solution)/shard_map/dynamic_slice | solution.py:68
  2.7 4.3 %copy.45 = bf16[256,6,2,512]{3,0,1,2:T(8,128)(2,1)} copy(bf16[256,6,2,512]{3,2,1,0:T(2,128)(2,1)} %param.5) | data formatting | bytes 6291456 | tf_op args[0]
  7.0 0.6 %fusion.29 = f32[256,6,2,256]{3,0,2,1:T(8,128)S(1)} fusion(bf16[256,256]{1,0:T(8,128)(2,1)S(1)} %copy-done.4, s32[]{:T(128)S(6)} %select_n.57, bf16[128,6,2,256]{3,2,1,0:T(2,128)(2,1)S(1)} %copy-done.1), kind=kOutput, calls=%fused_computation.48 | convolution fusion | flops 201326592 | bytes 3997700 | tf_op jit(solution)/shard_map/rk,kmlc->lmrc/dot_general | solution.py:72
  7.6 0.6 %fusion.11 = bf16[2,6,256,256]{3,2,0,1:T(8,128)(2,1)S(1)} fusion(f32[256,6,2,256]{3,0,2,1:T(8,128)S(1)} %fusion.29, bf16[128,6,2,256]{3,0,2,1:T(8,128)(2,1)S(1)} %collective-permute-done, bf16[256,128]{1,0:T(8,128)(2,1)S(1)} %constant_dynamic-slice_fusion.2), kind=kOutput, calls=%fused_computation.18 | convolution fusion | flops 202899456 | bytes 5570560 | tf_op jit(solution)/shard_map/rk,kmlc->lmrc/dot_general | solution.py:73
  8.2 1.3 %copy-done.2 = bf16[256,6,2,512]{3,0,1,2:T(8,128)(2,1)S(1)} copy-done((bf16[256,6,2,512]{3,0,1,2:T(8,128)(2,1)S(1)}, bf16[256,6,2,512]{3,0,1,2:T(8,128)(2,1)}, u32[]{:S(2)}) %copy-start.2) | copy-done | bytes 3145752
  9.5 0.7 %fusion = f32[256,512]{1,0:T(8,128)S(1)} fusion(bf16[2,6,256,512]{3,2,1,0:T(8,128)(2,1)S(1)} %bitcast.97, bf16[2,6,256,256]{3,2,0,1:T(8,128)(2,1)S(1)} %fusion.11, bf16[512,256]{1,0:T(8,128)(2,1)S(1)} %copy-done), kind=kOutput, calls=%fused_computation.4 | convolution fusion | flops 404881408 | bytes 3145728 | tf_op jit(solution)/shard_map/mrc,nc->mrn/dot_general | solution.py:86
  10.2 3.1 %collective-permute-start.1 = (bf16[128,512]{1,0:T(8,128)(2,1)S(1)}, bf16[128,512]{1,0:T(8,128)(2,1)S(1)}, u32[]{:S(2)}, u32[]{:S(2)}) collective-permute-start(bf16[128,512]{1,0:T(8,128)(2,1)S(1)} %dynamic-slice_convert_fusion.1), channel_id=1, source_target_pairs={{0,4},{4,0},{8,12},{12,8},{1,5},{5,1},{9,13},{13,9},{2,6},{6,2},{1... | collective-permute-start | bytes 393224 | tf_op jit(solution)/shard_map/ppermute | solution.py:23
  13.3 0.7 %fusion.2 = f32[256,512]{1,0:T(8,128)S(1)} fusion(bf16[2,6,256,512]{3,2,1,0:T(8,128)(2,1)S(1)} %bitcast.98, bf16[2,6,256,256]{3,2,0,1:T(8,128)(2,1)S(1)} %fusion.11, bf16[512,256]{1,0:T(8,128)(2,1)S(1)} %copy-done), kind=kOutput, calls=%fused_computation.6 | convolution fusion | flops 404881408 | bytes 3145728 | tf_op jit(solution)/shard_map/mrc,nc->mrn/dot_general | solution.py:86
  14.0 0.8 %fusion.58 = (f32[1,256,512]{2,0,1:T(1,128)S(1)}, f32[1,256,512]{2,0,1:T(1,128)S(1)}) fusion(f32[2,256,512]{2,0,1:T(2,128)S(1)} %bitcast.101), kind=kLoop, calls=%fused_computation.76 | loop fusion | bytes 2097152 | tf_op jit(solution)/shard_map/slice | solution.py:100
  14.8 0.5 %collective-permute-start.8 = (bf16[128,512]{1,0:T(8,128)(2,1)S(1)}, bf16[128,512]{1,0:T(8,128)(2,1)S(1)}, u32[]{:S(2)}, u32[]{:S(2)}) collective-permute-start(bf16[128,512]{1,0:T(8,128)(2,1)S(1)} %dynamic-slice_convert_fusion), channel_id=1, source_target_pairs={{0,4},{4,0},{8,12},{12,8},{1,5},{5,1},{9,13},{13,9},{2,6},{6,2},{1... | collective-permute-start | bytes 393224 | tf_op jit(solution)/shard_map/ppermute | solution.py:23
  15.3 1.7 %collective-permute-done.1 = bf16[128,512]{1,0:T(8,128)(2,1)S(1)} collective-permute-done((bf16[128,512]{1,0:T(8,128)(2,1)S(1)}, bf16[128,512]{1,0:T(8,128)(2,1)S(1)}, u32[]{:S(2)}, u32[]{:S(2)}) %collective-permute-start.1) | collective-permute-done | bytes 131104 | tf_op jit(solution)/shard_map/ppermute | solution.py:23
  17.0 2.8 %collective-permute-start.2 = (bf16[128,512]{1,0:T(8,128)(2,1)S(1)}, bf16[128,512]{1,0:T(8,128)(2,1)S(1)}, u32[]{:S(2)}, u32[]{:S(2)}) collective-permute-start(bf16[128,512]{1,0:T(8,128)(2,1)S(1)} %fusion.26), channel_id=1, source_target_pairs={{0,8},{4,12},{8,0},{12,4},{1,9},{5,13},{9,1},{13,5},{2,10},{6,14},... | collective-permute-start | bytes 393224 | tf_op jit(solution)/shard_map/ppermute | solution.py:30
  20.0 3.8 %collective-permute-start.9 = (bf16[128,512]{1,0:T(8,128)(2,1)S(1)}, bf16[128,512]{1,0:T(8,128)(2,1)S(1)}, u32[]{:S(2)}, u32[]{:S(2)}) collective-permute-start(bf16[128,512]{1,0:T(8,128)(2,1)S(1)} %fusion.27), channel_id=1, source_target_pairs={{0,8},{4,12},{8,0},{12,4},{1,9},{5,13},{9,1},{13,5},{2,10},{6,14},... | collective-permute-start | bytes 393224 | tf_op jit(solution)/shard_map/ppermute | solution.py:30
  23.9 5.8 %collective-permute-done.2 = bf16[128,512]{1,0:T(8,128)(2,1)S(1)} collective-permute-done((bf16[128,512]{1,0:T(8,128)(2,1)S(1)}, bf16[128,512]{1,0:T(8,128)(2,1)S(1)}, u32[]{:S(2)}, u32[]{:S(2)}) %collective-permute-start.2) | collective-permute-done | bytes 131104 | tf_op jit(solution)/shard_map/ppermute | solution.py:30
  29.8 1.6 %collective-permute-done.9 = bf16[128,512]{1,0:T(8,128)(2,1)S(1)} collective-permute-done((bf16[128,512]{1,0:T(8,128)(2,1)S(1)}, bf16[128,512]{1,0:T(8,128)(2,1)S(1)}, u32[]{:S(2)}, u32[]{:S(2)}) %collective-permute-start.9) | collective-permute-done | bytes 131104 | tf_op jit(solution)/shard_map/ppermute | solution.py:30
  31.4 0.5 %collective-permute-start.10 = (bf16[128,512]{1,0:T(8,128)(2,1)S(1)}, bf16[128,512]{1,0:T(8,128)(2,1)S(1)}, u32[]{:S(2)}, u32[]{:S(2)}) collective-permute-start(bf16[128,512]{1,0:T(8,128)(2,1)S(1)} %fusion.20), channel_id=1, source_target_pairs={{0,4},{4,0},{8,12},{12,8},{1,5},{5,1},{9,13},{13,9},{2,6},{6,2},{1... | collective-permute-start | bytes 393224 | tf_op jit(solution)/shard_map/ppermute | solution.py:40
  31.9 3.8 %collective-permute-done.3 = bf16[128,512]{1,0:T(8,128)(2,1)S(1)} collective-permute-done((bf16[128,512]{1,0:T(8,128)(2,1)S(1)}, bf16[128,512]{1,0:T(8,128)(2,1)S(1)}, u32[]{:S(2)}, u32[]{:S(2)}) %collective-permute-start.3) | collective-permute-done | bytes 131104 | tf_op jit(solution)/shard_map/ppermute | solution.py:40
  35.8 0.6 %fusion.12 = bf16[6,256,256]{2,1,0:T(8,128)(2,1)S(1)} fusion(f32[256,512]{1,0:T(8,128)S(1)} %maximum_convert_fusion, bf16[2,6,256,512]{3,2,1,0:T(8,128)(2,1)S(1)} %bitcast.99, bf16[512,256]{1,0:T(8,128)(2,1)S(1)} %copy-done), kind=kOutput, calls=%fused_computation.19 | convolution fusion | flops 405405696 | bytes 3145728 | tf_op jit(solution)/shard_map/mrn,nc->mrc/dot_general | solution.py:107
  36.6 0.5 %collective-permute-start.5 = (bf16[2,256,256]{2,1,0:T(8,128)(2,1)S(1)}, bf16[2,256,256]{2,1,0:T(8,128)(2,1)S(1)}, u32[]{:S(2)}, u32[]{:S(2)}) collective-permute-start(bf16[2,256,256]{2,1,0:T(8,128)(2,1)S(1)} %get-tuple-element.15), channel_id=1, source_target_pairs={{0,1},{1,0},{2,3},{3,2},{4,5},{5,4},{6,7},{7,6},{8,9},{9,8},{10,11... | collective-permute-start | bytes 786440 | tf_op jit(solution)/shard_map/ppermute | solution.py:8
  37.2 0.6 %fusion.15 = bf16[6,256,256]{2,1,0:T(8,128)(2,1)S(1)} fusion(f32[256,512]{1,0:T(8,128)S(1)} %maximum_convert_fusion.1, bf16[2,6,256,512]{3,2,1,0:T(8,128)(2,1)S(1)} %bitcast.100, bf16[512,256]{1,0:T(8,128)(2,1)S(1)} %copy-done), kind=kOutput, calls=%fused_computation.20 | convolution fusion | flops 405405696 | bytes 3145728 | tf_op jit(solution)/shard_map/mrn,nc->mrc/dot_general | solution.py:107
  37.9 0.5 %collective-permute-start.12 = (bf16[2,256,256]{2,1,0:T(8,128)(2,1)S(1)}, bf16[2,256,256]{2,1,0:T(8,128)(2,1)S(1)}, u32[]{:S(2)}, u32[]{:S(2)}) collective-permute-start(bf16[2,256,256]{2,1,0:T(8,128)(2,1)S(1)} %get-tuple-element.20), channel_id=1, source_target_pairs={{0,1},{1,0},{2,3},{3,2},{4,5},{5,4},{6,7},{7,6},{8,9},{9,8},{10,11... | collective-permute-start | bytes 786440 | tf_op jit(solution)/shard_map/ppermute | solution.py:8
  41.1 1.7 %copy.18 = bf16[128,6,2,256]{3,2,1,0:T(2,128)(2,1)} copy(bf16[128,6,2,256]{3,0,1,2:T(8,128)(2,1)S(1)} %fusion.8) | data formatting | bytes 1572864 | tf_op jit(solution)/shard_map/convert_element_type | solution.py:122
  (48 shorter events, 3.7 us)
Async XLA Ops:
  0.0 8.2 %copy-start = (bf16[512,256]{1,0:T(8,128)(2,1)S(1)}, bf16[512,256]{1,0:T(8,128)(2,1)}, u32[]{:S(2)}) copy-start(bf16[512,256]{1,0:T(8,128)(2,1)} %param.9) | copy-start | bytes 786436
  1.3 6.3 %collective-permute-start = (bf16[128,6,2,256]{3,0,2,1:T(8,128)(2,1)S(1)}, bf16[128,6,2,256]{3,0,2,1:T(8,128)(2,1)S(1)}, u32[]{:S(2)}, u32[]{:S(2)}) collective-permute-start(bf16[128,6,2,256]{3,0,2,1:T(8,128)(2,1)S(1)} %copy.8), channel_id=1, source_target_pairs={{0,1},{1,0},{2,3},{3,2},{4,5},{5,4},{6,7},{7,6},{8,9},{9,8},{10,11... | collective-permute-start | bytes 2359304 | tf_op jit(solution)/shard_map/ppermute | solution.py:8
  2.7 35.7 %collective-permute-start.4 = (bf16[256,128]{1,0:T(8,128)(2,1)S(1)}, bf16[256,128]{1,0:T(8,128)(2,1)S(1)}, u32[]{:S(2)}, u32[]{:S(2)}) collective-permute-start(bf16[256,128]{1,0:T(8,128)(2,1)S(1)} %constant_dynamic-slice_fusion.2), channel_id=1, source_target_pairs={{0,1},{1,0},{2,3},{3,2},{4,5},{5,4},{6,7},{7,6},{8,9},{9,8},{10,11... | collective-permute-start | bytes 196616 | tf_op jit(solution)/shard_map/ppermute | solution.py:8
  2.7 4.3 %copy-start.1 = (bf16[128,6,2,256]{3,2,1,0:T(2,128)(2,1)S(1)}, bf16[128,6,2,256]{3,2,1,0:T(2,128)(2,1)}, u32[]{:S(2)}) copy-start(bf16[128,6,2,256]{3,2,1,0:T(2,128)(2,1)} %param.6) | copy-start | bytes 2359300
  2.7 4.3 %copy-start.4 = (bf16[256,256]{1,0:T(8,128)(2,1)S(1)}, bf16[256,256]{1,0:T(8,128)(2,1)}, u32[]{:S(2)}) copy-start(bf16[256,256]{1,0:T(8,128)(2,1)} %param.8) | copy-start | bytes 393220
  7.6 1.9 %copy-start.2 = (bf16[256,6,2,512]{3,0,1,2:T(8,128)(2,1)S(1)}, bf16[256,6,2,512]{3,0,1,2:T(8,128)(2,1)}, u32[]{:S(2)}) copy-start(bf16[256,6,2,512]{3,0,1,2:T(8,128)(2,1)} %copy.45) | copy-start | bytes 9437188
  10.1 3.8 %copy-start.3 = (f32[256,2,512]{2,1,0:T(2,128)S(1)}, f32[256,2,512]{2,1,0:T(2,128)}, u32[]{:S(2)}) copy-start(f32[256,2,512]{2,1,0:T(2,128)} %param.7) | copy-start | bytes 3145732
  10.2 6.8 %collective-permute-start.1 = (bf16[128,512]{1,0:T(8,128)(2,1)S(1)}, bf16[128,512]{1,0:T(8,128)(2,1)S(1)}, u32[]{:S(2)}, u32[]{:S(2)}) collective-permute-start(bf16[128,512]{1,0:T(8,128)(2,1)S(1)} %dynamic-slice_convert_fusion.1), channel_id=1, source_target_pairs={{0,4},{4,0},{8,12},{12,8},{1,5},{5,1},{9,13},{13,9},{2,6},{6,2},{1... | collective-permute-start | bytes 393224 | tf_op jit(solution)/shard_map/ppermute | solution.py:23
  14.8 5.2 %collective-permute-start.8 = (bf16[128,512]{1,0:T(8,128)(2,1)S(1)}, bf16[128,512]{1,0:T(8,128)(2,1)S(1)}, u32[]{:S(2)}, u32[]{:S(2)}) collective-permute-start(bf16[128,512]{1,0:T(8,128)(2,1)S(1)} %dynamic-slice_convert_fusion), channel_id=1, source_target_pairs={{0,4},{4,0},{8,12},{12,8},{1,5},{5,1},{9,13},{13,9},{2,6},{6,2},{1... | collective-permute-start | bytes 393224 | tf_op jit(solution)/shard_map/ppermute | solution.py:23
  17.0 12.6 %collective-permute-start.2 = (bf16[128,512]{1,0:T(8,128)(2,1)S(1)}, bf16[128,512]{1,0:T(8,128)(2,1)S(1)}, u32[]{:S(2)}, u32[]{:S(2)}) collective-permute-start(bf16[128,512]{1,0:T(8,128)(2,1)S(1)} %fusion.26), channel_id=1, source_target_pairs={{0,8},{4,12},{8,0},{12,4},{1,9},{5,13},{9,1},{13,5},{2,10},{6,14},... | collective-permute-start | bytes 393224 | tf_op jit(solution)/shard_map/ppermute | solution.py:30
  20.0 11.3 %collective-permute-start.9 = (bf16[128,512]{1,0:T(8,128)(2,1)S(1)}, bf16[128,512]{1,0:T(8,128)(2,1)S(1)}, u32[]{:S(2)}, u32[]{:S(2)}) collective-permute-start(bf16[128,512]{1,0:T(8,128)(2,1)S(1)} %fusion.27), channel_id=1, source_target_pairs={{0,8},{4,12},{8,0},{12,4},{1,9},{5,13},{9,1},{13,5},{2,10},{6,14},... | collective-permute-start | bytes 393224 | tf_op jit(solution)/shard_map/ppermute | solution.py:30
  29.7 6.1 %collective-permute-start.3 = (bf16[128,512]{1,0:T(8,128)(2,1)S(1)}, bf16[128,512]{1,0:T(8,128)(2,1)S(1)}, u32[]{:S(2)}, u32[]{:S(2)}) collective-permute-start(bf16[128,512]{1,0:T(8,128)(2,1)S(1)} %fusion.21), channel_id=1, source_target_pairs={{0,4},{4,0},{8,12},{12,8},{1,5},{5,1},{9,13},{13,9},{2,6},{6,2},{1... | collective-permute-start | bytes 393224 | tf_op jit(solution)/shard_map/ppermute | solution.py:40
  31.4 5.7 %collective-permute-start.10 = (bf16[128,512]{1,0:T(8,128)(2,1)S(1)}, bf16[128,512]{1,0:T(8,128)(2,1)S(1)}, u32[]{:S(2)}, u32[]{:S(2)}) collective-permute-start(bf16[128,512]{1,0:T(8,128)(2,1)S(1)} %fusion.20), channel_id=1, source_target_pairs={{0,4},{4,0},{8,12},{12,8},{1,5},{5,1},{9,13},{13,9},{2,6},{6,2},{1... | collective-permute-start | bytes 393224 | tf_op jit(solution)/shard_map/ppermute | solution.py:40
  36.5 2.0 %collective-permute-start.6 = (bf16[2,256,256]{2,1,0:T(8,128)(2,1)S(1)}, bf16[2,256,256]{2,1,0:T(8,128)(2,1)S(1)}, u32[]{:S(2)}, u32[]{:S(2)}) collective-permute-start(bf16[2,256,256]{2,1,0:T(8,128)(2,1)S(1)} %get-tuple-element.17), channel_id=1, source_target_pairs={{0,1},{1,0},{2,3},{3,2},{4,5},{5,4},{6,7},{7,6},{8,9},{9,8},{10,11... | collective-permute-start | bytes 786440 | tf_op jit(solution)/shard_map/ppermute | solution.py:8
  36.6 2.5 %collective-permute-start.5 = (bf16[2,256,256]{2,1,0:T(8,128)(2,1)S(1)}, bf16[2,256,256]{2,1,0:T(8,128)(2,1)S(1)}, u32[]{:S(2)}, u32[]{:S(2)}) collective-permute-start(bf16[2,256,256]{2,1,0:T(8,128)(2,1)S(1)} %get-tuple-element.15), channel_id=1, source_target_pairs={{0,1},{1,0},{2,3},{3,2},{4,5},{5,4},{6,7},{7,6},{8,9},{9,8},{10,11... | collective-permute-start | bytes 786440 | tf_op jit(solution)/shard_map/ppermute | solution.py:8
  37.1 2.3 %collective-permute-start.7 = (bf16[2,256,256]{2,1,0:T(8,128)(2,1)S(1)}, bf16[2,256,256]{2,1,0:T(8,128)(2,1)S(1)}, u32[]{:S(2)}, u32[]{:S(2)}) collective-permute-start(bf16[2,256,256]{2,1,0:T(8,128)(2,1)S(1)} %get-tuple-element.16), channel_id=1, source_target_pairs={{0,1},{1,0},{2,3},{3,2},{4,5},{5,4},{6,7},{7,6},{8,9},{9,8},{10,11... | collective-permute-start | bytes 786440 | tf_op jit(solution)/shard_map/ppermute | solution.py:8
  37.9 1.7 %collective-permute-start.12 = (bf16[2,256,256]{2,1,0:T(8,128)(2,1)S(1)}, bf16[2,256,256]{2,1,0:T(8,128)(2,1)S(1)}, u32[]{:S(2)}, u32[]{:S(2)}) collective-permute-start(bf16[2,256,256]{2,1,0:T(8,128)(2,1)S(1)} %get-tuple-element.20), channel_id=1, source_target_pairs={{0,1},{1,0},{2,3},{3,2},{4,5},{5,4},{6,7},{7,6},{8,9},{9,8},{10,11... | collective-permute-start | bytes 786440 | tf_op jit(solution)/shard_map/ppermute | solution.py:8
  38.4 1.7 %collective-permute-start.11 = (bf16[2,256,256]{2,1,0:T(8,128)(2,1)S(1)}, bf16[2,256,256]{2,1,0:T(8,128)(2,1)S(1)}, u32[]{:S(2)}, u32[]{:S(2)}) collective-permute-start(bf16[2,256,256]{2,1,0:T(8,128)(2,1)S(1)} %get-tuple-element.18), channel_id=1, source_target_pairs={{0,1},{1,0},{2,3},{3,2},{4,5},{5,4},{6,7},{7,6},{8,9},{9,8},{10,11... | collective-permute-start | bytes 786440 | tf_op jit(solution)/shard_map/ppermute | solution.py:8
  38.5 1.8 %collective-permute-start.13 = (bf16[2,256,256]{2,1,0:T(8,128)(2,1)S(1)}, bf16[2,256,256]{2,1,0:T(8,128)(2,1)S(1)}, u32[]{:S(2)}, u32[]{:S(2)}) collective-permute-start(bf16[2,256,256]{2,1,0:T(8,128)(2,1)S(1)} %get-tuple-element.19), channel_id=1, source_target_pairs={{0,1},{1,0},{2,3},{3,2},{4,5},{5,4},{6,7},{7,6},{8,9},{9,8},{10,11... | collective-permute-start | bytes 786440 | tf_op jit(solution)/shard_map/ppermute | solution.py:8

commit v20 on v17

--- a/solution.py
+++ b/solution.py
@@ -66,7 +66,6 @@
 
     rf_own = lax.dynamic_slice_in_dim(row_factor, h * kh, kh, 1)
     rf_other = lax.dynamic_slice_in_dim(row_factor, (1 - h) * kh, kh, 1)
-    rf_for_partner = _swap(rf_other, "half")
     ctrl_other = _swap(control, "half")
     expanded_all = (
         jnp.einsum("rk,kmlc->lmrc", rf_own, control, preferred_element_type=jnp.float32)
@@ -104,10 +103,10 @@
         summed = jnp.einsum("rk,mrc->kmc", rf_own, projected, preferred_element_type=jnp.float32)
         other = []
         for lo, hi in chunks:
-            proj_other = _swap(projected[lo:hi], "half")
-            other.append(jnp.einsum(
-                "rk,mrc->kmc", rf_for_partner, proj_other, preferred_element_type=jnp.float32
-            ))
+            for_partner = jnp.einsum(
+                "rk,mrc->kmc", rf_other, projected[lo:hi], preferred_element_type=jnp.float32
+            )
+            other.append(_swap(for_partner, "half"))
         summed = summed + jnp.concatenate(other, axis=1)
         outs.append(summed)
     return (control.astype(jnp.float32) + jnp.stack(outs, axis=2)).astype(jnp.bfloat16)

time: 42.9 us -> 43.6 us (1.016)
  waiting for transfers between devices: 13.6 us -> 15.9 us
  local copies, waits for them, and re-layouts: 10.4 us -> 9.44 us
  starting transfers between devices: 12.4 us -> 11.7 us
    ppermute x4, waiting for transfers between devices: 9.75 us -> 11 us  [_reduce_scatter_rows(): recv = lax.ppermute(send, axis, [(i, i ^ d) for i in range(size)])]
    ppermute x8 -> x7, waiting for transfers between devices: 0.02 us -> 1.1 us  [_swap(): return lax.ppermute(x, axis, [(0, 1), (1, 0)])]
    dynamic_slice x1 -> x0, local copies, waits for them, and re-layouts: 0.84 us -> none  [local(): rf_other = lax.dynamic_slice_in_dim(row_factor, (1 - h) * kh, kh, 1)]
    ppermute x4, starting transfers between devices: 9.64 us -> 8.85 us  [_reduce_scatter_rows(): recv = lax.ppermute(send, axis, [(i, i ^ d) for i in range(size)])]
    ppermute x8 -> x7, starting transfers between devices: 2.21 us -> 2.23 us  [_swap(): return lax.ppermute(x, axis, [(0, 1), (1, 0)])]
  transfers between devices with their start and end apart: 14 -> 13, of which waited for: 5 -> 9; matrix products, arithmetic and copies ran while one was open for 27% -> 22% of each run, Pallas kernels for 0% -> 0%
where the time goes in v20:
time: 43.6 us; the launch traced here: 43.4 us
  waiting for transfers between devices  15.9 us (36%)
  starting transfers between devices  11.7 us (27%)
  local copies, waits for them, and re-layouts  9.44 us (22%)
  matrix products  5.49 us (13%)
  other arithmetic  0.63 us (1%)
    ppermute x4, waiting for transfers between devices, _reduce_scatter_rows(): recv = lax.ppermute(send, axis, [(i, i ^ d) for i in range(size)])  11 us
    ppermute x4, starting transfers between devices, _reduce_scatter_rows(): recv = lax.ppermute(send, axis, [(i, i ^ d) for i in range(size)])  8.85 us
    unnamed x12, local copies, waits for them, and re-layouts  6.84 us
    ppermute x2, waiting for transfers between devices, _all_gather_rows(): recv = lax.ppermute(x, axis, [(i, i ^ d) for i in range(size)])  3.84 us
    ppermute x7, starting transfers between devices, _swap(): return lax.ppermute(x, axis, [(0, 1), (1, 0)])  2.23 us
    convert_element_type x1, local copies, waits for them, and re-layouts, local(): (control.astype(jnp.float32) + jnp.stack(outs, axis=2)).astype(jnp.bfloat16)  1.69 us
    dot_general x2, matrix products, local(): jnp.einsum('mrc,nc->mrn', expanded, cf_next, preferred_element_type=jnp.f...  1.32 us
    dot_general x6, matrix products, local(): jnp.einsum('rk,mrc->kmc', rf_other, projected[lo:hi], preferred_element_t...  1.29 us
  transfers between devices with their start and end apart: 13, of which 9 were waited for; matrix products, arithmetic and copies ran while one was open for 22% of the time, Pallas kernels for 0%

profile of v20, /device:TPU:0, one launch (start us, length us, event | category | flops | bytes accessed | tf_op | source)
XLA Modules:
  0.0 43.4 jit_solution(7760429041898406946)
XLA Ops:
  0.0 1.3 %copy.8 = bf16[128,6,2,256]{3,0,2,1:T(8,128)(2,1)S(1)} copy(bf16[128,6,2,256]{3,2,1,0:T(2,128)(2,1)} %param.6) | data formatting | bytes 1572864 | tf_op args[1]
  1.3 0.5 %collective-permute-start = (bf16[128,6,2,256]{3,0,2,1:T(8,128)(2,1)S(1)}, bf16[128,6,2,256]{3,0,2,1:T(8,128)(2,1)S(1)}, u32[]{:S(2)}, u32[]{:S(2)}) collective-permute-start(bf16[128,6,2,256]{3,0,2,1:T(8,128)(2,1)S(1)} %copy.8), channel_id=1, source_target_pairs={{0,1},{1,0},{2,3},{3,2},{4,5},{5,4},{6,7},{7,6},{8,9},{9,8},{10,11... | collective-permute-start | bytes 2359304 | tf_op jit(solution)/shard_map/ppermute | solution.py:8
  1.8 4.3 %copy.45 = bf16[256,6,2,512]{3,0,1,2:T(8,128)(2,1)} copy(bf16[256,6,2,512]{3,2,1,0:T(2,128)(2,1)} %param.5) | data formatting | bytes 6291456 | tf_op args[0]
  6.1 0.6 %fusion.41 = f32[256,6,2,256]{3,0,2,1:T(8,128)S(1)} fusion(bf16[256,256]{1,0:T(8,128)(2,1)S(1)} %copy-done.2, s32[]{:T(128)S(6)} %select_n.57, bf16[128,6,2,256]{3,2,1,0:T(2,128)(2,1)S(1)} %copy-done.1), kind=kOutput, calls=%fused_computation.60 | convolution fusion | flops 201326592 | bytes 3997700 | tf_op jit(solution)/shard_map/rk,kmlc->lmrc/dot_general | solution.py:71
  6.7 0.6 %fusion.11 = bf16[2,6,256,256]{3,2,0,1:T(8,128)(2,1)S(1)} fusion(f32[256,6,2,256]{3,0,2,1:T(8,128)S(1)} %fusion.41, bf16[128,6,2,256]{3,0,2,1:T(8,128)(2,1)S(1)} %collective-permute-done, bf16[256,256]{1,0:T(8,128)(2,1)S(1)} %copy-done.2, s32[]{:T(128)S(6)} %select_n.60), kind=kOutput, calls=%fused_computation.18 | convolution fusion | flops 202899456 | bytes 5570564 | tf_op jit(solution)/shard_map/rk,kmlc->lmrc/dot_general | solution.py:72
  7.3 1.3 %copy-done.3 = bf16[256,6,2,512]{3,0,1,2:T(8,128)(2,1)S(1)} copy-done((bf16[256,6,2,512]{3,0,1,2:T(8,128)(2,1)S(1)}, bf16[256,6,2,512]{3,0,1,2:T(8,128)(2,1)}, u32[]{:S(2)}) %copy-start.3) | copy-done | bytes 3145752
  8.5 0.7 %fusion = f32[256,512]{1,0:T(8,128)S(1)} fusion(bf16[2,6,256,512]{3,2,1,0:T(8,128)(2,1)S(1)} %bitcast.91, bf16[2,6,256,256]{3,2,0,1:T(8,128)(2,1)S(1)} %fusion.11, bf16[512,256]{1,0:T(8,128)(2,1)S(1)} %copy-done), kind=kOutput, calls=%fused_computation.4 | convolution fusion | flops 404881408 | bytes 3145728 | tf_op jit(solution)/shard_map/mrc,nc->mrn/dot_general | solution.py:84
  9.2 2.7 %collective-permute-start.1 = (bf16[128,512]{1,0:T(8,128)(2,1)S(1)}, bf16[128,512]{1,0:T(8,128)(2,1)S(1)}, u32[]{:S(2)}, u32[]{:S(2)}) collective-permute-start(bf16[128,512]{1,0:T(8,128)(2,1)S(1)} %dynamic-slice_convert_fusion.1), channel_id=1, source_target_pairs={{0,4},{4,0},{8,12},{12,8},{1,5},{5,1},{9,13},{13,9},{2,6},{6,2},{1... | collective-permute-start | bytes 393224 | tf_op jit(solution)/shard_map/ppermute | solution.py:23
  11.9 0.8 %fusion.78 = (f32[1,256,512]{2,0,1:T(1,128)S(1)}, f32[1,256,512]{2,0,1:T(1,128)S(1)}) fusion(f32[2,256,512]{2,0,1:T(2,128)S(1)} %bitcast.95), kind=kLoop, calls=%fused_computation.95 | loop fusion | bytes 2097152 | tf_op jit(solution)/shard_map/slice | solution.py:89
  12.8 0.7 %fusion.2 = f32[256,512]{1,0:T(8,128)S(1)} fusion(bf16[2,6,256,512]{3,2,1,0:T(8,128)(2,1)S(1)} %bitcast.92, bf16[2,6,256,256]{3,2,0,1:T(8,128)(2,1)S(1)} %fusion.11, bf16[512,256]{1,0:T(8,128)(2,1)S(1)} %copy-done), kind=kOutput, calls=%fused_computation.6 | convolution fusion | flops 404881408 | bytes 3145728 | tf_op jit(solution)/shard_map/mrc,nc->mrn/dot_general | solution.py:84
  13.6 2.4 %collective-permute-done.1 = bf16[128,512]{1,0:T(8,128)(2,1)S(1)} collective-permute-done((bf16[128,512]{1,0:T(8,128)(2,1)S(1)}, bf16[128,512]{1,0:T(8,128)(2,1)S(1)}, u32[]{:S(2)}, u32[]{:S(2)}) %collective-permute-start.1) | collective-permute-done | bytes 131104 | tf_op jit(solution)/shard_map/ppermute | solution.py:23
  16.1 2.8 %collective-permute-start.2 = (bf16[128,512]{1,0:T(8,128)(2,1)S(1)}, bf16[128,512]{1,0:T(8,128)(2,1)S(1)}, u32[]{:S(2)}, u32[]{:S(2)}) collective-permute-start(bf16[128,512]{1,0:T(8,128)(2,1)S(1)} %fusion.38), channel_id=1, source_target_pairs={{0,8},{4,12},{8,0},{12,4},{1,9},{5,13},{9,1},{13,5},{2,10},{6,14},... | collective-permute-start | bytes 393224 | tf_op jit(solution)/shard_map/ppermute | solution.py:30
  19.1 3.2 %collective-permute-start.8 = (bf16[128,512]{1,0:T(8,128)(2,1)S(1)}, bf16[128,512]{1,0:T(8,128)(2,1)S(1)}, u32[]{:S(2)}, u32[]{:S(2)}) collective-permute-start(bf16[128,512]{1,0:T(8,128)(2,1)S(1)} %fusion.39), channel_id=1, source_target_pairs={{0,8},{4,12},{8,0},{12,4},{1,9},{5,13},{9,1},{13,5},{2,10},{6,14},... | collective-permute-start | bytes 393224 | tf_op jit(solution)/shard_map/ppermute | solution.py:30
  22.4 6.6 %collective-permute-done.2 = bf16[128,512]{1,0:T(8,128)(2,1)S(1)} collective-permute-done((bf16[128,512]{1,0:T(8,128)(2,1)S(1)}, bf16[128,512]{1,0:T(8,128)(2,1)S(1)}, u32[]{:S(2)}, u32[]{:S(2)}) %collective-permute-start.2) | collective-permute-done | bytes 131104 | tf_op jit(solution)/shard_map/ppermute | solution.py:30
  29.2 1.7 %collective-permute-done.8 = bf16[128,512]{1,0:T(8,128)(2,1)S(1)} collective-permute-done((bf16[128,512]{1,0:T(8,128)(2,1)S(1)}, bf16[128,512]{1,0:T(8,128)(2,1)S(1)}, u32[]{:S(2)}, u32[]{:S(2)}) %collective-permute-start.8) | collective-permute-done | bytes 131104 | tf_op jit(solution)/shard_map/ppermute | solution.py:30
  30.9 0.6 %collective-permute-start.9 = (bf16[128,512]{1,0:T(8,128)(2,1)S(1)}, bf16[128,512]{1,0:T(8,128)(2,1)S(1)}, u32[]{:S(2)}, u32[]{:S(2)}) collective-permute-start(bf16[128,512]{1,0:T(8,128)(2,1)S(1)} %fusion.32), channel_id=1, source_target_pairs={{0,4},{4,0},{8,12},{12,8},{1,5},{5,1},{9,13},{13,9},{2,6},{6,2},{1... | collective-permute-start | bytes 393224 | tf_op jit(solution)/shard_map/ppermute | solution.py:40
  31.5 3.8 %collective-permute-done.3 = bf16[128,512]{1,0:T(8,128)(2,1)S(1)} collective-permute-done((bf16[128,512]{1,0:T(8,128)(2,1)S(1)}, bf16[128,512]{1,0:T(8,128)(2,1)S(1)}, u32[]{:S(2)}, u32[]{:S(2)}) %collective-permute-start.3) | collective-permute-done | bytes 131104 | tf_op jit(solution)/shard_map/ppermute | solution.py:40
  35.4 0.6 %fusion.12 = bf16[6,256,256]{2,1,0:T(8,128)(2,1)S(1)} fusion(f32[256,512]{1,0:T(8,128)S(1)} %maximum_convert_fusion, bf16[2,6,256,512]{3,2,1,0:T(8,128)(2,1)S(1)} %bitcast.93, bf16[512,256]{1,0:T(8,128)(2,1)S(1)} %copy-done), kind=kOutput, calls=%fused_computation.19 | convolution fusion | flops 405405696 | bytes 3145728 | tf_op jit(solution)/shard_map/mrn,nc->mrc/dot_general | solution.py:97
  36.9 0.6 %fusion.15 = bf16[6,256,256]{2,1,0:T(8,128)(2,1)S(1)} fusion(f32[256,512]{1,0:T(8,128)S(1)} %maximum_convert_fusion.1, bf16[2,6,256,512]{3,2,1,0:T(8,128)(2,1)S(1)} %bitcast.94, bf16[512,256]{1,0:T(8,128)(2,1)S(1)} %copy-done), kind=kOutput, calls=%fused_computation.20 | convolution fusion | flops 405405696 | bytes 3145728 | tf_op jit(solution)/shard_map/mrn,nc->mrc/dot_general | solution.py:97
  37.9 0.6 %collective-permute-start.5 = (f32[128,2,256]{2,0,1:T(8,128)S(1)}, f32[128,2,256]{2,0,1:T(8,128)S(1)}, u32[]{:S(2)}, u32[]{:S(2)}) collective-permute-start(f32[128,2,256]{2,0,1:T(8,128)S(1)} %fusion.28), channel_id=1, source_target_pairs={{0,1},{1,0},{2,3},{3,2},{4,5},{5,4},{6,7},{7,6},{8,9},{9,8},{10,11... | collective-permute-start | bytes 786440 | tf_op jit(solution)/shard_map/ppermute | solution.py:8
  38.5 0.4 collective-permute-start.10
  39.3 0.4 %collective-permute-start.12 = (f32[128,2,256]{2,0,1:T(8,128)S(1)}, f32[128,2,256]{2,0,1:T(8,128)S(1)}, u32[]{:S(2)}, u32[]{:S(2)}) collective-permute-start(f32[128,2,256]{2,0,1:T(8,128)S(1)} %fusion.20), channel_id=1, source_target_pairs={{0,1},{1,0},{2,3},{3,2},{4,5},{5,4},{6,7},{7,6},{8,9},{9,8},{10,11... | collective-permute-start | bytes 786440 | tf_op jit(solution)/shard_map/ppermute | solution.py:8
  40.4 0.4 collective-permute-done.11
  41.7 1.7 %copy.18 = bf16[128,6,2,256]{3,2,1,0:T(2,128)(2,1)} copy(bf16[128,6,2,256]{3,0,1,2:T(8,128)(2,1)S(1)} %fusion.8) | data formatting | bytes 1572864 | tf_op jit(solution)/shard_map/convert_element_type | solution.py:112
  (43 shorter events, 3.9 us)
Async XLA Ops:
  0.0 7.3 %copy-start = (bf16[512,256]{1,0:T(8,128)(2,1)S(1)}, bf16[512,256]{1,0:T(8,128)(2,1)}, u32[]{:S(2)}) copy-start(bf16[512,256]{1,0:T(8,128)(2,1)} %param.9) | copy-start | bytes 786436
  1.3 5.4 %collective-permute-start = (bf16[128,6,2,256]{3,0,2,1:T(8,128)(2,1)S(1)}, bf16[128,6,2,256]{3,0,2,1:T(8,128)(2,1)S(1)}, u32[]{:S(2)}, u32[]{:S(2)}) collective-permute-start(bf16[128,6,2,256]{3,0,2,1:T(8,128)(2,1)S(1)} %copy.8), channel_id=1, source_target_pairs={{0,1},{1,0},{2,3},{3,2},{4,5},{5,4},{6,7},{7,6},{8,9},{9,8},{10,11... | collective-permute-start | bytes 2359304 | tf_op jit(solution)/shard_map/ppermute | solution.py:8
  1.8 4.3 %copy-start.1 = (bf16[128,6,2,256]{3,2,1,0:T(2,128)(2,1)S(1)}, bf16[128,6,2,256]{3,2,1,0:T(2,128)(2,1)}, u32[]{:S(2)}) copy-start(bf16[128,6,2,256]{3,2,1,0:T(2,128)(2,1)} %param.6) | copy-start | bytes 2359300
  1.8 4.3 %copy-start.2 = (bf16[256,256]{1,0:T(8,128)(2,1)S(1)}, bf16[256,256]{1,0:T(8,128)(2,1)}, u32[]{:S(2)}) copy-start(bf16[256,256]{1,0:T(8,128)(2,1)} %param.8) | copy-start | bytes 393220
  6.7 1.9 %copy-start.3 = (bf16[256,6,2,512]{3,0,1,2:T(8,128)(2,1)S(1)}, bf16[256,6,2,512]{3,0,1,2:T(8,128)(2,1)}, u32[]{:S(2)}) copy-start(bf16[256,6,2,512]{3,0,1,2:T(8,128)(2,1)} %copy.45) | copy-start | bytes 9437188
  7.3 4.7 %copy-start.4 = (f32[256,2,512]{2,1,0:T(2,128)S(1)}, f32[256,2,512]{2,1,0:T(2,128)}, u32[]{:S(2)}) copy-start(f32[256,2,512]{2,1,0:T(2,128)} %param.7) | copy-start | bytes 3145732
  9.2 6.8 %collective-permute-start.1 = (bf16[128,512]{1,0:T(8,128)(2,1)S(1)}, bf16[128,512]{1,0:T(8,128)(2,1)S(1)}, u32[]{:S(2)}, u32[]{:S(2)}) collective-permute-start(bf16[128,512]{1,0:T(8,128)(2,1)S(1)} %dynamic-slice_convert_fusion.1), channel_id=1, source_target_pairs={{0,4},{4,0},{8,12},{12,8},{1,5},{5,1},{9,13},{13,9},{2,6},{6,2},{1... | collective-permute-start | bytes 393224 | tf_op jit(solution)/shard_map/ppermute | solution.py:23
  13.5 5.6 %collective-permute-start.7 = (bf16[128,512]{1,0:T(8,128)(2,1)S(1)}, bf16[128,512]{1,0:T(8,128)(2,1)S(1)}, u32[]{:S(2)}, u32[]{:S(2)}) collective-permute-start(bf16[128,512]{1,0:T(8,128)(2,1)S(1)} %dynamic-slice_convert_fusion), channel_id=1, source_target_pairs={{0,4},{4,0},{8,12},{12,8},{1,5},{5,1},{9,13},{13,9},{2,6},{6,2},{1... | collective-permute-start | bytes 393224 | tf_op jit(solution)/shard_map/ppermute | solution.py:23
  16.1 12.9 %collective-permute-start.2 = (bf16[128,512]{1,0:T(8,128)(2,1)S(1)}, bf16[128,512]{1,0:T(8,128)(2,1)S(1)}, u32[]{:S(2)}, u32[]{:S(2)}) collective-permute-start(bf16[128,512]{1,0:T(8,128)(2,1)S(1)} %fusion.38), channel_id=1, source_target_pairs={{0,8},{4,12},{8,0},{12,4},{1,9},{5,13},{9,1},{13,5},{2,10},{6,14},... | collective-permute-start | bytes 393224 | tf_op jit(solution)/shard_map/ppermute | solution.py:30
  19.1 11.7 %collective-permute-start.8 = (bf16[128,512]{1,0:T(8,128)(2,1)S(1)}, bf16[128,512]{1,0:T(8,128)(2,1)S(1)}, u32[]{:S(2)}, u32[]{:S(2)}) collective-permute-start(bf16[128,512]{1,0:T(8,128)(2,1)S(1)} %fusion.39), channel_id=1, source_target_pairs={{0,8},{4,12},{8,0},{12,4},{1,9},{5,13},{9,1},{13,5},{2,10},{6,14},... | collective-permute-start | bytes 393224 | tf_op jit(solution)/shard_map/ppermute | solution.py:30
  29.1 6.3 %collective-permute-start.3 = (bf16[128,512]{1,0:T(8,128)(2,1)S(1)}, bf16[128,512]{1,0:T(8,128)(2,1)S(1)}, u32[]{:S(2)}, u32[]{:S(2)}) collective-permute-start(bf16[128,512]{1,0:T(8,128)(2,1)S(1)} %fusion.33), channel_id=1, source_target_pairs={{0,4},{4,0},{8,12},{12,8},{1,5},{5,1},{9,13},{13,9},{2,6},{6,2},{1... | collective-permute-start | bytes 393224 | tf_op jit(solution)/shard_map/ppermute | solution.py:40
  30.9 5.8 %collective-permute-start.9 = (bf16[128,512]{1,0:T(8,128)(2,1)S(1)}, bf16[128,512]{1,0:T(8,128)(2,1)S(1)}, u32[]{:S(2)}, u32[]{:S(2)}) collective-permute-start(bf16[128,512]{1,0:T(8,128)(2,1)S(1)} %fusion.32), channel_id=1, source_target_pairs={{0,4},{4,0},{8,12},{12,8},{1,5},{5,1},{9,13},{13,9},{2,6},{6,2},{1... | collective-permute-start | bytes 393224 | tf_op jit(solution)/shard_map/ppermute | solution.py:40
  36.5 2.9 %collective-permute-start.4 = (f32[128,2,256]{2,0,1:T(8,128)S(1)}, f32[128,2,256]{2,0,1:T(8,128)S(1)}, u32[]{:S(2)}, u32[]{:S(2)}) collective-permute-start(f32[128,2,256]{2,0,1:T(8,128)S(1)} %fusion.30), channel_id=1, source_target_pairs={{0,1},{1,0},{2,3},{3,2},{4,5},{5,4},{6,7},{7,6},{8,9},{9,8},{10,11... | collective-permute-start | bytes 786440 | tf_op jit(solution)/shard_map/ppermute | solution.py:8
  37.9 1.9 %collective-permute-start.5 = (f32[128,2,256]{2,0,1:T(8,128)S(1)}, f32[128,2,256]{2,0,1:T(8,128)S(1)}, u32[]{:S(2)}, u32[]{:S(2)}) collective-permute-start(f32[128,2,256]{2,0,1:T(8,128)S(1)} %fusion.28), channel_id=1, source_target_pairs={{0,1},{1,0},{2,3},{3,2},{4,5},{5,4},{6,7},{7,6},{8,9},{9,8},{10,11... | collective-permute-start | bytes 786440 | tf_op jit(solution)/shard_map/ppermute | solution.py:8
  38.5 1.5 %collective-permute-start.6 = (f32[128,2,256]{2,0,1:T(8,128)S(1)}, f32[128,2,256]{2,0,1:T(8,128)S(1)}, u32[]{:S(2)}, u32[]{:S(2)}) collective-permute-start(f32[128,2,256]{2,0,1:T(8,128)S(1)} %fusion.26), channel_id=1, source_target_pairs={{0,1},{1,0},{2,3},{3,2},{4,5},{5,4},{6,7},{7,6},{8,9},{9,8},{10,11... | collective-permute-start | bytes 786440 | tf_op jit(solution)/shard_map/ppermute | solution.py:8
  38.5 1.8 %collective-permute-start.10 = (f32[128,2,256]{2,0,1:T(8,128)S(1)}, f32[128,2,256]{2,0,1:T(8,128)S(1)}, u32[]{:S(2)}, u32[]{:S(2)}) collective-permute-start(f32[128,2,256]{2,0,1:T(8,128)S(1)} %fusion.24), channel_id=1, source_target_pairs={{0,1},{1,0},{2,3},{3,2},{4,5},{5,4},{6,7},{7,6},{8,9},{9,8},{10,11... | collective-permute-start | bytes 786440 | tf_op jit(solution)/shard_map/ppermute | solution.py:8
  39.2 1.6 %collective-permute-start.11 = (f32[128,2,256]{2,0,1:T(8,128)S(1)}, f32[128,2,256]{2,0,1:T(8,128)S(1)}, u32[]{:S(2)}, u32[]{:S(2)}) collective-permute-start(f32[128,2,256]{2,0,1:T(8,128)S(1)} %fusion.22), channel_id=1, source_target_pairs={{0,1},{1,0},{2,3},{3,2},{4,5},{5,4},{6,7},{7,6},{8,9},{9,8},{10,11... | collective-permute-start | bytes 786440 | tf_op jit(solution)/shard_map/ppermute | solution.py:8
  39.3 1.8 %collective-permute-start.12 = (f32[128,2,256]{2,0,1:T(8,128)S(1)}, f32[128,2,256]{2,0,1:T(8,128)S(1)}, u32[]{:S(2)}, u32[]{:S(2)}) collective-permute-start(f32[128,2,256]{2,0,1:T(8,128)S(1)} %fusion.20), channel_id=1, source_target_pairs={{0,1},{1,0},{2,3},{3,2},{4,5},{5,4},{6,7},{7,6},{8,9},{9,8},{10,11... | collective-permute-start | bytes 786440 | tf_op jit(solution)/shard_map/ppermute | solution.py:8

commit v21 on v17

--- a/solution.py
+++ b/solution.py
@@ -66,7 +66,7 @@
 
     rf_own = lax.dynamic_slice_in_dim(row_factor, h * kh, kh, 1)
     rf_other = lax.dynamic_slice_in_dim(row_factor, (1 - h) * kh, kh, 1)
-    rf_for_partner = _swap(rf_other, "half")
+    rf_partner = _swap(row_factor, "half")
     ctrl_other = _swap(control, "half")
     expanded_all = (
         jnp.einsum("rk,kmlc->lmrc", rf_own, control, preferred_element_type=jnp.float32)
@@ -101,6 +101,7 @@
         n_m = projected.shape[0]
         cuts = [i * n_m // 3 for i in range(4)]
         chunks = [(lo, hi) for lo, hi in zip(cuts[:-1], cuts[1:]) if lo < hi]
+        rf_for_partner = lax.dynamic_slice_in_dim(rf_partner, h * kh, kh, 1)
         summed = jnp.einsum("rk,mrc->kmc", rf_own, projected, preferred_element_type=jnp.float32)
         other = []
         for lo, hi in chunks:

time: 42.9 us -> 43.2 us (level)
    unnamed x12 -> x13, local copies, waits for them, and re-layouts: 6.86 us -> 7.85 us
    dynamic_slice x1 -> x0, local copies, waits for them, and re-layouts: 0.84 us -> none  [local(): rf_other = lax.dynamic_slice_in_dim(row_factor, (1 - h) * kh, kh, 1)]
  transfers between devices with their start and end apart: 14 -> 14, of which waited for: 5 -> 6; matrix products, arithmetic and copies ran while one was open for 27% -> 27% of each run, Pallas kernels for 0% -> 0%
where the time goes in v21:
time: 43.2 us; the launch traced here: 43 us
  waiting for transfers between devices  13.8 us (32%)
  starting transfers between devices  12.5 us (29%)
  local copies, waits for them, and re-layouts  10.6 us (25%)
  matrix products  5.32 us (12%)
  other arithmetic  0.62 us (1%)
    ppermute x4, waiting for transfers between devices, _reduce_scatter_rows(): recv = lax.ppermute(send, axis, [(i, i ^ d) for i in range(size)])  9.84 us
    ppermute x4, starting transfers between devices, _reduce_scatter_rows(): recv = lax.ppermute(send, axis, [(i, i ^ d) for i in range(size)])  9.61 us
    unnamed x13, local copies, waits for them, and re-layouts  7.85 us
    ppermute x2, waiting for transfers between devices, _all_gather_rows(): recv = lax.ppermute(x, axis, [(i, i ^ d) for i in range(size)])  3.81 us
    ppermute x8, starting transfers between devices, _swap(): return lax.ppermute(x, axis, [(0, 1), (1, 0)])  2.27 us
    convert_element_type x1, local copies, waits for them, and re-layouts, local(): (control.astype(jnp.float32) + jnp.stack(outs, axis=2)).astype(jnp.bfloat16)  1.69 us
    dot_general x2, matrix products, local(): jnp.einsum('mrc,nc->mrn', expanded, cf_next, preferred_element_type=jnp.f...  1.32 us
    dot_general x2, matrix products, local(): jnp.einsum('mrn,nc->mrc', scaled, col_factor, preferred_element_type=jnp....  1.17 us
  transfers between devices with their start and end apart: 14, of which 6 were waited for; matrix products, arithmetic and copies ran while one was open for 27% of the time, Pallas kernels for 0%

profile of v21, /device:TPU:0, one launch (start us, length us, event | category | flops | bytes accessed | tf_op | source)
XLA Modules:
  0.0 43.0 jit_solution(693171768802472499)
XLA Ops:
  0.0 1.3 %copy.8 = bf16[128,6,2,256]{3,0,2,1:T(8,128)(2,1)S(1)} copy(bf16[128,6,2,256]{3,2,1,0:T(2,128)(2,1)} %param.6) | data formatting | bytes 1572864 | tf_op args[1]
  1.3 0.5 %collective-permute-start = (bf16[128,6,2,256]{3,0,2,1:T(8,128)(2,1)S(1)}, bf16[128,6,2,256]{3,0,2,1:T(8,128)(2,1)S(1)}, u32[]{:S(2)}, u32[]{:S(2)}) collective-permute-start(bf16[128,6,2,256]{3,0,2,1:T(8,128)(2,1)S(1)} %copy.8), channel_id=1, source_target_pairs={{0,1},{1,0},{2,3},{3,2},{4,5},{5,4},{6,7},{7,6},{8,9},{9,8},{10,11... | collective-permute-start | bytes 2359304 | tf_op jit(solution)/shard_map/ppermute | solution.py:8
  1.8 1.0 %copy.11 = bf16[256,256]{0,1:T(8,128)(2,1)S(1)} copy(bf16[256,256]{1,0:T(8,128)(2,1)} %param.8) | data formatting | bytes 262144 | tf_op args[3]
  3.0 4.3 %copy.28 = bf16[256,6,2,512]{3,0,1,2:T(8,128)(2,1)} copy(bf16[256,6,2,512]{3,2,1,0:T(2,128)(2,1)} %param.5) | data formatting | bytes 6291456 | tf_op args[0]
  7.2 0.6 %fusion.29 = f32[256,6,2,256]{3,0,2,1:T(8,128)S(1)} fusion(bf16[256,256]{1,0:T(8,128)(2,1)S(1)} %copy-done.3, s32[]{:T(128)S(6)} %select_n.59, bf16[128,6,2,256]{3,2,1,0:T(2,128)(2,1)S(1)} %copy-done.1), kind=kOutput, calls=%fused_computation.48 | convolution fusion | flops 201326592 | bytes 3997700 | tf_op jit(solution)/shard_map/rk,kmlc->lmrc/dot_general | solution.py:72
  7.8 0.6 %fusion.11 = bf16[2,6,256,256]{3,2,0,1:T(8,128)(2,1)S(1)} fusion(f32[256,6,2,256]{3,0,2,1:T(8,128)S(1)} %fusion.29, bf16[128,6,2,256]{3,0,2,1:T(8,128)(2,1)S(1)} %collective-permute-done, bf16[256,256]{1,0:T(8,128)(2,1)S(1)} %copy-done.3, s32[]{:T(128)S(6)} %select_n.62), kind=kOutput, calls=%fused_computation.18 | convolution fusion | flops 202899456 | bytes 5570564 | tf_op jit(solution)/shard_map/rk,kmlc->lmrc/dot_general | solution.py:73
  8.4 1.3 %copy-done.2 = bf16[256,6,2,512]{3,0,1,2:T(8,128)(2,1)S(1)} copy-done((bf16[256,6,2,512]{3,0,1,2:T(8,128)(2,1)S(1)}, bf16[256,6,2,512]{3,0,1,2:T(8,128)(2,1)}, u32[]{:S(2)}) %copy-start.2) | copy-done | bytes 3145752
  9.7 0.7 %fusion = f32[256,512]{1,0:T(8,128)S(1)} fusion(bf16[2,6,256,512]{3,2,1,0:T(8,128)(2,1)S(1)} %bitcast.92, bf16[2,6,256,256]{3,2,0,1:T(8,128)(2,1)S(1)} %fusion.11, bf16[512,256]{1,0:T(8,128)(2,1)S(1)} %copy-done), kind=kOutput, calls=%fused_computation.4 | convolution fusion | flops 404881408 | bytes 3145728 | tf_op jit(solution)/shard_map/mrc,nc->mrn/dot_general | solution.py:85
  10.4 3.1 %collective-permute-start.1 = (bf16[128,512]{1,0:T(8,128)(2,1)S(1)}, bf16[128,512]{1,0:T(8,128)(2,1)S(1)}, u32[]{:S(2)}, u32[]{:S(2)}) collective-permute-start(bf16[128,512]{1,0:T(8,128)(2,1)S(1)} %dynamic-slice_convert_fusion.1), channel_id=1, source_target_pairs={{0,4},{4,0},{8,12},{12,8},{1,5},{5,1},{9,13},{13,9},{2,6},{6,2},{1... | collective-permute-start | bytes 393224 | tf_op jit(solution)/shard_map/ppermute | solution.py:23
  13.5 0.8 %fusion.72 = (f32[1,256,512]{2,0,1:T(1,128)S(1)}, f32[1,256,512]{2,0,1:T(1,128)S(1)}) fusion(f32[2,256,512]{2,0,1:T(2,128)S(1)} %bitcast.96), kind=kLoop, calls=%fused_computation.89 | loop fusion | bytes 2097152 | tf_op jit(solution)/shard_map/slice | solution.py:90
  14.3 0.7 %fusion.2 = f32[256,512]{1,0:T(8,128)S(1)} fusion(bf16[2,6,256,512]{3,2,1,0:T(8,128)(2,1)S(1)} %bitcast.93, bf16[2,6,256,256]{3,2,0,1:T(8,128)(2,1)S(1)} %fusion.11, bf16[512,256]{1,0:T(8,128)(2,1)S(1)} %copy-done), kind=kOutput, calls=%fused_computation.6 | convolution fusion | flops 404881408 | bytes 3145728 | tf_op jit(solution)/shard_map/mrc,nc->mrn/dot_general | solution.py:85
  15.2 2.2 %collective-permute-done.1 = bf16[128,512]{1,0:T(8,128)(2,1)S(1)} collective-permute-done((bf16[128,512]{1,0:T(8,128)(2,1)S(1)}, bf16[128,512]{1,0:T(8,128)(2,1)S(1)}, u32[]{:S(2)}, u32[]{:S(2)}) %collective-permute-start.1) | collective-permute-done | bytes 131104 | tf_op jit(solution)/shard_map/ppermute | solution.py:23
  17.4 2.7 %collective-permute-start.2 = (bf16[128,512]{1,0:T(8,128)(2,1)S(1)}, bf16[128,512]{1,0:T(8,128)(2,1)S(1)}, u32[]{:S(2)}, u32[]{:S(2)}) collective-permute-start(bf16[128,512]{1,0:T(8,128)(2,1)S(1)} %fusion.26), channel_id=1, source_target_pairs={{0,8},{4,12},{8,0},{12,4},{1,9},{5,13},{9,1},{13,5},{2,10},{6,14},... | collective-permute-start | bytes 393224 | tf_op jit(solution)/shard_map/ppermute | solution.py:30
  20.3 3.8 %collective-permute-start.9 = (bf16[128,512]{1,0:T(8,128)(2,1)S(1)}, bf16[128,512]{1,0:T(8,128)(2,1)S(1)}, u32[]{:S(2)}, u32[]{:S(2)}) collective-permute-start(bf16[128,512]{1,0:T(8,128)(2,1)S(1)} %fusion.27), channel_id=1, source_target_pairs={{0,8},{4,12},{8,0},{12,4},{1,9},{5,13},{9,1},{13,5},{2,10},{6,14},... | collective-permute-start | bytes 393224 | tf_op jit(solution)/shard_map/ppermute | solution.py:30
  24.0 5.9 %collective-permute-done.2 = bf16[128,512]{1,0:T(8,128)(2,1)S(1)} collective-permute-done((bf16[128,512]{1,0:T(8,128)(2,1)S(1)}, bf16[128,512]{1,0:T(8,128)(2,1)S(1)}, u32[]{:S(2)}, u32[]{:S(2)}) %collective-permute-start.2) | collective-permute-done | bytes 131104 | tf_op jit(solution)/shard_map/ppermute | solution.py:30
  30.1 1.6 %collective-permute-done.9 = bf16[128,512]{1,0:T(8,128)(2,1)S(1)} collective-permute-done((bf16[128,512]{1,0:T(8,128)(2,1)S(1)}, bf16[128,512]{1,0:T(8,128)(2,1)S(1)}, u32[]{:S(2)}, u32[]{:S(2)}) %collective-permute-start.9) | collective-permute-done | bytes 131104 | tf_op jit(solution)/shard_map/ppermute | solution.py:30
  31.7 0.5 %collective-permute-start.10 = (bf16[128,512]{1,0:T(8,128)(2,1)S(1)}, bf16[128,512]{1,0:T(8,128)(2,1)S(1)}, u32[]{:S(2)}, u32[]{:S(2)}) collective-permute-start(bf16[128,512]{1,0:T(8,128)(2,1)S(1)} %fusion.20), channel_id=1, source_target_pairs={{0,4},{4,0},{8,12},{12,8},{1,5},{5,1},{9,13},{13,9},{2,6},{6,2},{1... | collective-permute-start | bytes 393224 | tf_op jit(solution)/shard_map/ppermute | solution.py:40
  32.2 3.8 %collective-permute-done.3 = bf16[128,512]{1,0:T(8,128)(2,1)S(1)} collective-permute-done((bf16[128,512]{1,0:T(8,128)(2,1)S(1)}, bf16[128,512]{1,0:T(8,128)(2,1)S(1)}, u32[]{:S(2)}, u32[]{:S(2)}) %collective-permute-start.3) | collective-permute-done | bytes 131104 | tf_op jit(solution)/shard_map/ppermute | solution.py:40
  36.1 0.6 %fusion.12 = bf16[6,256,256]{2,1,0:T(8,128)(2,1)S(1)} fusion(f32[256,512]{1,0:T(8,128)S(1)} %maximum_convert_fusion, bf16[2,6,256,512]{3,2,1,0:T(8,128)(2,1)S(1)} %bitcast.94, bf16[512,256]{1,0:T(8,128)(2,1)S(1)} %copy-done), kind=kOutput, calls=%fused_computation.19 | convolution fusion | flops 405405696 | bytes 3145728 | tf_op jit(solution)/shard_map/mrn,nc->mrc/dot_general | solution.py:98
  36.8 0.5 %collective-permute-start.5 = (bf16[2,256,256]{2,1,0:T(8,128)(2,1)S(1)}, bf16[2,256,256]{2,1,0:T(8,128)(2,1)S(1)}, u32[]{:S(2)}, u32[]{:S(2)}) collective-permute-start(bf16[2,256,256]{2,1,0:T(8,128)(2,1)S(1)} %get-tuple-element.17), channel_id=1, source_target_pairs={{0,1},{1,0},{2,3},{3,2},{4,5},{5,4},{6,7},{7,6},{8,9},{9,8},{10,11... | collective-permute-start | bytes 786440 | tf_op jit(solution)/shard_map/ppermute | solution.py:8
  37.5 0.6 %fusion.15 = bf16[6,256,256]{2,1,0:T(8,128)(2,1)S(1)} fusion(f32[256,512]{1,0:T(8,128)S(1)} %maximum_convert_fusion.1, bf16[2,6,256,512]{3,2,1,0:T(8,128)(2,1)S(1)} %bitcast.95, bf16[512,256]{1,0:T(8,128)(2,1)S(1)} %copy-done), kind=kOutput, calls=%fused_computation.20 | convolution fusion | flops 405405696 | bytes 3145728 | tf_op jit(solution)/shard_map/mrn,nc->mrc/dot_general | solution.py:98
  38.2 0.5 %collective-permute-start.12 = (bf16[2,256,256]{2,1,0:T(8,128)(2,1)S(1)}, bf16[2,256,256]{2,1,0:T(8,128)(2,1)S(1)}, u32[]{:S(2)}, u32[]{:S(2)}) collective-permute-start(bf16[2,256,256]{2,1,0:T(8,128)(2,1)S(1)} %get-tuple-element.22), channel_id=1, source_target_pairs={{0,1},{1,0},{2,3},{3,2},{4,5},{5,4},{6,7},{7,6},{8,9},{9,8},{10,11... | collective-permute-start | bytes 786440 | tf_op jit(solution)/shard_map/ppermute | solution.py:8
  38.8 0.4 collective-permute-start.13
  41.3 1.7 %copy.13 = bf16[128,6,2,256]{3,2,1,0:T(2,128)(2,1)} copy(bf16[128,6,2,256]{3,0,1,2:T(8,128)(2,1)S(1)} %fusion.8) | data formatting | bytes 1572864 | tf_op jit(solution)/shard_map/convert_element_type | solution.py:114
  (48 shorter events, 3.4 us)
Async XLA Ops:
  0.0 8.4 %copy-start = (bf16[512,256]{1,0:T(8,128)(2,1)S(1)}, bf16[512,256]{1,0:T(8,128)(2,1)}, u32[]{:S(2)}) copy-start(bf16[512,256]{1,0:T(8,128)(2,1)} %param.9) | copy-start | bytes 786436
  1.3 6.5 %collective-permute-start = (bf16[128,6,2,256]{3,0,2,1:T(8,128)(2,1)S(1)}, bf16[128,6,2,256]{3,0,2,1:T(8,128)(2,1)S(1)}, u32[]{:S(2)}, u32[]{:S(2)}) collective-permute-start(bf16[128,6,2,256]{3,0,2,1:T(8,128)(2,1)S(1)} %copy.8), channel_id=1, source_target_pairs={{0,1},{1,0},{2,3},{3,2},{4,5},{5,4},{6,7},{7,6},{8,9},{9,8},{10,11... | collective-permute-start | bytes 2359304 | tf_op jit(solution)/shard_map/ppermute | solution.py:8
  2.8 35.8 %collective-permute-start.4 = (bf16[256,256]{0,1:T(8,128)(2,1)S(1)}, bf16[256,256]{0,1:T(8,128)(2,1)S(1)}, u32[]{:S(2)}, u32[]{:S(2)}) collective-permute-start(bf16[256,256]{0,1:T(8,128)(2,1)S(1)} %copy.11), channel_id=1, source_target_pairs={{0,1},{1,0},{2,3},{3,2},{4,5},{5,4},{6,7},{7,6},{8,9},{9,8},{10,11... | collective-permute-start | bytes 393224 | tf_op jit(solution)/shard_map/ppermute | solution.py:8
  2.9 4.3 %copy-start.1 = (bf16[128,6,2,256]{3,2,1,0:T(2,128)(2,1)S(1)}, bf16[128,6,2,256]{3,2,1,0:T(2,128)(2,1)}, u32[]{:S(2)}) copy-start(bf16[128,6,2,256]{3,2,1,0:T(2,128)(2,1)} %param.6) | copy-start | bytes 2359300
  2.9 4.3 %copy-start.3 = (bf16[256,256]{1,0:T(8,128)(2,1)S(1)}, bf16[256,256]{1,0:T(8,128)(2,1)}, u32[]{:S(2)}) copy-start(bf16[256,256]{1,0:T(8,128)(2,1)} %param.8) | copy-start | bytes 393220
  7.8 1.9 %copy-start.2 = (bf16[256,6,2,512]{3,0,1,2:T(8,128)(2,1)S(1)}, bf16[256,6,2,512]{3,0,1,2:T(8,128)(2,1)}, u32[]{:S(2)}) copy-start(bf16[256,6,2,512]{3,0,1,2:T(8,128)(2,1)} %copy.28) | copy-start | bytes 9437188
  8.4 5.1 %copy-start.4 = (f32[256,2,512]{2,1,0:T(2,128)S(1)}, f32[256,2,512]{2,1,0:T(2,128)}, u32[]{:S(2)}) copy-start(f32[256,2,512]{2,1,0:T(2,128)} %param.7) | copy-start | bytes 3145732
  10.4 7.0 %collective-permute-start.1 = (bf16[128,512]{1,0:T(8,128)(2,1)S(1)}, bf16[128,512]{1,0:T(8,128)(2,1)S(1)}, u32[]{:S(2)}, u32[]{:S(2)}) collective-permute-start(bf16[128,512]{1,0:T(8,128)(2,1)S(1)} %dynamic-slice_convert_fusion.1), channel_id=1, source_target_pairs={{0,4},{4,0},{8,12},{12,8},{1,5},{5,1},{9,13},{13,9},{2,6},{6,2},{1... | collective-permute-start | bytes 393224 | tf_op jit(solution)/shard_map/ppermute | solution.py:23
  15.0 5.2 %collective-permute-start.8 = (bf16[128,512]{1,0:T(8,128)(2,1)S(1)}, bf16[128,512]{1,0:T(8,128)(2,1)S(1)}, u32[]{:S(2)}, u32[]{:S(2)}) collective-permute-start(bf16[128,512]{1,0:T(8,128)(2,1)S(1)} %dynamic-slice_convert_fusion), channel_id=1, source_target_pairs={{0,4},{4,0},{8,12},{12,8},{1,5},{5,1},{9,13},{13,9},{2,6},{6,2},{1... | collective-permute-start | bytes 393224 | tf_op jit(solution)/shard_map/ppermute | solution.py:23
  17.4 12.5 %collective-permute-start.2 = (bf16[128,512]{1,0:T(8,128)(2,1)S(1)}, bf16[128,512]{1,0:T(8,128)(2,1)S(1)}, u32[]{:S(2)}, u32[]{:S(2)}) collective-permute-start(bf16[128,512]{1,0:T(8,128)(2,1)S(1)} %fusion.26), channel_id=1, source_target_pairs={{0,8},{4,12},{8,0},{12,4},{1,9},{5,13},{9,1},{13,5},{2,10},{6,14},... | collective-permute-start | bytes 393224 | tf_op jit(solution)/shard_map/ppermute | solution.py:30
  20.3 11.4 %collective-permute-start.9 = (bf16[128,512]{1,0:T(8,128)(2,1)S(1)}, bf16[128,512]{1,0:T(8,128)(2,1)S(1)}, u32[]{:S(2)}, u32[]{:S(2)}) collective-permute-start(bf16[128,512]{1,0:T(8,128)(2,1)S(1)} %fusion.27), channel_id=1, source_target_pairs={{0,8},{4,12},{8,0},{12,4},{1,9},{5,13},{9,1},{13,5},{2,10},{6,14},... | collective-permute-start | bytes 393224 | tf_op jit(solution)/shard_map/ppermute | solution.py:30
  30.0 6.0 %collective-permute-start.3 = (bf16[128,512]{1,0:T(8,128)(2,1)S(1)}, bf16[128,512]{1,0:T(8,128)(2,1)S(1)}, u32[]{:S(2)}, u32[]{:S(2)}) collective-permute-start(bf16[128,512]{1,0:T(8,128)(2,1)S(1)} %fusion.21), channel_id=1, source_target_pairs={{0,4},{4,0},{8,12},{12,8},{1,5},{5,1},{9,13},{13,9},{2,6},{6,2},{1... | collective-permute-start | bytes 393224 | tf_op jit(solution)/shard_map/ppermute | solution.py:40
  31.7 5.7 %collective-permute-start.10 = (bf16[128,512]{1,0:T(8,128)(2,1)S(1)}, bf16[128,512]{1,0:T(8,128)(2,1)S(1)}, u32[]{:S(2)}, u32[]{:S(2)}) collective-permute-start(bf16[128,512]{1,0:T(8,128)(2,1)S(1)} %fusion.20), channel_id=1, source_target_pairs={{0,4},{4,0},{8,12},{12,8},{1,5},{5,1},{9,13},{13,9},{2,6},{6,2},{1... | collective-permute-start | bytes 393224 | tf_op jit(solution)/shard_map/ppermute | solution.py:40
  36.8 2.0 %collective-permute-start.6 = (bf16[2,256,256]{2,1,0:T(8,128)(2,1)S(1)}, bf16[2,256,256]{2,1,0:T(8,128)(2,1)S(1)}, u32[]{:S(2)}, u32[]{:S(2)}) collective-permute-start(bf16[2,256,256]{2,1,0:T(8,128)(2,1)S(1)} %get-tuple-element.19), channel_id=1, source_target_pairs={{0,1},{1,0},{2,3},{3,2},{4,5},{5,4},{6,7},{7,6},{8,9},{9,8},{10,11... | collective-permute-start | bytes 786440 | tf_op jit(solution)/shard_map/ppermute | solution.py:8
  36.8 2.5 %collective-permute-start.5 = (bf16[2,256,256]{2,1,0:T(8,128)(2,1)S(1)}, bf16[2,256,256]{2,1,0:T(8,128)(2,1)S(1)}, u32[]{:S(2)}, u32[]{:S(2)}) collective-permute-start(bf16[2,256,256]{2,1,0:T(8,128)(2,1)S(1)} %get-tuple-element.17), channel_id=1, source_target_pairs={{0,1},{1,0},{2,3},{3,2},{4,5},{5,4},{6,7},{7,6},{8,9},{9,8},{10,11... | collective-permute-start | bytes 786440 | tf_op jit(solution)/shard_map/ppermute | solution.py:8
  37.3 2.2 %collective-permute-start.7 = (bf16[2,256,256]{2,1,0:T(8,128)(2,1)S(1)}, bf16[2,256,256]{2,1,0:T(8,128)(2,1)S(1)}, u32[]{:S(2)}, u32[]{:S(2)}) collective-permute-start(bf16[2,256,256]{2,1,0:T(8,128)(2,1)S(1)} %get-tuple-element.18), channel_id=1, source_target_pairs={{0,1},{1,0},{2,3},{3,2},{4,5},{5,4},{6,7},{7,6},{8,9},{9,8},{10,11... | collective-permute-start | bytes 786440 | tf_op jit(solution)/shard_map/ppermute | solution.py:8
  38.2 1.6 %collective-permute-start.12 = (bf16[2,256,256]{2,1,0:T(8,128)(2,1)S(1)}, bf16[2,256,256]{2,1,0:T(8,128)(2,1)S(1)}, u32[]{:S(2)}, u32[]{:S(2)}) collective-permute-start(bf16[2,256,256]{2,1,0:T(8,128)(2,1)S(1)} %get-tuple-element.22), channel_id=1, source_target_pairs={{0,1},{1,0},{2,3},{3,2},{4,5},{5,4},{6,7},{7,6},{8,9},{9,8},{10,11... | collective-permute-start | bytes 786440 | tf_op jit(solution)/shard_map/ppermute | solution.py:8
  38.6 1.7 %collective-permute-start.11 = (bf16[2,256,256]{2,1,0:T(8,128)(2,1)S(1)}, bf16[2,256,256]{2,1,0:T(8,128)(2,1)S(1)}, u32[]{:S(2)}, u32[]{:S(2)}) collective-permute-start(bf16[2,256,256]{2,1,0:T(8,128)(2,1)S(1)} %get-tuple-element.20), channel_id=1, source_target_pairs={{0,1},{1,0},{2,3},{3,2},{4,5},{5,4},{6,7},{7,6},{8,9},{9,8},{10,11... | collective-permute-start | bytes 786440 | tf_op jit(solution)/shard_map/ppermute | solution.py:8
  38.8 1.8 %collective-permute-start.13 = (bf16[2,256,256]{2,1,0:T(8,128)(2,1)S(1)}, bf16[2,256,256]{2,1,0:T(8,128)(2,1)S(1)}, u32[]{:S(2)}, u32[]{:S(2)}) collective-permute-start(bf16[2,256,256]{2,1,0:T(8,128)(2,1)S(1)} %get-tuple-element.21), channel_id=1, source_target_pairs={{0,1},{1,0},{2,3},{3,2},{4,5},{5,4},{6,7},{7,6},{8,9},{9,8},{10,11... | collective-permute-start | bytes 786440 | tf_op jit(solution)/shard_map/ppermute | solution.py:8

commit v22 on v17

--- a/solution.py
+++ b/solution.py
@@ -99,7 +99,7 @@
             "mrn,nc->mrc", scaled, col_factor, preferred_element_type=jnp.float32
         ).astype(jnp.bfloat16)
         n_m = projected.shape[0]
-        cuts = [i * n_m // 3 for i in range(4)]
+        cuts = [i * n_m // 2 for i in range(3)]
         chunks = [(lo, hi) for lo, hi in zip(cuts[:-1], cuts[1:]) if lo < hi]
         summed = jnp.einsum("rk,mrc->kmc", rf_own, projected, preferred_element_type=jnp.float32)
         other = []

time: 42.9 us -> 42.9 us (level)
  waiting for transfers between devices: 13.6 us -> 14.4 us
  starting transfers between devices: 12.4 us -> 11.9 us
    ppermute x8 -> x6, waiting for transfers between devices: 0.02 us -> 0.76 us  [_swap(): return lax.ppermute(x, axis, [(0, 1), (1, 0)])]
    ppermute x8 -> x6, starting transfers between devices: 2.21 us -> 1.71 us  [_swap(): return lax.ppermute(x, axis, [(0, 1), (1, 0)])]
    dot_general x6 -> x4, matrix products: 1.22 us -> 0.91 us  [local(): jnp.einsum('rk,mrc->kmc', rf_for_partner, proj_other, preferred_element_t...]
  transfers between devices with their start and end apart: 14 -> 12, of which waited for: 5 -> 9; matrix products, arithmetic and copies ran while one was open for 27% -> 26% of each run, Pallas kernels for 0% -> 0%
where the time goes in v22:
time: 42.9 us; the launch traced here: 42.7 us
  waiting for transfers between devices  14.4 us (34%)
  starting transfers between devices  11.9 us (28%)
  local copies, waits for them, and re-layouts  10.4 us (24%)
  matrix products  5.12 us (12%)
  other arithmetic  0.63 us (1%)
    ppermute x4, waiting for transfers between devices, _reduce_scatter_rows(): recv = lax.ppermute(send, axis, [(i, i ^ d) for i in range(size)])  9.76 us
    ppermute x4, starting transfers between devices, _reduce_scatter_rows(): recv = lax.ppermute(send, axis, [(i, i ^ d) for i in range(size)])  9.63 us
    unnamed x12, local copies, waits for them, and re-layouts  6.87 us
    ppermute x2, waiting for transfers between devices, _all_gather_rows(): recv = lax.ppermute(x, axis, [(i, i ^ d) for i in range(size)])  3.86 us
    ppermute x6, starting transfers between devices, _swap(): return lax.ppermute(x, axis, [(0, 1), (1, 0)])  1.71 us
    convert_element_type x1, local copies, waits for them, and re-layouts, local(): (control.astype(jnp.float32) + jnp.stack(outs, axis=2)).astype(jnp.bfloat16)  1.69 us
    dot_general x2, matrix products, local(): jnp.einsum('mrc,nc->mrn', expanded, cf_next, preferred_element_type=jnp.f...  1.32 us
    dot_general x2, matrix products, local(): jnp.einsum('mrn,nc->mrc', scaled, col_factor, preferred_element_type=jnp....  1.16 us
  transfers between devices with their start and end apart: 12, of which 9 were waited for; matrix products, arithmetic and copies ran while one was open for 26% of the time, Pallas kernels for 0%

profile of v22, /device:TPU:0, one launch (start us, length us, event | category | flops | bytes accessed | tf_op | source)
XLA Modules:
  0.0 42.7 jit_solution(17443229864029366416)
XLA Ops:
  0.0 1.3 %copy.8 = bf16[128,6,2,256]{3,0,2,1:T(8,128)(2,1)S(1)} copy(bf16[128,6,2,256]{3,2,1,0:T(2,128)(2,1)} %param.6) | data formatting | bytes 1572864 | tf_op args[1]
  1.3 0.5 %collective-permute-start = (bf16[128,6,2,256]{3,0,2,1:T(8,128)(2,1)S(1)}, bf16[128,6,2,256]{3,0,2,1:T(8,128)(2,1)S(1)}, u32[]{:S(2)}, u32[]{:S(2)}) collective-permute-start(bf16[128,6,2,256]{3,0,2,1:T(8,128)(2,1)S(1)} %copy.8), channel_id=1, source_target_pairs={{0,1},{1,0},{2,3},{3,2},{4,5},{5,4},{6,7},{7,6},{8,9},{9,8},{10,11... | collective-permute-start | bytes 2359304 | tf_op jit(solution)/shard_map/ppermute | solution.py:8
  1.8 0.8 %constant_dynamic-slice_fusion.2 = bf16[256,128]{1,0:T(8,128)(2,1)S(1)} fusion(bf16[256,256]{1,0:T(8,128)(2,1)} %param.8, s32[]{:T(128)S(6)} %select_n.60), kind=kLoop, calls=%fused_computation.69 | loop fusion | bytes 131076 | tf_op jit(solution)/shard_map/dynamic_slice | solution.py:68
  2.7 4.3 %copy.39 = bf16[256,6,2,512]{3,0,1,2:T(8,128)(2,1)} copy(bf16[256,6,2,512]{3,2,1,0:T(2,128)(2,1)} %param.5) | data formatting | bytes 6291456 | tf_op args[0]
  7.0 0.6 %fusion.29 = f32[256,6,2,256]{3,0,2,1:T(8,128)S(1)} fusion(bf16[256,256]{1,0:T(8,128)(2,1)S(1)} %copy-done.4, s32[]{:T(128)S(6)} %select_n.57, bf16[128,6,2,256]{3,2,1,0:T(2,128)(2,1)S(1)} %copy-done.1), kind=kOutput, calls=%fused_computation.48 | convolution fusion | flops 201326592 | bytes 3997700 | tf_op jit(solution)/shard_map/rk,kmlc->lmrc/dot_general | solution.py:72
  7.6 0.6 %fusion.11 = bf16[2,6,256,256]{3,2,0,1:T(8,128)(2,1)S(1)} fusion(f32[256,6,2,256]{3,0,2,1:T(8,128)S(1)} %fusion.29, bf16[128,6,2,256]{3,0,2,1:T(8,128)(2,1)S(1)} %collective-permute-done, bf16[256,128]{1,0:T(8,128)(2,1)S(1)} %constant_dynamic-slice_fusion.2), kind=kOutput, calls=%fused_computation.18 | convolution fusion | flops 202899456 | bytes 5570560 | tf_op jit(solution)/shard_map/rk,kmlc->lmrc/dot_general | solution.py:73
  8.2 1.3 %copy-done.2 = bf16[256,6,2,512]{3,0,1,2:T(8,128)(2,1)S(1)} copy-done((bf16[256,6,2,512]{3,0,1,2:T(8,128)(2,1)S(1)}, bf16[256,6,2,512]{3,0,1,2:T(8,128)(2,1)}, u32[]{:S(2)}) %copy-start.2) | copy-done | bytes 3145752
  9.5 0.7 %fusion = f32[256,512]{1,0:T(8,128)S(1)} fusion(bf16[2,6,256,512]{3,2,1,0:T(8,128)(2,1)S(1)} %bitcast.89, bf16[2,6,256,256]{3,2,0,1:T(8,128)(2,1)S(1)} %fusion.11, bf16[512,256]{1,0:T(8,128)(2,1)S(1)} %copy-done), kind=kOutput, calls=%fused_computation.4 | convolution fusion | flops 404881408 | bytes 3145728 | tf_op jit(solution)/shard_map/mrc,nc->mrn/dot_general | solution.py:85
  10.2 3.1 %collective-permute-start.1 = (bf16[128,512]{1,0:T(8,128)(2,1)S(1)}, bf16[128,512]{1,0:T(8,128)(2,1)S(1)}, u32[]{:S(2)}, u32[]{:S(2)}) collective-permute-start(bf16[128,512]{1,0:T(8,128)(2,1)S(1)} %dynamic-slice_convert_fusion.1), channel_id=1, source_target_pairs={{0,4},{4,0},{8,12},{12,8},{1,5},{5,1},{9,13},{13,9},{2,6},{6,2},{1... | collective-permute-start | bytes 393224 | tf_op jit(solution)/shard_map/ppermute | solution.py:23
  13.3 0.8 %fusion.54 = (f32[1,256,512]{2,0,1:T(1,128)S(1)}, f32[1,256,512]{2,0,1:T(1,128)S(1)}) fusion(f32[2,256,512]{2,0,1:T(2,128)S(1)} %bitcast.93), kind=kLoop, calls=%fused_computation.72 | loop fusion | bytes 2097152 | tf_op jit(solution)/shard_map/slice | solution.py:90
  14.1 0.7 %fusion.2 = f32[256,512]{1,0:T(8,128)S(1)} fusion(bf16[2,6,256,512]{3,2,1,0:T(8,128)(2,1)S(1)} %bitcast.90, bf16[2,6,256,256]{3,2,0,1:T(8,128)(2,1)S(1)} %fusion.11, bf16[512,256]{1,0:T(8,128)(2,1)S(1)} %copy-done), kind=kOutput, calls=%fused_computation.6 | convolution fusion | flops 404881408 | bytes 3145728 | tf_op jit(solution)/shard_map/mrc,nc->mrn/dot_general | solution.py:85
  14.9 2.2 %collective-permute-done.1 = bf16[128,512]{1,0:T(8,128)(2,1)S(1)} collective-permute-done((bf16[128,512]{1,0:T(8,128)(2,1)S(1)}, bf16[128,512]{1,0:T(8,128)(2,1)S(1)}, u32[]{:S(2)}, u32[]{:S(2)}) %collective-permute-start.1) | collective-permute-done | bytes 131104 | tf_op jit(solution)/shard_map/ppermute | solution.py:23
  17.2 2.6 %collective-permute-start.2 = (bf16[128,512]{1,0:T(8,128)(2,1)S(1)}, bf16[128,512]{1,0:T(8,128)(2,1)S(1)}, u32[]{:S(2)}, u32[]{:S(2)}) collective-permute-start(bf16[128,512]{1,0:T(8,128)(2,1)S(1)} %fusion.26), channel_id=1, source_target_pairs={{0,8},{4,12},{8,0},{12,4},{1,9},{5,13},{9,1},{13,5},{2,10},{6,14},... | collective-permute-start | bytes 393224 | tf_op jit(solution)/shard_map/ppermute | solution.py:30
  20.0 3.8 %collective-permute-start.8 = (bf16[128,512]{1,0:T(8,128)(2,1)S(1)}, bf16[128,512]{1,0:T(8,128)(2,1)S(1)}, u32[]{:S(2)}, u32[]{:S(2)}) collective-permute-start(bf16[128,512]{1,0:T(8,128)(2,1)S(1)} %fusion.27), channel_id=1, source_target_pairs={{0,8},{4,12},{8,0},{12,4},{1,9},{5,13},{9,1},{13,5},{2,10},{6,14},... | collective-permute-start | bytes 393224 | tf_op jit(solution)/shard_map/ppermute | solution.py:30
  23.8 5.8 %collective-permute-done.2 = bf16[128,512]{1,0:T(8,128)(2,1)S(1)} collective-permute-done((bf16[128,512]{1,0:T(8,128)(2,1)S(1)}, bf16[128,512]{1,0:T(8,128)(2,1)S(1)}, u32[]{:S(2)}, u32[]{:S(2)}) %collective-permute-start.2) | collective-permute-done | bytes 131104 | tf_op jit(solution)/shard_map/ppermute | solution.py:30
  29.8 1.6 %collective-permute-done.8 = bf16[128,512]{1,0:T(8,128)(2,1)S(1)} collective-permute-done((bf16[128,512]{1,0:T(8,128)(2,1)S(1)}, bf16[128,512]{1,0:T(8,128)(2,1)S(1)}, u32[]{:S(2)}, u32[]{:S(2)}) %collective-permute-start.8) | collective-permute-done | bytes 131104 | tf_op jit(solution)/shard_map/ppermute | solution.py:30
  31.4 0.5 %collective-permute-start.9 = (bf16[128,512]{1,0:T(8,128)(2,1)S(1)}, bf16[128,512]{1,0:T(8,128)(2,1)S(1)}, u32[]{:S(2)}, u32[]{:S(2)}) collective-permute-start(bf16[128,512]{1,0:T(8,128)(2,1)S(1)} %fusion.20), channel_id=1, source_target_pairs={{0,4},{4,0},{8,12},{12,8},{1,5},{5,1},{9,13},{13,9},{2,6},{6,2},{1... | collective-permute-start | bytes 393224 | tf_op jit(solution)/shard_map/ppermute | solution.py:40
  32.0 3.8 %collective-permute-done.3 = bf16[128,512]{1,0:T(8,128)(2,1)S(1)} collective-permute-done((bf16[128,512]{1,0:T(8,128)(2,1)S(1)}, bf16[128,512]{1,0:T(8,128)(2,1)S(1)}, u32[]{:S(2)}, u32[]{:S(2)}) %collective-permute-start.3) | collective-permute-done | bytes 131104 | tf_op jit(solution)/shard_map/ppermute | solution.py:40
  35.8 0.6 %fusion.12 = bf16[6,256,256]{2,1,0:T(8,128)(2,1)S(1)} fusion(f32[256,512]{1,0:T(8,128)S(1)} %maximum_convert_fusion, bf16[2,6,256,512]{3,2,1,0:T(8,128)(2,1)S(1)} %bitcast.91, bf16[512,256]{1,0:T(8,128)(2,1)S(1)} %copy-done), kind=kOutput, calls=%fused_computation.19 | convolution fusion | flops 405405696 | bytes 3145728 | tf_op jit(solution)/shard_map/mrn,nc->mrc/dot_general | solution.py:98
  36.5 0.5 %collective-permute-start.6 = (bf16[3,256,256]{2,1,0:T(8,128)(2,1)S(1)}, bf16[3,256,256]{2,1,0:T(8,128)(2,1)S(1)}, u32[]{:S(2)}, u32[]{:S(2)}) collective-permute-start(bf16[3,256,256]{2,1,0:T(8,128)(2,1)S(1)} %get-tuple-element.18), channel_id=1, source_target_pairs={{0,1},{1,0},{2,3},{3,2},{4,5},{5,4},{6,7},{7,6},{8,9},{9,8},{10,11... | collective-permute-start | bytes 1179656 | tf_op jit(solution)/shard_map/ppermute | solution.py:8
  37.2 0.6 %fusion.15 = bf16[6,256,256]{2,1,0:T(8,128)(2,1)S(1)} fusion(f32[256,512]{1,0:T(8,128)S(1)} %maximum_convert_fusion.1, bf16[2,6,256,512]{3,2,1,0:T(8,128)(2,1)S(1)} %bitcast.92, bf16[512,256]{1,0:T(8,128)(2,1)S(1)} %copy-done), kind=kOutput, calls=%fused_computation.20 | convolution fusion | flops 405405696 | bytes 3145728 | tf_op jit(solution)/shard_map/mrn,nc->mrc/dot_general | solution.py:98
  37.9 0.5 %collective-permute-start.11 = (bf16[3,256,256]{2,1,0:T(8,128)(2,1)S(1)}, bf16[3,256,256]{2,1,0:T(8,128)(2,1)S(1)}, u32[]{:S(2)}, u32[]{:S(2)}) collective-permute-start(bf16[3,256,256]{2,1,0:T(8,128)(2,1)S(1)} %get-tuple-element.20), channel_id=1, source_target_pairs={{0,1},{1,0},{2,3},{3,2},{4,5},{5,4},{6,7},{7,6},{8,9},{9,8},{10,11... | collective-permute-start | bytes 1179656 | tf_op jit(solution)/shard_map/ppermute | solution.py:8
  39.9 0.3 collective-permute-done.11
  41.0 1.7 %copy.16 = bf16[128,6,2,256]{3,2,1,0:T(2,128)(2,1)} copy(bf16[128,6,2,256]{3,0,1,2:T(8,128)(2,1)S(1)} %fusion.8) | data formatting | bytes 1572864 | tf_op jit(solution)/shard_map/convert_element_type | solution.py:113
  (42 shorter events, 3.4 us)
Async XLA Ops:
  0.0 8.2 %copy-start = (bf16[512,256]{1,0:T(8,128)(2,1)S(1)}, bf16[512,256]{1,0:T(8,128)(2,1)}, u32[]{:S(2)}) copy-start(bf16[512,256]{1,0:T(8,128)(2,1)} %param.9) | copy-start | bytes 786436
  1.3 6.3 %collective-permute-start = (bf16[128,6,2,256]{3,0,2,1:T(8,128)(2,1)S(1)}, bf16[128,6,2,256]{3,0,2,1:T(8,128)(2,1)S(1)}, u32[]{:S(2)}, u32[]{:S(2)}) collective-permute-start(bf16[128,6,2,256]{3,0,2,1:T(8,128)(2,1)S(1)} %copy.8), channel_id=1, source_target_pairs={{0,1},{1,0},{2,3},{3,2},{4,5},{5,4},{6,7},{7,6},{8,9},{9,8},{10,11... | collective-permute-start | bytes 2359304 | tf_op jit(solution)/shard_map/ppermute | solution.py:8
  2.7 35.8 %collective-permute-start.4 = (bf16[256,128]{1,0:T(8,128)(2,1)S(1)}, bf16[256,128]{1,0:T(8,128)(2,1)S(1)}, u32[]{:S(2)}, u32[]{:S(2)}) collective-permute-start(bf16[256,128]{1,0:T(8,128)(2,1)S(1)} %constant_dynamic-slice_fusion.2), channel_id=1, source_target_pairs={{0,1},{1,0},{2,3},{3,2},{4,5},{5,4},{6,7},{7,6},{8,9},{9,8},{10,11... | collective-permute-start | bytes 196616 | tf_op jit(solution)/shard_map/ppermute | solution.py:8
  2.7 4.3 %copy-start.1 = (bf16[128,6,2,256]{3,2,1,0:T(2,128)(2,1)S(1)}, bf16[128,6,2,256]{3,2,1,0:T(2,128)(2,1)}, u32[]{:S(2)}) copy-start(bf16[128,6,2,256]{3,2,1,0:T(2,128)(2,1)} %param.6) | copy-start | bytes 2359300
  2.7 4.3 %copy-start.4 = (bf16[256,256]{1,0:T(8,128)(2,1)S(1)}, bf16[256,256]{1,0:T(8,128)(2,1)}, u32[]{:S(2)}) copy-start(bf16[256,256]{1,0:T(8,128)(2,1)} %param.8) | copy-start | bytes 393220
  7.6 1.9 %copy-start.2 = (bf16[256,6,2,512]{3,0,1,2:T(8,128)(2,1)S(1)}, bf16[256,6,2,512]{3,0,1,2:T(8,128)(2,1)}, u32[]{:S(2)}) copy-start(bf16[256,6,2,512]{3,0,1,2:T(8,128)(2,1)} %copy.39) | copy-start | bytes 9437188
  8.2 5.1 %copy-start.3 = (f32[256,2,512]{2,1,0:T(2,128)S(1)}, f32[256,2,512]{2,1,0:T(2,128)}, u32[]{:S(2)}) copy-start(f32[256,2,512]{2,1,0:T(2,128)} %param.7) | copy-start | bytes 3145732
  10.2 7.0 %collective-permute-start.1 = (bf16[128,512]{1,0:T(8,128)(2,1)S(1)}, bf16[128,512]{1,0:T(8,128)(2,1)S(1)}, u32[]{:S(2)}, u32[]{:S(2)}) collective-permute-start(bf16[128,512]{1,0:T(8,128)(2,1)S(1)} %dynamic-slice_convert_fusion.1), channel_id=1, source_target_pairs={{0,4},{4,0},{8,12},{12,8},{1,5},{5,1},{9,13},{13,9},{2,6},{6,2},{1... | collective-permute-start | bytes 393224 | tf_op jit(solution)/shard_map/ppermute | solution.py:23
  14.8 5.2 %collective-permute-start.7 = (bf16[128,512]{1,0:T(8,128)(2,1)S(1)}, bf16[128,512]{1,0:T(8,128)(2,1)S(1)}, u32[]{:S(2)}, u32[]{:S(2)}) collective-permute-start(bf16[128,512]{1,0:T(8,128)(2,1)S(1)} %dynamic-slice_convert_fusion), channel_id=1, source_target_pairs={{0,4},{4,0},{8,12},{12,8},{1,5},{5,1},{9,13},{13,9},{2,6},{6,2},{1... | collective-permute-start | bytes 393224 | tf_op jit(solution)/shard_map/ppermute | solution.py:23
  17.2 12.5 %collective-permute-start.2 = (bf16[128,512]{1,0:T(8,128)(2,1)S(1)}, bf16[128,512]{1,0:T(8,128)(2,1)S(1)}, u32[]{:S(2)}, u32[]{:S(2)}) collective-permute-start(bf16[128,512]{1,0:T(8,128)(2,1)S(1)} %fusion.26), channel_id=1, source_target_pairs={{0,8},{4,12},{8,0},{12,4},{1,9},{5,13},{9,1},{13,5},{2,10},{6,14},... | collective-permute-start | bytes 393224 | tf_op jit(solution)/shard_map/ppermute | solution.py:30
  20.0 11.3 %collective-permute-start.8 = (bf16[128,512]{1,0:T(8,128)(2,1)S(1)}, bf16[128,512]{1,0:T(8,128)(2,1)S(1)}, u32[]{:S(2)}, u32[]{:S(2)}) collective-permute-start(bf16[128,512]{1,0:T(8,128)(2,1)S(1)} %fusion.27), channel_id=1, source_target_pairs={{0,8},{4,12},{8,0},{12,4},{1,9},{5,13},{9,1},{13,5},{2,10},{6,14},... | collective-permute-start | bytes 393224 | tf_op jit(solution)/shard_map/ppermute | solution.py:30
  29.7 6.0 %collective-permute-start.3 = (bf16[128,512]{1,0:T(8,128)(2,1)S(1)}, bf16[128,512]{1,0:T(8,128)(2,1)S(1)}, u32[]{:S(2)}, u32[]{:S(2)}) collective-permute-start(bf16[128,512]{1,0:T(8,128)(2,1)S(1)} %fusion.21), channel_id=1, source_target_pairs={{0,4},{4,0},{8,12},{12,8},{1,5},{5,1},{9,13},{13,9},{2,6},{6,2},{1... | collective-permute-start | bytes 393224 | tf_op jit(solution)/shard_map/ppermute | solution.py:40
  31.4 5.7 %collective-permute-start.9 = (bf16[128,512]{1,0:T(8,128)(2,1)S(1)}, bf16[128,512]{1,0:T(8,128)(2,1)S(1)}, u32[]{:S(2)}, u32[]{:S(2)}) collective-permute-start(bf16[128,512]{1,0:T(8,128)(2,1)S(1)} %fusion.20), channel_id=1, source_target_pairs={{0,4},{4,0},{8,12},{12,8},{1,5},{5,1},{9,13},{13,9},{2,6},{6,2},{1... | collective-permute-start | bytes 393224 | tf_op jit(solution)/shard_map/ppermute | solution.py:40
  36.5 2.0 %collective-permute-start.5 = (bf16[3,256,256]{2,1,0:T(8,128)(2,1)S(1)}, bf16[3,256,256]{2,1,0:T(8,128)(2,1)S(1)}, u32[]{:S(2)}, u32[]{:S(2)}) collective-permute-start(bf16[3,256,256]{2,1,0:T(8,128)(2,1)S(1)} %get-tuple-element.17), channel_id=1, source_target_pairs={{0,1},{1,0},{2,3},{3,2},{4,5},{5,4},{6,7},{7,6},{8,9},{9,8},{10,11... | collective-permute-start | bytes 1179656 | tf_op jit(solution)/shard_map/ppermute | solution.py:8
  36.5 2.3 %collective-permute-start.6 = (bf16[3,256,256]{2,1,0:T(8,128)(2,1)S(1)}, bf16[3,256,256]{2,1,0:T(8,128)(2,1)S(1)}, u32[]{:S(2)}, u32[]{:S(2)}) collective-permute-start(bf16[3,256,256]{2,1,0:T(8,128)(2,1)S(1)} %get-tuple-element.18), channel_id=1, source_target_pairs={{0,1},{1,0},{2,3},{3,2},{4,5},{5,4},{6,7},{7,6},{8,9},{9,8},{10,11... | collective-permute-start | bytes 1179656 | tf_op jit(solution)/shard_map/ppermute | solution.py:8
  37.9 1.8 %collective-permute-start.10 = (bf16[3,256,256]{2,1,0:T(8,128)(2,1)S(1)}, bf16[3,256,256]{2,1,0:T(8,128)(2,1)S(1)}, u32[]{:S(2)}, u32[]{:S(2)}) collective-permute-start(bf16[3,256,256]{2,1,0:T(8,128)(2,1)S(1)} %get-tuple-element.19), channel_id=1, source_target_pairs={{0,1},{1,0},{2,3},{3,2},{4,5},{5,4},{6,7},{7,6},{8,9},{9,8},{10,11... | collective-permute-start | bytes 1179656 | tf_op jit(solution)/shard_map/ppermute | solution.py:8
  37.9 2.3 %collective-permute-start.11 = (bf16[3,256,256]{2,1,0:T(8,128)(2,1)S(1)}, bf16[3,256,256]{2,1,0:T(8,128)(2,1)S(1)}, u32[]{:S(2)}, u32[]{:S(2)}) collective-permute-start(bf16[3,256,256]{2,1,0:T(8,128)(2,1)S(1)} %get-tuple-element.20), channel_id=1, source_target_pairs={{0,1},{1,0},{2,3},{3,2},{4,5},{5,4},{6,7},{7,6},{8,9},{9,8},{10,11... | collective-permute-start | bytes 1179656 | tf_op jit(solution)/shard_map/ppermute | solution.py:8

commit v23 on v22

--- a/solution.py
+++ b/solution.py
@@ -99,7 +99,7 @@
             "mrn,nc->mrc", scaled, col_factor, preferred_element_type=jnp.float32
         ).astype(jnp.bfloat16)
         n_m = projected.shape[0]
-        cuts = [i * n_m // 2 for i in range(3)]
+        cuts = [0, n_m]
         chunks = [(lo, hi) for lo, hi in zip(cuts[:-1], cuts[1:]) if lo < hi]
         summed = jnp.einsum("rk,mrc->kmc", rf_own, projected, preferred_element_type=jnp.float32)
         other = []

time: 42.9 us -> 42.6 us (level)
  waiting for transfers between devices: 14.4 us -> 16.7 us
  starting transfers between devices: 11.9 us -> 10.6 us
  local copies, waits for them, and re-layouts: 10.4 us -> 9.44 us
    ppermute x4, waiting for transfers between devices: 9.76 us -> 11 us  [_reduce_scatter_rows(): recv = lax.ppermute(send, axis, [(i, i ^ d) for i in range(size)])]
    dynamic_slice x1, local copies, waits for them, and re-layouts: 0.84 us -> 0.01 us  [local(): rf_other = lax.dynamic_slice_in_dim(row_factor, (1 - h) * kh, kh, 1)]
    ppermute x4, starting transfers between devices: 9.63 us -> 8.82 us  [_reduce_scatter_rows(): recv = lax.ppermute(send, axis, [(i, i ^ d) for i in range(size)])]
    ppermute x2, waiting for transfers between devices: 3.86 us -> 4.49 us  [_all_gather_rows(): recv = lax.ppermute(x, axis, [(i, i ^ d) for i in range(size)])]
    ppermute x6 -> x4, starting transfers between devices: 1.71 us -> 1.16 us  [_swap(): return lax.ppermute(x, axis, [(0, 1), (1, 0)])]
    ppermute x6 -> x4, waiting for transfers between devices: 0.76 us -> 1.27 us  [_swap(): return lax.ppermute(x, axis, [(0, 1), (1, 0)])]
    dot_general x4 -> x2, matrix products: 0.91 us -> 0.59 us  [local(): jnp.einsum('rk,mrc->kmc', rf_for_partner, proj_other, preferred_element_t...]
  transfers between devices with their start and end apart: 12 -> 10, of which waited for: 9 -> 7; matrix products, arithmetic and copies ran while one was open for 26% -> 21% of each run, Pallas kernels for 0% -> 0%
where the time goes in v23:
time: 42.6 us; the launch traced here: 42.5 us
  waiting for transfers between devices  16.7 us (39%)
  starting transfers between devices  10.6 us (25%)
  local copies, waits for them, and re-layouts  9.44 us (22%)
  matrix products  4.81 us (11%)
  other arithmetic  0.62 us (1%)
    ppermute x4, waiting for transfers between devices, _reduce_scatter_rows(): recv = lax.ppermute(send, axis, [(i, i ^ d) for i in range(size)])  11 us
    ppermute x4, starting transfers between devices, _reduce_scatter_rows(): recv = lax.ppermute(send, axis, [(i, i ^ d) for i in range(size)])  8.82 us
    unnamed x12, local copies, waits for them, and re-layouts  6.83 us
    ppermute x2, waiting for transfers between devices, _all_gather_rows(): recv = lax.ppermute(x, axis, [(i, i ^ d) for i in range(size)])  4.49 us
    convert_element_type x1, local copies, waits for them, and re-layouts, local(): (control.astype(jnp.float32) + jnp.stack(outs, axis=2)).astype(jnp.bfloat16)  1.69 us
    dot_general x2, matrix products, local(): jnp.einsum('mrc,nc->mrn', expanded, cf_next, preferred_element_type=jnp.f...  1.33 us
    ppermute x4, waiting for transfers between devices, _swap(): return lax.ppermute(x, axis, [(0, 1), (1, 0)])  1.27 us
    dot_general x2, matrix products, local(): jnp.einsum('mrn,nc->mrc', scaled, col_factor, preferred_element_type=jnp....  1.17 us
  transfers between devices with their start and end apart: 10, of which 7 were waited for; matrix products, arithmetic and copies ran while one was open for 21% of the time, Pallas kernels for 0%

profile of v23, /device:TPU:0, one launch (start us, length us, event | category | flops | bytes accessed | tf_op | source)
XLA Modules:
  0.0 42.5 jit_solution(3626188974039093390)
XLA Ops:
  0.0 1.3 %copy.8 = bf16[128,6,2,256]{3,0,2,1:T(8,128)(2,1)S(1)} copy(bf16[128,6,2,256]{3,2,1,0:T(2,128)(2,1)} %param.6) | data formatting | bytes 1572864 | tf_op args[1]
  1.3 0.5 %collective-permute-start = (bf16[128,6,2,256]{3,0,2,1:T(8,128)(2,1)S(1)}, bf16[128,6,2,256]{3,0,2,1:T(8,128)(2,1)S(1)}, u32[]{:S(2)}, u32[]{:S(2)}) collective-permute-start(bf16[128,6,2,256]{3,0,2,1:T(8,128)(2,1)S(1)} %copy.8), channel_id=1, source_target_pairs={{0,1},{1,0},{2,3},{3,2},{4,5},{5,4},{6,7},{7,6},{8,9},{9,8},{10,11... | collective-permute-start | bytes 2359304 | tf_op jit(solution)/shard_map/ppermute | solution.py:8
  1.8 4.3 %copy.33 = bf16[256,6,2,512]{3,0,1,2:T(8,128)(2,1)} copy(bf16[256,6,2,512]{3,2,1,0:T(2,128)(2,1)} %param.5) | data formatting | bytes 6291456 | tf_op args[0]
  6.1 0.6 %fusion.29 = f32[256,6,2,256]{3,0,2,1:T(8,128)S(1)} fusion(bf16[256,256]{1,0:T(8,128)(2,1)S(1)} %copy-done.4, s32[]{:T(128)S(6)} %select_n.57, bf16[128,6,2,256]{3,2,1,0:T(2,128)(2,1)S(1)} %copy-done.1), kind=kOutput, calls=%fused_computation.48 | convolution fusion | flops 201326592 | bytes 3997700 | tf_op jit(solution)/shard_map/rk,kmlc->lmrc/dot_general | solution.py:72
  6.7 0.6 %fusion.11 = bf16[2,6,256,256]{3,2,0,1:T(8,128)(2,1)S(1)} fusion(f32[256,6,2,256]{3,0,2,1:T(8,128)S(1)} %fusion.29, bf16[128,6,2,256]{3,0,2,1:T(8,128)(2,1)S(1)} %collective-permute-done, bf16[256,128]{1,0:T(8,128)(2,1)S(1)} %constant_dynamic-slice_fusion.2), kind=kOutput, calls=%fused_computation.18 | convolution fusion | flops 202899456 | bytes 5570560 | tf_op jit(solution)/shard_map/rk,kmlc->lmrc/dot_general | solution.py:73
  7.3 1.3 %copy-done.2 = bf16[256,6,2,512]{3,0,1,2:T(8,128)(2,1)S(1)} copy-done((bf16[256,6,2,512]{3,0,1,2:T(8,128)(2,1)S(1)}, bf16[256,6,2,512]{3,0,1,2:T(8,128)(2,1)}, u32[]{:S(2)}) %copy-start.2) | copy-done | bytes 3145752
  8.5 0.7 %fusion = f32[256,512]{1,0:T(8,128)S(1)} fusion(bf16[2,6,256,512]{3,2,1,0:T(8,128)(2,1)S(1)} %bitcast.77, bf16[2,6,256,256]{3,2,0,1:T(8,128)(2,1)S(1)} %fusion.11, bf16[512,256]{1,0:T(8,128)(2,1)S(1)} %copy-done), kind=kOutput, calls=%fused_computation.4 | convolution fusion | flops 404881408 | bytes 3145728 | tf_op jit(solution)/shard_map/mrc,nc->mrn/dot_general | solution.py:85
  9.2 2.7 %collective-permute-start.1 = (bf16[128,512]{1,0:T(8,128)(2,1)S(1)}, bf16[128,512]{1,0:T(8,128)(2,1)S(1)}, u32[]{:S(2)}, u32[]{:S(2)}) collective-permute-start(bf16[128,512]{1,0:T(8,128)(2,1)S(1)} %dynamic-slice_convert_fusion.1), channel_id=1, source_target_pairs={{0,4},{4,0},{8,12},{12,8},{1,5},{5,1},{9,13},{13,9},{2,6},{6,2},{1... | collective-permute-start | bytes 393224 | tf_op jit(solution)/shard_map/ppermute | solution.py:23
  11.9 0.8 %fusion.44 = (f32[1,256,512]{2,0,1:T(1,128)S(1)}, f32[1,256,512]{2,0,1:T(1,128)S(1)}) fusion(f32[2,256,512]{2,0,1:T(2,128)S(1)} %bitcast.81), kind=kLoop, calls=%fused_computation.66 | loop fusion | bytes 2097152 | tf_op jit(solution)/shard_map/slice | solution.py:90
  12.8 0.7 %fusion.2 = f32[256,512]{1,0:T(8,128)S(1)} fusion(bf16[2,6,256,512]{3,2,1,0:T(8,128)(2,1)S(1)} %bitcast.78, bf16[2,6,256,256]{3,2,0,1:T(8,128)(2,1)S(1)} %fusion.11, bf16[512,256]{1,0:T(8,128)(2,1)S(1)} %copy-done), kind=kOutput, calls=%fused_computation.6 | convolution fusion | flops 404881408 | bytes 3145728 | tf_op jit(solution)/shard_map/mrc,nc->mrn/dot_general | solution.py:85
  13.6 2.4 %collective-permute-done.1 = bf16[128,512]{1,0:T(8,128)(2,1)S(1)} collective-permute-done((bf16[128,512]{1,0:T(8,128)(2,1)S(1)}, bf16[128,512]{1,0:T(8,128)(2,1)S(1)}, u32[]{:S(2)}, u32[]{:S(2)}) %collective-permute-start.1) | collective-permute-done | bytes 131104 | tf_op jit(solution)/shard_map/ppermute | solution.py:23
  16.1 2.8 %collective-permute-start.2 = (bf16[128,512]{1,0:T(8,128)(2,1)S(1)}, bf16[128,512]{1,0:T(8,128)(2,1)S(1)}, u32[]{:S(2)}, u32[]{:S(2)}) collective-permute-start(bf16[128,512]{1,0:T(8,128)(2,1)S(1)} %fusion.26), channel_id=1, source_target_pairs={{0,8},{4,12},{8,0},{12,4},{1,9},{5,13},{9,1},{13,5},{2,10},{6,14},... | collective-permute-start | bytes 393224 | tf_op jit(solution)/shard_map/ppermute | solution.py:30
  19.1 3.2 %collective-permute-start.7 = (bf16[128,512]{1,0:T(8,128)(2,1)S(1)}, bf16[128,512]{1,0:T(8,128)(2,1)S(1)}, u32[]{:S(2)}, u32[]{:S(2)}) collective-permute-start(bf16[128,512]{1,0:T(8,128)(2,1)S(1)} %fusion.27), channel_id=1, source_target_pairs={{0,8},{4,12},{8,0},{12,4},{1,9},{5,13},{9,1},{13,5},{2,10},{6,14},... | collective-permute-start | bytes 393224 | tf_op jit(solution)/shard_map/ppermute | solution.py:30
  22.4 6.6 %collective-permute-done.2 = bf16[128,512]{1,0:T(8,128)(2,1)S(1)} collective-permute-done((bf16[128,512]{1,0:T(8,128)(2,1)S(1)}, bf16[128,512]{1,0:T(8,128)(2,1)S(1)}, u32[]{:S(2)}, u32[]{:S(2)}) %collective-permute-start.2) | collective-permute-done | bytes 131104 | tf_op jit(solution)/shard_map/ppermute | solution.py:30
  29.2 1.7 %collective-permute-done.7 = bf16[128,512]{1,0:T(8,128)(2,1)S(1)} collective-permute-done((bf16[128,512]{1,0:T(8,128)(2,1)S(1)}, bf16[128,512]{1,0:T(8,128)(2,1)S(1)}, u32[]{:S(2)}, u32[]{:S(2)}) %collective-permute-start.7) | collective-permute-done | bytes 131104 | tf_op jit(solution)/shard_map/ppermute | solution.py:30
  30.9 0.6 %collective-permute-start.8 = (bf16[128,512]{1,0:T(8,128)(2,1)S(1)}, bf16[128,512]{1,0:T(8,128)(2,1)S(1)}, u32[]{:S(2)}, u32[]{:S(2)}) collective-permute-start(bf16[128,512]{1,0:T(8,128)(2,1)S(1)} %fusion.20), channel_id=1, source_target_pairs={{0,4},{4,0},{8,12},{12,8},{1,5},{5,1},{9,13},{13,9},{2,6},{6,2},{1... | collective-permute-start | bytes 393224 | tf_op jit(solution)/shard_map/ppermute | solution.py:40
  31.5 3.8 %collective-permute-done.3 = bf16[128,512]{1,0:T(8,128)(2,1)S(1)} collective-permute-done((bf16[128,512]{1,0:T(8,128)(2,1)S(1)}, bf16[128,512]{1,0:T(8,128)(2,1)S(1)}, u32[]{:S(2)}, u32[]{:S(2)}) %collective-permute-start.3) | collective-permute-done | bytes 131104 | tf_op jit(solution)/shard_map/ppermute | solution.py:40
  35.4 0.6 %fusion.12 = bf16[6,256,256]{2,1,0:T(8,128)(2,1)S(1)} fusion(f32[256,512]{1,0:T(8,128)S(1)} %maximum_convert_fusion, bf16[2,6,256,512]{3,2,1,0:T(8,128)(2,1)S(1)} %bitcast.79, bf16[512,256]{1,0:T(8,128)(2,1)S(1)} %copy-done), kind=kOutput, calls=%fused_computation.19 | convolution fusion | flops 405405696 | bytes 3145728 | tf_op jit(solution)/shard_map/mrn,nc->mrc/dot_general | solution.py:98
  36.1 0.7 %collective-permute-done.8 = bf16[128,512]{1,0:T(8,128)(2,1)S(1)} collective-permute-done((bf16[128,512]{1,0:T(8,128)(2,1)S(1)}, bf16[128,512]{1,0:T(8,128)(2,1)S(1)}, u32[]{:S(2)}, u32[]{:S(2)}) %collective-permute-start.8) | collective-permute-done | bytes 131104 | tf_op jit(solution)/shard_map/ppermute | solution.py:40
  36.9 0.6 %fusion.15 = bf16[6,256,256]{2,1,0:T(8,128)(2,1)S(1)} fusion(f32[256,512]{1,0:T(8,128)S(1)} %maximum_convert_fusion.1, bf16[2,6,256,512]{3,2,1,0:T(8,128)(2,1)S(1)} %bitcast.80, bf16[512,256]{1,0:T(8,128)(2,1)S(1)} %copy-done), kind=kOutput, calls=%fused_computation.20 | convolution fusion | flops 405405696 | bytes 3145728 | tf_op jit(solution)/shard_map/mrn,nc->mrc/dot_general | solution.py:98
  37.5 0.5 %collective-permute-start.4 = (bf16[256,128]{1,0:T(8,128)(2,1)S(1)}, bf16[256,128]{1,0:T(8,128)(2,1)S(1)}, u32[]{:S(2)}, u32[]{:S(2)}) collective-permute-start(bf16[256,128]{1,0:T(8,128)(2,1)S(1)} %constant_dynamic-slice_fusion.2), channel_id=1, source_target_pairs={{0,1},{1,0},{2,3},{3,2},{4,5},{5,4},{6,7},{7,6},{8,9},{9,8},{10,11... | collective-permute-start | bytes 196616 | tf_op jit(solution)/shard_map/ppermute | solution.py:8
  38.3 0.3 fusion.33
  38.6 1.3 %collective-permute-done.4 = bf16[256,128]{1,0:T(8,128)(2,1)S(1)} collective-permute-done((bf16[256,128]{1,0:T(8,128)(2,1)S(1)}, bf16[256,128]{1,0:T(8,128)(2,1)S(1)}, u32[]{:S(2)}, u32[]{:S(2)}) %collective-permute-start.4) | collective-permute-done | bytes 65568 | tf_op jit(solution)/shard_map/ppermute | solution.py:8
  40.8 1.7 %copy.14 = bf16[128,6,2,256]{3,2,1,0:T(2,128)(2,1)} copy(bf16[128,6,2,256]{3,0,1,2:T(8,128)(2,1)S(1)} %fusion.8) | data formatting | bytes 1572864 | tf_op jit(solution)/shard_map/convert_element_type | solution.py:113
  (34 shorter events, 2.1 us)
Async XLA Ops:
  0.0 7.3 %copy-start = (bf16[512,256]{1,0:T(8,128)(2,1)S(1)}, bf16[512,256]{1,0:T(8,128)(2,1)}, u32[]{:S(2)}) copy-start(bf16[512,256]{1,0:T(8,128)(2,1)} %param.9) | copy-start | bytes 786436
  1.3 5.4 %collective-permute-start = (bf16[128,6,2,256]{3,0,2,1:T(8,128)(2,1)S(1)}, bf16[128,6,2,256]{3,0,2,1:T(8,128)(2,1)S(1)}, u32[]{:S(2)}, u32[]{:S(2)}) collective-permute-start(bf16[128,6,2,256]{3,0,2,1:T(8,128)(2,1)S(1)} %copy.8), channel_id=1, source_target_pairs={{0,1},{1,0},{2,3},{3,2},{4,5},{5,4},{6,7},{7,6},{8,9},{9,8},{10,11... | collective-permute-start | bytes 2359304 | tf_op jit(solution)/shard_map/ppermute | solution.py:8
  1.8 4.3 %copy-start.4 = (bf16[256,256]{1,0:T(8,128)(2,1)S(1)}, bf16[256,256]{1,0:T(8,128)(2,1)}, u32[]{:S(2)}) copy-start(bf16[256,256]{1,0:T(8,128)(2,1)} %param.8) | copy-start | bytes 393220
  1.8 4.3 %copy-start.1 = (bf16[128,6,2,256]{3,2,1,0:T(2,128)(2,1)S(1)}, bf16[128,6,2,256]{3,2,1,0:T(2,128)(2,1)}, u32[]{:S(2)}) copy-start(bf16[128,6,2,256]{3,2,1,0:T(2,128)(2,1)} %param.6) | copy-start | bytes 2359300
  6.7 1.9 %copy-start.2 = (bf16[256,6,2,512]{3,0,1,2:T(8,128)(2,1)S(1)}, bf16[256,6,2,512]{3,0,1,2:T(8,128)(2,1)}, u32[]{:S(2)}) copy-start(bf16[256,6,2,512]{3,0,1,2:T(8,128)(2,1)} %copy.33) | copy-start | bytes 9437188
  7.2 4.7 %copy-start.3 = (f32[256,2,512]{2,1,0:T(2,128)S(1)}, f32[256,2,512]{2,1,0:T(2,128)}, u32[]{:S(2)}) copy-start(f32[256,2,512]{2,1,0:T(2,128)} %param.7) | copy-start | bytes 3145732
  9.2 6.8 %collective-permute-start.1 = (bf16[128,512]{1,0:T(8,128)(2,1)S(1)}, bf16[128,512]{1,0:T(8,128)(2,1)S(1)}, u32[]{:S(2)}, u32[]{:S(2)}) collective-permute-start(bf16[128,512]{1,0:T(8,128)(2,1)S(1)} %dynamic-slice_convert_fusion.1), channel_id=1, source_target_pairs={{0,4},{4,0},{8,12},{12,8},{1,5},{5,1},{9,13},{13,9},{2,6},{6,2},{1... | collective-permute-start | bytes 393224 | tf_op jit(solution)/shard_map/ppermute | solution.py:23
  13.5 5.6 %collective-permute-start.6 = (bf16[128,512]{1,0:T(8,128)(2,1)S(1)}, bf16[128,512]{1,0:T(8,128)(2,1)S(1)}, u32[]{:S(2)}, u32[]{:S(2)}) collective-permute-start(bf16[128,512]{1,0:T(8,128)(2,1)S(1)} %dynamic-slice_convert_fusion), channel_id=1, source_target_pairs={{0,4},{4,0},{8,12},{12,8},{1,5},{5,1},{9,13},{13,9},{2,6},{6,2},{1... | collective-permute-start | bytes 393224 | tf_op jit(solution)/shard_map/ppermute | solution.py:23
  16.1 12.9 %collective-permute-start.2 = (bf16[128,512]{1,0:T(8,128)(2,1)S(1)}, bf16[128,512]{1,0:T(8,128)(2,1)S(1)}, u32[]{:S(2)}, u32[]{:S(2)}) collective-permute-start(bf16[128,512]{1,0:T(8,128)(2,1)S(1)} %fusion.26), channel_id=1, source_target_pairs={{0,8},{4,12},{8,0},{12,4},{1,9},{5,13},{9,1},{13,5},{2,10},{6,14},... | collective-permute-start | bytes 393224 | tf_op jit(solution)/shard_map/ppermute | solution.py:30
  19.1 11.7 %collective-permute-start.7 = (bf16[128,512]{1,0:T(8,128)(2,1)S(1)}, bf16[128,512]{1,0:T(8,128)(2,1)S(1)}, u32[]{:S(2)}, u32[]{:S(2)}) collective-permute-start(bf16[128,512]{1,0:T(8,128)(2,1)S(1)} %fusion.27), channel_id=1, source_target_pairs={{0,8},{4,12},{8,0},{12,4},{1,9},{5,13},{9,1},{13,5},{2,10},{6,14},... | collective-permute-start | bytes 393224 | tf_op jit(solution)/shard_map/ppermute | solution.py:30
  29.1 6.3 %collective-permute-start.3 = (bf16[128,512]{1,0:T(8,128)(2,1)S(1)}, bf16[128,512]{1,0:T(8,128)(2,1)S(1)}, u32[]{:S(2)}, u32[]{:S(2)}) collective-permute-start(bf16[128,512]{1,0:T(8,128)(2,1)S(1)} %fusion.21), channel_id=1, source_target_pairs={{0,4},{4,0},{8,12},{12,8},{1,5},{5,1},{9,13},{13,9},{2,6},{6,2},{1... | collective-permute-start | bytes 393224 | tf_op jit(solution)/shard_map/ppermute | solution.py:40
  30.9 5.8 %collective-permute-start.8 = (bf16[128,512]{1,0:T(8,128)(2,1)S(1)}, bf16[128,512]{1,0:T(8,128)(2,1)S(1)}, u32[]{:S(2)}, u32[]{:S(2)}) collective-permute-start(bf16[128,512]{1,0:T(8,128)(2,1)S(1)} %fusion.20), channel_id=1, source_target_pairs={{0,4},{4,0},{8,12},{12,8},{1,5},{5,1},{9,13},{13,9},{2,6},{6,2},{1... | collective-permute-start | bytes 393224 | tf_op jit(solution)/shard_map/ppermute | solution.py:40
  36.0 3.9 %collective-permute-start.5 = (bf16[6,256,256]{2,1,0:T(8,128)(2,1)S(1)}, bf16[6,256,256]{2,1,0:T(8,128)(2,1)S(1)}, u32[]{:S(2)}, u32[]{:S(2)}) collective-permute-start(bf16[6,256,256]{2,1,0:T(8,128)(2,1)S(1)} %fusion.12), channel_id=1, source_target_pairs={{0,1},{1,0},{2,3},{3,2},{4,5},{5,4},{6,7},{7,6},{8,9},{9,8},{10,11... | collective-permute-start | bytes 2359304 | tf_op jit(solution)/shard_map/ppermute | solution.py:8
  37.4 2.8 %collective-permute-start.9 = (bf16[6,256,256]{2,1,0:T(8,128)(2,1)S(1)}, bf16[6,256,256]{2,1,0:T(8,128)(2,1)S(1)}, u32[]{:S(2)}, u32[]{:S(2)}) collective-permute-start(bf16[6,256,256]{2,1,0:T(8,128)(2,1)S(1)} %fusion.15), channel_id=1, source_target_pairs={{0,1},{1,0},{2,3},{3,2},{4,5},{5,4},{6,7},{7,6},{8,9},{9,8},{10,11... | collective-permute-start | bytes 2359304 | tf_op jit(solution)/shard_map/ppermute | solution.py:8
  37.5 2.4 %collective-permute-start.4 = (bf16[256,128]{1,0:T(8,128)(2,1)S(1)}, bf16[256,128]{1,0:T(8,128)(2,1)S(1)}, u32[]{:S(2)}, u32[]{:S(2)}) collective-permute-start(bf16[256,128]{1,0:T(8,128)(2,1)S(1)} %constant_dynamic-slice_fusion.2), channel_id=1, source_target_pairs={{0,1},{1,0},{2,3},{3,2},{4,5},{5,4},{6,7},{7,6},{8,9},{9,8},{10,11... | collective-permute-start | bytes 196616 | tf_op jit(solution)/shard_map/ppermute | solution.py:8

commit v24 on v20

--- a/solution.py
+++ b/solution.py
@@ -98,7 +98,7 @@
             "mrn,nc->mrc", scaled, col_factor, preferred_element_type=jnp.float32
         ).astype(jnp.bfloat16)
         n_m = projected.shape[0]
-        cuts = [i * n_m // 3 for i in range(4)]
+        cuts = [0, n_m]
         chunks = [(lo, hi) for lo, hi in zip(cuts[:-1], cuts[1:]) if lo < hi]
         summed = jnp.einsum("rk,mrc->kmc", rf_own, projected, preferred_element_type=jnp.float32)
         other = []

time: 43.6 us -> 42.5 us (0.975)
  starting transfers between devices: 11.7 us -> 10.3 us
  waiting for transfers between devices: 15.9 us -> 17 us
  matrix products: 5.49 us -> 4.81 us
    ppermute x7 -> x3, starting transfers between devices: 2.23 us -> 0.82 us  [_swap(): return lax.ppermute(x, axis, [(0, 1), (1, 0)])]
    ppermute x7 -> x3, waiting for transfers between devices: 1.1 us -> 1.81 us  [_swap(): return lax.ppermute(x, axis, [(0, 1), (1, 0)])]
    dot_general x6 -> x2, matrix products: 1.29 us -> 0.6 us  [local(): jnp.einsum('rk,mrc->kmc', rf_other, projected[lo:hi], preferred_element_t...]
  transfers between devices with their start and end apart: 13 -> 9, of which waited for: 9 -> 8; matrix products, arithmetic and copies ran while one was open for 22% -> 21% of each run, Pallas kernels for 0% -> 0%
where the time goes in v24:
time: 42.5 us; the launch traced here: 42.3 us
  waiting for transfers between devices  17 us (40%)
  starting transfers between devices  10.3 us (24%)
  local copies, waits for them, and re-layouts  9.42 us (22%)
  matrix products  4.81 us (11%)
  other arithmetic  0.63 us (1%)
    ppermute x4, waiting for transfers between devices, _reduce_scatter_rows(): recv = lax.ppermute(send, axis, [(i, i ^ d) for i in range(size)])  11 us
    ppermute x4, starting transfers between devices, _reduce_scatter_rows(): recv = lax.ppermute(send, axis, [(i, i ^ d) for i in range(size)])  8.85 us
    unnamed x12, local copies, waits for them, and re-layouts  6.83 us
    ppermute x2, waiting for transfers between devices, _all_gather_rows(): recv = lax.ppermute(x, axis, [(i, i ^ d) for i in range(size)])  4.18 us
    ppermute x3, waiting for transfers between devices, _swap(): return lax.ppermute(x, axis, [(0, 1), (1, 0)])  1.81 us
    convert_element_type x1, local copies, waits for them, and re-layouts, local(): (control.astype(jnp.float32) + jnp.stack(outs, axis=2)).astype(jnp.bfloat16)  1.69 us
    dot_general x2, matrix products, local(): jnp.einsum('mrc,nc->mrn', expanded, cf_next, preferred_element_type=jnp.f...  1.32 us
    dot_general x2, matrix products, local(): jnp.einsum('mrn,nc->mrc', scaled, col_factor, preferred_element_type=jnp....  1.16 us
  transfers between devices with their start and end apart: 9, of which 8 were waited for; matrix products, arithmetic and copies ran while one was open for 21% of the time, Pallas kernels for 0%

profile of v24, /device:TPU:0, one launch (start us, length us, event | category | flops | bytes accessed | tf_op | source)
XLA Modules:
  0.0 42.3 jit_solution(8027895530537379627)
XLA Ops:
  0.0 1.3 %copy.8 = bf16[128,6,2,256]{3,0,2,1:T(8,128)(2,1)S(1)} copy(bf16[128,6,2,256]{3,2,1,0:T(2,128)(2,1)} %param.6) | data formatting | bytes 1572864 | tf_op args[1]
  1.3 0.5 %collective-permute-start = (bf16[128,6,2,256]{3,0,2,1:T(8,128)(2,1)S(1)}, bf16[128,6,2,256]{3,0,2,1:T(8,128)(2,1)S(1)}, u32[]{:S(2)}, u32[]{:S(2)}) collective-permute-start(bf16[128,6,2,256]{3,0,2,1:T(8,128)(2,1)S(1)} %copy.8), channel_id=1, source_target_pairs={{0,1},{1,0},{2,3},{3,2},{4,5},{5,4},{6,7},{7,6},{8,9},{9,8},{10,11... | collective-permute-start | bytes 2359304 | tf_op jit(solution)/shard_map/ppermute | solution.py:8
  1.8 4.3 %copy.33 = bf16[256,6,2,512]{3,0,1,2:T(8,128)(2,1)} copy(bf16[256,6,2,512]{3,2,1,0:T(2,128)(2,1)} %param.5) | data formatting | bytes 6291456 | tf_op args[0]
  6.1 0.6 %fusion.29 = f32[256,6,2,256]{3,0,2,1:T(8,128)S(1)} fusion(bf16[256,256]{1,0:T(8,128)(2,1)S(1)} %copy-done.3, s32[]{:T(128)S(6)} %select_n.57, bf16[128,6,2,256]{3,2,1,0:T(2,128)(2,1)S(1)} %copy-done.1), kind=kOutput, calls=%fused_computation.48 | convolution fusion | flops 201326592 | bytes 3997700 | tf_op jit(solution)/shard_map/rk,kmlc->lmrc/dot_general | solution.py:71
  6.7 0.6 %fusion.11 = bf16[2,6,256,256]{3,2,0,1:T(8,128)(2,1)S(1)} fusion(f32[256,6,2,256]{3,0,2,1:T(8,128)S(1)} %fusion.29, bf16[128,6,2,256]{3,0,2,1:T(8,128)(2,1)S(1)} %collective-permute-done, bf16[256,256]{1,0:T(8,128)(2,1)S(1)} %copy-done.3, s32[]{:T(128)S(6)} %select_n.60), kind=kOutput, calls=%fused_computation.18 | convolution fusion | flops 202899456 | bytes 5570564 | tf_op jit(solution)/shard_map/rk,kmlc->lmrc/dot_general | solution.py:72
  7.3 1.3 %copy-done.2 = bf16[256,6,2,512]{3,0,1,2:T(8,128)(2,1)S(1)} copy-done((bf16[256,6,2,512]{3,0,1,2:T(8,128)(2,1)S(1)}, bf16[256,6,2,512]{3,0,1,2:T(8,128)(2,1)}, u32[]{:S(2)}) %copy-start.2) | copy-done | bytes 3145752
  8.5 0.7 %fusion = f32[256,512]{1,0:T(8,128)S(1)} fusion(bf16[2,6,256,512]{3,2,1,0:T(8,128)(2,1)S(1)} %bitcast.77, bf16[2,6,256,256]{3,2,0,1:T(8,128)(2,1)S(1)} %fusion.11, bf16[512,256]{1,0:T(8,128)(2,1)S(1)} %copy-done), kind=kOutput, calls=%fused_computation.4 | convolution fusion | flops 404881408 | bytes 3145728 | tf_op jit(solution)/shard_map/mrc,nc->mrn/dot_general | solution.py:84
  9.2 2.7 %collective-permute-start.1 = (bf16[128,512]{1,0:T(8,128)(2,1)S(1)}, bf16[128,512]{1,0:T(8,128)(2,1)S(1)}, u32[]{:S(2)}, u32[]{:S(2)}) collective-permute-start(bf16[128,512]{1,0:T(8,128)(2,1)S(1)} %dynamic-slice_convert_fusion.1), channel_id=1, source_target_pairs={{0,4},{4,0},{8,12},{12,8},{1,5},{5,1},{9,13},{13,9},{2,6},{6,2},{1... | collective-permute-start | bytes 393224 | tf_op jit(solution)/shard_map/ppermute | solution.py:23
  11.9 0.8 %fusion.50 = (f32[1,256,512]{2,0,1:T(1,128)S(1)}, f32[1,256,512]{2,0,1:T(1,128)S(1)}) fusion(f32[2,256,512]{2,0,1:T(2,128)S(1)} %bitcast.81), kind=kLoop, calls=%fused_computation.71 | loop fusion | bytes 2097152 | tf_op jit(solution)/shard_map/slice | solution.py:89
  12.7 0.7 %fusion.2 = f32[256,512]{1,0:T(8,128)S(1)} fusion(bf16[2,6,256,512]{3,2,1,0:T(8,128)(2,1)S(1)} %bitcast.78, bf16[2,6,256,256]{3,2,0,1:T(8,128)(2,1)S(1)} %fusion.11, bf16[512,256]{1,0:T(8,128)(2,1)S(1)} %copy-done), kind=kOutput, calls=%fused_computation.6 | convolution fusion | flops 404881408 | bytes 3145728 | tf_op jit(solution)/shard_map/mrc,nc->mrn/dot_general | solution.py:84
  13.6 2.4 %collective-permute-done.1 = bf16[128,512]{1,0:T(8,128)(2,1)S(1)} collective-permute-done((bf16[128,512]{1,0:T(8,128)(2,1)S(1)}, bf16[128,512]{1,0:T(8,128)(2,1)S(1)}, u32[]{:S(2)}, u32[]{:S(2)}) %collective-permute-start.1) | collective-permute-done | bytes 131104 | tf_op jit(solution)/shard_map/ppermute | solution.py:23
  16.1 2.8 %collective-permute-start.2 = (bf16[128,512]{1,0:T(8,128)(2,1)S(1)}, bf16[128,512]{1,0:T(8,128)(2,1)S(1)}, u32[]{:S(2)}, u32[]{:S(2)}) collective-permute-start(bf16[128,512]{1,0:T(8,128)(2,1)S(1)} %fusion.26), channel_id=1, source_target_pairs={{0,8},{4,12},{8,0},{12,4},{1,9},{5,13},{9,1},{13,5},{2,10},{6,14},... | collective-permute-start | bytes 393224 | tf_op jit(solution)/shard_map/ppermute | solution.py:30
  19.1 3.2 %collective-permute-start.6 = (bf16[128,512]{1,0:T(8,128)(2,1)S(1)}, bf16[128,512]{1,0:T(8,128)(2,1)S(1)}, u32[]{:S(2)}, u32[]{:S(2)}) collective-permute-start(bf16[128,512]{1,0:T(8,128)(2,1)S(1)} %fusion.27), channel_id=1, source_target_pairs={{0,8},{4,12},{8,0},{12,4},{1,9},{5,13},{9,1},{13,5},{2,10},{6,14},... | collective-permute-start | bytes 393224 | tf_op jit(solution)/shard_map/ppermute | solution.py:30
  22.4 6.6 %collective-permute-done.2 = bf16[128,512]{1,0:T(8,128)(2,1)S(1)} collective-permute-done((bf16[128,512]{1,0:T(8,128)(2,1)S(1)}, bf16[128,512]{1,0:T(8,128)(2,1)S(1)}, u32[]{:S(2)}, u32[]{:S(2)}) %collective-permute-start.2) | collective-permute-done | bytes 131104 | tf_op jit(solution)/shard_map/ppermute | solution.py:30
  29.1 1.7 %collective-permute-done.6 = bf16[128,512]{1,0:T(8,128)(2,1)S(1)} collective-permute-done((bf16[128,512]{1,0:T(8,128)(2,1)S(1)}, bf16[128,512]{1,0:T(8,128)(2,1)S(1)}, u32[]{:S(2)}, u32[]{:S(2)}) %collective-permute-start.6) | collective-permute-done | bytes 131104 | tf_op jit(solution)/shard_map/ppermute | solution.py:30
  30.9 0.6 %collective-permute-start.7 = (bf16[128,512]{1,0:T(8,128)(2,1)S(1)}, bf16[128,512]{1,0:T(8,128)(2,1)S(1)}, u32[]{:S(2)}, u32[]{:S(2)}) collective-permute-start(bf16[128,512]{1,0:T(8,128)(2,1)S(1)} %fusion.20), channel_id=1, source_target_pairs={{0,4},{4,0},{8,12},{12,8},{1,5},{5,1},{9,13},{13,9},{2,6},{6,2},{1... | collective-permute-start | bytes 393224 | tf_op jit(solution)/shard_map/ppermute | solution.py:40
  31.5 3.8 %collective-permute-done.3 = bf16[128,512]{1,0:T(8,128)(2,1)S(1)} collective-permute-done((bf16[128,512]{1,0:T(8,128)(2,1)S(1)}, bf16[128,512]{1,0:T(8,128)(2,1)S(1)}, u32[]{:S(2)}, u32[]{:S(2)}) %collective-permute-start.3) | collective-permute-done | bytes 131104 | tf_op jit(solution)/shard_map/ppermute | solution.py:40
  35.4 0.6 %fusion.12 = bf16[6,256,256]{2,1,0:T(8,128)(2,1)S(1)} fusion(f32[256,512]{1,0:T(8,128)S(1)} %maximum_convert_fusion, bf16[2,6,256,512]{3,2,1,0:T(8,128)(2,1)S(1)} %bitcast.79, bf16[512,256]{1,0:T(8,128)(2,1)S(1)} %copy-done), kind=kOutput, calls=%fused_computation.19 | convolution fusion | flops 405405696 | bytes 3145728 | tf_op jit(solution)/shard_map/mrn,nc->mrc/dot_general | solution.py:97
  36.0 0.3 fusion.33
  36.4 0.3 collective-permute-done.7
  36.8 0.6 %fusion.15 = bf16[6,256,256]{2,1,0:T(8,128)(2,1)S(1)} fusion(f32[256,512]{1,0:T(8,128)S(1)} %maximum_convert_fusion.1, bf16[2,6,256,512]{3,2,1,0:T(8,128)(2,1)S(1)} %bitcast.80, bf16[512,256]{1,0:T(8,128)(2,1)S(1)} %copy-done), kind=kOutput, calls=%fused_computation.20 | convolution fusion | flops 405405696 | bytes 3145728 | tf_op jit(solution)/shard_map/mrn,nc->mrc/dot_general | solution.py:97
  37.9 0.7 %collective-permute-done.4 = f32[128,6,256]{2,0,1:T(8,128)S(1)} collective-permute-done((f32[128,6,256]{2,0,1:T(8,128)S(1)}, f32[128,6,256]{2,0,1:T(8,128)S(1)}, u32[]{:S(2)}, u32[]{:S(2)}) %collective-permute-start.4) | collective-permute-done | bytes 786464 | tf_op jit(solution)/shard_map/ppermute | solution.py:8
  39.0 1.1 %collective-permute-done.8 = f32[128,6,256]{2,0,1:T(8,128)S(1)} collective-permute-done((f32[128,6,256]{2,0,1:T(8,128)S(1)}, f32[128,6,256]{2,0,1:T(8,128)S(1)}, u32[]{:S(2)}, u32[]{:S(2)}) %collective-permute-start.8) | collective-permute-done | bytes 786464 | tf_op jit(solution)/shard_map/ppermute | solution.py:8
  40.6 1.7 %copy.14 = bf16[128,6,2,256]{3,2,1,0:T(2,128)(2,1)} copy(bf16[128,6,2,256]{3,0,1,2:T(8,128)(2,1)S(1)} %fusion.8) | data formatting | bytes 1572864 | tf_op jit(solution)/shard_map/convert_element_type | solution.py:112
  (31 shorter events, 2.3 us)
Async XLA Ops:
  0.0 7.3 %copy-start = (bf16[512,256]{1,0:T(8,128)(2,1)S(1)}, bf16[512,256]{1,0:T(8,128)(2,1)}, u32[]{:S(2)}) copy-start(bf16[512,256]{1,0:T(8,128)(2,1)} %param.9) | copy-start | bytes 786436
  1.3 5.3 %collective-permute-start = (bf16[128,6,2,256]{3,0,2,1:T(8,128)(2,1)S(1)}, bf16[128,6,2,256]{3,0,2,1:T(8,128)(2,1)S(1)}, u32[]{:S(2)}, u32[]{:S(2)}) collective-permute-start(bf16[128,6,2,256]{3,0,2,1:T(8,128)(2,1)S(1)} %copy.8), channel_id=1, source_target_pairs={{0,1},{1,0},{2,3},{3,2},{4,5},{5,4},{6,7},{7,6},{8,9},{9,8},{10,11... | collective-permute-start | bytes 2359304 | tf_op jit(solution)/shard_map/ppermute | solution.py:8
  1.8 4.3 %copy-start.1 = (bf16[128,6,2,256]{3,2,1,0:T(2,128)(2,1)S(1)}, bf16[128,6,2,256]{3,2,1,0:T(2,128)(2,1)}, u32[]{:S(2)}) copy-start(bf16[128,6,2,256]{3,2,1,0:T(2,128)(2,1)} %param.6) | copy-start | bytes 2359300
  1.8 4.3 %copy-start.3 = (bf16[256,256]{1,0:T(8,128)(2,1)S(1)}, bf16[256,256]{1,0:T(8,128)(2,1)}, u32[]{:S(2)}) copy-start(bf16[256,256]{1,0:T(8,128)(2,1)} %param.8) | copy-start | bytes 393220
  6.6 1.9 %copy-start.2 = (bf16[256,6,2,512]{3,0,1,2:T(8,128)(2,1)S(1)}, bf16[256,6,2,512]{3,0,1,2:T(8,128)(2,1)}, u32[]{:S(2)}) copy-start(bf16[256,6,2,512]{3,0,1,2:T(8,128)(2,1)} %copy.33) | copy-start | bytes 9437188
  7.2 4.7 %copy-start.4 = (f32[256,2,512]{2,1,0:T(2,128)S(1)}, f32[256,2,512]{2,1,0:T(2,128)}, u32[]{:S(2)}) copy-start(f32[256,2,512]{2,1,0:T(2,128)} %param.7) | copy-start | bytes 3145732
  9.2 6.8 %collective-permute-start.1 = (bf16[128,512]{1,0:T(8,128)(2,1)S(1)}, bf16[128,512]{1,0:T(8,128)(2,1)S(1)}, u32[]{:S(2)}, u32[]{:S(2)}) collective-permute-start(bf16[128,512]{1,0:T(8,128)(2,1)S(1)} %dynamic-slice_convert_fusion.1), channel_id=1, source_target_pairs={{0,4},{4,0},{8,12},{12,8},{1,5},{5,1},{9,13},{13,9},{2,6},{6,2},{1... | collective-permute-start | bytes 393224 | tf_op jit(solution)/shard_map/ppermute | solution.py:23
  13.4 5.6 %collective-permute-start.5 = (bf16[128,512]{1,0:T(8,128)(2,1)S(1)}, bf16[128,512]{1,0:T(8,128)(2,1)S(1)}, u32[]{:S(2)}, u32[]{:S(2)}) collective-permute-start(bf16[128,512]{1,0:T(8,128)(2,1)S(1)} %dynamic-slice_convert_fusion), channel_id=1, source_target_pairs={{0,4},{4,0},{8,12},{12,8},{1,5},{5,1},{9,13},{13,9},{2,6},{6,2},{1... | collective-permute-start | bytes 393224 | tf_op jit(solution)/shard_map/ppermute | solution.py:23
  16.1 12.9 %collective-permute-start.2 = (bf16[128,512]{1,0:T(8,128)(2,1)S(1)}, bf16[128,512]{1,0:T(8,128)(2,1)S(1)}, u32[]{:S(2)}, u32[]{:S(2)}) collective-permute-start(bf16[128,512]{1,0:T(8,128)(2,1)S(1)} %fusion.26), channel_id=1, source_target_pairs={{0,8},{4,12},{8,0},{12,4},{1,9},{5,13},{9,1},{13,5},{2,10},{6,14},... | collective-permute-start | bytes 393224 | tf_op jit(solution)/shard_map/ppermute | solution.py:30
  19.1 11.7 %collective-permute-start.6 = (bf16[128,512]{1,0:T(8,128)(2,1)S(1)}, bf16[128,512]{1,0:T(8,128)(2,1)S(1)}, u32[]{:S(2)}, u32[]{:S(2)}) collective-permute-start(bf16[128,512]{1,0:T(8,128)(2,1)S(1)} %fusion.27), channel_id=1, source_target_pairs={{0,8},{4,12},{8,0},{12,4},{1,9},{5,13},{9,1},{13,5},{2,10},{6,14},... | collective-permute-start | bytes 393224 | tf_op jit(solution)/shard_map/ppermute | solution.py:30
  29.1 6.3 %collective-permute-start.3 = (bf16[128,512]{1,0:T(8,128)(2,1)S(1)}, bf16[128,512]{1,0:T(8,128)(2,1)S(1)}, u32[]{:S(2)}, u32[]{:S(2)}) collective-permute-start(bf16[128,512]{1,0:T(8,128)(2,1)S(1)} %fusion.21), channel_id=1, source_target_pairs={{0,4},{4,0},{8,12},{12,8},{1,5},{5,1},{9,13},{13,9},{2,6},{6,2},{1... | collective-permute-start | bytes 393224 | tf_op jit(solution)/shard_map/ppermute | solution.py:40
  30.9 5.8 %collective-permute-start.7 = (bf16[128,512]{1,0:T(8,128)(2,1)S(1)}, bf16[128,512]{1,0:T(8,128)(2,1)S(1)}, u32[]{:S(2)}, u32[]{:S(2)}) collective-permute-start(bf16[128,512]{1,0:T(8,128)(2,1)S(1)} %fusion.20), channel_id=1, source_target_pairs={{0,4},{4,0},{8,12},{12,8},{1,5},{5,1},{9,13},{13,9},{2,6},{6,2},{1... | collective-permute-start | bytes 393224 | tf_op jit(solution)/shard_map/ppermute | solution.py:40
  36.3 2.4 %collective-permute-start.4 = (f32[128,6,256]{2,0,1:T(8,128)S(1)}, f32[128,6,256]{2,0,1:T(8,128)S(1)}, u32[]{:S(2)}, u32[]{:S(2)}) collective-permute-start(f32[128,6,256]{2,0,1:T(8,128)S(1)} %fusion.33), channel_id=1, source_target_pairs={{0,1},{1,0},{2,3},{3,2},{4,5},{5,4},{6,7},{7,6},{8,9},{9,8},{10,11... | collective-permute-start | bytes 2359304 | tf_op jit(solution)/shard_map/ppermute | solution.py:8
  37.7 2.4 %collective-permute-start.8 = (f32[128,6,256]{2,0,1:T(8,128)S(1)}, f32[128,6,256]{2,0,1:T(8,128)S(1)}, u32[]{:S(2)}, u32[]{:S(2)}) collective-permute-start(f32[128,6,256]{2,0,1:T(8,128)S(1)} %fusion.31), channel_id=1, source_target_pairs={{0,1},{1,0},{2,3},{3,2},{4,5},{5,4},{6,7},{7,6},{8,9},{9,8},{10,11... | collective-permute-start | bytes 2359304 | tf_op jit(solution)/shard_map/ppermute | solution.py:8

commit v25 on v24

--- a/solution.py
+++ b/solution.py
@@ -106,7 +106,7 @@
             for_partner = jnp.einsum(
                 "rk,mrc->kmc", rf_other, projected[lo:hi], preferred_element_type=jnp.float32
             )
-            other.append(_swap(for_partner, "half"))
+            other.append(_swap(for_partner.astype(jnp.bfloat16), "half").astype(jnp.float32))
         summed = summed + jnp.concatenate(other, axis=1)
         outs.append(summed)
     return (control.astype(jnp.float32) + jnp.stack(outs, axis=2)).astype(jnp.bfloat16)

time: 42.5 us -> 41.9 us (0.986)
  waiting for transfers between devices: 17 us -> 16.4 us
    ppermute x3, waiting for transfers between devices: 1.81 us -> 1.26 us  [_swap(): return lax.ppermute(x, axis, [(0, 1), (1, 0)])]
where the time goes in v25:
time: 41.9 us; the launch traced here: 41.8 us
  waiting for transfers between devices  16.4 us (39%)
  starting transfers between devices  10.3 us (25%)
  local copies, waits for them, and re-layouts  9.42 us (22%)
  matrix products  4.82 us (12%)
  other arithmetic  0.62 us (1%)
    ppermute x4, waiting for transfers between devices, _reduce_scatter_rows(): recv = lax.ppermute(send, axis, [(i, i ^ d) for i in range(size)])  11 us
    ppermute x4, starting transfers between devices, _reduce_scatter_rows(): recv = lax.ppermute(send, axis, [(i, i ^ d) for i in range(size)])  8.85 us
    unnamed x12, local copies, waits for them, and re-layouts  6.83 us
    ppermute x2, waiting for transfers between devices, _all_gather_rows(): recv = lax.ppermute(x, axis, [(i, i ^ d) for i in range(size)])  4.18 us
    convert_element_type x1, local copies, waits for them, and re-layouts, local(): (control.astype(jnp.float32) + jnp.stack(outs, axis=2)).astype(jnp.bfloat16)  1.69 us
    dot_general x2, matrix products, local(): jnp.einsum('mrc,nc->mrn', expanded, cf_next, preferred_element_type=jnp.f...  1.32 us
    ppermute x3, waiting for transfers between devices, _swap(): return lax.ppermute(x, axis, [(0, 1), (1, 0)])  1.26 us
    dot_general x2, matrix products, local(): jnp.einsum('mrn,nc->mrc', scaled, col_factor, preferred_element_type=jnp....  1.17 us
  transfers between devices with their start and end apart: 9, of which 8 were waited for; matrix products, arithmetic and copies ran while one was open for 21% of the time, Pallas kernels for 0%

profile of v25, /device:TPU:0, one launch (start us, length us, event | category | flops | bytes accessed | tf_op | source)
XLA Modules:
  0.0 41.8 jit_solution(3387441551011774498)
XLA Ops:
  0.0 1.3 %copy.8 = bf16[128,6,2,256]{3,0,2,1:T(8,128)(2,1)S(1)} copy(bf16[128,6,2,256]{3,2,1,0:T(2,128)(2,1)} %param.6) | data formatting | bytes 1572864 | tf_op args[1]
  1.3 0.5 %collective-permute-start = (bf16[128,6,2,256]{3,0,2,1:T(8,128)(2,1)S(1)}, bf16[128,6,2,256]{3,0,2,1:T(8,128)(2,1)S(1)}, u32[]{:S(2)}, u32[]{:S(2)}) collective-permute-start(bf16[128,6,2,256]{3,0,2,1:T(8,128)(2,1)S(1)} %copy.8), channel_id=1, source_target_pairs={{0,1},{1,0},{2,3},{3,2},{4,5},{5,4},{6,7},{7,6},{8,9},{9,8},{10,11... | collective-permute-start | bytes 2359304 | tf_op jit(solution)/shard_map/ppermute | solution.py:8
  1.8 4.3 %copy.33 = bf16[256,6,2,512]{3,0,1,2:T(8,128)(2,1)} copy(bf16[256,6,2,512]{3,2,1,0:T(2,128)(2,1)} %param.5) | data formatting | bytes 6291456 | tf_op args[0]
  6.1 0.6 %fusion.27 = f32[256,6,2,256]{3,0,2,1:T(8,128)S(1)} fusion(bf16[256,256]{1,0:T(8,128)(2,1)S(1)} %copy-done.3, s32[]{:T(128)S(6)} %select_n.57, bf16[128,6,2,256]{3,2,1,0:T(2,128)(2,1)S(1)} %copy-done.1), kind=kOutput, calls=%fused_computation.48 | convolution fusion | flops 201326592 | bytes 3997700 | tf_op jit(solution)/shard_map/rk,kmlc->lmrc/dot_general | solution.py:71
  6.7 0.6 %fusion.11 = bf16[2,6,256,256]{3,2,0,1:T(8,128)(2,1)S(1)} fusion(f32[256,6,2,256]{3,0,2,1:T(8,128)S(1)} %fusion.27, bf16[128,6,2,256]{3,0,2,1:T(8,128)(2,1)S(1)} %collective-permute-done, bf16[256,256]{1,0:T(8,128)(2,1)S(1)} %copy-done.3, s32[]{:T(128)S(6)} %select_n.60), kind=kOutput, calls=%fused_computation.18 | convolution fusion | flops 202899456 | bytes 5570564 | tf_op jit(solution)/shard_map/rk,kmlc->lmrc/dot_general | solution.py:72
  7.3 1.3 %copy-done.2 = bf16[256,6,2,512]{3,0,1,2:T(8,128)(2,1)S(1)} copy-done((bf16[256,6,2,512]{3,0,1,2:T(8,128)(2,1)S(1)}, bf16[256,6,2,512]{3,0,1,2:T(8,128)(2,1)}, u32[]{:S(2)}) %copy-start.2) | copy-done | bytes 3145752
  8.5 0.7 %fusion = f32[256,512]{1,0:T(8,128)S(1)} fusion(bf16[2,6,256,512]{3,2,1,0:T(8,128)(2,1)S(1)} %bitcast.81, bf16[2,6,256,256]{3,2,0,1:T(8,128)(2,1)S(1)} %fusion.11, bf16[512,256]{1,0:T(8,128)(2,1)S(1)} %copy-done), kind=kOutput, calls=%fused_computation.4 | convolution fusion | flops 404881408 | bytes 3145728 | tf_op jit(solution)/shard_map/mrc,nc->mrn/dot_general | solution.py:84
  9.2 2.7 %collective-permute-start.1 = (bf16[128,512]{1,0:T(8,128)(2,1)S(1)}, bf16[128,512]{1,0:T(8,128)(2,1)S(1)}, u32[]{:S(2)}, u32[]{:S(2)}) collective-permute-start(bf16[128,512]{1,0:T(8,128)(2,1)S(1)} %dynamic-slice_convert_fusion.1), channel_id=1, source_target_pairs={{0,4},{4,0},{8,12},{12,8},{1,5},{5,1},{9,13},{13,9},{2,6},{6,2},{1... | collective-permute-start | bytes 393224 | tf_op jit(solution)/shard_map/ppermute | solution.py:23
  11.9 0.8 %fusion.52 = (f32[1,256,512]{2,0,1:T(1,128)S(1)}, f32[1,256,512]{2,0,1:T(1,128)S(1)}) fusion(f32[2,256,512]{2,0,1:T(2,128)S(1)} %bitcast.85), kind=kLoop, calls=%fused_computation.71 | loop fusion | bytes 2097152 | tf_op jit(solution)/shard_map/slice | solution.py:89
  12.7 0.7 %fusion.2 = f32[256,512]{1,0:T(8,128)S(1)} fusion(bf16[2,6,256,512]{3,2,1,0:T(8,128)(2,1)S(1)} %bitcast.82, bf16[2,6,256,256]{3,2,0,1:T(8,128)(2,1)S(1)} %fusion.11, bf16[512,256]{1,0:T(8,128)(2,1)S(1)} %copy-done), kind=kOutput, calls=%fused_computation.6 | convolution fusion | flops 404881408 | bytes 3145728 | tf_op jit(solution)/shard_map/mrc,nc->mrn/dot_general | solution.py:84
  13.6 2.4 %collective-permute-done.1 = bf16[128,512]{1,0:T(8,128)(2,1)S(1)} collective-permute-done((bf16[128,512]{1,0:T(8,128)(2,1)S(1)}, bf16[128,512]{1,0:T(8,128)(2,1)S(1)}, u32[]{:S(2)}, u32[]{:S(2)}) %collective-permute-start.1) | collective-permute-done | bytes 131104 | tf_op jit(solution)/shard_map/ppermute | solution.py:23
  16.1 2.8 %collective-permute-start.2 = (bf16[128,512]{1,0:T(8,128)(2,1)S(1)}, bf16[128,512]{1,0:T(8,128)(2,1)S(1)}, u32[]{:S(2)}, u32[]{:S(2)}) collective-permute-start(bf16[128,512]{1,0:T(8,128)(2,1)S(1)} %fusion.24), channel_id=1, source_target_pairs={{0,8},{4,12},{8,0},{12,4},{1,9},{5,13},{9,1},{13,5},{2,10},{6,14},... | collective-permute-start | bytes 393224 | tf_op jit(solution)/shard_map/ppermute | solution.py:30
  19.1 3.2 %collective-permute-start.6 = (bf16[128,512]{1,0:T(8,128)(2,1)S(1)}, bf16[128,512]{1,0:T(8,128)(2,1)S(1)}, u32[]{:S(2)}, u32[]{:S(2)}) collective-permute-start(bf16[128,512]{1,0:T(8,128)(2,1)S(1)} %fusion.25), channel_id=1, source_target_pairs={{0,8},{4,12},{8,0},{12,4},{1,9},{5,13},{9,1},{13,5},{2,10},{6,14},... | collective-permute-start | bytes 393224 | tf_op jit(solution)/shard_map/ppermute | solution.py:30
  22.4 6.6 %collective-permute-done.2 = bf16[128,512]{1,0:T(8,128)(2,1)S(1)} collective-permute-done((bf16[128,512]{1,0:T(8,128)(2,1)S(1)}, bf16[128,512]{1,0:T(8,128)(2,1)S(1)}, u32[]{:S(2)}, u32[]{:S(2)}) %collective-permute-start.2) | collective-permute-done | bytes 131104 | tf_op jit(solution)/shard_map/ppermute | solution.py:30
  29.1 1.7 %collective-permute-done.6 = bf16[128,512]{1,0:T(8,128)(2,1)S(1)} collective-permute-done((bf16[128,512]{1,0:T(8,128)(2,1)S(1)}, bf16[128,512]{1,0:T(8,128)(2,1)S(1)}, u32[]{:S(2)}, u32[]{:S(2)}) %collective-permute-start.6) | collective-permute-done | bytes 131104 | tf_op jit(solution)/shard_map/ppermute | solution.py:30
  30.9 0.6 %collective-permute-start.7 = (bf16[128,512]{1,0:T(8,128)(2,1)S(1)}, bf16[128,512]{1,0:T(8,128)(2,1)S(1)}, u32[]{:S(2)}, u32[]{:S(2)}) collective-permute-start(bf16[128,512]{1,0:T(8,128)(2,1)S(1)} %fusion.18), channel_id=1, source_target_pairs={{0,4},{4,0},{8,12},{12,8},{1,5},{5,1},{9,13},{13,9},{2,6},{6,2},{1... | collective-permute-start | bytes 393224 | tf_op jit(solution)/shard_map/ppermute | solution.py:40
  31.5 3.8 %collective-permute-done.3 = bf16[128,512]{1,0:T(8,128)(2,1)S(1)} collective-permute-done((bf16[128,512]{1,0:T(8,128)(2,1)S(1)}, bf16[128,512]{1,0:T(8,128)(2,1)S(1)}, u32[]{:S(2)}, u32[]{:S(2)}) %collective-permute-start.3) | collective-permute-done | bytes 131104 | tf_op jit(solution)/shard_map/ppermute | solution.py:40
  35.4 0.6 %fusion.12 = bf16[6,256,256]{2,1,0:T(8,128)(2,1)S(1)} fusion(f32[256,512]{1,0:T(8,128)S(1)} %maximum_convert_fusion, bf16[2,6,256,512]{3,2,1,0:T(8,128)(2,1)S(1)} %bitcast.83, bf16[512,256]{1,0:T(8,128)(2,1)S(1)} %copy-done), kind=kOutput, calls=%fused_computation.19 | convolution fusion | flops 405405696 | bytes 3145728 | tf_op jit(solution)/shard_map/mrn,nc->mrc/dot_general | solution.py:97
  36.0 0.3 convolution_convert_fusion.1
  36.4 0.3 collective-permute-done.7
  36.8 0.6 %fusion.15 = bf16[6,256,256]{2,1,0:T(8,128)(2,1)S(1)} fusion(f32[256,512]{1,0:T(8,128)S(1)} %maximum_convert_fusion.1, bf16[2,6,256,512]{3,2,1,0:T(8,128)(2,1)S(1)} %bitcast.84, bf16[512,256]{1,0:T(8,128)(2,1)S(1)} %copy-done), kind=kOutput, calls=%fused_computation.20 | convolution fusion | flops 405405696 | bytes 3145728 | tf_op jit(solution)/shard_map/mrn,nc->mrc/dot_general | solution.py:97
  37.4 0.3 convolution_convert_fusion
  38.4 1.1 %collective-permute-done.8 = bf16[128,6,256]{2,0,1:T(8,128)(2,1)S(1)} collective-permute-done((bf16[128,6,256]{2,0,1:T(8,128)(2,1)S(1)}, bf16[128,6,256]{2,0,1:T(8,128)(2,1)S(1)}, u32[]{:S(2)}, u32[]{:S(2)}) %collective-permute-start.8) | collective-permute-done | bytes 393248 | tf_op jit(solution)/shard_map/ppermute | solution.py:8
  40.1 1.7 %copy.14 = bf16[128,6,2,256]{3,2,1,0:T(2,128)(2,1)} copy(bf16[128,6,2,256]{3,0,1,2:T(8,128)(2,1)S(1)} %fusion.8) | data formatting | bytes 1572864 | tf_op jit(solution)/shard_map/convert_element_type | solution.py:112
  (31 shorter events, 2.1 us)
Async XLA Ops:
  0.0 7.3 %copy-start = (bf16[512,256]{1,0:T(8,128)(2,1)S(1)}, bf16[512,256]{1,0:T(8,128)(2,1)}, u32[]{:S(2)}) copy-start(bf16[512,256]{1,0:T(8,128)(2,1)} %param.9) | copy-start | bytes 786436
  1.3 5.3 %collective-permute-start = (bf16[128,6,2,256]{3,0,2,1:T(8,128)(2,1)S(1)}, bf16[128,6,2,256]{3,0,2,1:T(8,128)(2,1)S(1)}, u32[]{:S(2)}, u32[]{:S(2)}) collective-permute-start(bf16[128,6,2,256]{3,0,2,1:T(8,128)(2,1)S(1)} %copy.8), channel_id=1, source_target_pairs={{0,1},{1,0},{2,3},{3,2},{4,5},{5,4},{6,7},{7,6},{8,9},{9,8},{10,11... | collective-permute-start | bytes 2359304 | tf_op jit(solution)/shard_map/ppermute | solution.py:8
  1.8 4.3 %copy-start.1 = (bf16[128,6,2,256]{3,2,1,0:T(2,128)(2,1)S(1)}, bf16[128,6,2,256]{3,2,1,0:T(2,128)(2,1)}, u32[]{:S(2)}) copy-start(bf16[128,6,2,256]{3,2,1,0:T(2,128)(2,1)} %param.6) | copy-start | bytes 2359300
  1.8 4.3 %copy-start.3 = (bf16[256,256]{1,0:T(8,128)(2,1)S(1)}, bf16[256,256]{1,0:T(8,128)(2,1)}, u32[]{:S(2)}) copy-start(bf16[256,256]{1,0:T(8,128)(2,1)} %param.8) | copy-start | bytes 393220
  6.6 1.9 %copy-start.2 = (bf16[256,6,2,512]{3,0,1,2:T(8,128)(2,1)S(1)}, bf16[256,6,2,512]{3,0,1,2:T(8,128)(2,1)}, u32[]{:S(2)}) copy-start(bf16[256,6,2,512]{3,0,1,2:T(8,128)(2,1)} %copy.33) | copy-start | bytes 9437188
  7.2 4.7 %copy-start.4 = (f32[256,2,512]{2,1,0:T(2,128)S(1)}, f32[256,2,512]{2,1,0:T(2,128)}, u32[]{:S(2)}) copy-start(f32[256,2,512]{2,1,0:T(2,128)} %param.7) | copy-start | bytes 3145732
  9.2 6.8 %collective-permute-start.1 = (bf16[128,512]{1,0:T(8,128)(2,1)S(1)}, bf16[128,512]{1,0:T(8,128)(2,1)S(1)}, u32[]{:S(2)}, u32[]{:S(2)}) collective-permute-start(bf16[128,512]{1,0:T(8,128)(2,1)S(1)} %dynamic-slice_convert_fusion.1), channel_id=1, source_target_pairs={{0,4},{4,0},{8,12},{12,8},{1,5},{5,1},{9,13},{13,9},{2,6},{6,2},{1... | collective-permute-start | bytes 393224 | tf_op jit(solution)/shard_map/ppermute | solution.py:23
  13.4 5.6 %collective-permute-start.5 = (bf16[128,512]{1,0:T(8,128)(2,1)S(1)}, bf16[128,512]{1,0:T(8,128)(2,1)S(1)}, u32[]{:S(2)}, u32[]{:S(2)}) collective-permute-start(bf16[128,512]{1,0:T(8,128)(2,1)S(1)} %dynamic-slice_convert_fusion), channel_id=1, source_target_pairs={{0,4},{4,0},{8,12},{12,8},{1,5},{5,1},{9,13},{13,9},{2,6},{6,2},{1... | collective-permute-start | bytes 393224 | tf_op jit(solution)/shard_map/ppermute | solution.py:23
  16.1 12.9 %collective-permute-start.2 = (bf16[128,512]{1,0:T(8,128)(2,1)S(1)}, bf16[128,512]{1,0:T(8,128)(2,1)S(1)}, u32[]{:S(2)}, u32[]{:S(2)}) collective-permute-start(bf16[128,512]{1,0:T(8,128)(2,1)S(1)} %fusion.24), channel_id=1, source_target_pairs={{0,8},{4,12},{8,0},{12,4},{1,9},{5,13},{9,1},{13,5},{2,10},{6,14},... | collective-permute-start | bytes 393224 | tf_op jit(solution)/shard_map/ppermute | solution.py:30
  19.1 11.7 %collective-permute-start.6 = (bf16[128,512]{1,0:T(8,128)(2,1)S(1)}, bf16[128,512]{1,0:T(8,128)(2,1)S(1)}, u32[]{:S(2)}, u32[]{:S(2)}) collective-permute-start(bf16[128,512]{1,0:T(8,128)(2,1)S(1)} %fusion.25), channel_id=1, source_target_pairs={{0,8},{4,12},{8,0},{12,4},{1,9},{5,13},{9,1},{13,5},{2,10},{6,14},... | collective-permute-start | bytes 393224 | tf_op jit(solution)/shard_map/ppermute | solution.py:30
  29.1 6.3 %collective-permute-start.3 = (bf16[128,512]{1,0:T(8,128)(2,1)S(1)}, bf16[128,512]{1,0:T(8,128)(2,1)S(1)}, u32[]{:S(2)}, u32[]{:S(2)}) collective-permute-start(bf16[128,512]{1,0:T(8,128)(2,1)S(1)} %fusion.19), channel_id=1, source_target_pairs={{0,4},{4,0},{8,12},{12,8},{1,5},{5,1},{9,13},{13,9},{2,6},{6,2},{1... | collective-permute-start | bytes 393224 | tf_op jit(solution)/shard_map/ppermute | solution.py:40
  30.9 5.8 %collective-permute-start.7 = (bf16[128,512]{1,0:T(8,128)(2,1)S(1)}, bf16[128,512]{1,0:T(8,128)(2,1)S(1)}, u32[]{:S(2)}, u32[]{:S(2)}) collective-permute-start(bf16[128,512]{1,0:T(8,128)(2,1)S(1)} %fusion.18), channel_id=1, source_target_pairs={{0,4},{4,0},{8,12},{12,8},{1,5},{5,1},{9,13},{13,9},{2,6},{6,2},{1... | collective-permute-start | bytes 393224 | tf_op jit(solution)/shard_map/ppermute | solution.py:40
  36.3 1.8 %collective-permute-start.4 = (bf16[128,6,256]{2,0,1:T(8,128)(2,1)S(1)}, bf16[128,6,256]{2,0,1:T(8,128)(2,1)S(1)}, u32[]{:S(2)}, u32[]{:S(2)}) collective-permute-start(bf16[128,6,256]{2,0,1:T(8,128)(2,1)S(1)} %convolution_convert_fusion.1), channel_id=1, source_target_pairs={{0,1},{1,0},{2,3},{3,2},{4,5},{5,4},{6,7},{7,6},{8,9},{9,8},{10,11... | collective-permute-start | bytes 1179656 | tf_op jit(solution)/shard_map/ppermute | solution.py:8
  37.7 1.8 %collective-permute-start.8 = (bf16[128,6,256]{2,0,1:T(8,128)(2,1)S(1)}, bf16[128,6,256]{2,0,1:T(8,128)(2,1)S(1)}, u32[]{:S(2)}, u32[]{:S(2)}) collective-permute-start(bf16[128,6,256]{2,0,1:T(8,128)(2,1)S(1)} %convolution_convert_fusion), channel_id=1, source_target_pairs={{0,1},{1,0},{2,3},{3,2},{4,5},{5,4},{6,7},{7,6},{8,9},{9,8},{10,11... | collective-permute-start | bytes 1179656 | tf_op jit(solution)/shard_map/ppermute | solution.py:8

commit v26 on v24

--- a/solution.py
+++ b/solution.py
@@ -100,7 +100,8 @@
         n_m = projected.shape[0]
         cuts = [0, n_m]
         chunks = [(lo, hi) for lo, hi in zip(cuts[:-1], cuts[1:]) if lo < hi]
-        summed = jnp.einsum("rk,mrc->kmc", rf_own, projected, preferred_element_type=jnp.float32)
+        summed = lax.optimization_barrier(
+            jnp.einsum("rk,mrc->kmc", rf_own, projected, preferred_element_type=jnp.float32))
         other = []
         for lo, hi in chunks:
             for_partner = jnp.einsum(

time: 42.5 us -> 42.3 us (level)
  waiting for transfers between devices: 17 us -> 16.5 us
  transfers between devices with their start and end apart: 9 -> 9, of which waited for: 8 -> 8; matrix products, arithmetic and copies ran while one was open for 21% -> 22% of each run, Pallas kernels for 0% -> 0%
where the time goes in v26:
time: 42.3 us; the launch traced here: 42.1 us
  waiting for transfers between devices  16.5 us (39%)
  starting transfers between devices  10.3 us (24%)
  local copies, waits for them, and re-layouts  9.42 us (22%)
  matrix products  4.81 us (11%)
  other arithmetic  0.83 us (2%)
    ppermute x4, waiting for transfers between devices, _reduce_scatter_rows(): recv = lax.ppermute(send, axis, [(i, i ^ d) for i in range(size)])  11 us
    ppermute x4, starting transfers between devices, _reduce_scatter_rows(): recv = lax.ppermute(send, axis, [(i, i ^ d) for i in range(size)])  8.85 us
    unnamed x12, local copies, waits for them, and re-layouts  6.83 us
    ppermute x2, waiting for transfers between devices, _all_gather_rows(): recv = lax.ppermute(x, axis, [(i, i ^ d) for i in range(size)])  4.18 us
    convert_element_type x1, local copies, waits for them, and re-layouts, local(): (control.astype(jnp.float32) + jnp.stack(outs, axis=2)).astype(jnp.bfloat16)  1.69 us
    ppermute x3, waiting for transfers between devices, _swap(): return lax.ppermute(x, axis, [(0, 1), (1, 0)])  1.41 us
    dot_general x2, matrix products, local(): jnp.einsum('mrc,nc->mrn', expanded, cf_next, preferred_element_type=jnp.f...  1.32 us
    dot_general x2, matrix products, local(): jnp.einsum('mrn,nc->mrc', scaled, col_factor, preferred_element_type=jnp....  1.16 us
  transfers between devices with their start and end apart: 9, of which 8 were waited for; matrix products, arithmetic and copies ran while one was open for 22% of the time, Pallas kernels for 0%

profile of v26, /device:TPU:0, one launch (start us, length us, event | category | flops | bytes accessed | tf_op | source)
XLA Modules:
  0.0 42.1 jit_solution(9938691077812473352)
XLA Ops:
  0.0 1.3 %copy.8 = bf16[128,6,2,256]{3,0,2,1:T(8,128)(2,1)S(1)} copy(bf16[128,6,2,256]{3,2,1,0:T(2,128)(2,1)} %param.6) | data formatting | bytes 1572864 | tf_op args[1]
  1.3 0.5 %collective-permute-start = (bf16[128,6,2,256]{3,0,2,1:T(8,128)(2,1)S(1)}, bf16[128,6,2,256]{3,0,2,1:T(8,128)(2,1)S(1)}, u32[]{:S(2)}, u32[]{:S(2)}) collective-permute-start(bf16[128,6,2,256]{3,0,2,1:T(8,128)(2,1)S(1)} %copy.8), channel_id=1, source_target_pairs={{0,1},{1,0},{2,3},{3,2},{4,5},{5,4},{6,7},{7,6},{8,9},{9,8},{10,11... | collective-permute-start | bytes 2359304 | tf_op jit(solution)/shard_map/ppermute | solution.py:8
  1.8 4.3 %copy.33 = bf16[256,6,2,512]{3,0,1,2:T(8,128)(2,1)} copy(bf16[256,6,2,512]{3,2,1,0:T(2,128)(2,1)} %param.5) | data formatting | bytes 6291456 | tf_op args[0]
  6.1 0.6 %fusion.27 = f32[256,6,2,256]{3,0,2,1:T(8,128)S(1)} fusion(bf16[256,256]{1,0:T(8,128)(2,1)S(1)} %copy-done.3, s32[]{:T(128)S(6)} %select_n.57, bf16[128,6,2,256]{3,2,1,0:T(2,128)(2,1)S(1)} %copy-done.1), kind=kOutput, calls=%fused_computation.46 | convolution fusion | flops 201326592 | bytes 3997700 | tf_op jit(solution)/shard_map/rk,kmlc->lmrc/dot_general | solution.py:71
  6.7 0.6 %fusion.11 = bf16[2,6,256,256]{3,2,0,1:T(8,128)(2,1)S(1)} fusion(f32[256,6,2,256]{3,0,2,1:T(8,128)S(1)} %fusion.27, bf16[128,6,2,256]{3,0,2,1:T(8,128)(2,1)S(1)} %collective-permute-done, bf16[256,256]{1,0:T(8,128)(2,1)S(1)} %copy-done.3, s32[]{:T(128)S(6)} %select_n.60), kind=kOutput, calls=%fused_computation.18 | convolution fusion | flops 202899456 | bytes 5570564 | tf_op jit(solution)/shard_map/rk,kmlc->lmrc/dot_general | solution.py:72
  7.3 1.3 %copy-done.2 = bf16[256,6,2,512]{3,0,1,2:T(8,128)(2,1)S(1)} copy-done((bf16[256,6,2,512]{3,0,1,2:T(8,128)(2,1)S(1)}, bf16[256,6,2,512]{3,0,1,2:T(8,128)(2,1)}, u32[]{:S(2)}) %copy-start.2) | copy-done | bytes 3145752
  8.5 0.7 %fusion = f32[256,512]{1,0:T(8,128)S(1)} fusion(bf16[2,6,256,512]{3,2,1,0:T(8,128)(2,1)S(1)} %bitcast.77, bf16[2,6,256,256]{3,2,0,1:T(8,128)(2,1)S(1)} %fusion.11, bf16[512,256]{1,0:T(8,128)(2,1)S(1)} %copy-done), kind=kOutput, calls=%fused_computation.4 | convolution fusion | flops 404881408 | bytes 3145728 | tf_op jit(solution)/shard_map/mrc,nc->mrn/dot_general | solution.py:84
  9.2 2.7 %collective-permute-start.1 = (bf16[128,512]{1,0:T(8,128)(2,1)S(1)}, bf16[128,512]{1,0:T(8,128)(2,1)S(1)}, u32[]{:S(2)}, u32[]{:S(2)}) collective-permute-start(bf16[128,512]{1,0:T(8,128)(2,1)S(1)} %dynamic-slice_convert_fusion.1), channel_id=1, source_target_pairs={{0,4},{4,0},{8,12},{12,8},{1,5},{5,1},{9,13},{13,9},{2,6},{6,2},{1... | collective-permute-start | bytes 393224 | tf_op jit(solution)/shard_map/ppermute | solution.py:23
  11.9 0.8 %fusion.50 = (f32[1,256,512]{2,0,1:T(1,128)S(1)}, f32[1,256,512]{2,0,1:T(1,128)S(1)}) fusion(f32[2,256,512]{2,0,1:T(2,128)S(1)} %bitcast.81), kind=kLoop, calls=%fused_computation.71 | loop fusion | bytes 2097152 | tf_op jit(solution)/shard_map/slice | solution.py:89
  12.7 0.7 %fusion.2 = f32[256,512]{1,0:T(8,128)S(1)} fusion(bf16[2,6,256,512]{3,2,1,0:T(8,128)(2,1)S(1)} %bitcast.78, bf16[2,6,256,256]{3,2,0,1:T(8,128)(2,1)S(1)} %fusion.11, bf16[512,256]{1,0:T(8,128)(2,1)S(1)} %copy-done), kind=kOutput, calls=%fused_computation.6 | convolution fusion | flops 404881408 | bytes 3145728 | tf_op jit(solution)/shard_map/mrc,nc->mrn/dot_general | solution.py:84
  13.6 2.4 %collective-permute-done.1 = bf16[128,512]{1,0:T(8,128)(2,1)S(1)} collective-permute-done((bf16[128,512]{1,0:T(8,128)(2,1)S(1)}, bf16[128,512]{1,0:T(8,128)(2,1)S(1)}, u32[]{:S(2)}, u32[]{:S(2)}) %collective-permute-start.1) | collective-permute-done | bytes 131104 | tf_op jit(solution)/shard_map/ppermute | solution.py:23
  16.1 2.8 %collective-permute-start.2 = (bf16[128,512]{1,0:T(8,128)(2,1)S(1)}, bf16[128,512]{1,0:T(8,128)(2,1)S(1)}, u32[]{:S(2)}, u32[]{:S(2)}) collective-permute-start(bf16[128,512]{1,0:T(8,128)(2,1)S(1)} %fusion.24), channel_id=1, source_target_pairs={{0,8},{4,12},{8,0},{12,4},{1,9},{5,13},{9,1},{13,5},{2,10},{6,14},... | collective-permute-start | bytes 393224 | tf_op jit(solution)/shard_map/ppermute | solution.py:30
  19.1 3.2 %collective-permute-start.6 = (bf16[128,512]{1,0:T(8,128)(2,1)S(1)}, bf16[128,512]{1,0:T(8,128)(2,1)S(1)}, u32[]{:S(2)}, u32[]{:S(2)}) collective-permute-start(bf16[128,512]{1,0:T(8,128)(2,1)S(1)} %fusion.25), channel_id=1, source_target_pairs={{0,8},{4,12},{8,0},{12,4},{1,9},{5,13},{9,1},{13,5},{2,10},{6,14},... | collective-permute-start | bytes 393224 | tf_op jit(solution)/shard_map/ppermute | solution.py:30
  22.4 6.6 %collective-permute-done.2 = bf16[128,512]{1,0:T(8,128)(2,1)S(1)} collective-permute-done((bf16[128,512]{1,0:T(8,128)(2,1)S(1)}, bf16[128,512]{1,0:T(8,128)(2,1)S(1)}, u32[]{:S(2)}, u32[]{:S(2)}) %collective-permute-start.2) | collective-permute-done | bytes 131104 | tf_op jit(solution)/shard_map/ppermute | solution.py:30
  29.1 1.7 %collective-permute-done.6 = bf16[128,512]{1,0:T(8,128)(2,1)S(1)} collective-permute-done((bf16[128,512]{1,0:T(8,128)(2,1)S(1)}, bf16[128,512]{1,0:T(8,128)(2,1)S(1)}, u32[]{:S(2)}, u32[]{:S(2)}) %collective-permute-start.6) | collective-permute-done | bytes 131104 | tf_op jit(solution)/shard_map/ppermute | solution.py:30
  30.9 0.6 %collective-permute-start.7 = (bf16[128,512]{1,0:T(8,128)(2,1)S(1)}, bf16[128,512]{1,0:T(8,128)(2,1)S(1)}, u32[]{:S(2)}, u32[]{:S(2)}) collective-permute-start(bf16[128,512]{1,0:T(8,128)(2,1)S(1)} %fusion.18), channel_id=1, source_target_pairs={{0,4},{4,0},{8,12},{12,8},{1,5},{5,1},{9,13},{13,9},{2,6},{6,2},{1... | collective-permute-start | bytes 393224 | tf_op jit(solution)/shard_map/ppermute | solution.py:40
  31.5 3.8 %collective-permute-done.3 = bf16[128,512]{1,0:T(8,128)(2,1)S(1)} collective-permute-done((bf16[128,512]{1,0:T(8,128)(2,1)S(1)}, bf16[128,512]{1,0:T(8,128)(2,1)S(1)}, u32[]{:S(2)}, u32[]{:S(2)}) %collective-permute-start.3) | collective-permute-done | bytes 131104 | tf_op jit(solution)/shard_map/ppermute | solution.py:40
  35.4 0.6 %fusion.12 = bf16[6,256,256]{2,1,0:T(8,128)(2,1)S(1)} fusion(f32[256,512]{1,0:T(8,128)S(1)} %maximum_convert_fusion, bf16[2,6,256,512]{3,2,1,0:T(8,128)(2,1)S(1)} %bitcast.79, bf16[512,256]{1,0:T(8,128)(2,1)S(1)} %copy-done), kind=kOutput, calls=%fused_computation.19 | convolution fusion | flops 405405696 | bytes 3145728 | tf_op jit(solution)/shard_map/mrn,nc->mrc/dot_general | solution.py:97
  36.0 0.3 fusion.31
  36.4 0.3 collective-permute-done.7
  36.8 0.6 %fusion.15 = bf16[6,256,256]{2,1,0:T(8,128)(2,1)S(1)} fusion(f32[256,512]{1,0:T(8,128)S(1)} %maximum_convert_fusion.1, bf16[2,6,256,512]{3,2,1,0:T(8,128)(2,1)S(1)} %bitcast.80, bf16[512,256]{1,0:T(8,128)(2,1)S(1)} %copy-done), kind=kOutput, calls=%fused_computation.20 | convolution fusion | flops 405405696 | bytes 3145728 | tf_op jit(solution)/shard_map/mrn,nc->mrc/dot_general | solution.py:97
  38.2 0.3 fusion.33
  38.8 1.3 %collective-permute-done.8 = f32[128,6,256]{2,0,1:T(8,128)S(1)} collective-permute-done((f32[128,6,256]{2,0,1:T(8,128)S(1)}, f32[128,6,256]{2,0,1:T(8,128)S(1)}, u32[]{:S(2)}, u32[]{:S(2)}) %collective-permute-start.8) | collective-permute-done | bytes 786464 | tf_op jit(solution)/shard_map/ppermute | solution.py:8
  40.4 1.7 %copy.14 = bf16[128,6,2,256]{3,2,1,0:T(2,128)(2,1)} copy(bf16[128,6,2,256]{3,0,1,2:T(8,128)(2,1)S(1)} %fusion.8) | data formatting | bytes 1572864 | tf_op jit(solution)/shard_map/convert_element_type | solution.py:113
  (33 shorter events, 2.3 us)
Async XLA Ops:
  0.0 7.3 %copy-start = (bf16[512,256]{1,0:T(8,128)(2,1)S(1)}, bf16[512,256]{1,0:T(8,128)(2,1)}, u32[]{:S(2)}) copy-start(bf16[512,256]{1,0:T(8,128)(2,1)} %param.9) | copy-start | bytes 786436
  1.3 5.3 %collective-permute-start = (bf16[128,6,2,256]{3,0,2,1:T(8,128)(2,1)S(1)}, bf16[128,6,2,256]{3,0,2,1:T(8,128)(2,1)S(1)}, u32[]{:S(2)}, u32[]{:S(2)}) collective-permute-start(bf16[128,6,2,256]{3,0,2,1:T(8,128)(2,1)S(1)} %copy.8), channel_id=1, source_target_pairs={{0,1},{1,0},{2,3},{3,2},{4,5},{5,4},{6,7},{7,6},{8,9},{9,8},{10,11... | collective-permute-start | bytes 2359304 | tf_op jit(solution)/shard_map/ppermute | solution.py:8
  1.8 4.3 %copy-start.1 = (bf16[128,6,2,256]{3,2,1,0:T(2,128)(2,1)S(1)}, bf16[128,6,2,256]{3,2,1,0:T(2,128)(2,1)}, u32[]{:S(2)}) copy-start(bf16[128,6,2,256]{3,2,1,0:T(2,128)(2,1)} %param.6) | copy-start | bytes 2359300
  1.8 4.3 %copy-start.3 = (bf16[256,256]{1,0:T(8,128)(2,1)S(1)}, bf16[256,256]{1,0:T(8,128)(2,1)}, u32[]{:S(2)}) copy-start(bf16[256,256]{1,0:T(8,128)(2,1)} %param.8) | copy-start | bytes 393220
  6.6 1.9 %copy-start.2 = (bf16[256,6,2,512]{3,0,1,2:T(8,128)(2,1)S(1)}, bf16[256,6,2,512]{3,0,1,2:T(8,128)(2,1)}, u32[]{:S(2)}) copy-start(bf16[256,6,2,512]{3,0,1,2:T(8,128)(2,1)} %copy.33) | copy-start | bytes 9437188
  7.2 4.7 %copy-start.4 = (f32[256,2,512]{2,1,0:T(2,128)S(1)}, f32[256,2,512]{2,1,0:T(2,128)}, u32[]{:S(2)}) copy-start(f32[256,2,512]{2,1,0:T(2,128)} %param.7) | copy-start | bytes 3145732
  9.2 6.8 %collective-permute-start.1 = (bf16[128,512]{1,0:T(8,128)(2,1)S(1)}, bf16[128,512]{1,0:T(8,128)(2,1)S(1)}, u32[]{:S(2)}, u32[]{:S(2)}) collective-permute-start(bf16[128,512]{1,0:T(8,128)(2,1)S(1)} %dynamic-slice_convert_fusion.1), channel_id=1, source_target_pairs={{0,4},{4,0},{8,12},{12,8},{1,5},{5,1},{9,13},{13,9},{2,6},{6,2},{1... | collective-permute-start | bytes 393224 | tf_op jit(solution)/shard_map/ppermute | solution.py:23
  13.4 5.6 %collective-permute-start.5 = (bf16[128,512]{1,0:T(8,128)(2,1)S(1)}, bf16[128,512]{1,0:T(8,128)(2,1)S(1)}, u32[]{:S(2)}, u32[]{:S(2)}) collective-permute-start(bf16[128,512]{1,0:T(8,128)(2,1)S(1)} %dynamic-slice_convert_fusion), channel_id=1, source_target_pairs={{0,4},{4,0},{8,12},{12,8},{1,5},{5,1},{9,13},{13,9},{2,6},{6,2},{1... | collective-permute-start | bytes 393224 | tf_op jit(solution)/shard_map/ppermute | solution.py:23
  16.1 12.9 %collective-permute-start.2 = (bf16[128,512]{1,0:T(8,128)(2,1)S(1)}, bf16[128,512]{1,0:T(8,128)(2,1)S(1)}, u32[]{:S(2)}, u32[]{:S(2)}) collective-permute-start(bf16[128,512]{1,0:T(8,128)(2,1)S(1)} %fusion.24), channel_id=1, source_target_pairs={{0,8},{4,12},{8,0},{12,4},{1,9},{5,13},{9,1},{13,5},{2,10},{6,14},... | collective-permute-start | bytes 393224 | tf_op jit(solution)/shard_map/ppermute | solution.py:30
  19.1 11.7 %collective-permute-start.6 = (bf16[128,512]{1,0:T(8,128)(2,1)S(1)}, bf16[128,512]{1,0:T(8,128)(2,1)S(1)}, u32[]{:S(2)}, u32[]{:S(2)}) collective-permute-start(bf16[128,512]{1,0:T(8,128)(2,1)S(1)} %fusion.25), channel_id=1, source_target_pairs={{0,8},{4,12},{8,0},{12,4},{1,9},{5,13},{9,1},{13,5},{2,10},{6,14},... | collective-permute-start | bytes 393224 | tf_op jit(solution)/shard_map/ppermute | solution.py:30
  29.1 6.3 %collective-permute-start.3 = (bf16[128,512]{1,0:T(8,128)(2,1)S(1)}, bf16[128,512]{1,0:T(8,128)(2,1)S(1)}, u32[]{:S(2)}, u32[]{:S(2)}) collective-permute-start(bf16[128,512]{1,0:T(8,128)(2,1)S(1)} %fusion.19), channel_id=1, source_target_pairs={{0,4},{4,0},{8,12},{12,8},{1,5},{5,1},{9,13},{13,9},{2,6},{6,2},{1... | collective-permute-start | bytes 393224 | tf_op jit(solution)/shard_map/ppermute | solution.py:40
  30.9 5.8 %collective-permute-start.7 = (bf16[128,512]{1,0:T(8,128)(2,1)S(1)}, bf16[128,512]{1,0:T(8,128)(2,1)S(1)}, u32[]{:S(2)}, u32[]{:S(2)}) collective-permute-start(bf16[128,512]{1,0:T(8,128)(2,1)S(1)} %fusion.18), channel_id=1, source_target_pairs={{0,4},{4,0},{8,12},{12,8},{1,5},{5,1},{9,13},{13,9},{2,6},{6,2},{1... | collective-permute-start | bytes 393224 | tf_op jit(solution)/shard_map/ppermute | solution.py:40
  36.3 2.4 %collective-permute-start.4 = (f32[128,6,256]{2,0,1:T(8,128)S(1)}, f32[128,6,256]{2,0,1:T(8,128)S(1)}, u32[]{:S(2)}, u32[]{:S(2)}) collective-permute-start(f32[128,6,256]{2,0,1:T(8,128)S(1)} %fusion.31), channel_id=1, source_target_pairs={{0,1},{1,0},{2,3},{3,2},{4,5},{5,4},{6,7},{7,6},{8,9},{9,8},{10,11... | collective-permute-start | bytes 2359304 | tf_op jit(solution)/shard_map/ppermute | solution.py:8
  37.7 2.4 %collective-permute-start.8 = (f32[128,6,256]{2,0,1:T(8,128)S(1)}, f32[128,6,256]{2,0,1:T(8,128)S(1)}, u32[]{:S(2)}, u32[]{:S(2)}) collective-permute-start(f32[128,6,256]{2,0,1:T(8,128)S(1)} %fusion.29), channel_id=1, source_target_pairs={{0,1},{1,0},{2,3},{3,2},{4,5},{5,4},{6,7},{7,6},{8,9},{9,8},{10,11... | collective-permute-start | bytes 2359304 | tf_op jit(solution)/shard_map/ppermute | solution.py:8

commit v27 on v24

--- a/solution.py
+++ b/solution.py
@@ -67,9 +67,13 @@
     rf_own = lax.dynamic_slice_in_dim(row_factor, h * kh, kh, 1)
     rf_other = lax.dynamic_slice_in_dim(row_factor, (1 - h) * kh, kh, 1)
     ctrl_other = _swap(control, "half")
-    expanded_all = (
-        jnp.einsum("rk,kmlc->lmrc", rf_own, control, preferred_element_type=jnp.float32)
-        + jnp.einsum("rk,kmlc->lmrc", rf_other, ctrl_other, preferred_element_type=jnp.float32)
+    ctrl_full = jnp.where(
+        h == 0,
+        jnp.concatenate([control, ctrl_other], axis=0),
+        jnp.concatenate([ctrl_other, control], axis=0),
+    )
+    expanded_all = jnp.einsum(
+        "rk,kmlc->lmrc", row_factor, ctrl_full, preferred_element_type=jnp.float32
     ).astype(jnp.bfloat16)
 
     pow2 = n_mem & (n_mem - 1) == 0 and rows % n_mem == 0

time: 42.5 us -> 48.9 us (1.15)
  waiting for transfers between devices: 17 us -> 23.5 us
  other arithmetic: 0.63 us -> 5.4 us
  local copies, waits for them, and re-layouts: 9.42 us -> 5.35 us
  starting transfers between devices: 10.3 us -> 7.42 us
  matrix products: 4.81 us -> 6.67 us
    ppermute x4, waiting for transfers between devices: 11 us -> 17.5 us  [_reduce_scatter_rows(): recv = lax.ppermute(send, axis, [(i, i ^ d) for i in range(size)])]
    select_n x0 -> x1, other arithmetic: none -> 4.77 us  [local(): jnp.where(h == 0, jnp.concatenate([control, ctrl_other], axis=0), jnp.con...]
    unnamed x12 -> x17, local copies, waits for them, and re-layouts: 6.83 us -> 2.74 us
    ppermute x4, starting transfers between devices: 8.85 us -> 5.85 us  [_reduce_scatter_rows(): recv = lax.ppermute(send, axis, [(i, i ^ d) for i in range(size)])]
    dot_general x2, matrix products: 0.6 us -> 2.93 us  [local(): jnp.einsum('rk,mrc->kmc', rf_own, projected, preferred_element_type=jnp.f...]
    dot_general x2 -> x1, matrix products: 1.13 us -> 0.62 us  [local(): jnp.einsum('rk,kmlc->lmrc', row_factor, ctrl_full, preferred_element_type...]
  transfers between devices with their start and end apart: 9 -> 9, of which waited for: 8 -> 6; matrix products, arithmetic and copies ran while one was open for 21% -> 12% of each run, Pallas kernels for 0% -> 0%
where the time goes in v27:
time: 48.9 us; the launch traced here: 48.7 us
  waiting for transfers between devices  23.5 us (48%)
  starting transfers between devices  7.42 us (15%)
  matrix products  6.67 us (14%)
  other arithmetic  5.4 us (11%)
  local copies, waits for them, and re-layouts  5.35 us (11%)
    ppermute x4, waiting for transfers between devices, _reduce_scatter_rows(): recv = lax.ppermute(send, axis, [(i, i ^ d) for i in range(size)])  17.5 us
    ppermute x4, starting transfers between devices, _reduce_scatter_rows(): recv = lax.ppermute(send, axis, [(i, i ^ d) for i in range(size)])  5.85 us
    select_n x1, other arithmetic, local(): jnp.where(h == 0, jnp.concatenate([control, ctrl_other], axis=0), jnp.con...  4.77 us
    ppermute x2, waiting for transfers between devices, _all_gather_rows(): recv = lax.ppermute(x, axis, [(i, i ^ d) for i in range(size)])  4.54 us
    dot_general x2, matrix products, local(): jnp.einsum('rk,mrc->kmc', rf_own, projected, preferred_element_type=jnp.f...  2.93 us
    unnamed x17, local copies, waits for them, and re-layouts  2.74 us
    convert_element_type x1, local copies, waits for them, and re-layouts, local(): (control.astype(jnp.float32) + jnp.stack(outs, axis=2)).astype(jnp.bfloat16)  1.69 us
    ppermute x3, waiting for transfers between devices, _swap(): return lax.ppermute(x, axis, [(0, 1), (1, 0)])  1.54 us
  transfers between devices with their start and end apart: 9, of which 6 were waited for; matrix products, arithmetic and copies ran while one was open for 12% of the time, Pallas kernels for 0%

profile of v27, /device:TPU:0, one launch (start us, length us, event | category | flops | bytes accessed | tf_op | source)
XLA Modules:
  0.0 48.7 jit_solution(15815991878524860586)
XLA Ops:
  0.0 0.5 collective-permute-start
  0.5 2.5 %copy.29 = bf16[256,6,2,512]{3,0,1,2:T(8,128)(2,1)S(1)} copy(bf16[256,6,2,512]{3,2,1,0:T(2,128)(2,1)} %param.5) | data formatting | bytes 6291456 | tf_op args[0]
  3.0 4.8 %broadcast_select_fusion = bf16[256,6,2,256]{3,2,1,0:T(2,128)(2,1)S(1)} fusion(pred[]{:T(512)S(6)} %eq.16, bf16[128,6,2,256]{3,2,1,0:T(2,128)(2,1)} %collective-permute-done, bf16[128,6,2,256]{3,2,1,0:T(2,128)(2,1)} %param.6), kind=kLoop, calls=%fused_computation.9 | loop fusion | flops 2359296 | bytes 3145729 | tf_op jit(solution)/shard_map/jit(_where)/select_n | solution.py:70
  7.8 0.6 %fusion.12 = bf16[2,6,256,256]{2,3,0,1:T(8,128)(2,1)S(1)} fusion(bf16[256,6,2,256]{3,2,1,0:T(2,128)(2,1)S(1)} %broadcast_select_fusion, bf16[256,256]{1,0:T(8,128)(2,1)S(1)} %copy-done.6), kind=kOutput, calls=%fused_computation.20 | convolution fusion | flops 403439616 | bytes 3276800 | tf_op jit(solution)/shard_map/rk,kmlc->lmrc/dot_general | solution.py:75
  8.5 0.7 %fusion = f32[256,512]{1,0:T(8,128)S(1)} fusion(bf16[2,6,256,512]{3,2,1,0:T(8,128)(2,1)S(1)} %bitcast.73, bf16[2,6,256,256]{2,3,0,1:T(8,128)(2,1)S(1)} %fusion.12, bf16[512,256]{1,0:T(8,128)(2,1)S(1)} %copy-done), kind=kOutput, calls=%fused_computation.4 | convolution fusion | flops 404881408 | bytes 3145728 | tf_op jit(solution)/shard_map/mrc,nc->mrn/dot_general | solution.py:88
  9.2 0.7 %fusion.2 = f32[256,512]{1,0:T(8,128)S(1)} fusion(bf16[2,6,256,512]{3,2,1,0:T(8,128)(2,1)S(1)} %bitcast.74, bf16[2,6,256,256]{2,3,0,1:T(8,128)(2,1)S(1)} %fusion.12, bf16[512,256]{1,0:T(8,128)(2,1)S(1)} %copy-done), kind=kOutput, calls=%fused_computation.6 | convolution fusion | flops 404881408 | bytes 3145728 | tf_op jit(solution)/shard_map/mrc,nc->mrn/dot_general | solution.py:88
  9.9 2.7 %collective-permute-start.5 = (bf16[128,512]{1,0:T(8,128)(2,1)S(1)}, bf16[128,512]{1,0:T(8,128)(2,1)S(1)}, u32[]{:S(2)}, u32[]{:S(2)}) collective-permute-start(bf16[128,512]{1,0:T(8,128)(2,1)S(1)} %dynamic-slice_convert_fusion), channel_id=1, source_target_pairs={{0,4},{4,0},{8,12},{12,8},{1,5},{5,1},{9,13},{13,9},{2,6},{6,2},{1... | collective-permute-start | bytes 393224 | tf_op jit(solution)/shard_map/ppermute | solution.py:23
  12.7 0.8 %fusion.46 = (f32[1,256,512]{2,0,1:T(1,128)S(1)}, f32[1,256,512]{2,0,1:T(1,128)S(1)}) fusion(f32[2,256,512]{2,0,1:T(2,128)S(1)} %bitcast.77), kind=kLoop, calls=%fused_computation.66 | loop fusion | bytes 2097152 | tf_op jit(solution)/shard_map/slice | solution.py:93
  13.6 5.9 %collective-permute-done.1 = bf16[128,512]{1,0:T(8,128)(2,1)S(1)} collective-permute-done((bf16[128,512]{1,0:T(8,128)(2,1)S(1)}, bf16[128,512]{1,0:T(8,128)(2,1)S(1)}, u32[]{:S(2)}, u32[]{:S(2)}) %collective-permute-start.1) | collective-permute-done | bytes 131104 | tf_op jit(solution)/shard_map/ppermute | solution.py:23
  19.6 2.8 %collective-permute-start.2 = (bf16[128,512]{1,0:T(8,128)(2,1)S(1)}, bf16[128,512]{1,0:T(8,128)(2,1)S(1)}, u32[]{:S(2)}, u32[]{:S(2)}) collective-permute-start(bf16[128,512]{1,0:T(8,128)(2,1)S(1)} %fusion.29), channel_id=1, source_target_pairs={{0,8},{4,12},{8,0},{12,4},{1,9},{5,13},{9,1},{13,5},{2,10},{6,14},... | collective-permute-start | bytes 393224 | tf_op jit(solution)/shard_map/ppermute | solution.py:30
  22.7 9.8 %collective-permute-done.2 = bf16[128,512]{1,0:T(8,128)(2,1)S(1)} collective-permute-done((bf16[128,512]{1,0:T(8,128)(2,1)S(1)}, bf16[128,512]{1,0:T(8,128)(2,1)S(1)}, u32[]{:S(2)}, u32[]{:S(2)}) %collective-permute-start.2) | collective-permute-done | bytes 131104 | tf_op jit(solution)/shard_map/ppermute | solution.py:30
  32.6 1.7 %collective-permute-done.6 = bf16[128,512]{1,0:T(8,128)(2,1)S(1)} collective-permute-done((bf16[128,512]{1,0:T(8,128)(2,1)S(1)}, bf16[128,512]{1,0:T(8,128)(2,1)S(1)}, u32[]{:S(2)}, u32[]{:S(2)}) %collective-permute-start.6) | collective-permute-done | bytes 131104 | tf_op jit(solution)/shard_map/ppermute | solution.py:30
  34.4 0.6 %collective-permute-start.7 = (bf16[128,512]{1,0:T(8,128)(2,1)S(1)}, bf16[128,512]{1,0:T(8,128)(2,1)S(1)}, u32[]{:S(2)}, u32[]{:S(2)}) collective-permute-start(bf16[128,512]{1,0:T(8,128)(2,1)S(1)} %fusion.23), channel_id=1, source_target_pairs={{0,4},{4,0},{8,12},{12,8},{1,5},{5,1},{9,13},{13,9},{2,6},{6,2},{1... | collective-permute-start | bytes 393224 | tf_op jit(solution)/shard_map/ppermute | solution.py:40
  35.0 3.8 %collective-permute-done.3 = bf16[128,512]{1,0:T(8,128)(2,1)S(1)} collective-permute-done((bf16[128,512]{1,0:T(8,128)(2,1)S(1)}, bf16[128,512]{1,0:T(8,128)(2,1)S(1)}, u32[]{:S(2)}, u32[]{:S(2)}) %collective-permute-start.3) | collective-permute-done | bytes 131104 | tf_op jit(solution)/shard_map/ppermute | solution.py:40
  38.9 0.6 %fusion.15 = bf16[6,256,256]{2,1,0:T(8,128)(2,1)S(1)} fusion(f32[256,512]{1,0:T(8,128)S(1)} %maximum_convert_fusion, bf16[2,6,256,512]{3,2,1,0:T(8,128)(2,1)S(1)} %bitcast.75, bf16[512,256]{1,0:T(8,128)(2,1)S(1)} %copy-done), kind=kOutput, calls=%fused_computation.21 | convolution fusion | flops 405405696 | bytes 3145728 | tf_op jit(solution)/shard_map/mrn,nc->mrc/dot_general | solution.py:101
  39.5 0.7 %collective-permute-done.7 = bf16[128,512]{1,0:T(8,128)(2,1)S(1)} collective-permute-done((bf16[128,512]{1,0:T(8,128)(2,1)S(1)}, bf16[128,512]{1,0:T(8,128)(2,1)S(1)}, u32[]{:S(2)}, u32[]{:S(2)}) %collective-permute-start.7) | collective-permute-done | bytes 131104 | tf_op jit(solution)/shard_map/ppermute | solution.py:40
  40.3 0.6 %fusion.18 = bf16[6,256,256]{2,1,0:T(8,128)(2,1)S(1)} fusion(f32[256,512]{1,0:T(8,128)S(1)} %maximum_convert_fusion.1, bf16[2,6,256,512]{3,2,1,0:T(8,128)(2,1)S(1)} %bitcast.76, bf16[512,256]{1,0:T(8,128)(2,1)S(1)} %copy-done), kind=kOutput, calls=%fused_computation.22 | convolution fusion | flops 405405696 | bytes 3145728 | tf_op jit(solution)/shard_map/mrn,nc->mrc/dot_general | solution.py:101
  40.9 0.3 fusion.34
  41.3 0.3 fusion.32
  41.8 0.4 collective-permute-start.8
  42.2 1.5 %collective-permute-done.4 = f32[128,6,256]{2,0,1:T(8,128)} collective-permute-done((f32[128,6,256]{2,0,1:T(8,128)S(1)}, f32[128,6,256]{2,0,1:T(8,128)}, u32[]{:S(2)}, u32[]{:S(2)}) %collective-permute-start.4) | collective-permute-done | bytes 786464 | tf_op jit(solution)/shard_map/ppermute | solution.py:8
  43.7 1.4 %fusion.22 = f32[128,6,1,256]{3,0,1,2:T(8,128)S(1)} fusion(f32[128,6,256]{2,0,1:T(8,128)} %collective-permute-done.4, bf16[6,256,256]{2,1,0:T(8,128)(2,1)S(1)} %copy-done.2, bf16[256,256]{1,0:T(8,128)(2,1)S(1)} %copy-done.6, s32[]{:T(128)S(6)} %select_n.65), kind=kOutput, calls=%fused_computation.26 | convolution fusion | flops 100859904 | bytes 2424836 | tf_op jit(solution)/shard_map/rk,mrc->kmc/dot_general | solution.py:107
  45.2 1.5 %fusion.21 = f32[128,6,1,256]{3,0,1,2:T(8,128)S(1)} fusion(f32[128,6,256]{2,0,1:T(8,128)} %collective-permute-done.8, bf16[6,256,256]{2,1,0:T(8,128)(2,1)S(1)} %copy-done.4, bf16[256,256]{1,0:T(8,128)(2,1)S(1)} %copy-done.6, s32[]{:T(128)S(6)} %select_n.65), kind=kOutput, calls=%fused_computation.24 | convolution fusion | flops 100859904 | bytes 2424836 | tf_op jit(solution)/shard_map/rk,mrc->kmc/dot_general | solution.py:107
  47.0 1.7 %copy.13 = bf16[128,6,2,256]{3,2,1,0:T(2,128)(2,1)} copy(bf16[128,6,2,256]{3,0,1,2:T(8,128)(2,1)S(1)} %fusion.8) | data formatting | bytes 1572864 | tf_op jit(solution)/shard_map/convert_element_type | solution.py:116
  (36 shorter events, 1.4 us)
Async XLA Ops:
  0.0 8.5 %copy-start = (bf16[512,256]{1,0:T(8,128)(2,1)S(1)}, bf16[512,256]{1,0:T(8,128)(2,1)}, u32[]{:S(2)}) copy-start(bf16[512,256]{1,0:T(8,128)(2,1)} %param.9) | copy-start | bytes 786436
  0.0 3.0 %collective-permute-start = (bf16[128,6,2,256]{3,2,1,0:T(2,128)(2,1)}, bf16[128,6,2,256]{3,2,1,0:T(2,128)(2,1)}, u32[]{:S(2)}, u32[]{:S(2)}) collective-permute-start(bf16[128,6,2,256]{3,2,1,0:T(2,128)(2,1)} %param.6), channel_id=1, source_target_pairs={{0,1},{1,0},{2,3},{3,2},{4,5},{5,4},{6,7},{7,6},{8,9},{9,8},{10,11... | collective-permute-start | bytes 2359304 | tf_op jit(solution)/shard_map/ppermute | solution.py:8
  3.0 4.8 %copy-start.6 = (bf16[256,256]{1,0:T(8,128)(2,1)S(1)}, bf16[256,256]{1,0:T(8,128)(2,1)}, u32[]{:S(2)}) copy-start(bf16[256,256]{1,0:T(8,128)(2,1)} %param.8) | copy-start | bytes 393220
  9.2 3.5 %copy-start.7 = (f32[256,2,512]{2,1,0:T(2,128)S(1)}, f32[256,2,512]{2,1,0:T(2,128)}, u32[]{:S(2)}) copy-start(f32[256,2,512]{2,1,0:T(2,128)} %param.7) | copy-start | bytes 3145732
  9.9 12.5 %collective-permute-start.5 = (bf16[128,512]{1,0:T(8,128)(2,1)S(1)}, bf16[128,512]{1,0:T(8,128)(2,1)S(1)}, u32[]{:S(2)}, u32[]{:S(2)}) collective-permute-start(bf16[128,512]{1,0:T(8,128)(2,1)S(1)} %dynamic-slice_convert_fusion), channel_id=1, source_target_pairs={{0,4},{4,0},{8,12},{12,8},{1,5},{5,1},{9,13},{13,9},{2,6},{6,2},{1... | collective-permute-start | bytes 393224 | tf_op jit(solution)/shard_map/ppermute | solution.py:23
  12.6 6.9 %collective-permute-start.1 = (bf16[128,512]{1,0:T(8,128)(2,1)S(1)}, bf16[128,512]{1,0:T(8,128)(2,1)S(1)}, u32[]{:S(2)}, u32[]{:S(2)}) collective-permute-start(bf16[128,512]{1,0:T(8,128)(2,1)S(1)} %dynamic-slice_convert_fusion.1), channel_id=1, source_target_pairs={{0,4},{4,0},{8,12},{12,8},{1,5},{5,1},{9,13},{13,9},{2,6},{6,2},{1... | collective-permute-start | bytes 393224 | tf_op jit(solution)/shard_map/ppermute | solution.py:23
  19.6 12.9 %collective-permute-start.2 = (bf16[128,512]{1,0:T(8,128)(2,1)S(1)}, bf16[128,512]{1,0:T(8,128)(2,1)S(1)}, u32[]{:S(2)}, u32[]{:S(2)}) collective-permute-start(bf16[128,512]{1,0:T(8,128)(2,1)S(1)} %fusion.29), channel_id=1, source_target_pairs={{0,8},{4,12},{8,0},{12,4},{1,9},{5,13},{9,1},{13,5},{2,10},{6,14},... | collective-permute-start | bytes 393224 | tf_op jit(solution)/shard_map/ppermute | solution.py:30
  22.4 11.9 %collective-permute-start.6 = (bf16[128,512]{1,0:T(8,128)(2,1)S(1)}, bf16[128,512]{1,0:T(8,128)(2,1)S(1)}, u32[]{:S(2)}, u32[]{:S(2)}) collective-permute-start(bf16[128,512]{1,0:T(8,128)(2,1)S(1)} %fusion.30), channel_id=1, source_target_pairs={{0,8},{4,12},{8,0},{12,4},{1,9},{5,13},{9,1},{13,5},{2,10},{6,14},... | collective-permute-start | bytes 393224 | tf_op jit(solution)/shard_map/ppermute | solution.py:30
  32.6 6.2 %collective-permute-start.3 = (bf16[128,512]{1,0:T(8,128)(2,1)S(1)}, bf16[128,512]{1,0:T(8,128)(2,1)S(1)}, u32[]{:S(2)}, u32[]{:S(2)}) collective-permute-start(bf16[128,512]{1,0:T(8,128)(2,1)S(1)} %fusion.24), channel_id=1, source_target_pairs={{0,4},{4,0},{8,12},{12,8},{1,5},{5,1},{9,13},{13,9},{2,6},{6,2},{1... | collective-permute-start | bytes 393224 | tf_op jit(solution)/shard_map/ppermute | solution.py:40
  34.4 5.8 %collective-permute-start.7 = (bf16[128,512]{1,0:T(8,128)(2,1)S(1)}, bf16[128,512]{1,0:T(8,128)(2,1)S(1)}, u32[]{:S(2)}, u32[]{:S(2)}) collective-permute-start(bf16[128,512]{1,0:T(8,128)(2,1)S(1)} %fusion.23), channel_id=1, source_target_pairs={{0,4},{4,0},{8,12},{12,8},{1,5},{5,1},{9,13},{13,9},{2,6},{6,2},{1... | collective-permute-start | bytes 393224 | tf_op jit(solution)/shard_map/ppermute | solution.py:40
  39.5 1.4 %copy-start.1 = (bf16[6,256,256]{2,1,0:T(8,128)(2,1)}, bf16[6,256,256]{2,1,0:T(8,128)(2,1)S(1)}, u32[]{:S(2)}) copy-start(bf16[6,256,256]{2,1,0:T(8,128)(2,1)S(1)} %fusion.15) | copy-start | bytes 2359300
  40.9 0.9 %copy-start.3 = (bf16[6,256,256]{2,1,0:T(8,128)(2,1)}, bf16[6,256,256]{2,1,0:T(8,128)(2,1)S(1)}, u32[]{:S(2)}) copy-start(bf16[6,256,256]{2,1,0:T(8,128)(2,1)S(1)} %fusion.18) | copy-start | bytes 2359300
  41.2 2.5 %copy-start.2 = (bf16[6,256,256]{2,1,0:T(8,128)(2,1)S(1)}, bf16[6,256,256]{2,1,0:T(8,128)(2,1)}, u32[]{:S(2)}) copy-start(bf16[6,256,256]{2,1,0:T(8,128)(2,1)} %copy-done.1) | copy-start | bytes 2359300
  41.2 2.5 %collective-permute-start.4 = (f32[128,6,256]{2,0,1:T(8,128)S(1)}, f32[128,6,256]{2,0,1:T(8,128)}, u32[]{:S(2)}, u32[]{:S(2)}) collective-permute-start(f32[128,6,256]{2,0,1:T(8,128)S(1)} %fusion.34), channel_id=1, source_target_pairs={{0,1},{1,0},{2,3},{3,2},{4,5},{5,4},{6,7},{7,6},{8,9},{9,8},{10,11... | collective-permute-start | bytes 2359304 | tf_op jit(solution)/shard_map/ppermute | solution.py:8
  41.8 3.4 %collective-permute-start.8 = (f32[128,6,256]{2,0,1:T(8,128)S(1)}, f32[128,6,256]{2,0,1:T(8,128)}, u32[]{:S(2)}, u32[]{:S(2)}) collective-permute-start(f32[128,6,256]{2,0,1:T(8,128)S(1)} %fusion.32), channel_id=1, source_target_pairs={{0,1},{1,0},{2,3},{3,2},{4,5},{5,4},{6,7},{7,6},{8,9},{9,8},{10,11... | collective-permute-start | bytes 2359304 | tf_op jit(solution)/shard_map/ppermute | solution.py:8
  42.2 3.0 %copy-start.4 = (bf16[6,256,256]{2,1,0:T(8,128)(2,1)S(1)}, bf16[6,256,256]{2,1,0:T(8,128)(2,1)}, u32[]{:S(2)}) copy-start(bf16[6,256,256]{2,1,0:T(8,128)(2,1)} %copy-done.3) | copy-start | bytes 2359300
  45.1 1.5 %copy-start.5 = (bf16[128,6,2,256]{3,2,1,0:T(2,128)(2,1)S(1)}, bf16[128,6,2,256]{3,2,1,0:T(2,128)(2,1)}, u32[]{:S(2)}) copy-start(bf16[128,6,2,256]{3,2,1,0:T(2,128)(2,1)} %param.6) | copy-start | bytes 2359300

commit v28 on v19

--- a/solution.py
+++ b/solution.py
@@ -66,7 +66,6 @@
 
     rf_own = lax.dynamic_slice_in_dim(row_factor, h * kh, kh, 1)
     rf_other = lax.dynamic_slice_in_dim(row_factor, (1 - h) * kh, kh, 1)
-    rf_for_partner = _swap(rf_other, "half")
     ctrl_other = _swap(control, "half")
     expanded_all = (
         jnp.einsum("rk,kmlc->lmrc", rf_own, control, preferred_element_type=jnp.float32)
@@ -108,15 +107,15 @@
             "mrn,nc->mrc", scaled, col_factor, preferred_element_type=jnp.float32
         ).astype(jnp.bfloat16)
         n_m = projected.shape[0]
-        cuts = [i * n_m // 3 for i in range(4)]
+        cuts = [0, n_m]
         chunks = [(lo, hi) for lo, hi in zip(cuts[:-1], cuts[1:]) if lo < hi]
         summed = jnp.einsum("rk,mrc->kmc", rf_own, projected, preferred_element_type=jnp.float32)
         other = []
         for lo, hi in chunks:
-            proj_other = _swap(projected[lo:hi], "half")
-            other.append(jnp.einsum(
-                "rk,mrc->kmc", rf_for_partner, proj_other, preferred_element_type=jnp.float32
-            ))
+            for_partner = jnp.einsum(
+                "rk,mrc->kmc", rf_other, projected[lo:hi], preferred_element_type=jnp.float32
+            )
+            other.append(_swap(for_partner, "half"))
         summed = summed + jnp.concatenate(other, axis=1)
         outs.append(summed)
     return (control.astype(jnp.float32) + jnp.stack(outs, axis=2)).astype(jnp.bfloat16)

time: 43 us -> 42.5 us (0.988)
  waiting for transfers between devices: 13.1 us -> 16.6 us
  starting transfers between devices: 12.9 us -> 10.7 us
  local copies, waits for them, and re-layouts: 10.4 us -> 9.44 us
  matrix products: 5.43 us -> 4.8 us
    ppermute x8 -> x3, waiting for transfers between devices: 0.02 us -> 1.81 us  [_swap(): return lax.ppermute(x, axis, [(0, 1), (1, 0)])]
    ppermute x8 -> x3, starting transfers between devices: 2.22 us -> 0.82 us  [_swap(): return lax.ppermute(x, axis, [(0, 1), (1, 0)])]
    ppermute x4, waiting for transfers between devices: 9.26 us -> 10.6 us  [_reduce_scatter_rows(): recv = lax.ppermute(send, axis, [(i, i ^ d) for i in range(size)])]
    ppermute x4, starting transfers between devices: 10.1 us -> 9.23 us  [_reduce_scatter_rows(): recv = lax.ppermute(send, axis, [(i, i ^ d) for i in range(size)])]
    dynamic_slice x1 -> x0, local copies, waits for them, and re-layouts: 0.84 us -> none  [local(): rf_other = lax.dynamic_slice_in_dim(row_factor, (1 - h) * kh, kh, 1)]
    dot_general x6 -> x2, matrix products: 1.22 us -> 0.59 us  [local(): jnp.einsum('rk,mrc->kmc', rf_other, projected[lo:hi], preferred_element_t...]
  transfers between devices with their start and end apart: 14 -> 9, of which waited for: 5 -> 8; matrix products, arithmetic and copies ran while one was open for 27% -> 21% of each run, Pallas kernels for 0% -> 0%
where the time goes in v28:
time: 42.5 us; the launch traced here: 42.3 us
  waiting for transfers between devices  16.6 us (39%)
  starting transfers between devices  10.7 us (25%)
  local copies, waits for them, and re-layouts  9.44 us (22%)
  matrix products  4.8 us (11%)
  other arithmetic  0.63 us (1%)
    ppermute x4, waiting for transfers between devices, _reduce_scatter_rows(): recv = lax.ppermute(send, axis, [(i, i ^ d) for i in range(size)])  10.6 us
    ppermute x4, starting transfers between devices, _reduce_scatter_rows(): recv = lax.ppermute(send, axis, [(i, i ^ d) for i in range(size)])  9.23 us
    unnamed x12, local copies, waits for them, and re-layouts  6.84 us
    ppermute x2, waiting for transfers between devices, _all_gather_rows(): recv = lax.ppermute(x, axis, [(i, i ^ d) for i in range(size)])  4.18 us
    ppermute x3, waiting for transfers between devices, _swap(): return lax.ppermute(x, axis, [(0, 1), (1, 0)])  1.81 us
    convert_element_type x1, local copies, waits for them, and re-layouts, local(): (control.astype(jnp.float32) + jnp.stack(outs, axis=2)).astype(jnp.bfloat16)  1.69 us
    dot_general x2, matrix products, local(): jnp.einsum('mrc,nc->mrn', expanded, cf_next, preferred_element_type=jnp.f...  1.32 us
    dot_general x2, matrix products, local(): jnp.einsum('mrn,nc->mrc', scaled, col_factor, preferred_element_type=jnp....  1.16 us
  transfers between devices with their start and end apart: 9, of which 8 were waited for; matrix products, arithmetic and copies ran while one was open for 21% of the time, Pallas kernels for 0%

profile of v28, /device:TPU:0, one launch (start us, length us, event | category | flops | bytes accessed | tf_op | source)
XLA Modules:
  0.0 42.3 jit_solution(5451590684135793252)
XLA Ops:
  0.0 1.3 %copy.8 = bf16[128,6,2,256]{3,0,2,1:T(8,128)(2,1)S(1)} copy(bf16[128,6,2,256]{3,2,1,0:T(2,128)(2,1)} %param.6) | data formatting | bytes 1572864 | tf_op args[1]
  1.3 0.5 %collective-permute-start = (bf16[128,6,2,256]{3,0,2,1:T(8,128)(2,1)S(1)}, bf16[128,6,2,256]{3,0,2,1:T(8,128)(2,1)S(1)}, u32[]{:S(2)}, u32[]{:S(2)}) collective-permute-start(bf16[128,6,2,256]{3,0,2,1:T(8,128)(2,1)S(1)} %copy.8), channel_id=1, source_target_pairs={{0,1},{1,0},{2,3},{3,2},{4,5},{5,4},{6,7},{7,6},{8,9},{9,8},{10,11... | collective-permute-start | bytes 2359304 | tf_op jit(solution)/shard_map/ppermute | solution.py:8
  1.8 4.3 %copy.33 = bf16[256,6,2,512]{3,0,1,2:T(8,128)(2,1)} copy(bf16[256,6,2,512]{3,2,1,0:T(2,128)(2,1)} %param.5) | data formatting | bytes 6291456 | tf_op args[0]
  6.1 0.6 %fusion.29 = f32[256,6,2,256]{3,0,2,1:T(8,128)S(1)} fusion(bf16[256,256]{1,0:T(8,128)(2,1)S(1)} %copy-done.3, s32[]{:T(128)S(6)} %select_n.57, bf16[128,6,2,256]{3,2,1,0:T(2,128)(2,1)S(1)} %copy-done.1), kind=kOutput, calls=%fused_computation.48 | convolution fusion | flops 201326592 | bytes 3997700 | tf_op jit(solution)/shard_map/rk,kmlc->lmrc/dot_general | solution.py:71
  6.7 0.6 %fusion.11 = bf16[2,6,256,256]{3,2,0,1:T(8,128)(2,1)S(1)} fusion(f32[256,6,2,256]{3,0,2,1:T(8,128)S(1)} %fusion.29, bf16[128,6,2,256]{3,0,2,1:T(8,128)(2,1)S(1)} %collective-permute-done, bf16[256,256]{1,0:T(8,128)(2,1)S(1)} %copy-done.3, s32[]{:T(128)S(6)} %select_n.60), kind=kOutput, calls=%fused_computation.18 | convolution fusion | flops 202899456 | bytes 5570564 | tf_op jit(solution)/shard_map/rk,kmlc->lmrc/dot_general | solution.py:72
  7.2 1.3 %copy-done.2 = bf16[256,6,2,512]{3,0,1,2:T(8,128)(2,1)S(1)} copy-done((bf16[256,6,2,512]{3,0,1,2:T(8,128)(2,1)S(1)}, bf16[256,6,2,512]{3,0,1,2:T(8,128)(2,1)}, u32[]{:S(2)}) %copy-start.2) | copy-done | bytes 3145752
  8.5 0.7 %fusion = f32[256,512]{1,0:T(8,128)S(1)} fusion(bf16[2,6,256,512]{3,2,1,0:T(8,128)(2,1)S(1)} %bitcast.77, bf16[2,6,256,256]{3,2,0,1:T(8,128)(2,1)S(1)} %fusion.11, bf16[512,256]{1,0:T(8,128)(2,1)S(1)} %copy-done), kind=kOutput, calls=%fused_computation.4 | convolution fusion | flops 404881408 | bytes 3145728 | tf_op jit(solution)/shard_map/mrc,nc->mrn/dot_general | solution.py:85
  9.2 2.7 %collective-permute-start.1 = (bf16[128,512]{1,0:T(8,128)(2,1)S(1)}, bf16[128,512]{1,0:T(8,128)(2,1)S(1)}, u32[]{:S(2)}, u32[]{:S(2)}) collective-permute-start(bf16[128,512]{1,0:T(8,128)(2,1)S(1)} %dynamic-slice_convert_fusion.1), channel_id=1, source_target_pairs={{0,4},{4,0},{8,12},{12,8},{1,5},{5,1},{9,13},{13,9},{2,6},{6,2},{1... | collective-permute-start | bytes 393224 | tf_op jit(solution)/shard_map/ppermute | solution.py:23
  11.9 0.7 %fusion.2 = f32[256,512]{1,0:T(8,128)S(1)} fusion(bf16[2,6,256,512]{3,2,1,0:T(8,128)(2,1)S(1)} %bitcast.78, bf16[2,6,256,256]{3,2,0,1:T(8,128)(2,1)S(1)} %fusion.11, bf16[512,256]{1,0:T(8,128)(2,1)S(1)} %copy-done), kind=kOutput, calls=%fused_computation.6 | convolution fusion | flops 404881408 | bytes 3145728 | tf_op jit(solution)/shard_map/mrc,nc->mrn/dot_general | solution.py:85
  12.6 0.8 %fusion.50 = (f32[1,256,512]{2,0,1:T(1,128)S(1)}, f32[1,256,512]{2,0,1:T(1,128)S(1)}) fusion(f32[2,256,512]{2,0,1:T(2,128)S(1)} %bitcast.81), kind=kLoop, calls=%fused_computation.71 | loop fusion | bytes 2097152 | tf_op jit(solution)/shard_map/slice | solution.py:99
  13.5 0.5 %collective-permute-start.5 = (bf16[128,512]{1,0:T(8,128)(2,1)S(1)}, bf16[128,512]{1,0:T(8,128)(2,1)S(1)}, u32[]{:S(2)}, u32[]{:S(2)}) collective-permute-start(bf16[128,512]{1,0:T(8,128)(2,1)S(1)} %dynamic-slice_convert_fusion), channel_id=1, source_target_pairs={{0,4},{4,0},{8,12},{12,8},{1,5},{5,1},{9,13},{13,9},{2,6},{6,2},{1... | collective-permute-start | bytes 393224 | tf_op jit(solution)/shard_map/ppermute | solution.py:23
  14.0 2.1 %collective-permute-done.1 = bf16[128,512]{1,0:T(8,128)(2,1)S(1)} collective-permute-done((bf16[128,512]{1,0:T(8,128)(2,1)S(1)}, bf16[128,512]{1,0:T(8,128)(2,1)S(1)}, u32[]{:S(2)}, u32[]{:S(2)}) %collective-permute-start.1) | collective-permute-done | bytes 131104 | tf_op jit(solution)/shard_map/ppermute | solution.py:23
  16.1 2.8 %collective-permute-start.2 = (bf16[128,512]{1,0:T(8,128)(2,1)S(1)}, bf16[128,512]{1,0:T(8,128)(2,1)S(1)}, u32[]{:S(2)}, u32[]{:S(2)}) collective-permute-start(bf16[128,512]{1,0:T(8,128)(2,1)S(1)} %fusion.26), channel_id=1, source_target_pairs={{0,8},{4,12},{8,0},{12,4},{1,9},{5,13},{9,1},{13,5},{2,10},{6,14},... | collective-permute-start | bytes 393224 | tf_op jit(solution)/shard_map/ppermute | solution.py:30
  19.1 3.3 %collective-permute-start.6 = (bf16[128,512]{1,0:T(8,128)(2,1)S(1)}, bf16[128,512]{1,0:T(8,128)(2,1)S(1)}, u32[]{:S(2)}, u32[]{:S(2)}) collective-permute-start(bf16[128,512]{1,0:T(8,128)(2,1)S(1)} %fusion.27), channel_id=1, source_target_pairs={{0,8},{4,12},{8,0},{12,4},{1,9},{5,13},{9,1},{13,5},{2,10},{6,14},... | collective-permute-start | bytes 393224 | tf_op jit(solution)/shard_map/ppermute | solution.py:30
  22.4 6.6 %collective-permute-done.2 = bf16[128,512]{1,0:T(8,128)(2,1)S(1)} collective-permute-done((bf16[128,512]{1,0:T(8,128)(2,1)S(1)}, bf16[128,512]{1,0:T(8,128)(2,1)S(1)}, u32[]{:S(2)}, u32[]{:S(2)}) %collective-permute-start.2) | collective-permute-done | bytes 131104 | tf_op jit(solution)/shard_map/ppermute | solution.py:30
  29.2 1.7 %collective-permute-done.6 = bf16[128,512]{1,0:T(8,128)(2,1)S(1)} collective-permute-done((bf16[128,512]{1,0:T(8,128)(2,1)S(1)}, bf16[128,512]{1,0:T(8,128)(2,1)S(1)}, u32[]{:S(2)}, u32[]{:S(2)}) %collective-permute-start.6) | collective-permute-done | bytes 131104 | tf_op jit(solution)/shard_map/ppermute | solution.py:30
  30.9 0.6 %collective-permute-start.7 = (bf16[128,512]{1,0:T(8,128)(2,1)S(1)}, bf16[128,512]{1,0:T(8,128)(2,1)S(1)}, u32[]{:S(2)}, u32[]{:S(2)}) collective-permute-start(bf16[128,512]{1,0:T(8,128)(2,1)S(1)} %fusion.20), channel_id=1, source_target_pairs={{0,4},{4,0},{8,12},{12,8},{1,5},{5,1},{9,13},{13,9},{2,6},{6,2},{1... | collective-permute-start | bytes 393224 | tf_op jit(solution)/shard_map/ppermute | solution.py:40
  31.5 3.8 %collective-permute-done.3 = bf16[128,512]{1,0:T(8,128)(2,1)S(1)} collective-permute-done((bf16[128,512]{1,0:T(8,128)(2,1)S(1)}, bf16[128,512]{1,0:T(8,128)(2,1)S(1)}, u32[]{:S(2)}, u32[]{:S(2)}) %collective-permute-start.3) | collective-permute-done | bytes 131104 | tf_op jit(solution)/shard_map/ppermute | solution.py:40
  35.4 0.6 %fusion.12 = bf16[6,256,256]{2,1,0:T(8,128)(2,1)S(1)} fusion(f32[256,512]{1,0:T(8,128)S(1)} %maximum_convert_fusion, bf16[2,6,256,512]{3,2,1,0:T(8,128)(2,1)S(1)} %bitcast.79, bf16[512,256]{1,0:T(8,128)(2,1)S(1)} %copy-done), kind=kOutput, calls=%fused_computation.19 | convolution fusion | flops 405405696 | bytes 3145728 | tf_op jit(solution)/shard_map/mrn,nc->mrc/dot_general | solution.py:106
  36.4 0.3 collective-permute-done.7
  36.8 0.6 %fusion.15 = bf16[6,256,256]{2,1,0:T(8,128)(2,1)S(1)} fusion(f32[256,512]{1,0:T(8,128)S(1)} %maximum_convert_fusion.1, bf16[2,6,256,512]{3,2,1,0:T(8,128)(2,1)S(1)} %bitcast.80, bf16[512,256]{1,0:T(8,128)(2,1)S(1)} %copy-done), kind=kOutput, calls=%fused_computation.20 | convolution fusion | flops 405405696 | bytes 3145728 | tf_op jit(solution)/shard_map/mrn,nc->mrc/dot_general | solution.py:106
  38.0 0.7 %collective-permute-done.4 = f32[128,6,256]{2,0,1:T(8,128)S(1)} collective-permute-done((f32[128,6,256]{2,0,1:T(8,128)S(1)}, f32[128,6,256]{2,0,1:T(8,128)S(1)}, u32[]{:S(2)}, u32[]{:S(2)}) %collective-permute-start.4) | collective-permute-done | bytes 786464 | tf_op jit(solution)/shard_map/ppermute | solution.py:8
  39.0 1.1 %collective-permute-done.8 = f32[128,6,256]{2,0,1:T(8,128)S(1)} collective-permute-done((f32[128,6,256]{2,0,1:T(8,128)S(1)}, f32[128,6,256]{2,0,1:T(8,128)S(1)}, u32[]{:S(2)}, u32[]{:S(2)}) %collective-permute-start.8) | collective-permute-done | bytes 786464 | tf_op jit(solution)/shard_map/ppermute | solution.py:8
  40.6 1.7 %copy.14 = bf16[128,6,2,256]{3,2,1,0:T(2,128)(2,1)} copy(bf16[128,6,2,256]{3,0,1,2:T(8,128)(2,1)S(1)} %fusion.8) | data formatting | bytes 1572864 | tf_op jit(solution)/shard_map/convert_element_type | solution.py:121
  (31 shorter events, 2.5 us)
Async XLA Ops:
  0.0 7.2 %copy-start = (bf16[512,256]{1,0:T(8,128)(2,1)S(1)}, bf16[512,256]{1,0:T(8,128)(2,1)}, u32[]{:S(2)}) copy-start(bf16[512,256]{1,0:T(8,128)(2,1)} %param.9) | copy-start | bytes 786436
  1.3 5.3 %collective-permute-start = (bf16[128,6,2,256]{3,0,2,1:T(8,128)(2,1)S(1)}, bf16[128,6,2,256]{3,0,2,1:T(8,128)(2,1)S(1)}, u32[]{:S(2)}, u32[]{:S(2)}) collective-permute-start(bf16[128,6,2,256]{3,0,2,1:T(8,128)(2,1)S(1)} %copy.8), channel_id=1, source_target_pairs={{0,1},{1,0},{2,3},{3,2},{4,5},{5,4},{6,7},{7,6},{8,9},{9,8},{10,11... | collective-permute-start | bytes 2359304 | tf_op jit(solution)/shard_map/ppermute | solution.py:8
  1.8 4.3 %copy-start.1 = (bf16[128,6,2,256]{3,2,1,0:T(2,128)(2,1)S(1)}, bf16[128,6,2,256]{3,2,1,0:T(2,128)(2,1)}, u32[]{:S(2)}) copy-start(bf16[128,6,2,256]{3,2,1,0:T(2,128)(2,1)} %param.6) | copy-start | bytes 2359300
  1.8 4.3 %copy-start.3 = (bf16[256,256]{1,0:T(8,128)(2,1)S(1)}, bf16[256,256]{1,0:T(8,128)(2,1)}, u32[]{:S(2)}) copy-start(bf16[256,256]{1,0:T(8,128)(2,1)} %param.8) | copy-start | bytes 393220
  6.6 1.9 %copy-start.2 = (bf16[256,6,2,512]{3,0,1,2:T(8,128)(2,1)S(1)}, bf16[256,6,2,512]{3,0,1,2:T(8,128)(2,1)}, u32[]{:S(2)}) copy-start(bf16[256,6,2,512]{3,0,1,2:T(8,128)(2,1)} %copy.33) | copy-start | bytes 9437188
  9.2 3.4 %copy-start.4 = (f32[256,2,512]{2,1,0:T(2,128)S(1)}, f32[256,2,512]{2,1,0:T(2,128)}, u32[]{:S(2)}) copy-start(f32[256,2,512]{2,1,0:T(2,128)} %param.7) | copy-start | bytes 3145732
  9.2 6.8 %collective-permute-start.1 = (bf16[128,512]{1,0:T(8,128)(2,1)S(1)}, bf16[128,512]{1,0:T(8,128)(2,1)S(1)}, u32[]{:S(2)}, u32[]{:S(2)}) collective-permute-start(bf16[128,512]{1,0:T(8,128)(2,1)S(1)} %dynamic-slice_convert_fusion.1), channel_id=1, source_target_pairs={{0,4},{4,0},{8,12},{12,8},{1,5},{5,1},{9,13},{13,9},{2,6},{6,2},{1... | collective-permute-start | bytes 393224 | tf_op jit(solution)/shard_map/ppermute | solution.py:23
  13.5 5.6 %collective-permute-start.5 = (bf16[128,512]{1,0:T(8,128)(2,1)S(1)}, bf16[128,512]{1,0:T(8,128)(2,1)S(1)}, u32[]{:S(2)}, u32[]{:S(2)}) collective-permute-start(bf16[128,512]{1,0:T(8,128)(2,1)S(1)} %dynamic-slice_convert_fusion), channel_id=1, source_target_pairs={{0,4},{4,0},{8,12},{12,8},{1,5},{5,1},{9,13},{13,9},{2,6},{6,2},{1... | collective-permute-start | bytes 393224 | tf_op jit(solution)/shard_map/ppermute | solution.py:23
  16.1 12.9 %collective-permute-start.2 = (bf16[128,512]{1,0:T(8,128)(2,1)S(1)}, bf16[128,512]{1,0:T(8,128)(2,1)S(1)}, u32[]{:S(2)}, u32[]{:S(2)}) collective-permute-start(bf16[128,512]{1,0:T(8,128)(2,1)S(1)} %fusion.26), channel_id=1, source_target_pairs={{0,8},{4,12},{8,0},{12,4},{1,9},{5,13},{9,1},{13,5},{2,10},{6,14},... | collective-permute-start | bytes 393224 | tf_op jit(solution)/shard_map/ppermute | solution.py:30
  19.1 11.7 %collective-permute-start.6 = (bf16[128,512]{1,0:T(8,128)(2,1)S(1)}, bf16[128,512]{1,0:T(8,128)(2,1)S(1)}, u32[]{:S(2)}, u32[]{:S(2)}) collective-permute-start(bf16[128,512]{1,0:T(8,128)(2,1)S(1)} %fusion.27), channel_id=1, source_target_pairs={{0,8},{4,12},{8,0},{12,4},{1,9},{5,13},{9,1},{13,5},{2,10},{6,14},... | collective-permute-start | bytes 393224 | tf_op jit(solution)/shard_map/ppermute | solution.py:30
  29.1 6.3 %collective-permute-start.3 = (bf16[128,512]{1,0:T(8,128)(2,1)S(1)}, bf16[128,512]{1,0:T(8,128)(2,1)S(1)}, u32[]{:S(2)}, u32[]{:S(2)}) collective-permute-start(bf16[128,512]{1,0:T(8,128)(2,1)S(1)} %fusion.21), channel_id=1, source_target_pairs={{0,4},{4,0},{8,12},{12,8},{1,5},{5,1},{9,13},{13,9},{2,6},{6,2},{1... | collective-permute-start | bytes 393224 | tf_op jit(solution)/shard_map/ppermute | solution.py:40
  30.9 5.8 %collective-permute-start.7 = (bf16[128,512]{1,0:T(8,128)(2,1)S(1)}, bf16[128,512]{1,0:T(8,128)(2,1)S(1)}, u32[]{:S(2)}, u32[]{:S(2)}) collective-permute-start(bf16[128,512]{1,0:T(8,128)(2,1)S(1)} %fusion.20), channel_id=1, source_target_pairs={{0,4},{4,0},{8,12},{12,8},{1,5},{5,1},{9,13},{13,9},{2,6},{6,2},{1... | collective-permute-start | bytes 393224 | tf_op jit(solution)/shard_map/ppermute | solution.py:40
  36.3 2.4 %collective-permute-start.4 = (f32[128,6,256]{2,0,1:T(8,128)S(1)}, f32[128,6,256]{2,0,1:T(8,128)S(1)}, u32[]{:S(2)}, u32[]{:S(2)}) collective-permute-start(f32[128,6,256]{2,0,1:T(8,128)S(1)} %fusion.33), channel_id=1, source_target_pairs={{0,1},{1,0},{2,3},{3,2},{4,5},{5,4},{6,7},{7,6},{8,9},{9,8},{10,11... | collective-permute-start | bytes 2359304 | tf_op jit(solution)/shard_map/ppermute | solution.py:8
  37.7 2.4 %collective-permute-start.8 = (f32[128,6,256]{2,0,1:T(8,128)S(1)}, f32[128,6,256]{2,0,1:T(8,128)S(1)}, u32[]{:S(2)}, u32[]{:S(2)}) collective-permute-start(f32[128,6,256]{2,0,1:T(8,128)S(1)} %fusion.31), channel_id=1, source_target_pairs={{0,1},{1,0},{2,3},{3,2},{4,5},{5,4},{6,7},{7,6},{8,9},{9,8},{10,11... | collective-permute-start | bytes 2359304 | tf_op jit(solution)/shard_map/ppermute | solution.py:8

commit v29 on v24

--- a/solution.py
+++ b/solution.py
@@ -98,7 +98,7 @@
             "mrn,nc->mrc", scaled, col_factor, preferred_element_type=jnp.float32
         ).astype(jnp.bfloat16)
         n_m = projected.shape[0]
-        cuts = [0, n_m]
+        cuts = [i * n_m // 2 for i in range(3)]
         chunks = [(lo, hi) for lo, hi in zip(cuts[:-1], cuts[1:]) if lo < hi]
         summed = jnp.einsum("rk,mrc->kmc", rf_own, projected, preferred_element_type=jnp.float32)
         other = []

time: 42.5 us -> 43.1 us (1.014)
  starting transfers between devices: 10.3 us -> 11.2 us
  waiting for transfers between devices: 17 us -> 16.3 us
    ppermute x3 -> x5, starting transfers between devices: 0.82 us -> 1.72 us  [_swap(): return lax.ppermute(x, axis, [(0, 1), (1, 0)])]
    dot_general x2 -> x4, matrix products: 0.6 us -> 0.96 us  [local(): jnp.einsum('rk,mrc->kmc', rf_other, projected[lo:hi], preferred_element_t...]
    ppermute x3 -> x5, waiting for transfers between devices: 1.81 us -> 1.47 us  [_swap(): return lax.ppermute(x, axis, [(0, 1), (1, 0)])]
  transfers between devices with their start and end apart: 9 -> 11, of which waited for: 8 -> 7; matrix products, arithmetic and copies ran while one was open for 21% -> 21% of each run, Pallas kernels for 0% -> 0%
where the time goes in v29:
time: 43.1 us; the launch traced here: 42.9 us
  waiting for transfers between devices  16.3 us (38%)
  starting transfers between devices  11.2 us (26%)
  local copies, waits for them, and re-layouts  9.43 us (22%)
  matrix products  5.16 us (12%)
  other arithmetic  0.62 us (1%)
    ppermute x4, waiting for transfers between devices, _reduce_scatter_rows(): recv = lax.ppermute(send, axis, [(i, i ^ d) for i in range(size)])  11 us
    ppermute x4, starting transfers between devices, _reduce_scatter_rows(): recv = lax.ppermute(send, axis, [(i, i ^ d) for i in range(size)])  8.85 us
    unnamed x12, local copies, waits for them, and re-layouts  6.84 us
    ppermute x2, waiting for transfers between devices, _all_gather_rows(): recv = lax.ppermute(x, axis, [(i, i ^ d) for i in range(size)])  3.84 us
    ppermute x5, starting transfers between devices, _swap(): return lax.ppermute(x, axis, [(0, 1), (1, 0)])  1.72 us
    convert_element_type x1, local copies, waits for them, and re-layouts, local(): (control.astype(jnp.float32) + jnp.stack(outs, axis=2)).astype(jnp.bfloat16)  1.69 us
    ppermute x5, waiting for transfers between devices, _swap(): return lax.ppermute(x, axis, [(0, 1), (1, 0)])  1.47 us
    dot_general x2, matrix products, local(): jnp.einsum('mrc,nc->mrn', expanded, cf_next, preferred_element_type=jnp.f...  1.32 us
  transfers between devices with their start and end apart: 11, of which 7 were waited for; matrix products, arithmetic and copies ran while one was open for 21% of the time, Pallas kernels for 0%

profile of v29, /device:TPU:0, one launch (start us, length us, event | category | flops | bytes accessed | tf_op | source)
XLA Modules:
  0.0 42.9 jit_solution(17487989972468524364)
XLA Ops:
  0.0 1.3 %copy.8 = bf16[128,6,2,256]{3,0,2,1:T(8,128)(2,1)S(1)} copy(bf16[128,6,2,256]{3,2,1,0:T(2,128)(2,1)} %param.6) | data formatting | bytes 1572864 | tf_op args[1]
  1.3 0.5 %collective-permute-start = (bf16[128,6,2,256]{3,0,2,1:T(8,128)(2,1)S(1)}, bf16[128,6,2,256]{3,0,2,1:T(8,128)(2,1)S(1)}, u32[]{:S(2)}, u32[]{:S(2)}) collective-permute-start(bf16[128,6,2,256]{3,0,2,1:T(8,128)(2,1)S(1)} %copy.8), channel_id=1, source_target_pairs={{0,1},{1,0},{2,3},{3,2},{4,5},{5,4},{6,7},{7,6},{8,9},{9,8},{10,11... | collective-permute-start | bytes 2359304 | tf_op jit(solution)/shard_map/ppermute | solution.py:8
  1.8 4.3 %copy.39 = bf16[256,6,2,512]{3,0,1,2:T(8,128)(2,1)} copy(bf16[256,6,2,512]{3,2,1,0:T(2,128)(2,1)} %param.5) | data formatting | bytes 6291456 | tf_op args[0]
  6.1 0.6 %fusion.37 = f32[256,6,2,256]{3,0,2,1:T(8,128)S(1)} fusion(bf16[256,256]{1,0:T(8,128)(2,1)S(1)} %copy-done.3, s32[]{:T(128)S(6)} %select_n.57, bf16[128,6,2,256]{3,2,1,0:T(2,128)(2,1)S(1)} %copy-done.1), kind=kOutput, calls=%fused_computation.56 | convolution fusion | flops 201326592 | bytes 3997700 | tf_op jit(solution)/shard_map/rk,kmlc->lmrc/dot_general | solution.py:71
  6.7 0.6 %fusion.11 = bf16[2,6,256,256]{3,2,0,1:T(8,128)(2,1)S(1)} fusion(f32[256,6,2,256]{3,0,2,1:T(8,128)S(1)} %fusion.37, bf16[128,6,2,256]{3,0,2,1:T(8,128)(2,1)S(1)} %collective-permute-done, bf16[256,256]{1,0:T(8,128)(2,1)S(1)} %copy-done.3, s32[]{:T(128)S(6)} %select_n.60), kind=kOutput, calls=%fused_computation.18 | convolution fusion | flops 202899456 | bytes 5570564 | tf_op jit(solution)/shard_map/rk,kmlc->lmrc/dot_general | solution.py:72
  7.3 1.3 %copy-done.2 = bf16[256,6,2,512]{3,0,1,2:T(8,128)(2,1)S(1)} copy-done((bf16[256,6,2,512]{3,0,1,2:T(8,128)(2,1)S(1)}, bf16[256,6,2,512]{3,0,1,2:T(8,128)(2,1)}, u32[]{:S(2)}) %copy-start.2) | copy-done | bytes 3145752
  8.5 0.7 %fusion = f32[256,512]{1,0:T(8,128)S(1)} fusion(bf16[2,6,256,512]{3,2,1,0:T(8,128)(2,1)S(1)} %bitcast.85, bf16[2,6,256,256]{3,2,0,1:T(8,128)(2,1)S(1)} %fusion.11, bf16[512,256]{1,0:T(8,128)(2,1)S(1)} %copy-done), kind=kOutput, calls=%fused_computation.4 | convolution fusion | flops 404881408 | bytes 3145728 | tf_op jit(solution)/shard_map/mrc,nc->mrn/dot_general | solution.py:84
  9.2 2.7 %collective-permute-start.1 = (bf16[128,512]{1,0:T(8,128)(2,1)S(1)}, bf16[128,512]{1,0:T(8,128)(2,1)S(1)}, u32[]{:S(2)}, u32[]{:S(2)}) collective-permute-start(bf16[128,512]{1,0:T(8,128)(2,1)S(1)} %dynamic-slice_convert_fusion.1), channel_id=1, source_target_pairs={{0,4},{4,0},{8,12},{12,8},{1,5},{5,1},{9,13},{13,9},{2,6},{6,2},{1... | collective-permute-start | bytes 393224 | tf_op jit(solution)/shard_map/ppermute | solution.py:23
  11.9 0.8 %fusion.68 = (f32[1,256,512]{2,0,1:T(1,128)S(1)}, f32[1,256,512]{2,0,1:T(1,128)S(1)}) fusion(f32[2,256,512]{2,0,1:T(2,128)S(1)} %bitcast.89), kind=kLoop, calls=%fused_computation.85 | loop fusion | bytes 2097152 | tf_op jit(solution)/shard_map/slice | solution.py:89
  12.7 0.7 %fusion.2 = f32[256,512]{1,0:T(8,128)S(1)} fusion(bf16[2,6,256,512]{3,2,1,0:T(8,128)(2,1)S(1)} %bitcast.86, bf16[2,6,256,256]{3,2,0,1:T(8,128)(2,1)S(1)} %fusion.11, bf16[512,256]{1,0:T(8,128)(2,1)S(1)} %copy-done), kind=kOutput, calls=%fused_computation.6 | convolution fusion | flops 404881408 | bytes 3145728 | tf_op jit(solution)/shard_map/mrc,nc->mrn/dot_general | solution.py:84
  13.6 2.4 %collective-permute-done.1 = bf16[128,512]{1,0:T(8,128)(2,1)S(1)} collective-permute-done((bf16[128,512]{1,0:T(8,128)(2,1)S(1)}, bf16[128,512]{1,0:T(8,128)(2,1)S(1)}, u32[]{:S(2)}, u32[]{:S(2)}) %collective-permute-start.1) | collective-permute-done | bytes 131104 | tf_op jit(solution)/shard_map/ppermute | solution.py:23
  16.1 2.8 %collective-permute-start.2 = (bf16[128,512]{1,0:T(8,128)(2,1)S(1)}, bf16[128,512]{1,0:T(8,128)(2,1)S(1)}, u32[]{:S(2)}, u32[]{:S(2)}) collective-permute-start(bf16[128,512]{1,0:T(8,128)(2,1)S(1)} %fusion.34), channel_id=1, source_target_pairs={{0,8},{4,12},{8,0},{12,4},{1,9},{5,13},{9,1},{13,5},{2,10},{6,14},... | collective-permute-start | bytes 393224 | tf_op jit(solution)/shard_map/ppermute | solution.py:30
  19.1 3.2 %collective-permute-start.7 = (bf16[128,512]{1,0:T(8,128)(2,1)S(1)}, bf16[128,512]{1,0:T(8,128)(2,1)S(1)}, u32[]{:S(2)}, u32[]{:S(2)}) collective-permute-start(bf16[128,512]{1,0:T(8,128)(2,1)S(1)} %fusion.35), channel_id=1, source_target_pairs={{0,8},{4,12},{8,0},{12,4},{1,9},{5,13},{9,1},{13,5},{2,10},{6,14},... | collective-permute-start | bytes 393224 | tf_op jit(solution)/shard_map/ppermute | solution.py:30
  22.4 6.6 %collective-permute-done.2 = bf16[128,512]{1,0:T(8,128)(2,1)S(1)} collective-permute-done((bf16[128,512]{1,0:T(8,128)(2,1)S(1)}, bf16[128,512]{1,0:T(8,128)(2,1)S(1)}, u32[]{:S(2)}, u32[]{:S(2)}) %collective-permute-start.2) | collective-permute-done | bytes 131104 | tf_op jit(solution)/shard_map/ppermute | solution.py:30
  29.2 1.7 %collective-permute-done.7 = bf16[128,512]{1,0:T(8,128)(2,1)S(1)} collective-permute-done((bf16[128,512]{1,0:T(8,128)(2,1)S(1)}, bf16[128,512]{1,0:T(8,128)(2,1)S(1)}, u32[]{:S(2)}, u32[]{:S(2)}) %collective-permute-start.7) | collective-permute-done | bytes 131104 | tf_op jit(solution)/shard_map/ppermute | solution.py:30
  30.9 0.6 %collective-permute-start.8 = (bf16[128,512]{1,0:T(8,128)(2,1)S(1)}, bf16[128,512]{1,0:T(8,128)(2,1)S(1)}, u32[]{:S(2)}, u32[]{:S(2)}) collective-permute-start(bf16[128,512]{1,0:T(8,128)(2,1)S(1)} %fusion.28), channel_id=1, source_target_pairs={{0,4},{4,0},{8,12},{12,8},{1,5},{5,1},{9,13},{13,9},{2,6},{6,2},{1... | collective-permute-start | bytes 393224 | tf_op jit(solution)/shard_map/ppermute | solution.py:40
  31.5 3.8 %collective-permute-done.3 = bf16[128,512]{1,0:T(8,128)(2,1)S(1)} collective-permute-done((bf16[128,512]{1,0:T(8,128)(2,1)S(1)}, bf16[128,512]{1,0:T(8,128)(2,1)S(1)}, u32[]{:S(2)}, u32[]{:S(2)}) %collective-permute-start.3) | collective-permute-done | bytes 131104 | tf_op jit(solution)/shard_map/ppermute | solution.py:40
  35.4 0.6 %fusion.12 = bf16[6,256,256]{2,1,0:T(8,128)(2,1)S(1)} fusion(f32[256,512]{1,0:T(8,128)S(1)} %maximum_convert_fusion, bf16[2,6,256,512]{3,2,1,0:T(8,128)(2,1)S(1)} %bitcast.87, bf16[512,256]{1,0:T(8,128)(2,1)S(1)} %copy-done), kind=kOutput, calls=%fused_computation.19 | convolution fusion | flops 405405696 | bytes 3145728 | tf_op jit(solution)/shard_map/mrn,nc->mrc/dot_general | solution.py:97
  36.6 0.6 %collective-permute-start.5 = (f32[128,3,256]{2,0,1:T(8,128)S(1)}, f32[128,3,256]{2,0,1:T(8,128)S(1)}, u32[]{:S(2)}, u32[]{:S(2)}) collective-permute-start(f32[128,3,256]{2,0,1:T(8,128)S(1)} %fusion.24), channel_id=1, source_target_pairs={{0,1},{1,0},{2,3},{3,2},{4,5},{5,4},{6,7},{7,6},{8,9},{9,8},{10,11... | collective-permute-start | bytes 1179656 | tf_op jit(solution)/shard_map/ppermute | solution.py:8
  37.2 0.6 %fusion.15 = bf16[6,256,256]{2,1,0:T(8,128)(2,1)S(1)} fusion(f32[256,512]{1,0:T(8,128)S(1)} %maximum_convert_fusion.1, bf16[2,6,256,512]{3,2,1,0:T(8,128)(2,1)S(1)} %bitcast.88, bf16[512,256]{1,0:T(8,128)(2,1)S(1)} %copy-done), kind=kOutput, calls=%fused_computation.20 | convolution fusion | flops 405405696 | bytes 3145728 | tf_op jit(solution)/shard_map/mrn,nc->mrc/dot_general | solution.py:97
  38.4 0.5 %collective-permute-start.10 = (f32[128,3,256]{2,0,1:T(8,128)S(1)}, f32[128,3,256]{2,0,1:T(8,128)S(1)}, u32[]{:S(2)}, u32[]{:S(2)}) collective-permute-start(f32[128,3,256]{2,0,1:T(8,128)S(1)} %fusion.20), channel_id=1, source_target_pairs={{0,1},{1,0},{2,3},{3,2},{4,5},{5,4},{6,7},{7,6},{8,9},{9,8},{10,11... | collective-permute-start | bytes 1179656 | tf_op jit(solution)/shard_map/ppermute | solution.py:8
  39.2 0.9 %collective-permute-done.9 = f32[128,3,256]{2,0,1:T(8,128)S(1)} collective-permute-done((f32[128,3,256]{2,0,1:T(8,128)S(1)}, f32[128,3,256]{2,0,1:T(8,128)S(1)}, u32[]{:S(2)}, u32[]{:S(2)}) %collective-permute-start.9) | collective-permute-done | bytes 393248 | tf_op jit(solution)/shard_map/ppermute | solution.py:8
  40.1 0.6 %collective-permute-done.10 = f32[128,3,256]{2,0,1:T(8,128)S(1)} collective-permute-done((f32[128,3,256]{2,0,1:T(8,128)S(1)}, f32[128,3,256]{2,0,1:T(8,128)S(1)}, u32[]{:S(2)}, u32[]{:S(2)}) %collective-permute-start.10) | collective-permute-done | bytes 393248 | tf_op jit(solution)/shard_map/ppermute | solution.py:8
  41.2 1.7 %copy.16 = bf16[128,6,2,256]{3,2,1,0:T(2,128)(2,1)} copy(bf16[128,6,2,256]{3,0,1,2:T(8,128)(2,1)S(1)} %fusion.8) | data formatting | bytes 1572864 | tf_op jit(solution)/shard_map/convert_element_type | solution.py:112
  (37 shorter events, 2.8 us)
Async XLA Ops:
  0.0 7.3 %copy-start = (bf16[512,256]{1,0:T(8,128)(2,1)S(1)}, bf16[512,256]{1,0:T(8,128)(2,1)}, u32[]{:S(2)}) copy-start(bf16[512,256]{1,0:T(8,128)(2,1)} %param.9) | copy-start | bytes 786436
  1.3 5.4 %collective-permute-start = (bf16[128,6,2,256]{3,0,2,1:T(8,128)(2,1)S(1)}, bf16[128,6,2,256]{3,0,2,1:T(8,128)(2,1)S(1)}, u32[]{:S(2)}, u32[]{:S(2)}) collective-permute-start(bf16[128,6,2,256]{3,0,2,1:T(8,128)(2,1)S(1)} %copy.8), channel_id=1, source_target_pairs={{0,1},{1,0},{2,3},{3,2},{4,5},{5,4},{6,7},{7,6},{8,9},{9,8},{10,11... | collective-permute-start | bytes 2359304 | tf_op jit(solution)/shard_map/ppermute | solution.py:8
  1.8 4.3 %copy-start.1 = (bf16[128,6,2,256]{3,2,1,0:T(2,128)(2,1)S(1)}, bf16[128,6,2,256]{3,2,1,0:T(2,128)(2,1)}, u32[]{:S(2)}) copy-start(bf16[128,6,2,256]{3,2,1,0:T(2,128)(2,1)} %param.6) | copy-start | bytes 2359300
  1.8 4.3 %copy-start.3 = (bf16[256,256]{1,0:T(8,128)(2,1)S(1)}, bf16[256,256]{1,0:T(8,128)(2,1)}, u32[]{:S(2)}) copy-start(bf16[256,256]{1,0:T(8,128)(2,1)} %param.8) | copy-start | bytes 393220
  6.6 1.9 %copy-start.2 = (bf16[256,6,2,512]{3,0,1,2:T(8,128)(2,1)S(1)}, bf16[256,6,2,512]{3,0,1,2:T(8,128)(2,1)}, u32[]{:S(2)}) copy-start(bf16[256,6,2,512]{3,0,1,2:T(8,128)(2,1)} %copy.39) | copy-start | bytes 9437188
  7.2 4.7 %copy-start.4 = (f32[256,2,512]{2,1,0:T(2,128)S(1)}, f32[256,2,512]{2,1,0:T(2,128)}, u32[]{:S(2)}) copy-start(f32[256,2,512]{2,1,0:T(2,128)} %param.7) | copy-start | bytes 3145732
  9.2 6.8 %collective-permute-start.1 = (bf16[128,512]{1,0:T(8,128)(2,1)S(1)}, bf16[128,512]{1,0:T(8,128)(2,1)S(1)}, u32[]{:S(2)}, u32[]{:S(2)}) collective-permute-start(bf16[128,512]{1,0:T(8,128)(2,1)S(1)} %dynamic-slice_convert_fusion.1), channel_id=1, source_target_pairs={{0,4},{4,0},{8,12},{12,8},{1,5},{5,1},{9,13},{13,9},{2,6},{6,2},{1... | collective-permute-start | bytes 393224 | tf_op jit(solution)/shard_map/ppermute | solution.py:23
  13.5 5.6 %collective-permute-start.6 = (bf16[128,512]{1,0:T(8,128)(2,1)S(1)}, bf16[128,512]{1,0:T(8,128)(2,1)S(1)}, u32[]{:S(2)}, u32[]{:S(2)}) collective-permute-start(bf16[128,512]{1,0:T(8,128)(2,1)S(1)} %dynamic-slice_convert_fusion), channel_id=1, source_target_pairs={{0,4},{4,0},{8,12},{12,8},{1,5},{5,1},{9,13},{13,9},{2,6},{6,2},{1... | collective-permute-start | bytes 393224 | tf_op jit(solution)/shard_map/ppermute | solution.py:23
  16.1 12.9 %collective-permute-start.2 = (bf16[128,512]{1,0:T(8,128)(2,1)S(1)}, bf16[128,512]{1,0:T(8,128)(2,1)S(1)}, u32[]{:S(2)}, u32[]{:S(2)}) collective-permute-start(bf16[128,512]{1,0:T(8,128)(2,1)S(1)} %fusion.34), channel_id=1, source_target_pairs={{0,8},{4,12},{8,0},{12,4},{1,9},{5,13},{9,1},{13,5},{2,10},{6,14},... | collective-permute-start | bytes 393224 | tf_op jit(solution)/shard_map/ppermute | solution.py:30
  19.1 11.7 %collective-permute-start.7 = (bf16[128,512]{1,0:T(8,128)(2,1)S(1)}, bf16[128,512]{1,0:T(8,128)(2,1)S(1)}, u32[]{:S(2)}, u32[]{:S(2)}) collective-permute-start(bf16[128,512]{1,0:T(8,128)(2,1)S(1)} %fusion.35), channel_id=1, source_target_pairs={{0,8},{4,12},{8,0},{12,4},{1,9},{5,13},{9,1},{13,5},{2,10},{6,14},... | collective-permute-start | bytes 393224 | tf_op jit(solution)/shard_map/ppermute | solution.py:30
  29.1 6.3 %collective-permute-start.3 = (bf16[128,512]{1,0:T(8,128)(2,1)S(1)}, bf16[128,512]{1,0:T(8,128)(2,1)S(1)}, u32[]{:S(2)}, u32[]{:S(2)}) collective-permute-start(bf16[128,512]{1,0:T(8,128)(2,1)S(1)} %fusion.29), channel_id=1, source_target_pairs={{0,4},{4,0},{8,12},{12,8},{1,5},{5,1},{9,13},{13,9},{2,6},{6,2},{1... | collective-permute-start | bytes 393224 | tf_op jit(solution)/shard_map/ppermute | solution.py:40
  30.9 6.2 %collective-permute-start.8 = (bf16[128,512]{1,0:T(8,128)(2,1)S(1)}, bf16[128,512]{1,0:T(8,128)(2,1)S(1)}, u32[]{:S(2)}, u32[]{:S(2)}) collective-permute-start(bf16[128,512]{1,0:T(8,128)(2,1)S(1)} %fusion.28), channel_id=1, source_target_pairs={{0,4},{4,0},{8,12},{12,8},{1,5},{5,1},{9,13},{13,9},{2,6},{6,2},{1... | collective-permute-start | bytes 393224 | tf_op jit(solution)/shard_map/ppermute | solution.py:40
  36.3 2.6 %collective-permute-start.4 = (f32[128,3,256]{2,0,1:T(8,128)S(1)}, f32[128,3,256]{2,0,1:T(8,128)S(1)}, u32[]{:S(2)}, u32[]{:S(2)}) collective-permute-start(f32[128,3,256]{2,0,1:T(8,128)S(1)} %fusion.26), channel_id=1, source_target_pairs={{0,1},{1,0},{2,3},{3,2},{4,5},{5,4},{6,7},{7,6},{8,9},{9,8},{10,11... | collective-permute-start | bytes 1179656 | tf_op jit(solution)/shard_map/ppermute | solution.py:8
  36.6 2.3 %collective-permute-start.5 = (f32[128,3,256]{2,0,1:T(8,128)S(1)}, f32[128,3,256]{2,0,1:T(8,128)S(1)}, u32[]{:S(2)}, u32[]{:S(2)}) collective-permute-start(f32[128,3,256]{2,0,1:T(8,128)S(1)} %fusion.24), channel_id=1, source_target_pairs={{0,1},{1,0},{2,3},{3,2},{4,5},{5,4},{6,7},{7,6},{8,9},{9,8},{10,11... | collective-permute-start | bytes 1179656 | tf_op jit(solution)/shard_map/ppermute | solution.py:8
  38.3 1.8 %collective-permute-start.9 = (f32[128,3,256]{2,0,1:T(8,128)S(1)}, f32[128,3,256]{2,0,1:T(8,128)S(1)}, u32[]{:S(2)}, u32[]{:S(2)}) collective-permute-start(f32[128,3,256]{2,0,1:T(8,128)S(1)} %fusion.22), channel_id=1, source_target_pairs={{0,1},{1,0},{2,3},{3,2},{4,5},{5,4},{6,7},{7,6},{8,9},{9,8},{10,11... | collective-permute-start | bytes 1179656 | tf_op jit(solution)/shard_map/ppermute | solution.py:8
  38.4 2.3 %collective-permute-start.10 = (f32[128,3,256]{2,0,1:T(8,128)S(1)}, f32[128,3,256]{2,0,1:T(8,128)S(1)}, u32[]{:S(2)}, u32[]{:S(2)}) collective-permute-start(f32[128,3,256]{2,0,1:T(8,128)S(1)} %fusion.20), channel_id=1, source_target_pairs={{0,1},{1,0},{2,3},{3,2},{4,5},{5,4},{6,7},{7,6},{8,9},{9,8},{10,11... | collective-permute-start | bytes 1179656 | tf_op jit(solution)/shard_map/ppermute | solution.py:8

commit v30 on v24

--- a/solution.py
+++ b/solution.py
@@ -84,7 +84,6 @@
         fields = jnp.einsum("mrc,nc->mrn", expanded, cf_next, preferred_element_type=jnp.float32)
         inc = jnp.sum(a.astype(jnp.float32) * fields, axis=0)
         if l == 0:
-            precision, inc = lax.optimization_barrier((precision, inc))
             prec_t = jnp.transpose(precision, (1, 0, 2))
         prec = prec_t[l]
         if pow2:

time: 42.5 us -> 43.7 us (1.028)
  matrix products: 4.81 us -> 6.1 us
  waiting for transfers between devices: 17 us -> 18 us
  local copies, waits for them, and re-layouts: 9.42 us -> 8.65 us
    dot_general x1, matrix products: 0.58 us -> 1.86 us  [local(): jnp.einsum('rk,kmlc->lmrc', rf_other, ctrl_other, preferred_element_type=...]
    ppermute x4, waiting for transfers between devices: 11 us -> 12.2 us  [_reduce_scatter_rows(): recv = lax.ppermute(send, axis, [(i, i ^ d) for i in range(size)])]
    unnamed x12, local copies, waits for them, and re-layouts: 6.83 us -> 6.04 us
  transfers between devices with their start and end apart: 9 -> 9, of which waited for: 8 -> 7; matrix products, arithmetic and copies ran while one was open for 21% -> 20% of each run, Pallas kernels for 0% -> 0%
where the time goes in v30:
time: 43.7 us; the launch traced here: 43.6 us
  waiting for transfers between devices  18 us (41%)
  starting transfers between devices  10 us (23%)
  local copies, waits for them, and re-layouts  8.65 us (20%)
  matrix products  6.1 us (14%)
  other arithmetic  0.61 us (1%)
    ppermute x4, waiting for transfers between devices, _reduce_scatter_rows(): recv = lax.ppermute(send, axis, [(i, i ^ d) for i in range(size)])  12.2 us
    ppermute x4, starting transfers between devices, _reduce_scatter_rows(): recv = lax.ppermute(send, axis, [(i, i ^ d) for i in range(size)])  8.55 us
    unnamed x12, local copies, waits for them, and re-layouts  6.04 us
    ppermute x2, waiting for transfers between devices, _all_gather_rows(): recv = lax.ppermute(x, axis, [(i, i ^ d) for i in range(size)])  4.04 us
    dot_general x1, matrix products, local(): jnp.einsum('rk,kmlc->lmrc', rf_other, ctrl_other, preferred_element_type=...  1.86 us
    ppermute x3, waiting for transfers between devices, _swap(): return lax.ppermute(x, axis, [(0, 1), (1, 0)])  1.83 us
    convert_element_type x1, local copies, waits for them, and re-layouts, local(): (control.astype(jnp.float32) + jnp.stack(outs, axis=2)).astype(jnp.bfloat16)  1.69 us
    dot_general x2, matrix products, local(): jnp.einsum('mrc,nc->mrn', expanded, cf_next, preferred_element_type=jnp.f...  1.33 us
  transfers between devices with their start and end apart: 9, of which 7 were waited for; matrix products, arithmetic and copies ran while one was open for 20% of the time, Pallas kernels for 0%

profile of v30, /device:TPU:0, one launch (start us, length us, event | category | flops | bytes accessed | tf_op | source)
XLA Modules:
  0.0 43.6 jit_solution(3315624815918894126)
XLA Ops:
  0.0 1.3 %copy.8 = bf16[128,6,2,256]{3,0,2,1:T(8,128)(2,1)S(1)} copy(bf16[128,6,2,256]{3,2,1,0:T(2,128)(2,1)} %param.6) | data formatting | bytes 1572864 | tf_op args[1]
  1.3 0.5 %collective-permute-start = (bf16[128,6,2,256]{3,0,2,1:T(8,128)(2,1)S(1)}, bf16[128,6,2,256]{3,0,2,1:T(8,128)(2,1)}, u32[]{:S(2)}, u32[]{:S(2)}) collective-permute-start(bf16[128,6,2,256]{3,0,2,1:T(8,128)(2,1)S(1)} %copy.8), channel_id=1, source_target_pairs={{0,1},{1,0},{2,3},{3,2},{4,5},{5,4},{6,7},{7,6},{8,9},{9,8},{10,11... | collective-permute-start | bytes 2359304 | tf_op jit(solution)/shard_map/ppermute | solution.py:8
  1.8 4.3 %copy.33 = bf16[256,6,2,512]{3,0,1,2:T(8,128)(2,1)} copy(bf16[256,6,2,512]{3,2,1,0:T(2,128)(2,1)} %param.5) | data formatting | bytes 6291456 | tf_op args[0]
  6.1 0.8 %fusion.50 = (f32[1,256,512]{2,0,1:T(1,128)S(1)}, f32[1,256,512]{2,0,1:T(1,128)S(1)}) fusion(f32[2,256,512]{2,0,1:T(2,128)S(1)} %bitcast.81), kind=kLoop, calls=%fused_computation.71 | loop fusion | bytes 2097152 | tf_op jit(solution)/shard_map/slice | solution.py:88
  7.2 0.6 %fusion.29 = f32[256,6,2,256]{3,0,2,1:T(8,128)S(1)} fusion(bf16[256,256]{1,0:T(8,128)(2,1)S(1)} %copy-done.3, s32[]{:T(128)S(6)} %select_n.57, bf16[128,6,2,256]{3,2,1,0:T(2,128)(2,1)S(1)} %copy-done.1), kind=kOutput, calls=%fused_computation.48 | convolution fusion | flops 201326592 | bytes 3997700 | tf_op jit(solution)/shard_map/rk,kmlc->lmrc/dot_general | solution.py:71
  7.8 1.9 %fusion.11 = bf16[2,6,256,256]{3,2,0,1:T(8,128)(2,1)S(1)} fusion(f32[256,6,2,256]{3,0,2,1:T(8,128)S(1)} %fusion.29, bf16[128,6,2,256]{3,0,2,1:T(8,128)(2,1)} %collective-permute-done, bf16[256,256]{1,0:T(8,128)(2,1)S(1)} %copy-done.3, s32[]{:T(128)S(6)} %select_n.61), kind=kOutput, calls=%fused_computation.18 | convolution fusion | flops 202899456 | bytes 5570564 | tf_op jit(solution)/shard_map/rk,kmlc->lmrc/dot_general | solution.py:72
  9.9 0.7 %fusion = f32[256,512]{1,0:T(8,128)S(1)} fusion(bf16[2,6,256,512]{3,2,1,0:T(8,128)(2,1)S(1)} %bitcast.77, bf16[2,6,256,256]{3,2,0,1:T(8,128)(2,1)S(1)} %fusion.11, bf16[512,256]{1,0:T(8,128)(2,1)S(1)} %copy-done), kind=kOutput, calls=%fused_computation.4 | convolution fusion | flops 404881408 | bytes 3145728 | tf_op jit(solution)/shard_map/mrc,nc->mrn/dot_general | solution.py:84
  10.6 2.7 %collective-permute-start.1 = (bf16[128,512]{1,0:T(8,128)(2,1)S(1)}, bf16[128,512]{1,0:T(8,128)(2,1)S(1)}, u32[]{:S(2)}, u32[]{:S(2)}) collective-permute-start(bf16[128,512]{1,0:T(8,128)(2,1)S(1)} %dynamic-slice_convert_fusion.1), channel_id=1, source_target_pairs={{0,4},{4,0},{8,12},{12,8},{1,5},{5,1},{9,13},{13,9},{2,6},{6,2},{1... | collective-permute-start | bytes 393224 | tf_op jit(solution)/shard_map/ppermute | solution.py:23
  13.3 0.7 %fusion.2 = f32[256,512]{1,0:T(8,128)S(1)} fusion(bf16[2,6,256,512]{3,2,1,0:T(8,128)(2,1)S(1)} %bitcast.78, bf16[2,6,256,256]{3,2,0,1:T(8,128)(2,1)S(1)} %fusion.11, bf16[512,256]{1,0:T(8,128)(2,1)S(1)} %copy-done), kind=kOutput, calls=%fused_computation.6 | convolution fusion | flops 404881408 | bytes 3145728 | tf_op jit(solution)/shard_map/mrc,nc->mrn/dot_general | solution.py:84
  14.1 3.6 %collective-permute-done.1 = bf16[128,512]{1,0:T(8,128)(2,1)S(1)} collective-permute-done((bf16[128,512]{1,0:T(8,128)(2,1)S(1)}, bf16[128,512]{1,0:T(8,128)(2,1)S(1)}, u32[]{:S(2)}, u32[]{:S(2)}) %collective-permute-start.1) | collective-permute-done | bytes 131104 | tf_op jit(solution)/shard_map/ppermute | solution.py:23
  17.7 3.0 %collective-permute-start.2 = (bf16[128,512]{1,0:T(8,128)(2,1)S(1)}, bf16[128,512]{1,0:T(8,128)(2,1)S(1)}, u32[]{:S(2)}, u32[]{:S(2)}) collective-permute-start(bf16[128,512]{1,0:T(8,128)(2,1)S(1)} %fusion.26), channel_id=1, source_target_pairs={{0,8},{4,12},{8,0},{12,4},{1,9},{5,13},{9,1},{13,5},{2,10},{6,14},... | collective-permute-start | bytes 393224 | tf_op jit(solution)/shard_map/ppermute | solution.py:30
  20.7 2.8 %collective-permute-start.6 = (bf16[128,512]{1,0:T(8,128)(2,1)S(1)}, bf16[128,512]{1,0:T(8,128)(2,1)S(1)}, u32[]{:S(2)}, u32[]{:S(2)}) collective-permute-start(bf16[128,512]{1,0:T(8,128)(2,1)S(1)} %fusion.27), channel_id=1, source_target_pairs={{0,8},{4,12},{8,0},{12,4},{1,9},{5,13},{9,1},{13,5},{2,10},{6,14},... | collective-permute-start | bytes 393224 | tf_op jit(solution)/shard_map/ppermute | solution.py:30
  23.5 7.0 %collective-permute-done.2 = bf16[128,512]{1,0:T(8,128)(2,1)S(1)} collective-permute-done((bf16[128,512]{1,0:T(8,128)(2,1)S(1)}, bf16[128,512]{1,0:T(8,128)(2,1)S(1)}, u32[]{:S(2)}, u32[]{:S(2)}) %collective-permute-start.2) | collective-permute-done | bytes 131104 | tf_op jit(solution)/shard_map/ppermute | solution.py:30
  30.7 1.6 %collective-permute-done.6 = bf16[128,512]{1,0:T(8,128)(2,1)S(1)} collective-permute-done((bf16[128,512]{1,0:T(8,128)(2,1)S(1)}, bf16[128,512]{1,0:T(8,128)(2,1)S(1)}, u32[]{:S(2)}, u32[]{:S(2)}) %collective-permute-start.6) | collective-permute-done | bytes 131104 | tf_op jit(solution)/shard_map/ppermute | solution.py:30
  32.3 0.6 %collective-permute-start.7 = (bf16[128,512]{1,0:T(8,128)(2,1)S(1)}, bf16[128,512]{1,0:T(8,128)(2,1)S(1)}, u32[]{:S(2)}, u32[]{:S(2)}) collective-permute-start(bf16[128,512]{1,0:T(8,128)(2,1)S(1)} %fusion.20), channel_id=1, source_target_pairs={{0,4},{4,0},{8,12},{12,8},{1,5},{5,1},{9,13},{13,9},{2,6},{6,2},{1... | collective-permute-start | bytes 393224 | tf_op jit(solution)/shard_map/ppermute | solution.py:40
  32.9 3.7 %collective-permute-done.3 = bf16[128,512]{1,0:T(8,128)(2,1)S(1)} collective-permute-done((bf16[128,512]{1,0:T(8,128)(2,1)S(1)}, bf16[128,512]{1,0:T(8,128)(2,1)S(1)}, u32[]{:S(2)}, u32[]{:S(2)}) %collective-permute-start.3) | collective-permute-done | bytes 131104 | tf_op jit(solution)/shard_map/ppermute | solution.py:40
  36.7 0.6 %fusion.12 = bf16[6,256,256]{2,1,0:T(8,128)(2,1)S(1)} fusion(f32[256,512]{1,0:T(8,128)S(1)} %maximum_convert_fusion, bf16[2,6,256,512]{3,2,1,0:T(8,128)(2,1)S(1)} %bitcast.79, bf16[512,256]{1,0:T(8,128)(2,1)S(1)} %copy-done), kind=kOutput, calls=%fused_computation.19 | convolution fusion | flops 405405696 | bytes 3145728 | tf_op jit(solution)/shard_map/mrn,nc->mrc/dot_general | solution.py:96
  37.7 0.3 collective-permute-done.7
  38.1 0.6 %fusion.15 = bf16[6,256,256]{2,1,0:T(8,128)(2,1)S(1)} fusion(f32[256,512]{1,0:T(8,128)S(1)} %maximum_convert_fusion.1, bf16[2,6,256,512]{3,2,1,0:T(8,128)(2,1)S(1)} %bitcast.80, bf16[512,256]{1,0:T(8,128)(2,1)S(1)} %copy-done), kind=kOutput, calls=%fused_computation.20 | convolution fusion | flops 405405696 | bytes 3145728 | tf_op jit(solution)/shard_map/mrn,nc->mrc/dot_general | solution.py:96
  39.2 0.7 %collective-permute-done.4 = f32[128,6,256]{2,0,1:T(8,128)S(1)} collective-permute-done((f32[128,6,256]{2,0,1:T(8,128)S(1)}, f32[128,6,256]{2,0,1:T(8,128)S(1)}, u32[]{:S(2)}, u32[]{:S(2)}) %collective-permute-start.4) | collective-permute-done | bytes 786464 | tf_op jit(solution)/shard_map/ppermute | solution.py:8
  39.9 0.3 fusion.19
  40.2 1.1 %collective-permute-done.8 = f32[128,6,256]{2,0,1:T(8,128)S(1)} collective-permute-done((f32[128,6,256]{2,0,1:T(8,128)S(1)}, f32[128,6,256]{2,0,1:T(8,128)S(1)}, u32[]{:S(2)}, u32[]{:S(2)}) %collective-permute-start.8) | collective-permute-done | bytes 786464 | tf_op jit(solution)/shard_map/ppermute | solution.py:8
  41.3 0.3 fusion.18
  41.9 1.7 %copy.14 = bf16[128,6,2,256]{3,2,1,0:T(2,128)(2,1)} copy(bf16[128,6,2,256]{3,0,1,2:T(8,128)(2,1)S(1)} %fusion.8) | data formatting | bytes 1572864 | tf_op jit(solution)/shard_map/convert_element_type | solution.py:111
  (31 shorter events, 2.2 us)
Async XLA Ops:
  0.0 9.7 %copy-start = (bf16[512,256]{1,0:T(8,128)(2,1)S(1)}, bf16[512,256]{1,0:T(8,128)(2,1)}, u32[]{:S(2)}) copy-start(bf16[512,256]{1,0:T(8,128)(2,1)} %param.9) | copy-start | bytes 786436
  1.3 6.5 %collective-permute-start = (bf16[128,6,2,256]{3,0,2,1:T(8,128)(2,1)S(1)}, bf16[128,6,2,256]{3,0,2,1:T(8,128)(2,1)}, u32[]{:S(2)}, u32[]{:S(2)}) collective-permute-start(bf16[128,6,2,256]{3,0,2,1:T(8,128)(2,1)S(1)} %copy.8), channel_id=1, source_target_pairs={{0,1},{1,0},{2,3},{3,2},{4,5},{5,4},{6,7},{7,6},{8,9},{9,8},{10,11... | collective-permute-start | bytes 2359304 | tf_op jit(solution)/shard_map/ppermute | solution.py:8
  1.8 4.3 %copy-start.4 = (f32[256,2,512]{2,1,0:T(2,128)S(1)}, f32[256,2,512]{2,1,0:T(2,128)}, u32[]{:S(2)}) copy-start(f32[256,2,512]{2,1,0:T(2,128)} %param.7) | copy-start | bytes 3145732
  6.1 1.1 %copy-start.1 = (bf16[128,6,2,256]{3,2,1,0:T(2,128)(2,1)S(1)}, bf16[128,6,2,256]{3,2,1,0:T(2,128)(2,1)}, u32[]{:S(2)}) copy-start(bf16[128,6,2,256]{3,2,1,0:T(2,128)(2,1)} %param.6) | copy-start | bytes 2359300
  6.1 1.1 %copy-start.3 = (bf16[256,256]{1,0:T(8,128)(2,1)S(1)}, bf16[256,256]{1,0:T(8,128)(2,1)}, u32[]{:S(2)}) copy-start(bf16[256,256]{1,0:T(8,128)(2,1)} %param.8) | copy-start | bytes 393220
  7.8 2.1 %copy-start.2 = (bf16[256,6,2,512]{3,0,1,2:T(8,128)(2,1)S(1)}, bf16[256,6,2,512]{3,0,1,2:T(8,128)(2,1)}, u32[]{:S(2)}) copy-start(bf16[256,6,2,512]{3,0,1,2:T(8,128)(2,1)} %copy.33) | copy-start | bytes 9437188
  10.6 7.0 %collective-permute-start.1 = (bf16[128,512]{1,0:T(8,128)(2,1)S(1)}, bf16[128,512]{1,0:T(8,128)(2,1)S(1)}, u32[]{:S(2)}, u32[]{:S(2)}) collective-permute-start(bf16[128,512]{1,0:T(8,128)(2,1)S(1)} %dynamic-slice_convert_fusion.1), channel_id=1, source_target_pairs={{0,4},{4,0},{8,12},{12,8},{1,5},{5,1},{9,13},{13,9},{2,6},{6,2},{1... | collective-permute-start | bytes 393224 | tf_op jit(solution)/shard_map/ppermute | solution.py:23
  14.0 6.7 %collective-permute-start.5 = (bf16[128,512]{1,0:T(8,128)(2,1)S(1)}, bf16[128,512]{1,0:T(8,128)(2,1)S(1)}, u32[]{:S(2)}, u32[]{:S(2)}) collective-permute-start(bf16[128,512]{1,0:T(8,128)(2,1)S(1)} %dynamic-slice_convert_fusion), channel_id=1, source_target_pairs={{0,4},{4,0},{8,12},{12,8},{1,5},{5,1},{9,13},{13,9},{2,6},{6,2},{1... | collective-permute-start | bytes 393224 | tf_op jit(solution)/shard_map/ppermute | solution.py:23
  17.7 12.9 %collective-permute-start.2 = (bf16[128,512]{1,0:T(8,128)(2,1)S(1)}, bf16[128,512]{1,0:T(8,128)(2,1)S(1)}, u32[]{:S(2)}, u32[]{:S(2)}) collective-permute-start(bf16[128,512]{1,0:T(8,128)(2,1)S(1)} %fusion.26), channel_id=1, source_target_pairs={{0,8},{4,12},{8,0},{12,4},{1,9},{5,13},{9,1},{13,5},{2,10},{6,14},... | collective-permute-start | bytes 393224 | tf_op jit(solution)/shard_map/ppermute | solution.py:30
  20.7 11.5 %collective-permute-start.6 = (bf16[128,512]{1,0:T(8,128)(2,1)S(1)}, bf16[128,512]{1,0:T(8,128)(2,1)S(1)}, u32[]{:S(2)}, u32[]{:S(2)}) collective-permute-start(bf16[128,512]{1,0:T(8,128)(2,1)S(1)} %fusion.27), channel_id=1, source_target_pairs={{0,8},{4,12},{8,0},{12,4},{1,9},{5,13},{9,1},{13,5},{2,10},{6,14},... | collective-permute-start | bytes 393224 | tf_op jit(solution)/shard_map/ppermute | solution.py:30
  30.6 6.0 %collective-permute-start.3 = (bf16[128,512]{1,0:T(8,128)(2,1)S(1)}, bf16[128,512]{1,0:T(8,128)(2,1)S(1)}, u32[]{:S(2)}, u32[]{:S(2)}) collective-permute-start(bf16[128,512]{1,0:T(8,128)(2,1)S(1)} %fusion.21), channel_id=1, source_target_pairs={{0,4},{4,0},{8,12},{12,8},{1,5},{5,1},{9,13},{13,9},{2,6},{6,2},{1... | collective-permute-start | bytes 393224 | tf_op jit(solution)/shard_map/ppermute | solution.py:40
  32.3 5.7 %collective-permute-start.7 = (bf16[128,512]{1,0:T(8,128)(2,1)S(1)}, bf16[128,512]{1,0:T(8,128)(2,1)S(1)}, u32[]{:S(2)}, u32[]{:S(2)}) collective-permute-start(bf16[128,512]{1,0:T(8,128)(2,1)S(1)} %fusion.20), channel_id=1, source_target_pairs={{0,4},{4,0},{8,12},{12,8},{1,5},{5,1},{9,13},{13,9},{2,6},{6,2},{1... | collective-permute-start | bytes 393224 | tf_op jit(solution)/shard_map/ppermute | solution.py:40
  37.6 2.4 %collective-permute-start.4 = (f32[128,6,256]{2,0,1:T(8,128)S(1)}, f32[128,6,256]{2,0,1:T(8,128)S(1)}, u32[]{:S(2)}, u32[]{:S(2)}) collective-permute-start(f32[128,6,256]{2,0,1:T(8,128)S(1)} %fusion.33), channel_id=1, source_target_pairs={{0,1},{1,0},{2,3},{3,2},{4,5},{5,4},{6,7},{7,6},{8,9},{9,8},{10,11... | collective-permute-start | bytes 2359304 | tf_op jit(solution)/shard_map/ppermute | solution.py:8
  39.0 2.4 %collective-permute-start.8 = (f32[128,6,256]{2,0,1:T(8,128)S(1)}, f32[128,6,256]{2,0,1:T(8,128)S(1)}, u32[]{:S(2)}, u32[]{:S(2)}) collective-permute-start(f32[128,6,256]{2,0,1:T(8,128)S(1)} %fusion.31), channel_id=1, source_target_pairs={{0,1},{1,0},{2,3},{3,2},{4,5},{5,4},{6,7},{7,6},{8,9},{9,8},{10,11... | collective-permute-start | bytes 2359304 | tf_op jit(solution)/shard_map/ppermute | solution.py:8
